TPU v7x, 32 devices: a whole 2x2x4 slice. The times are simulated.
32 devices in a mesh: section: 4 (over y, core), site: 8 (over z, x).
Axes of the slice: x: 2, y: 2, z: 4, core: 2. Of those that a mesh axis runs over, the one named last changes fastest.
Arguments:
- acts: bfloat16 [4, 8, 4096], P('section', 'site'), may hold values from -36 to 36
- patches: bfloat16 [4, 2048, 1024], P('section', 'site'), may hold values from -36 to 36
- site_tiles: int32 [8, 256], replicated, may hold values from 0 to 2047, as said below
- site_count: int32 [8], replicated, may hold values from 128 to 256, as said below
- q_weight: bfloat16 [4, 2048, 4096], P('section', 'site'), may hold values from -0.09375 to 0.09375
- q_gain: float32 [4, 128], P('section'), may hold values from 1 to 2.5
- k_gain: float32 [4, 128], P('section'), may hold values from 1 to 2.5
- tile_in: bfloat16 [4, 1024, 512], P('section', 'site'), may hold values from -0.1875 to 0.1875
- tile_out: bfloat16 [4, 512, 4096], P('section', 'site'), may hold values from -0.25 to 0.25
- out_weight: bfloat16 [4, 2048, 4096], P('section', 'site'), may hold values from -0.125 to 0.125
- ffn_gain: float32 [4, 4096], P('section'), may hold values from 0.25 to 1.75
- gate_weight: bfloat16 [4, 7168, 4096], P('section', 'site'), may hold values from -0.09375 to 0.09375
- up_weight: bfloat16 [4, 7168, 4096], P('section', 'site'), may hold values from -0.09375 to 0.09375
- down_weight: bfloat16 [4, 7168, 4096], P('section', 'site'), may hold values from -0.0625 to 0.0625
Outputs:
- passed: bfloat16 [4, 8, 4096], P('section', 'site')
Inputs may be any that keep to these rules, and one draw needn't show every extreme that they name: `site_tiles`: shard k owns tiles k * 256 to (k + 1) * 256 - 1. Of the live entries (l < site_count[n]) of the one site held by a device, at most 40 name tiles of one shard, and in every device exactly 40 name tiles of some shard. All entries of one device's sites are different tiles. `site_count`: sites n with n % 1 == 0, except site 8 - 1, have all 256 entries live; site 8 - 1 has exactly 128.
All inputs are finite; a program needn't handle non-finite values.
Results may differ from a plain program's by a relative error of at most 0.0055.
Values may be sent and summed in bfloat16 or wider, within the bound.
No kernel may reach another device: no remote copies, remote signals or barrier semaphores. Data moves between devices by JAX's collectives and lax.ppermute only.
A program may use at most 128 MiB of HBM per device.

v0:
```python
import math

import jax
import jax.numpy as jnp
from jax import lax
from jax.sharding import PartitionSpec as P

HEADS = 16


epsilon = 1e-05


def shifted(value, axis, steps):
    count = lax.axis_size(axis)
    pairs = [(source, (source + steps) % count) for source in range(count)]
    return lax.ppermute(value, axis, pairs)


def by_rows(left, weight_rows):
    return lax.dot_general(
        left, weight_rows, (((1,), (1,)), ((), ())), preferred_element_type=jnp.float32
    )


def head_norm(values, gain_row):
    shaped = values.astype(jnp.float32).reshape(values.shape[0], -1, gain_row.shape[0])
    scaled = (
        shaped * lax.rsqrt(jnp.mean(shaped * shaped, axis=-1, keepdims=True) + epsilon) * gain_row
    )
    return scaled.reshape(values.shape[0], -1)


def rms_norm(values, gain_row):
    return (
        values * lax.rsqrt(jnp.mean(values * values, axis=-1, keepdims=True) + epsilon) * gain_row
    )


def encode(tile_rows, weight_in, weight_out, key_gain):
    hidden = jax.nn.gelu(
        jnp.dot(tile_rows, weight_in, preferred_element_type=jnp.float32), approximate=True
    ).astype(jnp.bfloat16)
    keyval = jnp.dot(hidden, weight_out, preferred_element_type=jnp.float32)
    half_width = keyval.shape[1] // 2
    normed_keys = head_norm(keyval[:, :half_width], key_gain)
    return jnp.concatenate([normed_keys, keyval[:, half_width:]], axis=1).astype(jnp.bfloat16)


def shards(
    acts,
    patches,
    site_tiles,
    site_count,
    q_weight,
    q_gain,
    k_gain,
    tile_in,
    tile_out,
    out_weight,
    ffn_gain,
    gate_weight,
    up_weight,
    down_weight,
):
    group_size = lax.axis_size("site")
    my_index = lax.axis_index("site")
    sites_here = acts.shape[1]
    list_width = site_tiles.shape[1]
    tiles_here = patches.shape[1]
    head_size = q_gain.shape[1]
    capacity = max(2, 5 * sites_here * list_width // (4 * group_size))
    current = acts[0]
    weight_in, weight_out = (
        lax.all_gather(tile_in[0], "site", axis=0, tiled=True),
        lax.all_gather(tile_out[0], "site", axis=0, tiled=True),
    )
    slot_index = jnp.arange(list_width, dtype=jnp.int32)
    live_all = slot_index[None, :] < site_count[:, None]
    owner_all = site_tiles // tiles_here
    local_all = site_tiles % tiles_here
    mine_mask = jnp.logical_and(live_all, owner_all == my_index).astype(jnp.int32)
    slot_rank = jnp.cumsum(mine_mask, axis=1) - 1
    targets = jnp.where(
        mine_mask == 1,
        jnp.arange(group_size, dtype=jnp.int32)[:, None] * capacity + slot_rank,
        group_size * capacity,
    )
    send_index = (
        jnp.zeros((group_size * capacity + 1,), jnp.int32)
        .at[targets.reshape(-1)]
        .set(local_all.reshape(-1))
    )
    send_index = send_index[:-1].reshape(group_size, capacity)
    my_tiles = lax.dynamic_slice_in_dim(site_tiles, my_index * sites_here, sites_here, 0)
    my_count = lax.dynamic_slice_in_dim(site_count, my_index * sites_here, sites_here, 0)
    my_live = slot_index[None, :] < my_count[:, None]
    my_owner = (my_tiles // tiles_here).reshape(-1)
    one_hot = jnp.logical_and(
        my_owner[:, None] == jnp.arange(group_size, dtype=jnp.int32)[None, :],
        my_live.reshape(-1)[:, None],
    ).astype(jnp.int32)
    my_rank = jnp.sum(jnp.cumsum(one_hot, axis=0) * one_hot, axis=1) - 1
    fetch_index = jnp.where(my_live.reshape(-1), my_owner * capacity + my_rank, 0)
    encoded = encode(patches[0], weight_in, weight_out, k_gain[0])
    arrived = lax.all_to_all(encoded[send_index], "site", split_axis=0, concat_axis=0, tiled=True)
    pair_kv = arrived.reshape(group_size * capacity, -1)[fetch_index]
    pair_kv = pair_kv.reshape(sites_here, list_width, 2, HEADS, head_size)
    everyone = lax.all_gather(current, "site", axis=0, tiled=True)
    q_part = by_rows(everyone, q_weight[0]).astype(jnp.bfloat16)
    my_queries = lax.all_to_all(q_part, "site", split_axis=0, concat_axis=1, tiled=True)
    queries = head_norm(my_queries, q_gain[0]).astype(jnp.bfloat16)
    query_heads = queries.reshape(sites_here, HEADS, head_size)
    scores = jnp.einsum(
        "nhd,nlhd->nhl", query_heads, pair_kv[:, :, 0], preferred_element_type=jnp.float32
    ) / math.sqrt(head_size)
    exponents = jnp.exp(scores) * my_live.astype(jnp.float32)[:, None, :]
    weights = (exponents / jnp.sum(exponents, axis=-1, keepdims=True)).astype(jnp.bfloat16)
    combined = jnp.einsum(
        "nhl,nlhd->nhd", weights, pair_kv[:, :, 1], preferred_element_type=jnp.float32
    )
    combined = combined.reshape(sites_here, -1).astype(jnp.bfloat16)
    columns = lax.all_to_all(combined, "site", split_axis=1, concat_axis=0, tiled=True)
    residual = current.astype(jnp.float32) + lax.psum_scatter(
        jnp.dot(columns, out_weight[0], preferred_element_type=jnp.float32),
        "site",
        scatter_dimension=0,
        tiled=True,
    )
    normed = rms_norm(residual, ffn_gain[0]).astype(jnp.bfloat16)
    normed_rows = lax.all_gather(normed, "site", axis=0, tiled=True)
    gate_sum = by_rows(normed_rows, gate_weight[0])
    up_sum = by_rows(normed_rows, up_weight[0])
    hidden = (jax.nn.silu(gate_sum) * up_sum).astype(jnp.bfloat16)
    output_rows = (
        residual
        + lax.psum_scatter(
            jnp.dot(hidden, down_weight[0], preferred_element_type=jnp.float32),
            "site",
            scatter_dimension=0,
            tiled=True,
        )
    ).astype(jnp.bfloat16)
    return shifted(output_rows[None], "section", 1)


def solution(mesh):
    return jax.shard_map(
        shards,
        mesh=mesh,
        in_specs=(
            P("section", "site", None),
            P("section", "site", None),
            P(),
            P(),
            P("section", "site", None),
            P("section", None),
            P("section", None),
            P("section", "site", None),
            P("section", "site", None),
            P("section", "site", None),
            P("section", None),
            P("section", "site", None),
            P("section", "site", None),
            P("section", "site", None),
        ),
        out_specs=P("section", "site", None),
        check_vma=False,
    )
```

profile of v0, /device:TPU:0, one launch (start us, length us, event | category | flops | bytes accessed | tf_op | source)
XLA Modules:
  0.0 436.5 jit_solution(14200362407360964330)
XLA Ops:
  6.5 0.0 all-gather.7.cloned.1.call-start
  6.6 0.7 all-gather.7.cloned.1.call-update
  7.3 0.0 all-gather.9.cloned.1.call-start
  7.3 0.7 all-gather.9.cloned.1.call-update
  8.0 32.7 %all-gather = bf16[8,1,4096]{2,1,0:T(2,128)(2,1)S(1)} all-gather(bf16[1,1,4096]{2,1,0:T(2,128)(2,1)} %param.14), channel_id=2, replica_groups=mesh['section'=4,'site'=8] {'site'}, dimensions={0}, use_global_device_ids=true | all-gather | bytes 73728 | tf_op jit(solution)/shard_map/all_gather | solution.py:109
  40.7 2.2 fusion.23
  43.0 0.6 broadcast.242
  43.6 0.6 reduce.9
  44.2 0.6 reshape.383
  44.8 5.4 %all-to-all-start = ((bf16[8,2,128]{2,1,0:T(2,128)(2,1)}), bf16[8,2,128]{2,1,0:T(2,128)(2,1)S(1)}, u32[]{:S(2)}, u32[]{:S(2)}) async-start(bf16[8,2,128]{2,1,0:T(2,128)(2,1)} %reshape.383), calls=%async_computation | async-start | bytes 8192 | tf_op jit(solution)/shard_map/all_to_all | solution.py:111
  50.3 0.1 convert_bitcast_fusion.1
  50.3 0.6 reduce-window.14
  50.9 0.2 slice_reduce_fusion.1
  51.2 0.1 fusion.78
  51.3 8.0 %scatter_custom_fusion = s32[321]{0:T(512)S(1)} fusion(s32[2048]{0:T(1024)S(1)} %bitcast.159, s32[2048]{0:T(1024)S(1)} %bitcast.158, s32[]{:T(128)} %constant.85.clone.1), kind=kCustom, calls=%fused_computation.118 | custom fusion | bytes 1288 | tf_op jit(solution)/shard_map/scatter | solution.py:92
  59.3 0.1 reshape.335
  59.4 0.1 reshape.344
  59.5 0.0 all-gather.7.cloned.1.call-done
  59.6 67.3 %all-gather.9.cloned.1.call-done = bf16[1,512,4096]{2,1,0:T(8,128)(2,1)} async-done(((bf16[1,64,4096]{2,1,0:T(8,128)(2,1)}), bf16[1,512,4096]{2,1,0:T(8,128)(2,1)}) %all-gather.9.cloned.1.call-update) | async-done | bytes 4194320 | tf_op jit(solution)/shard_map/all_gather | solution.py:76
  126.9 6.1 %fusion.6 = f32[256,4096]{1,0:T(8,128)} fusion(bf16[1,512,4096]{2,1,0:T(8,128)(2,1)} %all-gather.9.cloned.1.call-done, bf16[1,1024,512]{2,1,0:T(8,128)(2,1)} %all-gather.7.cloned.1.call-done, bf16[1,256,1024]{2,1,0:T(8,128)(2,1)S(1)} %copy-done.1), kind=kOutput, calls=%fused_computation.9 | convolution fusion | flops 1343356928 | bytes 9961472 | tf_op jit(solution)/shard_map/dot_general | solution.py:44
  133.0 1.7 slice.54
  134.7 1.7 multiply_bitcast_fusion
  136.5 1.7 copy.37
  138.2 2.2 reduce_sum.46
  140.4 0.1 copy.25
  140.5 0.1 copy.26
  140.6 0.6 mul.170
  141.2 2.4 fusion.9
  143.6 1.5 pad_maximum_fusion
  145.1 9.9 %gather_fusion = bf16[320,4096]{1,0:T(8,128)(2,1)} fusion(bf16[256,4096]{1,0:T(8,128)(2,1)} %pad_maximum_fusion, s32[1024]{0:T(1024)S(1)} %pad_clamp_fusion.1), kind=kCustom, calls=%fused_computation | custom fusion | bytes 5244160 | tf_op jit(solution)/shard_map/gather | solution.py:106
  155.1 4.5 %all-to-all-start.1 = ((bf16[8,40,4096]{2,1,0:T(8,128)(2,1)}), bf16[8,40,4096]{2,1,0:T(8,128)(2,1)}, u32[]{:S(2)}, u32[]{:S(2)}) async-start(bf16[8,40,4096]{2,1,0:T(8,128)(2,1)} %bitcast.144), calls=%async_computation.1 | async-start | bytes 5242880 | tf_op jit(solution)/shard_map/all_to_all | solution.py:106
  159.6 0.2 all-reduce.5.cloned.1.call-start
  159.8 0.6 dynamic_slice.6
  160.4 0.7 add_compare_fusion
  161.1 0.6 reduce-window.16
  161.7 0.2 slice_reduce_fusion
  162.0 0.7 iota_compare_fusion.3
  162.6 0.1 fusion.76
  162.7 0.7 compare_select_fusion.2
  163.5 0.1 reduce_sum.45
  163.6 0.1 fusion.87
  163.7 54.5 %all-to-all-done.1 = bf16[8,40,4096]{2,1,0:T(8,128)(2,1)} async-done(((bf16[8,40,4096]{2,1,0:T(8,128)(2,1)}), bf16[8,40,4096]{2,1,0:T(8,128)(2,1)}, u32[]{:S(2)}, u32[]{:S(2)}) %all-to-all-start.1) | async-done | bytes 2621472 | tf_op jit(solution)/shard_map/all_to_all | solution.py:106
  218.2 7.3 %gather_fusion.1 = bf16[256,4096]{1,0:T(8,128)(2,1)} fusion(bf16[320,4096]{1,0:T(8,128)(2,1)} %bitcast.16, s32[1024]{0:T(1024)S(1)} %pad_clamp_fusion), kind=kCustom, calls=%fused_computation.1 | custom fusion | bytes 4195328 | tf_op jit(solution)/shard_map/gather | solution.py:107
  225.5 2.1 copy.41
  227.5 0.4 slice_bitcast_fusion.1
  227.9 0.4 fusion.30
  228.3 0.1 fusion.73
  228.4 0.1 fusion.80
  228.5 0.3 fusion.28
  228.9 0.7 reduce.10
  229.6 9.9 %all_to_all.31 = bf16[8,2,128]{2,1,0:T(2,128)(2,1)S(1)} all-to-all(bf16[8,2,128]{2,1,0:T(2,128)(2,1)S(1)} %reshape.385), channel_id=1, replica_groups=mesh['section'=4,'site'=8] {'site'}, dimensions={0} | all-to-all | bytes 8192 | tf_op jit(solution)/shard_map/all_to_all | solution.py:123
  239.4 1.0 fusion.10
  240.5 0.0 all-reduce.7.cloned.1.call-start
  240.6 0.6 dynamic-slice
  241.2 66.5 %all-reduce.5.cloned.1.call-done = f32[8,4096]{1,0:T(8,128)} async-done(((f32[8,4096]{1,0:T(8,128)}), f32[8,4096]{1,0:T(8,128)}) %all-reduce.5.cloned.1.call-update) | async-done | bytes 131088
  307.6 2.2 multiply_reduce_fusion
  310.4 30.5 %all-gather.3 = bf16[8,1,4096]{2,1,0:T(2,128)(2,1)S(1)} all-gather(bf16[1,1,4096]{2,1,0:T(2,128)(2,1)S(1)} %convert_bitcast_fusion), channel_id=1, replica_groups=mesh['section'=4,'site'=8] {'site'}, dimensions={0}, use_global_device_ids=true | all-gather | bytes 73728 | tf_op jit(solution)/shard_map/all_gather | solution.py:131
  341.0 5.1 %fusion.4 = f32[8,896]{1,0:T(8,128)S(1)} fusion(bf16[1,896,4096]{2,1,0:T(8,128)(2,1)} %param.25, bf16[8,1,4096]{2,1,0:T(2,128)(2,1)S(1)} %all-gather.3), kind=kOutput, calls=%fused_computation.7 | convolution fusion | flops 58720256 | bytes 7434240 | tf_op jit(solution)/shard_map/dot_general | solution.py:21
  346.1 9.3 %fusion = f32[8,4096]{1,0:T(8,128)} fusion(bf16[1,896,4096]{2,1,0:T(8,128)(2,1)} %param.27, bf16[1,896,4096]{2,1,0:T(8,128)(2,1)} %param.26, f32[8,896]{1,0:T(8,128)S(1)} %fusion.4, bf16[8,1,4096]{2,1,0:T(2,128)(2,1)S(1)} %all-gather.3), kind=kOutput, calls=%fused_computation.3 | convolution fusion | flops 117483520 | bytes 14905344 | tf_op jit(solution)/shard_map/dot_general | solution.py:138
  355.4 69.1 %all-reduce.7.cloned.1.call-done = f32[8,4096]{1,0:T(8,128)} async-done(((f32[8,4096]{1,0:T(8,128)}), f32[8,4096]{1,0:T(8,128)}) %all-reduce.7.cloned.1.call-update) | async-done | bytes 131088
  424.6 1.6 fusion.68
  426.1 0.1 collective-permute-start
  426.2 3.2 collective-permute-done
  429.4 0.6 copy.79
  (47 shorter events, 0.4 us)
Async XLA Ops:
  6.5 232.9 %copy-start = (bf16[1,256,4096]{2,1,0:T(8,128)(2,1)S(1)}, bf16[1,256,4096]{2,1,0:T(8,128)(2,1)}, u32[]{:S(2)}) copy-start(bf16[1,256,4096]{2,1,0:T(8,128)(2,1)} %param.23) | copy-start | bytes 6291460
  6.5 43.7 %copy-start.3 = (s32[8,256]{1,0:T(8,128)S(1)}, s32[8,256]{1,0:T(8,128)}, u32[]{:S(2)}) copy-start(s32[8,256]{1,0:T(8,128)} %param.16) | copy-start | bytes 24580
  6.5 43.7 %copy-start.6 = (s32[8]{0:T(128)S(1)}, s32[8]{0:T(128)}, u32[]{:S(2)}) copy-start(s32[8]{0:T(128)} %param.17) | copy-start | bytes 100
  6.5 53.0 %copy-start.5 = (f32[1,128]{1,0:T(1,128)S(1)}, f32[1,128]{1,0:T(1,128)}, u32[]{:S(2)}) copy-start(f32[1,128]{1,0:T(1,128)} %param.20) | copy-start | bytes 1540
  6.5 120.3 %copy-start.1 = (bf16[1,256,1024]{2,1,0:T(8,128)(2,1)S(1)}, bf16[1,256,1024]{2,1,0:T(8,128)(2,1)}, u32[]{:S(2)}) copy-start(bf16[1,256,1024]{2,1,0:T(8,128)(2,1)} %param.15) | copy-start | bytes 1572868
  6.5 53.0 %all-gather.7.cloned.1.call-start = ((), (), s32[]{:S(2)}) async-start(), calls=%async_computation.3 | async-start | bytes 1179648 | tf_op jit(solution)/shard_map/all_gather | solution.py:75
  7.3 119.6 %all-gather.9.cloned.1.call-start = ((), (), s32[]{:S(2)}) async-start(), calls=%async_computation.4 | async-start | bytes 4718592 | tf_op jit(solution)/shard_map/all_gather | solution.py:76
  44.8 110.3 %all-to-all-start = ((bf16[8,2,128]{2,1,0:T(2,128)(2,1)}), bf16[8,2,128]{2,1,0:T(2,128)(2,1)S(1)}, u32[]{:S(2)}, u32[]{:S(2)}) async-start(bf16[8,2,128]{2,1,0:T(2,128)(2,1)} %reshape.383), calls=%async_computation | async-start | bytes 8192 | tf_op jit(solution)/shard_map/all_to_all | solution.py:111
  155.1 8.5 %copy-start.7 = (f32[1,128]{1,0:T(1,128)S(1)}, f32[1,128]{1,0:T(1,128)}, u32[]{:S(2)}) copy-start(f32[1,128]{1,0:T(1,128)} %param.19) | copy-start | bytes 1540
  155.1 63.1 %all-to-all-start.1 = ((bf16[8,40,4096]{2,1,0:T(8,128)(2,1)}), bf16[8,40,4096]{2,1,0:T(8,128)(2,1)}, u32[]{:S(2)}, u32[]{:S(2)}) async-start(bf16[8,40,4096]{2,1,0:T(8,128)(2,1)} %bitcast.144), calls=%async_computation.1 | async-start | bytes 5242880 | tf_op jit(solution)/shard_map/all_to_all | solution.py:106
  159.6 148.0 %all-reduce.5.cloned.1.call-start = ((), (), s32[]{:S(2)}) async-start(), calls=%async_computation.5 | async-start | bytes 262144
  227.9 12.7 %copy-start.8 = (u32[32]{0:T(128)S(1)}, u32[32]{0:T(128)}, u32[]{:S(2)}) copy-start(u32[32]{0:T(128)} %constant.112) | copy-start | bytes 388
  227.9 79.7 %copy-start.2 = (bf16[1,1,4096]{2,1,0:T(2,128)(2,1)S(1)}, bf16[1,1,4096]{2,1,0:T(2,128)(2,1)}, u32[]{:S(2)}) copy-start(bf16[1,1,4096]{2,1,0:T(2,128)(2,1)} %param.14) | copy-start | bytes 24580
  227.9 82.5 %copy-start.4 = (f32[1,4096]{1,0:T(1,128)S(1)}, f32[1,4096]{1,0:T(1,128)}, u32[]{:S(2)}) copy-start(f32[1,4096]{1,0:T(1,128)} %param.24) | copy-start | bytes 49156
  240.5 184.1 %all-reduce.7.cloned.1.call-start = ((), (), s32[]{:S(2)}) async-start(), calls=%async_computation.6 | async-start | bytes 262144
  426.1 3.2 collective-permute-start
Sparse Core Ops, SparseCore 0:
  9.5 42.8 all-gather.6
  54.6 72.2 all-gather.8
  240.6 66.9 all-reduce.4
  355.6 68.9 all-reduce.6
where the time goes:
time: 437 us; the launch traced here: 436 us
  waiting for transfers between devices  262 us (60%)
  blocking collectives  73.1 us (17%)
  local copies, waits for them, and re-layouts  35.5 us (8%)
  matrix products  24.6 us (6%)
  other arithmetic  16.9 us (4%)
  between operations  14 us (3%)
  starting transfers between devices  10.4 us (2%)
    unnamed x6, waiting for transfers between devices  137 us
    all_gather x1, waiting for transfers between devices, shards(): lax.all_gather(tile_out[0], 'site', axis=0, tiled=True)  67.3 us
    all_to_all x1, waiting for transfers between devices, shards(): lax.all_to_all(encoded[send_index], 'site', split_axis=0, concat_axis=0,...  54.5 us
    all_gather x1, blocking collectives, shards(): everyone = lax.all_gather(current, 'site', axis=0, tiled=True)  32.7 us
    all_gather x1, blocking collectives, shards(): normed_rows = lax.all_gather(normed, 'site', axis=0, tiled=True)  30.5 us
    gather x1, local copies, waits for them, and re-layouts, shards(): encoded[send_index]  9.94 us
    all_to_all x1, blocking collectives, shards(): lax.all_to_all(combined, 'site', split_axis=1, concat_axis=0, tiled=True)  9.88 us
    dot_general x1, matrix products, shards(): jnp.dot(hidden, down_weight[0], preferred_element_type=jnp.float32)  9.34 us
  transfers between devices with their start and end apart: 7, of which 5 were waited for; matrix products, arithmetic and copies ran while one was open for 10% of the time, Pallas kernels for 0%

commit v1 on v0

v1 whole, which is shorter than its diff:
```python
import math

import jax
import jax.numpy as jnp
from jax import lax
from jax.sharding import PartitionSpec as P

HEADS = 16


epsilon = 1e-05

DIRECT_LIMIT = 8


def shift_pairs(count, steps):
    return [(source, (source + steps) % count) for source in range(count)]


def by_rows(left, weight_rows):
    return lax.dot_general(
        left, weight_rows, (((1,), (1,)), ((), ())), preferred_element_type=jnp.float32
    )


def head_norm(values, gain_row):
    shaped = values.astype(jnp.float32).reshape(values.shape[0], -1, gain_row.shape[0])
    scaled = (
        shaped * lax.rsqrt(jnp.mean(shaped * shaped, axis=-1, keepdims=True) + epsilon) * gain_row
    )
    return scaled.reshape(values.shape[0], -1)


def rms_norm(values, gain_row):
    return (
        values * lax.rsqrt(jnp.mean(values * values, axis=-1, keepdims=True) + epsilon) * gain_row
    )


def encode(tile_rows, weight_in, weight_out, key_gain):
    hidden = jax.nn.gelu(
        jnp.dot(tile_rows, weight_in, preferred_element_type=jnp.float32), approximate=True
    ).astype(jnp.bfloat16)
    keyval = jnp.dot(hidden, weight_out, preferred_element_type=jnp.float32)
    half_width = keyval.shape[1] // 2
    normed_keys = head_norm(keyval[:, :half_width], key_gain)
    return jnp.concatenate([normed_keys, keyval[:, half_width:]], axis=1).astype(jnp.bfloat16)


def to_source_order(slots, count, me):
    return jnp.take(slots, (me - jnp.arange(count, dtype=jnp.int32)) % count, axis=0)


def site_gather(value, count, me):
    if count > DIRECT_LIMIT:
        return lax.all_gather(value, "site", axis=0, tiled=False)
    slots = [value] + [
        lax.ppermute(value, "site", shift_pairs(count, steps)) for steps in range(1, count)
    ]
    return to_source_order(jnp.stack(slots), count, me)


def site_exchange(by_target, count, me):
    if count > DIRECT_LIMIT:
        return lax.all_to_all(by_target, "site", split_axis=0, concat_axis=0, tiled=True)
    slots = [lax.dynamic_index_in_dim(by_target, me, 0, keepdims=False)]
    for steps in range(1, count):
        piece = lax.dynamic_index_in_dim(by_target, (me + steps) % count, 0, keepdims=False)
        slots.append(lax.ppermute(piece, "site", shift_pairs(count, steps)))
    return to_source_order(jnp.stack(slots), count, me)


def ring_gather(values, count, me):
    if count > DIRECT_LIMIT:
        return [lax.all_gather(value, "site", axis=0, tiled=False) for value in values]
    order = list(range(0, count, 2)) + [i for i in range(count - 1, -1, -1) if i % 2 == 1]
    place = [0] * count
    for position, device in enumerate(order):
        place[device] = position
    forward = [(order[p], order[(p + 1) % count]) for p in range(count)]
    backward = [(order[p], order[(p - 1) % count]) for p in range(count)]
    order_arr = jnp.array(order, dtype=jnp.int32)
    my_place = jnp.array(place, dtype=jnp.int32)[me]
    forward_steps = count // 2
    backward_steps = count - 1 - forward_steps
    slot_source = [me]
    slots = [[value] for value in values]
    moving = list(values)
    for steps in range(1, forward_steps + 1):
        moving = [lax.ppermute(value, "site", forward) for value in moving]
        for slot, value in zip(slots, moving):
            slot.append(value)
        slot_source.append(order_arr[(my_place - steps) % count])
    moving = list(values)
    for steps in range(1, backward_steps + 1):
        moving = [lax.ppermute(value, "site", backward) for value in moving]
        for slot, value in zip(slots, moving):
            slot.append(value)
        slot_source.append(order_arr[(my_place + steps) % count])
    source_of_slot = jnp.stack(slot_source)
    slot_of_source = jnp.zeros((count,), jnp.int32).at[source_of_slot].set(
        jnp.arange(count, dtype=jnp.int32)
    )
    return [jnp.take(jnp.stack(slot), slot_of_source, axis=0) for slot in slots]


def shards(
    acts,
    patches,
    site_tiles,
    site_count,
    q_weight,
    q_gain,
    k_gain,
    tile_in,
    tile_out,
    out_weight,
    ffn_gain,
    gate_weight,
    up_weight,
    down_weight,
):
    group_size = lax.axis_size("site")
    section_count = lax.axis_size("section")
    my_index = lax.axis_index("site")
    sites_here = acts.shape[1]
    list_width = site_tiles.shape[1]
    tiles_here = patches.shape[1]
    head_size = q_gain.shape[1]
    capacity = max(2, 5 * sites_here * list_width // (4 * group_size))
    entries = sites_here * list_width
    current = acts[0]

    gathered_in, gathered_out = ring_gather([tile_in[0], tile_out[0]], group_size, my_index)
    weight_in = gathered_in.reshape(-1, gathered_in.shape[-1])
    weight_out = gathered_out.reshape(-1, gathered_out.shape[-1])

    slot_index = jnp.arange(list_width, dtype=jnp.int32)
    live_all = (slot_index[None, :] < site_count[:, None]).reshape(group_size, entries)
    owner_all = (site_tiles // tiles_here).reshape(group_size, entries)
    local_all = (site_tiles % tiles_here).reshape(group_size, entries)
    mine_mask = jnp.logical_and(live_all, owner_all == my_index)
    slot_rank = jnp.cumsum(mine_mask.astype(jnp.int32), axis=1) - 1
    picks = jnp.logical_and(
        mine_mask[:, :, None],
        slot_rank[:, :, None] == jnp.arange(capacity, dtype=jnp.int32)[None, None, :],
    )
    send_index = jnp.sum(jnp.where(picks, local_all[:, :, None], 0), axis=1)
    send_rows = patches[0][send_index.reshape(-1)].reshape(group_size, capacity, -1)
    arrived = site_exchange(send_rows, group_size, my_index)

    my_tiles = lax.dynamic_slice_in_dim(site_tiles, my_index * sites_here, sites_here, 0)
    my_count = lax.dynamic_slice_in_dim(site_count, my_index * sites_here, sites_here, 0)
    my_live = slot_index[None, :] < my_count[:, None]
    my_owner = (my_tiles // tiles_here).reshape(-1)
    one_hot = jnp.logical_and(
        my_owner[:, None] == jnp.arange(group_size, dtype=jnp.int32)[None, :],
        my_live.reshape(-1)[:, None],
    ).astype(jnp.int32)
    my_rank = jnp.sum(jnp.cumsum(one_hot, axis=0) * one_hot, axis=1) - 1
    fetch_index = jnp.where(my_live.reshape(-1), my_owner * capacity + my_rank, 0)
    pair_rows = arrived.reshape(group_size * capacity, -1)[fetch_index]
    pair_kv = encode(pair_rows, weight_in, weight_out, k_gain[0])
    pair_kv = pair_kv.reshape(sites_here, list_width, 2, HEADS, head_size)

    everyone = site_gather(current, group_size, my_index).reshape(-1, current.shape[-1])
    q_part = by_rows(everyone, q_weight[0]).astype(jnp.bfloat16)
    q_blocks = site_exchange(
        q_part.reshape(group_size, sites_here, -1), group_size, my_index
    )
    my_queries = jnp.moveaxis(q_blocks, 0, 1).reshape(sites_here, -1)
    queries = head_norm(my_queries, q_gain[0]).astype(jnp.bfloat16)
    query_heads = queries.reshape(sites_here, HEADS, head_size)
    scores = jnp.einsum(
        "nhd,nlhd->nhl", query_heads, pair_kv[:, :, 0], preferred_element_type=jnp.float32
    ) / math.sqrt(head_size)
    exponents = jnp.exp(scores) * my_live.astype(jnp.float32)[:, None, :]
    weights = (exponents / jnp.sum(exponents, axis=-1, keepdims=True)).astype(jnp.bfloat16)
    combined = jnp.einsum(
        "nhl,nlhd->nhd", weights, pair_kv[:, :, 1], preferred_element_type=jnp.float32
    )
    combined = combined.reshape(sites_here, -1).astype(jnp.bfloat16)
    column_blocks = jnp.moveaxis(combined.reshape(sites_here, group_size, -1), 1, 0)
    columns = site_exchange(column_blocks, group_size, my_index).reshape(
        group_size * sites_here, -1
    )
    attn_part = jnp.dot(columns, out_weight[0], preferred_element_type=jnp.float32)
    attn_sum = jnp.sum(
        site_exchange(attn_part.reshape(group_size, sites_here, -1), group_size, my_index),
        axis=0,
    )
    residual = current.astype(jnp.float32) + attn_sum
    normed = rms_norm(residual, ffn_gain[0]).astype(jnp.bfloat16)
    normed_rows = site_gather(normed, group_size, my_index).reshape(-1, normed.shape[-1])
    gate_sum = by_rows(normed_rows, gate_weight[0])
    up_sum = by_rows(normed_rows, up_weight[0])
    hidden = (jax.nn.silu(gate_sum) * up_sum).astype(jnp.bfloat16)
    down_part = jnp.dot(hidden, down_weight[0], preferred_element_type=jnp.float32)
    down_part = down_part.reshape(group_size, sites_here, -1)
    if group_size > DIRECT_LIMIT:
        down_sum = lax.psum_scatter(down_part, "site", scatter_dimension=0, tiled=True)[0]
        output_rows = (residual + down_sum).astype(jnp.bfloat16)
        pairs = shift_pairs(section_count, 1)
        return lax.ppermute(output_rows[None], "section", pairs)
    contributions = []
    for steps in range(group_size):
        piece = lax.dynamic_index_in_dim(
            down_part, (my_index + steps) % group_size, 0, keepdims=False
        )
        if steps == 0:
            piece = piece + residual
        pairs = [
            (
                section * group_size + site,
                ((section + 1) % section_count) * group_size + (site + steps) % group_size,
            )
            for section in range(section_count)
            for site in range(group_size)
        ]
        contributions.append(lax.ppermute(piece, ("section", "site"), pairs))
    output_rows = sum(contributions[1:], contributions[0]).astype(jnp.bfloat16)
    return output_rows[None]


def solution(mesh):
    return jax.shard_map(
        shards,
        mesh=mesh,
        in_specs=(
            P("section", "site", None),
            P("section", "site", None),
            P(),
            P(),
            P("section", "site", None),
            P("section", None),
            P("section", None),
            P("section", "site", None),
            P("section", "site", None),
            P("section", "site", None),
            P("section", None),
            P("section", "site", None),
            P("section", "site", None),
            P("section", "site", None),
        ),
        out_specs=P("section", "site", None),
        check_vma=False,
    )
```

time: 437 us -> 278 us (0.64)
  waiting for transfers between devices: 262 us -> 69.9 us
  starting transfers between devices: 10.4 us -> 90.5 us
  blocking collectives: 73.1 us -> 0 us
  local copies, waits for them, and re-layouts: 35.5 us -> 61.9 us
  other arithmetic: 16.9 us -> 25 us
  between operations: 14 us -> 5.92 us
    unnamed x6 -> x0, waiting for transfers between devices: 137 us -> none
    ppermute x1 -> x64, starting transfers between devices: 0.06 us -> 90.5 us  [the longest x28 39.4 us: site_exchange(): slots.append(lax.ppermute(piece, 'site', shift_pairs(count, steps)))]
    all_gather x2 -> x0, waiting for transfers between devices: 67.3 us -> none  [the longest x1 67.3 us: shards(): lax.all_gather(tile_out[0], 'site', axis=0, tiled=True)]
    ppermute x1 -> x64, waiting for transfers between devices: 3.15 us -> 69.9 us  [the longest x28 40.8 us: site_exchange(): slots.append(lax.ppermute(piece, 'site', shift_pairs(count, steps)))]
    all_gather x2 -> x0, blocking collectives: 63.2 us -> none  [the longest x1 32.7 us: shards(): everyone = lax.all_gather(current, 'site', axis=0, tiled=True)]
    all_to_all x2 -> x0, waiting for transfers between devices: 54.5 us -> none  [the longest x1 54.5 us: shards(): lax.all_to_all(encoded[send_index], 'site', split_axis=0, concat_axis=0,...]
    unnamed x28 -> x54, local copies, waits for them, and re-layouts: 5.66 us -> 24.6 us
    all_to_all x2 -> x0, starting transfers between devices: 9.95 us -> none  [the longest x1 5.44 us: shards(): lax.all_to_all(q_part, 'site', split_axis=0, concat_axis=1, tiled=True)]
  transfers between devices with their start and end apart: 7 -> 64, of which waited for: 5 -> 25; matrix products, arithmetic and copies ran while one was open for 10% -> 21% of each run, Pallas kernels for 0% -> 0%
where the time goes in v1:
time: 278 us; the launch traced here: 276 us
  starting transfers between devices  90.5 us (33%)
  waiting for transfers between devices  69.9 us (25%)
  local copies, waits for them, and re-layouts  61.9 us (22%)
  other arithmetic  25 us (9%)
  matrix products  23.1 us (8%)
  between operations  5.92 us (2%)
    ppermute x28, waiting for transfers between devices, site_exchange(): slots.append(lax.ppermute(piece, 'site', shift_pairs(count, steps)))  40.8 us
    ppermute x28, starting transfers between devices, site_exchange(): slots.append(lax.ppermute(piece, 'site', shift_pairs(count, steps)))  39.4 us
    ppermute x14, starting transfers between devices, site_gather(): lax.ppermute(value, 'site', shift_pairs(count, steps))  25.5 us
    unnamed x54, local copies, waits for them, and re-layouts  24.6 us
    ppermute x8, waiting for transfers between devices, ring_gather(): moving = [lax.ppermute(value, 'site', forward) for value in moving]  19.9 us
    ppermute x8, starting transfers between devices, shards(): contributions.append(lax.ppermute(piece, ('section', 'site'), pairs))  12 us
    dot_general x1, matrix products, shards(): jnp.dot(hidden, down_weight[0], preferred_element_type=jnp.float32)  8.69 us
    gather x2, local copies, waits for them, and re-layouts, ring_gather(): return [jnp.take(jnp.stack(slot), slot_of_source, axis=0) for slot in slots]  8.08 us
  transfers between devices with their start and end apart: 64, of which 25 were waited for; matrix products, arithmetic and copies ran while one was open for 21% of the time, Pallas kernels for 0%

profile of v1, /device:TPU:0, one launch (start us, length us, event | category | flops | bytes accessed | tf_op | source)
XLA Modules:
  0.0 276.5 jit_solution(8127418103139599502)
XLA Ops:
  0.0 2.9 %collective-permute-start = (bf16[1,4096]{1,0:T(2,128)(2,1)}, bf16[1,4096]{1,0:T(2,128)(2,1)S(1)}, u32[]{:S(2)}, u32[]{:S(2)}) collective-permute-start(bf16[1,4096]{1,0:T(2,128)(2,1)} %bitcast.296), channel_id=1, source_target_pairs={{0,1},{1,2},{2,3},{3,4},{4,5},{5,6},{6,7},{7,0},{8,9},{9,10},{10,1... | collective-permute-start | bytes 24584 | tf_op jit(solution)/shard_map/ppermute | solution.py:58
  4.5 2.6 collective-permute-start.2
  8.3 2.6 collective-permute-start.4
  16.8 1.6 fusion.102
  18.4 4.4 %stack.251 = s32[8,1]{0,1:T(1,128)S(1)} concatenate(s32[1,1]{0,1:T(1,128)} %bitcast.53, s32[1,1]{0,1:T(1,128)} %bitcast.55, s32[1,1]{0,1:T(1,128)} %bitcast.57, s32[1,1]{0,1:T(1,128)} %bitcast.59, s32[1,1]{0,1:T(1,128)} %bitcast.61, s32[1,1]{0,1:T(1,128)} %bitcast.63, s32[1,1]{0,1:T(1,128)} %bitcast.65, s32[1,1]{0,1:T(1,128)} %bitcast.67), dimensions={0} | concatenate | bytes 64 | tf_op jit(solution)/shard_map/stack | solution.py:100
  28.8 1.9 constant_dynamic-update-slice_fusion.1
  35.8 1.6 constant_dynamic-update-slice_fusion
  39.3 2.1 gather_fusion
  48.9 2.2 fusion.18
  51.2 1.6 collective-permute-start.7
  53.6 2.2 collective-permute-start.9
  55.8 2.1 collective-permute-start.10
  57.9 3.1 %collective-permute-start.11 = (bf16[1,256]{1,0:T(2,128)(2,1)S(1)}, bf16[1,256]{1,0:T(2,128)(2,1)S(1)}, u32[]{:S(2)}, u32[]{:S(2)}) collective-permute-start(bf16[1,256]{1,0:T(2,128)(2,1)S(1)} %get-tuple-element.45), channel_id=1, source_target_pairs={{0,5},{1,6},{2,7},{3,0},{4,1},{5,2},{6,3},{7,4},{8,13},{9,14},{10,... | collective-permute-start | bytes 1544 | tf_op jit(solution)/shard_map/ppermute | solution.py:69
  68.8 9.8 %collective-permute-done.14 = bf16[40,1024]{1,0:T(8,128)(2,1)S(1)} collective-permute-done((bf16[40,1024]{1,0:T(8,128)(2,1)}, bf16[40,1024]{1,0:T(8,128)(2,1)S(1)}, u32[]{:S(2)}, u32[]{:S(2)}) %collective-permute-start.14) | collective-permute-done | bytes 81952 | tf_op jit(solution)/shard_map/ppermute | solution.py:69
  79.9 5.8 %collective-permute-done.15 = bf16[40,1024]{1,0:T(8,128)(2,1)S(1)} collective-permute-done((bf16[40,1024]{1,0:T(8,128)(2,1)}, bf16[40,1024]{1,0:T(8,128)(2,1)S(1)}, u32[]{:S(2)}, u32[]{:S(2)}) %collective-permute-start.15) | collective-permute-done | bytes 81952 | tf_op jit(solution)/shard_map/ppermute | solution.py:69
  86.3 5.6 %collective-permute-done.16 = bf16[40,1024]{1,0:T(8,128)(2,1)S(1)} collective-permute-done((bf16[40,1024]{1,0:T(8,128)(2,1)S(1)}, bf16[40,1024]{1,0:T(8,128)(2,1)S(1)}, u32[]{:S(2)}, u32[]{:S(2)}) %collective-permute-start.16) | collective-permute-done | bytes 81952 | tf_op jit(solution)/shard_map/ppermute | solution.py:69
  92.7 4.6 %collective-permute-done.17 = bf16[40,1024]{1,0:T(8,128)(2,1)S(1)} collective-permute-done((bf16[40,1024]{1,0:T(8,128)(2,1)S(1)}, bf16[40,1024]{1,0:T(8,128)(2,1)S(1)}, u32[]{:S(2)}, u32[]{:S(2)}) %collective-permute-start.17) | collective-permute-done | bytes 81952 | tf_op jit(solution)/shard_map/ppermute | solution.py:69
  98.1 4.5 %collective-permute-done.18 = bf16[40,1024]{1,0:T(8,128)(2,1)S(1)} collective-permute-done((bf16[40,1024]{1,0:T(8,128)(2,1)S(1)}, bf16[40,1024]{1,0:T(8,128)(2,1)S(1)}, u32[]{:S(2)}, u32[]{:S(2)}) %collective-permute-start.18) | collective-permute-done | bytes 81952 | tf_op jit(solution)/shard_map/ppermute | solution.py:69
  102.6 3.2 %collective-permute-start.19 = (bf16[40,1024]{1,0:T(8,128)(2,1)S(1)}, bf16[40,1024]{1,0:T(8,128)(2,1)S(1)}, u32[]{:S(2)}, u32[]{:S(2)}) collective-permute-start(bf16[40,1024]{1,0:T(8,128)(2,1)S(1)} %get-tuple-element.12), channel_id=1, source_target_pairs={{0,6},{1,7},{2,0},{3,1},{4,2},{5,3},{6,4},{7,5},{8,14},{9,15},{10,... | collective-permute-start | bytes 245768 | tf_op jit(solution)/shard_map/ppermute | solution.py:69
  106.4 2.1 collective-permute-done.19
  108.5 1.6 collective-permute-start.20
  110.8 2.7 collective-permute-done.20
  114.1 1.8 gather_fusion.1
  116.7 2.1 gather_fusion.2
  118.8 2.0 collective-permute-start.26
  122.4 3.0 %collective-permute-done.22 = bf16[128,512]{1,0:T(8,128)(2,1)S(1)} collective-permute-done((bf16[128,512]{1,0:T(8,128)(2,1)}, bf16[128,512]{1,0:T(8,128)(2,1)S(1)}, u32[]{:S(2)}, u32[]{:S(2)}) %collective-permute-start.22) | collective-permute-done | bytes 131104 | tf_op jit(solution)/shard_map/ppermute | solution.py:90
  125.5 2.0 collective-permute-start.27
  128.2 2.3 collective-permute-done.23
  131.2 2.4 collective-permute-start.29
  133.6 1.9 bitcast_dynamic-update-slice_fusion.6
  137.5 1.6 bitcast_dynamic-update-slice_fusion.9
  140.5 2.9 %gather_fusion.3 = bf16[8,128,512]{2,1,0:T(8,128)(2,1)} fusion(bf16[8,128,512]{2,1,0:T(8,128)(2,1)} %bitcast_dynamic-update-slice_fusion.7, s32[1024]{0:T(1024)} %pad_clamp_fusion), kind=kCustom, calls=%fused_computation.7 | custom fusion | bytes 2097184 | tf_op jit(solution)/shard_map/jit(_take)/gather | solution.py:104
  147.3 1.9 bitcast_dynamic-update-slice_fusion.5
  149.2 5.5 %collective-permute-done.30 = bf16[64,4096]{1,0:T(8,128)(2,1)S(1)} collective-permute-done((bf16[64,4096]{1,0:T(8,128)(2,1)}, bf16[64,4096]{1,0:T(8,128)(2,1)S(1)}, u32[]{:S(2)}, u32[]{:S(2)}) %collective-permute-start.30) | collective-permute-done | bytes 524320 | tf_op jit(solution)/shard_map/ppermute | solution.py:90
  156.5 7.4 %collective-permute-done.31 = bf16[64,4096]{1,0:T(8,128)(2,1)S(1)} collective-permute-done((bf16[64,4096]{1,0:T(8,128)(2,1)S(1)}, bf16[64,4096]{1,0:T(8,128)(2,1)S(1)}, u32[]{:S(2)}, u32[]{:S(2)}) %collective-permute-start.31) | collective-permute-done | bytes 524320 | tf_op jit(solution)/shard_map/ppermute | solution.py:90
  164.7 1.9 bitcast_dynamic-update-slice_fusion.2
  166.6 1.9 bitcast_dynamic-update-slice_fusion.1
  169.3 5.1 %gather_fusion.4 = bf16[8,64,4096]{2,1,0:T(8,128)(2,1)} fusion(bf16[8,64,4096]{2,1,0:T(8,128)(2,1)} %bitcast_dynamic-update-slice_fusion, s32[1024]{0:T(1024)} %pad_clamp_fusion), kind=kCustom, calls=%fused_computation.8 | custom fusion | bytes 8388640 | tf_op jit(solution)/shard_map/jit(_take)/gather | solution.py:104
  174.5 4.7 %bitcast_select_fusion = bf16[512,4096]{1,0:T(8,128)(2,1)} fusion(bf16[8,64,4096]{2,1,0:T(8,128)(2,1)} %gather_fusion.4, pred[512]{0:T(512)(128)(4,1)S(1)} %copy-done.12), kind=kLoop, calls=%fused_computation.17 | loop fusion | flops 2097152 | bytes 8389120 | tf_op jit(solution)/shard_map/jit(_take)/select_n | solution.py:104
  179.1 6.0 %fusion.36 = f32[256,4096]{1,0:T(8,128)} fusion(bf16[512,4096]{1,0:T(8,128)(2,1)} %bitcast_select_fusion, bf16[256,1024]{1,0:T(8,128)(2,1)} %gather_fusion.2, bf16[1024,512]{1,0:T(8,128)(2,1)S(1)} %bitcast_select_fusion.1), kind=kOutput, calls=%fused_computation.58 | convolution fusion | flops 1343356928 | bytes 9961472 | tf_op jit(solution)/shard_map/dot_general | solution.py:44
  185.1 1.7 slice.66
  186.9 1.7 multiply_bitcast_fusion
  188.6 1.7 copy.31
  190.4 2.2 reduce_sum.68
  193.4 2.4 fusion.7
  199.4 2.0 collective-permute-start.36
  201.4 2.8 collective-permute-start.37
  204.8 3.8 %collective-permute-start.39 = (bf16[1,256]{1,0:T(2,128)(2,1)S(1)}, bf16[1,256]{1,0:T(2,128)(2,1)S(1)}, u32[]{:S(2)}, u32[]{:S(2)}) collective-permute-start(bf16[1,256]{1,0:T(2,128)(2,1)S(1)} %get-tuple-element.37), channel_id=1, source_target_pairs={{0,5},{1,6},{2,7},{3,0},{4,1},{5,2},{6,3},{7,4},{8,13},{9,14},{10,... | collective-permute-start | bytes 1544 | tf_op jit(solution)/shard_map/ppermute | solution.py:69
  210.1 2.0 collective-permute-done.40
  216.5 1.9 collective-permute-start.44
  218.4 2.4 collective-permute-start.45
  220.8 1.9 collective-permute-start.46
  229.6 1.7 collective-permute-start.49
  231.3 2.0 collective-permute-start.50
  233.6 2.5 collective-permute-start.52
  236.2 2.3 collective-permute-start.53
  239.6 1.8 collective-permute-start.55
  244.2 5.1 %fusion.4 = f32[8,896]{1,0:T(8,128)S(1)} fusion(bf16[1,896,4096]{2,1,0:T(8,128)(2,1)} %param.31, bf16[8,4096]{1,0:T(8,128)(2,1)S(1)} %gather_fusion.9, pred[8]{0:T(512)(128)(4,1)S(1)} %copy-done.7), kind=kOutput, calls=%fused_computation.15 | convolution fusion | flops 58753024 | bytes 7434248 | tf_op jit(solution)/shard_map/dot_general | solution.py:21
  249.3 8.7 %fusion = f32[8,4096]{1,0:T(8,128)S(1)} fusion(bf16[1,896,4096]{2,1,0:T(8,128)(2,1)} %param.33, bf16[1,896,4096]{2,1,0:T(8,128)(2,1)} %param.32, bf16[8,4096]{1,0:T(8,128)(2,1)S(1)} %gather_fusion.9, pred[8]{0:T(512)(128)(4,1)S(1)} %copy-done.7, f32[8,896]{1,0:T(8,128)S(1)} %fusion.4), kind=kOutput, calls=%fused_computation.11 | convolution fusion | flops 117516288 | bytes 14905352 | tf_op jit(solution)/shard_map/dot_general | solution.py:198
  258.2 4.0 %collective-permute-start.62 = (f32[1,4096]{1,0:T(1,128)S(1)}, f32[1,4096]{1,0:T(1,128)S(1)}, u32[]{:S(2)}, u32[]{:S(2)}) collective-permute-start(f32[1,4096]{1,0:T(1,128)S(1)} %get-tuple-element.21), channel_id=1, source_target_pairs={{0,14},{1,15},{2,8},{3,9},{4,10},{5,11},{6,12},{7,13},{8,22},{9,23... | collective-permute-start | bytes 49160 | tf_op jit(solution)/shard_map/ppermute | solution.py:220
  262.5 2.3 collective-permute-start.60
  265.0 3.6 %collective-permute-start.58 = (f32[1,4096]{1,0:T(1,128)S(1)}, f32[1,4096]{1,0:T(1,128)S(1)}, u32[]{:S(2)}, u32[]{:S(2)}) collective-permute-start(f32[1,4096]{1,0:T(1,128)S(1)} %get-tuple-element.25), channel_id=1, source_target_pairs={{0,10},{1,11},{2,12},{3,13},{4,14},{5,15},{6,8},{7,9},{8,18},{9,19... | collective-permute-start | bytes 49160 | tf_op jit(solution)/shard_map/ppermute | solution.py:220
  271.0 2.4 collective-permute-done.58
  273.4 2.4 collective-permute-done.57
  (220 shorter events, 77.8 us)
Async XLA Ops:
  0.0 42.2 %collective-permute-start = (bf16[1,4096]{1,0:T(2,128)(2,1)}, bf16[1,4096]{1,0:T(2,128)(2,1)S(1)}, u32[]{:S(2)}, u32[]{:S(2)}) collective-permute-start(bf16[1,4096]{1,0:T(2,128)(2,1)} %bitcast.296), channel_id=1, source_target_pairs={{0,1},{1,2},{2,3},{3,4},{4,5},{5,6},{6,7},{7,0},{8,9},{9,10},{10,1... | collective-permute-start | bytes 24584 | tf_op jit(solution)/shard_map/ppermute | solution.py:58
  2.9 40.7 %collective-permute-start.1 = (bf16[1,4096]{1,0:T(2,128)(2,1)}, bf16[1,4096]{1,0:T(2,128)(2,1)S(1)}, u32[]{:S(2)}, u32[]{:S(2)}) collective-permute-start(bf16[1,4096]{1,0:T(2,128)(2,1)} %bitcast.297), channel_id=1, source_target_pairs={{0,2},{1,3},{2,4},{3,5},{4,6},{5,7},{6,0},{7,1},{8,10},{9,11},{10,... | collective-permute-start | bytes 24584 | tf_op jit(solution)/shard_map/ppermute | solution.py:58
  4.5 41.3 %collective-permute-start.2 = (bf16[1,4096]{1,0:T(2,128)(2,1)}, bf16[1,4096]{1,0:T(2,128)(2,1)}, u32[]{:S(2)}, u32[]{:S(2)}) collective-permute-start(bf16[1,4096]{1,0:T(2,128)(2,1)} %bitcast.298), channel_id=1, source_target_pairs={{0,3},{1,4},{2,5},{3,6},{4,7},{5,0},{6,1},{7,2},{8,11},{9,12},{10,... | collective-permute-start | bytes 24584 | tf_op jit(solution)/shard_map/ppermute | solution.py:58
  7.1 38.7 %collective-permute-start.3 = (bf16[1,4096]{1,0:T(2,128)(2,1)}, bf16[1,4096]{1,0:T(2,128)(2,1)}, u32[]{:S(2)}, u32[]{:S(2)}) collective-permute-start(bf16[1,4096]{1,0:T(2,128)(2,1)} %bitcast.299), channel_id=1, source_target_pairs={{0,4},{1,5},{2,6},{3,7},{4,0},{5,1},{6,2},{7,3},{8,12},{9,13},{10,... | collective-permute-start | bytes 24584 | tf_op jit(solution)/shard_map/ppermute | solution.py:58
  8.3 37.5 %collective-permute-start.4 = (bf16[1,4096]{1,0:T(2,128)(2,1)}, bf16[1,4096]{1,0:T(2,128)(2,1)}, u32[]{:S(2)}, u32[]{:S(2)}) collective-permute-start(bf16[1,4096]{1,0:T(2,128)(2,1)} %bitcast.300), channel_id=1, source_target_pairs={{0,5},{1,6},{2,7},{3,0},{4,1},{5,2},{6,3},{7,4},{8,13},{9,14},{10,... | collective-permute-start | bytes 24584 | tf_op jit(solution)/shard_map/ppermute | solution.py:58
  42.2 3.8 %collective-permute-start.5 = (bf16[1,4096]{1,0:T(2,128)(2,1)S(1)}, bf16[1,4096]{1,0:T(2,128)(2,1)S(1)}, u32[]{:S(2)}, u32[]{:S(2)}) collective-permute-start(bf16[1,4096]{1,0:T(2,128)(2,1)S(1)} %bitcast.301), channel_id=1, source_target_pairs={{0,6},{1,7},{2,0},{3,1},{4,2},{5,3},{6,4},{7,5},{8,14},{9,15},{10,... | collective-permute-start | bytes 24584 | tf_op jit(solution)/shard_map/ppermute | solution.py:58
  43.7 3.7 %collective-permute-start.6 = (bf16[1,4096]{1,0:T(2,128)(2,1)S(1)}, bf16[1,4096]{1,0:T(2,128)(2,1)S(1)}, u32[]{:S(2)}, u32[]{:S(2)}) collective-permute-start(bf16[1,4096]{1,0:T(2,128)(2,1)S(1)} %bitcast.302), channel_id=1, source_target_pairs={{0,7},{1,0},{2,1},{3,2},{4,3},{5,4},{6,5},{7,6},{8,15},{9,8},{10,9... | collective-permute-start | bytes 24584 | tf_op jit(solution)/shard_map/ppermute | solution.py:58
  51.2 9.8 %collective-permute-start.7 = (bf16[1,256]{1,0:T(2,128)(2,1)S(1)}, bf16[1,256]{1,0:T(2,128)(2,1)S(1)}, u32[]{:S(2)}, u32[]{:S(2)}) collective-permute-start(bf16[1,256]{1,0:T(2,128)(2,1)S(1)} %get-tuple-element.49), channel_id=1, source_target_pairs={{0,1},{1,2},{2,3},{3,4},{4,5},{5,6},{6,7},{7,0},{8,9},{9,10},{10,1... | collective-permute-start | bytes 1544 | tf_op jit(solution)/shard_map/ppermute | solution.py:69
  52.8 8.4 %collective-permute-start.8 = (bf16[1,256]{1,0:T(2,128)(2,1)S(1)}, bf16[1,256]{1,0:T(2,128)(2,1)S(1)}, u32[]{:S(2)}, u32[]{:S(2)}) collective-permute-start(bf16[1,256]{1,0:T(2,128)(2,1)S(1)} %get-tuple-element.48), channel_id=1, source_target_pairs={{0,2},{1,3},{2,4},{3,5},{4,6},{5,7},{6,0},{7,1},{8,10},{9,11},{10,... | collective-permute-start | bytes 1544 | tf_op jit(solution)/shard_map/ppermute | solution.py:69
  53.6 8.9 %collective-permute-start.9 = (bf16[1,256]{1,0:T(2,128)(2,1)S(1)}, bf16[1,256]{1,0:T(2,128)(2,1)S(1)}, u32[]{:S(2)}, u32[]{:S(2)}) collective-permute-start(bf16[1,256]{1,0:T(2,128)(2,1)S(1)} %get-tuple-element.47), channel_id=1, source_target_pairs={{0,3},{1,4},{2,5},{3,6},{4,7},{5,0},{6,1},{7,2},{8,11},{9,12},{10,... | collective-permute-start | bytes 1544 | tf_op jit(solution)/shard_map/ppermute | solution.py:69
  55.8 7.4 %collective-permute-start.10 = (bf16[1,256]{1,0:T(2,128)(2,1)S(1)}, bf16[1,256]{1,0:T(2,128)(2,1)S(1)}, u32[]{:S(2)}, u32[]{:S(2)}) collective-permute-start(bf16[1,256]{1,0:T(2,128)(2,1)S(1)} %get-tuple-element.46), channel_id=1, source_target_pairs={{0,4},{1,5},{2,6},{3,7},{4,0},{5,1},{6,2},{7,3},{8,12},{9,13},{10,... | collective-permute-start | bytes 1544 | tf_op jit(solution)/shard_map/ppermute | solution.py:69
  57.9 6.6 %collective-permute-start.11 = (bf16[1,256]{1,0:T(2,128)(2,1)S(1)}, bf16[1,256]{1,0:T(2,128)(2,1)S(1)}, u32[]{:S(2)}, u32[]{:S(2)}) collective-permute-start(bf16[1,256]{1,0:T(2,128)(2,1)S(1)} %get-tuple-element.45), channel_id=1, source_target_pairs={{0,5},{1,6},{2,7},{3,0},{4,1},{5,2},{6,3},{7,4},{8,13},{9,14},{10,... | collective-permute-start | bytes 1544 | tf_op jit(solution)/shard_map/ppermute | solution.py:69
  61.0 4.2 %collective-permute-start.12 = (bf16[1,256]{1,0:T(2,128)(2,1)S(1)}, bf16[1,256]{1,0:T(2,128)(2,1)S(1)}, u32[]{:S(2)}, u32[]{:S(2)}) collective-permute-start(bf16[1,256]{1,0:T(2,128)(2,1)S(1)} %get-tuple-element.44), channel_id=1, source_target_pairs={{0,6},{1,7},{2,0},{3,1},{4,2},{5,3},{6,4},{7,5},{8,14},{9,15},{10,... | collective-permute-start | bytes 1544 | tf_op jit(solution)/shard_map/ppermute | solution.py:69
  61.2 5.4 %collective-permute-start.13 = (bf16[1,256]{1,0:T(2,128)(2,1)S(1)}, bf16[1,256]{1,0:T(2,128)(2,1)S(1)}, u32[]{:S(2)}, u32[]{:S(2)}) collective-permute-start(bf16[1,256]{1,0:T(2,128)(2,1)S(1)} %get-tuple-element.43), channel_id=1, source_target_pairs={{0,7},{1,0},{2,1},{3,2},{4,3},{5,4},{6,5},{7,6},{8,15},{9,8},{10,9... | collective-permute-start | bytes 1544 | tf_op jit(solution)/shard_map/ppermute | solution.py:69
  62.5 68.7 %collective-permute-start.28 = (bf16[64,4096]{1,0:T(8,128)(2,1)}, bf16[64,4096]{1,0:T(8,128)(2,1)}, u32[]{:S(2)}, u32[]{:S(2)}) collective-permute-start(bf16[64,4096]{1,0:T(8,128)(2,1)} %bitcast.292), channel_id=1, source_target_pairs={{0,2},{2,4},{4,6},{6,7},{7,5},{5,3},{3,1},{1,0},{8,10},{10,12},{12... | collective-permute-start | bytes 1572872 | tf_op jit(solution)/shard_map/ppermute | solution.py:90
  63.2 72.4 %collective-permute-start.32 = (bf16[64,4096]{1,0:T(8,128)(2,1)}, bf16[64,4096]{1,0:T(8,128)(2,1)}, u32[]{:S(2)}, u32[]{:S(2)}) collective-permute-start(bf16[64,4096]{1,0:T(8,128)(2,1)} %bitcast.293), channel_id=1, source_target_pairs={{0,1},{2,0},{4,2},{6,4},{7,6},{5,7},{3,5},{1,3},{8,9},{10,8},{12,1... | collective-permute-start | bytes 1572872 | tf_op jit(solution)/shard_map/ppermute | solution.py:96
  64.6 54.2 %collective-permute-start.21 = (bf16[128,512]{1,0:T(8,128)(2,1)S(1)}, bf16[128,512]{1,0:T(8,128)(2,1)}, u32[]{:S(2)}, u32[]{:S(2)}) collective-permute-start(bf16[128,512]{1,0:T(8,128)(2,1)S(1)} %bitcast.306), channel_id=1, source_target_pairs={{0,2},{2,4},{4,6},{6,7},{7,5},{5,3},{3,1},{1,0},{8,10},{10,12},{12... | collective-permute-start | bytes 393224 | tf_op jit(solution)/shard_map/ppermute | solution.py:90
  65.2 53.6 %collective-permute-start.25 = (bf16[128,512]{1,0:T(8,128)(2,1)S(1)}, bf16[128,512]{1,0:T(8,128)(2,1)}, u32[]{:S(2)}, u32[]{:S(2)}) collective-permute-start(bf16[128,512]{1,0:T(8,128)(2,1)S(1)} %bitcast.307), channel_id=1, source_target_pairs={{0,1},{2,0},{4,2},{6,4},{7,6},{5,7},{3,5},{1,3},{8,9},{10,8},{12,1... | collective-permute-start | bytes 393224 | tf_op jit(solution)/shard_map/ppermute | solution.py:96
  66.6 12.1 %collective-permute-start.14 = (bf16[40,1024]{1,0:T(8,128)(2,1)}, bf16[40,1024]{1,0:T(8,128)(2,1)S(1)}, u32[]{:S(2)}, u32[]{:S(2)}) collective-permute-start(bf16[40,1024]{1,0:T(8,128)(2,1)} %get-tuple-element.17), channel_id=1, source_target_pairs={{0,1},{1,2},{2,3},{3,4},{4,5},{5,6},{6,7},{7,0},{8,9},{9,10},{10,1... | collective-permute-start | bytes 245768 | tf_op jit(solution)/shard_map/ppermute | solution.py:69
  78.7 7.0 %collective-permute-start.15 = (bf16[40,1024]{1,0:T(8,128)(2,1)}, bf16[40,1024]{1,0:T(8,128)(2,1)S(1)}, u32[]{:S(2)}, u32[]{:S(2)}) collective-permute-start(bf16[40,1024]{1,0:T(8,128)(2,1)} %get-tuple-element.16), channel_id=1, source_target_pairs={{0,2},{1,3},{2,4},{3,5},{4,6},{5,7},{6,0},{7,1},{8,10},{9,11},{10,... | collective-permute-start | bytes 245768 | tf_op jit(solution)/shard_map/ppermute | solution.py:69
  85.7 6.2 %collective-permute-start.16 = (bf16[40,1024]{1,0:T(8,128)(2,1)S(1)}, bf16[40,1024]{1,0:T(8,128)(2,1)S(1)}, u32[]{:S(2)}, u32[]{:S(2)}) collective-permute-start(bf16[40,1024]{1,0:T(8,128)(2,1)S(1)} %get-tuple-element.15), channel_id=1, source_target_pairs={{0,3},{1,4},{2,5},{3,6},{4,7},{5,0},{6,1},{7,2},{8,11},{9,12},{10,... | collective-permute-start | bytes 245768 | tf_op jit(solution)/shard_map/ppermute | solution.py:69
  91.9 5.3 %collective-permute-start.17 = (bf16[40,1024]{1,0:T(8,128)(2,1)S(1)}, bf16[40,1024]{1,0:T(8,128)(2,1)S(1)}, u32[]{:S(2)}, u32[]{:S(2)}) collective-permute-start(bf16[40,1024]{1,0:T(8,128)(2,1)S(1)} %get-tuple-element.14), channel_id=1, source_target_pairs={{0,4},{1,5},{2,6},{3,7},{4,0},{5,1},{6,2},{7,3},{8,12},{9,13},{10,... | collective-permute-start | bytes 245768 | tf_op jit(solution)/shard_map/ppermute | solution.py:69
  97.3 5.3 %collective-permute-start.18 = (bf16[40,1024]{1,0:T(8,128)(2,1)S(1)}, bf16[40,1024]{1,0:T(8,128)(2,1)S(1)}, u32[]{:S(2)}, u32[]{:S(2)}) collective-permute-start(bf16[40,1024]{1,0:T(8,128)(2,1)S(1)} %get-tuple-element.13), channel_id=1, source_target_pairs={{0,5},{1,6},{2,7},{3,0},{4,1},{5,2},{6,3},{7,4},{8,13},{9,14},{10,... | collective-permute-start | bytes 245768 | tf_op jit(solution)/shard_map/ppermute | solution.py:69
  102.6 5.9 %collective-permute-start.19 = (bf16[40,1024]{1,0:T(8,128)(2,1)S(1)}, bf16[40,1024]{1,0:T(8,128)(2,1)S(1)}, u32[]{:S(2)}, u32[]{:S(2)}) collective-permute-start(bf16[40,1024]{1,0:T(8,128)(2,1)S(1)} %get-tuple-element.12), channel_id=1, source_target_pairs={{0,6},{1,7},{2,0},{3,1},{4,2},{5,3},{6,4},{7,5},{8,14},{9,15},{10,... | collective-permute-start | bytes 245768 | tf_op jit(solution)/shard_map/ppermute | solution.py:69
  108.5 4.9 %collective-permute-start.20 = (bf16[40,1024]{1,0:T(8,128)(2,1)S(1)}, bf16[40,1024]{1,0:T(8,128)(2,1)S(1)}, u32[]{:S(2)}, u32[]{:S(2)}) collective-permute-start(bf16[40,1024]{1,0:T(8,128)(2,1)S(1)} %get-tuple-element.11), channel_id=1, source_target_pairs={{0,7},{1,0},{2,1},{3,2},{4,3},{5,4},{6,5},{7,6},{8,15},{9,8},{10,9... | collective-permute-start | bytes 245768 | tf_op jit(solution)/shard_map/ppermute | solution.py:69
  118.8 6.6 %collective-permute-start.22 = (bf16[128,512]{1,0:T(8,128)(2,1)}, bf16[128,512]{1,0:T(8,128)(2,1)S(1)}, u32[]{:S(2)}, u32[]{:S(2)}) collective-permute-start(bf16[128,512]{1,0:T(8,128)(2,1)} %collective-permute-done.21), channel_id=1, source_target_pairs={{0,2},{2,4},{4,6},{6,7},{7,5},{5,3},{3,1},{1,0},{8,10},{10,12},{12... | collective-permute-start | bytes 393224 | tf_op jit(solution)/shard_map/ppermute | solution.py:90
  118.8 6.6 %collective-permute-start.26 = (bf16[128,512]{1,0:T(8,128)(2,1)}, bf16[128,512]{1,0:T(8,128)(2,1)S(1)}, u32[]{:S(2)}, u32[]{:S(2)}) collective-permute-start(bf16[128,512]{1,0:T(8,128)(2,1)} %collective-permute-done.25), channel_id=1, source_target_pairs={{0,1},{2,0},{4,2},{6,4},{7,6},{5,7},{3,5},{1,3},{8,9},{10,8},{12,1... | collective-permute-start | bytes 393224 | tf_op jit(solution)/shard_map/ppermute | solution.py:96
  125.4 5.0 %collective-permute-start.23 = (bf16[128,512]{1,0:T(8,128)(2,1)S(1)}, bf16[128,512]{1,0:T(8,128)(2,1)S(1)}, u32[]{:S(2)}, u32[]{:S(2)}) collective-permute-start(bf16[128,512]{1,0:T(8,128)(2,1)S(1)} %collective-permute-done.22), channel_id=1, source_target_pairs={{0,2},{2,4},{4,6},{6,7},{7,5},{5,3},{3,1},{1,0},{8,10},{10,12},{12... | collective-permute-start | bytes 393224 | tf_op jit(solution)/shard_map/ppermute | solution.py:90
  125.5 14.3 %collective-permute-start.27 = (bf16[128,512]{1,0:T(8,128)(2,1)S(1)}, bf16[128,512]{1,0:T(8,128)(2,1)S(1)}, u32[]{:S(2)}, u32[]{:S(2)}) collective-permute-start(bf16[128,512]{1,0:T(8,128)(2,1)S(1)} %collective-permute-done.26), channel_id=1, source_target_pairs={{0,1},{2,0},{4,2},{6,4},{7,6},{5,7},{3,5},{1,3},{8,9},{10,8},{12,1... | collective-permute-start | bytes 393224 | tf_op jit(solution)/shard_map/ppermute | solution.py:96
  130.4 6.4 %collective-permute-start.24 = (bf16[128,512]{1,0:T(8,128)(2,1)S(1)}, bf16[128,512]{1,0:T(8,128)(2,1)S(1)}, u32[]{:S(2)}, u32[]{:S(2)}) collective-permute-start(bf16[128,512]{1,0:T(8,128)(2,1)S(1)} %collective-permute-done.23), channel_id=1, source_target_pairs={{0,2},{2,4},{4,6},{6,7},{7,5},{5,3},{3,1},{1,0},{8,10},{10,12},{12... | collective-permute-start | bytes 393224 | tf_op jit(solution)/shard_map/ppermute | solution.py:90
  131.2 14.1 %collective-permute-start.29 = (bf16[64,4096]{1,0:T(8,128)(2,1)}, bf16[64,4096]{1,0:T(8,128)(2,1)}, u32[]{:S(2)}, u32[]{:S(2)}) collective-permute-start(bf16[64,4096]{1,0:T(8,128)(2,1)} %collective-permute-done.28), channel_id=1, source_target_pairs={{0,2},{2,4},{4,6},{6,7},{7,5},{5,3},{3,1},{1,0},{8,10},{10,12},{12... | collective-permute-start | bytes 1572872 | tf_op jit(solution)/shard_map/ppermute | solution.py:90
  135.6 10.5 %collective-permute-start.33 = (bf16[64,4096]{1,0:T(8,128)(2,1)}, bf16[64,4096]{1,0:T(8,128)(2,1)}, u32[]{:S(2)}, u32[]{:S(2)}) collective-permute-start(bf16[64,4096]{1,0:T(8,128)(2,1)} %collective-permute-done.32), channel_id=1, source_target_pairs={{0,1},{2,0},{4,2},{6,4},{7,6},{5,7},{3,5},{1,3},{8,9},{10,8},{12,1... | collective-permute-start | bytes 1572872 | tf_op jit(solution)/shard_map/ppermute | solution.py:96
  145.3 9.4 %collective-permute-start.30 = (bf16[64,4096]{1,0:T(8,128)(2,1)}, bf16[64,4096]{1,0:T(8,128)(2,1)S(1)}, u32[]{:S(2)}, u32[]{:S(2)}) collective-permute-start(bf16[64,4096]{1,0:T(8,128)(2,1)} %collective-permute-done.29), channel_id=1, source_target_pairs={{0,2},{2,4},{4,6},{6,7},{7,5},{5,3},{3,1},{1,0},{8,10},{10,12},{12... | collective-permute-start | bytes 1572872 | tf_op jit(solution)/shard_map/ppermute | solution.py:90
  146.0 22.4 %collective-permute-start.34 = (bf16[64,4096]{1,0:T(8,128)(2,1)}, bf16[64,4096]{1,0:T(8,128)(2,1)S(1)}, u32[]{:S(2)}, u32[]{:S(2)}) collective-permute-start(bf16[64,4096]{1,0:T(8,128)(2,1)} %collective-permute-done.33), channel_id=1, source_target_pairs={{0,1},{2,0},{4,2},{6,4},{7,6},{5,7},{3,5},{1,3},{8,9},{10,8},{12,1... | collective-permute-start | bytes 1572872 | tf_op jit(solution)/shard_map/ppermute | solution.py:96
  154.7 9.2 %collective-permute-start.31 = (bf16[64,4096]{1,0:T(8,128)(2,1)S(1)}, bf16[64,4096]{1,0:T(8,128)(2,1)S(1)}, u32[]{:S(2)}, u32[]{:S(2)}) collective-permute-start(bf16[64,4096]{1,0:T(8,128)(2,1)S(1)} %collective-permute-done.30), channel_id=1, source_target_pairs={{0,2},{2,4},{4,6},{6,7},{7,5},{5,3},{3,1},{1,0},{8,10},{10,12},{12... | collective-permute-start | bytes 1572872 | tf_op jit(solution)/shard_map/ppermute | solution.py:90
  197.9 10.7 %collective-permute-start.35 = (bf16[1,256]{1,0:T(2,128)(2,1)S(1)}, bf16[1,256]{1,0:T(2,128)(2,1)S(1)}, u32[]{:S(2)}, u32[]{:S(2)}) collective-permute-start(bf16[1,256]{1,0:T(2,128)(2,1)S(1)} %get-tuple-element.41), channel_id=1, source_target_pairs={{0,1},{1,2},{2,3},{3,4},{4,5},{5,6},{6,7},{7,0},{8,9},{9,10},{10,1... | collective-permute-start | bytes 1544 | tf_op jit(solution)/shard_map/ppermute | solution.py:69
  199.4 10.2 %collective-permute-start.36 = (bf16[1,256]{1,0:T(2,128)(2,1)S(1)}, bf16[1,256]{1,0:T(2,128)(2,1)S(1)}, u32[]{:S(2)}, u32[]{:S(2)}) collective-permute-start(bf16[1,256]{1,0:T(2,128)(2,1)S(1)} %get-tuple-element.40), channel_id=1, source_target_pairs={{0,2},{1,3},{2,4},{3,5},{4,6},{5,7},{6,0},{7,1},{8,10},{9,11},{10,... | collective-permute-start | bytes 1544 | tf_op jit(solution)/shard_map/ppermute | solution.py:69
  201.4 8.7 %collective-permute-start.37 = (bf16[1,256]{1,0:T(2,128)(2,1)S(1)}, bf16[1,256]{1,0:T(2,128)(2,1)S(1)}, u32[]{:S(2)}, u32[]{:S(2)}) collective-permute-start(bf16[1,256]{1,0:T(2,128)(2,1)S(1)} %get-tuple-element.39), channel_id=1, source_target_pairs={{0,3},{1,4},{2,5},{3,6},{4,7},{5,0},{6,1},{7,2},{8,11},{9,12},{10,... | collective-permute-start | bytes 1544 | tf_op jit(solution)/shard_map/ppermute | solution.py:69
  204.2 5.9 %collective-permute-start.38 = (bf16[1,256]{1,0:T(2,128)(2,1)S(1)}, bf16[1,256]{1,0:T(2,128)(2,1)S(1)}, u32[]{:S(2)}, u32[]{:S(2)}) collective-permute-start(bf16[1,256]{1,0:T(2,128)(2,1)S(1)} %get-tuple-element.38), channel_id=1, source_target_pairs={{0,4},{1,5},{2,6},{3,7},{4,0},{5,1},{6,2},{7,3},{8,12},{9,13},{10,... | collective-permute-start | bytes 1544 | tf_op jit(solution)/shard_map/ppermute | solution.py:69
  204.8 5.4 %collective-permute-start.39 = (bf16[1,256]{1,0:T(2,128)(2,1)S(1)}, bf16[1,256]{1,0:T(2,128)(2,1)S(1)}, u32[]{:S(2)}, u32[]{:S(2)}) collective-permute-start(bf16[1,256]{1,0:T(2,128)(2,1)S(1)} %get-tuple-element.37), channel_id=1, source_target_pairs={{0,5},{1,6},{2,7},{3,0},{4,1},{5,2},{6,3},{7,4},{8,13},{9,14},{10,... | collective-permute-start | bytes 1544 | tf_op jit(solution)/shard_map/ppermute | solution.py:69
  208.6 3.6 %collective-permute-start.40 = (bf16[1,256]{1,0:T(2,128)(2,1)S(1)}, bf16[1,256]{1,0:T(2,128)(2,1)S(1)}, u32[]{:S(2)}, u32[]{:S(2)}) collective-permute-start(bf16[1,256]{1,0:T(2,128)(2,1)S(1)} %get-tuple-element.36), channel_id=1, source_target_pairs={{0,6},{1,7},{2,0},{3,1},{4,2},{5,3},{6,4},{7,5},{8,14},{9,15},{10,... | collective-permute-start | bytes 1544 | tf_op jit(solution)/shard_map/ppermute | solution.py:69
  209.6 3.6 %collective-permute-start.41 = (bf16[1,256]{1,0:T(2,128)(2,1)S(1)}, bf16[1,256]{1,0:T(2,128)(2,1)S(1)}, u32[]{:S(2)}, u32[]{:S(2)}) collective-permute-start(bf16[1,256]{1,0:T(2,128)(2,1)S(1)} %get-tuple-element.35), channel_id=1, source_target_pairs={{0,7},{1,0},{2,1},{3,2},{4,3},{5,4},{6,5},{7,6},{8,15},{9,8},{10,9... | collective-permute-start | bytes 1544 | tf_op jit(solution)/shard_map/ppermute | solution.py:69
  214.5 8.2 %collective-permute-start.42 = (f32[1,4096]{1,0:T(1,128)S(1)}, f32[1,4096]{1,0:T(1,128)S(1)}, u32[]{:S(2)}, u32[]{:S(2)}) collective-permute-start(f32[1,4096]{1,0:T(1,128)S(1)} %get-tuple-element.33), channel_id=1, source_target_pairs={{0,1},{1,2},{2,3},{3,4},{4,5},{5,6},{6,7},{7,0},{8,9},{9,10},{10,1... | collective-permute-start | bytes 49160 | tf_op jit(solution)/shard_map/ppermute | solution.py:69
  215.8 7.7 %collective-permute-start.43 = (f32[1,4096]{1,0:T(1,128)S(1)}, f32[1,4096]{1,0:T(1,128)S(1)}, u32[]{:S(2)}, u32[]{:S(2)}) collective-permute-start(f32[1,4096]{1,0:T(1,128)S(1)} %get-tuple-element.32), channel_id=1, source_target_pairs={{0,2},{1,3},{2,4},{3,5},{4,6},{5,7},{6,0},{7,1},{8,10},{9,11},{10,... | collective-permute-start | bytes 49160 | tf_op jit(solution)/shard_map/ppermute | solution.py:69
  216.5 8.2 %collective-permute-start.44 = (f32[1,4096]{1,0:T(1,128)S(1)}, f32[1,4096]{1,0:T(1,128)S(1)}, u32[]{:S(2)}, u32[]{:S(2)}) collective-permute-start(f32[1,4096]{1,0:T(1,128)S(1)} %get-tuple-element.31), channel_id=1, source_target_pairs={{0,3},{1,4},{2,5},{3,6},{4,7},{5,0},{6,1},{7,2},{8,11},{9,12},{10,... | collective-permute-start | bytes 49160 | tf_op jit(solution)/shard_map/ppermute | solution.py:69
  218.4 6.3 %collective-permute-start.45 = (f32[1,4096]{1,0:T(1,128)S(1)}, f32[1,4096]{1,0:T(1,128)S(1)}, u32[]{:S(2)}, u32[]{:S(2)}) collective-permute-start(f32[1,4096]{1,0:T(1,128)S(1)} %get-tuple-element.30), channel_id=1, source_target_pairs={{0,4},{1,5},{2,6},{3,7},{4,0},{5,1},{6,2},{7,3},{8,12},{9,13},{10,... | collective-permute-start | bytes 49160 | tf_op jit(solution)/shard_map/ppermute | solution.py:69
  220.8 4.6 %collective-permute-start.46 = (f32[1,4096]{1,0:T(1,128)S(1)}, f32[1,4096]{1,0:T(1,128)S(1)}, u32[]{:S(2)}, u32[]{:S(2)}) collective-permute-start(f32[1,4096]{1,0:T(1,128)S(1)} %get-tuple-element.29), channel_id=1, source_target_pairs={{0,5},{1,6},{2,7},{3,0},{4,1},{5,2},{6,3},{7,4},{8,13},{9,14},{10,... | collective-permute-start | bytes 49160 | tf_op jit(solution)/shard_map/ppermute | solution.py:69
  222.7 3.7 %collective-permute-start.47 = (f32[1,4096]{1,0:T(1,128)S(1)}, f32[1,4096]{1,0:T(1,128)S(1)}, u32[]{:S(2)}, u32[]{:S(2)}) collective-permute-start(f32[1,4096]{1,0:T(1,128)S(1)} %get-tuple-element.28), channel_id=1, source_target_pairs={{0,6},{1,7},{2,0},{3,1},{4,2},{5,3},{6,4},{7,5},{8,14},{9,15},{10,... | collective-permute-start | bytes 49160 | tf_op jit(solution)/shard_map/ppermute | solution.py:69
  223.5 3.7 %collective-permute-start.48 = (f32[1,4096]{1,0:T(1,128)S(1)}, f32[1,4096]{1,0:T(1,128)S(1)}, u32[]{:S(2)}, u32[]{:S(2)}) collective-permute-start(f32[1,4096]{1,0:T(1,128)S(1)} %get-tuple-element.27), channel_id=1, source_target_pairs={{0,7},{1,0},{2,1},{3,2},{4,3},{5,4},{6,5},{7,6},{8,15},{9,8},{10,9... | collective-permute-start | bytes 49160 | tf_op jit(solution)/shard_map/ppermute | solution.py:69
  229.6 8.8 %collective-permute-start.49 = (bf16[1,4096]{1,0:T(2,128)(2,1)S(1)}, bf16[1,4096]{1,0:T(2,128)(2,1)S(1)}, u32[]{:S(2)}, u32[]{:S(2)}) collective-permute-start(bf16[1,4096]{1,0:T(2,128)(2,1)S(1)} %multiply_convert_fusion), channel_id=1, source_target_pairs={{0,1},{1,2},{2,3},{3,4},{4,5},{5,6},{6,7},{7,0},{8,9},{9,10},{10,1... | collective-permute-start | bytes 24584 | tf_op jit(solution)/shard_map/ppermute | solution.py:58
  231.3 8.2 %collective-permute-start.50 = (bf16[1,4096]{1,0:T(2,128)(2,1)S(1)}, bf16[1,4096]{1,0:T(2,128)(2,1)S(1)}, u32[]{:S(2)}, u32[]{:S(2)}) collective-permute-start(bf16[1,4096]{1,0:T(2,128)(2,1)S(1)} %multiply_convert_fusion), channel_id=1, source_target_pairs={{0,2},{1,3},{2,4},{3,5},{4,6},{5,7},{6,0},{7,1},{8,10},{9,11},{10,... | collective-permute-start | bytes 24584 | tf_op jit(solution)/shard_map/ppermute | solution.py:58
  233.3 8.1 %collective-permute-start.51 = (bf16[1,4096]{1,0:T(2,128)(2,1)S(1)}, bf16[1,4096]{1,0:T(2,128)(2,1)S(1)}, u32[]{:S(2)}, u32[]{:S(2)}) collective-permute-start(bf16[1,4096]{1,0:T(2,128)(2,1)S(1)} %multiply_convert_fusion), channel_id=1, source_target_pairs={{0,3},{1,4},{2,5},{3,6},{4,7},{5,0},{6,1},{7,2},{8,11},{9,12},{10,... | collective-permute-start | bytes 24584 | tf_op jit(solution)/shard_map/ppermute | solution.py:58
  233.6 7.7 %collective-permute-start.52 = (bf16[1,4096]{1,0:T(2,128)(2,1)S(1)}, bf16[1,4096]{1,0:T(2,128)(2,1)S(1)}, u32[]{:S(2)}, u32[]{:S(2)}) collective-permute-start(bf16[1,4096]{1,0:T(2,128)(2,1)S(1)} %multiply_convert_fusion), channel_id=1, source_target_pairs={{0,4},{1,5},{2,6},{3,7},{4,0},{5,1},{6,2},{7,3},{8,12},{9,13},{10,... | collective-permute-start | bytes 24584 | tf_op jit(solution)/shard_map/ppermute | solution.py:58
  236.2 5.2 %collective-permute-start.53 = (bf16[1,4096]{1,0:T(2,128)(2,1)S(1)}, bf16[1,4096]{1,0:T(2,128)(2,1)S(1)}, u32[]{:S(2)}, u32[]{:S(2)}) collective-permute-start(bf16[1,4096]{1,0:T(2,128)(2,1)S(1)} %multiply_convert_fusion), channel_id=1, source_target_pairs={{0,5},{1,6},{2,7},{3,0},{4,1},{5,2},{6,3},{7,4},{8,13},{9,14},{10,... | collective-permute-start | bytes 24584 | tf_op jit(solution)/shard_map/ppermute | solution.py:58
  238.5 3.7 %collective-permute-start.54 = (bf16[1,4096]{1,0:T(2,128)(2,1)S(1)}, bf16[1,4096]{1,0:T(2,128)(2,1)S(1)}, u32[]{:S(2)}, u32[]{:S(2)}) collective-permute-start(bf16[1,4096]{1,0:T(2,128)(2,1)S(1)} %multiply_convert_fusion), channel_id=1, source_target_pairs={{0,6},{1,7},{2,0},{3,1},{4,2},{5,3},{6,4},{7,5},{8,14},{9,15},{10,... | collective-permute-start | bytes 24584 | tf_op jit(solution)/shard_map/ppermute | solution.py:58
  239.6 3.7 %collective-permute-start.55 = (bf16[1,4096]{1,0:T(2,128)(2,1)S(1)}, bf16[1,4096]{1,0:T(2,128)(2,1)S(1)}, u32[]{:S(2)}, u32[]{:S(2)}) collective-permute-start(bf16[1,4096]{1,0:T(2,128)(2,1)S(1)} %multiply_convert_fusion), channel_id=1, source_target_pairs={{0,7},{1,0},{2,1},{3,2},{4,3},{5,4},{6,5},{7,6},{8,15},{9,8},{10,9... | collective-permute-start | bytes 24584 | tf_op jit(solution)/shard_map/ppermute | solution.py:58
  258.1 6.9 %collective-permute-start.63 = (f32[1,4096]{1,0:T(1,128)S(1)}, f32[1,4096]{1,0:T(1,128)S(1)}, u32[]{:S(2)}, u32[]{:S(2)}) collective-permute-start(f32[1,4096]{1,0:T(1,128)S(1)} %get-tuple-element.20), channel_id=1, source_target_pairs={{0,15},{1,8},{2,9},{3,10},{4,11},{5,12},{6,13},{7,14},{8,23},{9,16... | collective-permute-start | bytes 49160 | tf_op jit(solution)/shard_map/ppermute | solution.py:220
  258.2 10.4 %collective-permute-start.62 = (f32[1,4096]{1,0:T(1,128)S(1)}, f32[1,4096]{1,0:T(1,128)S(1)}, u32[]{:S(2)}, u32[]{:S(2)}) collective-permute-start(f32[1,4096]{1,0:T(1,128)S(1)} %get-tuple-element.21), channel_id=1, source_target_pairs={{0,14},{1,15},{2,8},{3,9},{4,10},{5,11},{6,12},{7,13},{8,22},{9,23... | collective-permute-start | bytes 49160 | tf_op jit(solution)/shard_map/ppermute | solution.py:220
  262.2 6.8 %collective-permute-start.61 = (f32[1,4096]{1,0:T(1,128)S(1)}, f32[1,4096]{1,0:T(1,128)S(1)}, u32[]{:S(2)}, u32[]{:S(2)}) collective-permute-start(f32[1,4096]{1,0:T(1,128)S(1)} %get-tuple-element.22), channel_id=1, source_target_pairs={{0,13},{1,14},{2,15},{3,8},{4,9},{5,10},{6,11},{7,12},{8,21},{9,22... | collective-permute-start | bytes 49160 | tf_op jit(solution)/shard_map/ppermute | solution.py:220
  262.5 7.7 %collective-permute-start.60 = (f32[1,4096]{1,0:T(1,128)S(1)}, f32[1,4096]{1,0:T(1,128)S(1)}, u32[]{:S(2)}, u32[]{:S(2)}) collective-permute-start(f32[1,4096]{1,0:T(1,128)S(1)} %get-tuple-element.23), channel_id=1, source_target_pairs={{0,12},{1,13},{2,14},{3,15},{4,8},{5,9},{6,10},{7,11},{8,20},{9,21... | collective-permute-start | bytes 49160 | tf_op jit(solution)/shard_map/ppermute | solution.py:220
  264.8 6.2 %collective-permute-start.59 = (f32[1,4096]{1,0:T(1,128)S(1)}, f32[1,4096]{1,0:T(1,128)S(1)}, u32[]{:S(2)}, u32[]{:S(2)}) collective-permute-start(f32[1,4096]{1,0:T(1,128)S(1)} %get-tuple-element.24), channel_id=1, source_target_pairs={{0,11},{1,12},{2,13},{3,14},{4,15},{5,8},{6,9},{7,10},{8,19},{9,20... | collective-permute-start | bytes 49160 | tf_op jit(solution)/shard_map/ppermute | solution.py:220
  265.0 8.4 %collective-permute-start.58 = (f32[1,4096]{1,0:T(1,128)S(1)}, f32[1,4096]{1,0:T(1,128)S(1)}, u32[]{:S(2)}, u32[]{:S(2)}) collective-permute-start(f32[1,4096]{1,0:T(1,128)S(1)} %get-tuple-element.25), channel_id=1, source_target_pairs={{0,10},{1,11},{2,12},{3,13},{4,14},{5,15},{6,8},{7,9},{8,18},{9,19... | collective-permute-start | bytes 49160 | tf_op jit(solution)/shard_map/ppermute | solution.py:220
  268.6 4.8 %collective-permute-start.56 = (f32[1,4096]{1,0:T(1,128)S(1)}, f32[1,4096]{1,0:T(1,128)S(1)}, u32[]{:S(2)}, u32[]{:S(2)}) collective-permute-start(f32[1,4096]{1,0:T(1,128)S(1)} %get-tuple-element.26), channel_id=1, source_target_pairs={{0,8},{1,9},{2,10},{3,11},{4,12},{5,13},{6,14},{7,15},{8,16},{9,17... | collective-permute-start | bytes 49160 | tf_op jit(solution)/shard_map/ppermute | solution.py:220
  269.0 6.8 %collective-permute-start.57 = (f32[1,4096]{1,0:T(1,128)S(1)}, f32[1,4096]{1,0:T(1,128)S(1)}, u32[]{:S(2)}, u32[]{:S(2)}) collective-permute-start(f32[1,4096]{1,0:T(1,128)S(1)} %get-tuple-element.19), channel_id=1, source_target_pairs={{0,9},{1,10},{2,11},{3,12},{4,13},{5,14},{6,15},{7,8},{8,17},{9,18... | collective-permute-start | bytes 49160 | tf_op jit(solution)/shard_map/ppermute | solution.py:220
  (16 other events, 568.9 us)

commit v2 on v1

v2 whole, which is shorter than its diff:
```python
import math

import jax
import jax.numpy as jnp
from jax import lax
from jax.sharding import PartitionSpec as P

HEADS = 16


epsilon = 1e-05

DIRECT_LIMIT = 8


def shift_pairs(count, steps):
    return [(source, (source + steps) % count) for source in range(count)]


def by_rows(left, weight_rows):
    return lax.dot_general(
        left, weight_rows, (((1,), (1,)), ((), ())), preferred_element_type=jnp.float32
    )


def head_norm(values, gain_row):
    shaped = values.astype(jnp.float32).reshape(values.shape[0], -1, gain_row.shape[0])
    scaled = (
        shaped * lax.rsqrt(jnp.mean(shaped * shaped, axis=-1, keepdims=True) + epsilon) * gain_row
    )
    return scaled.reshape(values.shape[0], -1)


def rms_norm(values, gain_row):
    return (
        values * lax.rsqrt(jnp.mean(values * values, axis=-1, keepdims=True) + epsilon) * gain_row
    )


def to_source_order(slots, count, me):
    return jnp.take(slots, (me - jnp.arange(count, dtype=jnp.int32)) % count, axis=0)


def xor_pairs(count, bit):
    return [(source, source ^ (1 << bit)) for source in range(count)]


def direct_ok(count):
    return count <= DIRECT_LIMIT and count & (count - 1) == 0


def site_exchange(by_target, count, me):
    if not direct_ok(count):
        return lax.all_to_all(by_target, "site", split_axis=0, concat_axis=0, tiled=True)
    slots = [lax.dynamic_index_in_dim(by_target, me, 0, keepdims=False)]
    for steps in range(1, count):
        piece = lax.dynamic_index_in_dim(by_target, (me + steps) % count, 0, keepdims=False)
        slots.append(lax.ppermute(piece, "site", shift_pairs(count, steps)))
    return to_source_order(jnp.stack(slots), count, me)


def halving_exchange(by_target, count, me):
    if not direct_ok(count):
        return lax.all_to_all(by_target, "site", split_axis=0, concat_axis=0, tiled=True)
    bits = count.bit_length() - 1
    rest = by_target.shape[1:]
    state = by_target.reshape((2,) * bits + rest)
    for bit in range(bits):
        axis = bits - 1 - bit
        mine = (me >> bit) & 1
        keep = lax.dynamic_index_in_dim(state, mine, axis, keepdims=True)
        send = lax.dynamic_index_in_dim(state, 1 - mine, axis, keepdims=True)
        recv = lax.ppermute(send, "site", xor_pairs(count, bit))
        state = jnp.where(
            mine == 0,
            jnp.concatenate([keep, recv], axis),
            jnp.concatenate([recv, keep], axis),
        )
    return state.reshape((count,) + rest)


def doubling_gather(value, count, me):
    if not direct_ok(count):
        return lax.all_gather(value, "site", axis=0, tiled=False)
    bits = count.bit_length() - 1
    state = value[None]
    for bit in range(bits):
        recv = lax.ppermute(state, "site", xor_pairs(count, bit))
        mine = (me >> bit) & 1
        state = jnp.where(
            mine == 0, jnp.concatenate([state, recv], 0), jnp.concatenate([recv, state], 0)
        )
    return state


def halving_sum(parts, count, me):
    if not direct_ok(count):
        return lax.psum_scatter(parts, "site", scatter_dimension=0, tiled=True)[0]
    bits = count.bit_length() - 1
    rest = parts.shape[1:]
    state = parts.reshape((2,) * bits + rest)
    for bit in range(bits):
        axis = bits - 1 - bit
        mine = (me >> bit) & 1
        keep = lax.dynamic_index_in_dim(state, mine, axis, keepdims=True)
        send = lax.dynamic_index_in_dim(state, 1 - mine, axis, keepdims=True)
        state = keep + lax.ppermute(send, "site", xor_pairs(count, bit))
    return state.reshape(rest)


def ring_gather(value, count, me):
    if not direct_ok(count):
        return lax.all_gather(value, "site", axis=0, tiled=False), jnp.arange(count, dtype=jnp.int32)
    order = list(range(0, count, 2)) + [i for i in range(count - 1, -1, -1) if i % 2 == 1]
    place = [0] * count
    for position, device in enumerate(order):
        place[device] = position
    forward = [(order[p], order[(p + 1) % count]) for p in range(count)]
    backward = [(order[p], order[(p - 1) % count]) for p in range(count)]
    forward_steps = count // 2
    backward_steps = count - 1 - forward_steps
    slots = [value]
    moving = value
    for _ in range(forward_steps):
        moving = lax.ppermute(moving, "site", forward)
        slots.append(moving)
    moving = value
    for _ in range(backward_steps):
        moving = lax.ppermute(moving, "site", backward)
        slots.append(moving)
    offsets = [0] + [-s for s in range(1, forward_steps + 1)] + list(range(1, backward_steps + 1))
    my_place = jnp.array(place, dtype=jnp.int32)[me]
    source_of_slot = jnp.array(order, dtype=jnp.int32)[
        (my_place + jnp.array(offsets, dtype=jnp.int32)) % count
    ]
    return jnp.stack(slots), source_of_slot


def shards(
    acts,
    patches,
    site_tiles,
    site_count,
    q_weight,
    q_gain,
    k_gain,
    tile_in,
    tile_out,
    out_weight,
    ffn_gain,
    gate_weight,
    up_weight,
    down_weight,
):
    group_size = lax.axis_size("site")
    section_count = lax.axis_size("section")
    my_index = lax.axis_index("site")
    sites_here = acts.shape[1]
    list_width = site_tiles.shape[1]
    tiles_here = patches.shape[1]
    head_size = q_gain.shape[1]
    capacity = max(2, 5 * sites_here * list_width // (4 * group_size))
    entries = sites_here * list_width
    current = acts[0]
    model_width = current.shape[-1]
    row_width = patches.shape[-1]

    width_in = tile_in.shape[-1]
    in_rows = tile_in.shape[1] * width_in // tile_out.shape[-1]
    packed_weights = jnp.concatenate(
        [tile_in[0].reshape(in_rows, tile_out.shape[-1]), tile_out[0]], axis=0
    )
    weight_slots, source_of_slot = ring_gather(packed_weights, group_size, my_index)
    weight_in = weight_slots[:, :in_rows].reshape(-1, width_in)
    weight_out = weight_slots[:, in_rows:].reshape(-1, weight_slots.shape[-1])

    slot_index = jnp.arange(list_width, dtype=jnp.int32)
    live_all = (slot_index[None, :] < site_count[:, None]).reshape(group_size, entries)
    owner_all = (site_tiles // tiles_here).reshape(group_size, entries)
    local_all = (site_tiles % tiles_here).reshape(group_size, entries)
    mine_mask = jnp.logical_and(live_all, owner_all == my_index)
    slot_rank = jnp.cumsum(mine_mask.astype(jnp.int32), axis=1) - 1
    picks = jnp.logical_and(
        mine_mask[:, :, None],
        slot_rank[:, :, None] == jnp.arange(capacity, dtype=jnp.int32)[None, None, :],
    )
    send_index = jnp.sum(jnp.where(picks, local_all[:, :, None], 0), axis=1)
    send_rows = patches[0][send_index.reshape(-1)].reshape(group_size, capacity, row_width)
    act_rows = sites_here * model_width // row_width
    packed = model_width % row_width == 0
    if packed:
        act_block = jnp.broadcast_to(
            current.reshape(1, act_rows, row_width), (group_size, act_rows, row_width)
        )
        arrived = site_exchange(
            jnp.concatenate([send_rows, act_block], axis=1), group_size, my_index
        )
        everyone = arrived[:, capacity:].reshape(-1, model_width)
        arrived = arrived[:, :capacity]
    else:
        arrived = site_exchange(send_rows, group_size, my_index)
        everyone = doubling_gather(current, group_size, my_index).reshape(-1, model_width)

    my_tiles = lax.dynamic_slice_in_dim(site_tiles, my_index * sites_here, sites_here, 0)
    my_count = lax.dynamic_slice_in_dim(site_count, my_index * sites_here, sites_here, 0)
    my_live = slot_index[None, :] < my_count[:, None]
    my_owner = (my_tiles // tiles_here).reshape(-1)
    one_hot = jnp.logical_and(
        my_owner[:, None] == jnp.arange(group_size, dtype=jnp.int32)[None, :],
        my_live.reshape(-1)[:, None],
    ).astype(jnp.int32)
    my_rank = jnp.sum(jnp.cumsum(one_hot, axis=0) * one_hot, axis=1) - 1
    fetch_index = jnp.where(my_live.reshape(-1), my_owner * capacity + my_rank, 0)
    pair_rows = arrived.reshape(group_size * capacity, row_width)[fetch_index]

    rows_in = pair_rows.reshape(entries, group_size, -1)
    rows_in = jnp.take(rows_in, source_of_slot, axis=1).reshape(entries, -1)
    hidden = jax.nn.gelu(
        jnp.dot(rows_in, weight_in, preferred_element_type=jnp.float32), approximate=True
    ).astype(jnp.bfloat16)
    hidden = jnp.take(hidden.reshape(entries, group_size, -1), source_of_slot, axis=1)
    keyval = jnp.dot(hidden.reshape(entries, -1), weight_out, preferred_element_type=jnp.float32)
    half_width = keyval.shape[1] // 2
    normed_keys = head_norm(keyval[:, :half_width], k_gain[0])
    pair_kv = jnp.concatenate([normed_keys, keyval[:, half_width:]], axis=1).astype(jnp.bfloat16)
    pair_kv = pair_kv.reshape(sites_here, list_width, 2, HEADS, head_size)

    q_part = by_rows(everyone, q_weight[0]).astype(jnp.bfloat16)
    q_blocks = halving_exchange(
        q_part.reshape(group_size, sites_here, -1), group_size, my_index
    )
    my_queries = jnp.moveaxis(q_blocks, 0, 1).reshape(sites_here, -1)
    queries = head_norm(my_queries, q_gain[0]).astype(jnp.bfloat16)
    query_heads = queries.reshape(sites_here, HEADS, head_size)
    scores = jnp.einsum(
        "nhd,nlhd->nhl", query_heads, pair_kv[:, :, 0], preferred_element_type=jnp.float32
    ) / math.sqrt(head_size)
    exponents = jnp.exp(scores) * my_live.astype(jnp.float32)[:, None, :]
    weights = (exponents / jnp.sum(exponents, axis=-1, keepdims=True)).astype(jnp.bfloat16)
    combined = jnp.einsum(
        "nhl,nlhd->nhd", weights, pair_kv[:, :, 1], preferred_element_type=jnp.float32
    )
    combined = combined.reshape(sites_here, -1).astype(jnp.bfloat16)
    column_blocks = jnp.moveaxis(combined.reshape(sites_here, group_size, -1), 1, 0)
    columns = halving_exchange(column_blocks, group_size, my_index).reshape(
        group_size * sites_here, -1
    )
    attn_part = jnp.dot(columns, out_weight[0], preferred_element_type=jnp.float32)
    attn_sum = halving_sum(attn_part.reshape(group_size, sites_here, -1), group_size, my_index)
    residual = current.astype(jnp.float32) + attn_sum
    normed = rms_norm(residual, ffn_gain[0]).astype(jnp.bfloat16)
    normed_rows = doubling_gather(normed, group_size, my_index).reshape(-1, model_width)
    gate_sum = by_rows(normed_rows, gate_weight[0])
    up_sum = by_rows(normed_rows, up_weight[0])
    hidden_ffn = (jax.nn.silu(gate_sum) * up_sum).astype(jnp.bfloat16)
    down_part = jnp.dot(hidden_ffn, down_weight[0], preferred_element_type=jnp.float32)
    down_sum = halving_sum(down_part.reshape(group_size, sites_here, -1), group_size, my_index)
    output_rows = (residual + down_sum).astype(jnp.bfloat16)
    return lax.ppermute(output_rows[None], "section", shift_pairs(section_count, 1))


def solution(mesh):
    return jax.shard_map(
        shards,
        mesh=mesh,
        in_specs=(
            P("section", "site", None),
            P("section", "site", None),
            P(),
            P(),
            P("section", "site", None),
            P("section", None),
            P("section", None),
            P("section", "site", None),
            P("section", "site", None),
            P("section", "site", None),
            P("section", None),
            P("section", "site", None),
            P("section", "site", None),
            P("section", "site", None),
        ),
        out_specs=P("section", "site", None),
        check_vma=False,
    )
```

time: 278 us -> 202 us (0.73)
  starting transfers between devices: 90.5 us -> 56 us
  local copies, waits for them, and re-layouts: 61.9 us -> 36.8 us
  waiting for transfers between devices: 69.9 us -> 63.6 us
  other arithmetic: 25 us -> 20.3 us
  between operations: 5.92 us -> 1.36 us
    ppermute x28 -> x7, waiting for transfers between devices: 40.8 us -> 1.16 us  [site_exchange(): slots.append(lax.ppermute(piece, 'site', shift_pairs(count, steps)))]
    ppermute x36 -> x23, waiting for transfers between devices: 29.1 us -> 62.4 us  [the longest x4 32.1 us: ring_gather(): moving = lax.ppermute(moving, 'site', forward)]
    ppermute x28 -> x7, starting transfers between devices: 39.4 us -> 14.4 us  [site_exchange(): slots.append(lax.ppermute(piece, 'site', shift_pairs(count, steps)))]
    ppermute x36 -> x23, starting transfers between devices: 51.2 us -> 41.6 us  [the longest x6 14.2 us: halving_sum(): state = keep + lax.ppermute(send, 'site', xor_pairs(count, bit))]
    gather x4 -> x5, local copies, waits for them, and re-layouts: 12.3 us -> 5.12 us  [the longest x1 2.09 us: shards(): patches[0][send_index.reshape(-1)].reshape(group_size, capacity, row_width)]
    unnamed x54 -> x39, local copies, waits for them, and re-layouts: 24.6 us -> 18.5 us
    dot_general x2 -> x3, matrix products: 7.31 us -> 12.4 us  [by_rows(): lax.dot_general(left, weight_rows, (((1,), (1,)), ((), ())), preferred_el...]
    select_n x6 -> x13, other arithmetic: 7.49 us -> 2.51 us  [the longest x1 1.36 us: shards(): pair_rows = arrived.reshape(group_size * capacity, row_width)[fetch_index]]
  transfers between devices with their start and end apart: 64 -> 30, of which waited for: 25 -> 20; matrix products, arithmetic and copies ran while one was open for 21% -> 20% of each run, Pallas kernels for 0% -> 0%
where the time goes in v2:
time: 202 us; the launch traced here: 201 us
  waiting for transfers between devices  63.6 us (31%)
  starting transfers between devices  56 us (28%)
  local copies, waits for them, and re-layouts  36.8 us (18%)
  matrix products  23.2 us (11%)
  other arithmetic  20.3 us (10%)
    ppermute x4, waiting for transfers between devices, ring_gather(): moving = lax.ppermute(moving, 'site', forward)  32.1 us
    unnamed x39, local copies, waits for them, and re-layouts  18.5 us
    ppermute x7, starting transfers between devices, site_exchange(): slots.append(lax.ppermute(piece, 'site', shift_pairs(count, steps)))  14.4 us
    ppermute x6, starting transfers between devices, halving_sum(): state = keep + lax.ppermute(send, 'site', xor_pairs(count, bit))  14.2 us
    dot_general x3, matrix products, by_rows(): lax.dot_general(left, weight_rows, (((1,), (1,)), ((), ())), preferred_el...  12.4 us
    ppermute x6, waiting for transfers between devices, halving_sum(): state = keep + lax.ppermute(send, 'site', xor_pairs(count, bit))  11.9 us
    ppermute x6, starting transfers between devices, halving_exchange(): recv = lax.ppermute(send, 'site', xor_pairs(count, bit))  11.2 us
    ppermute x6, waiting for transfers between devices, halving_exchange(): recv = lax.ppermute(send, 'site', xor_pairs(count, bit))  10.2 us
  transfers between devices with their start and end apart: 30, of which 20 were waited for; matrix products, arithmetic and copies ran while one was open for 20% of the time, Pallas kernels for 0%

profile of v2, /device:TPU:0, one launch (start us, length us, event | category | flops | bytes accessed | tf_op | source)
XLA Modules:
  0.0 201.3 jit_solution(4802078827464618316)
XLA Ops:
  1.1 1.9 pad_maximum_fusion
  3.1 3.0 %collective-permute-start.10 = (bf16[80,4096]{1,0:T(8,128)(2,1)}, bf16[80,4096]{1,0:T(8,128)(2,1)}, u32[]{:S(2)}, u32[]{:S(2)}) collective-permute-start(bf16[80,4096]{1,0:T(8,128)(2,1)} %pad_maximum_fusion), channel_id=1, source_target_pairs={{0,2},{2,4},{4,6},{6,7},{7,5},{5,3},{3,1},{1,0},{8,10},{10,12},{12... | collective-permute-start | bytes 1966088 | tf_op jit(solution)/shard_map/ppermute | solution.py:125
  8.3 1.2 dynamic_slice.127
  12.9 2.1 %gather_fusion = bf16[320,1024]{1,0:T(8,128)(2,1)S(1)} fusion(bf16[256,1024]{1,0:T(8,128)(2,1)S(1)} %bitcast.207, s32[1024]{0:T(1024)S(1)} %pad_clamp_fusion.4), kind=kCustom, calls=%fused_computation | custom fusion | bytes 1312000 | tf_op jit(solution)/shard_map/gather | solution.py:188
  15.8 1.9 collective-permute-start
  17.7 1.6 collective-permute-start.1
  19.3 2.6 %collective-permute-start.2 = (bf16[44,1024]{1,0:T(8,128)(2,1)S(1)}, bf16[44,1024]{1,0:T(8,128)(2,1)}, u32[]{:S(2)}, u32[]{:S(2)}) collective-permute-start(bf16[44,1024]{1,0:T(8,128)(2,1)S(1)} %get-tuple-element.15), channel_id=1, source_target_pairs={{0,3},{1,4},{2,5},{3,6},{4,7},{5,0},{6,1},{7,2},{8,11},{9,12},{10,... | collective-permute-start | bytes 270344 | tf_op jit(solution)/shard_map/ppermute | solution.py:58
  21.9 1.9 bitcast_dynamic-update-slice_fusion.7
  26.6 1.4 compare_select_fusion.1
  28.7 1.3 collective-permute-start.3
  30.0 1.5 bitcast_dynamic-update-slice_fusion.14
  31.5 2.6 %collective-permute-start.4 = (bf16[44,1024]{1,0:T(8,128)(2,1)}, bf16[44,1024]{1,0:T(8,128)(2,1)S(1)}, u32[]{:S(2)}, u32[]{:S(2)}) collective-permute-start(bf16[44,1024]{1,0:T(8,128)(2,1)} %get-tuple-element.18), channel_id=1, source_target_pairs={{0,5},{1,6},{2,7},{3,0},{4,1},{5,2},{6,3},{7,4},{8,13},{9,14},{10,... | collective-permute-start | bytes 270344 | tf_op jit(solution)/shard_map/ppermute | solution.py:58
  34.1 1.5 bitcast_dynamic-update-slice_fusion.13
  35.7 2.9 %collective-permute-start.5 = (bf16[44,1024]{1,0:T(8,128)(2,1)S(1)}, bf16[44,1024]{1,0:T(8,128)(2,1)S(1)}, u32[]{:S(2)}, u32[]{:S(2)}) collective-permute-start(bf16[44,1024]{1,0:T(8,128)(2,1)S(1)} %get-tuple-element.17), channel_id=1, source_target_pairs={{0,6},{1,7},{2,0},{3,1},{4,2},{5,3},{6,4},{7,5},{8,14},{9,15},{10,... | collective-permute-start | bytes 270344 | tf_op jit(solution)/shard_map/ppermute | solution.py:58
  38.5 1.5 bitcast_dynamic-update-slice_fusion.12
  40.1 1.5 collective-permute-start.6
  45.3 1.7 gather_fusion.1
  48.2 2.2 %fusion.19 = bf16[8,256]{1,0:T(8,128)(2,1)S(1)} fusion(bf16[8,4096]{1,0:T(8,128)(2,1)S(1)} %bitcast.218, bf16[1,256,4096]{2,1,0:T(8,128)(2,1)} %param.21), kind=kOutput, calls=%fused_computation.34 | convolution fusion | flops 16779264 | bytes 2166784 | tf_op jit(solution)/shard_map/dot_general | solution.py:21
  51.7 1.2 gather_fusion.3
  52.9 1.2 collective-permute-done.7
  55.0 2.8 %collective-permute-done.8 = bf16[2,1,2,1,256]{4,2,1,3,0:T(2,128)(2,1)S(1)} collective-permute-done((bf16[2,1,2,1,256]{4,2,1,3,0:T(2,128)(2,1)S(1)}, bf16[2,1,2,1,256]{4,2,1,3,0:T(2,128)(2,1)S(1)}, u32[]{:S(2)}, u32[]{:S(2)}) %collective-permute-start.8) | collective-permute-done | bytes 2080 | tf_op jit(solution)/shard_map/ppermute | solution.py:73
  57.9 2.1 %collective-permute-start.9 = (bf16[1,2,2,1,256]{4,2,1,3,0:T(2,128)(2,1)S(1)}, bf16[1,2,2,1,256]{4,2,1,3,0:T(2,128)(2,1)S(1)}, u32[]{:S(2)}, u32[]{:S(2)}) collective-permute-start(bf16[1,2,2,1,256]{4,2,1,3,0:T(2,128)(2,1)S(1)} %get-tuple-element.26), channel_id=1, source_target_pairs={{0,4},{1,5},{2,6},{3,7},{4,0},{5,1},{6,2},{7,3},{8,12},{9,13},{10,... | collective-permute-start | bytes 6152 | tf_op jit(solution)/shard_map/ppermute | solution.py:73
  61.1 1.4 collective-permute-done.9
  64.8 2.0 bitcast_dynamic-update-slice_fusion.6
  66.8 11.2 %collective-permute-done.11 = bf16[80,4096]{1,0:T(8,128)(2,1)S(1)} collective-permute-done((bf16[80,4096]{1,0:T(8,128)(2,1)}, bf16[80,4096]{1,0:T(8,128)(2,1)S(1)}, u32[]{:S(2)}, u32[]{:S(2)}) %collective-permute-start.11) | collective-permute-done | bytes 655392 | tf_op jit(solution)/shard_map/ppermute | solution.py:125
  80.9 13.1 %collective-permute-done.12 = bf16[80,4096]{1,0:T(8,128)(2,1)S(1)} collective-permute-done((bf16[80,4096]{1,0:T(8,128)(2,1)S(1)}, bf16[80,4096]{1,0:T(8,128)(2,1)S(1)}, u32[]{:S(2)}, u32[]{:S(2)}) %collective-permute-start.12) | collective-permute-done | bytes 655392 | tf_op jit(solution)/shard_map/ppermute | solution.py:125
  94.0 1.9 collective-permute-start.13
  96.9 7.7 %collective-permute-done.13 = bf16[80,4096]{1,0:T(8,128)(2,1)S(1)} collective-permute-done((bf16[80,4096]{1,0:T(8,128)(2,1)S(1)}, bf16[80,4096]{1,0:T(8,128)(2,1)S(1)}, u32[]{:S(2)}, u32[]{:S(2)}) %collective-permute-start.13) | collective-permute-done | bytes 655392 | tf_op jit(solution)/shard_map/ppermute | solution.py:125
  105.5 2.0 bitcast_dynamic-update-slice_fusion.2
  109.3 1.3 slice.65
  110.6 1.3 reshape.989
  111.9 1.9 fusion.33
  114.5 3.6 %convolution_bitcast_fusion = f32[256,4096]{1,0:T(8,128)S(1)} fusion(bf16[8,80,4096]{2,1,0:T(8,128)(2,1)} %bitcast_dynamic-update-slice_fusion, bf16[8,256,64]{1,2,0:T(8,128)(2,1)S(1)} %gather_fusion.5, pred[8]{0:T(512)(128)(4,1)S(1)} %compare_and_fusion), kind=kOutput, calls=%fused_computation.12 | convolution fusion | flops 1073872896 | bytes 8650760 | tf_op jit(solution)/shard_map/dot_general | solution.py:222
  118.4 2.1 %copy.57 = f32[32,8,16,128]{3,2,1,0:T(8,128)} copy(f32[32,8,16,128]{3,1,2,0:T(8,128)S(1)} %multiply_bitcast_fusion) | data formatting | bytes 4194304
  120.8 2.2 %reduce_sum.57 = f32[256,16]{1,0:T(8,128)S(1)} reduce(f32[256,16,128]{2,1,0:T(8,128)} %bitcast.211, f32[]{:T(128)} %constant.267.clone.1), dimensions={2}, to_apply=%region_7.8 | reduce | flops 520192 | bytes 2113540 | tf_op jit(solution)/shard_map/reduce_sum | solution.py:29
  123.8 2.4 %fusion.8 = bf16[256,2048]{1,0:T(8,128)(2,1)S(1)} fusion(f32[32,8,16,128]{3,2,1,0:T(8,128)S(1)} %bitcast.209, f32[256,4096]{1,0:T(8,128)} %copy-done.3, f32[2048]{0:T(1024)S(1)} %broadcast_bitcast_fusion), kind=kLoop, calls=%fused_computation.24 | loop fusion | flops 1572864 | bytes 5251072 | tf_op jit(solution)/shard_map/convert.3
  128.2 3.4 %collective-permute-start.17 = (bf16[2,2,1,1,256]{4,2,1,3,0:T(2,128)(2,1)S(1)}, bf16[2,2,1,1,256]{4,2,1,3,0:T(2,128)(2,1)S(1)}, u32[]{:S(2)}, u32[]{:S(2)}) collective-permute-start(bf16[2,2,1,1,256]{4,2,1,3,0:T(2,128)(2,1)S(1)} %get-tuple-element.24), channel_id=1, source_target_pairs={{0,1},{1,0},{2,3},{3,2},{4,5},{5,4},{6,7},{7,6},{8,9},{9,8},{10,11... | collective-permute-start | bytes 6152 | tf_op jit(solution)/shard_map/ppermute | solution.py:73
  131.7 1.6 collective-permute-done.17
  133.3 2.1 %collective-permute-start.18 = (bf16[2,1,2,1,256]{4,2,1,3,0:T(2,128)(2,1)S(1)}, bf16[2,1,2,1,256]{4,2,1,3,0:T(2,128)(2,1)S(1)}, u32[]{:S(2)}, u32[]{:S(2)}) collective-permute-start(bf16[2,1,2,1,256]{4,2,1,3,0:T(2,128)(2,1)S(1)} %get-tuple-element.22), channel_id=1, source_target_pairs={{0,2},{1,3},{2,0},{3,1},{4,6},{5,7},{6,4},{7,5},{8,10},{9,11},{10,... | collective-permute-start | bytes 6152 | tf_op jit(solution)/shard_map/ppermute | solution.py:73
  135.4 1.6 collective-permute-done.18
  137.0 3.4 %collective-permute-start.19 = (bf16[1,2,2,1,256]{4,2,1,3,0:T(2,128)(2,1)S(1)}, bf16[1,2,2,1,256]{4,2,1,3,0:T(2,128)(2,1)S(1)}, u32[]{:S(2)}, u32[]{:S(2)}) collective-permute-start(bf16[1,2,2,1,256]{4,2,1,3,0:T(2,128)(2,1)S(1)} %get-tuple-element.20), channel_id=1, source_target_pairs={{0,4},{1,5},{2,6},{3,7},{4,0},{5,1},{6,2},{7,3},{8,12},{9,13},{10,... | collective-permute-start | bytes 6152 | tf_op jit(solution)/shard_map/ppermute | solution.py:73
  140.4 1.6 collective-permute-done.19
  142.4 2.1 %collective-permute-start.20 = (f32[2,2,1,1,4096]{4,2,3,1,0:T(1,128)S(1)}, f32[2,2,1,1,4096]{4,2,3,1,0:T(1,128)S(1)}, u32[]{:S(2)}, u32[]{:S(2)}) collective-permute-start(f32[2,2,1,1,4096]{4,2,3,1,0:T(1,128)S(1)} %dynamic-slice_bitcast_fusion.1), channel_id=1, source_target_pairs={{0,1},{1,0},{2,3},{3,2},{4,5},{5,4},{6,7},{7,6},{8,9},{9,8},{10,11... | collective-permute-start | bytes 196616 | tf_op jit(solution)/shard_map/ppermute | solution.py:107
  144.5 2.2 %collective-permute-done.20 = f32[2,2,1,1,4096]{4,2,3,1,0:T(1,128)S(1)} collective-permute-done((f32[2,2,1,1,4096]{4,2,3,1,0:T(1,128)S(1)}, f32[2,2,1,1,4096]{4,2,3,1,0:T(1,128)S(1)}, u32[]{:S(2)}, u32[]{:S(2)}) %collective-permute-start.20) | collective-permute-done | bytes 65568 | tf_op jit(solution)/shard_map/ppermute | solution.py:107
  146.9 2.0 collective-permute-start.21
  148.9 2.0 collective-permute-done.21
  150.9 3.0 %collective-permute-start.22 = (f32[1,1,1,1,4096]{4,2,3,1,0:T(1,128)S(1)}, f32[1,1,1,1,4096]{4,2,3,1,0:T(1,128)S(1)}, u32[]{:S(2)}, u32[]{:S(2)}) collective-permute-start(f32[1,1,1,1,4096]{4,2,3,1,0:T(1,128)S(1)} %constant_dynamic-slice_fusion.2), channel_id=1, source_target_pairs={{0,4},{1,5},{2,6},{3,7},{4,0},{5,1},{6,2},{7,3},{8,12},{9,13},{10,... | collective-permute-start | bytes 49160 | tf_op jit(solution)/shard_map/ppermute | solution.py:107
  153.9 1.7 collective-permute-done.22
  157.0 2.1 %collective-permute-start.23 = (bf16[1,1,4096]{2,0,1:T(2,128)(2,1)S(1)}, bf16[1,1,4096]{2,0,1:T(2,128)(2,1)S(1)}, u32[]{:S(2)}, u32[]{:S(2)}) collective-permute-start(bf16[1,1,4096]{2,0,1:T(2,128)(2,1)S(1)} %bitcast.219), channel_id=1, source_target_pairs={{0,1},{1,0},{2,3},{3,2},{4,5},{5,4},{6,7},{7,6},{8,9},{9,8},{10,11... | collective-permute-start | bytes 24584 | tf_op jit(solution)/shard_map/ppermute | solution.py:88
  159.1 1.7 collective-permute-done.23
  160.9 2.0 collective-permute-start.24
  163.1 1.6 collective-permute-done.24
  164.8 3.0 %collective-permute-start.25 = (bf16[4,1,4096]{2,0,1:T(4,128)(2,1)S(1)}, bf16[4,1,4096]{2,0,1:T(4,128)(2,1)S(1)}, u32[]{:S(2)}, u32[]{:S(2)}) collective-permute-start(bf16[4,1,4096]{2,0,1:T(4,128)(2,1)S(1)} %maximum_select_fusion.2), channel_id=1, source_target_pairs={{0,4},{1,5},{2,6},{3,7},{4,0},{5,1},{6,2},{7,3},{8,12},{9,13},{10,... | collective-permute-start | bytes 98312 | tf_op jit(solution)/shard_map/ppermute | solution.py:88
  167.8 1.8 collective-permute-done.25
  169.6 5.1 %fusion.4 = f32[8,896]{1,0:T(8,128)S(1)} fusion(bf16[1,896,4096]{2,1,0:T(8,128)(2,1)} %param.28, bf16[4,4096]{1,0:T(4,128)(2,1)S(1)} %bitcast.223, bf16[4,4096]{1,0:T(4,128)(2,1)S(1)} %maximum_select_fusion.1, pred[]{:T(512)S(6)} %eq.72), kind=kOutput, calls=%fused_computation.10 | convolution fusion | flops 59015168 | bytes 7434241 | tf_op jit(solution)/shard_map/dot_general | solution.py:21
  174.7 5.1 %fusion.16 = bf16[8,896]{1,0:T(8,128)(2,1)S(1)} fusion(bf16[1,896,4096]{2,1,0:T(8,128)(2,1)} %param.29, f32[8,896]{1,0:T(8,128)S(1)} %fusion.4, bf16[4,4096]{1,0:T(4,128)(2,1)S(1)} %bitcast.224, bf16[4,4096]{1,0:T(4,128)(2,1)S(1)} %maximum_select_fusion.1, pred[]{:T(512)S(6)} %eq.72), kind=kOutput, calls=%fused_computation.33 | convolution fusion | flops 59058176 | bytes 7448577 | tf_op jit(solution)/shard_map/dot_general | solution.py:21
  179.8 4.2 %fusion = f32[2,2,2,4096]{3,2,1,0:T(2,128)S(1)} fusion(bf16[2,2,2,896]{3,2,1,0:T(2,128)(2,1)S(1)} %dot_general.37, bf16[1,896,4096]{2,1,0:T(8,128)(2,1)} %param.30), kind=kOutput, calls=%fused_computation.6 | convolution fusion | flops 58720256 | bytes 7485440 | tf_op jit(solution)/shard_map/dot_general | solution.py:256
  184.1 2.1 %collective-permute-start.26 = (f32[2,2,1,1,4096]{4,2,3,1,0:T(1,128)S(1)}, f32[2,2,1,1,4096]{4,2,3,1,0:T(1,128)S(1)}, u32[]{:S(2)}, u32[]{:S(2)}) collective-permute-start(f32[2,2,1,1,4096]{4,2,3,1,0:T(1,128)S(1)} %dynamic-slice_bitcast_fusion), channel_id=1, source_target_pairs={{0,1},{1,0},{2,3},{3,2},{4,5},{5,4},{6,7},{7,6},{8,9},{9,8},{10,11... | collective-permute-start | bytes 196616 | tf_op jit(solution)/shard_map/ppermute | solution.py:107
  186.3 2.2 %collective-permute-done.26 = f32[2,2,1,1,4096]{4,2,3,1,0:T(1,128)S(1)} collective-permute-done((f32[2,2,1,1,4096]{4,2,3,1,0:T(1,128)S(1)}, f32[2,2,1,1,4096]{4,2,3,1,0:T(1,128)S(1)}, u32[]{:S(2)}, u32[]{:S(2)}) %collective-permute-start.26) | collective-permute-done | bytes 65568 | tf_op jit(solution)/shard_map/ppermute | solution.py:107
  188.6 2.0 collective-permute-start.27
  190.6 2.0 collective-permute-done.27
  192.7 3.0 %collective-permute-start.28 = (f32[1,1,1,1,4096]{4,2,3,1,0:T(1,128)S(1)}, f32[1,1,1,1,4096]{4,2,3,1,0:T(1,128)S(1)}, u32[]{:S(2)}, u32[]{:S(2)}) collective-permute-start(f32[1,1,1,1,4096]{4,2,3,1,0:T(1,128)S(1)} %constant_dynamic-slice_fusion), channel_id=1, source_target_pairs={{0,4},{1,5},{2,6},{3,7},{4,0},{5,1},{6,2},{7,3},{8,12},{9,13},{10,... | collective-permute-start | bytes 49160 | tf_op jit(solution)/shard_map/ppermute | solution.py:107
  195.7 1.7 collective-permute-done.28
  197.5 3.2 %collective-permute-done.29 = bf16[1,1,4096]{2,1,0:T(2,128)(2,1)S(1)} collective-permute-done((bf16[1,1,4096]{2,1,0:T(2,128)(2,1)S(1)}, bf16[1,1,4096]{2,1,0:T(2,128)(2,1)S(1)}, u32[]{:S(2)}, u32[]{:S(2)}) %collective-permute-start.29) | collective-permute-done | bytes 8224 | tf_op jit(solution)/shard_map/ppermute | solution.py:259
  (152 shorter events, 34.3 us)
Async XLA Ops:
  0.0 142.0 %copy-start = (bf16[1,256,4096]{2,1,0:T(8,128)(2,1)S(1)}, bf16[1,256,4096]{2,1,0:T(8,128)(2,1)}, u32[]{:S(2)}) copy-start(bf16[1,256,4096]{2,1,0:T(8,128)(2,1)} %param.26) | copy-start | bytes 6291460
  0.0 12.9 %copy-start.2 = (bf16[1,256,1024]{2,1,0:T(8,128)(2,1)S(1)}, bf16[1,256,1024]{2,1,0:T(8,128)(2,1)}, u32[]{:S(2)}) copy-start(bf16[1,256,1024]{2,1,0:T(8,128)(2,1)} %param.18) | copy-start | bytes 1572868
  3.1 59.7 %collective-permute-start.10 = (bf16[80,4096]{1,0:T(8,128)(2,1)}, bf16[80,4096]{1,0:T(8,128)(2,1)}, u32[]{:S(2)}, u32[]{:S(2)}) collective-permute-start(bf16[80,4096]{1,0:T(8,128)(2,1)} %pad_maximum_fusion), channel_id=1, source_target_pairs={{0,2},{2,4},{4,6},{6,7},{7,5},{5,3},{3,1},{1,0},{8,10},{10,12},{12... | collective-permute-start | bytes 1966088 | tf_op jit(solution)/shard_map/ppermute | solution.py:125
  6.1 57.8 %collective-permute-start.14 = (bf16[80,4096]{1,0:T(8,128)(2,1)}, bf16[80,4096]{1,0:T(8,128)(2,1)}, u32[]{:S(2)}, u32[]{:S(2)}) collective-permute-start(bf16[80,4096]{1,0:T(8,128)(2,1)} %pad_maximum_fusion), channel_id=1, source_target_pairs={{0,1},{2,0},{4,2},{6,4},{7,6},{5,7},{3,5},{1,3},{8,9},{10,8},{12,1... | collective-permute-start | bytes 1966088 | tf_op jit(solution)/shard_map/ppermute | solution.py:129
  12.9 11.6 %copy-start.10 = (s32[8]{0:T(128)S(1)}, s32[8]{0:T(128)}, u32[]{:S(2)}) copy-start(s32[8]{0:T(128)} %constant.279.clone) | copy-start | bytes 100
  12.9 12.2 %copy-start.9 = (s32[8]{0:T(128)S(1)}, s32[8]{0:T(128)}, u32[]{:S(2)}) copy-start(s32[8]{0:T(128)} %constant.281.clone) | copy-start | bytes 100
  12.9 12.8 %copy-start.1 = (s32[8]{0:T(128)S(1)}, s32[8]{0:T(128)}, u32[]{:S(2)}) copy-start(s32[8]{0:T(128)} %constant.280.clone) | copy-start | bytes 100
  12.9 15.0 %copy-start.7 = (f32[1,128]{1,0:T(1,128)S(1)}, f32[1,128]{1,0:T(1,128)}, u32[]{:S(2)}) copy-start(f32[1,128]{1,0:T(1,128)} %param.23) | copy-start | bytes 1540
  15.8 12.9 %collective-permute-start = (bf16[44,1024]{1,0:T(8,128)(2,1)S(1)}, bf16[44,1024]{1,0:T(8,128)(2,1)}, u32[]{:S(2)}, u32[]{:S(2)}) collective-permute-start(bf16[44,1024]{1,0:T(8,128)(2,1)S(1)} %get-tuple-element.13), channel_id=1, source_target_pairs={{0,1},{1,2},{2,3},{3,4},{4,5},{5,6},{6,7},{7,0},{8,9},{9,10},{10,1... | collective-permute-start | bytes 270344 | tf_op jit(solution)/shard_map/ppermute | solution.py:58
  17.7 13.8 %collective-permute-start.1 = (bf16[44,1024]{1,0:T(8,128)(2,1)S(1)}, bf16[44,1024]{1,0:T(8,128)(2,1)}, u32[]{:S(2)}, u32[]{:S(2)}) collective-permute-start(bf16[44,1024]{1,0:T(8,128)(2,1)S(1)} %get-tuple-element.14), channel_id=1, source_target_pairs={{0,2},{1,3},{2,4},{3,5},{4,6},{5,7},{6,0},{7,1},{8,10},{9,11},{10,... | collective-permute-start | bytes 270344 | tf_op jit(solution)/shard_map/ppermute | solution.py:58
  19.3 16.4 %collective-permute-start.2 = (bf16[44,1024]{1,0:T(8,128)(2,1)S(1)}, bf16[44,1024]{1,0:T(8,128)(2,1)}, u32[]{:S(2)}, u32[]{:S(2)}) collective-permute-start(bf16[44,1024]{1,0:T(8,128)(2,1)S(1)} %get-tuple-element.15), channel_id=1, source_target_pairs={{0,3},{1,4},{2,5},{3,6},{4,7},{5,0},{6,1},{7,2},{8,11},{9,12},{10,... | collective-permute-start | bytes 270344 | tf_op jit(solution)/shard_map/ppermute | solution.py:58
  28.7 11.4 %collective-permute-start.3 = (bf16[44,1024]{1,0:T(8,128)(2,1)S(1)}, bf16[44,1024]{1,0:T(8,128)(2,1)S(1)}, u32[]{:S(2)}, u32[]{:S(2)}) collective-permute-start(bf16[44,1024]{1,0:T(8,128)(2,1)S(1)} %get-tuple-element.16), channel_id=1, source_target_pairs={{0,4},{1,5},{2,6},{3,7},{4,0},{5,1},{6,2},{7,3},{8,12},{9,13},{10,... | collective-permute-start | bytes 270344 | tf_op jit(solution)/shard_map/ppermute | solution.py:58
  31.5 10.7 %collective-permute-start.4 = (bf16[44,1024]{1,0:T(8,128)(2,1)}, bf16[44,1024]{1,0:T(8,128)(2,1)S(1)}, u32[]{:S(2)}, u32[]{:S(2)}) collective-permute-start(bf16[44,1024]{1,0:T(8,128)(2,1)} %get-tuple-element.18), channel_id=1, source_target_pairs={{0,5},{1,6},{2,7},{3,0},{4,1},{5,2},{6,3},{7,4},{8,13},{9,14},{10,... | collective-permute-start | bytes 270344 | tf_op jit(solution)/shard_map/ppermute | solution.py:58
  35.7 7.2 %collective-permute-start.5 = (bf16[44,1024]{1,0:T(8,128)(2,1)S(1)}, bf16[44,1024]{1,0:T(8,128)(2,1)S(1)}, u32[]{:S(2)}, u32[]{:S(2)}) collective-permute-start(bf16[44,1024]{1,0:T(8,128)(2,1)S(1)} %get-tuple-element.17), channel_id=1, source_target_pairs={{0,6},{1,7},{2,0},{3,1},{4,2},{5,3},{6,4},{7,5},{8,14},{9,15},{10,... | collective-permute-start | bytes 270344 | tf_op jit(solution)/shard_map/ppermute | solution.py:58
  40.1 4.6 %collective-permute-start.6 = (bf16[44,1024]{1,0:T(8,128)(2,1)S(1)}, bf16[44,1024]{1,0:T(8,128)(2,1)S(1)}, u32[]{:S(2)}, u32[]{:S(2)}) collective-permute-start(bf16[44,1024]{1,0:T(8,128)(2,1)S(1)} %get-tuple-element.11), channel_id=1, source_target_pairs={{0,7},{1,0},{2,1},{3,2},{4,3},{5,4},{6,5},{7,6},{8,15},{9,8},{10,9... | collective-permute-start | bytes 270344 | tf_op jit(solution)/shard_map/ppermute | solution.py:58
  47.2 0.9 copy-start.4
  50.4 3.7 %collective-permute-start.7 = (bf16[2,2,1,1,256]{4,2,1,3,0:T(2,128)(2,1)S(1)}, bf16[2,2,1,1,256]{4,2,1,3,0:T(2,128)(2,1)S(1)}, u32[]{:S(2)}, u32[]{:S(2)}) collective-permute-start(bf16[2,2,1,1,256]{4,2,1,3,0:T(2,128)(2,1)S(1)} %get-tuple-element.30), channel_id=1, source_target_pairs={{0,1},{1,0},{2,3},{3,2},{4,5},{5,4},{6,7},{7,6},{8,9},{9,8},{10,11... | collective-permute-start | bytes 6152 | tf_op jit(solution)/shard_map/ppermute | solution.py:73
  51.7 11.0 %copy-start.8 = (f32[1,128]{1,0:T(1,128)S(1)}, f32[1,128]{1,0:T(1,128)}, u32[]{:S(2)}) copy-start(f32[1,128]{1,0:T(1,128)} %param.22) | copy-start | bytes 1540
  54.2 3.7 %collective-permute-start.8 = (bf16[2,1,2,1,256]{4,2,1,3,0:T(2,128)(2,1)S(1)}, bf16[2,1,2,1,256]{4,2,1,3,0:T(2,128)(2,1)S(1)}, u32[]{:S(2)}, u32[]{:S(2)}) collective-permute-start(bf16[2,1,2,1,256]{4,2,1,3,0:T(2,128)(2,1)S(1)} %get-tuple-element.28), channel_id=1, source_target_pairs={{0,2},{1,3},{2,0},{3,1},{4,6},{5,7},{6,4},{7,5},{8,10},{9,11},{10,... | collective-permute-start | bytes 6152 | tf_op jit(solution)/shard_map/ppermute | solution.py:73
  57.9 4.6 %collective-permute-start.9 = (bf16[1,2,2,1,256]{4,2,1,3,0:T(2,128)(2,1)S(1)}, bf16[1,2,2,1,256]{4,2,1,3,0:T(2,128)(2,1)S(1)}, u32[]{:S(2)}, u32[]{:S(2)}) collective-permute-start(bf16[1,2,2,1,256]{4,2,1,3,0:T(2,128)(2,1)S(1)} %get-tuple-element.26), channel_id=1, source_target_pairs={{0,4},{1,5},{2,6},{3,7},{4,0},{5,1},{6,2},{7,3},{8,12},{9,13},{10,... | collective-permute-start | bytes 6152 | tf_op jit(solution)/shard_map/ppermute | solution.py:73
  62.8 15.2 %collective-permute-start.11 = (bf16[80,4096]{1,0:T(8,128)(2,1)}, bf16[80,4096]{1,0:T(8,128)(2,1)S(1)}, u32[]{:S(2)}, u32[]{:S(2)}) collective-permute-start(bf16[80,4096]{1,0:T(8,128)(2,1)} %collective-permute-done.10), channel_id=1, source_target_pairs={{0,2},{2,4},{4,6},{6,7},{7,5},{5,3},{3,1},{1,0},{8,10},{10,12},{12... | collective-permute-start | bytes 1966088 | tf_op jit(solution)/shard_map/ppermute | solution.py:125
  63.9 15.1 %collective-permute-start.15 = (bf16[80,4096]{1,0:T(8,128)(2,1)}, bf16[80,4096]{1,0:T(8,128)(2,1)S(1)}, u32[]{:S(2)}, u32[]{:S(2)}) collective-permute-start(bf16[80,4096]{1,0:T(8,128)(2,1)} %collective-permute-done.14), channel_id=1, source_target_pairs={{0,1},{2,0},{4,2},{6,4},{7,6},{5,7},{3,5},{1,3},{8,9},{10,8},{12,1... | collective-permute-start | bytes 1966088 | tf_op jit(solution)/shard_map/ppermute | solution.py:129
  78.0 16.0 %collective-permute-start.12 = (bf16[80,4096]{1,0:T(8,128)(2,1)S(1)}, bf16[80,4096]{1,0:T(8,128)(2,1)S(1)}, u32[]{:S(2)}, u32[]{:S(2)}) collective-permute-start(bf16[80,4096]{1,0:T(8,128)(2,1)S(1)} %collective-permute-done.11), channel_id=1, source_target_pairs={{0,2},{2,4},{4,6},{6,7},{7,5},{5,3},{3,1},{1,0},{8,10},{10,12},{12... | collective-permute-start | bytes 1966088 | tf_op jit(solution)/shard_map/ppermute | solution.py:125
  79.0 29.3 %collective-permute-start.16 = (bf16[80,4096]{1,0:T(8,128)(2,1)S(1)}, bf16[80,4096]{1,0:T(8,128)(2,1)S(1)}, u32[]{:S(2)}, u32[]{:S(2)}) collective-permute-start(bf16[80,4096]{1,0:T(8,128)(2,1)S(1)} %collective-permute-done.15), channel_id=1, source_target_pairs={{0,1},{2,0},{4,2},{6,4},{7,6},{5,7},{3,5},{1,3},{8,9},{10,8},{12,1... | collective-permute-start | bytes 1966088 | tf_op jit(solution)/shard_map/ppermute | solution.py:129
  94.0 10.6 %collective-permute-start.13 = (bf16[80,4096]{1,0:T(8,128)(2,1)S(1)}, bf16[80,4096]{1,0:T(8,128)(2,1)S(1)}, u32[]{:S(2)}, u32[]{:S(2)}) collective-permute-start(bf16[80,4096]{1,0:T(8,128)(2,1)S(1)} %collective-permute-done.12), channel_id=1, source_target_pairs={{0,2},{2,4},{4,6},{6,7},{7,5},{5,3},{3,1},{1,0},{8,10},{10,12},{12... | collective-permute-start | bytes 1966088 | tf_op jit(solution)/shard_map/ppermute | solution.py:125
  118.1 2.7 %copy-start.3 = (f32[256,4096]{1,0:T(8,128)}, f32[256,4096]{1,0:T(8,128)S(1)}, u32[]{:S(2)}) copy-start(f32[256,4096]{1,0:T(8,128)S(1)} %convolution_bitcast_fusion) | copy-start | bytes 12582916
  126.9 28.7 %copy-start.5 = (bf16[1,1,4096]{2,1,0:T(2,128)(2,1)S(1)}, bf16[1,1,4096]{2,1,0:T(2,128)(2,1)}, u32[]{:S(2)}) copy-start(bf16[1,1,4096]{2,1,0:T(2,128)(2,1)} %param.17) | copy-start | bytes 24580
  126.9 30.1 %copy-start.6 = (f32[1,4096]{1,0:T(1,128)S(1)}, f32[1,4096]{1,0:T(1,128)}, u32[]{:S(2)}) copy-start(f32[1,4096]{1,0:T(1,128)} %param.27) | copy-start | bytes 49156
  128.2 5.0 %collective-permute-start.17 = (bf16[2,2,1,1,256]{4,2,1,3,0:T(2,128)(2,1)S(1)}, bf16[2,2,1,1,256]{4,2,1,3,0:T(2,128)(2,1)S(1)}, u32[]{:S(2)}, u32[]{:S(2)}) collective-permute-start(bf16[2,2,1,1,256]{4,2,1,3,0:T(2,128)(2,1)S(1)} %get-tuple-element.24), channel_id=1, source_target_pairs={{0,1},{1,0},{2,3},{3,2},{4,5},{5,4},{6,7},{7,6},{8,9},{9,8},{10,11... | collective-permute-start | bytes 6152 | tf_op jit(solution)/shard_map/ppermute | solution.py:73
  133.3 3.7 %collective-permute-start.18 = (bf16[2,1,2,1,256]{4,2,1,3,0:T(2,128)(2,1)S(1)}, bf16[2,1,2,1,256]{4,2,1,3,0:T(2,128)(2,1)S(1)}, u32[]{:S(2)}, u32[]{:S(2)}) collective-permute-start(bf16[2,1,2,1,256]{4,2,1,3,0:T(2,128)(2,1)S(1)} %get-tuple-element.22), channel_id=1, source_target_pairs={{0,2},{1,3},{2,0},{3,1},{4,6},{5,7},{6,4},{7,5},{8,10},{9,11},{10,... | collective-permute-start | bytes 6152 | tf_op jit(solution)/shard_map/ppermute | solution.py:73
  137.0 4.9 %collective-permute-start.19 = (bf16[1,2,2,1,256]{4,2,1,3,0:T(2,128)(2,1)S(1)}, bf16[1,2,2,1,256]{4,2,1,3,0:T(2,128)(2,1)S(1)}, u32[]{:S(2)}, u32[]{:S(2)}) collective-permute-start(bf16[1,2,2,1,256]{4,2,1,3,0:T(2,128)(2,1)S(1)} %get-tuple-element.20), channel_id=1, source_target_pairs={{0,4},{1,5},{2,6},{3,7},{4,0},{5,1},{6,2},{7,3},{8,12},{9,13},{10,... | collective-permute-start | bytes 6152 | tf_op jit(solution)/shard_map/ppermute | solution.py:73
  142.4 4.3 %collective-permute-start.20 = (f32[2,2,1,1,4096]{4,2,3,1,0:T(1,128)S(1)}, f32[2,2,1,1,4096]{4,2,3,1,0:T(1,128)S(1)}, u32[]{:S(2)}, u32[]{:S(2)}) collective-permute-start(f32[2,2,1,1,4096]{4,2,3,1,0:T(1,128)S(1)} %dynamic-slice_bitcast_fusion.1), channel_id=1, source_target_pairs={{0,1},{1,0},{2,3},{3,2},{4,5},{5,4},{6,7},{7,6},{8,9},{9,8},{10,11... | collective-permute-start | bytes 196616 | tf_op jit(solution)/shard_map/ppermute | solution.py:107
  146.9 4.0 %collective-permute-start.21 = (f32[2,1,1,1,4096]{4,2,3,1,0:T(1,128)S(1)}, f32[2,1,1,1,4096]{4,2,3,1,0:T(1,128)S(1)}, u32[]{:S(2)}, u32[]{:S(2)}) collective-permute-start(f32[2,1,1,1,4096]{4,2,3,1,0:T(1,128)S(1)} %constant_dynamic-slice_fusion.3), channel_id=1, source_target_pairs={{0,2},{1,3},{2,0},{3,1},{4,6},{5,7},{6,4},{7,5},{8,10},{9,11},{10,... | collective-permute-start | bytes 98312 | tf_op jit(solution)/shard_map/ppermute | solution.py:107
  150.9 4.7 %collective-permute-start.22 = (f32[1,1,1,1,4096]{4,2,3,1,0:T(1,128)S(1)}, f32[1,1,1,1,4096]{4,2,3,1,0:T(1,128)S(1)}, u32[]{:S(2)}, u32[]{:S(2)}) collective-permute-start(f32[1,1,1,1,4096]{4,2,3,1,0:T(1,128)S(1)} %constant_dynamic-slice_fusion.2), channel_id=1, source_target_pairs={{0,4},{1,5},{2,6},{3,7},{4,0},{5,1},{6,2},{7,3},{8,12},{9,13},{10,... | collective-permute-start | bytes 49160 | tf_op jit(solution)/shard_map/ppermute | solution.py:107
  157.0 3.8 %collective-permute-start.23 = (bf16[1,1,4096]{2,0,1:T(2,128)(2,1)S(1)}, bf16[1,1,4096]{2,0,1:T(2,128)(2,1)S(1)}, u32[]{:S(2)}, u32[]{:S(2)}) collective-permute-start(bf16[1,1,4096]{2,0,1:T(2,128)(2,1)S(1)} %bitcast.219), channel_id=1, source_target_pairs={{0,1},{1,0},{2,3},{3,2},{4,5},{5,4},{6,7},{7,6},{8,9},{9,8},{10,11... | collective-permute-start | bytes 24584 | tf_op jit(solution)/shard_map/ppermute | solution.py:88
  160.9 3.8 %collective-permute-start.24 = (bf16[2,1,4096]{2,0,1:T(2,128)(2,1)S(1)}, bf16[2,1,4096]{2,0,1:T(2,128)(2,1)S(1)}, u32[]{:S(2)}, u32[]{:S(2)}) collective-permute-start(bf16[2,1,4096]{2,0,1:T(2,128)(2,1)S(1)} %broadcast_select_fusion.1), channel_id=1, source_target_pairs={{0,2},{1,3},{2,0},{3,1},{4,6},{5,7},{6,4},{7,5},{8,10},{9,11},{10,... | collective-permute-start | bytes 49160 | tf_op jit(solution)/shard_map/ppermute | solution.py:88
  164.8 4.9 %collective-permute-start.25 = (bf16[4,1,4096]{2,0,1:T(4,128)(2,1)S(1)}, bf16[4,1,4096]{2,0,1:T(4,128)(2,1)S(1)}, u32[]{:S(2)}, u32[]{:S(2)}) collective-permute-start(bf16[4,1,4096]{2,0,1:T(4,128)(2,1)S(1)} %maximum_select_fusion.2), channel_id=1, source_target_pairs={{0,4},{1,5},{2,6},{3,7},{4,0},{5,1},{6,2},{7,3},{8,12},{9,13},{10,... | collective-permute-start | bytes 98312 | tf_op jit(solution)/shard_map/ppermute | solution.py:88
  184.1 4.4 %collective-permute-start.26 = (f32[2,2,1,1,4096]{4,2,3,1,0:T(1,128)S(1)}, f32[2,2,1,1,4096]{4,2,3,1,0:T(1,128)S(1)}, u32[]{:S(2)}, u32[]{:S(2)}) collective-permute-start(f32[2,2,1,1,4096]{4,2,3,1,0:T(1,128)S(1)} %dynamic-slice_bitcast_fusion), channel_id=1, source_target_pairs={{0,1},{1,0},{2,3},{3,2},{4,5},{5,4},{6,7},{7,6},{8,9},{9,8},{10,11... | collective-permute-start | bytes 196616 | tf_op jit(solution)/shard_map/ppermute | solution.py:107
  188.6 4.0 %collective-permute-start.27 = (f32[2,1,1,1,4096]{4,2,3,1,0:T(1,128)S(1)}, f32[2,1,1,1,4096]{4,2,3,1,0:T(1,128)S(1)}, u32[]{:S(2)}, u32[]{:S(2)}) collective-permute-start(f32[2,1,1,1,4096]{4,2,3,1,0:T(1,128)S(1)} %constant_dynamic-slice_fusion.1), channel_id=1, source_target_pairs={{0,2},{1,3},{2,0},{3,1},{4,6},{5,7},{6,4},{7,5},{8,10},{9,11},{10,... | collective-permute-start | bytes 98312 | tf_op jit(solution)/shard_map/ppermute | solution.py:107
  192.7 4.8 %collective-permute-start.28 = (f32[1,1,1,1,4096]{4,2,3,1,0:T(1,128)S(1)}, f32[1,1,1,1,4096]{4,2,3,1,0:T(1,128)S(1)}, u32[]{:S(2)}, u32[]{:S(2)}) collective-permute-start(f32[1,1,1,1,4096]{4,2,3,1,0:T(1,128)S(1)} %constant_dynamic-slice_fusion), channel_id=1, source_target_pairs={{0,4},{1,5},{2,6},{3,7},{4,0},{5,1},{6,2},{7,3},{8,12},{9,13},{10,... | collective-permute-start | bytes 49160 | tf_op jit(solution)/shard_map/ppermute | solution.py:107
  197.5 3.2 %collective-permute-start.29 = (bf16[1,1,4096]{2,1,0:T(2,128)(2,1)S(1)}, bf16[1,1,4096]{2,1,0:T(2,128)(2,1)S(1)}, u32[]{:S(2)}, u32[]{:S(2)}) collective-permute-start(bf16[1,1,4096]{2,1,0:T(2,128)(2,1)S(1)} %fusion.55), channel_id=1, source_target_pairs={{0,8},{8,16},{16,24},{24,0},{1,9},{9,17},{17,25},{25,1},{2,10},{10... | collective-permute-start | bytes 24584 | tf_op jit(solution)/shard_map/ppermute | solution.py:259

commit v3 on v2

--- a/solution.py
+++ b/solution.py
@@ -108,32 +108,69 @@
     return state.reshape(rest)
 
 
-def ring_gather(value, count, me):
-    if not direct_ok(count):
-        return lax.all_gather(value, "site", axis=0, tiled=False), jnp.arange(count, dtype=jnp.int32)
-    order = list(range(0, count, 2)) + [i for i in range(count - 1, -1, -1) if i % 2 == 1]
-    place = [0] * count
-    for position, device in enumerate(order):
-        place[device] = position
-    forward = [(order[p], order[(p + 1) % count]) for p in range(count)]
-    backward = [(order[p], order[(p - 1) % count]) for p in range(count)]
-    forward_steps = count // 2
-    backward_steps = count - 1 - forward_steps
-    slots = [value]
-    moving = value
-    for _ in range(forward_steps):
-        moving = lax.ppermute(moving, "site", forward)
-        slots.append(moving)
-    moving = value
-    for _ in range(backward_steps):
-        moving = lax.ppermute(moving, "site", backward)
-        slots.append(moving)
-    offsets = [0] + [-s for s in range(1, forward_steps + 1)] + list(range(1, backward_steps + 1))
-    my_place = jnp.array(place, dtype=jnp.int32)[me]
-    source_of_slot = jnp.array(order, dtype=jnp.int32)[
-        (my_place + jnp.array(offsets, dtype=jnp.int32)) % count
-    ]
-    return jnp.stack(slots), source_of_slot
+def doubling_sum(parts, count):
+    state = parts
+    for bit in range(count.bit_length() - 1):
+        state = state + lax.ppermute(state, "site", xor_pairs(count, bit))
+    return state
+
+
+class RingGather:
+    def __init__(self, value, count, me):
+        self.count = count
+        self.direct = direct_ok(count)
+        if not self.direct:
+            self.slots = lax.all_gather(value, "site", axis=0, tiled=False)
+            self.sources = jnp.arange(count, dtype=jnp.int32)
+            return
+        order = list(range(0, count, 2)) + [i for i in range(count - 1, -1, -1) if i % 2 == 1]
+        place = [0] * count
+        for position, device in enumerate(order):
+            place[device] = position
+        self.forward = [(order[p], order[(p + 1) % count]) for p in range(count)]
+        self.backward = [(order[p], order[(p - 1) % count]) for p in range(count)]
+        self.forward_left = count // 2
+        self.backward_left = count - 1 - self.forward_left
+        offsets = [0] + [-s for s in range(1, self.forward_left + 1)]
+        offsets += list(range(1, self.backward_left + 1))
+        my_place = jnp.array(place, dtype=jnp.int32)[me]
+        self.sources = jnp.array(order, dtype=jnp.int32)[
+            (my_place + jnp.array(offsets, dtype=jnp.int32)) % count
+        ]
+        self.forward_slots = []
+        self.backward_slots = []
+        self.ahead = value
+        self.behind = value
+        self.value = value
+        self._issue()
+
+    def _issue(self):
+        if self.forward_left > 0:
+            self.ahead = lax.ppermute(self.ahead, "site", self.forward)
+            self.forward_slots.append(self.ahead)
+            self.forward_left -= 1
+        if self.backward_left > 0:
+            self.behind = lax.ppermute(self.behind, "site", self.backward)
+            self.backward_slots.append(self.behind)
+            self.backward_left -= 1
+
+    def step(self, tied):
+        if not self.direct or (self.forward_left == 0 and self.backward_left == 0):
+            return tied
+        self.ahead, self.behind, tied = lax.optimization_barrier((self.ahead, self.behind, tied))
+        self.forward_slots[-1] = self.ahead
+        if self.backward_slots:
+            self.backward_slots[-1] = self.behind
+        self._issue()
+        return tied
+
+    def finish(self):
+        if not self.direct:
+            return self.slots, self.sources
+        while self.forward_left > 0 or self.backward_left > 0:
+            self._issue()
+        slots = [self.value] + self.forward_slots + self.backward_slots
+        return jnp.stack(slots), self.sources
 
 
 def shards(
@@ -170,9 +207,7 @@
     packed_weights = jnp.concatenate(
         [tile_in[0].reshape(in_rows, tile_out.shape[-1]), tile_out[0]], axis=0
     )
-    weight_slots, source_of_slot = ring_gather(packed_weights, group_size, my_index)
-    weight_in = weight_slots[:, :in_rows].reshape(-1, width_in)
-    weight_out = weight_slots[:, in_rows:].reshape(-1, weight_slots.shape[-1])
+    ring = RingGather(packed_weights, group_size, my_index)
 
     slot_index = jnp.arange(list_width, dtype=jnp.int32)
     live_all = (slot_index[None, :] < site_count[:, None]).reshape(group_size, entries)
@@ -192,14 +227,23 @@
         act_block = jnp.broadcast_to(
             current.reshape(1, act_rows, row_width), (group_size, act_rows, row_width)
         )
-        arrived = site_exchange(
-            jnp.concatenate([send_rows, act_block], axis=1), group_size, my_index
-        )
+        send_rows = jnp.concatenate([send_rows, act_block], axis=1)
+    send_rows = ring.step(send_rows)
+    arrived = lax.all_to_all(send_rows, "site", split_axis=0, concat_axis=0, tiled=True)
+    if packed:
         everyone = arrived[:, capacity:].reshape(-1, model_width)
         arrived = arrived[:, :capacity]
     else:
-        arrived = site_exchange(send_rows, group_size, my_index)
         everyone = doubling_gather(current, group_size, my_index).reshape(-1, model_width)
+    q_part = by_rows(everyone, q_weight[0]).astype(jnp.bfloat16)
+    q_part = ring.step(q_part)
+    q_blocks = halving_exchange(
+        q_part.reshape(group_size, sites_here, -1), group_size, my_index
+    )
+    q_blocks = ring.step(q_blocks)
+    weight_slots, source_of_slot = ring.finish()
+    weight_in = weight_slots[:, :in_rows].reshape(-1, width_in)
+    weight_out = weight_slots[:, in_rows:].reshape(-1, weight_slots.shape[-1])
 
     my_tiles = lax.dynamic_slice_in_dim(site_tiles, my_index * sites_here, sites_here, 0)
     my_count = lax.dynamic_slice_in_dim(site_count, my_index * sites_here, sites_here, 0)
@@ -225,10 +269,6 @@
     pair_kv = jnp.concatenate([normed_keys, keyval[:, half_width:]], axis=1).astype(jnp.bfloat16)
     pair_kv = pair_kv.reshape(sites_here, list_width, 2, HEADS, head_size)
 
-    q_part = by_rows(everyone, q_weight[0]).astype(jnp.bfloat16)
-    q_blocks = halving_exchange(
-        q_part.reshape(group_size, sites_here, -1), group_size, my_index
-    )
     my_queries = jnp.moveaxis(q_blocks, 0, 1).reshape(sites_here, -1)
     queries = head_norm(my_queries, q_gain[0]).astype(jnp.bfloat16)
     query_heads = queries.reshape(sites_here, HEADS, head_size)
@@ -246,17 +286,56 @@
         group_size * sites_here, -1
     )
     attn_part = jnp.dot(columns, out_weight[0], preferred_element_type=jnp.float32)
-    attn_sum = halving_sum(attn_part.reshape(group_size, sites_here, -1), group_size, my_index)
-    residual = current.astype(jnp.float32) + attn_sum
-    normed = rms_norm(residual, ffn_gain[0]).astype(jnp.bfloat16)
-    normed_rows = doubling_gather(normed, group_size, my_index).reshape(-1, model_width)
+    attn_part = attn_part.reshape(group_size, sites_here, -1)
+    if direct_ok(group_size):
+        attn_all = doubling_sum(attn_part, group_size)
+        residual_all = everyone.reshape(group_size, sites_here, -1).astype(jnp.float32) + attn_all
+        residual = lax.dynamic_index_in_dim(residual_all, my_index, 0, keepdims=False)
+        normed_rows = rms_norm(residual_all, ffn_gain[0]).astype(jnp.bfloat16)
+        normed_rows = normed_rows.reshape(-1, model_width)
+    else:
+        attn_sum = halving_sum(attn_part, group_size, my_index)
+        residual = current.astype(jnp.float32) + attn_sum
+        normed = rms_norm(residual, ffn_gain[0]).astype(jnp.bfloat16)
+        normed_rows = doubling_gather(normed, group_size, my_index).reshape(-1, model_width)
     gate_sum = by_rows(normed_rows, gate_weight[0])
     up_sum = by_rows(normed_rows, up_weight[0])
     hidden_ffn = (jax.nn.silu(gate_sum) * up_sum).astype(jnp.bfloat16)
     down_part = jnp.dot(hidden_ffn, down_weight[0], preferred_element_type=jnp.float32)
-    down_sum = halving_sum(down_part.reshape(group_size, sites_here, -1), group_size, my_index)
-    output_rows = (residual + down_sum).astype(jnp.bfloat16)
-    return lax.ppermute(output_rows[None], "section", shift_pairs(section_count, 1))
+    down_part = down_part.reshape(group_size, sites_here, -1)
+    if not direct_ok(group_size) or group_size == 1:
+        down_sum = halving_sum(down_part, group_size, my_index)
+        output_rows = (residual + down_sum).astype(jnp.bfloat16)
+        return lax.ppermute(output_rows[None], "section", shift_pairs(section_count, 1))
+    bits = group_size.bit_length() - 1
+    rest = down_part.shape[1:]
+    state = down_part.reshape((2,) * bits + rest)
+    for bit in range(bits):
+        axis = bits - 1 - bit
+        mine = (my_index >> bit) & 1
+        keep = lax.dynamic_index_in_dim(state, mine, axis, keepdims=True)
+        send = lax.dynamic_index_in_dim(state, 1 - mine, axis, keepdims=True)
+        if bit < bits - 1:
+            state = keep + lax.ppermute(send, "site", xor_pairs(group_size, bit))
+            continue
+        own = keep.reshape(rest) + residual
+        forward = [
+            (section * group_size + site, ((section + 1) % section_count) * group_size + site)
+            for section in range(section_count)
+            for site in range(group_size)
+        ]
+        across = [
+            (
+                section * group_size + site,
+                ((section + 1) % section_count) * group_size + (site ^ (1 << bit)),
+            )
+            for section in range(section_count)
+            for site in range(group_size)
+        ]
+        mine_part = lax.ppermute(own, ("section", "site"), forward)
+        other_part = lax.ppermute(send.reshape(rest), ("section", "site"), across)
+        output_rows = (mine_part + other_part).astype(jnp.bfloat16)
+    return output_rows[None]
 
 
 def solution(mesh):

time: 202 us -> 189 us (0.936)
  starting transfers between devices: 56 us -> 37.5 us
  waiting for transfers between devices: 63.6 us -> 70.5 us
  local copies, waits for them, and re-layouts: 36.8 us -> 32.2 us
  other arithmetic: 20.3 us -> 23.3 us
    ppermute x24 -> x14, starting transfers between devices: 44.8 us -> 22.9 us  [the longest x4 11.1 us: _issue(): self.ahead = lax.ppermute(self.ahead, 'site', self.forward)]
    ppermute x24 -> x14, waiting for transfers between devices: 53.4 us -> 36.5 us  [the longest x4 13.5 us: _issue(): self.ahead = lax.ppermute(self.ahead, 'site', self.forward)]
    all_to_all x0 -> x1, waiting for transfers between devices: none -> 16.9 us  [shards(): lax.all_to_all(send_rows, 'site', split_axis=0, concat_axis=0, tiled=True)]
    ppermute x6, waiting for transfers between devices: 10.2 us -> 17.1 us  [halving_exchange(): recv = lax.ppermute(send, 'site', xor_pairs(count, bit))]
    all_to_all x0 -> x1, starting transfers between devices: none -> 6.25 us  [shards(): lax.all_to_all(send_rows, 'site', split_axis=0, concat_axis=0, tiled=True)]
    unnamed x39 -> x25, local copies, waits for them, and re-layouts: 18.5 us -> 13.6 us
    ppermute x6, starting transfers between devices: 11.2 us -> 8.3 us  [halving_exchange(): recv = lax.ppermute(send, 'site', xor_pairs(count, bit))]
  transfers between devices with their start and end apart: 30 -> 21, of which waited for: 20 -> 17; matrix products, arithmetic and copies ran while one was open for 20% -> 18% of each run, Pallas kernels for 0% -> 0%
where the time goes in v3:
time: 189 us; the launch traced here: 187 us
  waiting for transfers between devices  70.5 us (37%)
  starting transfers between devices  37.5 us (20%)
  local copies, waits for them, and re-layouts  32.2 us (17%)
  other arithmetic  23.3 us (12%)
  matrix products  23.2 us (12%)
    ppermute x6, waiting for transfers between devices, halving_exchange(): recv = lax.ppermute(send, 'site', xor_pairs(count, bit))  17.1 us
    all_to_all x1, waiting for transfers between devices, shards(): lax.all_to_all(send_rows, 'site', split_axis=0, concat_axis=0, tiled=True)  16.9 us
    unnamed x25, local copies, waits for them, and re-layouts  13.6 us
    ppermute x4, waiting for transfers between devices, _issue(): self.ahead = lax.ppermute(self.ahead, 'site', self.forward)  13.5 us
    dot_general x3, matrix products, by_rows(): lax.dot_general(left, weight_rows, (((1,), (1,)), ((), ())), preferred_el...  12.4 us
    ppermute x3, waiting for transfers between devices, doubling_sum(): state = state + lax.ppermute(state, 'site', xor_pairs(count, bit))  12.1 us
    ppermute x4, starting transfers between devices, _issue(): self.ahead = lax.ppermute(self.ahead, 'site', self.forward)  11.1 us
    ppermute x6, starting transfers between devices, halving_exchange(): recv = lax.ppermute(send, 'site', xor_pairs(count, bit))  8.3 us
  transfers between devices with their start and end apart: 21, of which 17 were waited for; matrix products, arithmetic and copies ran while one was open for 18% of the time, Pallas kernels for 0%

profile of v3, /device:TPU:0, one launch (start us, length us, event | category | flops | bytes accessed | tf_op | source)
XLA Modules:
  0.0 187.1 jit_solution(10216980682922727300)
XLA Ops:
  0.0 1.1 reshape_squeeze.4
  1.1 1.9 %pad_maximum_fusion.1 = bf16[80,4096]{1,0:T(8,128)(2,1)} fusion(bf16[64,4096]{1,0:T(8,128)(2,1)} %bitcast.165, bf16[16,4096]{1,0:T(8,128)(2,1)S(1)} %reshape_squeeze.4), kind=kLoop, calls=%fused_computation.34 | loop fusion | flops 1310720 | bytes 1310720 | tf_op jit(solution)/shard_map/concatenate | solution.py:207
  3.1 3.0 %collective-permute-start = (bf16[80,4096]{1,0:T(8,128)(2,1)}, bf16[80,4096]{1,0:T(8,128)(2,1)}, u32[]{:S(2)}, u32[]{:S(2)}) collective-permute-start(bf16[80,4096]{1,0:T(8,128)(2,1)} %pad_maximum_fusion.1), channel_id=1, source_target_pairs={{0,2},{2,4},{4,6},{6,7},{7,5},{5,3},{3,1},{1,0},{8,10},{10,12},{12... | collective-permute-start | bytes 1966088 | tf_op jit(solution)/shard_map/ppermute | solution.py:149
  6.8 0.8 convert_bitcast_fusion.1
  8.3 1.3 dynamic_slice.80
  10.2 1.2 iota_compare_fusion.4
  11.4 0.8 reduce.7
  12.2 1.2 dynamic_slice.79
  13.4 1.3 compare_select_fusion.5
  14.7 1.3 gather_fusion.1
  18.3 1.4 compare_select_fusion.1
  20.2 2.1 %gather_fusion = bf16[320,1024]{1,0:T(8,128)(2,1)S(1)} fusion(bf16[256,1024]{1,0:T(8,128)(2,1)S(1)} %bitcast.158, s32[1024]{0:T(1024)S(1)} %get-tuple-element.44), kind=kCustom, calls=%fused_computation | custom fusion | bytes 1312000 | tf_op jit(solution)/shard_map/gather | solution.py:223
  22.4 1.1 pad_maximum_fusion
  23.4 1.9 %bitcast_dynamic-update-slice_fusion.7 = bf16[8,80,4096]{2,1,0:T(8,128)(2,1)} fusion(bf16[64,4096]{1,0:T(8,128)(2,1)} %bitcast.166, bf16[16,4096]{1,0:T(8,128)(2,1)S(1)} %reshape_squeeze.4), kind=kLoop, calls=%fused_computation.42 | loop fusion | flops 1310719 | bytes 1310720
  25.4 6.3 %all-to-all-start = ((bf16[8,44,1024]{2,1,0:T(8,128)(2,1)}), bf16[8,44,1024]{2,1,0:T(8,128)(2,1)S(1)}, u32[]{:S(2)}, u32[]{:S(2)}) async-start(bf16[8,44,1024]{2,1,0:T(8,128)(2,1)} %pad_maximum_fusion), calls=%async_computation | async-start | bytes 1572864 | tf_op jit(solution)/shard_map/all_to_all | solution.py:232
  32.2 2.0 %collective-permute-start.2 = (bf16[80,4096]{1,0:T(8,128)(2,1)}, bf16[80,4096]{1,0:T(8,128)(2,1)}, u32[]{:S(2)}, u32[]{:S(2)}) collective-permute-start(bf16[80,4096]{1,0:T(8,128)(2,1)} %collective-permute-done), channel_id=1, source_target_pairs={{0,2},{2,4},{4,6},{6,7},{7,5},{5,3},{3,1},{1,0},{8,10},{10,12},{12... | collective-permute-start | bytes 1966088 | tf_op jit(solution)/shard_map/ppermute | solution.py:149
  34.3 2.0 %bitcast_dynamic-update-slice_fusion.6 = bf16[8,80,4096]{2,1,0:T(8,128)(2,1)} fusion(bf16[8,80,4096]{2,1,0:T(8,128)(2,1)} %bitcast_dynamic-update-slice_fusion.7, bf16[80,4096]{1,0:T(8,128)(2,1)} %collective-permute-done), kind=kLoop, calls=%fused_computation.41 | loop fusion | bytes 1310720
  36.3 16.9 %all-to-all-done = bf16[8,44,1024]{2,1,0:T(8,128)(2,1)S(1)} async-done(((bf16[8,44,1024]{2,1,0:T(8,128)(2,1)}), bf16[8,44,1024]{2,1,0:T(8,128)(2,1)S(1)}, u32[]{:S(2)}, u32[]{:S(2)}) %all-to-all-start) | async-done | bytes 720928 | tf_op jit(solution)/shard_map/all_to_all | solution.py:232
  53.9 2.2 %fusion.18 = bf16[8,256]{1,0:T(8,128)(2,1)S(1)} fusion(bf16[8,4096]{1,0:T(8,128)(2,1)S(1)} %bitcast.168, bf16[1,256,4096]{2,1,0:T(8,128)(2,1)} %param.21), kind=kOutput, calls=%fused_computation.25 | convolution fusion | flops 16779264 | bytes 2166784 | tf_op jit(solution)/shard_map/dot_general | solution.py:21
  56.2 1.9 %collective-permute-done.2 = bf16[80,4096]{1,0:T(8,128)(2,1)} collective-permute-done((bf16[80,4096]{1,0:T(8,128)(2,1)}, bf16[80,4096]{1,0:T(8,128)(2,1)}, u32[]{:S(2)}, u32[]{:S(2)}) %collective-permute-start.2) | collective-permute-done | bytes 655392 | tf_op jit(solution)/shard_map/ppermute | solution.py:149
  58.1 2.1 %collective-permute-done.3 = bf16[80,4096]{1,0:T(8,128)(2,1)} collective-permute-done((bf16[80,4096]{1,0:T(8,128)(2,1)}, bf16[80,4096]{1,0:T(8,128)(2,1)}, u32[]{:S(2)}, u32[]{:S(2)}) %collective-permute-start.3) | collective-permute-done | bytes 655392 | tf_op jit(solution)/shard_map/ppermute | solution.py:153
  60.2 5.8 %collective-permute-start.4 = (bf16[80,4096]{1,0:T(8,128)(2,1)}, bf16[80,4096]{1,0:T(8,128)(2,1)}, u32[]{:S(2)}, u32[]{:S(2)}) collective-permute-start(bf16[80,4096]{1,0:T(8,128)(2,1)} %collective-permute-done.2), channel_id=1, source_target_pairs={{0,2},{2,4},{4,6},{6,7},{7,5},{5,3},{3,1},{1,0},{8,10},{10,12},{12... | collective-permute-start | bytes 1966088 | tf_op jit(solution)/shard_map/ppermute | solution.py:149
  66.6 2.0 %bitcast_dynamic-update-slice_fusion.5 = bf16[8,80,4096]{2,1,0:T(8,128)(2,1)} fusion(bf16[8,80,4096]{2,1,0:T(8,128)(2,1)} %bitcast_dynamic-update-slice_fusion.6, bf16[80,4096]{1,0:T(8,128)(2,1)} %collective-permute-done.2), kind=kLoop, calls=%fused_computation.40 | loop fusion | bytes 1310720
  68.6 2.0 %collective-permute-start.5 = (bf16[80,4096]{1,0:T(8,128)(2,1)}, bf16[80,4096]{1,0:T(8,128)(2,1)}, u32[]{:S(2)}, u32[]{:S(2)}) collective-permute-start(bf16[80,4096]{1,0:T(8,128)(2,1)} %collective-permute-done.3), channel_id=1, source_target_pairs={{0,1},{2,0},{4,2},{6,4},{7,6},{5,7},{3,5},{1,3},{8,9},{10,8},{12,1... | collective-permute-start | bytes 1966088 | tf_op jit(solution)/shard_map/ppermute | solution.py:153
  70.7 1.4 gather_fusion.2
  72.2 3.9 %collective-permute-done.6 = bf16[2,2,1,1,256]{4,2,1,0,3:T(2,128)(2,1)} collective-permute-done((bf16[2,2,1,1,256]{4,2,1,0,3:T(2,128)(2,1)}, bf16[2,2,1,1,256]{4,2,1,0,3:T(2,128)(2,1)}, u32[]{:S(2)}, u32[]{:S(2)}) %collective-permute-start.6) | collective-permute-done | bytes 2080 | tf_op jit(solution)/shard_map/ppermute | solution.py:73
  76.0 0.8 broadcast_select_fusion.1
  77.0 0.8 gather_fusion.3
  77.8 6.2 %collective-permute-done.7 = bf16[2,1,2,1,256]{4,2,1,0,3:T(2,128)(2,1)S(1)} collective-permute-done((bf16[2,1,2,1,256]{4,2,1,0,3:T(2,128)(2,1)S(1)}, bf16[2,1,2,1,256]{4,2,1,0,3:T(2,128)(2,1)S(1)}, u32[]{:S(2)}, u32[]{:S(2)}) %collective-permute-start.7) | collective-permute-done | bytes 2080 | tf_op jit(solution)/shard_map/ppermute | solution.py:73
  84.0 3.0 %collective-permute-start.8 = (bf16[1,2,2,1,256]{4,2,1,0,3:T(2,128)(2,1)S(1)}, bf16[1,2,2,1,256]{4,2,1,0,3:T(2,128)(2,1)S(1)}, u32[]{:S(2)}, u32[]{:S(2)}) collective-permute-start(bf16[1,2,2,1,256]{4,2,1,0,3:T(2,128)(2,1)S(1)} %get-tuple-element.38), channel_id=1, source_target_pairs={{0,4},{1,5},{2,6},{3,7},{4,0},{5,1},{6,2},{7,3},{8,12},{9,13},{10,... | collective-permute-start | bytes 6152 | tf_op jit(solution)/shard_map/ppermute | solution.py:73
  87.1 1.1 copy.40
  89.1 2.0 %bitcast_dynamic-update-slice_fusion.4 = bf16[8,80,4096]{2,1,0:T(8,128)(2,1)} fusion(bf16[8,80,4096]{2,1,0:T(8,128)(2,1)} %bitcast_dynamic-update-slice_fusion.5, bf16[80,4096]{1,0:T(8,128)(2,1)} %collective-permute-done.4), kind=kLoop, calls=%fused_computation.39 | loop fusion | bytes 1310720
  91.1 11.6 %collective-permute-done.9 = bf16[80,4096]{1,0:T(8,128)(2,1)S(1)} collective-permute-done((bf16[80,4096]{1,0:T(8,128)(2,1)}, bf16[80,4096]{1,0:T(8,128)(2,1)S(1)}, u32[]{:S(2)}, u32[]{:S(2)}) %collective-permute-start.9) | collective-permute-done | bytes 655392 | tf_op jit(solution)/shard_map/ppermute | solution.py:149
  102.6 0.9 bitcast_dynamic-update-slice_fusion.3
  103.5 2.0 %bitcast_dynamic-update-slice_fusion.2 = bf16[8,80,4096]{2,1,0:T(8,128)(2,1)} fusion(bf16[8,80,4096]{2,1,0:T(8,128)(2,1)} %bitcast_dynamic-update-slice_fusion.3, bf16[80,4096]{1,0:T(8,128)(2,1)} %collective-permute-done.1), kind=kLoop, calls=%fused_computation.37 | loop fusion | bytes 1310720
  105.5 2.0 %bitcast_dynamic-update-slice_fusion.1 = bf16[8,80,4096]{2,1,0:T(8,128)(2,1)} fusion(bf16[8,80,4096]{2,1,0:T(8,128)(2,1)} %bitcast_dynamic-update-slice_fusion.2, bf16[80,4096]{1,0:T(8,128)(2,1)} %collective-permute-done.3), kind=kLoop, calls=%fused_computation.36 | loop fusion | bytes 1310720
  107.4 2.0 %bitcast_dynamic-update-slice_fusion = bf16[8,80,4096]{2,1,0:T(8,128)(2,1)} fusion(bf16[8,80,4096]{2,1,0:T(8,128)(2,1)} %bitcast_dynamic-update-slice_fusion.1, bf16[80,4096]{1,0:T(8,128)(2,1)} %collective-permute-done.5), kind=kLoop, calls=%fused_computation.35 | loop fusion | bytes 1310720 | tf_op jit(solution)/shard_map/stack | solution.py:173
  109.4 1.3 slice.63
  110.7 1.3 reshape.731
  112.0 1.9 %fusion.32 = bf16[256,512]{1,0:T(8,128)(2,1)S(1)} fusion(bf16[256,1024]{0,1:T(8,128)(2,1)} %bitcast.167, bf16[1024,512]{1,0:T(8,128)(2,1)} %reshape.731), kind=kOutput, calls=%fused_computation.50 | convolution fusion | flops 269615104 | bytes 1835008 | tf_op jit(solution)/shard_map/dot_general | solution.py:263
  114.8 3.6 %convolution_bitcast_fusion = f32[256,4096]{1,0:T(8,128)S(1)} fusion(bf16[8,80,4096]{2,1,0:T(8,128)(2,1)} %bitcast_dynamic-update-slice_fusion, bf16[8,256,64]{1,2,0:T(8,128)(2,1)S(1)} %gather_fusion.4, pred[8]{0:T(512)(128)(4,1)S(1)} %compare_and_fusion), kind=kOutput, calls=%fused_computation.11 | convolution fusion | flops 1073872896 | bytes 8650760 | tf_op jit(solution)/shard_map/dot_general | solution.py:266
  118.7 2.1 %copy.53 = f32[32,8,16,128]{3,2,1,0:T(8,128)} copy(f32[32,8,16,128]{3,1,2,0:T(8,128)S(1)} %multiply_bitcast_fusion) | data formatting | bytes 4194304
  121.0 2.2 %reduce_sum.57 = f32[256,16]{1,0:T(8,128)S(1)} reduce(f32[256,16,128]{2,1,0:T(8,128)} %bitcast.162, f32[]{:T(128)} %constant.180.clone.1), dimensions={2}, to_apply=%region_7.8 | reduce | flops 520192 | bytes 2113540 | tf_op jit(solution)/shard_map/reduce_sum | solution.py:29
  124.0 2.4 %fusion.8 = bf16[256,2048]{1,0:T(8,128)(2,1)S(1)} fusion(f32[32,8,16,128]{3,2,1,0:T(8,128)S(1)} %bitcast.160, f32[256,4096]{1,0:T(8,128)} %copy-done.2, f32[2048]{0:T(1024)S(1)} %broadcast_bitcast_fusion), kind=kLoop, calls=%fused_computation.16 | loop fusion | flops 1572864 | bytes 5251072 | tf_op jit(solution)/shard_map/convert.3
  128.5 1.5 collective-permute-start.10
  130.0 2.2 %collective-permute-done.10 = bf16[2,2,1,1,256]{4,2,1,0,3:T(2,128)(2,1)S(1)} collective-permute-done((bf16[2,2,1,1,256]{4,2,1,0,3:T(2,128)(2,1)S(1)}, bf16[2,2,1,1,256]{4,2,1,0,3:T(2,128)(2,1)S(1)}, u32[]{:S(2)}, u32[]{:S(2)}) %collective-permute-start.10) | collective-permute-done | bytes 2080 | tf_op jit(solution)/shard_map/ppermute | solution.py:73
  132.2 1.2 collective-permute-start.11
  133.4 2.4 %collective-permute-done.11 = bf16[2,1,2,1,256]{4,2,1,0,3:T(2,128)(2,1)S(1)} collective-permute-done((bf16[2,1,2,1,256]{4,2,1,0,3:T(2,128)(2,1)S(1)}, bf16[2,1,2,1,256]{4,2,1,0,3:T(2,128)(2,1)S(1)}, u32[]{:S(2)}, u32[]{:S(2)}) %collective-permute-start.11) | collective-permute-done | bytes 2080 | tf_op jit(solution)/shard_map/ppermute | solution.py:73
  135.9 2.5 %collective-permute-start.12 = (bf16[1,2,2,1,256]{4,2,1,0,3:T(2,128)(2,1)S(1)}, bf16[1,2,2,1,256]{4,2,1,0,3:T(2,128)(2,1)S(1)}, u32[]{:S(2)}, u32[]{:S(2)}) collective-permute-start(bf16[1,2,2,1,256]{4,2,1,0,3:T(2,128)(2,1)S(1)} %get-tuple-element.32), channel_id=1, source_target_pairs={{0,4},{1,5},{2,6},{3,7},{4,0},{5,1},{6,2},{7,3},{8,12},{9,13},{10,... | collective-permute-start | bytes 6152 | tf_op jit(solution)/shard_map/ppermute | solution.py:73
  138.4 2.0 %collective-permute-done.12 = bf16[1,2,2,1,256]{4,2,1,0,3:T(2,128)(2,1)S(1)} collective-permute-done((bf16[1,2,2,1,256]{4,2,1,0,3:T(2,128)(2,1)S(1)}, bf16[1,2,2,1,256]{4,2,1,0,3:T(2,128)(2,1)S(1)}, u32[]{:S(2)}, u32[]{:S(2)}) %collective-permute-start.12) | collective-permute-done | bytes 2080 | tf_op jit(solution)/shard_map/ppermute | solution.py:73
  140.9 1.4 collective-permute-start.13
  142.3 3.5 %collective-permute-done.13 = f32[8,1,4096]{2,0,1:T(8,128)S(1)} collective-permute-done((f32[8,1,4096]{2,0,1:T(8,128)S(1)}, f32[8,1,4096]{2,0,1:T(8,128)S(1)}, u32[]{:S(2)}, u32[]{:S(2)}) %collective-permute-start.13) | collective-permute-done | bytes 131104 | tf_op jit(solution)/shard_map/ppermute | solution.py:114
  145.9 1.2 collective-permute-start.14
  147.1 3.8 %collective-permute-done.14 = f32[8,1,4096]{2,0,1:T(8,128)S(1)} collective-permute-done((f32[8,1,4096]{2,0,1:T(8,128)S(1)}, f32[8,1,4096]{2,0,1:T(8,128)S(1)}, u32[]{:S(2)}, u32[]{:S(2)}) %collective-permute-start.14) | collective-permute-done | bytes 131104 | tf_op jit(solution)/shard_map/ppermute | solution.py:114
  150.9 2.5 %collective-permute-start.15 = (f32[8,1,4096]{2,0,1:T(8,128)S(1)}, f32[8,1,4096]{2,0,1:T(8,128)S(1)}, u32[]{:S(2)}, u32[]{:S(2)}) collective-permute-start(f32[8,1,4096]{2,0,1:T(8,128)S(1)} %add.236), channel_id=1, source_target_pairs={{0,4},{1,5},{2,6},{3,7},{4,0},{5,1},{6,2},{7,3},{8,12},{9,13},{10,... | collective-permute-start | bytes 393224 | tf_op jit(solution)/shard_map/ppermute | solution.py:114
  153.5 4.7 %collective-permute-done.15 = f32[8,1,4096]{2,0,1:T(8,128)S(1)} collective-permute-done((f32[8,1,4096]{2,0,1:T(8,128)S(1)}, f32[8,1,4096]{2,0,1:T(8,128)S(1)}, u32[]{:S(2)}, u32[]{:S(2)}) %collective-permute-start.15) | collective-permute-done | bytes 131104 | tf_op jit(solution)/shard_map/ppermute | solution.py:114
  158.4 5.1 %fusion.4 = f32[8,896]{1,0:T(8,128)S(1)} fusion(bf16[1,896,4096]{2,1,0:T(8,128)(2,1)} %param.28, f32[8,1,4096]{2,0,1:T(8,128)S(1)} %get-tuple-element.24, f32[4096]{0:T(1024)S(1)} %bitcast.169, f32[8]{0:T(128)S(1)} %add_rsqrt_fusion.1), kind=kOutput, calls=%fused_computation.9 | convolution fusion | flops 58818560 | bytes 7516192 | tf_op jit(solution)/shard_map/dot_general | solution.py:21
  163.5 5.1 %fusion.15 = bf16[8,896]{1,0:T(8,128)(2,1)S(1)} fusion(bf16[1,896,4096]{2,1,0:T(8,128)(2,1)} %param.29, f32[8,896]{1,0:T(8,128)S(1)} %fusion.4, f32[8,1,4096]{2,0,1:T(8,128)S(1)} %get-tuple-element.24, f32[4096]{0:T(1024)S(1)} %bitcast.170, f32[8]{0:T(128)S(1)} %add_rsqrt_fusion.1), kind=kOutput, calls=%fused_computation.24 | convolution fusion | flops 58861568 | bytes 7530528 | tf_op jit(solution)/shard_map/dot_general | solution.py:21
  168.6 4.2 %fusion = f32[2,2,2,4096]{3,2,1,0:T(2,128)S(1)} fusion(bf16[2,2,2,896]{3,2,1,0:T(2,128)(2,1)S(1)} %dot_general.37, bf16[1,896,4096]{2,1,0:T(8,128)(2,1)} %param.30), kind=kOutput, calls=%fused_computation.5 | convolution fusion | flops 58720256 | bytes 7485440 | tf_op jit(solution)/shard_map/dot_general | solution.py:304
  172.9 1.5 collective-permute-start.16
  174.4 2.8 %collective-permute-done.16 = f32[2,2,1,1,4096]{4,2,3,1,0:T(1,128)S(1)} collective-permute-done((f32[2,2,1,1,4096]{4,2,3,1,0:T(1,128)S(1)}, f32[2,2,1,1,4096]{4,2,3,1,0:T(1,128)S(1)}, u32[]{:S(2)}, u32[]{:S(2)}) %collective-permute-start.16) | collective-permute-done | bytes 65568 | tf_op jit(solution)/shard_map/ppermute | solution.py:319
  177.6 3.7 %collective-permute-done.17 = f32[2,1,1,1,4096]{4,2,3,1,0:T(1,128)S(1)} collective-permute-done((f32[2,1,1,1,4096]{4,2,3,1,0:T(1,128)S(1)}, f32[2,1,1,1,4096]{4,2,3,1,0:T(1,128)S(1)}, u32[]{:S(2)}, u32[]{:S(2)}) %collective-permute-start.17) | collective-permute-done | bytes 32800 | tf_op jit(solution)/shard_map/ppermute | solution.py:319
  181.5 2.8 %collective-permute-start.19 = (f32[1,4096]{1,0:T(1,128)S(1)}, f32[1,4096]{1,0:T(1,128)S(1)}, u32[]{:S(2)}, u32[]{:S(2)}) collective-permute-start(f32[1,4096]{1,0:T(1,128)S(1)} %dynamic-slice_bitcast_fusion.1), channel_id=1, source_target_pairs={{0,12},{1,13},{2,14},{3,15},{4,8},{5,9},{6,10},{7,11},{8,20},{9,21... | collective-permute-start | bytes 49160 | tf_op jit(solution)/shard_map/ppermute | solution.py:336
  184.7 1.9 collective-permute-done.19
  (111 shorter events, 14.5 us)
Async XLA Ops:
  0.0 140.5 %copy-start = (bf16[1,256,4096]{2,1,0:T(8,128)(2,1)S(1)}, bf16[1,256,4096]{2,1,0:T(8,128)(2,1)}, u32[]{:S(2)}) copy-start(bf16[1,256,4096]{2,1,0:T(8,128)(2,1)} %param.26) | copy-start | bytes 6291460
  0.0 20.2 %copy-start.1 = (bf16[1,256,1024]{2,1,0:T(8,128)(2,1)S(1)}, bf16[1,256,1024]{2,1,0:T(8,128)(2,1)}, u32[]{:S(2)}) copy-start(bf16[1,256,1024]{2,1,0:T(8,128)(2,1)} %param.18) | copy-start | bytes 1572868
  3.1 22.3 %collective-permute-start = (bf16[80,4096]{1,0:T(8,128)(2,1)}, bf16[80,4096]{1,0:T(8,128)(2,1)}, u32[]{:S(2)}, u32[]{:S(2)}) collective-permute-start(bf16[80,4096]{1,0:T(8,128)(2,1)} %pad_maximum_fusion.1), channel_id=1, source_target_pairs={{0,2},{2,4},{4,6},{6,7},{7,5},{5,3},{3,1},{1,0},{8,10},{10,12},{12... | collective-permute-start | bytes 1966088 | tf_op jit(solution)/shard_map/ppermute | solution.py:149
  6.1 19.3 %collective-permute-start.1 = (bf16[80,4096]{1,0:T(8,128)(2,1)}, bf16[80,4096]{1,0:T(8,128)(2,1)}, u32[]{:S(2)}, u32[]{:S(2)}) collective-permute-start(bf16[80,4096]{1,0:T(8,128)(2,1)} %pad_maximum_fusion.1), channel_id=1, source_target_pairs={{0,1},{2,0},{4,2},{6,4},{7,6},{5,7},{3,5},{1,3},{8,9},{10,8},{12,1... | collective-permute-start | bytes 1966088 | tf_op jit(solution)/shard_map/ppermute | solution.py:153
  20.2 12.0 %copy-start.6 = (f32[1,128]{1,0:T(1,128)S(1)}, f32[1,128]{1,0:T(1,128)}, u32[]{:S(2)}) copy-start(f32[1,128]{1,0:T(1,128)} %param.23) | copy-start | bytes 1540
  25.4 27.8 %all-to-all-start = ((bf16[8,44,1024]{2,1,0:T(8,128)(2,1)}), bf16[8,44,1024]{2,1,0:T(8,128)(2,1)S(1)}, u32[]{:S(2)}, u32[]{:S(2)}) async-start(bf16[8,44,1024]{2,1,0:T(8,128)(2,1)} %pad_maximum_fusion), calls=%async_computation | async-start | bytes 1572864 | tf_op jit(solution)/shard_map/all_to_all | solution.py:232
  32.2 25.9 %collective-permute-start.2 = (bf16[80,4096]{1,0:T(8,128)(2,1)}, bf16[80,4096]{1,0:T(8,128)(2,1)}, u32[]{:S(2)}, u32[]{:S(2)}) collective-permute-start(bf16[80,4096]{1,0:T(8,128)(2,1)} %collective-permute-done), channel_id=1, source_target_pairs={{0,2},{2,4},{4,6},{6,7},{7,5},{5,3},{3,1},{1,0},{8,10},{10,12},{12... | collective-permute-start | bytes 1966088 | tf_op jit(solution)/shard_map/ppermute | solution.py:149
  34.3 26.0 %collective-permute-start.3 = (bf16[80,4096]{1,0:T(8,128)(2,1)}, bf16[80,4096]{1,0:T(8,128)(2,1)}, u32[]{:S(2)}, u32[]{:S(2)}) collective-permute-start(bf16[80,4096]{1,0:T(8,128)(2,1)} %collective-permute-done.1), channel_id=1, source_target_pairs={{0,1},{2,0},{4,2},{6,4},{7,6},{5,7},{3,5},{1,3},{8,9},{10,8},{12,1... | collective-permute-start | bytes 1966088 | tf_op jit(solution)/shard_map/ppermute | solution.py:153
  60.2 28.4 %collective-permute-start.4 = (bf16[80,4096]{1,0:T(8,128)(2,1)}, bf16[80,4096]{1,0:T(8,128)(2,1)}, u32[]{:S(2)}, u32[]{:S(2)}) collective-permute-start(bf16[80,4096]{1,0:T(8,128)(2,1)} %collective-permute-done.2), channel_id=1, source_target_pairs={{0,2},{2,4},{4,6},{6,7},{7,5},{5,3},{3,1},{1,0},{8,10},{10,12},{12... | collective-permute-start | bytes 1966088 | tf_op jit(solution)/shard_map/ppermute | solution.py:149
  66.6 9.4 %collective-permute-start.6 = (bf16[2,2,1,1,256]{4,2,1,0,3:T(2,128)(2,1)}, bf16[2,2,1,1,256]{4,2,1,0,3:T(2,128)(2,1)}, u32[]{:S(2)}, u32[]{:S(2)}) collective-permute-start(bf16[2,2,1,1,256]{4,2,1,0,3:T(2,128)(2,1)} %get-tuple-element.42), channel_id=1, source_target_pairs={{0,1},{1,0},{2,3},{3,2},{4,5},{5,4},{6,7},{7,6},{8,9},{9,8},{10,11... | collective-permute-start | bytes 6152 | tf_op jit(solution)/shard_map/ppermute | solution.py:73
  68.6 20.0 %collective-permute-start.5 = (bf16[80,4096]{1,0:T(8,128)(2,1)}, bf16[80,4096]{1,0:T(8,128)(2,1)}, u32[]{:S(2)}, u32[]{:S(2)}) collective-permute-start(bf16[80,4096]{1,0:T(8,128)(2,1)} %collective-permute-done.3), channel_id=1, source_target_pairs={{0,1},{2,0},{4,2},{6,4},{7,6},{5,7},{3,5},{1,3},{8,9},{10,8},{12,1... | collective-permute-start | bytes 1966088 | tf_op jit(solution)/shard_map/ppermute | solution.py:153
  70.7 18.3 %copy-start.7 = (f32[1,128]{1,0:T(1,128)S(1)}, f32[1,128]{1,0:T(1,128)}, u32[]{:S(2)}) copy-start(f32[1,128]{1,0:T(1,128)} %param.22) | copy-start | bytes 1540
  76.8 7.1 %collective-permute-start.7 = (bf16[2,1,2,1,256]{4,2,1,0,3:T(2,128)(2,1)S(1)}, bf16[2,1,2,1,256]{4,2,1,0,3:T(2,128)(2,1)S(1)}, u32[]{:S(2)}, u32[]{:S(2)}) collective-permute-start(bf16[2,1,2,1,256]{4,2,1,0,3:T(2,128)(2,1)S(1)} %get-tuple-element.40), channel_id=1, source_target_pairs={{0,2},{1,3},{2,0},{3,1},{4,6},{5,7},{6,4},{7,5},{8,10},{9,11},{10,... | collective-permute-start | bytes 6152 | tf_op jit(solution)/shard_map/ppermute | solution.py:73
  84.0 4.6 %collective-permute-start.8 = (bf16[1,2,2,1,256]{4,2,1,0,3:T(2,128)(2,1)S(1)}, bf16[1,2,2,1,256]{4,2,1,0,3:T(2,128)(2,1)S(1)}, u32[]{:S(2)}, u32[]{:S(2)}) collective-permute-start(bf16[1,2,2,1,256]{4,2,1,0,3:T(2,128)(2,1)S(1)} %get-tuple-element.38), channel_id=1, source_target_pairs={{0,4},{1,5},{2,6},{3,7},{4,0},{5,1},{6,2},{7,3},{8,12},{9,13},{10,... | collective-permute-start | bytes 6152 | tf_op jit(solution)/shard_map/ppermute | solution.py:73
  88.7 14.0 %collective-permute-start.9 = (bf16[80,4096]{1,0:T(8,128)(2,1)}, bf16[80,4096]{1,0:T(8,128)(2,1)S(1)}, u32[]{:S(2)}, u32[]{:S(2)}) collective-permute-start(bf16[80,4096]{1,0:T(8,128)(2,1)} %collective-permute-done.4), channel_id=1, source_target_pairs={{0,2},{2,4},{4,6},{6,7},{7,5},{5,3},{3,1},{1,0},{8,10},{10,12},{12... | collective-permute-start | bytes 1966088 | tf_op jit(solution)/shard_map/ppermute | solution.py:149
  118.4 2.6 %copy-start.2 = (f32[256,4096]{1,0:T(8,128)}, f32[256,4096]{1,0:T(8,128)S(1)}, u32[]{:S(2)}) copy-start(f32[256,4096]{1,0:T(8,128)S(1)} %convolution_bitcast_fusion) | copy-start | bytes 12582916
  126.6 1.3 copy-start.5
  127.1 26.3 %copy-start.3 = (f32[8,4,1024]{2,1,0:T(4,128)S(1)}, f32[8,4,1024]{2,1,0:T(4,128)}, u32[]{:S(2)}) copy-start(f32[8,4,1024]{2,1,0:T(4,128)} %get-tuple-element.30) | copy-start | bytes 393220
  127.1 31.3 %copy-start.4 = (f32[1,4096]{1,0:T(1,128)S(1)}, f32[1,4096]{1,0:T(1,128)}, u32[]{:S(2)}) copy-start(f32[1,4096]{1,0:T(1,128)} %param.27) | copy-start | bytes 49156
  128.5 3.7 %collective-permute-start.10 = (bf16[2,2,1,1,256]{4,2,1,0,3:T(2,128)(2,1)S(1)}, bf16[2,2,1,1,256]{4,2,1,0,3:T(2,128)(2,1)S(1)}, u32[]{:S(2)}, u32[]{:S(2)}) collective-permute-start(bf16[2,2,1,1,256]{4,2,1,0,3:T(2,128)(2,1)S(1)} %get-tuple-element.36), channel_id=1, source_target_pairs={{0,1},{1,0},{2,3},{3,2},{4,5},{5,4},{6,7},{7,6},{8,9},{9,8},{10,11... | collective-permute-start | bytes 6152 | tf_op jit(solution)/shard_map/ppermute | solution.py:73
  132.2 3.7 %collective-permute-start.11 = (bf16[2,1,2,1,256]{4,2,1,0,3:T(2,128)(2,1)S(1)}, bf16[2,1,2,1,256]{4,2,1,0,3:T(2,128)(2,1)S(1)}, u32[]{:S(2)}, u32[]{:S(2)}) collective-permute-start(bf16[2,1,2,1,256]{4,2,1,0,3:T(2,128)(2,1)S(1)} %get-tuple-element.34), channel_id=1, source_target_pairs={{0,2},{1,3},{2,0},{3,1},{4,6},{5,7},{6,4},{7,5},{8,10},{9,11},{10,... | collective-permute-start | bytes 6152 | tf_op jit(solution)/shard_map/ppermute | solution.py:73
  135.9 4.5 %collective-permute-start.12 = (bf16[1,2,2,1,256]{4,2,1,0,3:T(2,128)(2,1)S(1)}, bf16[1,2,2,1,256]{4,2,1,0,3:T(2,128)(2,1)S(1)}, u32[]{:S(2)}, u32[]{:S(2)}) collective-permute-start(bf16[1,2,2,1,256]{4,2,1,0,3:T(2,128)(2,1)S(1)} %get-tuple-element.32), channel_id=1, source_target_pairs={{0,4},{1,5},{2,6},{3,7},{4,0},{5,1},{6,2},{7,3},{8,12},{9,13},{10,... | collective-permute-start | bytes 6152 | tf_op jit(solution)/shard_map/ppermute | solution.py:73
  140.9 5.0 %collective-permute-start.13 = (f32[8,1,4096]{2,0,1:T(8,128)S(1)}, f32[8,1,4096]{2,0,1:T(8,128)S(1)}, u32[]{:S(2)}, u32[]{:S(2)}) collective-permute-start(f32[8,1,4096]{2,0,1:T(8,128)S(1)} %convolution_bitcast_fusion.1), channel_id=1, source_target_pairs={{0,1},{1,0},{2,3},{3,2},{4,5},{5,4},{6,7},{7,6},{8,9},{9,8},{10,11... | collective-permute-start | bytes 393224 | tf_op jit(solution)/shard_map/ppermute | solution.py:114
  145.9 5.0 %collective-permute-start.14 = (f32[8,1,4096]{2,0,1:T(8,128)S(1)}, f32[8,1,4096]{2,0,1:T(8,128)S(1)}, u32[]{:S(2)}, u32[]{:S(2)}) collective-permute-start(f32[8,1,4096]{2,0,1:T(8,128)S(1)} %add.235), channel_id=1, source_target_pairs={{0,2},{1,3},{2,0},{3,1},{4,6},{5,7},{6,4},{7,5},{8,10},{9,11},{10,... | collective-permute-start | bytes 393224 | tf_op jit(solution)/shard_map/ppermute | solution.py:114
  150.9 7.3 %collective-permute-start.15 = (f32[8,1,4096]{2,0,1:T(8,128)S(1)}, f32[8,1,4096]{2,0,1:T(8,128)S(1)}, u32[]{:S(2)}, u32[]{:S(2)}) collective-permute-start(f32[8,1,4096]{2,0,1:T(8,128)S(1)} %add.236), channel_id=1, source_target_pairs={{0,4},{1,5},{2,6},{3,7},{4,0},{5,1},{6,2},{7,3},{8,12},{9,13},{10,... | collective-permute-start | bytes 393224 | tf_op jit(solution)/shard_map/ppermute | solution.py:114
  172.9 4.3 %collective-permute-start.16 = (f32[2,2,1,1,4096]{4,2,3,1,0:T(1,128)S(1)}, f32[2,2,1,1,4096]{4,2,3,1,0:T(1,128)S(1)}, u32[]{:S(2)}, u32[]{:S(2)}) collective-permute-start(f32[2,2,1,1,4096]{4,2,3,1,0:T(1,128)S(1)} %dynamic-slice_bitcast_fusion), channel_id=1, source_target_pairs={{0,1},{1,0},{2,3},{3,2},{4,5},{5,4},{6,7},{7,6},{8,9},{9,8},{10,11... | collective-permute-start | bytes 196616 | tf_op jit(solution)/shard_map/ppermute | solution.py:319
  177.4 4.0 %collective-permute-start.17 = (f32[2,1,1,1,4096]{4,2,3,1,0:T(1,128)S(1)}, f32[2,1,1,1,4096]{4,2,3,1,0:T(1,128)S(1)}, u32[]{:S(2)}, u32[]{:S(2)}) collective-permute-start(f32[2,1,1,1,4096]{4,2,3,1,0:T(1,128)S(1)} %constant_dynamic-slice_fusion), channel_id=1, source_target_pairs={{0,2},{1,3},{2,0},{3,1},{4,6},{5,7},{6,4},{7,5},{8,10},{9,11},{10,... | collective-permute-start | bytes 98312 | tf_op jit(solution)/shard_map/ppermute | solution.py:319
  181.4 3.2 %collective-permute-start.18 = (f32[1,4096]{1,0:T(1,128)S(1)}, f32[1,4096]{1,0:T(1,128)S(1)}, u32[]{:S(2)}, u32[]{:S(2)}) collective-permute-start(f32[1,4096]{1,0:T(1,128)S(1)} %bitcast_add_fusion.1), channel_id=1, source_target_pairs={{0,8},{1,9},{2,10},{3,11},{4,12},{5,13},{6,14},{7,15},{8,16},{9,17... | collective-permute-start | bytes 49160 | tf_op jit(solution)/shard_map/ppermute | solution.py:335
  181.5 5.0 %collective-permute-start.19 = (f32[1,4096]{1,0:T(1,128)S(1)}, f32[1,4096]{1,0:T(1,128)S(1)}, u32[]{:S(2)}, u32[]{:S(2)}) collective-permute-start(f32[1,4096]{1,0:T(1,128)S(1)} %dynamic-slice_bitcast_fusion.1), channel_id=1, source_target_pairs={{0,12},{1,13},{2,14},{3,15},{4,8},{5,9},{6,10},{7,11},{8,20},{9,21... | collective-permute-start | bytes 49160 | tf_op jit(solution)/shard_map/ppermute | solution.py:336

commit v4 on v3

--- a/solution.py
+++ b/solution.py
@@ -164,6 +164,23 @@
         self._issue()
         return tied
 
+    def slots_in_arrival(self):
+        if not self.direct:
+            return [self.slots[i] for i in range(self.count)], [self.sources[i] for i in range(self.count)]
+        while self.forward_left > 0 or self.backward_left > 0:
+            self._issue()
+        slots = [self.value]
+        positions = [0]
+        forward_count = len(self.forward_slots)
+        for step in range(max(forward_count, len(self.backward_slots))):
+            if step < forward_count:
+                slots.append(self.forward_slots[step])
+                positions.append(1 + step)
+            if step < len(self.backward_slots):
+                slots.append(self.backward_slots[step])
+                positions.append(1 + forward_count + step)
+        return slots, [self.sources[p] for p in positions]
+
     def finish(self):
         if not self.direct:
             return self.slots, self.sources
@@ -202,12 +219,16 @@
     model_width = current.shape[-1]
     row_width = patches.shape[-1]
 
-    width_in = tile_in.shape[-1]
-    in_rows = tile_in.shape[1] * width_in // tile_out.shape[-1]
-    packed_weights = jnp.concatenate(
-        [tile_in[0].reshape(in_rows, tile_out.shape[-1]), tile_out[0]], axis=0
-    )
-    ring = RingGather(packed_weights, group_size, my_index)
+    ring_in = RingGather(tile_in[0], group_size, my_index)
+    in_slots, in_sources = ring_in.finish()
+    ring_out = RingGather(tile_out[0], group_size, my_index)
+    weight_in = in_slots.reshape(-1, in_slots.shape[-1])
+    own_rows = jnp.take(patches[0].reshape(tiles_here, group_size, -1), in_sources, axis=1)
+    tile_hidden = jax.nn.gelu(
+        jnp.dot(own_rows.reshape(tiles_here, -1), weight_in, preferred_element_type=jnp.float32),
+        approximate=True,
+    ).astype(jnp.bfloat16)
+    hidden_width = tile_hidden.shape[-1]
 
     slot_index = jnp.arange(list_width, dtype=jnp.int32)
     live_all = (slot_index[None, :] < site_count[:, None]).reshape(group_size, entries)
@@ -220,15 +241,15 @@
         slot_rank[:, :, None] == jnp.arange(capacity, dtype=jnp.int32)[None, None, :],
     )
     send_index = jnp.sum(jnp.where(picks, local_all[:, :, None], 0), axis=1)
-    send_rows = patches[0][send_index.reshape(-1)].reshape(group_size, capacity, row_width)
-    act_rows = sites_here * model_width // row_width
-    packed = model_width % row_width == 0
+    send_rows = tile_hidden[send_index.reshape(-1)].reshape(group_size, capacity, hidden_width)
+    act_rows = sites_here * model_width // hidden_width
+    packed = model_width % hidden_width == 0
     if packed:
         act_block = jnp.broadcast_to(
-            current.reshape(1, act_rows, row_width), (group_size, act_rows, row_width)
+            current.reshape(1, act_rows, hidden_width), (group_size, act_rows, hidden_width)
         )
         send_rows = jnp.concatenate([send_rows, act_block], axis=1)
-    send_rows = ring.step(send_rows)
+    send_rows = ring_out.step(send_rows)
     arrived = lax.all_to_all(send_rows, "site", split_axis=0, concat_axis=0, tiled=True)
     if packed:
         everyone = arrived[:, capacity:].reshape(-1, model_width)
@@ -236,14 +257,11 @@
     else:
         everyone = doubling_gather(current, group_size, my_index).reshape(-1, model_width)
     q_part = by_rows(everyone, q_weight[0]).astype(jnp.bfloat16)
-    q_part = ring.step(q_part)
+    q_part = ring_out.step(q_part)
     q_blocks = halving_exchange(
         q_part.reshape(group_size, sites_here, -1), group_size, my_index
     )
-    q_blocks = ring.step(q_blocks)
-    weight_slots, source_of_slot = ring.finish()
-    weight_in = weight_slots[:, :in_rows].reshape(-1, width_in)
-    weight_out = weight_slots[:, in_rows:].reshape(-1, weight_slots.shape[-1])
+    q_blocks = ring_out.step(q_blocks)
 
     my_tiles = lax.dynamic_slice_in_dim(site_tiles, my_index * sites_here, sites_here, 0)
     my_count = lax.dynamic_slice_in_dim(site_count, my_index * sites_here, sites_here, 0)
@@ -255,15 +273,19 @@
     ).astype(jnp.int32)
     my_rank = jnp.sum(jnp.cumsum(one_hot, axis=0) * one_hot, axis=1) - 1
     fetch_index = jnp.where(my_live.reshape(-1), my_owner * capacity + my_rank, 0)
-    pair_rows = arrived.reshape(group_size * capacity, row_width)[fetch_index]
-
-    rows_in = pair_rows.reshape(entries, group_size, -1)
-    rows_in = jnp.take(rows_in, source_of_slot, axis=1).reshape(entries, -1)
-    hidden = jax.nn.gelu(
-        jnp.dot(rows_in, weight_in, preferred_element_type=jnp.float32), approximate=True
-    ).astype(jnp.bfloat16)
-    hidden = jnp.take(hidden.reshape(entries, group_size, -1), source_of_slot, axis=1)
-    keyval = jnp.dot(hidden.reshape(entries, -1), weight_out, preferred_element_type=jnp.float32)
+    pair_hidden = arrived.reshape(group_size * capacity, hidden_width)[fetch_index]
+
+    shard_rows = tile_out.shape[1]
+    keyval = None
+    if not ring_out.direct:
+        out_slots, out_sources = [ring_out.slots.reshape(-1, ring_out.slots.shape[-1])], [0]
+        shard_rows = hidden_width
+    else:
+        out_slots, out_sources = ring_out.slots_in_arrival()
+    for slot, source in zip(out_slots, out_sources):
+        columns_here = lax.dynamic_slice_in_dim(pair_hidden, source * shard_rows, shard_rows, 1)
+        term = jnp.dot(columns_here, slot, preferred_element_type=jnp.float32)
+        keyval = term if keyval is None else keyval + term
     half_width = keyval.shape[1] // 2
     normed_keys = head_norm(keyval[:, :half_width], k_gain[0])
     pair_kv = jnp.concatenate([normed_keys, keyval[:, half_width:]], axis=1).astype(jnp.bfloat16)

time: 189 us -> 175 us (0.926)
  waiting for transfers between devices: 70.5 us -> 45.4 us
  matrix products: 23.2 us -> 41.9 us
  local copies, waits for them, and re-layouts: 32.2 us -> 15.8 us
  starting transfers between devices: 37.5 us -> 49.2 us
  other arithmetic: 23.3 us -> 15.8 us
  between operations: 0.46 us -> 5.52 us
    dot_general x2 -> x9, matrix products: 5.53 us -> 24.2 us  [the longest x8 23.6 us: shards(): term = jnp.dot(columns_here, slot, preferred_element_type=jnp.float32)]
    all_to_all x1, waiting for transfers between devices: 16.9 us -> 2.62 us  [shards(): lax.all_to_all(send_rows, 'site', split_axis=0, concat_axis=0, tiled=True)]
    ppermute x6, waiting for transfers between devices: 17.1 us -> 7.91 us  [halving_exchange(): recv = lax.ppermute(send, 'site', xor_pairs(count, bit))]
    unnamed x25 -> x27, local copies, waits for them, and re-layouts: 13.6 us -> 5.1 us
    ppermute x6, starting transfers between devices: 8.3 us -> 14.2 us  [halving_exchange(): recv = lax.ppermute(send, 'site', xor_pairs(count, bit))]
    ppermute x1, starting transfers between devices: 0.06 us -> 3.43 us  [shards(): mine_part = lax.ppermute(own, ('section', 'site'), forward)]
    ppermute x1, starting transfers between devices: 2.78 us -> 0.06 us  [shards(): other_part = lax.ppermute(send.reshape(rest), ('section', 'site'), across)]
    unnamed x5 -> x4, other arithmetic: 3.7 us -> 1.11 us
  transfers between devices with their start and end apart: 21 -> 28, of which waited for: 17 -> 18; matrix products, arithmetic and copies ran while one was open for 18% -> 23% of each run, Pallas kernels for 0% -> 0%
where the time goes in v4:
time: 175 us; the launch traced here: 174 us
  starting transfers between devices  49.2 us (28%)
  waiting for transfers between devices  45.4 us (26%)
  matrix products  41.9 us (24%)
  local copies, waits for them, and re-layouts  15.8 us (9%)
  other arithmetic  15.8 us (9%)
  between operations  5.52 us (3%)
    dot_general x8, matrix products, shards(): term = jnp.dot(columns_here, slot, preferred_element_type=jnp.float32)  23.6 us
    ppermute x8, waiting for transfers between devices, _issue(): self.ahead = lax.ppermute(self.ahead, 'site', self.forward)  14.9 us
    ppermute x6, starting transfers between devices, halving_exchange(): recv = lax.ppermute(send, 'site', xor_pairs(count, bit))  14.2 us
    ppermute x8, starting transfers between devices, _issue(): self.ahead = lax.ppermute(self.ahead, 'site', self.forward)  13.5 us
    dot_general x3, matrix products, by_rows(): lax.dot_general(left, weight_rows, (((1,), (1,)), ((), ())), preferred_el...  12.4 us
    ppermute x3, waiting for transfers between devices, doubling_sum(): state = state + lax.ppermute(state, 'site', xor_pairs(count, bit))  10.7 us
    ppermute x6, waiting for transfers between devices, halving_exchange(): recv = lax.ppermute(send, 'site', xor_pairs(count, bit))  7.91 us
    ppermute x3, starting transfers between devices, doubling_sum(): state = state + lax.ppermute(state, 'site', xor_pairs(count, bit))  6.6 us
  transfers between devices with their start and end apart: 28, of which 18 were waited for; matrix products, arithmetic and copies ran while one was open for 23% of the time, Pallas kernels for 0%

profile of v4, /device:TPU:0, one launch (start us, length us, event | category | flops | bytes accessed | tf_op | source)
XLA Modules:
  0.0 173.7 jit_solution(1185450426964816577)
XLA Ops:
  0.0 3.0 %collective-permute-start.2 = (bf16[128,512]{1,0:T(8,128)(2,1)}, bf16[128,512]{1,0:T(8,128)(2,1)S(1)}, u32[]{:S(2)}, u32[]{:S(2)}) collective-permute-start(bf16[128,512]{1,0:T(8,128)(2,1)} %bitcast.177), channel_id=1, source_target_pairs={{0,2},{2,4},{4,6},{6,7},{7,5},{5,3},{3,1},{1,0},{8,10},{10,12},{12... | collective-permute-start | bytes 393224 | tf_op jit(solution)/shard_map/ppermute | solution.py:149
  3.0 2.0 %collective-permute-start = (bf16[64,4096]{1,0:T(8,128)(2,1)}, bf16[64,4096]{1,0:T(8,128)(2,1)}, u32[]{:S(2)}, u32[]{:S(2)}) collective-permute-start(bf16[64,4096]{1,0:T(8,128)(2,1)} %bitcast.174), channel_id=1, source_target_pairs={{0,2},{2,4},{4,6},{6,7},{7,5},{5,3},{3,1},{1,0},{8,10},{10,12},{12... | collective-permute-start | bytes 1572872 | tf_op jit(solution)/shard_map/ppermute | solution.py:149
  5.1 1.3 dynamic_slice.107
  7.6 1.2 dynamic_slice.100
  8.9 1.3 compare_select_fusion.5
  10.2 1.3 gather_fusion
  12.2 0.8 convert_bitcast_fusion.1
  15.9 1.2 copy.36
  17.4 0.8 reduce.7
  18.9 0.9 constant_dynamic-update-slice_fusion
  19.8 2.1 %collective-permute-start.3 = (bf16[128,512]{1,0:T(8,128)(2,1)S(1)}, bf16[128,512]{1,0:T(8,128)(2,1)S(1)}, u32[]{:S(2)}, u32[]{:S(2)}) collective-permute-start(bf16[128,512]{1,0:T(8,128)(2,1)S(1)} %collective-permute-done.2), channel_id=1, source_target_pairs={{0,2},{2,4},{4,6},{6,7},{7,5},{5,3},{3,1},{1,0},{8,10},{10,12},{12... | collective-permute-start | bytes 393224 | tf_op jit(solution)/shard_map/ppermute | solution.py:149
  21.9 2.9 %collective-permute-done.3 = bf16[128,512]{1,0:T(8,128)(2,1)S(1)} collective-permute-done((bf16[128,512]{1,0:T(8,128)(2,1)S(1)}, bf16[128,512]{1,0:T(8,128)(2,1)S(1)}, u32[]{:S(2)}, u32[]{:S(2)}) %collective-permute-start.3) | collective-permute-done | bytes 131104 | tf_op jit(solution)/shard_map/ppermute | solution.py:149
  24.8 2.0 %collective-permute-start.4 = (bf16[128,512]{1,0:T(8,128)(2,1)S(1)}, bf16[128,512]{1,0:T(8,128)(2,1)S(1)}, u32[]{:S(2)}, u32[]{:S(2)}) collective-permute-start(bf16[128,512]{1,0:T(8,128)(2,1)S(1)} %collective-permute-done.3), channel_id=1, source_target_pairs={{0,2},{2,4},{4,6},{6,7},{7,5},{5,3},{3,1},{1,0},{8,10},{10,12},{12... | collective-permute-start | bytes 393224 | tf_op jit(solution)/shard_map/ppermute | solution.py:149
  26.9 3.3 %collective-permute-done.4 = bf16[128,512]{1,0:T(8,128)(2,1)S(1)} collective-permute-done((bf16[128,512]{1,0:T(8,128)(2,1)S(1)}, bf16[128,512]{1,0:T(8,128)(2,1)S(1)}, u32[]{:S(2)}, u32[]{:S(2)}) %collective-permute-start.4) | collective-permute-done | bytes 131104 | tf_op jit(solution)/shard_map/ppermute | solution.py:149
  30.2 2.3 %collective-permute-start.5 = (bf16[128,512]{1,0:T(8,128)(2,1)S(1)}, bf16[128,512]{1,0:T(8,128)(2,1)S(1)}, u32[]{:S(2)}, u32[]{:S(2)}) collective-permute-start(bf16[128,512]{1,0:T(8,128)(2,1)S(1)} %collective-permute-done.4), channel_id=1, source_target_pairs={{0,2},{2,4},{4,6},{6,7},{7,5},{5,3},{3,1},{1,0},{8,10},{10,12},{12... | collective-permute-start | bytes 393224 | tf_op jit(solution)/shard_map/ppermute | solution.py:149
  32.6 3.2 %collective-permute-done.5 = bf16[128,512]{1,0:T(8,128)(2,1)S(1)} collective-permute-done((bf16[128,512]{1,0:T(8,128)(2,1)S(1)}, bf16[128,512]{1,0:T(8,128)(2,1)S(1)}, u32[]{:S(2)}, u32[]{:S(2)}) %collective-permute-start.5) | collective-permute-done | bytes 131104 | tf_op jit(solution)/shard_map/ppermute | solution.py:149
  36.4 2.0 %gather_fusion.2 = bf16[320,512]{1,0:T(8,128)(2,1)S(1)} fusion(bf16[256,512]{1,0:T(8,128)(2,1)S(1)} %fusion.36, s32[1024]{0:T(1024)S(1)} %pad_clamp_fusion.1), kind=kCustom, calls=%fused_computation.2 | custom fusion | bytes 656640 | tf_op jit(solution)/shard_map/gather | solution.py:244
  38.5 0.8 pad_maximum_fusion
  39.3 6.3 %all-to-all-start = ((bf16[8,48,512]{2,1,0:T(8,128)(2,1)}), bf16[8,48,512]{2,1,0:T(8,128)(2,1)S(1)}, u32[]{:S(2)}, u32[]{:S(2)}) async-start(bf16[8,48,512]{2,1,0:T(8,128)(2,1)} %pad_maximum_fusion), calls=%async_computation | async-start | bytes 786432 | tf_op jit(solution)/shard_map/all_to_all | solution.py:253
  46.3 1.3 compare_select_fusion.1
  47.7 2.1 %collective-permute-start.10 = (bf16[64,4096]{1,0:T(8,128)(2,1)}, bf16[64,4096]{1,0:T(8,128)(2,1)}, u32[]{:S(2)}, u32[]{:S(2)}) collective-permute-start(bf16[64,4096]{1,0:T(8,128)(2,1)} %collective-permute-done.1), channel_id=1, source_target_pairs={{0,1},{2,0},{4,2},{6,4},{7,6},{5,7},{3,5},{1,3},{8,9},{10,8},{12,1... | collective-permute-start | bytes 1572872 | tf_op jit(solution)/shard_map/ppermute | solution.py:153
  54.8 2.6 %all-to-all-done = bf16[8,48,512]{2,1,0:T(8,128)(2,1)S(1)} async-done(((bf16[8,48,512]{2,1,0:T(8,128)(2,1)}), bf16[8,48,512]{2,1,0:T(8,128)(2,1)S(1)}, u32[]{:S(2)}, u32[]{:S(2)}) %all-to-all-start) | async-done | bytes 393248 | tf_op jit(solution)/shard_map/all_to_all | solution.py:253
  57.5 2.2 %fusion.22 = bf16[8,256]{1,0:T(8,128)(2,1)S(1)} fusion(bf16[8,4096]{1,0:T(8,128)(2,1)S(1)} %bitcast.176, bf16[1,256,4096]{2,1,0:T(8,128)(2,1)} %param.24), kind=kOutput, calls=%fused_computation.30 | convolution fusion | flops 16779264 | bytes 2166784 | tf_op jit(solution)/shard_map/dot_general | solution.py:21
  59.7 2.2 %collective-permute-done.10 = bf16[64,4096]{1,0:T(8,128)(2,1)} collective-permute-done((bf16[64,4096]{1,0:T(8,128)(2,1)}, bf16[64,4096]{1,0:T(8,128)(2,1)}, u32[]{:S(2)}, u32[]{:S(2)}) %collective-permute-start.10) | collective-permute-done | bytes 524320 | tf_op jit(solution)/shard_map/ppermute | solution.py:153
  61.9 2.1 %collective-permute-start.13 = (bf16[2,2,1,1,256]{4,2,1,0,3:T(2,128)(2,1)S(1)}, bf16[2,2,1,1,256]{4,2,1,0,3:T(2,128)(2,1)S(1)}, u32[]{:S(2)}, u32[]{:S(2)}) collective-permute-start(bf16[2,2,1,1,256]{4,2,1,0,3:T(2,128)(2,1)S(1)} %get-tuple-element.42), channel_id=1, source_target_pairs={{0,1},{1,0},{2,3},{3,2},{4,5},{5,4},{6,7},{7,6},{8,9},{9,8},{10,11... | collective-permute-start | bytes 6152 | tf_op jit(solution)/shard_map/ppermute | solution.py:73
  64.1 1.2 gather_fusion.3
  65.2 0.8 fusion.55
  66.0 3.8 %convolution_add_fusion.1 = f32[256,4096]{1,0:T(8,128)} fusion(f32[256,4096]{1,0:T(8,128)S(1)} %fusion.55, bf16[64,4096]{1,0:T(8,128)(2,1)} %collective-permute-done, bf16[256,512]{1,0:T(8,128)(2,1)S(1)} %gather_fusion.3, s32[]{:T(128)S(6)} %select_n.279), kind=kOutput, calls=%fused_computation.12 | convolution fusion | flops 135266304 | bytes 8978436 | tf_op jit(solution)/shard_map/dot_general | solution.py:287
  69.8 2.1 %collective-permute-start.14 = (bf16[2,1,2,1,256]{4,2,1,0,3:T(2,128)(2,1)S(1)}, bf16[2,1,2,1,256]{4,2,1,0,3:T(2,128)(2,1)S(1)}, u32[]{:S(2)}, u32[]{:S(2)}) collective-permute-start(bf16[2,1,2,1,256]{4,2,1,0,3:T(2,128)(2,1)S(1)} %get-tuple-element.40), channel_id=1, source_target_pairs={{0,2},{1,3},{2,0},{3,1},{4,6},{5,7},{6,4},{7,5},{8,10},{9,11},{10,... | collective-permute-start | bytes 6152 | tf_op jit(solution)/shard_map/ppermute | solution.py:73
  72.0 3.8 %fusion.49 = f32[256,4096]{1,0:T(8,128)} fusion(bf16[64,4096]{1,0:T(8,128)(2,1)} %collective-permute-done.10, bf16[256,512]{1,0:T(8,128)(2,1)S(1)} %gather_fusion.3, s32[]{:T(128)S(6)} %select_n.282), kind=kOutput, calls=%fused_computation.73 | convolution fusion | flops 134217728 | bytes 4784132 | tf_op jit(solution)/shard_map/dot_general | solution.py:287
  75.8 3.5 %collective-permute-start.15 = (bf16[1,2,2,1,256]{4,2,1,0,3:T(2,128)(2,1)S(1)}, bf16[1,2,2,1,256]{4,2,1,0,3:T(2,128)(2,1)S(1)}, u32[]{:S(2)}, u32[]{:S(2)}) collective-permute-start(bf16[1,2,2,1,256]{4,2,1,0,3:T(2,128)(2,1)S(1)} %get-tuple-element.38), channel_id=1, source_target_pairs={{0,4},{1,5},{2,6},{3,7},{4,0},{5,1},{6,2},{7,3},{8,12},{9,13},{10,... | collective-permute-start | bytes 6152 | tf_op jit(solution)/shard_map/ppermute | solution.py:73
  79.3 3.7 %fusion.51 = f32[256,4096]{1,0:T(8,128)} fusion(bf16[64,4096]{1,0:T(8,128)(2,1)} %collective-permute-done.9, bf16[256,512]{1,0:T(8,128)(2,1)S(1)} %gather_fusion.3, s32[]{:T(128)S(6)} %select_n.281), kind=kOutput, calls=%fused_computation.75 | convolution fusion | flops 134217728 | bytes 4784132 | tf_op jit(solution)/shard_map/dot_general | solution.py:287
  83.1 2.4 %collective-permute-done.15 = bf16[1,2,2,1,256]{4,2,1,0,3:T(2,128)(2,1)S(1)} collective-permute-done((bf16[1,2,2,1,256]{4,2,1,0,3:T(2,128)(2,1)S(1)}, bf16[1,2,2,1,256]{4,2,1,0,3:T(2,128)(2,1)S(1)}, u32[]{:S(2)}, u32[]{:S(2)}) %collective-permute-start.15) | collective-permute-done | bytes 2080 | tf_op jit(solution)/shard_map/ppermute | solution.py:73
  85.5 2.3 %collective-permute-done.11 = bf16[64,4096]{1,0:T(8,128)(2,1)S(1)} collective-permute-done((bf16[64,4096]{1,0:T(8,128)(2,1)}, bf16[64,4096]{1,0:T(8,128)(2,1)S(1)}, u32[]{:S(2)}, u32[]{:S(2)}) %collective-permute-start.11) | collective-permute-done | bytes 524320 | tf_op jit(solution)/shard_map/ppermute | solution.py:149
  87.8 1.9 %collective-permute-start.16 = (bf16[64,4096]{1,0:T(8,128)(2,1)S(1)}, bf16[64,4096]{1,0:T(8,128)(2,1)}, u32[]{:S(2)}, u32[]{:S(2)}) collective-permute-start(bf16[64,4096]{1,0:T(8,128)(2,1)S(1)} %collective-permute-done.11), channel_id=1, source_target_pairs={{0,2},{2,4},{4,6},{6,7},{7,5},{5,3},{3,1},{1,0},{8,10},{10,12},{12... | collective-permute-start | bytes 1572872 | tf_op jit(solution)/shard_map/ppermute | solution.py:149
  89.7 2.7 %fusion.47 = f32[256,4096]{1,0:T(8,128)} fusion(bf16[64,4096]{1,0:T(8,128)(2,1)S(1)} %collective-permute-done.11, bf16[256,512]{1,0:T(8,128)(2,1)S(1)} %gather_fusion.3, s32[]{:T(128)S(6)} %select_n.283), kind=kOutput, calls=%fused_computation.71 | convolution fusion | flops 134217728 | bytes 4784132 | tf_op jit(solution)/shard_map/dot_general | solution.py:287
  92.6 1.9 %fusion.45 = f32[256,4096]{1,0:T(8,128)S(1)} fusion(bf16[64,4096]{1,0:T(8,128)(2,1)} %collective-permute-done.12, bf16[256,512]{1,0:T(8,128)(2,1)S(1)} %gather_fusion.3, s32[]{:T(128)S(6)} %select_n.284), kind=kOutput, calls=%fused_computation.69 | convolution fusion | flops 134217728 | bytes 4784132 | tf_op jit(solution)/shard_map/dot_general | solution.py:287
  94.5 3.2 %collective-permute-done.16 = bf16[64,4096]{1,0:T(8,128)(2,1)} collective-permute-done((bf16[64,4096]{1,0:T(8,128)(2,1)S(1)}, bf16[64,4096]{1,0:T(8,128)(2,1)}, u32[]{:S(2)}, u32[]{:S(2)}) %collective-permute-start.16) | collective-permute-done | bytes 524320 | tf_op jit(solution)/shard_map/ppermute | solution.py:149
  97.7 1.8 %fusion.43 = f32[256,4096]{1,0:T(8,128)S(1)} fusion(bf16[64,4096]{1,0:T(8,128)(2,1)} %collective-permute-done.16, bf16[256,512]{1,0:T(8,128)(2,1)S(1)} %gather_fusion.3, s32[]{:T(128)S(6)} %select_n.285), kind=kOutput, calls=%fused_computation.67 | convolution fusion | flops 134217728 | bytes 4784132 | tf_op jit(solution)/shard_map/dot_general | solution.py:287
  99.5 5.2 %fusion.10 = f32[256,4096]{1,0:T(8,128)S(1)} fusion(f32[256,4096]{1,0:T(8,128)S(1)} %fusion.43, f32[256,4096]{1,0:T(8,128)S(1)} %fusion.45, f32[256,4096]{1,0:T(8,128)} %fusion.47, f32[256,4096]{1,0:T(8,128)S(1)} %copy-done.3, f32[256,4096]{1,0:T(8,128)} %fusion.51, f32[256,4096]{1,0:T(8,128)S(1)} %copy-done.2, ...), kind=kOutput, calls=%fused_computation.16 | convolution fusion | flops 140509184 | bytes 29949956 | tf_op jit(solution)/shard_map/dot_general | solution.py:287
  105.0 2.1 %copy.48 = f32[32,8,16,128]{3,2,1,0:T(8,128)} copy(f32[32,8,16,128]{3,1,2,0:T(8,128)S(1)} %multiply_bitcast_fusion) | data formatting | bytes 4194304
  107.4 2.2 %reduce_sum.57 = f32[256,16]{1,0:T(8,128)S(1)} reduce(f32[256,16,128]{2,1,0:T(8,128)} %bitcast.171, f32[]{:T(128)} %constant.189.clone.1), dimensions={2}, to_apply=%region_7.8 | reduce | flops 520192 | bytes 2113540 | tf_op jit(solution)/shard_map/reduce_sum | solution.py:29
  110.4 2.4 %fusion.12 = bf16[256,2048]{1,0:T(8,128)(2,1)S(1)} fusion(f32[32,8,16,128]{3,2,1,0:T(8,128)S(1)} %bitcast.169, f32[256,4096]{1,0:T(8,128)} %copy-done.1, f32[2048]{0:T(1024)S(1)} %broadcast_bitcast_fusion), kind=kLoop, calls=%fused_computation.20 | loop fusion | flops 1572864 | bytes 5251072 | tf_op jit(solution)/shard_map/convert.3
  114.8 2.1 %collective-permute-start.17 = (bf16[2,2,1,1,256]{4,2,1,0,3:T(2,128)(2,1)S(1)}, bf16[2,2,1,1,256]{4,2,1,0,3:T(2,128)(2,1)S(1)}, u32[]{:S(2)}, u32[]{:S(2)}) collective-permute-start(bf16[2,2,1,1,256]{4,2,1,0,3:T(2,128)(2,1)S(1)} %get-tuple-element.36), channel_id=1, source_target_pairs={{0,1},{1,0},{2,3},{3,2},{4,5},{5,4},{6,7},{7,6},{8,9},{9,8},{10,11... | collective-permute-start | bytes 6152 | tf_op jit(solution)/shard_map/ppermute | solution.py:73
  116.9 1.6 collective-permute-done.17
  118.6 1.3 collective-permute-start.18
  119.9 2.3 %collective-permute-done.18 = bf16[2,1,2,1,256]{4,2,1,0,3:T(2,128)(2,1)S(1)} collective-permute-done((bf16[2,1,2,1,256]{4,2,1,0,3:T(2,128)(2,1)S(1)}, bf16[2,1,2,1,256]{4,2,1,0,3:T(2,128)(2,1)S(1)}, u32[]{:S(2)}, u32[]{:S(2)}) %collective-permute-start.18) | collective-permute-done | bytes 2080 | tf_op jit(solution)/shard_map/ppermute | solution.py:73
  122.3 3.1 %collective-permute-start.19 = (bf16[1,2,2,1,256]{4,2,1,0,3:T(2,128)(2,1)S(1)}, bf16[1,2,2,1,256]{4,2,1,0,3:T(2,128)(2,1)S(1)}, u32[]{:S(2)}, u32[]{:S(2)}) collective-permute-start(bf16[1,2,2,1,256]{4,2,1,0,3:T(2,128)(2,1)S(1)} %get-tuple-element.32), channel_id=1, source_target_pairs={{0,4},{1,5},{2,6},{3,7},{4,0},{5,1},{6,2},{7,3},{8,12},{9,13},{10,... | collective-permute-start | bytes 6152 | tf_op jit(solution)/shard_map/ppermute | solution.py:73
  125.3 1.6 collective-permute-done.19
  127.3 1.9 %collective-permute-start.20 = (f32[8,1,4096]{2,0,1:T(8,128)S(1)}, f32[8,1,4096]{2,0,1:T(8,128)S(1)}, u32[]{:S(2)}, u32[]{:S(2)}) collective-permute-start(f32[8,1,4096]{2,0,1:T(8,128)S(1)} %convolution_bitcast_fusion), channel_id=1, source_target_pairs={{0,1},{1,0},{2,3},{3,2},{4,5},{5,4},{6,7},{7,6},{8,9},{9,8},{10,11... | collective-permute-start | bytes 393224 | tf_op jit(solution)/shard_map/ppermute | solution.py:114
  129.2 3.0 %collective-permute-done.20 = f32[8,1,4096]{2,0,1:T(8,128)S(1)} collective-permute-done((f32[8,1,4096]{2,0,1:T(8,128)S(1)}, f32[8,1,4096]{2,0,1:T(8,128)S(1)}, u32[]{:S(2)}, u32[]{:S(2)}) %collective-permute-start.20) | collective-permute-done | bytes 131104 | tf_op jit(solution)/shard_map/ppermute | solution.py:114
  132.3 1.7 collective-permute-start.21
  134.0 3.3 %collective-permute-done.21 = f32[8,1,4096]{2,0,1:T(8,128)S(1)} collective-permute-done((f32[8,1,4096]{2,0,1:T(8,128)S(1)}, f32[8,1,4096]{2,0,1:T(8,128)S(1)}, u32[]{:S(2)}, u32[]{:S(2)}) %collective-permute-start.21) | collective-permute-done | bytes 131104 | tf_op jit(solution)/shard_map/ppermute | solution.py:114
  137.4 3.0 %collective-permute-start.22 = (f32[8,1,4096]{2,0,1:T(8,128)S(1)}, f32[8,1,4096]{2,0,1:T(8,128)S(1)}, u32[]{:S(2)}, u32[]{:S(2)}) collective-permute-start(f32[8,1,4096]{2,0,1:T(8,128)S(1)} %add.312), channel_id=1, source_target_pairs={{0,4},{1,5},{2,6},{3,7},{4,0},{5,1},{6,2},{7,3},{8,12},{9,13},{10,... | collective-permute-start | bytes 393224 | tf_op jit(solution)/shard_map/ppermute | solution.py:114
  140.4 4.3 %collective-permute-done.22 = f32[8,1,4096]{2,0,1:T(8,128)S(1)} collective-permute-done((f32[8,1,4096]{2,0,1:T(8,128)S(1)}, f32[8,1,4096]{2,0,1:T(8,128)S(1)}, u32[]{:S(2)}, u32[]{:S(2)}) %collective-permute-start.22) | collective-permute-done | bytes 131104 | tf_op jit(solution)/shard_map/ppermute | solution.py:114
  144.9 5.1 %fusion.4 = f32[8,896]{1,0:T(8,128)S(1)} fusion(bf16[1,896,4096]{2,1,0:T(8,128)(2,1)} %param.31, f32[8,1,4096]{2,0,1:T(8,128)S(1)} %get-tuple-element.24, f32[4096]{0:T(1024)S(1)} %bitcast.179, f32[8]{0:T(128)S(1)} %add_rsqrt_fusion.1), kind=kOutput, calls=%fused_computation.8 | convolution fusion | flops 58818560 | bytes 7516192 | tf_op jit(solution)/shard_map/dot_general | solution.py:21
  149.9 5.1 %fusion.19 = bf16[8,896]{1,0:T(8,128)(2,1)S(1)} fusion(bf16[1,896,4096]{2,1,0:T(8,128)(2,1)} %param.32, f32[8,896]{1,0:T(8,128)S(1)} %fusion.4, f32[8,1,4096]{2,0,1:T(8,128)S(1)} %get-tuple-element.24, f32[4096]{0:T(1024)S(1)} %bitcast.180, f32[8]{0:T(128)S(1)} %add_rsqrt_fusion.1), kind=kOutput, calls=%fused_computation.29 | convolution fusion | flops 58861568 | bytes 7530528 | tf_op jit(solution)/shard_map/dot_general | solution.py:21
  155.0 4.2 %fusion = f32[2,2,2,4096]{3,2,1,0:T(2,128)S(1)} fusion(bf16[2,2,2,896]{3,2,1,0:T(2,128)(2,1)S(1)} %dot_general.65, bf16[1,896,4096]{2,1,0:T(8,128)(2,1)} %param.33), kind=kOutput, calls=%fused_computation.4 | convolution fusion | flops 58720256 | bytes 7485440 | tf_op jit(solution)/shard_map/dot_general | solution.py:326
  159.4 1.9 %collective-permute-start.23 = (f32[2,2,1,1,4096]{4,2,3,1,0:T(1,128)S(1)}, f32[2,2,1,1,4096]{4,2,3,1,0:T(1,128)S(1)}, u32[]{:S(2)}, u32[]{:S(2)}) collective-permute-start(f32[2,2,1,1,4096]{4,2,3,1,0:T(1,128)S(1)} %dynamic-slice_bitcast_fusion), channel_id=1, source_target_pairs={{0,1},{1,0},{2,3},{3,2},{4,5},{5,4},{6,7},{7,6},{8,9},{9,8},{10,11... | collective-permute-start | bytes 196616 | tf_op jit(solution)/shard_map/ppermute | solution.py:341
  161.2 2.4 %collective-permute-done.23 = f32[2,2,1,1,4096]{4,2,3,1,0:T(1,128)S(1)} collective-permute-done((f32[2,2,1,1,4096]{4,2,3,1,0:T(1,128)S(1)}, f32[2,2,1,1,4096]{4,2,3,1,0:T(1,128)S(1)}, u32[]{:S(2)}, u32[]{:S(2)}) %collective-permute-start.23) | collective-permute-done | bytes 65568 | tf_op jit(solution)/shard_map/ppermute | solution.py:341
  163.8 1.1 collective-permute-start.24
  164.9 2.9 %collective-permute-done.24 = f32[2,1,1,1,4096]{4,2,3,1,0:T(1,128)S(1)} collective-permute-done((f32[2,1,1,1,4096]{4,2,3,1,0:T(1,128)S(1)}, f32[2,1,1,1,4096]{4,2,3,1,0:T(1,128)S(1)}, u32[]{:S(2)}, u32[]{:S(2)}) %collective-permute-start.24) | collective-permute-done | bytes 32800 | tf_op jit(solution)/shard_map/ppermute | solution.py:341
  167.9 3.4 %collective-permute-start.25 = (f32[1,4096]{1,0:T(1,128)S(1)}, f32[1,4096]{1,0:T(1,128)S(1)}, u32[]{:S(2)}, u32[]{:S(2)}) collective-permute-start(f32[1,4096]{1,0:T(1,128)S(1)} %bitcast_add_fusion.1), channel_id=1, source_target_pairs={{0,8},{1,9},{2,10},{3,11},{4,12},{5,13},{6,14},{7,15},{8,16},{9,17... | collective-permute-start | bytes 49160 | tf_op jit(solution)/shard_map/ppermute | solution.py:357
  171.4 1.6 collective-permute-done.26
  (127 shorter events, 12.8 us)
Async XLA Ops:
  0.0 126.9 %copy-start = (bf16[1,256,4096]{2,1,0:T(8,128)(2,1)S(1)}, bf16[1,256,4096]{2,1,0:T(8,128)(2,1)}, u32[]{:S(2)}) copy-start(bf16[1,256,4096]{2,1,0:T(8,128)(2,1)} %param.29) | copy-start | bytes 6291460
  0.0 19.8 %collective-permute-start.2 = (bf16[128,512]{1,0:T(8,128)(2,1)}, bf16[128,512]{1,0:T(8,128)(2,1)S(1)}, u32[]{:S(2)}, u32[]{:S(2)}) collective-permute-start(bf16[128,512]{1,0:T(8,128)(2,1)} %bitcast.177), channel_id=1, source_target_pairs={{0,2},{2,4},{4,6},{6,7},{7,5},{5,3},{3,1},{1,0},{8,10},{10,12},{12... | collective-permute-start | bytes 393224 | tf_op jit(solution)/shard_map/ppermute | solution.py:149
  3.0 18.9 %collective-permute-start.6 = (bf16[128,512]{1,0:T(8,128)(2,1)}, bf16[128,512]{1,0:T(8,128)(2,1)S(1)}, u32[]{:S(2)}, u32[]{:S(2)}) collective-permute-start(bf16[128,512]{1,0:T(8,128)(2,1)} %bitcast.178), channel_id=1, source_target_pairs={{0,1},{2,0},{4,2},{6,4},{7,6},{5,7},{3,5},{1,3},{8,9},{10,8},{12,1... | collective-permute-start | bytes 393224 | tf_op jit(solution)/shard_map/ppermute | solution.py:153
  3.0 36.2 %collective-permute-start = (bf16[64,4096]{1,0:T(8,128)(2,1)}, bf16[64,4096]{1,0:T(8,128)(2,1)}, u32[]{:S(2)}, u32[]{:S(2)}) collective-permute-start(bf16[64,4096]{1,0:T(8,128)(2,1)} %bitcast.174), channel_id=1, source_target_pairs={{0,2},{2,4},{4,6},{6,7},{7,5},{5,3},{3,1},{1,0},{8,10},{10,12},{12... | collective-permute-start | bytes 1572872 | tf_op jit(solution)/shard_map/ppermute | solution.py:149
  5.1 34.2 %collective-permute-start.1 = (bf16[64,4096]{1,0:T(8,128)(2,1)}, bf16[64,4096]{1,0:T(8,128)(2,1)}, u32[]{:S(2)}, u32[]{:S(2)}) collective-permute-start(bf16[64,4096]{1,0:T(8,128)(2,1)} %bitcast.175), channel_id=1, source_target_pairs={{0,1},{2,0},{4,2},{6,4},{7,6},{5,7},{3,5},{1,3},{8,9},{10,8},{12,1... | collective-permute-start | bytes 1572872 | tf_op jit(solution)/shard_map/ppermute | solution.py:153
  19.8 5.0 %collective-permute-start.3 = (bf16[128,512]{1,0:T(8,128)(2,1)S(1)}, bf16[128,512]{1,0:T(8,128)(2,1)S(1)}, u32[]{:S(2)}, u32[]{:S(2)}) collective-permute-start(bf16[128,512]{1,0:T(8,128)(2,1)S(1)} %collective-permute-done.2), channel_id=1, source_target_pairs={{0,2},{2,4},{4,6},{6,7},{7,5},{5,3},{3,1},{1,0},{8,10},{10,12},{12... | collective-permute-start | bytes 393224 | tf_op jit(solution)/shard_map/ppermute | solution.py:149
  21.9 5.0 %collective-permute-start.7 = (bf16[128,512]{1,0:T(8,128)(2,1)S(1)}, bf16[128,512]{1,0:T(8,128)(2,1)S(1)}, u32[]{:S(2)}, u32[]{:S(2)}) collective-permute-start(bf16[128,512]{1,0:T(8,128)(2,1)S(1)} %collective-permute-done.6), channel_id=1, source_target_pairs={{0,1},{2,0},{4,2},{6,4},{7,6},{5,7},{3,5},{1,3},{8,9},{10,8},{12,1... | collective-permute-start | bytes 393224 | tf_op jit(solution)/shard_map/ppermute | solution.py:153
  24.8 5.4 %collective-permute-start.4 = (bf16[128,512]{1,0:T(8,128)(2,1)S(1)}, bf16[128,512]{1,0:T(8,128)(2,1)S(1)}, u32[]{:S(2)}, u32[]{:S(2)}) collective-permute-start(bf16[128,512]{1,0:T(8,128)(2,1)S(1)} %collective-permute-done.3), channel_id=1, source_target_pairs={{0,2},{2,4},{4,6},{6,7},{7,5},{5,3},{3,1},{1,0},{8,10},{10,12},{12... | collective-permute-start | bytes 393224 | tf_op jit(solution)/shard_map/ppermute | solution.py:149
  26.9 9.0 %collective-permute-start.8 = (bf16[128,512]{1,0:T(8,128)(2,1)S(1)}, bf16[128,512]{1,0:T(8,128)(2,1)S(1)}, u32[]{:S(2)}, u32[]{:S(2)}) collective-permute-start(bf16[128,512]{1,0:T(8,128)(2,1)S(1)} %collective-permute-done.7), channel_id=1, source_target_pairs={{0,1},{2,0},{4,2},{6,4},{7,6},{5,7},{3,5},{1,3},{8,9},{10,8},{12,1... | collective-permute-start | bytes 393224 | tf_op jit(solution)/shard_map/ppermute | solution.py:153
  30.2 5.5 %collective-permute-start.5 = (bf16[128,512]{1,0:T(8,128)(2,1)S(1)}, bf16[128,512]{1,0:T(8,128)(2,1)S(1)}, u32[]{:S(2)}, u32[]{:S(2)}) collective-permute-start(bf16[128,512]{1,0:T(8,128)(2,1)S(1)} %collective-permute-done.4), channel_id=1, source_target_pairs={{0,2},{2,4},{4,6},{6,7},{7,5},{5,3},{3,1},{1,0},{8,10},{10,12},{12... | collective-permute-start | bytes 393224 | tf_op jit(solution)/shard_map/ppermute | solution.py:149
  35.8 11.8 %copy-start.6 = (f32[1,128]{1,0:T(1,128)S(1)}, f32[1,128]{1,0:T(1,128)}, u32[]{:S(2)}) copy-start(f32[1,128]{1,0:T(1,128)} %param.26) | copy-start | bytes 1540
  38.5 26.7 %copy-start.4 = (bf16[1,64,4096]{2,1,0:T(8,128)(2,1)S(1)}, bf16[1,64,4096]{2,1,0:T(8,128)(2,1)}, u32[]{:S(2)}) copy-start(bf16[1,64,4096]{2,1,0:T(8,128)(2,1)} %param.28) | copy-start | bytes 1572868
  39.3 18.1 %all-to-all-start = ((bf16[8,48,512]{2,1,0:T(8,128)(2,1)}), bf16[8,48,512]{2,1,0:T(8,128)(2,1)S(1)}, u32[]{:S(2)}, u32[]{:S(2)}) async-start(bf16[8,48,512]{2,1,0:T(8,128)(2,1)} %pad_maximum_fusion), calls=%async_computation | async-start | bytes 786432 | tf_op jit(solution)/shard_map/all_to_all | solution.py:253
  47.7 14.2 %collective-permute-start.10 = (bf16[64,4096]{1,0:T(8,128)(2,1)}, bf16[64,4096]{1,0:T(8,128)(2,1)}, u32[]{:S(2)}, u32[]{:S(2)}) collective-permute-start(bf16[64,4096]{1,0:T(8,128)(2,1)} %collective-permute-done.1), channel_id=1, source_target_pairs={{0,1},{2,0},{4,2},{6,4},{7,6},{5,7},{3,5},{1,3},{8,9},{10,8},{12,1... | collective-permute-start | bytes 1572872 | tf_op jit(solution)/shard_map/ppermute | solution.py:153
  49.7 12.2 %collective-permute-start.9 = (bf16[64,4096]{1,0:T(8,128)(2,1)}, bf16[64,4096]{1,0:T(8,128)(2,1)}, u32[]{:S(2)}, u32[]{:S(2)}) collective-permute-start(bf16[64,4096]{1,0:T(8,128)(2,1)} %collective-permute-done), channel_id=1, source_target_pairs={{0,2},{2,4},{4,6},{6,7},{7,5},{5,3},{3,1},{1,0},{8,10},{10,12},{12... | collective-permute-start | bytes 1572872 | tf_op jit(solution)/shard_map/ppermute | solution.py:149
  61.9 7.8 %collective-permute-start.13 = (bf16[2,2,1,1,256]{4,2,1,0,3:T(2,128)(2,1)S(1)}, bf16[2,2,1,1,256]{4,2,1,0,3:T(2,128)(2,1)S(1)}, u32[]{:S(2)}, u32[]{:S(2)}) collective-permute-start(bf16[2,2,1,1,256]{4,2,1,0,3:T(2,128)(2,1)S(1)} %get-tuple-element.42), channel_id=1, source_target_pairs={{0,1},{1,0},{2,3},{3,2},{4,5},{5,4},{6,7},{7,6},{8,9},{9,8},{10,11... | collective-permute-start | bytes 6152 | tf_op jit(solution)/shard_map/ppermute | solution.py:73
  64.0 23.8 %collective-permute-start.12 = (bf16[64,4096]{1,0:T(8,128)(2,1)}, bf16[64,4096]{1,0:T(8,128)(2,1)}, u32[]{:S(2)}, u32[]{:S(2)}) collective-permute-start(bf16[64,4096]{1,0:T(8,128)(2,1)} %collective-permute-done.10), channel_id=1, source_target_pairs={{0,1},{2,0},{4,2},{6,4},{7,6},{5,7},{3,5},{1,3},{8,9},{10,8},{12,1... | collective-permute-start | bytes 1572872 | tf_op jit(solution)/shard_map/ppermute | solution.py:153
  69.8 5.9 %collective-permute-start.14 = (bf16[2,1,2,1,256]{4,2,1,0,3:T(2,128)(2,1)S(1)}, bf16[2,1,2,1,256]{4,2,1,0,3:T(2,128)(2,1)S(1)}, u32[]{:S(2)}, u32[]{:S(2)}) collective-permute-start(bf16[2,1,2,1,256]{4,2,1,0,3:T(2,128)(2,1)S(1)} %get-tuple-element.40), channel_id=1, source_target_pairs={{0,2},{1,3},{2,0},{3,1},{4,6},{5,7},{6,4},{7,5},{8,10},{9,11},{10,... | collective-permute-start | bytes 6152 | tf_op jit(solution)/shard_map/ppermute | solution.py:73
  75.7 12.0 %collective-permute-start.11 = (bf16[64,4096]{1,0:T(8,128)(2,1)}, bf16[64,4096]{1,0:T(8,128)(2,1)S(1)}, u32[]{:S(2)}, u32[]{:S(2)}) collective-permute-start(bf16[64,4096]{1,0:T(8,128)(2,1)} %collective-permute-done.9), channel_id=1, source_target_pairs={{0,2},{2,4},{4,6},{6,7},{7,5},{5,3},{3,1},{1,0},{8,10},{10,12},{12... | collective-permute-start | bytes 1572872 | tf_op jit(solution)/shard_map/ppermute | solution.py:149
  75.8 16.7 %copy-start.7 = (f32[1,128]{1,0:T(1,128)S(1)}, f32[1,128]{1,0:T(1,128)}, u32[]{:S(2)}) copy-start(f32[1,128]{1,0:T(1,128)} %param.25) | copy-start | bytes 1540
  75.8 9.7 %collective-permute-start.15 = (bf16[1,2,2,1,256]{4,2,1,0,3:T(2,128)(2,1)S(1)}, bf16[1,2,2,1,256]{4,2,1,0,3:T(2,128)(2,1)S(1)}, u32[]{:S(2)}, u32[]{:S(2)}) collective-permute-start(bf16[1,2,2,1,256]{4,2,1,0,3:T(2,128)(2,1)S(1)} %get-tuple-element.38), channel_id=1, source_target_pairs={{0,4},{1,5},{2,6},{3,7},{4,0},{5,1},{6,2},{7,3},{8,12},{9,13},{10,... | collective-permute-start | bytes 6152 | tf_op jit(solution)/shard_map/ppermute | solution.py:73
  87.8 9.9 %collective-permute-start.16 = (bf16[64,4096]{1,0:T(8,128)(2,1)S(1)}, bf16[64,4096]{1,0:T(8,128)(2,1)}, u32[]{:S(2)}, u32[]{:S(2)}) collective-permute-start(bf16[64,4096]{1,0:T(8,128)(2,1)S(1)} %collective-permute-done.11), channel_id=1, source_target_pairs={{0,2},{2,4},{4,6},{6,7},{7,5},{5,3},{3,1},{1,0},{8,10},{10,12},{12... | collective-permute-start | bytes 1572872 | tf_op jit(solution)/shard_map/ppermute | solution.py:149
  92.6 6.9 %copy-start.2 = (f32[256,4096]{1,0:T(8,128)S(1)}, f32[256,4096]{1,0:T(8,128)}, u32[]{:S(2)}) copy-start(f32[256,4096]{1,0:T(8,128)} %convolution_add_fusion.1) | copy-start | bytes 12582916
  92.6 6.9 %copy-start.3 = (f32[256,4096]{1,0:T(8,128)S(1)}, f32[256,4096]{1,0:T(8,128)}, u32[]{:S(2)}) copy-start(f32[256,4096]{1,0:T(8,128)} %fusion.49) | copy-start | bytes 12582916
  104.7 2.7 %copy-start.1 = (f32[256,4096]{1,0:T(8,128)}, f32[256,4096]{1,0:T(8,128)S(1)}, u32[]{:S(2)}) copy-start(f32[256,4096]{1,0:T(8,128)S(1)} %fusion.10) | copy-start | bytes 12582916
  113.5 31.4 %copy-start.5 = (f32[1,4096]{1,0:T(1,128)S(1)}, f32[1,4096]{1,0:T(1,128)}, u32[]{:S(2)}) copy-start(f32[1,4096]{1,0:T(1,128)} %param.30) | copy-start | bytes 49156
  114.8 3.7 %collective-permute-start.17 = (bf16[2,2,1,1,256]{4,2,1,0,3:T(2,128)(2,1)S(1)}, bf16[2,2,1,1,256]{4,2,1,0,3:T(2,128)(2,1)S(1)}, u32[]{:S(2)}, u32[]{:S(2)}) collective-permute-start(bf16[2,2,1,1,256]{4,2,1,0,3:T(2,128)(2,1)S(1)} %get-tuple-element.36), channel_id=1, source_target_pairs={{0,1},{1,0},{2,3},{3,2},{4,5},{5,4},{6,7},{7,6},{8,9},{9,8},{10,11... | collective-permute-start | bytes 6152 | tf_op jit(solution)/shard_map/ppermute | solution.py:73
  118.6 3.7 %collective-permute-start.18 = (bf16[2,1,2,1,256]{4,2,1,0,3:T(2,128)(2,1)S(1)}, bf16[2,1,2,1,256]{4,2,1,0,3:T(2,128)(2,1)S(1)}, u32[]{:S(2)}, u32[]{:S(2)}) collective-permute-start(bf16[2,1,2,1,256]{4,2,1,0,3:T(2,128)(2,1)S(1)} %get-tuple-element.34), channel_id=1, source_target_pairs={{0,2},{1,3},{2,0},{3,1},{4,6},{5,7},{6,4},{7,5},{8,10},{9,11},{10,... | collective-permute-start | bytes 6152 | tf_op jit(solution)/shard_map/ppermute | solution.py:73
  122.3 4.6 %collective-permute-start.19 = (bf16[1,2,2,1,256]{4,2,1,0,3:T(2,128)(2,1)S(1)}, bf16[1,2,2,1,256]{4,2,1,0,3:T(2,128)(2,1)S(1)}, u32[]{:S(2)}, u32[]{:S(2)}) collective-permute-start(bf16[1,2,2,1,256]{4,2,1,0,3:T(2,128)(2,1)S(1)} %get-tuple-element.32), channel_id=1, source_target_pairs={{0,4},{1,5},{2,6},{3,7},{4,0},{5,1},{6,2},{7,3},{8,12},{9,13},{10,... | collective-permute-start | bytes 6152 | tf_op jit(solution)/shard_map/ppermute | solution.py:73
  127.3 5.0 %collective-permute-start.20 = (f32[8,1,4096]{2,0,1:T(8,128)S(1)}, f32[8,1,4096]{2,0,1:T(8,128)S(1)}, u32[]{:S(2)}, u32[]{:S(2)}) collective-permute-start(f32[8,1,4096]{2,0,1:T(8,128)S(1)} %convolution_bitcast_fusion), channel_id=1, source_target_pairs={{0,1},{1,0},{2,3},{3,2},{4,5},{5,4},{6,7},{7,6},{8,9},{9,8},{10,11... | collective-permute-start | bytes 393224 | tf_op jit(solution)/shard_map/ppermute | solution.py:114
  132.3 5.0 %collective-permute-start.21 = (f32[8,1,4096]{2,0,1:T(8,128)S(1)}, f32[8,1,4096]{2,0,1:T(8,128)S(1)}, u32[]{:S(2)}, u32[]{:S(2)}) collective-permute-start(f32[8,1,4096]{2,0,1:T(8,128)S(1)} %add.311), channel_id=1, source_target_pairs={{0,2},{1,3},{2,0},{3,1},{4,6},{5,7},{6,4},{7,5},{8,10},{9,11},{10,... | collective-permute-start | bytes 393224 | tf_op jit(solution)/shard_map/ppermute | solution.py:114
  137.4 7.3 %collective-permute-start.22 = (f32[8,1,4096]{2,0,1:T(8,128)S(1)}, f32[8,1,4096]{2,0,1:T(8,128)S(1)}, u32[]{:S(2)}, u32[]{:S(2)}) collective-permute-start(f32[8,1,4096]{2,0,1:T(8,128)S(1)} %add.312), channel_id=1, source_target_pairs={{0,4},{1,5},{2,6},{3,7},{4,0},{5,1},{6,2},{7,3},{8,12},{9,13},{10,... | collective-permute-start | bytes 393224 | tf_op jit(solution)/shard_map/ppermute | solution.py:114
  159.4 4.3 %collective-permute-start.23 = (f32[2,2,1,1,4096]{4,2,3,1,0:T(1,128)S(1)}, f32[2,2,1,1,4096]{4,2,3,1,0:T(1,128)S(1)}, u32[]{:S(2)}, u32[]{:S(2)}) collective-permute-start(f32[2,2,1,1,4096]{4,2,3,1,0:T(1,128)S(1)} %dynamic-slice_bitcast_fusion), channel_id=1, source_target_pairs={{0,1},{1,0},{2,3},{3,2},{4,5},{5,4},{6,7},{7,6},{8,9},{9,8},{10,11... | collective-permute-start | bytes 196616 | tf_op jit(solution)/shard_map/ppermute | solution.py:341
  163.8 4.0 %collective-permute-start.24 = (f32[2,1,1,1,4096]{4,2,3,1,0:T(1,128)S(1)}, f32[2,1,1,1,4096]{4,2,3,1,0:T(1,128)S(1)}, u32[]{:S(2)}, u32[]{:S(2)}) collective-permute-start(f32[2,1,1,1,4096]{4,2,3,1,0:T(1,128)S(1)} %constant_dynamic-slice_fusion), channel_id=1, source_target_pairs={{0,2},{1,3},{2,0},{3,1},{4,6},{5,7},{6,4},{7,5},{8,10},{9,11},{10,... | collective-permute-start | bytes 98312 | tf_op jit(solution)/shard_map/ppermute | solution.py:341
  167.9 5.1 %collective-permute-start.26 = (f32[1,4096]{1,0:T(1,128)S(1)}, f32[1,4096]{1,0:T(1,128)S(1)}, u32[]{:S(2)}, u32[]{:S(2)}) collective-permute-start(f32[1,4096]{1,0:T(1,128)S(1)} %dynamic-slice_bitcast_fusion.1), channel_id=1, source_target_pairs={{0,12},{1,13},{2,14},{3,15},{4,8},{5,9},{6,10},{7,11},{8,20},{9,21... | collective-permute-start | bytes 49160 | tf_op jit(solution)/shard_map/ppermute | solution.py:358
  167.9 5.1 %collective-permute-start.25 = (f32[1,4096]{1,0:T(1,128)S(1)}, f32[1,4096]{1,0:T(1,128)S(1)}, u32[]{:S(2)}, u32[]{:S(2)}) collective-permute-start(f32[1,4096]{1,0:T(1,128)S(1)} %bitcast_add_fusion.1), channel_id=1, source_target_pairs={{0,8},{1,9},{2,10},{3,11},{4,12},{5,13},{6,14},{7,15},{8,16},{9,17... | collective-permute-start | bytes 49160 | tf_op jit(solution)/shard_map/ppermute | solution.py:357

commit v5 on v4

--- a/solution.py
+++ b/solution.py
@@ -360,9 +360,148 @@
     return output_rows[None]
 
 
+def heads_split(
+    acts,
+    patches,
+    site_tiles,
+    site_count,
+    q_weight,
+    q_gain,
+    k_gain,
+    tile_in,
+    tile_out,
+    out_weight,
+    ffn_gain,
+    gate_weight,
+    up_weight,
+    down_weight,
+):
+    group_size = lax.axis_size("site")
+    section_count = lax.axis_size("section")
+    my_index = lax.axis_index("site")
+    sites_here = acts.shape[1]
+    list_width = site_tiles.shape[1]
+    tiles_here = patches.shape[1]
+    head_size = q_gain.shape[1]
+    heads_here = HEADS // group_size
+    current = acts[0]
+    model_width = current.shape[-1]
+    hidden_width = tile_in.shape[-1]
+    all_sites = group_size * sites_here
+
+    act_rows = sites_here * model_width // hidden_width
+    ring_in = RingGather(
+        jnp.concatenate([tile_in[0], current.reshape(act_rows, hidden_width)], axis=0),
+        group_size,
+        my_index,
+    )
+    in_slots, in_sources = ring_in.finish()
+    in_rows = tile_in.shape[1]
+    slot_of_source = jnp.argmax(
+        in_sources[None, :] == jnp.arange(group_size, dtype=jnp.int32)[:, None], axis=1
+    ).astype(jnp.int32)
+    everyone = jnp.take(in_slots[:, in_rows:], slot_of_source, axis=0).reshape(all_sites, model_width)
+    weight_in = in_slots[:, :in_rows].reshape(-1, hidden_width)
+    own_rows = jnp.take(patches[0].reshape(tiles_here, group_size, -1), in_sources, axis=1)
+    tile_hidden = jax.nn.gelu(
+        jnp.dot(own_rows.reshape(tiles_here, -1), weight_in, preferred_element_type=jnp.float32),
+        approximate=True,
+    ).astype(jnp.bfloat16)
+
+    kv_width = tile_out.shape[-1]
+    my_cols = heads_here * head_size
+    col_blocks = tile_out[0].reshape(tile_out.shape[1], 2, group_size, my_cols)
+    col_blocks = jnp.transpose(col_blocks, (2, 0, 1, 3)).reshape(group_size, tile_out.shape[1], 2 * my_cols)
+    weight_out = lax.all_to_all(col_blocks, "site", split_axis=0, concat_axis=0, tiled=True)
+    weight_out = weight_out.reshape(-1, 2 * my_cols)
+    del kv_width
+
+    q_part = by_rows(everyone, q_weight[0]).astype(jnp.bfloat16)
+    queries = head_norm(q_part, q_gain[0]).astype(jnp.bfloat16)
+    query_heads = queries.reshape(all_sites, heads_here, head_size)
+
+    ring_hidden = RingGather(tile_hidden, group_size, my_index)
+    hidden_slots, hidden_sources = ring_hidden.finish()
+    hidden_slot_of_source = jnp.argmax(
+        hidden_sources[None, :] == jnp.arange(group_size, dtype=jnp.int32)[:, None], axis=1
+    ).astype(jnp.int32)
+    slot_kv = []
+    for slot in range(group_size):
+        keyval = jnp.dot(hidden_slots[slot], weight_out, preferred_element_type=jnp.float32)
+        normed_keys = head_norm(keyval[:, :my_cols], k_gain[0])
+        slot_kv.append(
+            jnp.concatenate([normed_keys, keyval[:, my_cols:]], axis=1).astype(jnp.bfloat16)
+        )
+    table = jnp.stack(slot_kv).reshape(group_size * tiles_here, 2 * my_cols)
+    owner = site_tiles // tiles_here
+    rows = jnp.take(hidden_slot_of_source, owner) * tiles_here + site_tiles % tiles_here
+    pair_kv = table[rows.reshape(-1)].reshape(all_sites, list_width, 2, heads_here, head_size)
+
+    slot_index = jnp.arange(list_width, dtype=jnp.int32)
+    live = (slot_index[None, :] < site_count[:, None]).astype(jnp.float32)
+    scores = jnp.einsum(
+        "nhd,nlhd->nhl", query_heads, pair_kv[:, :, 0], preferred_element_type=jnp.float32
+    ) / math.sqrt(head_size)
+    exponents = jnp.exp(scores) * live[:, None, :]
+    weights = (exponents / jnp.sum(exponents, axis=-1, keepdims=True)).astype(jnp.bfloat16)
+    combined = jnp.einsum(
+        "nhl,nlhd->nhd", weights, pair_kv[:, :, 1], preferred_element_type=jnp.float32
+    )
+    combined = combined.reshape(all_sites, my_cols).astype(jnp.bfloat16)
+    attn_part = jnp.dot(combined, out_weight[0], preferred_element_type=jnp.float32)
+    attn_all = doubling_sum(attn_part.reshape(group_size, sites_here, -1), group_size)
+    residual_all = everyone.reshape(group_size, sites_here, -1).astype(jnp.float32) + attn_all
+    residual = lax.dynamic_index_in_dim(residual_all, my_index, 0, keepdims=False)
+    normed_rows = rms_norm(residual_all, ffn_gain[0]).astype(jnp.bfloat16).reshape(-1, model_width)
+    gate_sum = by_rows(normed_rows, gate_weight[0])
+    up_sum = by_rows(normed_rows, up_weight[0])
+    hidden_ffn = (jax.nn.silu(gate_sum) * up_sum).astype(jnp.bfloat16)
+    down_part = jnp.dot(hidden_ffn, down_weight[0], preferred_element_type=jnp.float32)
+    down_part = down_part.reshape(group_size, sites_here, -1)
+    return last_round(down_part, residual, group_size, section_count, my_index)
+
+
+def last_round(down_part, residual, group_size, section_count, my_index):
+    bits = group_size.bit_length() - 1
+    rest = down_part.shape[1:]
+    state = down_part.reshape((2,) * bits + rest)
+    for bit in range(bits):
+        axis = bits - 1 - bit
+        mine = (my_index >> bit) & 1
+        keep = lax.dynamic_index_in_dim(state, mine, axis, keepdims=True)
+        send = lax.dynamic_index_in_dim(state, 1 - mine, axis, keepdims=True)
+        if bit < bits - 1:
+            state = keep + lax.ppermute(send, "site", xor_pairs(group_size, bit))
+            continue
+        own = keep.reshape(rest) + residual
+        forward = [
+            (section * group_size + site, ((section + 1) % section_count) * group_size + site)
+            for section in range(section_count)
+            for site in range(group_size)
+        ]
+        across = [
+            (
+                section * group_size + site,
+                ((section + 1) % section_count) * group_size + (site ^ (1 << bit)),
+            )
+            for section in range(section_count)
+            for site in range(group_size)
+        ]
+        mine_part = lax.ppermute(own, ("section", "site"), forward)
+        other_part = lax.ppermute(send.reshape(rest), ("section", "site"), across)
+        return (mine_part + other_part).astype(jnp.bfloat16)[None]
+
+
 def solution(mesh):
+    group_size = mesh.shape["site"]
+    split_heads = (
+        direct_ok(group_size)
+        and group_size > 1
+        and HEADS % group_size == 0
+        and mesh.shape["section"] > 0
+    )
     return jax.shard_map(
-        shards,
+        heads_split if split_heads else shards,
         mesh=mesh,
         in_specs=(
             P("section", "site", None),

time: 175 us -> 212 us (1.21)
  local copies, waits for them, and re-layouts: 15.8 us -> 74 us
  other arithmetic: 15.8 us -> 39 us
  matrix products: 41.9 us -> 25.4 us
  starting transfers between devices: 49.2 us -> 33.5 us
  waiting for transfers between devices: 45.4 us -> 37.5 us
  between operations: 5.52 us -> 0.79 us
    gather x3 -> x6, local copies, waits for them, and re-layouts: 3.82 us -> 25.8 us  [the longest x2 12.6 us: heads_split(): jnp.take(hidden_slot_of_source, owner) * tiles_here]
    dot_general x13, matrix products: 29.5 us -> 12.9 us  [the longest x8 7.11 us: heads_split(): jnp.dot(hidden_slots[slot], weight_out, preferred_element_type=jnp.float32)]
    ppermute x10 -> x4, starting transfers between devices: 20.6 us -> 4.11 us  [the longest x1 2.86 us: last_round(): mine_part = lax.ppermute(own, ('section', 'site'), forward)]
    rsqrt x2 -> x9, other arithmetic: 0.03 us -> 11.3 us  [head_norm(): lax.rsqrt(jnp.mean(shaped * shaped, axis=-1, keepdims=True) + epsilon)]
    concatenate x0 -> x8, local copies, waits for them, and re-layouts: none -> 10.1 us  [heads_split(): jnp.concatenate([normed_keys, keyval[:, my_cols:]], axis=1)]
    mul x2 -> x10, local copies, waits for them, and re-layouts: 0.61 us -> 10.1 us  [head_norm(): shaped * lax.rsqrt(jnp.mean(shaped * shaped, axis=-1, keepdims=True) + ep...]
    mul x1 -> x8, local copies, waits for them, and re-layouts: 0.01 us -> 9.17 us  [head_norm(): shaped * shaped]
    reduce_sum x2 -> x8, other arithmetic: 2.33 us -> 9.28 us  [head_norm(): jnp.mean(shaped * shaped, axis=-1, keepdims=True) + epsilon]
  transfers between devices with their start and end apart: 28 -> 22, of which waited for: 18 -> 12; matrix products, arithmetic and copies ran while one was open for 23% -> 33% of each run, Pallas kernels for 0% -> 0%
where the time goes in v5:
time: 212 us; the launch traced here: 210 us
  local copies, waits for them, and re-layouts  74 us (35%)
  other arithmetic  39 us (18%)
  waiting for transfers between devices  37.5 us (18%)
  starting transfers between devices  33.5 us (16%)
  matrix products  25.4 us (12%)
    ppermute x8, starting transfers between devices, _issue(): self.ahead = lax.ppermute(self.ahead, 'site', self.forward)  14.9 us
    ppermute x3, waiting for transfers between devices, doubling_sum(): state = state + lax.ppermute(state, 'site', xor_pairs(count, bit))  12.7 us
    gather x2, local copies, waits for them, and re-layouts, heads_split(): jnp.take(hidden_slot_of_source, owner) * tiles_here  12.6 us
    dot_general x3, matrix products, by_rows(): lax.dot_general(left, weight_rows, (((1,), (1,)), ((), ())), preferred_el...  12.5 us
    ppermute x8, waiting for transfers between devices, _issue(): self.ahead = lax.ppermute(self.ahead, 'site', self.forward)  11.6 us
    rsqrt x9, other arithmetic, head_norm(): lax.rsqrt(jnp.mean(shaped * shaped, axis=-1, keepdims=True) + epsilon)  11.3 us
    gather x1, local copies, waits for them, and re-layouts, heads_split(): table[rows.reshape(-1)]  11.1 us
    concatenate x8, local copies, waits for them, and re-layouts, heads_split(): jnp.concatenate([normed_keys, keyval[:, my_cols:]], axis=1)  10.1 us
  transfers between devices with their start and end apart: 22, of which 12 were waited for; matrix products, arithmetic and copies ran while one was open for 33% of the time, Pallas kernels for 0%

profile of v5, /device:TPU:0, one launch (start us, length us, event | category | flops | bytes accessed | tf_op | source)
XLA Modules:
  0.0 210.2 jit_solution(16119069361311511705)
XLA Ops:
  0.9 1.6 pad_maximum_fusion
  2.5 3.0 %collective-permute-start = (bf16[136,512]{1,0:T(8,128)(2,1)}, bf16[136,512]{1,0:T(8,128)(2,1)}, u32[]{:S(2)}, u32[]{:S(2)}) collective-permute-start(bf16[136,512]{1,0:T(8,128)(2,1)} %pad_maximum_fusion), channel_id=1, source_target_pairs={{0,2},{2,4},{4,6},{6,7},{7,5},{5,3},{3,1},{1,0},{8,10},{10,12},{12... | collective-permute-start | bytes 417800 | tf_op jit(solution)/shard_map/ppermute | solution.py:149
  5.6 1.2 copy.66
  8.3 6.3 %all-to-all-start = ((bf16[8,64,512]{2,1,0:T(8,128)(2,1)}), bf16[8,64,512]{2,1,0:T(8,128)(2,1)S(1)}, u32[]{:S(2)}, u32[]{:S(2)}) async-start(bf16[8,64,512]{2,1,0:T(8,128)(2,1)} %reshape.580), calls=%async_computation | async-start | bytes 1048576 | tf_op jit(solution)/shard_map/all_to_all | solution.py:415
  19.6 12.6 %gather_fusion.3 = s32[2048]{0:T(1024)S(1)} fusion(s32[8]{0:T(128)S(1)} %get-tuple-element.7, s32[2048]{0:T(1024)S(1)} %broadcast_clamp_fusion.1), kind=kCustom, calls=%fused_computation.3 | custom fusion | bytes 24576 | tf_op jit(solution)/shard_map/jit(_take)/gather | solution.py:437
  33.3 1.3 copy.40
  34.7 1.4 gather_fusion.2
  36.1 2.1 collective-permute-start.1
  39.2 2.3 %collective-permute-done.1 = bf16[136,512]{1,0:T(8,128)(2,1)S(1)} collective-permute-done((bf16[136,512]{1,0:T(8,128)(2,1)}, bf16[136,512]{1,0:T(8,128)(2,1)S(1)}, u32[]{:S(2)}, u32[]{:S(2)}) %collective-permute-start.1) | collective-permute-done | bytes 139296 | tf_op jit(solution)/shard_map/ppermute | solution.py:149
  41.4 2.0 collective-permute-start.2
  43.5 3.6 %collective-permute-done.2 = bf16[136,512]{1,0:T(8,128)(2,1)S(1)} collective-permute-done((bf16[136,512]{1,0:T(8,128)(2,1)S(1)}, bf16[136,512]{1,0:T(8,128)(2,1)S(1)}, u32[]{:S(2)}, u32[]{:S(2)}) %collective-permute-start.2) | collective-permute-done | bytes 139296 | tf_op jit(solution)/shard_map/ppermute | solution.py:149
  47.1 2.5 %collective-permute-start.3 = (bf16[136,512]{1,0:T(8,128)(2,1)S(1)}, bf16[136,512]{1,0:T(8,128)(2,1)S(1)}, u32[]{:S(2)}, u32[]{:S(2)}) collective-permute-start(bf16[136,512]{1,0:T(8,128)(2,1)S(1)} %collective-permute-done.2), channel_id=1, source_target_pairs={{0,2},{2,4},{4,6},{6,7},{7,5},{5,3},{3,1},{1,0},{8,10},{10,12},{12... | collective-permute-start | bytes 417800 | tf_op jit(solution)/shard_map/ppermute | solution.py:149
  49.6 3.8 %collective-permute-done.3 = bf16[136,512]{1,0:T(8,128)(2,1)S(1)} collective-permute-done((bf16[136,512]{1,0:T(8,128)(2,1)S(1)}, bf16[136,512]{1,0:T(8,128)(2,1)S(1)}, u32[]{:S(2)}, u32[]{:S(2)}) %collective-permute-start.3) | collective-permute-done | bytes 139296 | tf_op jit(solution)/shard_map/ppermute | solution.py:149
  54.0 1.6 collective-permute-start.11
  58.1 2.3 %bitcast_reduce_fusion = (f32[8,2]{0,1:T(2,128)S(1)}, f32[8,256]{1,0:T(8,128)S(1)}) fusion(bf16[8,4096]{1,0:T(8,128)(2,1)S(1)} %bitcast.287, bf16[1,256,4096]{2,1,0:T(8,128)(2,1)} %param.24), kind=kOutput, calls=%fused_computation.154 | convolution fusion | flops 16785392 | bytes 2170944 | tf_op jit(solution)/shard_map/dot_general | solution.py:21
  60.5 2.5 %collective-permute-done.11 = bf16[256,512]{1,0:T(8,128)(2,1)} collective-permute-done((bf16[256,512]{1,0:T(8,128)(2,1)S(1)}, bf16[256,512]{1,0:T(8,128)(2,1)}, u32[]{:S(2)}, u32[]{:S(2)}) %collective-permute-start.11) | collective-permute-done | bytes 262176 | tf_op jit(solution)/shard_map/ppermute | solution.py:153
  63.1 1.4 collective-permute-start.12
  64.5 1.4 collective-permute-start.8
  65.9 1.3 fusion.105
  69.7 1.8 mul.321
  71.5 2.0 reduce_sum.101
  73.4 1.6 add_rsqrt_fusion.6
  75.9 1.3 reduce_sum.100
  77.8 1.2 fusion.109
  82.7 1.6 add_rsqrt_fusion.2
  84.3 1.6 fusion.67
  85.9 1.2 fusion.106
  90.8 1.6 add_rsqrt_fusion.5
  92.4 1.6 fusion.64
  94.0 1.2 fusion.110
  99.5 1.6 add_rsqrt_fusion.1
  101.1 1.4 collective-permute-start.9
  102.5 1.6 fusion.68
  104.1 1.3 collective-permute-done.13
  109.4 1.6 add_rsqrt_fusion
  111.0 1.6 fusion.69
  112.6 1.2 fusion.107
  117.5 1.5 collective-permute-start.10
  118.9 1.6 add_rsqrt_fusion.4
  120.5 1.6 fusion.65
  122.1 1.9 collective-permute-done.10
  125.9 1.1 mul.339
  129.2 1.2 mul.358
  130.7 1.2 mul.334
  132.0 1.2 mul.328
  133.2 1.2 mul.322
  134.4 1.2 mul.352
  135.7 1.2 mul.312
  136.9 1.2 mul.346
  145.0 11.1 %gather_fusion.4 = bf16[2048,512]{1,0:T(8,128)(2,1)} fusion(bf16[2048,512]{1,0:T(8,128)(2,1)} %bitcast.42, s32[2048]{0:T(1024)S(1)} %broadcast_clamp_fusion), kind=kCustom, calls=%fused_computation.4 | custom fusion | bytes 4202496 | tf_op jit(solution)/shard_map/gather | solution.py:438
  156.0 4.0 %reshape.584 = bf16[8,256,2,2,128]{4,3,2,1,0:T(2,128)(2,1)} reshape(bf16[2048,512]{1,0:T(8,128)(2,1)} %gather_fusion.4) | data formatting | bytes 4194304 | tf_op jit(solution)/shard_map/reshape | solution.py:438
  160.0 2.7 %slice_bitcast_fusion.1 = (bf16[8,256,2,128]{3,2,1,0:T(2,128)(2,1)S(1)}, bf16[8,256,2,128]{3,2,1,0:T(2,128)(2,1)S(1)}) fusion(bf16[8,256,2,2,128]{4,3,2,1,0:T(2,128)(2,1)} %reshape.584), kind=kLoop, calls=%fused_computation.25 | loop fusion | bytes 4194304 | tf_op jit(solution)/shard_map/squeeze | solution.py:443
  164.5 4.4 %collective-permute-done.14 = f32[8,1,4096]{2,0,1:T(8,128)S(1)} collective-permute-done((f32[8,1,4096]{2,0,1:T(8,128)S(1)}, f32[8,1,4096]{2,0,1:T(8,128)S(1)}, u32[]{:S(2)}, u32[]{:S(2)}) %collective-permute-start.14) | collective-permute-done | bytes 131104 | tf_op jit(solution)/shard_map/ppermute | solution.py:114
  168.8 1.5 collective-permute-start.15
  170.4 3.5 %collective-permute-done.15 = f32[8,1,4096]{2,0,1:T(8,128)S(1)} collective-permute-done((f32[8,1,4096]{2,0,1:T(8,128)S(1)}, f32[8,1,4096]{2,0,1:T(8,128)S(1)}, u32[]{:S(2)}, u32[]{:S(2)}) %collective-permute-start.15) | collective-permute-done | bytes 131104 | tf_op jit(solution)/shard_map/ppermute | solution.py:114
  173.9 2.4 %collective-permute-start.16 = (f32[8,1,4096]{2,0,1:T(8,128)S(1)}, f32[8,1,4096]{2,0,1:T(8,128)S(1)}, u32[]{:S(2)}, u32[]{:S(2)}) collective-permute-start(f32[8,1,4096]{2,0,1:T(8,128)S(1)} %add.261), channel_id=1, source_target_pairs={{0,4},{1,5},{2,6},{3,7},{4,0},{5,1},{6,2},{7,3},{8,12},{9,13},{10,... | collective-permute-start | bytes 393224 | tf_op jit(solution)/shard_map/ppermute | solution.py:114
  176.4 4.9 %collective-permute-done.16 = f32[8,1,4096]{2,0,1:T(8,128)S(1)} collective-permute-done((f32[8,1,4096]{2,0,1:T(8,128)S(1)}, f32[8,1,4096]{2,0,1:T(8,128)S(1)}, u32[]{:S(2)}, u32[]{:S(2)}) %collective-permute-start.16) | collective-permute-done | bytes 131104 | tf_op jit(solution)/shard_map/ppermute | solution.py:114
  181.5 5.1 %fusion.5 = f32[8,896]{1,0:T(8,128)S(1)} fusion(bf16[1,896,4096]{2,1,0:T(8,128)(2,1)} %param.31, f32[8,1,4096]{2,0,1:T(8,128)S(1)} %get-tuple-element.10, f32[4096]{0:T(1024)S(1)} %bitcast.288, f32[8]{0:T(128)S(1)} %add_rsqrt_fusion.9), kind=kOutput, calls=%fused_computation.10 | convolution fusion | flops 58818560 | bytes 7516192 | tf_op jit(solution)/shard_map/dot_general | solution.py:21
  186.5 5.1 %fusion.14 = bf16[8,896]{1,0:T(8,128)(2,1)S(1)} fusion(bf16[1,896,4096]{2,1,0:T(8,128)(2,1)} %param.32, f32[8,896]{1,0:T(8,128)S(1)} %fusion.5, f32[8,1,4096]{2,0,1:T(8,128)S(1)} %get-tuple-element.10, f32[4096]{0:T(1024)S(1)} %bitcast.289, f32[8]{0:T(128)S(1)} %add_rsqrt_fusion.9), kind=kOutput, calls=%fused_computation.19 | convolution fusion | flops 58861568 | bytes 7530528 | tf_op jit(solution)/shard_map/dot_general | solution.py:21
  191.7 4.2 %fusion.1 = f32[2,2,2,4096]{3,2,1,0:T(2,128)S(1)} fusion(bf16[2,2,2,896]{3,2,1,0:T(2,128)(2,1)S(1)} %dot_general.65, bf16[1,896,4096]{2,1,0:T(8,128)(2,1)} %param.33), kind=kOutput, calls=%fused_computation.6 | convolution fusion | flops 58720256 | bytes 7485440 | tf_op jit(solution)/shard_map/dot_general | solution.py:459
  196.6 3.7 %collective-permute-done.17 = f32[2,2,1,1,4096]{4,2,3,1,0:T(1,128)S(1)} collective-permute-done((f32[2,2,1,1,4096]{4,2,3,1,0:T(1,128)S(1)}, f32[2,2,1,1,4096]{4,2,3,1,0:T(1,128)S(1)}, u32[]{:S(2)}, u32[]{:S(2)}) %collective-permute-start.17) | collective-permute-done | bytes 65568 | tf_op jit(solution)/shard_map/ppermute | solution.py:474
  200.9 3.5 %collective-permute-done.18 = f32[2,1,1,1,4096]{4,2,3,1,0:T(1,128)S(1)} collective-permute-done((f32[2,1,1,1,4096]{4,2,3,1,0:T(1,128)S(1)}, f32[2,1,1,1,4096]{4,2,3,1,0:T(1,128)S(1)}, u32[]{:S(2)}, u32[]{:S(2)}) %collective-permute-start.18) | collective-permute-done | bytes 32800 | tf_op jit(solution)/shard_map/ppermute | solution.py:474
  204.5 2.9 %collective-permute-start.19 = (f32[1,4096]{1,0:T(1,128)S(1)}, f32[1,4096]{1,0:T(1,128)S(1)}, u32[]{:S(2)}, u32[]{:S(2)}) collective-permute-start(f32[1,4096]{1,0:T(1,128)S(1)} %bitcast_add_fusion.1), channel_id=1, source_target_pairs={{0,8},{1,9},{2,10},{3,11},{4,12},{5,13},{6,14},{7,15},{8,16},{9,17... | collective-permute-start | bytes 49160 | tf_op jit(solution)/shard_map/ppermute | solution.py:490
  207.4 2.1 %collective-permute-done.20 = f32[1,4096]{1,0:T(1,128)S(1)} collective-permute-done((f32[1,4096]{1,0:T(1,128)S(1)}, f32[1,4096]{1,0:T(1,128)S(1)}, u32[]{:S(2)}, u32[]{:S(2)}) %collective-permute-start.20) | collective-permute-done | bytes 16416 | tf_op jit(solution)/shard_map/ppermute | solution.py:491
  (191 shorter events, 50.8 us)
Async XLA Ops:
  0.0 163.5 %copy-start = (bf16[1,256,4096]{2,1,0:T(8,128)(2,1)S(1)}, bf16[1,256,4096]{2,1,0:T(8,128)(2,1)}, u32[]{:S(2)}) copy-start(bf16[1,256,4096]{2,1,0:T(8,128)(2,1)} %param.29) | copy-start | bytes 6291460
  2.5 33.6 %collective-permute-start = (bf16[136,512]{1,0:T(8,128)(2,1)}, bf16[136,512]{1,0:T(8,128)(2,1)}, u32[]{:S(2)}, u32[]{:S(2)}) collective-permute-start(bf16[136,512]{1,0:T(8,128)(2,1)} %pad_maximum_fusion), channel_id=1, source_target_pairs={{0,2},{2,4},{4,6},{6,7},{7,5},{5,3},{3,1},{1,0},{8,10},{10,12},{12... | collective-permute-start | bytes 417800 | tf_op jit(solution)/shard_map/ppermute | solution.py:149
  5.6 32.6 %collective-permute-start.4 = (bf16[136,512]{1,0:T(8,128)(2,1)}, bf16[136,512]{1,0:T(8,128)(2,1)S(1)}, u32[]{:S(2)}, u32[]{:S(2)}) collective-permute-start(bf16[136,512]{1,0:T(8,128)(2,1)} %pad_maximum_fusion), channel_id=1, source_target_pairs={{0,1},{2,0},{4,2},{6,4},{7,6},{5,7},{3,5},{1,3},{8,9},{10,8},{12,1... | collective-permute-start | bytes 417800 | tf_op jit(solution)/shard_map/ppermute | solution.py:153
  5.6 9.0 %copy-start.36 = (s32[8]{0:T(128)S(1)}, s32[8]{0:T(128)}, u32[]{:S(2)}) copy-start(s32[8]{0:T(128)} %constant.171.clone) | copy-start | bytes 100
  5.6 9.6 %copy-start.35 = (s32[8]{0:T(128)S(1)}, s32[8]{0:T(128)}, u32[]{:S(2)}) copy-start(s32[8]{0:T(128)} %constant.173.clone) | copy-start | bytes 100
  5.6 10.3 %copy-start.1 = (s32[8]{0:T(128)S(1)}, s32[8]{0:T(128)}, u32[]{:S(2)}) copy-start(s32[8]{0:T(128)} %constant.172.clone) | copy-start | bytes 100
  6.8 11.0 %copy-start.33 = (f32[1,128]{1,0:T(1,128)S(1)}, f32[1,128]{1,0:T(1,128)}, u32[]{:S(2)}) copy-start(f32[1,128]{1,0:T(1,128)} %param.25) | copy-start | bytes 1540
  6.8 11.6 %copy-start.34 = (f32[1,128]{1,0:T(1,128)S(1)}, f32[1,128]{1,0:T(1,128)}, u32[]{:S(2)}) copy-start(f32[1,128]{1,0:T(1,128)} %param.26) | copy-start | bytes 1540
  6.8 12.7 %copy-start.32 = (s32[8]{0:T(128)S(1)}, s32[8]{0:T(128)}, u32[]{:S(2)}) copy-start(s32[8]{0:T(128)} %param.23) | copy-start | bytes 100
  6.8 12.7 %copy-start.28 = (s32[8,256]{1,0:T(8,128)S(1)}, s32[8,256]{1,0:T(8,128)}, u32[]{:S(2)}) copy-start(s32[8,256]{1,0:T(8,128)} %param.22) | copy-start | bytes 24580
  8.3 57.5 %all-to-all-start = ((bf16[8,64,512]{2,1,0:T(8,128)(2,1)}), bf16[8,64,512]{2,1,0:T(8,128)(2,1)S(1)}, u32[]{:S(2)}, u32[]{:S(2)}) async-start(bf16[8,64,512]{2,1,0:T(8,128)(2,1)} %reshape.580), calls=%async_computation | async-start | bytes 1048576 | tf_op jit(solution)/shard_map/all_to_all | solution.py:415
  19.6 12.8 %copy-start.16 = (bf16[1,256,1024]{2,1,0:T(8,128)(2,1)S(1)}, bf16[1,256,1024]{2,1,0:T(8,128)(2,1)}, u32[]{:S(2)}) copy-start(bf16[1,256,1024]{2,1,0:T(8,128)(2,1)} %param.21) | copy-start | bytes 1572868
  32.2 3.9 %copy-start.17 = (bf16[1,128,512]{2,1,0:T(8,128)(2,1)S(1)}, bf16[1,128,512]{2,1,0:T(8,128)(2,1)}, u32[]{:S(2)}) copy-start(bf16[1,128,512]{2,1,0:T(8,128)(2,1)} %param.27) | copy-start | bytes 393220
  36.1 17.3 %copy-start.18 = (bf16[8,256,128]{2,1,0:T(8,128)(2,1)S(1)}, bf16[8,256,128]{2,1,0:T(8,128)(2,1)}, u32[]{:S(2)}) copy-start(bf16[8,256,128]{2,1,0:T(8,128)(2,1)} %gather_fusion.2) | copy-start | bytes 1572868
  36.1 5.3 %collective-permute-start.1 = (bf16[136,512]{1,0:T(8,128)(2,1)}, bf16[136,512]{1,0:T(8,128)(2,1)S(1)}, u32[]{:S(2)}, u32[]{:S(2)}) collective-permute-start(bf16[136,512]{1,0:T(8,128)(2,1)} %collective-permute-done), channel_id=1, source_target_pairs={{0,2},{2,4},{4,6},{6,7},{7,5},{5,3},{3,1},{1,0},{8,10},{10,12},{12... | collective-permute-start | bytes 417800 | tf_op jit(solution)/shard_map/ppermute | solution.py:149
  38.2 5.3 %collective-permute-start.5 = (bf16[136,512]{1,0:T(8,128)(2,1)S(1)}, bf16[136,512]{1,0:T(8,128)(2,1)S(1)}, u32[]{:S(2)}, u32[]{:S(2)}) collective-permute-start(bf16[136,512]{1,0:T(8,128)(2,1)S(1)} %collective-permute-done.4), channel_id=1, source_target_pairs={{0,1},{2,0},{4,2},{6,4},{7,6},{5,7},{3,5},{1,3},{8,9},{10,8},{12,1... | collective-permute-start | bytes 417800 | tf_op jit(solution)/shard_map/ppermute | solution.py:153
  41.4 5.6 %collective-permute-start.2 = (bf16[136,512]{1,0:T(8,128)(2,1)S(1)}, bf16[136,512]{1,0:T(8,128)(2,1)S(1)}, u32[]{:S(2)}, u32[]{:S(2)}) collective-permute-start(bf16[136,512]{1,0:T(8,128)(2,1)S(1)} %collective-permute-done.1), channel_id=1, source_target_pairs={{0,2},{2,4},{4,6},{6,7},{7,5},{5,3},{3,1},{1,0},{8,10},{10,12},{12... | collective-permute-start | bytes 417800 | tf_op jit(solution)/shard_map/ppermute | solution.py:149
  43.5 9.9 %collective-permute-start.6 = (bf16[136,512]{1,0:T(8,128)(2,1)S(1)}, bf16[136,512]{1,0:T(8,128)(2,1)S(1)}, u32[]{:S(2)}, u32[]{:S(2)}) collective-permute-start(bf16[136,512]{1,0:T(8,128)(2,1)S(1)} %collective-permute-done.5), channel_id=1, source_target_pairs={{0,1},{2,0},{4,2},{6,4},{7,6},{5,7},{3,5},{1,3},{8,9},{10,8},{12,1... | collective-permute-start | bytes 417800 | tf_op jit(solution)/shard_map/ppermute | solution.py:153
  47.1 6.3 %collective-permute-start.3 = (bf16[136,512]{1,0:T(8,128)(2,1)S(1)}, bf16[136,512]{1,0:T(8,128)(2,1)S(1)}, u32[]{:S(2)}, u32[]{:S(2)}) collective-permute-start(bf16[136,512]{1,0:T(8,128)(2,1)S(1)} %collective-permute-done.2), channel_id=1, source_target_pairs={{0,2},{2,4},{4,6},{6,7},{7,5},{5,3},{3,1},{1,0},{8,10},{10,12},{12... | collective-permute-start | bytes 417800 | tf_op jit(solution)/shard_map/ppermute | solution.py:149
  54.0 6.4 %copy-start.30 = (f32[256]{0:T(256)S(1)}, f32[256]{0:T(256)}, u32[]{:S(2)}) copy-start(f32[256]{0:T(256)} %broadcast_bitcast_fusion.1) | copy-start | bytes 3076
  54.0 9.0 %collective-permute-start.11 = (bf16[256,512]{1,0:T(8,128)(2,1)S(1)}, bf16[256,512]{1,0:T(8,128)(2,1)}, u32[]{:S(2)}, u32[]{:S(2)}) collective-permute-start(bf16[256,512]{1,0:T(8,128)(2,1)S(1)} %fusion.39), channel_id=1, source_target_pairs={{0,1},{2,0},{4,2},{6,4},{7,6},{5,7},{3,5},{1,3},{8,9},{10,8},{12,1... | collective-permute-start | bytes 786440 | tf_op jit(solution)/shard_map/ppermute | solution.py:153
  55.6 8.8 %collective-permute-start.7 = (bf16[256,512]{1,0:T(8,128)(2,1)S(1)}, bf16[256,512]{1,0:T(8,128)(2,1)}, u32[]{:S(2)}, u32[]{:S(2)}) collective-permute-start(bf16[256,512]{1,0:T(8,128)(2,1)S(1)} %fusion.39), channel_id=1, source_target_pairs={{0,2},{2,4},{4,6},{6,7},{7,5},{5,3},{3,1},{1,0},{8,10},{10,12},{12... | collective-permute-start | bytes 786440 | tf_op jit(solution)/shard_map/ppermute | solution.py:149
  63.1 30.9 %collective-permute-start.12 = (bf16[256,512]{1,0:T(8,128)(2,1)}, bf16[256,512]{1,0:T(8,128)(2,1)}, u32[]{:S(2)}, u32[]{:S(2)}) collective-permute-start(bf16[256,512]{1,0:T(8,128)(2,1)} %collective-permute-done.11), channel_id=1, source_target_pairs={{0,1},{2,0},{4,2},{6,4},{7,6},{5,7},{3,5},{1,3},{8,9},{10,8},{12,1... | collective-permute-start | bytes 786440 | tf_op jit(solution)/shard_map/ppermute | solution.py:153
  64.5 21.4 %collective-permute-start.8 = (bf16[256,512]{1,0:T(8,128)(2,1)}, bf16[256,512]{1,0:T(8,128)(2,1)}, u32[]{:S(2)}, u32[]{:S(2)}) collective-permute-start(bf16[256,512]{1,0:T(8,128)(2,1)} %collective-permute-done.7), channel_id=1, source_target_pairs={{0,2},{2,4},{4,6},{6,7},{7,5},{5,3},{3,1},{1,0},{8,10},{10,12},{12... | collective-permute-start | bytes 786440 | tf_op jit(solution)/shard_map/ppermute | solution.py:149
  68.8 0.8 copy-start.2
  79.1 0.8 copy-start.4
  87.1 0.8 copy-start.6
  95.2 0.8 copy-start.8
  98.9 6.6 %collective-permute-start.13 = (bf16[256,512]{1,0:T(8,128)(2,1)}, bf16[256,512]{1,0:T(8,128)(2,1)S(1)}, u32[]{:S(2)}, u32[]{:S(2)}) collective-permute-start(bf16[256,512]{1,0:T(8,128)(2,1)} %collective-permute-done.12), channel_id=1, source_target_pairs={{0,1},{2,0},{4,2},{6,4},{7,6},{5,7},{3,5},{1,3},{8,9},{10,8},{12,1... | collective-permute-start | bytes 786440 | tf_op jit(solution)/shard_map/ppermute | solution.py:153
  101.1 11.5 %collective-permute-start.9 = (bf16[256,512]{1,0:T(8,128)(2,1)}, bf16[256,512]{1,0:T(8,128)(2,1)}, u32[]{:S(2)}, u32[]{:S(2)}) collective-permute-start(bf16[256,512]{1,0:T(8,128)(2,1)} %collective-permute-done.8), channel_id=1, source_target_pairs={{0,2},{2,4},{4,6},{6,7},{7,5},{5,3},{3,1},{1,0},{8,10},{10,12},{12... | collective-permute-start | bytes 786440 | tf_op jit(solution)/shard_map/ppermute | solution.py:149
  105.8 0.8 copy-start.10
  113.9 0.8 copy-start.12
  117.5 6.6 %collective-permute-start.10 = (bf16[256,512]{1,0:T(8,128)(2,1)}, bf16[256,512]{1,0:T(8,128)(2,1)S(1)}, u32[]{:S(2)}, u32[]{:S(2)}) collective-permute-start(bf16[256,512]{1,0:T(8,128)(2,1)} %collective-permute-done.9), channel_id=1, source_target_pairs={{0,2},{2,4},{4,6},{6,7},{7,5},{5,3},{3,1},{1,0},{8,10},{10,12},{12... | collective-permute-start | bytes 786440 | tf_op jit(solution)/shard_map/ppermute | solution.py:149
  124.4 0.8 copy-start.14
  125.9 12.3 %copy-start.3 = (f32[256,512]{1,0:T(8,128)S(1)}, f32[256,512]{1,0:T(8,128)}, u32[]{:S(2)}) copy-start(f32[256,512]{1,0:T(8,128)} %copy-done.2) | copy-start | bytes 1572868
  125.9 12.3 %copy-start.31 = (f32[256]{0:T(256)S(1)}, f32[256]{0:T(256)}, u32[]{:S(2)}) copy-start(f32[256]{0:T(256)} %broadcast_bitcast_fusion) | copy-start | bytes 3076
  128.1 10.1 %copy-start.5 = (f32[256,512]{1,0:T(8,128)S(1)}, f32[256,512]{1,0:T(8,128)}, u32[]{:S(2)}) copy-start(f32[256,512]{1,0:T(8,128)} %copy-done.4) | copy-start | bytes 1572868
  128.1 10.2 %copy-start.7 = (f32[256,512]{1,0:T(8,128)S(1)}, f32[256,512]{1,0:T(8,128)}, u32[]{:S(2)}) copy-start(f32[256,512]{1,0:T(8,128)} %copy-done.6) | copy-start | bytes 1572868
  128.1 10.2 %copy-start.9 = (f32[256,512]{1,0:T(8,128)S(1)}, f32[256,512]{1,0:T(8,128)}, u32[]{:S(2)}) copy-start(f32[256,512]{1,0:T(8,128)} %copy-done.8) | copy-start | bytes 1572868
  128.1 10.2 %copy-start.11 = (f32[256,512]{1,0:T(8,128)S(1)}, f32[256,512]{1,0:T(8,128)}, u32[]{:S(2)}) copy-start(f32[256,512]{1,0:T(8,128)} %copy-done.10) | copy-start | bytes 1572868
  128.1 10.2 %copy-start.13 = (f32[256,512]{1,0:T(8,128)S(1)}, f32[256,512]{1,0:T(8,128)}, u32[]{:S(2)}) copy-start(f32[256,512]{1,0:T(8,128)} %copy-done.12) | copy-start | bytes 1572868
  128.1 10.2 %copy-start.15 = (f32[256,512]{1,0:T(8,128)S(1)}, f32[256,512]{1,0:T(8,128)}, u32[]{:S(2)}) copy-start(f32[256,512]{1,0:T(8,128)} %copy-done.14) | copy-start | bytes 1572868
  138.2 0.9 copy-start.20
  138.3 1.6 copy-start.19
  138.3 2.3 %copy-start.22 = (bf16[1,256,256]{2,1,0:T(8,128)(2,1)S(1)}, bf16[1,256,256]{2,1,0:T(8,128)(2,1)}, u32[]{:S(2)}) copy-start(bf16[1,256,256]{2,1,0:T(8,128)(2,1)} %fusion.64) | copy-start | bytes 393220
  138.3 3.0 %copy-start.25 = (bf16[1,256,256]{2,1,0:T(8,128)(2,1)S(1)}, bf16[1,256,256]{2,1,0:T(8,128)(2,1)}, u32[]{:S(2)}) copy-start(bf16[1,256,256]{2,1,0:T(8,128)(2,1)} %fusion.65) | copy-start | bytes 393220
  138.8 3.2 %copy-start.26 = (bf16[1,256,256]{2,1,0:T(8,128)(2,1)S(1)}, bf16[1,256,256]{2,1,0:T(8,128)(2,1)}, u32[]{:S(2)}) copy-start(bf16[1,256,256]{2,1,0:T(8,128)(2,1)} %fusion.66) | copy-start | bytes 393220
  138.8 4.0 %copy-start.21 = (bf16[1,256,256]{2,1,0:T(8,128)(2,1)S(1)}, bf16[1,256,256]{2,1,0:T(8,128)(2,1)}, u32[]{:S(2)}) copy-start(bf16[1,256,256]{2,1,0:T(8,128)(2,1)} %fusion.67) | copy-start | bytes 393220
  138.8 4.7 %copy-start.23 = (bf16[1,256,256]{2,1,0:T(8,128)(2,1)S(1)}, bf16[1,256,256]{2,1,0:T(8,128)(2,1)}, u32[]{:S(2)}) copy-start(bf16[1,256,256]{2,1,0:T(8,128)(2,1)} %fusion.68) | copy-start | bytes 393220
  138.8 5.4 %copy-start.24 = (bf16[1,256,256]{2,1,0:T(8,128)(2,1)S(1)}, bf16[1,256,256]{2,1,0:T(8,128)(2,1)}, u32[]{:S(2)}) copy-start(bf16[1,256,256]{2,1,0:T(8,128)(2,1)} %fusion.69) | copy-start | bytes 393220
  163.2 18.1 %copy-start.29 = (pred[8]{0:T(512)(128)(4,1)S(1)}, pred[8]{0:T(512)(128)(4,1)}, u32[]{:S(2)}) copy-start(pred[8]{0:T(512)(128)(4,1)} %compare_and_fusion.1) | copy-start | bytes 28
  163.2 18.3 %copy-start.27 = (f32[1,4096]{1,0:T(1,128)S(1)}, f32[1,4096]{1,0:T(1,128)}, u32[]{:S(2)}) copy-start(f32[1,4096]{1,0:T(1,128)} %param.30) | copy-start | bytes 49156
  163.8 5.0 %collective-permute-start.14 = (f32[8,1,4096]{2,0,1:T(8,128)S(1)}, f32[8,1,4096]{2,0,1:T(8,128)S(1)}, u32[]{:S(2)}, u32[]{:S(2)}) collective-permute-start(f32[8,1,4096]{2,0,1:T(8,128)S(1)} %convolution_bitcast_fusion), channel_id=1, source_target_pairs={{0,1},{1,0},{2,3},{3,2},{4,5},{5,4},{6,7},{7,6},{8,9},{9,8},{10,11... | collective-permute-start | bytes 393224 | tf_op jit(solution)/shard_map/ppermute | solution.py:114
  168.8 5.0 %collective-permute-start.15 = (f32[8,1,4096]{2,0,1:T(8,128)S(1)}, f32[8,1,4096]{2,0,1:T(8,128)S(1)}, u32[]{:S(2)}, u32[]{:S(2)}) collective-permute-start(f32[8,1,4096]{2,0,1:T(8,128)S(1)} %add.260), channel_id=1, source_target_pairs={{0,2},{1,3},{2,0},{3,1},{4,6},{5,7},{6,4},{7,5},{8,10},{9,11},{10,... | collective-permute-start | bytes 393224 | tf_op jit(solution)/shard_map/ppermute | solution.py:114
  173.9 7.3 %collective-permute-start.16 = (f32[8,1,4096]{2,0,1:T(8,128)S(1)}, f32[8,1,4096]{2,0,1:T(8,128)S(1)}, u32[]{:S(2)}, u32[]{:S(2)}) collective-permute-start(f32[8,1,4096]{2,0,1:T(8,128)S(1)} %add.261), channel_id=1, source_target_pairs={{0,4},{1,5},{2,6},{3,7},{4,0},{5,1},{6,2},{7,3},{8,12},{9,13},{10,... | collective-permute-start | bytes 393224 | tf_op jit(solution)/shard_map/ppermute | solution.py:114
  196.0 4.3 %collective-permute-start.17 = (f32[2,2,1,1,4096]{4,2,3,1,0:T(1,128)S(1)}, f32[2,2,1,1,4096]{4,2,3,1,0:T(1,128)S(1)}, u32[]{:S(2)}, u32[]{:S(2)}) collective-permute-start(f32[2,2,1,1,4096]{4,2,3,1,0:T(1,128)S(1)} %dynamic-slice_bitcast_fusion), channel_id=1, source_target_pairs={{0,1},{1,0},{2,3},{3,2},{4,5},{5,4},{6,7},{7,6},{8,9},{9,8},{10,11... | collective-permute-start | bytes 196616 | tf_op jit(solution)/shard_map/ppermute | solution.py:474
  200.4 4.0 %collective-permute-start.18 = (f32[2,1,1,1,4096]{4,2,3,1,0:T(1,128)S(1)}, f32[2,1,1,1,4096]{4,2,3,1,0:T(1,128)S(1)}, u32[]{:S(2)}, u32[]{:S(2)}) collective-permute-start(f32[2,1,1,1,4096]{4,2,3,1,0:T(1,128)S(1)} %constant_dynamic-slice_fusion), channel_id=1, source_target_pairs={{0,2},{1,3},{2,0},{3,1},{4,6},{5,7},{6,4},{7,5},{8,10},{9,11},{10,... | collective-permute-start | bytes 98312 | tf_op jit(solution)/shard_map/ppermute | solution.py:474
  204.5 5.1 %collective-permute-start.20 = (f32[1,4096]{1,0:T(1,128)S(1)}, f32[1,4096]{1,0:T(1,128)S(1)}, u32[]{:S(2)}, u32[]{:S(2)}) collective-permute-start(f32[1,4096]{1,0:T(1,128)S(1)} %dynamic-slice_bitcast_fusion.1), channel_id=1, source_target_pairs={{0,12},{1,13},{2,14},{3,15},{4,8},{5,9},{6,10},{7,11},{8,20},{9,21... | collective-permute-start | bytes 49160 | tf_op jit(solution)/shard_map/ppermute | solution.py:491
  204.5 5.0 %collective-permute-start.19 = (f32[1,4096]{1,0:T(1,128)S(1)}, f32[1,4096]{1,0:T(1,128)S(1)}, u32[]{:S(2)}, u32[]{:S(2)}) collective-permute-start(f32[1,4096]{1,0:T(1,128)S(1)} %bitcast_add_fusion.1), channel_id=1, source_target_pairs={{0,8},{1,9},{2,10},{3,11},{4,12},{5,13},{6,14},{7,15},{8,16},{9,17... | collective-permute-start | bytes 49160 | tf_op jit(solution)/shard_map/ppermute | solution.py:490

commit v6 on v5

--- a/solution.py
+++ b/solution.py
@@ -422,30 +422,28 @@
 
     ring_hidden = RingGather(tile_hidden, group_size, my_index)
     hidden_slots, hidden_sources = ring_hidden.finish()
-    hidden_slot_of_source = jnp.argmax(
-        hidden_sources[None, :] == jnp.arange(group_size, dtype=jnp.int32)[:, None], axis=1
-    ).astype(jnp.int32)
-    slot_kv = []
-    for slot in range(group_size):
-        keyval = jnp.dot(hidden_slots[slot], weight_out, preferred_element_type=jnp.float32)
-        normed_keys = head_norm(keyval[:, :my_cols], k_gain[0])
-        slot_kv.append(
-            jnp.concatenate([normed_keys, keyval[:, my_cols:]], axis=1).astype(jnp.bfloat16)
-        )
-    table = jnp.stack(slot_kv).reshape(group_size * tiles_here, 2 * my_cols)
-    owner = site_tiles // tiles_here
-    rows = jnp.take(hidden_slot_of_source, owner) * tiles_here + site_tiles % tiles_here
-    pair_kv = table[rows.reshape(-1)].reshape(all_sites, list_width, 2, heads_here, head_size)
-
+    table_hidden = hidden_slots.reshape(group_size * tiles_here, hidden_width)
+    keyval = jnp.dot(table_hidden, weight_out, preferred_element_type=jnp.float32)
+    normed_keys = head_norm(keyval[:, :my_cols], k_gain[0])
+    table = jnp.concatenate([normed_keys, keyval[:, my_cols:]], axis=1).astype(jnp.bfloat16)
+    table = table.reshape(group_size * tiles_here, 2, heads_here, head_size)
+
+    tile_of_row = (
+        hidden_sources[:, None] * tiles_here + jnp.arange(tiles_here, dtype=jnp.int32)[None, :]
+    ).reshape(-1)
     slot_index = jnp.arange(list_width, dtype=jnp.int32)
-    live = (slot_index[None, :] < site_count[:, None]).astype(jnp.float32)
+    live = slot_index[None, :] < site_count[:, None]
+    named = jnp.logical_and(
+        site_tiles[:, :, None] == tile_of_row[None, None, :], live[:, :, None]
+    )
+    uses = jnp.sum(named.astype(jnp.float32), axis=1)
     scores = jnp.einsum(
-        "nhd,nlhd->nhl", query_heads, pair_kv[:, :, 0], preferred_element_type=jnp.float32
+        "nhd,rhd->nhr", query_heads, table[:, 0], preferred_element_type=jnp.float32
     ) / math.sqrt(head_size)
-    exponents = jnp.exp(scores) * live[:, None, :]
+    exponents = jnp.exp(scores) * uses[:, None, :]
     weights = (exponents / jnp.sum(exponents, axis=-1, keepdims=True)).astype(jnp.bfloat16)
     combined = jnp.einsum(
-        "nhl,nlhd->nhd", weights, pair_kv[:, :, 1], preferred_element_type=jnp.float32
+        "nhr,rhd->nhd", weights, table[:, 1], preferred_element_type=jnp.float32
     )
     combined = combined.reshape(all_sites, my_cols).astype(jnp.bfloat16)
     attn_part = jnp.dot(combined, out_weight[0], preferred_element_type=jnp.float32)

time: 212 us -> 130 us (0.61)
  local copies, waits for them, and re-layouts: 74 us -> 16.1 us
  other arithmetic: 39 us -> 8.68 us
  waiting for transfers between devices: 37.5 us -> 47.1 us
  matrix products: 25.4 us -> 22.1 us
    gather x3 -> x0, local copies, waits for them, and re-layouts: 23.7 us -> none  [the longest x2 12.6 us: heads_split(): jnp.take(hidden_slot_of_source, owner) * tiles_here]
    ppermute x8, waiting for transfers between devices: 11.6 us -> 26.1 us  [_issue(): self.ahead = lax.ppermute(self.ahead, 'site', self.forward)]
    rsqrt x9 -> x2, other arithmetic: 11.3 us -> 0.02 us  [head_norm(): lax.rsqrt(jnp.mean(shaped * shaped, axis=-1, keepdims=True) + epsilon)]
    concatenate x8 -> x0, local copies, waits for them, and re-layouts: 10.1 us -> none  [heads_split(): jnp.concatenate([normed_keys, keyval[:, my_cols:]], axis=1)]
    mul x8 -> x0, local copies, waits for them, and re-layouts: 9.17 us -> none  [head_norm(): shaped * shaped]
    reduce_sum x8 -> x1, other arithmetic: 9.28 us -> 0.19 us  [head_norm(): jnp.mean(shaped * shaped, axis=-1, keepdims=True) + epsilon]
    mul x10 -> x2, local copies, waits for them, and re-layouts: 10.1 us -> 1.11 us  [head_norm(): shaped * lax.rsqrt(jnp.mean(shaped * shaped, axis=-1, keepdims=True) + ep...]
    unnamed x13 -> x4, other arithmetic: 6.74 us -> 1.07 us
  transfers between devices with their start and end apart: 22 -> 22, of which waited for: 12 -> 14; matrix products, arithmetic and copies ran while one was open for 33% -> 18% of each run, Pallas kernels for 0% -> 0%
where the time goes in v6:
time: 130 us; the launch traced here: 129 us
  waiting for transfers between devices  47.1 us (36%)
  starting transfers between devices  34.8 us (27%)
  matrix products  22.1 us (17%)
  local copies, waits for them, and re-layouts  16.1 us (12%)
  other arithmetic  8.68 us (7%)
    ppermute x8, waiting for transfers between devices, _issue(): self.ahead = lax.ppermute(self.ahead, 'site', self.forward)  26.1 us
    ppermute x8, starting transfers between devices, _issue(): self.ahead = lax.ppermute(self.ahead, 'site', self.forward)  18.1 us
    dot_general x3, matrix products, by_rows(): lax.dot_general(left, weight_rows, (((1,), (1,)), ((), ())), preferred_el...  12.5 us
    ppermute x3, waiting for transfers between devices, doubling_sum(): state = state + lax.ppermute(state, 'site', xor_pairs(count, bit))  12.1 us
    unnamed x44, local copies, waits for them, and re-layouts  7.91 us
    ppermute x2, waiting for transfers between devices, last_round(): state = keep + lax.ppermute(send, 'site', xor_pairs(group_size, bit))  6.53 us
    all_to_all x1, starting transfers between devices, heads_split(): lax.all_to_all(col_blocks, 'site', split_axis=0, concat_axis=0, tiled=True)  6.25 us
    ppermute x3, starting transfers between devices, doubling_sum(): state = state + lax.ppermute(state, 'site', xor_pairs(count, bit))  5.2 us
  transfers between devices with their start and end apart: 22, of which 14 were waited for; matrix products, arithmetic and copies ran while one was open for 18% of the time, Pallas kernels for 0%

profile of v6, /device:TPU:0, one launch (start us, length us, event | category | flops | bytes accessed | tf_op | source)
XLA Modules:
  0.0 129.2 jit_solution(2515935496358179033)
XLA Ops:
  0.0 0.9 reduce.19
  0.9 1.6 %pad_maximum_fusion = bf16[136,512]{1,0:T(8,128)(2,1)} fusion(bf16[8,512]{1,0:T(8,128)(2,1)S(1)} %reshape_squeeze.9, bf16[128,512]{1,0:T(8,128)(2,1)} %bitcast.167), kind=kLoop, calls=%fused_computation.54 | loop fusion | flops 278528 | bytes 278528 | tf_op jit(solution)/shard_map/concatenate | solution.py:394
  2.5 3.0 %collective-permute-start = (bf16[136,512]{1,0:T(8,128)(2,1)}, bf16[136,512]{1,0:T(8,128)(2,1)}, u32[]{:S(2)}, u32[]{:S(2)}) collective-permute-start(bf16[136,512]{1,0:T(8,128)(2,1)} %pad_maximum_fusion), channel_id=1, source_target_pairs={{0,2},{2,4},{4,6},{6,7},{7,5},{5,3},{3,1},{1,0},{8,10},{10,12},{12... | collective-permute-start | bytes 417800 | tf_op jit(solution)/shard_map/ppermute | solution.py:149
  5.6 1.2 copy.39
  6.8 0.4 copy.43
  7.2 1.1 reshape.231
  8.3 6.3 %all-to-all-start = ((bf16[8,64,512]{2,1,0:T(8,128)(2,1)}), bf16[8,64,512]{2,1,0:T(8,128)(2,1)S(1)}, u32[]{:S(2)}, u32[]{:S(2)}) async-start(bf16[8,64,512]{2,1,0:T(8,128)(2,1)} %reshape.231), calls=%async_computation | async-start | bytes 1048576 | tf_op jit(solution)/shard_map/all_to_all | solution.py:415
  14.6 0.6 dynamic_slice.31
  15.2 0.7 compare_select_fusion.3
  15.9 0.6 gather_fusion
  16.6 0.6 iota_reduce_fusion
  17.2 0.5 broadcast_bitcast_fusion
  17.8 0.6 broadcast_bitcast_fusion.1
  18.5 3.1 %convert_reduce_fusion = f32[8,2048]{1,0:T(8,128)S(1)} fusion(s32[2048]{0:T(1024)S(1)} %bitcast.172, s32[8,256]{1,0:T(8,128)S(1)} %copy-done.6, pred[8,256]{1,0:T(8,128)(4,1)S(1)} %iota_compare_fusion), kind=kLoop, calls=%fused_computation.3 | loop fusion | flops 16760832 | bytes 83968 | tf_op jit(solution)/shard_map/reduce_sum | solution.py:439
  21.7 1.0 copy.31
  22.7 1.3 %copy.32 = bf16[256,8,128]{2,0,1:T(8,128)(2,1)S(1)} copy(bf16[256,8,128]{0,2,1:T(8,128)(2,1)} %bitcast.165) | data formatting | bytes 1048576 | tf_op jit(solution)/shard_map/reshape;squeeze | solution.py:405
  24.0 1.4 %gather_fusion.2 = bf16[8,256,128]{2,1,0:T(8,128)(2,1)} fusion(bf16[256,8,128]{2,0,1:T(8,128)(2,1)S(1)} %copy.32, s32[1024]{0:T(1024)S(1)} %pad_clamp_fusion), kind=kCustom, calls=%fused_computation.2 | custom fusion | bytes 1048608 | tf_op jit(solution)/shard_map/jit(_take)/gather | solution.py:405
  25.4 2.1 %collective-permute-start.1 = (bf16[136,512]{1,0:T(8,128)(2,1)}, bf16[136,512]{1,0:T(8,128)(2,1)S(1)}, u32[]{:S(2)}, u32[]{:S(2)}) collective-permute-start(bf16[136,512]{1,0:T(8,128)(2,1)} %collective-permute-done), channel_id=1, source_target_pairs={{0,2},{2,4},{4,6},{6,7},{7,5},{5,3},{3,1},{1,0},{8,10},{10,12},{12... | collective-permute-start | bytes 417800 | tf_op jit(solution)/shard_map/ppermute | solution.py:149
  27.5 0.9 bitcast_dynamic-update-slice_fusion.14
  28.5 2.3 %collective-permute-done.1 = bf16[136,512]{1,0:T(8,128)(2,1)S(1)} collective-permute-done((bf16[136,512]{1,0:T(8,128)(2,1)}, bf16[136,512]{1,0:T(8,128)(2,1)S(1)}, u32[]{:S(2)}, u32[]{:S(2)}) %collective-permute-start.1) | collective-permute-done | bytes 139296 | tf_op jit(solution)/shard_map/ppermute | solution.py:149
  30.7 2.0 %collective-permute-start.2 = (bf16[136,512]{1,0:T(8,128)(2,1)S(1)}, bf16[136,512]{1,0:T(8,128)(2,1)S(1)}, u32[]{:S(2)}, u32[]{:S(2)}) collective-permute-start(bf16[136,512]{1,0:T(8,128)(2,1)S(1)} %collective-permute-done.1), channel_id=1, source_target_pairs={{0,2},{2,4},{4,6},{6,7},{7,5},{5,3},{3,1},{1,0},{8,10},{10,12},{12... | collective-permute-start | bytes 417800 | tf_op jit(solution)/shard_map/ppermute | solution.py:149
  32.8 3.6 %collective-permute-done.2 = bf16[136,512]{1,0:T(8,128)(2,1)S(1)} collective-permute-done((bf16[136,512]{1,0:T(8,128)(2,1)S(1)}, bf16[136,512]{1,0:T(8,128)(2,1)S(1)}, u32[]{:S(2)}, u32[]{:S(2)}) %collective-permute-start.2) | collective-permute-done | bytes 139296 | tf_op jit(solution)/shard_map/ppermute | solution.py:149
  36.4 2.5 %collective-permute-start.3 = (bf16[136,512]{1,0:T(8,128)(2,1)S(1)}, bf16[136,512]{1,0:T(8,128)(2,1)S(1)}, u32[]{:S(2)}, u32[]{:S(2)}) collective-permute-start(bf16[136,512]{1,0:T(8,128)(2,1)S(1)} %collective-permute-done.2), channel_id=1, source_target_pairs={{0,2},{2,4},{4,6},{6,7},{7,5},{5,3},{3,1},{1,0},{8,10},{10,12},{12... | collective-permute-start | bytes 417800 | tf_op jit(solution)/shard_map/ppermute | solution.py:149
  38.9 2.7 %collective-permute-done.3 = bf16[136,512]{1,0:T(8,128)(2,1)S(1)} collective-permute-done((bf16[136,512]{1,0:T(8,128)(2,1)S(1)}, bf16[136,512]{1,0:T(8,128)(2,1)S(1)}, u32[]{:S(2)}, u32[]{:S(2)}) %collective-permute-start.3) | collective-permute-done | bytes 139296 | tf_op jit(solution)/shard_map/ppermute | solution.py:149
  41.7 1.4 %bitcast_dynamic-update-slice_fusion.7 = (bf16[8,256,512]{2,1,0:T(8,128)(2,1)}, bf16[256,512]{1,0:T(8,128)(2,1)}) fusion(bf16[8,136,512]{2,1,0:T(8,128)(2,1)S(1)} %bitcast_dynamic-update-slice_fusion.8, bf16[8,256,128]{2,1,0:T(8,128)(2,1)S(1)} %copy-done.4, pred[8]{0:T(512)(128)(4,1)S(1)} %compare_and_fusion), kind=kOutput, calls=%fused_computation.52 | convolution fusion | flops 269877248 | bytes 2097664 | tf_op jit(solution)/shard_map/dot_general | solution.py:407
  43.1 2.5 %collective-permute-start.7 = (bf16[256,512]{1,0:T(8,128)(2,1)}, bf16[256,512]{1,0:T(8,128)(2,1)S(1)}, u32[]{:S(2)}, u32[]{:S(2)}) collective-permute-start(bf16[256,512]{1,0:T(8,128)(2,1)} %get-tuple-element.10), channel_id=1, source_target_pairs={{0,2},{2,4},{4,6},{6,7},{7,5},{5,3},{3,1},{1,0},{8,10},{10,12},{12... | collective-permute-start | bytes 786440 | tf_op jit(solution)/shard_map/ppermute | solution.py:149
  45.7 0.6 gather_fusion.1
  46.3 6.0 %collective-permute-done.7 = bf16[256,512]{1,0:T(8,128)(2,1)S(1)} collective-permute-done((bf16[256,512]{1,0:T(8,128)(2,1)}, bf16[256,512]{1,0:T(8,128)(2,1)S(1)}, u32[]{:S(2)}, u32[]{:S(2)}) %collective-permute-start.7) | collective-permute-done | bytes 262176 | tf_op jit(solution)/shard_map/ppermute | solution.py:149
  52.4 2.4 %collective-permute-start.8 = (bf16[256,512]{1,0:T(8,128)(2,1)S(1)}, bf16[256,512]{1,0:T(8,128)(2,1)S(1)}, u32[]{:S(2)}, u32[]{:S(2)}) collective-permute-start(bf16[256,512]{1,0:T(8,128)(2,1)S(1)} %collective-permute-done.7), channel_id=1, source_target_pairs={{0,2},{2,4},{4,6},{6,7},{7,5},{5,3},{3,1},{1,0},{8,10},{10,12},{12... | collective-permute-start | bytes 786440 | tf_op jit(solution)/shard_map/ppermute | solution.py:149
  54.7 2.3 %bitcast_reduce_fusion.1 = (f32[8,2]{0,1:T(2,128)S(1)}, f32[8,256]{1,0:T(8,128)S(1)}) fusion(bf16[8,4096]{1,0:T(8,128)(2,1)S(1)} %bitcast.169, bf16[1,256,4096]{2,1,0:T(8,128)(2,1)} %param.24), kind=kOutput, calls=%fused_computation.80 | convolution fusion | flops 16785392 | bytes 2170944 | tf_op jit(solution)/shard_map/dot_general | solution.py:21
  57.1 3.7 %collective-permute-done.8 = bf16[256,512]{1,0:T(8,128)(2,1)S(1)} collective-permute-done((bf16[256,512]{1,0:T(8,128)(2,1)S(1)}, bf16[256,512]{1,0:T(8,128)(2,1)S(1)}, u32[]{:S(2)}, u32[]{:S(2)}) %collective-permute-start.8) | collective-permute-done | bytes 262176 | tf_op jit(solution)/shard_map/ppermute | solution.py:149
  60.8 2.0 %collective-permute-start.9 = (bf16[256,512]{1,0:T(8,128)(2,1)S(1)}, bf16[256,512]{1,0:T(8,128)(2,1)S(1)}, u32[]{:S(2)}, u32[]{:S(2)}) collective-permute-start(bf16[256,512]{1,0:T(8,128)(2,1)S(1)} %collective-permute-done.8), channel_id=1, source_target_pairs={{0,2},{2,4},{4,6},{6,7},{7,5},{5,3},{3,1},{1,0},{8,10},{10,12},{12... | collective-permute-start | bytes 786440 | tf_op jit(solution)/shard_map/ppermute | solution.py:149
  62.8 0.7 bitcast_dynamic-update-slice_fusion.6
  63.6 4.8 %collective-permute-done.9 = bf16[256,512]{1,0:T(8,128)(2,1)S(1)} collective-permute-done((bf16[256,512]{1,0:T(8,128)(2,1)S(1)}, bf16[256,512]{1,0:T(8,128)(2,1)S(1)}, u32[]{:S(2)}, u32[]{:S(2)}) %collective-permute-start.9) | collective-permute-done | bytes 262176 | tf_op jit(solution)/shard_map/ppermute | solution.py:149
  68.4 1.7 %collective-permute-start.10 = (bf16[256,512]{1,0:T(8,128)(2,1)S(1)}, bf16[256,512]{1,0:T(8,128)(2,1)S(1)}, u32[]{:S(2)}, u32[]{:S(2)}) collective-permute-start(bf16[256,512]{1,0:T(8,128)(2,1)S(1)} %collective-permute-done.9), channel_id=1, source_target_pairs={{0,2},{2,4},{4,6},{6,7},{7,5},{5,3},{3,1},{1,0},{8,10},{10,12},{12... | collective-permute-start | bytes 786440 | tf_op jit(solution)/shard_map/ppermute | solution.py:149
  70.1 0.7 bitcast_dynamic-update-slice_fusion.5
  70.8 0.4 collective-permute-start.13
  71.1 0.7 bitcast_dynamic-update-slice_fusion.4
  71.9 2.9 %collective-permute-done.10 = bf16[256,512]{1,0:T(8,128)(2,1)S(1)} collective-permute-done((bf16[256,512]{1,0:T(8,128)(2,1)S(1)}, bf16[256,512]{1,0:T(8,128)(2,1)S(1)}, u32[]{:S(2)}, u32[]{:S(2)}) %collective-permute-start.10) | collective-permute-done | bytes 262176 | tf_op jit(solution)/shard_map/ppermute | solution.py:149
  74.8 0.7 bitcast_dynamic-update-slice_fusion.3
  75.5 0.7 bitcast_dynamic-update-slice_fusion.2
  76.2 0.7 bitcast_dynamic-update-slice_fusion.1
  77.1 0.7 bitcast_dynamic-update-slice_fusion
  77.9 2.9 %fusion.60 = f32[2048,512]{0,1:T(8,128)S(1)} fusion(bf16[2048,512]{1,0:T(8,128)(2,1)} %bitcast.23, bf16[512,512]{1,0:T(8,128)(2,1)S(1)} %bitcast.162), kind=kOutput, calls=%fused_computation.110 | convolution fusion | flops 1073741824 | bytes 6815744 | tf_op jit(solution)/shard_map/dot_general | solution.py:426
  81.2 0.3 copy-done.8
  81.5 0.2 fusion.13
  81.8 0.3 fusion.8
  82.1 0.8 convolution_bitcast_fusion
  82.9 1.2 collective-permute-start.14
  84.1 3.7 %collective-permute-done.14 = f32[8,1,4096]{2,0,1:T(8,128)S(1)} collective-permute-done((f32[8,1,4096]{2,0,1:T(8,128)S(1)}, f32[8,1,4096]{2,0,1:T(8,128)S(1)}, u32[]{:S(2)}, u32[]{:S(2)}) %collective-permute-start.14) | collective-permute-done | bytes 131104 | tf_op jit(solution)/shard_map/ppermute | solution.py:114
  87.9 1.5 %collective-permute-start.15 = (f32[8,1,4096]{2,0,1:T(8,128)S(1)}, f32[8,1,4096]{2,0,1:T(8,128)S(1)}, u32[]{:S(2)}, u32[]{:S(2)}) collective-permute-start(f32[8,1,4096]{2,0,1:T(8,128)S(1)} %add.194), channel_id=1, source_target_pairs={{0,2},{1,3},{2,0},{3,1},{4,6},{5,7},{6,4},{7,5},{8,10},{9,11},{10,... | collective-permute-start | bytes 393224 | tf_op jit(solution)/shard_map/ppermute | solution.py:114
  89.4 3.5 %collective-permute-done.15 = f32[8,1,4096]{2,0,1:T(8,128)S(1)} collective-permute-done((f32[8,1,4096]{2,0,1:T(8,128)S(1)}, f32[8,1,4096]{2,0,1:T(8,128)S(1)}, u32[]{:S(2)}, u32[]{:S(2)}) %collective-permute-start.15) | collective-permute-done | bytes 131104 | tf_op jit(solution)/shard_map/ppermute | solution.py:114
  92.9 2.4 %collective-permute-start.16 = (f32[8,1,4096]{2,0,1:T(8,128)S(1)}, f32[8,1,4096]{2,0,1:T(8,128)S(1)}, u32[]{:S(2)}, u32[]{:S(2)}) collective-permute-start(f32[8,1,4096]{2,0,1:T(8,128)S(1)} %add.195), channel_id=1, source_target_pairs={{0,4},{1,5},{2,6},{3,7},{4,0},{5,1},{6,2},{7,3},{8,12},{9,13},{10,... | collective-permute-start | bytes 393224 | tf_op jit(solution)/shard_map/ppermute | solution.py:114
  95.4 4.9 %collective-permute-done.16 = f32[8,1,4096]{2,0,1:T(8,128)S(1)} collective-permute-done((f32[8,1,4096]{2,0,1:T(8,128)S(1)}, f32[8,1,4096]{2,0,1:T(8,128)S(1)}, u32[]{:S(2)}, u32[]{:S(2)}) %collective-permute-start.16) | collective-permute-done | bytes 131104 | tf_op jit(solution)/shard_map/ppermute | solution.py:114
  100.5 5.1 %fusion.4 = f32[8,896]{1,0:T(8,128)S(1)} fusion(bf16[1,896,4096]{2,1,0:T(8,128)(2,1)} %param.31, f32[8,1,4096]{2,0,1:T(8,128)S(1)} %get-tuple-element.8, f32[4096]{0:T(1024)S(1)} %bitcast.170, f32[8]{0:T(128)S(1)} %add_rsqrt_fusion.2), kind=kOutput, calls=%fused_computation.8 | convolution fusion | flops 58818560 | bytes 7516192 | tf_op jit(solution)/shard_map/dot_general | solution.py:21
  105.6 5.1 %fusion.17 = bf16[8,896]{1,0:T(8,128)(2,1)S(1)} fusion(bf16[1,896,4096]{2,1,0:T(8,128)(2,1)} %param.32, f32[8,896]{1,0:T(8,128)S(1)} %fusion.4, f32[8,1,4096]{2,0,1:T(8,128)S(1)} %get-tuple-element.8, f32[4096]{0:T(1024)S(1)} %bitcast.171, f32[8]{0:T(128)S(1)} %add_rsqrt_fusion.2), kind=kOutput, calls=%fused_computation.26 | convolution fusion | flops 58861568 | bytes 7530528 | tf_op jit(solution)/shard_map/dot_general | solution.py:21
  110.7 4.2 %fusion = f32[2,2,2,4096]{3,2,1,0:T(2,128)S(1)} fusion(bf16[2,2,2,896]{3,2,1,0:T(2,128)(2,1)S(1)} %dot_general.37, bf16[1,896,4096]{2,1,0:T(8,128)(2,1)} %param.33), kind=kOutput, calls=%fused_computation.4 | convolution fusion | flops 58720256 | bytes 7485440 | tf_op jit(solution)/shard_map/dot_general | solution.py:457
  115.0 1.3 %collective-permute-start.17 = (f32[2,2,1,1,4096]{4,2,3,1,0:T(1,128)S(1)}, f32[2,2,1,1,4096]{4,2,3,1,0:T(1,128)S(1)}, u32[]{:S(2)}, u32[]{:S(2)}) collective-permute-start(f32[2,2,1,1,4096]{4,2,3,1,0:T(1,128)S(1)} %dynamic-slice_bitcast_fusion), channel_id=1, source_target_pairs={{0,1},{1,0},{2,3},{3,2},{4,5},{5,4},{6,7},{7,6},{8,9},{9,8},{10,11... | collective-permute-start | bytes 196616 | tf_op jit(solution)/shard_map/ppermute | solution.py:472
  116.3 3.0 %collective-permute-done.17 = f32[2,2,1,1,4096]{4,2,3,1,0:T(1,128)S(1)} collective-permute-done((f32[2,2,1,1,4096]{4,2,3,1,0:T(1,128)S(1)}, f32[2,2,1,1,4096]{4,2,3,1,0:T(1,128)S(1)}, u32[]{:S(2)}, u32[]{:S(2)}) %collective-permute-start.17) | collective-permute-done | bytes 65568 | tf_op jit(solution)/shard_map/ppermute | solution.py:472
  119.5 0.5 collective-permute-start.18
  119.9 3.5 %collective-permute-done.18 = f32[2,1,1,1,4096]{4,2,3,1,0:T(1,128)S(1)} collective-permute-done((f32[2,1,1,1,4096]{4,2,3,1,0:T(1,128)S(1)}, f32[2,1,1,1,4096]{4,2,3,1,0:T(1,128)S(1)}, u32[]{:S(2)}, u32[]{:S(2)}) %collective-permute-start.18) | collective-permute-done | bytes 32800 | tf_op jit(solution)/shard_map/ppermute | solution.py:472
  123.6 2.8 %collective-permute-start.19 = (f32[1,4096]{1,0:T(1,128)S(1)}, f32[1,4096]{1,0:T(1,128)S(1)}, u32[]{:S(2)}, u32[]{:S(2)}) collective-permute-start(f32[1,4096]{1,0:T(1,128)S(1)} %bitcast_add_fusion.1), channel_id=1, source_target_pairs={{0,8},{1,9},{2,10},{3,11},{4,12},{5,13},{6,14},{7,15},{8,16},{9,17... | collective-permute-start | bytes 49160 | tf_op jit(solution)/shard_map/ppermute | solution.py:488
  126.4 2.1 %collective-permute-done.20 = f32[1,4096]{1,0:T(1,128)S(1)} collective-permute-done((f32[1,4096]{1,0:T(1,128)S(1)}, f32[1,4096]{1,0:T(1,128)S(1)}, u32[]{:S(2)}, u32[]{:S(2)}) %collective-permute-start.20) | collective-permute-done | bytes 16416 | tf_op jit(solution)/shard_map/ppermute | solution.py:489
  128.6 0.6 convert_bitcast_fusion
  (80 shorter events, 1.9 us)
Async XLA Ops:
  0.0 82.1 %copy-start = (bf16[1,256,4096]{2,1,0:T(8,128)(2,1)S(1)}, bf16[1,256,4096]{2,1,0:T(8,128)(2,1)}, u32[]{:S(2)}) copy-start(bf16[1,256,4096]{2,1,0:T(8,128)(2,1)} %param.29) | copy-start | bytes 6291460
  2.5 22.9 %collective-permute-start = (bf16[136,512]{1,0:T(8,128)(2,1)}, bf16[136,512]{1,0:T(8,128)(2,1)}, u32[]{:S(2)}, u32[]{:S(2)}) collective-permute-start(bf16[136,512]{1,0:T(8,128)(2,1)} %pad_maximum_fusion), channel_id=1, source_target_pairs={{0,2},{2,4},{4,6},{6,7},{7,5},{5,3},{3,1},{1,0},{8,10},{10,12},{12... | collective-permute-start | bytes 417800 | tf_op jit(solution)/shard_map/ppermute | solution.py:149
  5.5 21.9 %collective-permute-start.4 = (bf16[136,512]{1,0:T(8,128)(2,1)}, bf16[136,512]{1,0:T(8,128)(2,1)S(1)}, u32[]{:S(2)}, u32[]{:S(2)}) collective-permute-start(bf16[136,512]{1,0:T(8,128)(2,1)} %pad_maximum_fusion), channel_id=1, source_target_pairs={{0,1},{2,0},{4,2},{6,4},{7,6},{5,7},{3,5},{1,3},{8,9},{10,8},{12,1... | collective-permute-start | bytes 417800 | tf_op jit(solution)/shard_map/ppermute | solution.py:153
  5.5 9.1 %copy-start.13 = (s32[8]{0:T(128)S(1)}, s32[8]{0:T(128)}, u32[]{:S(2)}) copy-start(s32[8]{0:T(128)} %constant.122.clone) | copy-start | bytes 100
  5.5 9.7 %copy-start.12 = (s32[8]{0:T(128)S(1)}, s32[8]{0:T(128)}, u32[]{:S(2)}) copy-start(s32[8]{0:T(128)} %constant.124.clone) | copy-start | bytes 100
  5.5 10.3 %copy-start.1 = (s32[8]{0:T(128)S(1)}, s32[8]{0:T(128)}, u32[]{:S(2)}) copy-start(s32[8]{0:T(128)} %constant.123.clone) | copy-start | bytes 100
  6.7 10.5 %copy-start.10 = (f32[1,128]{1,0:T(1,128)S(1)}, f32[1,128]{1,0:T(1,128)}, u32[]{:S(2)}) copy-start(f32[1,128]{1,0:T(1,128)} %param.25) | copy-start | bytes 1540
  6.8 11.0 %copy-start.11 = (f32[1,128]{1,0:T(1,128)S(1)}, f32[1,128]{1,0:T(1,128)}, u32[]{:S(2)}) copy-start(f32[1,128]{1,0:T(1,128)} %param.26) | copy-start | bytes 1540
  6.8 11.6 %copy-start.9 = (s32[8]{0:T(128)S(1)}, s32[8]{0:T(128)}, u32[]{:S(2)}) copy-start(s32[8]{0:T(128)} %param.23) | copy-start | bytes 100
  6.8 11.7 %copy-start.6 = (s32[8,256]{1,0:T(8,128)S(1)}, s32[8,256]{1,0:T(8,128)}, u32[]{:S(2)}) copy-start(s32[8,256]{1,0:T(8,128)} %param.22) | copy-start | bytes 24580
  6.8 14.9 %copy-start.2 = (bf16[1,256,1024]{2,1,0:T(8,128)(2,1)S(1)}, bf16[1,256,1024]{2,1,0:T(8,128)(2,1)}, u32[]{:S(2)}) copy-start(bf16[1,256,1024]{2,1,0:T(8,128)(2,1)} %param.21) | copy-start | bytes 1572868
  8.3 69.5 %all-to-all-start = ((bf16[8,64,512]{2,1,0:T(8,128)(2,1)}), bf16[8,64,512]{2,1,0:T(8,128)(2,1)S(1)}, u32[]{:S(2)}, u32[]{:S(2)}) async-start(bf16[8,64,512]{2,1,0:T(8,128)(2,1)} %reshape.231), calls=%async_computation | async-start | bytes 1048576 | tf_op jit(solution)/shard_map/all_to_all | solution.py:415
  14.6 10.8 %copy-start.3 = (bf16[1,128,512]{2,1,0:T(8,128)(2,1)S(1)}, bf16[1,128,512]{2,1,0:T(8,128)(2,1)}, u32[]{:S(2)}) copy-start(bf16[1,128,512]{2,1,0:T(8,128)(2,1)} %param.27) | copy-start | bytes 393220
  25.4 16.3 %copy-start.4 = (bf16[8,256,128]{2,1,0:T(8,128)(2,1)S(1)}, bf16[8,256,128]{2,1,0:T(8,128)(2,1)}, u32[]{:S(2)}) copy-start(bf16[8,256,128]{2,1,0:T(8,128)(2,1)} %gather_fusion.2) | copy-start | bytes 1572868
  25.4 5.3 %collective-permute-start.1 = (bf16[136,512]{1,0:T(8,128)(2,1)}, bf16[136,512]{1,0:T(8,128)(2,1)S(1)}, u32[]{:S(2)}, u32[]{:S(2)}) collective-permute-start(bf16[136,512]{1,0:T(8,128)(2,1)} %collective-permute-done), channel_id=1, source_target_pairs={{0,2},{2,4},{4,6},{6,7},{7,5},{5,3},{3,1},{1,0},{8,10},{10,12},{12... | collective-permute-start | bytes 417800 | tf_op jit(solution)/shard_map/ppermute | solution.py:149
  27.5 5.3 %collective-permute-start.5 = (bf16[136,512]{1,0:T(8,128)(2,1)S(1)}, bf16[136,512]{1,0:T(8,128)(2,1)S(1)}, u32[]{:S(2)}, u32[]{:S(2)}) collective-permute-start(bf16[136,512]{1,0:T(8,128)(2,1)S(1)} %collective-permute-done.4), channel_id=1, source_target_pairs={{0,1},{2,0},{4,2},{6,4},{7,6},{5,7},{3,5},{1,3},{8,9},{10,8},{12,1... | collective-permute-start | bytes 417800 | tf_op jit(solution)/shard_map/ppermute | solution.py:153
  30.7 5.6 %collective-permute-start.2 = (bf16[136,512]{1,0:T(8,128)(2,1)S(1)}, bf16[136,512]{1,0:T(8,128)(2,1)S(1)}, u32[]{:S(2)}, u32[]{:S(2)}) collective-permute-start(bf16[136,512]{1,0:T(8,128)(2,1)S(1)} %collective-permute-done.1), channel_id=1, source_target_pairs={{0,2},{2,4},{4,6},{6,7},{7,5},{5,3},{3,1},{1,0},{8,10},{10,12},{12... | collective-permute-start | bytes 417800 | tf_op jit(solution)/shard_map/ppermute | solution.py:149
  32.7 8.9 %collective-permute-start.6 = (bf16[136,512]{1,0:T(8,128)(2,1)S(1)}, bf16[136,512]{1,0:T(8,128)(2,1)S(1)}, u32[]{:S(2)}, u32[]{:S(2)}) collective-permute-start(bf16[136,512]{1,0:T(8,128)(2,1)S(1)} %collective-permute-done.5), channel_id=1, source_target_pairs={{0,1},{2,0},{4,2},{6,4},{7,6},{5,7},{3,5},{1,3},{8,9},{10,8},{12,1... | collective-permute-start | bytes 417800 | tf_op jit(solution)/shard_map/ppermute | solution.py:153
  36.4 5.2 %collective-permute-start.3 = (bf16[136,512]{1,0:T(8,128)(2,1)S(1)}, bf16[136,512]{1,0:T(8,128)(2,1)S(1)}, u32[]{:S(2)}, u32[]{:S(2)}) collective-permute-start(bf16[136,512]{1,0:T(8,128)(2,1)S(1)} %collective-permute-done.2), channel_id=1, source_target_pairs={{0,2},{2,4},{4,6},{6,7},{7,5},{5,3},{3,1},{1,0},{8,10},{10,12},{12... | collective-permute-start | bytes 417800 | tf_op jit(solution)/shard_map/ppermute | solution.py:149
  43.1 9.3 %collective-permute-start.7 = (bf16[256,512]{1,0:T(8,128)(2,1)}, bf16[256,512]{1,0:T(8,128)(2,1)S(1)}, u32[]{:S(2)}, u32[]{:S(2)}) collective-permute-start(bf16[256,512]{1,0:T(8,128)(2,1)} %get-tuple-element.10), channel_id=1, source_target_pairs={{0,2},{2,4},{4,6},{6,7},{7,5},{5,3},{3,1},{1,0},{8,10},{10,12},{12... | collective-permute-start | bytes 786440 | tf_op jit(solution)/shard_map/ppermute | solution.py:149
  45.6 17.2 %collective-permute-start.11 = (bf16[256,512]{1,0:T(8,128)(2,1)}, bf16[256,512]{1,0:T(8,128)(2,1)S(1)}, u32[]{:S(2)}, u32[]{:S(2)}) collective-permute-start(bf16[256,512]{1,0:T(8,128)(2,1)} %get-tuple-element.10), channel_id=1, source_target_pairs={{0,1},{2,0},{4,2},{6,4},{7,6},{5,7},{3,5},{1,3},{8,9},{10,8},{12,1... | collective-permute-start | bytes 786440 | tf_op jit(solution)/shard_map/ppermute | solution.py:153
  52.4 8.4 %collective-permute-start.8 = (bf16[256,512]{1,0:T(8,128)(2,1)S(1)}, bf16[256,512]{1,0:T(8,128)(2,1)S(1)}, u32[]{:S(2)}, u32[]{:S(2)}) collective-permute-start(bf16[256,512]{1,0:T(8,128)(2,1)S(1)} %collective-permute-done.7), channel_id=1, source_target_pairs={{0,2},{2,4},{4,6},{6,7},{7,5},{5,3},{3,1},{1,0},{8,10},{10,12},{12... | collective-permute-start | bytes 786440 | tf_op jit(solution)/shard_map/ppermute | solution.py:149
  60.8 7.6 %collective-permute-start.9 = (bf16[256,512]{1,0:T(8,128)(2,1)S(1)}, bf16[256,512]{1,0:T(8,128)(2,1)S(1)}, u32[]{:S(2)}, u32[]{:S(2)}) collective-permute-start(bf16[256,512]{1,0:T(8,128)(2,1)S(1)} %collective-permute-done.8), channel_id=1, source_target_pairs={{0,2},{2,4},{4,6},{6,7},{7,5},{5,3},{3,1},{1,0},{8,10},{10,12},{12... | collective-permute-start | bytes 786440 | tf_op jit(solution)/shard_map/ppermute | solution.py:149
  62.8 7.9 %collective-permute-start.12 = (bf16[256,512]{1,0:T(8,128)(2,1)S(1)}, bf16[256,512]{1,0:T(8,128)(2,1)S(1)}, u32[]{:S(2)}, u32[]{:S(2)}) collective-permute-start(bf16[256,512]{1,0:T(8,128)(2,1)S(1)} %collective-permute-done.11), channel_id=1, source_target_pairs={{0,1},{2,0},{4,2},{6,4},{7,6},{5,7},{3,5},{1,3},{8,9},{10,8},{12,1... | collective-permute-start | bytes 786440 | tf_op jit(solution)/shard_map/ppermute | solution.py:153
  68.4 6.4 %collective-permute-start.10 = (bf16[256,512]{1,0:T(8,128)(2,1)S(1)}, bf16[256,512]{1,0:T(8,128)(2,1)S(1)}, u32[]{:S(2)}, u32[]{:S(2)}) collective-permute-start(bf16[256,512]{1,0:T(8,128)(2,1)S(1)} %collective-permute-done.9), channel_id=1, source_target_pairs={{0,2},{2,4},{4,6},{6,7},{7,5},{5,3},{3,1},{1,0},{8,10},{10,12},{12... | collective-permute-start | bytes 786440 | tf_op jit(solution)/shard_map/ppermute | solution.py:149
  70.8 6.4 %collective-permute-start.13 = (bf16[256,512]{1,0:T(8,128)(2,1)S(1)}, bf16[256,512]{1,0:T(8,128)(2,1)S(1)}, u32[]{:S(2)}, u32[]{:S(2)}) collective-permute-start(bf16[256,512]{1,0:T(8,128)(2,1)S(1)} %collective-permute-done.12), channel_id=1, source_target_pairs={{0,1},{2,0},{4,2},{6,4},{7,6},{5,7},{3,5},{1,3},{8,9},{10,8},{12,1... | collective-permute-start | bytes 786440 | tf_op jit(solution)/shard_map/ppermute | solution.py:153
  80.8 0.7 copy-start.8
  81.1 0.6 copy-start.7
  82.1 18.4 %copy-start.5 = (f32[1,4096]{1,0:T(1,128)S(1)}, f32[1,4096]{1,0:T(1,128)}, u32[]{:S(2)}) copy-start(f32[1,4096]{1,0:T(1,128)} %param.30) | copy-start | bytes 49156
  82.9 5.0 %collective-permute-start.14 = (f32[8,1,4096]{2,0,1:T(8,128)S(1)}, f32[8,1,4096]{2,0,1:T(8,128)S(1)}, u32[]{:S(2)}, u32[]{:S(2)}) collective-permute-start(f32[8,1,4096]{2,0,1:T(8,128)S(1)} %convolution_bitcast_fusion), channel_id=1, source_target_pairs={{0,1},{1,0},{2,3},{3,2},{4,5},{5,4},{6,7},{7,6},{8,9},{9,8},{10,11... | collective-permute-start | bytes 393224 | tf_op jit(solution)/shard_map/ppermute | solution.py:114
  87.9 5.0 %collective-permute-start.15 = (f32[8,1,4096]{2,0,1:T(8,128)S(1)}, f32[8,1,4096]{2,0,1:T(8,128)S(1)}, u32[]{:S(2)}, u32[]{:S(2)}) collective-permute-start(f32[8,1,4096]{2,0,1:T(8,128)S(1)} %add.194), channel_id=1, source_target_pairs={{0,2},{1,3},{2,0},{3,1},{4,6},{5,7},{6,4},{7,5},{8,10},{9,11},{10,... | collective-permute-start | bytes 393224 | tf_op jit(solution)/shard_map/ppermute | solution.py:114
  92.9 7.3 %collective-permute-start.16 = (f32[8,1,4096]{2,0,1:T(8,128)S(1)}, f32[8,1,4096]{2,0,1:T(8,128)S(1)}, u32[]{:S(2)}, u32[]{:S(2)}) collective-permute-start(f32[8,1,4096]{2,0,1:T(8,128)S(1)} %add.195), channel_id=1, source_target_pairs={{0,4},{1,5},{2,6},{3,7},{4,0},{5,1},{6,2},{7,3},{8,12},{9,13},{10,... | collective-permute-start | bytes 393224 | tf_op jit(solution)/shard_map/ppermute | solution.py:114
  115.0 4.3 %collective-permute-start.17 = (f32[2,2,1,1,4096]{4,2,3,1,0:T(1,128)S(1)}, f32[2,2,1,1,4096]{4,2,3,1,0:T(1,128)S(1)}, u32[]{:S(2)}, u32[]{:S(2)}) collective-permute-start(f32[2,2,1,1,4096]{4,2,3,1,0:T(1,128)S(1)} %dynamic-slice_bitcast_fusion), channel_id=1, source_target_pairs={{0,1},{1,0},{2,3},{3,2},{4,5},{5,4},{6,7},{7,6},{8,9},{9,8},{10,11... | collective-permute-start | bytes 196616 | tf_op jit(solution)/shard_map/ppermute | solution.py:472
  119.5 4.0 %collective-permute-start.18 = (f32[2,1,1,1,4096]{4,2,3,1,0:T(1,128)S(1)}, f32[2,1,1,1,4096]{4,2,3,1,0:T(1,128)S(1)}, u32[]{:S(2)}, u32[]{:S(2)}) collective-permute-start(f32[2,1,1,1,4096]{4,2,3,1,0:T(1,128)S(1)} %constant_dynamic-slice_fusion), channel_id=1, source_target_pairs={{0,2},{1,3},{2,0},{3,1},{4,6},{5,7},{6,4},{7,5},{8,10},{9,11},{10,... | collective-permute-start | bytes 98312 | tf_op jit(solution)/shard_map/ppermute | solution.py:472
  123.5 5.0 %collective-permute-start.20 = (f32[1,4096]{1,0:T(1,128)S(1)}, f32[1,4096]{1,0:T(1,128)S(1)}, u32[]{:S(2)}, u32[]{:S(2)}) collective-permute-start(f32[1,4096]{1,0:T(1,128)S(1)} %dynamic-slice_bitcast_fusion.1), channel_id=1, source_target_pairs={{0,12},{1,13},{2,14},{3,15},{4,8},{5,9},{6,10},{7,11},{8,20},{9,21... | collective-permute-start | bytes 49160 | tf_op jit(solution)/shard_map/ppermute | solution.py:489
  123.6 5.0 %collective-permute-start.19 = (f32[1,4096]{1,0:T(1,128)S(1)}, f32[1,4096]{1,0:T(1,128)S(1)}, u32[]{:S(2)}, u32[]{:S(2)}) collective-permute-start(f32[1,4096]{1,0:T(1,128)S(1)} %bitcast_add_fusion.1), channel_id=1, source_target_pairs={{0,8},{1,9},{2,10},{3,11},{4,12},{5,13},{6,14},{7,15},{8,16},{9,17... | collective-permute-start | bytes 49160 | tf_op jit(solution)/shard_map/ppermute | solution.py:488

commit v7 on v6

--- a/solution.py
+++ b/solution.py
@@ -389,24 +389,37 @@
     hidden_width = tile_in.shape[-1]
     all_sites = group_size * sites_here
 
-    act_rows = sites_here * model_width // hidden_width
+    row_width = patches.shape[-1]
+    in_rows = tile_in.shape[1] * hidden_width // row_width
+    act_rows = sites_here * model_width // row_width
     ring_in = RingGather(
-        jnp.concatenate([tile_in[0], current.reshape(act_rows, hidden_width)], axis=0),
+        jnp.concatenate(
+            [
+                patches[0],
+                tile_in[0].reshape(in_rows, row_width),
+                current.reshape(act_rows, row_width),
+            ],
+            axis=0,
+        ),
         group_size,
         my_index,
     )
     in_slots, in_sources = ring_in.finish()
-    in_rows = tile_in.shape[1]
     slot_of_source = jnp.argmax(
         in_sources[None, :] == jnp.arange(group_size, dtype=jnp.int32)[:, None], axis=1
     ).astype(jnp.int32)
-    everyone = jnp.take(in_slots[:, in_rows:], slot_of_source, axis=0).reshape(all_sites, model_width)
-    weight_in = in_slots[:, :in_rows].reshape(-1, hidden_width)
-    own_rows = jnp.take(patches[0].reshape(tiles_here, group_size, -1), in_sources, axis=1)
-    tile_hidden = jax.nn.gelu(
-        jnp.dot(own_rows.reshape(tiles_here, -1), weight_in, preferred_element_type=jnp.float32),
+    by_source = jnp.take(in_slots[:, tiles_here:], slot_of_source, axis=0)
+    everyone = by_source[:, in_rows:].reshape(all_sites, model_width)
+    weight_in = by_source[:, :in_rows].reshape(-1, hidden_width)
+    table_hidden = jax.nn.gelu(
+        jnp.dot(
+            in_slots[:, :tiles_here].reshape(group_size * tiles_here, row_width),
+            weight_in,
+            preferred_element_type=jnp.float32,
+        ),
         approximate=True,
     ).astype(jnp.bfloat16)
+    hidden_sources = in_sources
 
     kv_width = tile_out.shape[-1]
     my_cols = heads_here * head_size
@@ -420,9 +433,6 @@
     queries = head_norm(q_part, q_gain[0]).astype(jnp.bfloat16)
     query_heads = queries.reshape(all_sites, heads_here, head_size)
 
-    ring_hidden = RingGather(tile_hidden, group_size, my_index)
-    hidden_slots, hidden_sources = ring_hidden.finish()
-    table_hidden = hidden_slots.reshape(group_size * tiles_here, hidden_width)
     keyval = jnp.dot(table_hidden, weight_out, preferred_element_type=jnp.float32)
     normed_keys = head_norm(keyval[:, :my_cols], k_gain[0])
     table = jnp.concatenate([normed_keys, keyval[:, my_cols:]], axis=1).astype(jnp.bfloat16)

time: 130 us -> 155 us (1.19)
  waiting for transfers between devices: 47.1 us -> 70.9 us
  starting transfers between devices: 34.8 us -> 26.1 us
  matrix products: 22.1 us -> 26.4 us
  other arithmetic: 8.68 us -> 12.7 us
    ppermute x8 -> x4, waiting for transfers between devices: 26.1 us -> 43.8 us  [_issue(): self.ahead = lax.ppermute(self.ahead, 'site', self.forward)]
    dot_general x1, matrix products: 2.9 us -> 8.57 us  [heads_split(): jnp.dot(table_hidden, weight_out, preferred_element_type=jnp.float32)]
    ppermute x8 -> x4, starting transfers between devices: 18.1 us -> 13.2 us  [_issue(): self.ahead = lax.ppermute(self.ahead, 'site', self.forward)]
    unnamed x44 -> x35, local copies, waits for them, and re-layouts: 7.91 us -> 3.69 us
    slice x1 -> x3, local copies, waits for them, and re-layouts: 0.01 us -> 3.53 us  [the longest x1 2.38 us: heads_split(): in_slots[:, :tiles_here].reshape(group_size * tiles_here, row_width)]
    ppermute x3, waiting for transfers between devices: 12.1 us -> 14.7 us  [doubling_sum(): state = state + lax.ppermute(state, 'site', xor_pairs(count, bit))]
    reshape x0 -> x1, local copies, waits for them, and re-layouts: none -> 2.27 us  [heads_split(): weight_in = by_source[:, :in_rows].reshape(-1, hidden_width)]
    reduce_sum x1, other arithmetic: 0.19 us -> 1.93 us  [head_norm(): jnp.mean(shaped * shaped, axis=-1, keepdims=True) + epsilon]
  transfers between devices with their start and end apart: 22 -> 15, of which waited for: 14 -> 11; matrix products, arithmetic and copies ran while one was open for 18% -> 14% of each run, Pallas kernels for 0% -> 0%
where the time goes in v7:
time: 155 us; the launch traced here: 154 us
  waiting for transfers between devices  70.9 us (46%)
  matrix products  26.4 us (17%)
  starting transfers between devices  26.1 us (17%)
  local copies, waits for them, and re-layouts  17.6 us (11%)
  other arithmetic  12.7 us (8%)
    ppermute x4, waiting for transfers between devices, _issue(): self.ahead = lax.ppermute(self.ahead, 'site', self.forward)  43.8 us
    ppermute x3, waiting for transfers between devices, doubling_sum(): state = state + lax.ppermute(state, 'site', xor_pairs(count, bit))  14.7 us
    ppermute x4, starting transfers between devices, _issue(): self.ahead = lax.ppermute(self.ahead, 'site', self.forward)  13.2 us
    dot_general x3, matrix products, by_rows(): lax.dot_general(left, weight_rows, (((1,), (1,)), ((), ())), preferred_el...  12.5 us
    dot_general x1, matrix products, heads_split(): jnp.dot(table_hidden, weight_out, preferred_element_type=jnp.float32)  8.57 us
    ppermute x2, waiting for transfers between devices, last_round(): state = keep + lax.ppermute(send, 'site', xor_pairs(group_size, bit))  7.63 us
    all_to_all x1, starting transfers between devices, heads_split(): lax.all_to_all(col_blocks, 'site', split_axis=0, concat_axis=0, tiled=True)  6.25 us
    dot_general x1, matrix products, heads_split(): jnp.dot(hidden_ffn, down_weight[0], preferred_element_type=jnp.float32)  4.22 us
  transfers between devices with their start and end apart: 15, of which 11 were waited for; matrix products, arithmetic and copies ran while one was open for 14% of the time, Pallas kernels for 0%

profile of v7, /device:TPU:0, one launch (start us, length us, event | category | flops | bytes accessed | tf_op | source)
XLA Modules:
  0.0 154.0 jit_solution(18235671085738624921)
XLA Ops:
  0.1 1.1 reshape_squeeze.9
  1.2 0.8 reduce.19
  2.0 2.0 %pad_maximum_fusion = bf16[324,1024]{1,0:T(8,128)(2,1)} fusion(bf16[4,1024]{1,0:T(4,128)(2,1)S(1)} %reshape_squeeze.10, bf16[64,1024]{1,0:T(8,128)(2,1)S(1)} %reshape_squeeze.9, bf16[256,1024]{1,0:T(8,128)(2,1)} %bitcast.134), kind=kLoop, calls=%fused_computation.44 | loop fusion | flops 1990656 | bytes 1327104 | tf_op jit(solution)/shard_map/concatenate | solution.py:396
  3.9 3.0 %collective-permute-start = (bf16[324,1024]{1,0:T(8,128)(2,1)}, bf16[324,1024]{1,0:T(8,128)(2,1)}, u32[]{:S(2)}, u32[]{:S(2)}) collective-permute-start(bf16[324,1024]{1,0:T(8,128)(2,1)} %pad_maximum_fusion), channel_id=1, source_target_pairs={{0,2},{2,4},{4,6},{6,7},{7,5},{5,3},{3,1},{1,0},{8,10},{10,12},{12... | collective-permute-start | bytes 1990664 | tf_op jit(solution)/shard_map/ppermute | solution.py:149
  7.0 1.1 copy.29
  8.1 0.4 copy.33
  8.5 1.2 reshape.174
  9.7 6.3 %all-to-all-start = ((bf16[8,64,512]{2,1,0:T(8,128)(2,1)}), bf16[8,64,512]{2,1,0:T(8,128)(2,1)}, u32[]{:S(2)}, u32[]{:S(2)}) async-start(bf16[8,64,512]{2,1,0:T(8,128)(2,1)} %reshape.174), calls=%async_computation | async-start | bytes 1048576 | tf_op jit(solution)/shard_map/all_to_all | solution.py:428
  16.0 0.6 dynamic_slice.28
  16.6 0.7 compare_select_fusion.1
  17.2 0.6 gather_fusion
  17.9 0.6 iota_reduce_fusion
  18.6 4.4 %collective-permute-done = bf16[324,1024]{1,0:T(8,128)(2,1)} collective-permute-done((bf16[324,1024]{1,0:T(8,128)(2,1)}, bf16[324,1024]{1,0:T(8,128)(2,1)}, u32[]{:S(2)}, u32[]{:S(2)}) %collective-permute-start) | collective-permute-done | bytes 663584 | tf_op jit(solution)/shard_map/ppermute | solution.py:149
  23.0 3.3 %collective-permute-start.1 = (bf16[324,1024]{1,0:T(8,128)(2,1)}, bf16[324,1024]{1,0:T(8,128)(2,1)S(1)}, u32[]{:S(2)}, u32[]{:S(2)}) collective-permute-start(bf16[324,1024]{1,0:T(8,128)(2,1)} %collective-permute-done), channel_id=1, source_target_pairs={{0,2},{2,4},{4,6},{6,7},{7,5},{5,3},{3,1},{1,0},{8,10},{10,12},{12... | collective-permute-start | bytes 1990664 | tf_op jit(solution)/shard_map/ppermute | solution.py:149
  26.3 0.6 broadcast_bitcast_fusion
  26.9 0.1 add_bitcast_fusion
  27.0 17.5 %collective-permute-done.1 = bf16[324,1024]{1,0:T(8,128)(2,1)S(1)} collective-permute-done((bf16[324,1024]{1,0:T(8,128)(2,1)}, bf16[324,1024]{1,0:T(8,128)(2,1)S(1)}, u32[]{:S(2)}, u32[]{:S(2)}) %collective-permute-start.1) | collective-permute-done | bytes 663584 | tf_op jit(solution)/shard_map/ppermute | solution.py:149
  44.5 4.4 %collective-permute-start.2 = (bf16[324,1024]{1,0:T(8,128)(2,1)S(1)}, bf16[324,1024]{1,0:T(8,128)(2,1)S(1)}, u32[]{:S(2)}, u32[]{:S(2)}) collective-permute-start(bf16[324,1024]{1,0:T(8,128)(2,1)S(1)} %collective-permute-done.1), channel_id=1, source_target_pairs={{0,2},{2,4},{4,6},{6,7},{7,5},{5,3},{3,1},{1,0},{8,10},{10,12},{12... | collective-permute-start | bytes 1990664 | tf_op jit(solution)/shard_map/ppermute | solution.py:149
  48.9 0.1 iota_compare_fusion
  48.9 0.0 collective-permute-start.5
  49.0 3.8 %convert_reduce_fusion = f32[8,2048]{1,0:T(8,128)} fusion(s32[2048]{0:T(1024)S(1)} %bitcast.140, s32[8,256]{1,0:T(8,128)S(1)} %copy-done.6, pred[8,256]{1,0:T(8,128)(4,1)S(1)} %iota_compare_fusion), kind=kLoop, calls=%fused_computation.2 | loop fusion | flops 16760832 | bytes 83968 | tf_op jit(solution)/shard_map/reduce_sum | solution.py:449
  52.7 9.6 %collective-permute-done.2 = bf16[324,1024]{1,0:T(8,128)(2,1)S(1)} collective-permute-done((bf16[324,1024]{1,0:T(8,128)(2,1)S(1)}, bf16[324,1024]{1,0:T(8,128)(2,1)S(1)}, u32[]{:S(2)}, u32[]{:S(2)}) %collective-permute-start.2) | collective-permute-done | bytes 663584 | tf_op jit(solution)/shard_map/ppermute | solution.py:149
  62.3 2.5 %collective-permute-start.3 = (bf16[324,1024]{1,0:T(8,128)(2,1)S(1)}, bf16[324,1024]{1,0:T(8,128)(2,1)S(1)}, u32[]{:S(2)}, u32[]{:S(2)}) collective-permute-start(bf16[324,1024]{1,0:T(8,128)(2,1)S(1)} %collective-permute-done.2), channel_id=1, source_target_pairs={{0,2},{2,4},{4,6},{6,7},{7,5},{5,3},{3,1},{1,0},{8,10},{10,12},{12... | collective-permute-start | bytes 1990664 | tf_op jit(solution)/shard_map/ppermute | solution.py:149
  64.8 1.1 bitcast_dynamic-update-slice_fusion.6
  65.9 0.6 collective-permute-start.6
  66.7 12.3 %collective-permute-done.3 = bf16[324,1024]{1,0:T(8,128)(2,1)S(1)} collective-permute-done((bf16[324,1024]{1,0:T(8,128)(2,1)S(1)}, bf16[324,1024]{1,0:T(8,128)(2,1)S(1)}, u32[]{:S(2)}, u32[]{:S(2)}) %collective-permute-start.3) | collective-permute-done | bytes 663584 | tf_op jit(solution)/shard_map/ppermute | solution.py:149
  79.0 1.1 bitcast_dynamic-update-slice_fusion.2
  80.2 1.2 collective-permute-done.6
  81.4 0.1 slice.31
  81.5 2.4 %slice.33 = bf16[8,256,1024]{2,1,0:T(8,128)(2,1)} slice(bf16[8,324,1024]{2,1,0:T(8,128)(2,1)S(1)} %bitcast_dynamic-update-slice_fusion), slice={[0:8], [0:256], [0:1024]} | slice | bytes 8388608 | tf_op jit(solution)/shard_map/slice | solution.py:416
  83.9 1.6 %gather_fusion.1 = bf16[8,68,1024]{2,1,0:T(8,128)(2,1)} fusion(bf16[8,68,1024]{2,1,0:T(8,128)(2,1)S(1)} %slice.31, s32[1024]{0:T(1024)S(1)} %pad_clamp_fusion), kind=kCustom, calls=%fused_computation.1 | custom fusion | bytes 2228256 | tf_op jit(solution)/shard_map/jit(_take)/gather | solution.py:411
  85.5 1.4 broadcast_select_fusion
  87.0 1.1 slice.34
  88.0 2.3 %reshape.173 = bf16[1024,512]{1,0:T(8,128)(2,1)} reshape(bf16[8,64,1024]{2,1,0:T(8,128)(2,1)} %slice.34) | data formatting | bytes 2097152 | tf_op jit(solution)/shard_map/reshape | solution.py:413
  90.4 8.6 %fusion.17 = f32[2048,512]{0,1:T(8,128)} fusion(bf16[512,512]{1,0:T(8,128)(2,1)} %bitcast.12, bf16[2048,1024]{1,0:T(8,128)(2,1)} %bitcast.129, bf16[1024,512]{1,0:T(8,128)(2,1)} %reshape.173), kind=kOutput, calls=%fused_computation.23 | convolution fusion | flops 3230662656 | bytes 9961472 | tf_op jit(solution)/shard_map/dot_general | solution.py:436
  98.9 1.9 %bitcast_reduce_fusion = f32[2048,2]{0,1:T(2,128)S(1)} fusion(f32[2048,512]{0,1:T(8,128)} %fusion.17), kind=kLoop, calls=%fused_computation.31 | loop fusion | flops 1044480 | bytes 2113536 | tf_op jit(solution)/shard_map/reduce_sum | solution.py:29
  100.9 0.0 copy-start.7
  100.9 1.7 %slice.44 = bf16[2048,256]{0,1:T(8,128)(2,1)S(1)} slice(f32[2048,512]{0,1:T(8,128)} %fusion.17), slice={[0:2048], [256:512]} | slice | bytes 2097152 | tf_op jit(solution)/shard_map/slice | solution.py:438
  102.7 2.3 %bitcast_reduce_fusion.1 = (f32[8,2]{0,1:T(2,128)S(1)}, f32[8,256]{1,0:T(8,128)S(1)}) fusion(bf16[8,4096]{1,0:T(8,128)(2,1)S(1)} %bitcast.137, bf16[1,256,4096]{2,1,0:T(8,128)(2,1)} %param.21), kind=kOutput, calls=%fused_computation.72 | convolution fusion | flops 16785392 | bytes 2170944 | tf_op jit(solution)/shard_map/dot_general | solution.py:21
  105.0 0.0 copy-done.2
  105.1 0.2 fusion.23
  105.3 0.3 fusion.16
  105.6 0.8 convolution_bitcast_fusion
  106.4 0.5 collective-permute-start.7
  107.0 4.4 %collective-permute-done.7 = f32[8,1,4096]{2,0,1:T(8,128)S(1)} collective-permute-done((f32[8,1,4096]{2,0,1:T(8,128)S(1)}, f32[8,1,4096]{2,0,1:T(8,128)S(1)}, u32[]{:S(2)}, u32[]{:S(2)}) %collective-permute-start.7) | collective-permute-done | bytes 131104 | tf_op jit(solution)/shard_map/ppermute | solution.py:114
  111.4 1.8 %collective-permute-start.8 = (f32[8,1,4096]{2,0,1:T(8,128)S(1)}, f32[8,1,4096]{2,0,1:T(8,128)S(1)}, u32[]{:S(2)}, u32[]{:S(2)}) collective-permute-start(f32[8,1,4096]{2,0,1:T(8,128)S(1)} %add.159), channel_id=1, source_target_pairs={{0,2},{1,3},{2,0},{3,1},{4,6},{5,7},{6,4},{7,5},{8,10},{9,11},{10,... | collective-permute-start | bytes 393224 | tf_op jit(solution)/shard_map/ppermute | solution.py:114
  113.2 4.6 %collective-permute-done.8 = f32[8,1,4096]{2,0,1:T(8,128)S(1)} collective-permute-done((f32[8,1,4096]{2,0,1:T(8,128)S(1)}, f32[8,1,4096]{2,0,1:T(8,128)S(1)}, u32[]{:S(2)}, u32[]{:S(2)}) %collective-permute-start.8) | collective-permute-done | bytes 131104 | tf_op jit(solution)/shard_map/ppermute | solution.py:114
  117.9 1.6 %collective-permute-start.9 = (f32[8,1,4096]{2,0,1:T(8,128)S(1)}, f32[8,1,4096]{2,0,1:T(8,128)S(1)}, u32[]{:S(2)}, u32[]{:S(2)}) collective-permute-start(f32[8,1,4096]{2,0,1:T(8,128)S(1)} %add.160), channel_id=1, source_target_pairs={{0,4},{1,5},{2,6},{3,7},{4,0},{5,1},{6,2},{7,3},{8,12},{9,13},{10,... | collective-permute-start | bytes 393224 | tf_op jit(solution)/shard_map/ppermute | solution.py:114
  119.5 0.1 reshape.182
  119.6 5.6 %collective-permute-done.9 = f32[8,1,4096]{2,0,1:T(8,128)S(1)} collective-permute-done((f32[8,1,4096]{2,0,1:T(8,128)S(1)}, f32[8,1,4096]{2,0,1:T(8,128)S(1)}, u32[]{:S(2)}, u32[]{:S(2)}) %collective-permute-start.9) | collective-permute-done | bytes 131104 | tf_op jit(solution)/shard_map/ppermute | solution.py:114
  125.2 0.1 multiply_reduce_fusion
  125.4 5.1 %fusion.4 = f32[8,896]{1,0:T(8,128)S(1)} fusion(bf16[1,896,4096]{2,1,0:T(8,128)(2,1)} %param.28, f32[8,1,4096]{2,0,1:T(8,128)S(1)} %get-tuple-element.8, f32[4096]{0:T(1024)S(1)} %bitcast.138, f32[8]{0:T(128)S(1)} %add_rsqrt_fusion.2), kind=kOutput, calls=%fused_computation.7 | convolution fusion | flops 58818560 | bytes 7516192 | tf_op jit(solution)/shard_map/dot_general | solution.py:21
  130.5 5.1 %fusion.31 = bf16[8,896]{1,0:T(8,128)(2,1)S(1)} fusion(bf16[1,896,4096]{2,1,0:T(8,128)(2,1)} %param.29, f32[8,896]{1,0:T(8,128)S(1)} %fusion.4, f32[8,1,4096]{2,0,1:T(8,128)S(1)} %get-tuple-element.8, f32[4096]{0:T(1024)S(1)} %bitcast.139, f32[8]{0:T(128)S(1)} %add_rsqrt_fusion.2), kind=kOutput, calls=%fused_computation.39 | convolution fusion | flops 58861568 | bytes 7530528 | tf_op jit(solution)/shard_map/dot_general | solution.py:21
  135.6 4.2 %fusion = f32[2,2,2,4096]{3,2,1,0:T(2,128)S(1)} fusion(bf16[2,2,2,896]{3,2,1,0:T(2,128)(2,1)S(1)} %dot_general.37, bf16[1,896,4096]{2,1,0:T(8,128)(2,1)} %param.30), kind=kOutput, calls=%fused_computation.3 | convolution fusion | flops 58720256 | bytes 7485440 | tf_op jit(solution)/shard_map/dot_general | solution.py:467
  139.8 0.1 dynamic-slice_bitcast_fusion
  139.9 0.6 collective-permute-start.10
  140.5 3.7 %collective-permute-done.10 = f32[2,2,1,1,4096]{4,2,3,1,0:T(1,128)S(1)} collective-permute-done((f32[2,2,1,1,4096]{4,2,3,1,0:T(1,128)S(1)}, f32[2,2,1,1,4096]{4,2,3,1,0:T(1,128)S(1)}, u32[]{:S(2)}, u32[]{:S(2)}) %collective-permute-start.10) | collective-permute-done | bytes 65568 | tf_op jit(solution)/shard_map/ppermute | solution.py:482
  144.2 0.1 bitcast_add_fusion
  144.3 0.1 collective-permute-start.11
  144.4 3.9 %collective-permute-done.11 = f32[2,1,1,1,4096]{4,2,3,1,0:T(1,128)S(1)} collective-permute-done((f32[2,1,1,1,4096]{4,2,3,1,0:T(1,128)S(1)}, f32[2,1,1,1,4096]{4,2,3,1,0:T(1,128)S(1)}, u32[]{:S(2)}, u32[]{:S(2)}) %collective-permute-start.11) | collective-permute-done | bytes 32800 | tf_op jit(solution)/shard_map/ppermute | solution.py:482
  148.4 0.1 collective-permute-start.13
  148.5 1.3 collective-permute-start.12
  149.8 3.6 %collective-permute-done.13 = f32[1,4096]{1,0:T(1,128)S(1)} collective-permute-done((f32[1,4096]{1,0:T(1,128)S(1)}, f32[1,4096]{1,0:T(1,128)S(1)}, u32[]{:S(2)}, u32[]{:S(2)}) %collective-permute-start.13) | collective-permute-done | bytes 16416 | tf_op jit(solution)/shard_map/ppermute | solution.py:499
  153.4 0.6 convert_bitcast_fusion
  (55 shorter events, 0.6 us)
Async XLA Ops:
  0.0 105.6 %copy-start = (bf16[1,256,4096]{2,1,0:T(8,128)(2,1)S(1)}, bf16[1,256,4096]{2,1,0:T(8,128)(2,1)}, u32[]{:S(2)}) copy-start(bf16[1,256,4096]{2,1,0:T(8,128)(2,1)} %param.26) | copy-start | bytes 6291460
  0.0 16.0 %copy-start.12 = (s32[8]{0:T(128)S(1)}, s32[8]{0:T(128)}, u32[]{:S(2)}) copy-start(s32[8]{0:T(128)} %constant.105.clone) | copy-start | bytes 100
  0.0 16.5 %copy-start.11 = (s32[8]{0:T(128)S(1)}, s32[8]{0:T(128)}, u32[]{:S(2)}) copy-start(s32[8]{0:T(128)} %constant.107.clone) | copy-start | bytes 100
  0.0 17.2 %copy-start.1 = (s32[8]{0:T(128)S(1)}, s32[8]{0:T(128)}, u32[]{:S(2)}) copy-start(s32[8]{0:T(128)} %constant.106.clone) | copy-start | bytes 100
  0.0 26.8 %copy-start.3 = (bf16[1,256,1024]{2,1,0:T(8,128)(2,1)S(1)}, bf16[1,256,1024]{2,1,0:T(8,128)(2,1)}, u32[]{:S(2)}) copy-start(bf16[1,256,1024]{2,1,0:T(8,128)(2,1)} %param.18) | copy-start | bytes 1572868
  0.0 18.5 %copy-start.9 = (f32[1,128]{1,0:T(1,128)S(1)}, f32[1,128]{1,0:T(1,128)}, u32[]{:S(2)}) copy-start(f32[1,128]{1,0:T(1,128)} %param.23) | copy-start | bytes 1540
  0.0 26.2 %copy-start.10 = (f32[1,128]{1,0:T(1,128)S(1)}, f32[1,128]{1,0:T(1,128)}, u32[]{:S(2)}) copy-start(f32[1,128]{1,0:T(1,128)} %param.22) | copy-start | bytes 1540
  0.0 48.8 %copy-start.8 = (s32[8]{0:T(128)S(1)}, s32[8]{0:T(128)}, u32[]{:S(2)}) copy-start(s32[8]{0:T(128)} %param.20) | copy-start | bytes 100
  0.1 48.9 %copy-start.6 = (s32[8,256]{1,0:T(8,128)S(1)}, s32[8,256]{1,0:T(8,128)}, u32[]{:S(2)}) copy-start(s32[8,256]{1,0:T(8,128)} %param.19) | copy-start | bytes 24580
  3.9 19.1 %collective-permute-start = (bf16[324,1024]{1,0:T(8,128)(2,1)}, bf16[324,1024]{1,0:T(8,128)(2,1)}, u32[]{:S(2)}, u32[]{:S(2)}) collective-permute-start(bf16[324,1024]{1,0:T(8,128)(2,1)} %pad_maximum_fusion), channel_id=1, source_target_pairs={{0,2},{2,4},{4,6},{6,7},{7,5},{5,3},{3,1},{1,0},{8,10},{10,12},{12... | collective-permute-start | bytes 1990664 | tf_op jit(solution)/shard_map/ppermute | solution.py:149
  7.0 42.0 %collective-permute-start.4 = (bf16[324,1024]{1,0:T(8,128)(2,1)}, bf16[324,1024]{1,0:T(8,128)(2,1)}, u32[]{:S(2)}, u32[]{:S(2)}) collective-permute-start(bf16[324,1024]{1,0:T(8,128)(2,1)} %pad_maximum_fusion), channel_id=1, source_target_pairs={{0,1},{2,0},{4,2},{6,4},{7,6},{5,7},{3,5},{1,3},{8,9},{10,8},{12,1... | collective-permute-start | bytes 1990664 | tf_op jit(solution)/shard_map/ppermute | solution.py:153
  9.7 80.7 %all-to-all-start = ((bf16[8,64,512]{2,1,0:T(8,128)(2,1)}), bf16[8,64,512]{2,1,0:T(8,128)(2,1)}, u32[]{:S(2)}, u32[]{:S(2)}) async-start(bf16[8,64,512]{2,1,0:T(8,128)(2,1)} %reshape.174), calls=%async_computation | async-start | bytes 1048576 | tf_op jit(solution)/shard_map/all_to_all | solution.py:428
  23.0 21.5 %collective-permute-start.1 = (bf16[324,1024]{1,0:T(8,128)(2,1)}, bf16[324,1024]{1,0:T(8,128)(2,1)S(1)}, u32[]{:S(2)}, u32[]{:S(2)}) collective-permute-start(bf16[324,1024]{1,0:T(8,128)(2,1)} %collective-permute-done), channel_id=1, source_target_pairs={{0,2},{2,4},{4,6},{6,7},{7,5},{5,3},{3,1},{1,0},{8,10},{10,12},{12... | collective-permute-start | bytes 1990664 | tf_op jit(solution)/shard_map/ppermute | solution.py:149
  44.5 17.9 %collective-permute-start.2 = (bf16[324,1024]{1,0:T(8,128)(2,1)S(1)}, bf16[324,1024]{1,0:T(8,128)(2,1)S(1)}, u32[]{:S(2)}, u32[]{:S(2)}) collective-permute-start(bf16[324,1024]{1,0:T(8,128)(2,1)S(1)} %collective-permute-done.1), channel_id=1, source_target_pairs={{0,2},{2,4},{4,6},{6,7},{7,5},{5,3},{3,1},{1,0},{8,10},{10,12},{12... | collective-permute-start | bytes 1990664 | tf_op jit(solution)/shard_map/ppermute | solution.py:149
  48.9 17.0 %collective-permute-start.5 = (bf16[324,1024]{1,0:T(8,128)(2,1)}, bf16[324,1024]{1,0:T(8,128)(2,1)S(1)}, u32[]{:S(2)}, u32[]{:S(2)}) collective-permute-start(bf16[324,1024]{1,0:T(8,128)(2,1)} %collective-permute-done.4), channel_id=1, source_target_pairs={{0,1},{2,0},{4,2},{6,4},{7,6},{5,7},{3,5},{1,3},{8,9},{10,8},{12,1... | collective-permute-start | bytes 1990664 | tf_op jit(solution)/shard_map/ppermute | solution.py:153
  62.3 16.6 %collective-permute-start.3 = (bf16[324,1024]{1,0:T(8,128)(2,1)S(1)}, bf16[324,1024]{1,0:T(8,128)(2,1)S(1)}, u32[]{:S(2)}, u32[]{:S(2)}) collective-permute-start(bf16[324,1024]{1,0:T(8,128)(2,1)S(1)} %collective-permute-done.2), channel_id=1, source_target_pairs={{0,2},{2,4},{4,6},{6,7},{7,5},{5,3},{3,1},{1,0},{8,10},{10,12},{12... | collective-permute-start | bytes 1990664 | tf_op jit(solution)/shard_map/ppermute | solution.py:149
  65.9 15.4 %collective-permute-start.6 = (bf16[324,1024]{1,0:T(8,128)(2,1)S(1)}, bf16[324,1024]{1,0:T(8,128)(2,1)S(1)}, u32[]{:S(2)}, u32[]{:S(2)}) collective-permute-start(bf16[324,1024]{1,0:T(8,128)(2,1)S(1)} %collective-permute-done.5), channel_id=1, source_target_pairs={{0,1},{2,0},{4,2},{6,4},{7,6},{5,7},{3,5},{1,3},{8,9},{10,8},{12,1... | collective-permute-start | bytes 1990664 | tf_op jit(solution)/shard_map/ppermute | solution.py:153
  98.9 6.1 %copy-start.2 = (f32[2048,512]{0,1:T(8,128)S(1)}, f32[2048,512]{0,1:T(8,128)}, u32[]{:S(2)}) copy-start(f32[2048,512]{0,1:T(8,128)} %fusion.17) | copy-start | bytes 12582916
  100.9 4.4 %copy-start.4 = (f32[8,2048]{1,0:T(8,128)S(1)}, f32[8,2048]{1,0:T(8,128)}, u32[]{:S(2)}) copy-start(f32[8,2048]{1,0:T(8,128)} %convert_reduce_fusion) | copy-start | bytes 196612
  100.9 4.4 %copy-start.7 = (f32[256]{0:T(256)S(1)}, f32[256]{0:T(256)}, u32[]{:S(2)}) copy-start(f32[256]{0:T(256)} %broadcast_bitcast_fusion) | copy-start | bytes 3076
  105.0 20.3 %copy-start.5 = (f32[1,4096]{1,0:T(1,128)S(1)}, f32[1,4096]{1,0:T(1,128)}, u32[]{:S(2)}) copy-start(f32[1,4096]{1,0:T(1,128)} %param.27) | copy-start | bytes 49156
  106.4 5.0 %collective-permute-start.7 = (f32[8,1,4096]{2,0,1:T(8,128)S(1)}, f32[8,1,4096]{2,0,1:T(8,128)S(1)}, u32[]{:S(2)}, u32[]{:S(2)}) collective-permute-start(f32[8,1,4096]{2,0,1:T(8,128)S(1)} %convolution_bitcast_fusion), channel_id=1, source_target_pairs={{0,1},{1,0},{2,3},{3,2},{4,5},{5,4},{6,7},{7,6},{8,9},{9,8},{10,11... | collective-permute-start | bytes 393224 | tf_op jit(solution)/shard_map/ppermute | solution.py:114
  111.4 6.4 %collective-permute-start.8 = (f32[8,1,4096]{2,0,1:T(8,128)S(1)}, f32[8,1,4096]{2,0,1:T(8,128)S(1)}, u32[]{:S(2)}, u32[]{:S(2)}) collective-permute-start(f32[8,1,4096]{2,0,1:T(8,128)S(1)} %add.159), channel_id=1, source_target_pairs={{0,2},{1,3},{2,0},{3,1},{4,6},{5,7},{6,4},{7,5},{8,10},{9,11},{10,... | collective-permute-start | bytes 393224 | tf_op jit(solution)/shard_map/ppermute | solution.py:114
  117.9 7.3 %collective-permute-start.9 = (f32[8,1,4096]{2,0,1:T(8,128)S(1)}, f32[8,1,4096]{2,0,1:T(8,128)S(1)}, u32[]{:S(2)}, u32[]{:S(2)}) collective-permute-start(f32[8,1,4096]{2,0,1:T(8,128)S(1)} %add.160), channel_id=1, source_target_pairs={{0,4},{1,5},{2,6},{3,7},{4,0},{5,1},{6,2},{7,3},{8,12},{9,13},{10,... | collective-permute-start | bytes 393224 | tf_op jit(solution)/shard_map/ppermute | solution.py:114
  139.9 4.3 %collective-permute-start.10 = (f32[2,2,1,1,4096]{4,2,3,1,0:T(1,128)S(1)}, f32[2,2,1,1,4096]{4,2,3,1,0:T(1,128)S(1)}, u32[]{:S(2)}, u32[]{:S(2)}) collective-permute-start(f32[2,2,1,1,4096]{4,2,3,1,0:T(1,128)S(1)} %dynamic-slice_bitcast_fusion), channel_id=1, source_target_pairs={{0,1},{1,0},{2,3},{3,2},{4,5},{5,4},{6,7},{7,6},{8,9},{9,8},{10,11... | collective-permute-start | bytes 196616 | tf_op jit(solution)/shard_map/ppermute | solution.py:482
  144.3 4.0 %collective-permute-start.11 = (f32[2,1,1,1,4096]{4,2,3,1,0:T(1,128)S(1)}, f32[2,1,1,1,4096]{4,2,3,1,0:T(1,128)S(1)}, u32[]{:S(2)}, u32[]{:S(2)}) collective-permute-start(f32[2,1,1,1,4096]{4,2,3,1,0:T(1,128)S(1)} %constant_dynamic-slice_fusion), channel_id=1, source_target_pairs={{0,2},{1,3},{2,0},{3,1},{4,6},{5,7},{6,4},{7,5},{8,10},{9,11},{10,... | collective-permute-start | bytes 98312 | tf_op jit(solution)/shard_map/ppermute | solution.py:482
  148.4 5.0 %collective-permute-start.13 = (f32[1,4096]{1,0:T(1,128)S(1)}, f32[1,4096]{1,0:T(1,128)S(1)}, u32[]{:S(2)}, u32[]{:S(2)}) collective-permute-start(f32[1,4096]{1,0:T(1,128)S(1)} %dynamic-slice_bitcast_fusion.1), channel_id=1, source_target_pairs={{0,12},{1,13},{2,14},{3,15},{4,8},{5,9},{6,10},{7,11},{8,20},{9,21... | collective-permute-start | bytes 49160 | tf_op jit(solution)/shard_map/ppermute | solution.py:499
  148.5 4.9 %collective-permute-start.12 = (f32[1,4096]{1,0:T(1,128)S(1)}, f32[1,4096]{1,0:T(1,128)S(1)}, u32[]{:S(2)}, u32[]{:S(2)}) collective-permute-start(f32[1,4096]{1,0:T(1,128)S(1)} %bitcast_add_fusion.1), channel_id=1, source_target_pairs={{0,8},{1,9},{2,10},{3,11},{4,12},{5,13},{6,14},{7,15},{8,16},{9,17... | collective-permute-start | bytes 49160 | tf_op jit(solution)/shard_map/ppermute | solution.py:498

commit v8 on v6

--- a/solution.py
+++ b/solution.py
@@ -395,6 +395,15 @@
         group_size,
         my_index,
     )
+    kv_width = tile_out.shape[-1]
+    my_cols = heads_here * head_size
+    col_blocks = tile_out[0].reshape(tile_out.shape[1], 2, group_size, my_cols)
+    col_blocks = jnp.transpose(col_blocks, (2, 0, 1, 3)).reshape(group_size, tile_out.shape[1], 2 * my_cols)
+    col_blocks, site_tiles, site_count = ring_in.step((col_blocks, site_tiles, site_count))
+    weight_out = lax.all_to_all(col_blocks, "site", split_axis=0, concat_axis=0, tiled=True)
+    weight_out = weight_out.reshape(-1, 2 * my_cols)
+    del kv_width
+
     in_slots, in_sources = ring_in.finish()
     in_rows = tile_in.shape[1]
     slot_of_source = jnp.argmax(
@@ -407,14 +416,6 @@
         jnp.dot(own_rows.reshape(tiles_here, -1), weight_in, preferred_element_type=jnp.float32),
         approximate=True,
     ).astype(jnp.bfloat16)
-
-    kv_width = tile_out.shape[-1]
-    my_cols = heads_here * head_size
-    col_blocks = tile_out[0].reshape(tile_out.shape[1], 2, group_size, my_cols)
-    col_blocks = jnp.transpose(col_blocks, (2, 0, 1, 3)).reshape(group_size, tile_out.shape[1], 2 * my_cols)
-    weight_out = lax.all_to_all(col_blocks, "site", split_axis=0, concat_axis=0, tiled=True)
-    weight_out = weight_out.reshape(-1, 2 * my_cols)
-    del kv_width
 
     q_part = by_rows(everyone, q_weight[0]).astype(jnp.bfloat16)
     queries = head_norm(q_part, q_gain[0]).astype(jnp.bfloat16)

time: 130 us -> 147 us (1.13)
  local copies, waits for them, and re-layouts: 16.1 us -> 22.5 us
  other arithmetic: 8.68 us -> 14.1 us
  matrix products: 22.1 us -> 24.7 us
  starting transfers between devices: 34.8 us -> 36.5 us
    ppermute x6, starting transfers between devices: 0.53 us -> 6.35 us  [_issue(): self.behind = lax.ppermute(self.behind, 'site', self.backward)]
    ppermute x8, starting transfers between devices: 18.1 us -> 14.2 us  [_issue(): self.ahead = lax.ppermute(self.ahead, 'site', self.forward)]
    unnamed x44 -> x36, local copies, waits for them, and re-layouts: 7.91 us -> 11.8 us
  transfers between devices with their start and end apart: 22 -> 22, of which waited for: 14 -> 12; matrix products, arithmetic and copies ran while one was open for 18% -> 25% of each run, Pallas kernels for 0% -> 0%
where the time goes in v8:
time: 147 us; the launch traced here: 146 us
  waiting for transfers between devices  48 us (33%)
  starting transfers between devices  36.5 us (25%)
  matrix products  24.7 us (17%)
  local copies, waits for them, and re-layouts  22.5 us (15%)
  other arithmetic  14.1 us (10%)
    ppermute x8, waiting for transfers between devices, _issue(): self.ahead = lax.ppermute(self.ahead, 'site', self.forward)  27 us
    ppermute x8, starting transfers between devices, _issue(): self.ahead = lax.ppermute(self.ahead, 'site', self.forward)  14.2 us
    dot_general x3, matrix products, by_rows(): lax.dot_general(left, weight_rows, (((1,), (1,)), ((), ())), preferred_el...  12.5 us
    unnamed x36, local copies, waits for them, and re-layouts  11.8 us
    ppermute x3, waiting for transfers between devices, doubling_sum(): state = state + lax.ppermute(state, 'site', xor_pairs(count, bit))  11.6 us
    ppermute x6, starting transfers between devices, _issue(): self.behind = lax.ppermute(self.behind, 'site', self.backward)  6.35 us
    all_to_all x1, starting transfers between devices, heads_split(): lax.all_to_all(col_blocks, 'site', split_axis=0, concat_axis=0, tiled=True)  6.26 us
    ppermute x2, waiting for transfers between devices, last_round(): state = keep + lax.ppermute(send, 'site', xor_pairs(group_size, bit))  5.72 us
  transfers between devices with their start and end apart: 22, of which 12 were waited for; matrix products, arithmetic and copies ran while one was open for 25% of the time, Pallas kernels for 0%

profile of v8, /device:TPU:0, one launch (start us, length us, event | category | flops | bytes accessed | tf_op | source)
XLA Modules:
  0.0 146.1 jit_solution(16220882832234366629)
XLA Ops:
  0.0 0.9 reduce.19
  1.0 1.6 %pad_maximum_fusion = bf16[136,512]{1,0:T(8,128)(2,1)} fusion(bf16[8,512]{1,0:T(8,128)(2,1)S(1)} %reshape_squeeze.9, bf16[128,512]{1,0:T(8,128)(2,1)} %bitcast.168), kind=kLoop, calls=%fused_computation.53 | loop fusion | flops 278528 | bytes 278528 | tf_op jit(solution)/shard_map/concatenate | solution.py:394
  2.5 3.0 %collective-permute-start = (bf16[136,512]{1,0:T(8,128)(2,1)}, bf16[136,512]{1,0:T(8,128)(2,1)S(1)}, u32[]{:S(2)}, u32[]{:S(2)}) collective-permute-start(bf16[136,512]{1,0:T(8,128)(2,1)} %pad_maximum_fusion), channel_id=1, source_target_pairs={{0,2},{2,4},{4,6},{6,7},{7,5},{5,3},{3,1},{1,0},{8,10},{10,12},{12... | collective-permute-start | bytes 417800 | tf_op jit(solution)/shard_map/ppermute | solution.py:149
  5.6 1.2 dynamic_slice.31
  6.8 1.2 compare_select_fusion.3
  8.0 1.3 gather_fusion
  11.0 1.2 broadcast_bitcast_fusion
  12.2 1.2 broadcast_bitcast_fusion.1
  15.3 1.2 copy.32
  16.8 1.2 copy.39
  18.4 1.1 reshape.230
  19.6 0.8 gather_fusion.2
  20.4 1.4 bitcast_dynamic-update-slice_fusion.15
  21.7 6.3 %all-to-all-start = ((bf16[8,64,512]{2,1,0:T(8,128)(2,1)}), bf16[8,64,512]{2,1,0:T(8,128)(2,1)S(1)}, u32[]{:S(2)}, u32[]{:S(2)}) async-start(bf16[8,64,512]{2,1,0:T(8,128)(2,1)} %reshape.230), calls=%async_computation | async-start | bytes 1048576 | tf_op jit(solution)/shard_map/all_to_all | solution.py:403
  28.0 2.0 %collective-permute-start.2 = (bf16[136,512]{1,0:T(8,128)(2,1)S(1)}, bf16[136,512]{1,0:T(8,128)(2,1)S(1)}, u32[]{:S(2)}, u32[]{:S(2)}) collective-permute-start(bf16[136,512]{1,0:T(8,128)(2,1)S(1)} %collective-permute-done), channel_id=1, source_target_pairs={{0,2},{2,4},{4,6},{6,7},{7,5},{5,3},{3,1},{1,0},{8,10},{10,12},{12... | collective-permute-start | bytes 417800 | tf_op jit(solution)/shard_map/ppermute | solution.py:149
  30.1 0.7 bitcast_dynamic-update-slice_fusion.14
  30.7 0.7 iota_compare_fusion
  31.4 7.6 %collective-permute-done.2 = bf16[136,512]{1,0:T(8,128)(2,1)S(1)} collective-permute-done((bf16[136,512]{1,0:T(8,128)(2,1)S(1)}, bf16[136,512]{1,0:T(8,128)(2,1)S(1)}, u32[]{:S(2)}, u32[]{:S(2)}) %collective-permute-start.2) | collective-permute-done | bytes 139296 | tf_op jit(solution)/shard_map/ppermute | solution.py:149
  39.1 4.2 %collective-permute-start.3 = (bf16[136,512]{1,0:T(8,128)(2,1)S(1)}, bf16[136,512]{1,0:T(8,128)(2,1)S(1)}, u32[]{:S(2)}, u32[]{:S(2)}) collective-permute-start(bf16[136,512]{1,0:T(8,128)(2,1)S(1)} %collective-permute-done.2), channel_id=1, source_target_pairs={{0,2},{2,4},{4,6},{6,7},{7,5},{5,3},{3,1},{1,0},{8,10},{10,12},{12... | collective-permute-start | bytes 417800 | tf_op jit(solution)/shard_map/ppermute | solution.py:149
  43.3 0.7 bitcast_dynamic-update-slice_fusion.13
  44.0 1.9 %collective-permute-done.3 = bf16[136,512]{1,0:T(8,128)(2,1)S(1)} collective-permute-done((bf16[136,512]{1,0:T(8,128)(2,1)S(1)}, bf16[136,512]{1,0:T(8,128)(2,1)S(1)}, u32[]{:S(2)}, u32[]{:S(2)}) %collective-permute-start.3) | collective-permute-done | bytes 139296 | tf_op jit(solution)/shard_map/ppermute | solution.py:149
  45.9 2.5 %collective-permute-start.4 = (bf16[136,512]{1,0:T(8,128)(2,1)S(1)}, bf16[136,512]{1,0:T(8,128)(2,1)S(1)}, u32[]{:S(2)}, u32[]{:S(2)}) collective-permute-start(bf16[136,512]{1,0:T(8,128)(2,1)S(1)} %collective-permute-done.3), channel_id=1, source_target_pairs={{0,2},{2,4},{4,6},{6,7},{7,5},{5,3},{3,1},{1,0},{8,10},{10,12},{12... | collective-permute-start | bytes 417800 | tf_op jit(solution)/shard_map/ppermute | solution.py:149
  48.4 0.7 bitcast_dynamic-update-slice_fusion.12
  49.0 4.0 %collective-permute-done.4 = bf16[136,512]{1,0:T(8,128)(2,1)S(1)} collective-permute-done((bf16[136,512]{1,0:T(8,128)(2,1)S(1)}, bf16[136,512]{1,0:T(8,128)(2,1)S(1)}, u32[]{:S(2)}, u32[]{:S(2)}) %collective-permute-start.4) | collective-permute-done | bytes 139296 | tf_op jit(solution)/shard_map/ppermute | solution.py:149
  54.3 0.7 bitcast_dynamic-update-slice_fusion.9
  55.0 0.7 bitcast_dynamic-update-slice_fusion.8
  55.7 2.6 %bitcast_dynamic-update-slice_fusion.7 = (bf16[8,256,512]{2,1,0:T(8,128)(2,1)}, bf16[256,512]{1,0:T(8,128)(2,1)}) fusion(bf16[8,136,512]{2,1,0:T(8,128)(2,1)} %bitcast_dynamic-update-slice_fusion.8, bf16[8,256,128]{2,1,0:T(8,128)(2,1)S(1)} %gather_fusion.2, pred[8]{0:T(512)(128)(4,1)S(1)} %copy-done.9), kind=kOutput, calls=%fused_computation.51 | convolution fusion | flops 269877248 | bytes 2097160 | tf_op jit(solution)/shard_map/dot_general | solution.py:416
  58.8 3.1 %convert_reduce_fusion = f32[8,2048]{1,0:T(8,128)S(1)} fusion(s32[2048]{0:T(1024)S(1)} %bitcast.173, s32[8,256]{1,0:T(8,128)S(1)} %copy-done.5, pred[8,256]{1,0:T(8,128)(4,1)S(1)} %iota_compare_fusion), kind=kLoop, calls=%fused_computation.3 | loop fusion | flops 16760832 | bytes 83968 | tf_op jit(solution)/shard_map/reduce_sum | solution.py:440
  61.9 0.8 slice.25
  62.7 1.6 %collective-permute-start.11 = (bf16[256,512]{1,0:T(8,128)(2,1)}, bf16[256,512]{1,0:T(8,128)(2,1)S(1)}, u32[]{:S(2)}, u32[]{:S(2)}) collective-permute-start(bf16[256,512]{1,0:T(8,128)(2,1)} %get-tuple-element.20), channel_id=1, source_target_pairs={{0,1},{2,0},{4,2},{6,4},{7,6},{5,7},{3,5},{1,3},{8,9},{10,8},{12,1... | collective-permute-start | bytes 786440 | tf_op jit(solution)/shard_map/ppermute | solution.py:153
  64.4 0.7 gather_fusion.1
  65.2 0.9 collective-permute-start.8
  66.1 2.3 %bitcast_reduce_fusion.1 = (f32[8,2]{0,1:T(2,128)S(1)}, f32[8,256]{1,0:T(8,128)S(1)}) fusion(bf16[8,4096]{1,0:T(8,128)(2,1)S(1)} %bitcast.170, bf16[1,256,4096]{2,1,0:T(8,128)(2,1)} %param.24), kind=kOutput, calls=%fused_computation.81 | convolution fusion | flops 16785392 | bytes 2170944 | tf_op jit(solution)/shard_map/dot_general | solution.py:21
  68.4 4.5 %collective-permute-done.8 = bf16[256,512]{1,0:T(8,128)(2,1)S(1)} collective-permute-done((bf16[256,512]{1,0:T(8,128)(2,1)S(1)}, bf16[256,512]{1,0:T(8,128)(2,1)S(1)}, u32[]{:S(2)}, u32[]{:S(2)}) %collective-permute-start.8) | collective-permute-done | bytes 262176 | tf_op jit(solution)/shard_map/ppermute | solution.py:149
  72.9 1.2 collective-permute-start.9
  74.0 2.1 %collective-permute-start.12 = (bf16[256,512]{1,0:T(8,128)(2,1)S(1)}, bf16[256,512]{1,0:T(8,128)(2,1)S(1)}, u32[]{:S(2)}, u32[]{:S(2)}) collective-permute-start(bf16[256,512]{1,0:T(8,128)(2,1)S(1)} %collective-permute-done.11), channel_id=1, source_target_pairs={{0,1},{2,0},{4,2},{6,4},{7,6},{5,7},{3,5},{1,3},{8,9},{10,8},{12,1... | collective-permute-start | bytes 786440 | tf_op jit(solution)/shard_map/ppermute | solution.py:153
  76.2 0.7 bitcast_dynamic-update-slice_fusion.6
  76.9 6.1 %collective-permute-done.9 = bf16[256,512]{1,0:T(8,128)(2,1)S(1)} collective-permute-done((bf16[256,512]{1,0:T(8,128)(2,1)S(1)}, bf16[256,512]{1,0:T(8,128)(2,1)S(1)}, u32[]{:S(2)}, u32[]{:S(2)}) %collective-permute-start.9) | collective-permute-done | bytes 262176 | tf_op jit(solution)/shard_map/ppermute | solution.py:149
  83.0 0.7 bitcast_dynamic-update-slice_fusion.5
  83.7 2.6 %collective-permute-start.13 = (bf16[256,512]{1,0:T(8,128)(2,1)S(1)}, bf16[256,512]{1,0:T(8,128)(2,1)S(1)}, u32[]{:S(2)}, u32[]{:S(2)}) collective-permute-start(bf16[256,512]{1,0:T(8,128)(2,1)S(1)} %collective-permute-done.12), channel_id=1, source_target_pairs={{0,1},{2,0},{4,2},{6,4},{7,6},{5,7},{3,5},{1,3},{8,9},{10,8},{12,1... | collective-permute-start | bytes 786440 | tf_op jit(solution)/shard_map/ppermute | solution.py:153
  86.3 0.7 bitcast_dynamic-update-slice_fusion.4
  87.0 2.9 %collective-permute-done.10 = bf16[256,512]{1,0:T(8,128)(2,1)S(1)} collective-permute-done((bf16[256,512]{1,0:T(8,128)(2,1)S(1)}, bf16[256,512]{1,0:T(8,128)(2,1)S(1)}, u32[]{:S(2)}, u32[]{:S(2)}) %collective-permute-start.10) | collective-permute-done | bytes 262176 | tf_op jit(solution)/shard_map/ppermute | solution.py:149
  89.9 0.7 bitcast_dynamic-update-slice_fusion.3
  90.6 0.7 bitcast_dynamic-update-slice_fusion.2
  91.4 0.7 bitcast_dynamic-update-slice_fusion.1
  92.1 0.7 bitcast_dynamic-update-slice_fusion
  92.8 2.9 %fusion.59 = f32[2048,512]{0,1:T(8,128)S(1)} fusion(bf16[2048,512]{1,0:T(8,128)(2,1)} %bitcast.24, bf16[512,512]{1,0:T(8,128)(2,1)S(1)} %bitcast.163), kind=kOutput, calls=%fused_computation.110 | convolution fusion | flops 1073741824 | bytes 6815744 | tf_op jit(solution)/shard_map/dot_general | solution.py:427
  96.7 1.0 multiply_reduce_fusion.1
  97.6 1.5 convolution_bitcast_fusion
  99.1 2.0 %collective-permute-start.14 = (f32[8,1,4096]{2,0,1:T(8,128)S(1)}, f32[8,1,4096]{2,0,1:T(8,128)S(1)}, u32[]{:S(2)}, u32[]{:S(2)}) collective-permute-start(f32[8,1,4096]{2,0,1:T(8,128)S(1)} %convolution_bitcast_fusion), channel_id=1, source_target_pairs={{0,1},{1,0},{2,3},{3,2},{4,5},{5,4},{6,7},{7,6},{8,9},{9,8},{10,11... | collective-permute-start | bytes 393224 | tf_op jit(solution)/shard_map/ppermute | solution.py:114
  101.1 2.9 %collective-permute-done.14 = f32[8,1,4096]{2,0,1:T(8,128)S(1)} collective-permute-done((f32[8,1,4096]{2,0,1:T(8,128)S(1)}, f32[8,1,4096]{2,0,1:T(8,128)S(1)}, u32[]{:S(2)}, u32[]{:S(2)}) %collective-permute-start.14) | collective-permute-done | bytes 131104 | tf_op jit(solution)/shard_map/ppermute | solution.py:114
  104.1 1.8 %collective-permute-start.15 = (f32[8,1,4096]{2,0,1:T(8,128)S(1)}, f32[8,1,4096]{2,0,1:T(8,128)S(1)}, u32[]{:S(2)}, u32[]{:S(2)}) collective-permute-start(f32[8,1,4096]{2,0,1:T(8,128)S(1)} %add.194), channel_id=1, source_target_pairs={{0,2},{1,3},{2,0},{3,1},{4,6},{5,7},{6,4},{7,5},{8,10},{9,11},{10,... | collective-permute-start | bytes 393224 | tf_op jit(solution)/shard_map/ppermute | solution.py:114
  105.9 3.2 %collective-permute-done.15 = f32[8,1,4096]{2,0,1:T(8,128)S(1)} collective-permute-done((f32[8,1,4096]{2,0,1:T(8,128)S(1)}, f32[8,1,4096]{2,0,1:T(8,128)S(1)}, u32[]{:S(2)}, u32[]{:S(2)}) %collective-permute-start.15) | collective-permute-done | bytes 131104 | tf_op jit(solution)/shard_map/ppermute | solution.py:114
  109.2 1.8 %collective-permute-start.16 = (f32[8,1,4096]{2,0,1:T(8,128)S(1)}, f32[8,1,4096]{2,0,1:T(8,128)S(1)}, u32[]{:S(2)}, u32[]{:S(2)}) collective-permute-start(f32[8,1,4096]{2,0,1:T(8,128)S(1)} %add.195), channel_id=1, source_target_pairs={{0,4},{1,5},{2,6},{3,7},{4,0},{5,1},{6,2},{7,3},{8,12},{9,13},{10,... | collective-permute-start | bytes 393224 | tf_op jit(solution)/shard_map/ppermute | solution.py:114
  111.0 5.5 %collective-permute-done.16 = f32[8,1,4096]{2,0,1:T(8,128)S(1)} collective-permute-done((f32[8,1,4096]{2,0,1:T(8,128)S(1)}, f32[8,1,4096]{2,0,1:T(8,128)S(1)}, u32[]{:S(2)}, u32[]{:S(2)}) %collective-permute-start.16) | collective-permute-done | bytes 131104 | tf_op jit(solution)/shard_map/ppermute | solution.py:114
  116.5 0.8 multiply_reduce_fusion
  117.4 5.1 %fusion.4 = f32[8,896]{1,0:T(8,128)S(1)} fusion(bf16[1,896,4096]{2,1,0:T(8,128)(2,1)} %param.31, f32[8,1,4096]{2,0,1:T(8,128)S(1)} %get-tuple-element.18, f32[4096]{0:T(1024)S(1)} %bitcast.171, f32[8]{0:T(128)S(1)} %add_rsqrt_fusion.2), kind=kOutput, calls=%fused_computation.8 | convolution fusion | flops 58818560 | bytes 7516192 | tf_op jit(solution)/shard_map/dot_general | solution.py:21
  122.4 5.1 %fusion.16 = bf16[8,896]{1,0:T(8,128)(2,1)S(1)} fusion(bf16[1,896,4096]{2,1,0:T(8,128)(2,1)} %param.32, f32[8,896]{1,0:T(8,128)S(1)} %fusion.4, f32[8,1,4096]{2,0,1:T(8,128)S(1)} %get-tuple-element.18, f32[4096]{0:T(1024)S(1)} %bitcast.172, f32[8]{0:T(128)S(1)} %add_rsqrt_fusion.2), kind=kOutput, calls=%fused_computation.25 | convolution fusion | flops 58861568 | bytes 7530528 | tf_op jit(solution)/shard_map/dot_general | solution.py:21
  127.5 4.2 %fusion = f32[2,2,2,4096]{3,2,1,0:T(2,128)S(1)} fusion(bf16[2,2,2,896]{3,2,1,0:T(2,128)(2,1)S(1)} %dot_general.37, bf16[1,896,4096]{2,1,0:T(8,128)(2,1)} %param.33), kind=kOutput, calls=%fused_computation.4 | convolution fusion | flops 58720256 | bytes 7485440 | tf_op jit(solution)/shard_map/dot_general | solution.py:458
  131.9 2.1 %collective-permute-start.17 = (f32[2,2,1,1,4096]{4,2,3,1,0:T(1,128)S(1)}, f32[2,2,1,1,4096]{4,2,3,1,0:T(1,128)S(1)}, u32[]{:S(2)}, u32[]{:S(2)}) collective-permute-start(f32[2,2,1,1,4096]{4,2,3,1,0:T(1,128)S(1)} %dynamic-slice_bitcast_fusion), channel_id=1, source_target_pairs={{0,1},{1,0},{2,3},{3,2},{4,5},{5,4},{6,7},{7,6},{8,9},{9,8},{10,11... | collective-permute-start | bytes 196616 | tf_op jit(solution)/shard_map/ppermute | solution.py:473
  133.9 2.2 %collective-permute-done.17 = f32[2,2,1,1,4096]{4,2,3,1,0:T(1,128)S(1)} collective-permute-done((f32[2,2,1,1,4096]{4,2,3,1,0:T(1,128)S(1)}, f32[2,2,1,1,4096]{4,2,3,1,0:T(1,128)S(1)}, u32[]{:S(2)}, u32[]{:S(2)}) %collective-permute-start.17) | collective-permute-done | bytes 65568 | tf_op jit(solution)/shard_map/ppermute | solution.py:473
  136.8 3.5 %collective-permute-done.18 = f32[2,1,1,1,4096]{4,2,3,1,0:T(1,128)S(1)} collective-permute-done((f32[2,1,1,1,4096]{4,2,3,1,0:T(1,128)S(1)}, f32[2,1,1,1,4096]{4,2,3,1,0:T(1,128)S(1)}, u32[]{:S(2)}, u32[]{:S(2)}) %collective-permute-start.18) | collective-permute-done | bytes 32800 | tf_op jit(solution)/shard_map/ppermute | solution.py:473
  140.4 1.4 collective-permute-start.19
  141.9 3.6 %collective-permute-done.20 = f32[1,4096]{1,0:T(1,128)S(1)} collective-permute-done((f32[1,4096]{1,0:T(1,128)S(1)}, f32[1,4096]{1,0:T(1,128)S(1)}, u32[]{:S(2)}, u32[]{:S(2)}) %collective-permute-start.20) | collective-permute-done | bytes 16416 | tf_op jit(solution)/shard_map/ppermute | solution.py:490
  (72 shorter events, 8.7 us)
Async XLA Ops:
  0.0 97.6 %copy-start = (bf16[1,256,4096]{2,1,0:T(8,128)(2,1)S(1)}, bf16[1,256,4096]{2,1,0:T(8,128)(2,1)}, u32[]{:S(2)}) copy-start(bf16[1,256,4096]{2,1,0:T(8,128)(2,1)} %param.29) | copy-start | bytes 6291460
  0.9 15.6 %copy-start.2 = (bf16[8,512]{1,0:T(8,128)(2,1)}, bf16[8,512]{1,0:T(8,128)(2,1)S(1)}, u32[]{:S(2)}) copy-start(bf16[8,512]{1,0:T(8,128)(2,1)S(1)} %reshape_squeeze.9) | copy-start | bytes 24580
  2.5 19.2 %collective-permute-start = (bf16[136,512]{1,0:T(8,128)(2,1)}, bf16[136,512]{1,0:T(8,128)(2,1)S(1)}, u32[]{:S(2)}, u32[]{:S(2)}) collective-permute-start(bf16[136,512]{1,0:T(8,128)(2,1)} %pad_maximum_fusion), channel_id=1, source_target_pairs={{0,2},{2,4},{4,6},{6,7},{7,5},{5,3},{3,1},{1,0},{8,10},{10,12},{12... | collective-permute-start | bytes 417800 | tf_op jit(solution)/shard_map/ppermute | solution.py:149
  5.5 16.2 %collective-permute-start.1 = (bf16[136,512]{1,0:T(8,128)(2,1)}, bf16[136,512]{1,0:T(8,128)(2,1)S(1)}, u32[]{:S(2)}, u32[]{:S(2)}) collective-permute-start(bf16[136,512]{1,0:T(8,128)(2,1)} %pad_maximum_fusion), channel_id=1, source_target_pairs={{0,1},{2,0},{4,2},{6,4},{7,6},{5,7},{3,5},{1,3},{8,9},{10,8},{12,1... | collective-permute-start | bytes 417800 | tf_op jit(solution)/shard_map/ppermute | solution.py:153
  16.8 3.5 %copy-start.1 = (bf16[1,128,512]{2,1,0:T(8,128)(2,1)S(1)}, bf16[1,128,512]{2,1,0:T(8,128)(2,1)}, u32[]{:S(2)}) copy-start(bf16[1,128,512]{2,1,0:T(8,128)(2,1)} %param.27) | copy-start | bytes 393220
  21.7 34.0 %copy-start.9 = (pred[8]{0:T(512)(128)(4,1)S(1)}, pred[8]{0:T(512)(128)(4,1)}, u32[]{:S(2)}) copy-start(pred[8]{0:T(512)(128)(4,1)} %compare_and_fusion) | copy-start | bytes 28
  21.7 71.1 %all-to-all-start = ((bf16[8,64,512]{2,1,0:T(8,128)(2,1)}), bf16[8,64,512]{2,1,0:T(8,128)(2,1)S(1)}, u32[]{:S(2)}, u32[]{:S(2)}) async-start(bf16[8,64,512]{2,1,0:T(8,128)(2,1)} %reshape.230), calls=%async_computation | async-start | bytes 1048576 | tf_op jit(solution)/shard_map/all_to_all | solution.py:403
  28.0 11.1 %collective-permute-start.2 = (bf16[136,512]{1,0:T(8,128)(2,1)S(1)}, bf16[136,512]{1,0:T(8,128)(2,1)S(1)}, u32[]{:S(2)}, u32[]{:S(2)}) collective-permute-start(bf16[136,512]{1,0:T(8,128)(2,1)S(1)} %collective-permute-done), channel_id=1, source_target_pairs={{0,2},{2,4},{4,6},{6,7},{7,5},{5,3},{3,1},{1,0},{8,10},{10,12},{12... | collective-permute-start | bytes 417800 | tf_op jit(solution)/shard_map/ppermute | solution.py:149
  30.0 13.3 %collective-permute-start.5 = (bf16[136,512]{1,0:T(8,128)(2,1)S(1)}, bf16[136,512]{1,0:T(8,128)(2,1)S(1)}, u32[]{:S(2)}, u32[]{:S(2)}) collective-permute-start(bf16[136,512]{1,0:T(8,128)(2,1)S(1)} %collective-permute-done.1), channel_id=1, source_target_pairs={{0,1},{2,0},{4,2},{6,4},{7,6},{5,7},{3,5},{1,3},{8,9},{10,8},{12,1... | collective-permute-start | bytes 417800 | tf_op jit(solution)/shard_map/ppermute | solution.py:153
  39.1 6.8 %collective-permute-start.3 = (bf16[136,512]{1,0:T(8,128)(2,1)S(1)}, bf16[136,512]{1,0:T(8,128)(2,1)S(1)}, u32[]{:S(2)}, u32[]{:S(2)}) collective-permute-start(bf16[136,512]{1,0:T(8,128)(2,1)S(1)} %collective-permute-done.2), channel_id=1, source_target_pairs={{0,2},{2,4},{4,6},{6,7},{7,5},{5,3},{3,1},{1,0},{8,10},{10,12},{12... | collective-permute-start | bytes 417800 | tf_op jit(solution)/shard_map/ppermute | solution.py:149
  43.3 11.7 %collective-permute-start.6 = (bf16[136,512]{1,0:T(8,128)(2,1)S(1)}, bf16[136,512]{1,0:T(8,128)(2,1)S(1)}, u32[]{:S(2)}, u32[]{:S(2)}) collective-permute-start(bf16[136,512]{1,0:T(8,128)(2,1)S(1)} %collective-permute-done.5), channel_id=1, source_target_pairs={{0,1},{2,0},{4,2},{6,4},{7,6},{5,7},{3,5},{1,3},{8,9},{10,8},{12,1... | collective-permute-start | bytes 417800 | tf_op jit(solution)/shard_map/ppermute | solution.py:153
  45.9 7.1 %collective-permute-start.4 = (bf16[136,512]{1,0:T(8,128)(2,1)S(1)}, bf16[136,512]{1,0:T(8,128)(2,1)S(1)}, u32[]{:S(2)}, u32[]{:S(2)}) collective-permute-start(bf16[136,512]{1,0:T(8,128)(2,1)S(1)} %collective-permute-done.3), channel_id=1, source_target_pairs={{0,2},{2,4},{4,6},{6,7},{7,5},{5,3},{3,1},{1,0},{8,10},{10,12},{12... | collective-permute-start | bytes 417800 | tf_op jit(solution)/shard_map/ppermute | solution.py:149
  55.7 3.1 %copy-start.4 = (s32[1,2,8,128]{3,1,2,0:T(2,128)S(1)}, s32[1,2,8,128]{3,1,2,0:T(2,128)}, u32[]{:S(2)}) copy-start(s32[1,2,8,128]{3,1,2,0:T(2,128)} %copy.41) | copy-start | bytes 24580
  55.7 3.1 %copy-start.5 = (s32[8,256]{1,0:T(8,128)S(1)}, s32[8,256]{1,0:T(8,128)}, u32[]{:S(2)}) copy-start(s32[8,256]{1,0:T(8,128)} %param.22) | copy-start | bytes 24580
  55.7 9.4 %copy-start.6 = (pred[8]{0:T(512)(128)(4,1)S(1)}, pred[8]{0:T(512)(128)(4,1)}, u32[]{:S(2)}) copy-start(pred[8]{0:T(512)(128)(4,1)} %compare_and_fusion.1) | copy-start | bytes 28
  58.3 6.8 %collective-permute-start.7 = (bf16[256,512]{1,0:T(8,128)(2,1)}, bf16[256,512]{1,0:T(8,128)(2,1)S(1)}, u32[]{:S(2)}, u32[]{:S(2)}) collective-permute-start(bf16[256,512]{1,0:T(8,128)(2,1)} %get-tuple-element.20), channel_id=1, source_target_pairs={{0,2},{2,4},{4,6},{6,7},{7,5},{5,3},{3,1},{1,0},{8,10},{10,12},{12... | collective-permute-start | bytes 786440 | tf_op jit(solution)/shard_map/ppermute | solution.py:149
  62.7 11.3 %collective-permute-start.11 = (bf16[256,512]{1,0:T(8,128)(2,1)}, bf16[256,512]{1,0:T(8,128)(2,1)S(1)}, u32[]{:S(2)}, u32[]{:S(2)}) collective-permute-start(bf16[256,512]{1,0:T(8,128)(2,1)} %get-tuple-element.20), channel_id=1, source_target_pairs={{0,1},{2,0},{4,2},{6,4},{7,6},{5,7},{3,5},{1,3},{8,9},{10,8},{12,1... | collective-permute-start | bytes 786440 | tf_op jit(solution)/shard_map/ppermute | solution.py:153
  65.2 7.7 %collective-permute-start.8 = (bf16[256,512]{1,0:T(8,128)(2,1)S(1)}, bf16[256,512]{1,0:T(8,128)(2,1)S(1)}, u32[]{:S(2)}, u32[]{:S(2)}) collective-permute-start(bf16[256,512]{1,0:T(8,128)(2,1)S(1)} %collective-permute-done.7), channel_id=1, source_target_pairs={{0,2},{2,4},{4,6},{6,7},{7,5},{5,3},{3,1},{1,0},{8,10},{10,12},{12... | collective-permute-start | bytes 786440 | tf_op jit(solution)/shard_map/ppermute | solution.py:149
  72.9 10.1 %collective-permute-start.9 = (bf16[256,512]{1,0:T(8,128)(2,1)S(1)}, bf16[256,512]{1,0:T(8,128)(2,1)S(1)}, u32[]{:S(2)}, u32[]{:S(2)}) collective-permute-start(bf16[256,512]{1,0:T(8,128)(2,1)S(1)} %collective-permute-done.8), channel_id=1, source_target_pairs={{0,2},{2,4},{4,6},{6,7},{7,5},{5,3},{3,1},{1,0},{8,10},{10,12},{12... | collective-permute-start | bytes 786440 | tf_op jit(solution)/shard_map/ppermute | solution.py:149
  74.0 9.7 %collective-permute-start.12 = (bf16[256,512]{1,0:T(8,128)(2,1)S(1)}, bf16[256,512]{1,0:T(8,128)(2,1)S(1)}, u32[]{:S(2)}, u32[]{:S(2)}) collective-permute-start(bf16[256,512]{1,0:T(8,128)(2,1)S(1)} %collective-permute-done.11), channel_id=1, source_target_pairs={{0,1},{2,0},{4,2},{6,4},{7,6},{5,7},{3,5},{1,3},{8,9},{10,8},{12,1... | collective-permute-start | bytes 786440 | tf_op jit(solution)/shard_map/ppermute | solution.py:153
  83.0 6.9 %collective-permute-start.10 = (bf16[256,512]{1,0:T(8,128)(2,1)S(1)}, bf16[256,512]{1,0:T(8,128)(2,1)S(1)}, u32[]{:S(2)}, u32[]{:S(2)}) collective-permute-start(bf16[256,512]{1,0:T(8,128)(2,1)S(1)} %collective-permute-done.9), channel_id=1, source_target_pairs={{0,2},{2,4},{4,6},{6,7},{7,5},{5,3},{3,1},{1,0},{8,10},{10,12},{12... | collective-permute-start | bytes 786440 | tf_op jit(solution)/shard_map/ppermute | solution.py:149
  83.7 8.3 %collective-permute-start.13 = (bf16[256,512]{1,0:T(8,128)(2,1)S(1)}, bf16[256,512]{1,0:T(8,128)(2,1)S(1)}, u32[]{:S(2)}, u32[]{:S(2)}) collective-permute-start(bf16[256,512]{1,0:T(8,128)(2,1)S(1)} %collective-permute-done.12), channel_id=1, source_target_pairs={{0,1},{2,0},{4,2},{6,4},{7,6},{5,7},{3,5},{1,3},{8,9},{10,8},{12,1... | collective-permute-start | bytes 786440 | tf_op jit(solution)/shard_map/ppermute | solution.py:153
  95.7 0.7 copy-start.7
  96.1 0.6 copy-start.8
  97.6 19.7 %copy-start.3 = (f32[1,4096]{1,0:T(1,128)S(1)}, f32[1,4096]{1,0:T(1,128)}, u32[]{:S(2)}) copy-start(f32[1,4096]{1,0:T(1,128)} %param.30) | copy-start | bytes 49156
  99.1 5.0 %collective-permute-start.14 = (f32[8,1,4096]{2,0,1:T(8,128)S(1)}, f32[8,1,4096]{2,0,1:T(8,128)S(1)}, u32[]{:S(2)}, u32[]{:S(2)}) collective-permute-start(f32[8,1,4096]{2,0,1:T(8,128)S(1)} %convolution_bitcast_fusion), channel_id=1, source_target_pairs={{0,1},{1,0},{2,3},{3,2},{4,5},{5,4},{6,7},{7,6},{8,9},{9,8},{10,11... | collective-permute-start | bytes 393224 | tf_op jit(solution)/shard_map/ppermute | solution.py:114
  104.1 5.0 %collective-permute-start.15 = (f32[8,1,4096]{2,0,1:T(8,128)S(1)}, f32[8,1,4096]{2,0,1:T(8,128)S(1)}, u32[]{:S(2)}, u32[]{:S(2)}) collective-permute-start(f32[8,1,4096]{2,0,1:T(8,128)S(1)} %add.194), channel_id=1, source_target_pairs={{0,2},{1,3},{2,0},{3,1},{4,6},{5,7},{6,4},{7,5},{8,10},{9,11},{10,... | collective-permute-start | bytes 393224 | tf_op jit(solution)/shard_map/ppermute | solution.py:114
  109.2 7.3 %collective-permute-start.16 = (f32[8,1,4096]{2,0,1:T(8,128)S(1)}, f32[8,1,4096]{2,0,1:T(8,128)S(1)}, u32[]{:S(2)}, u32[]{:S(2)}) collective-permute-start(f32[8,1,4096]{2,0,1:T(8,128)S(1)} %add.195), channel_id=1, source_target_pairs={{0,4},{1,5},{2,6},{3,7},{4,0},{5,1},{6,2},{7,3},{8,12},{9,13},{10,... | collective-permute-start | bytes 393224 | tf_op jit(solution)/shard_map/ppermute | solution.py:114
  131.9 4.3 %collective-permute-start.17 = (f32[2,2,1,1,4096]{4,2,3,1,0:T(1,128)S(1)}, f32[2,2,1,1,4096]{4,2,3,1,0:T(1,128)S(1)}, u32[]{:S(2)}, u32[]{:S(2)}) collective-permute-start(f32[2,2,1,1,4096]{4,2,3,1,0:T(1,128)S(1)} %dynamic-slice_bitcast_fusion), channel_id=1, source_target_pairs={{0,1},{1,0},{2,3},{3,2},{4,5},{5,4},{6,7},{7,6},{8,9},{9,8},{10,11... | collective-permute-start | bytes 196616 | tf_op jit(solution)/shard_map/ppermute | solution.py:473
  136.3 4.0 %collective-permute-start.18 = (f32[2,1,1,1,4096]{4,2,3,1,0:T(1,128)S(1)}, f32[2,1,1,1,4096]{4,2,3,1,0:T(1,128)S(1)}, u32[]{:S(2)}, u32[]{:S(2)}) collective-permute-start(f32[2,1,1,1,4096]{4,2,3,1,0:T(1,128)S(1)} %constant_dynamic-slice_fusion), channel_id=1, source_target_pairs={{0,2},{1,3},{2,0},{3,1},{4,6},{5,7},{6,4},{7,5},{8,10},{9,11},{10,... | collective-permute-start | bytes 98312 | tf_op jit(solution)/shard_map/ppermute | solution.py:473
  140.4 5.1 %collective-permute-start.20 = (f32[1,4096]{1,0:T(1,128)S(1)}, f32[1,4096]{1,0:T(1,128)S(1)}, u32[]{:S(2)}, u32[]{:S(2)}) collective-permute-start(f32[1,4096]{1,0:T(1,128)S(1)} %dynamic-slice_bitcast_fusion.1), channel_id=1, source_target_pairs={{0,12},{1,13},{2,14},{3,15},{4,8},{5,9},{6,10},{7,11},{8,20},{9,21... | collective-permute-start | bytes 49160 | tf_op jit(solution)/shard_map/ppermute | solution.py:490
  140.4 5.0 %collective-permute-start.19 = (f32[1,4096]{1,0:T(1,128)S(1)}, f32[1,4096]{1,0:T(1,128)S(1)}, u32[]{:S(2)}, u32[]{:S(2)}) collective-permute-start(f32[1,4096]{1,0:T(1,128)S(1)} %bitcast_add_fusion.1), channel_id=1, source_target_pairs={{0,8},{1,9},{2,10},{3,11},{4,12},{5,13},{6,14},{7,15},{8,16},{9,17... | collective-permute-start | bytes 49160 | tf_op jit(solution)/shard_map/ppermute | solution.py:489

commit v9 on v6

--- a/solution.py
+++ b/solution.py
@@ -3,6 +3,8 @@
 import jax
 import jax.numpy as jnp
 from jax import lax
+from jax.experimental import pallas as pl
+from jax.experimental.pallas import tpu as pltpu
 from jax.sharding import PartitionSpec as P
 
 HEADS = 16
@@ -360,6 +362,40 @@
     return output_rows[None]
 
 
+def ffn_block(rows_ref, gate_ref, up_ref, down_ref, out_ref):
+    step = pl.program_id(0)
+
+    @pl.when(step == 0)
+    def _():
+        out_ref[...] = jnp.zeros_like(out_ref)
+
+    rows = rows_ref[...]
+    dims = (((1,), (1,)), ((), ()))
+    gate_sum = lax.dot_general(rows, gate_ref[...], dims, preferred_element_type=jnp.float32)
+    up_sum = lax.dot_general(rows, up_ref[...], dims, preferred_element_type=jnp.float32)
+    hidden = (gate_sum * jax.nn.sigmoid(gate_sum) * up_sum).astype(jnp.bfloat16)
+    out_ref[...] += jnp.dot(hidden, down_ref[...], preferred_element_type=jnp.float32)
+
+
+def gated_ffn(rows, gate, up, down):
+    units, width = gate.shape
+    block = 128 if units % 128 == 0 else units
+    count = rows.shape[0]
+    return pl.pallas_call(
+        ffn_block,
+        grid=(units // block,),
+        in_specs=[
+            pl.BlockSpec((count, width), lambda i: (0, 0)),
+            pl.BlockSpec((block, width), lambda i: (i, 0)),
+            pl.BlockSpec((block, width), lambda i: (i, 0)),
+            pl.BlockSpec((block, width), lambda i: (i, 0)),
+        ],
+        out_specs=pl.BlockSpec((count, width), lambda i: (0, 0)),
+        out_shape=jax.ShapeDtypeStruct((count, width), jnp.float32),
+        compiler_params=pltpu.CompilerParams(dimension_semantics=("arbitrary",)),
+    )(rows, gate, up, down)
+
+
 def heads_split(
     acts,
     patches,
@@ -451,10 +487,7 @@
     residual_all = everyone.reshape(group_size, sites_here, -1).astype(jnp.float32) + attn_all
     residual = lax.dynamic_index_in_dim(residual_all, my_index, 0, keepdims=False)
     normed_rows = rms_norm(residual_all, ffn_gain[0]).astype(jnp.bfloat16).reshape(-1, model_width)
-    gate_sum = by_rows(normed_rows, gate_weight[0])
-    up_sum = by_rows(normed_rows, up_weight[0])
-    hidden_ffn = (jax.nn.silu(gate_sum) * up_sum).astype(jnp.bfloat16)
-    down_part = jnp.dot(hidden_ffn, down_weight[0], preferred_element_type=jnp.float32)
+    down_part = gated_ffn(normed_rows, gate_weight[0], up_weight[0], down_weight[0])
     down_part = down_part.reshape(group_size, sites_here, -1)
     return last_round(down_part, residual, group_size, section_count, my_index)
 

time: 130 us -> 129 us (level)
  matrix products: 22.1 us -> 7.73 us
  Pallas kernels: 0 us -> 12.4 us
    pallas_call x0 -> x1, Pallas kernels: none -> 12.4 us  [gated_ffn(): pl.pallas_call(ffn_block, grid=(units // block,), in_specs=[pl.BlockSpec(...]
    dot_general x3 -> x1, matrix products: 12.5 us -> 2.31 us  [by_rows(): lax.dot_general(left, weight_rows, (((1,), (1,)), ((), ())), preferred_el...]
    dot_general x1 -> x0, matrix products: 4.22 us -> none  [heads_split(): jnp.dot(hidden_ffn, down_weight[0], preferred_element_type=jnp.float32)]
  transfers between devices with their start and end apart: 22 -> 22, of which waited for: 14 -> 14; matrix products, arithmetic and copies ran while one was open for 18% -> 19% of each run, Pallas kernels for 0% -> 0%
where the time goes in v9:
time: 129 us
  waiting for transfers between devices  47.1 us (37%)
  starting transfers between devices  34.8 us (27%)
  local copies, waits for them, and re-layouts  17.1 us (13%)
  Pallas kernels  12.4 us (10%)
  other arithmetic  9.39 us (7%)
  matrix products  7.73 us (6%)
    ppermute x8, waiting for transfers between devices, _issue(): self.ahead = lax.ppermute(self.ahead, 'site', self.forward)  26.1 us
    ppermute x8, starting transfers between devices, _issue(): self.ahead = lax.ppermute(self.ahead, 'site', self.forward)  18.1 us
    pallas_call x1, Pallas kernels, gated_ffn(): pl.pallas_call(ffn_block, grid=(units // block,), in_specs=[pl.BlockSpec(...  12.4 us
    ppermute x3, waiting for transfers between devices, doubling_sum(): state = state + lax.ppermute(state, 'site', xor_pairs(count, bit))  12.1 us
    unnamed x44, local copies, waits for them, and re-layouts  7.91 us
    ppermute x2, waiting for transfers between devices, last_round(): state = keep + lax.ppermute(send, 'site', xor_pairs(group_size, bit))  6.53 us
    all_to_all x1, starting transfers between devices, heads_split(): lax.all_to_all(col_blocks, 'site', split_axis=0, concat_axis=0, tiled=True)  6.25 us
    ppermute x3, starting transfers between devices, doubling_sum(): state = state + lax.ppermute(state, 'site', xor_pairs(count, bit))  5.2 us
  transfers between devices with their start and end apart: 22, of which 14 were waited for; matrix products, arithmetic and copies ran while one was open for 19% of the time, Pallas kernels for 0%

profile of v9, /device:TPU:0, one launch (start us, length us, event | category | flops | bytes accessed | tf_op | source)
XLA Modules:
  0.0 128.9 jit_solution(9939799471928939262)
XLA Ops:
  0.0 0.9 reduce.19
  0.9 1.6 %pad_maximum_fusion = bf16[136,512]{1,0:T(8,128)(2,1)} fusion(bf16[8,512]{1,0:T(8,128)(2,1)S(1)} %reshape_squeeze.9, bf16[128,512]{1,0:T(8,128)(2,1)} %bitcast.149), kind=kLoop, calls=%fused_computation.46 | loop fusion | flops 278528 | bytes 278528 | tf_op jit(solution)/shard_map/concatenate | solution.py:430
  2.5 3.0 %collective-permute-start = (bf16[136,512]{1,0:T(8,128)(2,1)}, bf16[136,512]{1,0:T(8,128)(2,1)}, u32[]{:S(2)}, u32[]{:S(2)}) collective-permute-start(bf16[136,512]{1,0:T(8,128)(2,1)} %pad_maximum_fusion), channel_id=1, source_target_pairs={{0,2},{2,4},{4,6},{6,7},{7,5},{5,3},{3,1},{1,0},{8,10},{10,12},{12... | collective-permute-start | bytes 417800 | tf_op jit(solution)/shard_map/ppermute | solution.py:151
  5.6 1.2 copy.38
  6.8 0.4 copy.42
  7.2 1.1 reshape.224
  8.3 6.3 %all-to-all-start = ((bf16[8,64,512]{2,1,0:T(8,128)(2,1)}), bf16[8,64,512]{2,1,0:T(8,128)(2,1)S(1)}, u32[]{:S(2)}, u32[]{:S(2)}) async-start(bf16[8,64,512]{2,1,0:T(8,128)(2,1)} %reshape.224), calls=%async_computation | async-start | bytes 1048576 | tf_op jit(solution)/shard_map/all_to_all | solution.py:451
  14.6 0.6 dynamic_slice.31
  15.2 0.7 compare_select_fusion.3
  15.9 0.6 gather_fusion
  16.6 0.6 iota_reduce_fusion
  17.2 0.5 broadcast_bitcast_fusion
  17.8 0.6 broadcast_bitcast_fusion.1
  18.5 3.1 %convert_reduce_fusion = f32[8,2048]{1,0:T(8,128)S(1)} fusion(s32[2048]{0:T(1024)S(1)} %bitcast.152, s32[8,256]{1,0:T(8,128)S(1)} %copy-done.6, pred[8,256]{1,0:T(8,128)(4,1)S(1)} %iota_compare_fusion), kind=kLoop, calls=%fused_computation.3 | loop fusion | flops 16760832 | bytes 83968 | tf_op jit(solution)/shard_map/reduce_sum | solution.py:475
  21.7 1.0 copy.31
  22.7 1.3 %copy.32 = bf16[256,8,128]{2,0,1:T(8,128)(2,1)S(1)} copy(bf16[256,8,128]{0,2,1:T(8,128)(2,1)} %bitcast.147) | data formatting | bytes 1048576 | tf_op jit(solution)/shard_map/reshape;squeeze | solution.py:441
  24.0 1.4 %gather_fusion.2 = bf16[8,256,128]{2,1,0:T(8,128)(2,1)} fusion(bf16[256,8,128]{2,0,1:T(8,128)(2,1)S(1)} %copy.32, s32[1024]{0:T(1024)S(1)} %pad_clamp_fusion), kind=kCustom, calls=%fused_computation.2 | custom fusion | bytes 1048608 | tf_op jit(solution)/shard_map/jit(_take)/gather | solution.py:441
  25.4 2.1 %collective-permute-start.1 = (bf16[136,512]{1,0:T(8,128)(2,1)}, bf16[136,512]{1,0:T(8,128)(2,1)S(1)}, u32[]{:S(2)}, u32[]{:S(2)}) collective-permute-start(bf16[136,512]{1,0:T(8,128)(2,1)} %collective-permute-done), channel_id=1, source_target_pairs={{0,2},{2,4},{4,6},{6,7},{7,5},{5,3},{3,1},{1,0},{8,10},{10,12},{12... | collective-permute-start | bytes 417800 | tf_op jit(solution)/shard_map/ppermute | solution.py:151
  27.5 0.9 bitcast_dynamic-update-slice_fusion.14
  28.5 2.3 %collective-permute-done.1 = bf16[136,512]{1,0:T(8,128)(2,1)S(1)} collective-permute-done((bf16[136,512]{1,0:T(8,128)(2,1)}, bf16[136,512]{1,0:T(8,128)(2,1)S(1)}, u32[]{:S(2)}, u32[]{:S(2)}) %collective-permute-start.1) | collective-permute-done | bytes 139296 | tf_op jit(solution)/shard_map/ppermute | solution.py:151
  30.7 2.0 %collective-permute-start.2 = (bf16[136,512]{1,0:T(8,128)(2,1)S(1)}, bf16[136,512]{1,0:T(8,128)(2,1)S(1)}, u32[]{:S(2)}, u32[]{:S(2)}) collective-permute-start(bf16[136,512]{1,0:T(8,128)(2,1)S(1)} %collective-permute-done.1), channel_id=1, source_target_pairs={{0,2},{2,4},{4,6},{6,7},{7,5},{5,3},{3,1},{1,0},{8,10},{10,12},{12... | collective-permute-start | bytes 417800 | tf_op jit(solution)/shard_map/ppermute | solution.py:151
  32.8 3.6 %collective-permute-done.2 = bf16[136,512]{1,0:T(8,128)(2,1)S(1)} collective-permute-done((bf16[136,512]{1,0:T(8,128)(2,1)S(1)}, bf16[136,512]{1,0:T(8,128)(2,1)S(1)}, u32[]{:S(2)}, u32[]{:S(2)}) %collective-permute-start.2) | collective-permute-done | bytes 139296 | tf_op jit(solution)/shard_map/ppermute | solution.py:151
  36.4 2.5 %collective-permute-start.3 = (bf16[136,512]{1,0:T(8,128)(2,1)S(1)}, bf16[136,512]{1,0:T(8,128)(2,1)S(1)}, u32[]{:S(2)}, u32[]{:S(2)}) collective-permute-start(bf16[136,512]{1,0:T(8,128)(2,1)S(1)} %collective-permute-done.2), channel_id=1, source_target_pairs={{0,2},{2,4},{4,6},{6,7},{7,5},{5,3},{3,1},{1,0},{8,10},{10,12},{12... | collective-permute-start | bytes 417800 | tf_op jit(solution)/shard_map/ppermute | solution.py:151
  38.9 2.7 %collective-permute-done.3 = bf16[136,512]{1,0:T(8,128)(2,1)S(1)} collective-permute-done((bf16[136,512]{1,0:T(8,128)(2,1)S(1)}, bf16[136,512]{1,0:T(8,128)(2,1)S(1)}, u32[]{:S(2)}, u32[]{:S(2)}) %collective-permute-start.3) | collective-permute-done | bytes 139296 | tf_op jit(solution)/shard_map/ppermute | solution.py:151
  41.7 1.4 %bitcast_dynamic-update-slice_fusion.7 = (bf16[8,256,512]{2,1,0:T(8,128)(2,1)}, bf16[256,512]{1,0:T(8,128)(2,1)}) fusion(bf16[8,136,512]{2,1,0:T(8,128)(2,1)S(1)} %bitcast_dynamic-update-slice_fusion.8, bf16[8,256,128]{2,1,0:T(8,128)(2,1)S(1)} %copy-done.4, pred[8]{0:T(512)(128)(4,1)S(1)} %compare_and_fusion), kind=kOutput, calls=%fused_computation.44 | convolution fusion | flops 269877248 | bytes 2097664 | tf_op jit(solution)/shard_map/dot_general | solution.py:443
  43.1 2.5 %collective-permute-start.7 = (bf16[256,512]{1,0:T(8,128)(2,1)}, bf16[256,512]{1,0:T(8,128)(2,1)S(1)}, u32[]{:S(2)}, u32[]{:S(2)}) collective-permute-start(bf16[256,512]{1,0:T(8,128)(2,1)} %get-tuple-element.10), channel_id=1, source_target_pairs={{0,2},{2,4},{4,6},{6,7},{7,5},{5,3},{3,1},{1,0},{8,10},{10,12},{12... | collective-permute-start | bytes 786440 | tf_op jit(solution)/shard_map/ppermute | solution.py:151
  45.7 0.6 gather_fusion.1
  46.3 6.0 %collective-permute-done.7 = bf16[256,512]{1,0:T(8,128)(2,1)S(1)} collective-permute-done((bf16[256,512]{1,0:T(8,128)(2,1)}, bf16[256,512]{1,0:T(8,128)(2,1)S(1)}, u32[]{:S(2)}, u32[]{:S(2)}) %collective-permute-start.7) | collective-permute-done | bytes 262176 | tf_op jit(solution)/shard_map/ppermute | solution.py:151
  52.4 2.4 %collective-permute-start.8 = (bf16[256,512]{1,0:T(8,128)(2,1)S(1)}, bf16[256,512]{1,0:T(8,128)(2,1)S(1)}, u32[]{:S(2)}, u32[]{:S(2)}) collective-permute-start(bf16[256,512]{1,0:T(8,128)(2,1)S(1)} %collective-permute-done.7), channel_id=1, source_target_pairs={{0,2},{2,4},{4,6},{6,7},{7,5},{5,3},{3,1},{1,0},{8,10},{10,12},{12... | collective-permute-start | bytes 786440 | tf_op jit(solution)/shard_map/ppermute | solution.py:151
  54.7 2.3 %bitcast_reduce_fusion.1 = (f32[8,2]{0,1:T(2,128)S(1)}, f32[8,256]{1,0:T(8,128)S(1)}) fusion(bf16[8,4096]{1,0:T(8,128)(2,1)S(1)} %bitcast.151, bf16[1,256,4096]{2,1,0:T(8,128)(2,1)} %param.24), kind=kOutput, calls=%fused_computation.71 | convolution fusion | flops 16785392 | bytes 2170944 | tf_op jit(solution)/shard_map/dot_general | solution.py:23
  57.1 3.7 %collective-permute-done.8 = bf16[256,512]{1,0:T(8,128)(2,1)S(1)} collective-permute-done((bf16[256,512]{1,0:T(8,128)(2,1)S(1)}, bf16[256,512]{1,0:T(8,128)(2,1)S(1)}, u32[]{:S(2)}, u32[]{:S(2)}) %collective-permute-start.8) | collective-permute-done | bytes 262176 | tf_op jit(solution)/shard_map/ppermute | solution.py:151
  60.8 2.0 %collective-permute-start.9 = (bf16[256,512]{1,0:T(8,128)(2,1)S(1)}, bf16[256,512]{1,0:T(8,128)(2,1)S(1)}, u32[]{:S(2)}, u32[]{:S(2)}) collective-permute-start(bf16[256,512]{1,0:T(8,128)(2,1)S(1)} %collective-permute-done.8), channel_id=1, source_target_pairs={{0,2},{2,4},{4,6},{6,7},{7,5},{5,3},{3,1},{1,0},{8,10},{10,12},{12... | collective-permute-start | bytes 786440 | tf_op jit(solution)/shard_map/ppermute | solution.py:151
  62.8 0.7 bitcast_dynamic-update-slice_fusion.6
  63.6 4.8 %collective-permute-done.9 = bf16[256,512]{1,0:T(8,128)(2,1)S(1)} collective-permute-done((bf16[256,512]{1,0:T(8,128)(2,1)S(1)}, bf16[256,512]{1,0:T(8,128)(2,1)S(1)}, u32[]{:S(2)}, u32[]{:S(2)}) %collective-permute-start.9) | collective-permute-done | bytes 262176 | tf_op jit(solution)/shard_map/ppermute | solution.py:151
  68.4 1.7 %collective-permute-start.10 = (bf16[256,512]{1,0:T(8,128)(2,1)S(1)}, bf16[256,512]{1,0:T(8,128)(2,1)S(1)}, u32[]{:S(2)}, u32[]{:S(2)}) collective-permute-start(bf16[256,512]{1,0:T(8,128)(2,1)S(1)} %collective-permute-done.9), channel_id=1, source_target_pairs={{0,2},{2,4},{4,6},{6,7},{7,5},{5,3},{3,1},{1,0},{8,10},{10,12},{12... | collective-permute-start | bytes 786440 | tf_op jit(solution)/shard_map/ppermute | solution.py:151
  70.1 0.7 bitcast_dynamic-update-slice_fusion.5
  70.8 0.4 collective-permute-start.13
  71.1 0.7 bitcast_dynamic-update-slice_fusion.4
  71.9 2.9 %collective-permute-done.10 = bf16[256,512]{1,0:T(8,128)(2,1)S(1)} collective-permute-done((bf16[256,512]{1,0:T(8,128)(2,1)S(1)}, bf16[256,512]{1,0:T(8,128)(2,1)S(1)}, u32[]{:S(2)}, u32[]{:S(2)}) %collective-permute-start.10) | collective-permute-done | bytes 262176 | tf_op jit(solution)/shard_map/ppermute | solution.py:151
  74.8 0.7 bitcast_dynamic-update-slice_fusion.3
  75.5 0.7 bitcast_dynamic-update-slice_fusion.2
  76.2 0.7 bitcast_dynamic-update-slice_fusion.1
  77.1 0.7 bitcast_dynamic-update-slice_fusion
  77.9 2.9 %fusion.46 = f32[2048,512]{0,1:T(8,128)S(1)} fusion(bf16[2048,512]{1,0:T(8,128)(2,1)} %bitcast.23, bf16[512,512]{1,0:T(8,128)(2,1)S(1)} %bitcast.144), kind=kOutput, calls=%fused_computation.102 | convolution fusion | flops 1073741824 | bytes 6815744 | tf_op jit(solution)/shard_map/dot_general | solution.py:462
  81.2 0.3 copy-done.8
  81.5 0.2 fusion.7
  81.8 0.3 fusion.2
  82.1 0.8 convolution_bitcast_fusion
  82.9 1.2 collective-permute-start.14
  84.1 3.7 %collective-permute-done.14 = f32[8,1,4096]{2,0,1:T(8,128)S(1)} collective-permute-done((f32[8,1,4096]{2,0,1:T(8,128)S(1)}, f32[8,1,4096]{2,0,1:T(8,128)S(1)}, u32[]{:S(2)}, u32[]{:S(2)}) %collective-permute-start.14) | collective-permute-done | bytes 131104 | tf_op jit(solution)/shard_map/ppermute | solution.py:116
  87.9 1.5 %collective-permute-start.15 = (f32[8,1,4096]{2,0,1:T(8,128)S(1)}, f32[8,1,4096]{2,0,1:T(8,128)S(1)}, u32[]{:S(2)}, u32[]{:S(2)}) collective-permute-start(f32[8,1,4096]{2,0,1:T(8,128)S(1)} %add.190), channel_id=1, source_target_pairs={{0,2},{1,3},{2,0},{3,1},{4,6},{5,7},{6,4},{7,5},{8,10},{9,11},{10,... | collective-permute-start | bytes 393224 | tf_op jit(solution)/shard_map/ppermute | solution.py:116
  89.4 3.5 %collective-permute-done.15 = f32[8,1,4096]{2,0,1:T(8,128)S(1)} collective-permute-done((f32[8,1,4096]{2,0,1:T(8,128)S(1)}, f32[8,1,4096]{2,0,1:T(8,128)S(1)}, u32[]{:S(2)}, u32[]{:S(2)}) %collective-permute-start.15) | collective-permute-done | bytes 131104 | tf_op jit(solution)/shard_map/ppermute | solution.py:116
  92.9 2.4 %collective-permute-start.16 = (f32[8,1,4096]{2,0,1:T(8,128)S(1)}, f32[8,1,4096]{2,0,1:T(8,128)S(1)}, u32[]{:S(2)}, u32[]{:S(2)}) collective-permute-start(f32[8,1,4096]{2,0,1:T(8,128)S(1)} %add.191), channel_id=1, source_target_pairs={{0,4},{1,5},{2,6},{3,7},{4,0},{5,1},{6,2},{7,3},{8,12},{9,13},{10,... | collective-permute-start | bytes 393224 | tf_op jit(solution)/shard_map/ppermute | solution.py:116
  95.4 4.9 %collective-permute-done.16 = f32[8,1,4096]{2,0,1:T(8,128)S(1)} collective-permute-done((f32[8,1,4096]{2,0,1:T(8,128)S(1)}, f32[8,1,4096]{2,0,1:T(8,128)S(1)}, u32[]{:S(2)}, u32[]{:S(2)}) %collective-permute-start.16) | collective-permute-done | bytes 131104 | tf_op jit(solution)/shard_map/ppermute | solution.py:116
  100.5 0.7 fusion.32.rows_ref
  101.2 12.4 %shard_map.190 = f32[8,4096]{1,0:T(8,128)} custom-call(bf16[8,4096]{1,0:T(8,128)(2,1)} %fusion.32.rows_ref, bf16[896,4096]{1,0:T(8,128)(2,1)} %bitcast.139, bf16[896,4096]{1,0:T(8,128)(2,1)} %bitcast.140, bf16[896,4096]{1,0:T(8,128)(2,1)} %bitcast.141), custom_call_target="tpu_custom_call" | custom-call | tf_op jit(solution)/shard_map/pallas_call | solution.py:384
  113.6 1.0 reshape_reshape.4
  114.7 1.3 %collective-permute-start.17 = (f32[2,2,1,1,4096]{4,2,1,0,3:T(1,128)S(1)}, f32[2,2,1,1,4096]{4,2,1,0,3:T(1,128)S(1)}, u32[]{:S(2)}, u32[]{:S(2)}) collective-permute-start(f32[2,2,1,1,4096]{4,2,1,0,3:T(1,128)S(1)} %constant_dynamic-slice_fusion.1), channel_id=1, source_target_pairs={{0,1},{1,0},{2,3},{3,2},{4,5},{5,4},{6,7},{7,6},{8,9},{9,8},{10,11... | collective-permute-start | bytes 196616 | tf_op jit(solution)/shard_map/ppermute | solution.py:505
  116.0 3.0 %collective-permute-done.17 = f32[2,2,1,1,4096]{4,2,1,0,3:T(1,128)S(1)} collective-permute-done((f32[2,2,1,1,4096]{4,2,1,0,3:T(1,128)S(1)}, f32[2,2,1,1,4096]{4,2,1,0,3:T(1,128)S(1)}, u32[]{:S(2)}, u32[]{:S(2)}) %collective-permute-start.17) | collective-permute-done | bytes 65568 | tf_op jit(solution)/shard_map/ppermute | solution.py:505
  119.1 0.5 collective-permute-start.18
  119.6 3.5 %collective-permute-done.18 = f32[2,1,1,1,4096]{4,2,1,0,3:T(1,128)S(1)} collective-permute-done((f32[2,1,1,1,4096]{4,2,1,0,3:T(1,128)S(1)}, f32[2,1,1,1,4096]{4,2,1,0,3:T(1,128)S(1)}, u32[]{:S(2)}, u32[]{:S(2)}) %collective-permute-start.18) | collective-permute-done | bytes 32800 | tf_op jit(solution)/shard_map/ppermute | solution.py:505
  123.3 2.8 %collective-permute-start.19 = (f32[1,4096]{1,0:T(1,128)S(1)}, f32[1,4096]{1,0:T(1,128)S(1)}, u32[]{:S(2)}, u32[]{:S(2)}) collective-permute-start(f32[1,4096]{1,0:T(1,128)S(1)} %bitcast_add_fusion), channel_id=1, source_target_pairs={{0,8},{1,9},{2,10},{3,11},{4,12},{5,13},{6,14},{7,15},{8,16},{9,17... | collective-permute-start | bytes 49160 | tf_op jit(solution)/shard_map/ppermute | solution.py:521
  126.1 2.1 %collective-permute-done.20 = f32[1,4096]{1,0:T(1,128)S(1)} collective-permute-done((f32[1,4096]{1,0:T(1,128)S(1)}, f32[1,4096]{1,0:T(1,128)S(1)}, u32[]{:S(2)}, u32[]{:S(2)}) %collective-permute-start.20) | collective-permute-done | bytes 16416 | tf_op jit(solution)/shard_map/ppermute | solution.py:522
  128.2 0.6 convert_bitcast_fusion
  (79 shorter events, 1.9 us)
Async XLA Ops:
  0.0 82.1 %copy-start = (bf16[1,256,4096]{2,1,0:T(8,128)(2,1)S(1)}, bf16[1,256,4096]{2,1,0:T(8,128)(2,1)}, u32[]{:S(2)}) copy-start(bf16[1,256,4096]{2,1,0:T(8,128)(2,1)} %param.29) | copy-start | bytes 6291460
  2.5 22.9 %collective-permute-start = (bf16[136,512]{1,0:T(8,128)(2,1)}, bf16[136,512]{1,0:T(8,128)(2,1)}, u32[]{:S(2)}, u32[]{:S(2)}) collective-permute-start(bf16[136,512]{1,0:T(8,128)(2,1)} %pad_maximum_fusion), channel_id=1, source_target_pairs={{0,2},{2,4},{4,6},{6,7},{7,5},{5,3},{3,1},{1,0},{8,10},{10,12},{12... | collective-permute-start | bytes 417800 | tf_op jit(solution)/shard_map/ppermute | solution.py:151
  5.5 21.9 %collective-permute-start.4 = (bf16[136,512]{1,0:T(8,128)(2,1)}, bf16[136,512]{1,0:T(8,128)(2,1)S(1)}, u32[]{:S(2)}, u32[]{:S(2)}) collective-permute-start(bf16[136,512]{1,0:T(8,128)(2,1)} %pad_maximum_fusion), channel_id=1, source_target_pairs={{0,1},{2,0},{4,2},{6,4},{7,6},{5,7},{3,5},{1,3},{8,9},{10,8},{12,1... | collective-permute-start | bytes 417800 | tf_op jit(solution)/shard_map/ppermute | solution.py:155
  5.5 9.1 %copy-start.13 = (s32[8]{0:T(128)S(1)}, s32[8]{0:T(128)}, u32[]{:S(2)}) copy-start(s32[8]{0:T(128)} %constant.120.clone) | copy-start | bytes 100
  5.5 9.7 %copy-start.12 = (s32[8]{0:T(128)S(1)}, s32[8]{0:T(128)}, u32[]{:S(2)}) copy-start(s32[8]{0:T(128)} %constant.122.clone) | copy-start | bytes 100
  5.5 10.3 %copy-start.1 = (s32[8]{0:T(128)S(1)}, s32[8]{0:T(128)}, u32[]{:S(2)}) copy-start(s32[8]{0:T(128)} %constant.121.clone) | copy-start | bytes 100
  6.7 10.5 %copy-start.10 = (f32[1,128]{1,0:T(1,128)S(1)}, f32[1,128]{1,0:T(1,128)}, u32[]{:S(2)}) copy-start(f32[1,128]{1,0:T(1,128)} %param.25) | copy-start | bytes 1540
  6.8 11.0 %copy-start.11 = (f32[1,128]{1,0:T(1,128)S(1)}, f32[1,128]{1,0:T(1,128)}, u32[]{:S(2)}) copy-start(f32[1,128]{1,0:T(1,128)} %param.26) | copy-start | bytes 1540
  6.8 11.6 %copy-start.9 = (s32[8]{0:T(128)S(1)}, s32[8]{0:T(128)}, u32[]{:S(2)}) copy-start(s32[8]{0:T(128)} %param.23) | copy-start | bytes 100
  6.8 11.7 %copy-start.6 = (s32[8,256]{1,0:T(8,128)S(1)}, s32[8,256]{1,0:T(8,128)}, u32[]{:S(2)}) copy-start(s32[8,256]{1,0:T(8,128)} %param.22) | copy-start | bytes 24580
  6.8 14.9 %copy-start.2 = (bf16[1,256,1024]{2,1,0:T(8,128)(2,1)S(1)}, bf16[1,256,1024]{2,1,0:T(8,128)(2,1)}, u32[]{:S(2)}) copy-start(bf16[1,256,1024]{2,1,0:T(8,128)(2,1)} %param.21) | copy-start | bytes 1572868
  8.3 69.5 %all-to-all-start = ((bf16[8,64,512]{2,1,0:T(8,128)(2,1)}), bf16[8,64,512]{2,1,0:T(8,128)(2,1)S(1)}, u32[]{:S(2)}, u32[]{:S(2)}) async-start(bf16[8,64,512]{2,1,0:T(8,128)(2,1)} %reshape.224), calls=%async_computation | async-start | bytes 1048576 | tf_op jit(solution)/shard_map/all_to_all | solution.py:451
  14.6 10.8 %copy-start.3 = (bf16[1,128,512]{2,1,0:T(8,128)(2,1)S(1)}, bf16[1,128,512]{2,1,0:T(8,128)(2,1)}, u32[]{:S(2)}) copy-start(bf16[1,128,512]{2,1,0:T(8,128)(2,1)} %param.27) | copy-start | bytes 393220
  25.4 16.3 %copy-start.4 = (bf16[8,256,128]{2,1,0:T(8,128)(2,1)S(1)}, bf16[8,256,128]{2,1,0:T(8,128)(2,1)}, u32[]{:S(2)}) copy-start(bf16[8,256,128]{2,1,0:T(8,128)(2,1)} %gather_fusion.2) | copy-start | bytes 1572868
  25.4 5.3 %collective-permute-start.1 = (bf16[136,512]{1,0:T(8,128)(2,1)}, bf16[136,512]{1,0:T(8,128)(2,1)S(1)}, u32[]{:S(2)}, u32[]{:S(2)}) collective-permute-start(bf16[136,512]{1,0:T(8,128)(2,1)} %collective-permute-done), channel_id=1, source_target_pairs={{0,2},{2,4},{4,6},{6,7},{7,5},{5,3},{3,1},{1,0},{8,10},{10,12},{12... | collective-permute-start | bytes 417800 | tf_op jit(solution)/shard_map/ppermute | solution.py:151
  27.5 5.3 %collective-permute-start.5 = (bf16[136,512]{1,0:T(8,128)(2,1)S(1)}, bf16[136,512]{1,0:T(8,128)(2,1)S(1)}, u32[]{:S(2)}, u32[]{:S(2)}) collective-permute-start(bf16[136,512]{1,0:T(8,128)(2,1)S(1)} %collective-permute-done.4), channel_id=1, source_target_pairs={{0,1},{2,0},{4,2},{6,4},{7,6},{5,7},{3,5},{1,3},{8,9},{10,8},{12,1... | collective-permute-start | bytes 417800 | tf_op jit(solution)/shard_map/ppermute | solution.py:155
  30.7 5.6 %collective-permute-start.2 = (bf16[136,512]{1,0:T(8,128)(2,1)S(1)}, bf16[136,512]{1,0:T(8,128)(2,1)S(1)}, u32[]{:S(2)}, u32[]{:S(2)}) collective-permute-start(bf16[136,512]{1,0:T(8,128)(2,1)S(1)} %collective-permute-done.1), channel_id=1, source_target_pairs={{0,2},{2,4},{4,6},{6,7},{7,5},{5,3},{3,1},{1,0},{8,10},{10,12},{12... | collective-permute-start | bytes 417800 | tf_op jit(solution)/shard_map/ppermute | solution.py:151
  32.7 8.9 %collective-permute-start.6 = (bf16[136,512]{1,0:T(8,128)(2,1)S(1)}, bf16[136,512]{1,0:T(8,128)(2,1)S(1)}, u32[]{:S(2)}, u32[]{:S(2)}) collective-permute-start(bf16[136,512]{1,0:T(8,128)(2,1)S(1)} %collective-permute-done.5), channel_id=1, source_target_pairs={{0,1},{2,0},{4,2},{6,4},{7,6},{5,7},{3,5},{1,3},{8,9},{10,8},{12,1... | collective-permute-start | bytes 417800 | tf_op jit(solution)/shard_map/ppermute | solution.py:155
  36.4 5.2 %collective-permute-start.3 = (bf16[136,512]{1,0:T(8,128)(2,1)S(1)}, bf16[136,512]{1,0:T(8,128)(2,1)S(1)}, u32[]{:S(2)}, u32[]{:S(2)}) collective-permute-start(bf16[136,512]{1,0:T(8,128)(2,1)S(1)} %collective-permute-done.2), channel_id=1, source_target_pairs={{0,2},{2,4},{4,6},{6,7},{7,5},{5,3},{3,1},{1,0},{8,10},{10,12},{12... | collective-permute-start | bytes 417800 | tf_op jit(solution)/shard_map/ppermute | solution.py:151
  43.1 9.3 %collective-permute-start.7 = (bf16[256,512]{1,0:T(8,128)(2,1)}, bf16[256,512]{1,0:T(8,128)(2,1)S(1)}, u32[]{:S(2)}, u32[]{:S(2)}) collective-permute-start(bf16[256,512]{1,0:T(8,128)(2,1)} %get-tuple-element.10), channel_id=1, source_target_pairs={{0,2},{2,4},{4,6},{6,7},{7,5},{5,3},{3,1},{1,0},{8,10},{10,12},{12... | collective-permute-start | bytes 786440 | tf_op jit(solution)/shard_map/ppermute | solution.py:151
  45.6 17.2 %collective-permute-start.11 = (bf16[256,512]{1,0:T(8,128)(2,1)}, bf16[256,512]{1,0:T(8,128)(2,1)S(1)}, u32[]{:S(2)}, u32[]{:S(2)}) collective-permute-start(bf16[256,512]{1,0:T(8,128)(2,1)} %get-tuple-element.10), channel_id=1, source_target_pairs={{0,1},{2,0},{4,2},{6,4},{7,6},{5,7},{3,5},{1,3},{8,9},{10,8},{12,1... | collective-permute-start | bytes 786440 | tf_op jit(solution)/shard_map/ppermute | solution.py:155
  52.4 8.4 %collective-permute-start.8 = (bf16[256,512]{1,0:T(8,128)(2,1)S(1)}, bf16[256,512]{1,0:T(8,128)(2,1)S(1)}, u32[]{:S(2)}, u32[]{:S(2)}) collective-permute-start(bf16[256,512]{1,0:T(8,128)(2,1)S(1)} %collective-permute-done.7), channel_id=1, source_target_pairs={{0,2},{2,4},{4,6},{6,7},{7,5},{5,3},{3,1},{1,0},{8,10},{10,12},{12... | collective-permute-start | bytes 786440 | tf_op jit(solution)/shard_map/ppermute | solution.py:151
  60.8 7.6 %collective-permute-start.9 = (bf16[256,512]{1,0:T(8,128)(2,1)S(1)}, bf16[256,512]{1,0:T(8,128)(2,1)S(1)}, u32[]{:S(2)}, u32[]{:S(2)}) collective-permute-start(bf16[256,512]{1,0:T(8,128)(2,1)S(1)} %collective-permute-done.8), channel_id=1, source_target_pairs={{0,2},{2,4},{4,6},{6,7},{7,5},{5,3},{3,1},{1,0},{8,10},{10,12},{12... | collective-permute-start | bytes 786440 | tf_op jit(solution)/shard_map/ppermute | solution.py:151
  62.8 7.9 %collective-permute-start.12 = (bf16[256,512]{1,0:T(8,128)(2,1)S(1)}, bf16[256,512]{1,0:T(8,128)(2,1)S(1)}, u32[]{:S(2)}, u32[]{:S(2)}) collective-permute-start(bf16[256,512]{1,0:T(8,128)(2,1)S(1)} %collective-permute-done.11), channel_id=1, source_target_pairs={{0,1},{2,0},{4,2},{6,4},{7,6},{5,7},{3,5},{1,3},{8,9},{10,8},{12,1... | collective-permute-start | bytes 786440 | tf_op jit(solution)/shard_map/ppermute | solution.py:155
  68.4 6.4 %collective-permute-start.10 = (bf16[256,512]{1,0:T(8,128)(2,1)S(1)}, bf16[256,512]{1,0:T(8,128)(2,1)S(1)}, u32[]{:S(2)}, u32[]{:S(2)}) collective-permute-start(bf16[256,512]{1,0:T(8,128)(2,1)S(1)} %collective-permute-done.9), channel_id=1, source_target_pairs={{0,2},{2,4},{4,6},{6,7},{7,5},{5,3},{3,1},{1,0},{8,10},{10,12},{12... | collective-permute-start | bytes 786440 | tf_op jit(solution)/shard_map/ppermute | solution.py:151
  70.8 6.4 %collective-permute-start.13 = (bf16[256,512]{1,0:T(8,128)(2,1)S(1)}, bf16[256,512]{1,0:T(8,128)(2,1)S(1)}, u32[]{:S(2)}, u32[]{:S(2)}) collective-permute-start(bf16[256,512]{1,0:T(8,128)(2,1)S(1)} %collective-permute-done.12), channel_id=1, source_target_pairs={{0,1},{2,0},{4,2},{6,4},{7,6},{5,7},{3,5},{1,3},{8,9},{10,8},{12,1... | collective-permute-start | bytes 786440 | tf_op jit(solution)/shard_map/ppermute | solution.py:155
  80.8 0.7 copy-start.8
  81.1 0.6 copy-start.7
  82.1 18.4 %copy-start.5 = (f32[1,4096]{1,0:T(1,128)S(1)}, f32[1,4096]{1,0:T(1,128)}, u32[]{:S(2)}) copy-start(f32[1,4096]{1,0:T(1,128)} %param.30) | copy-start | bytes 49156
  82.9 5.0 %collective-permute-start.14 = (f32[8,1,4096]{2,0,1:T(8,128)S(1)}, f32[8,1,4096]{2,0,1:T(8,128)S(1)}, u32[]{:S(2)}, u32[]{:S(2)}) collective-permute-start(f32[8,1,4096]{2,0,1:T(8,128)S(1)} %convolution_bitcast_fusion), channel_id=1, source_target_pairs={{0,1},{1,0},{2,3},{3,2},{4,5},{5,4},{6,7},{7,6},{8,9},{9,8},{10,11... | collective-permute-start | bytes 393224 | tf_op jit(solution)/shard_map/ppermute | solution.py:116
  87.9 5.0 %collective-permute-start.15 = (f32[8,1,4096]{2,0,1:T(8,128)S(1)}, f32[8,1,4096]{2,0,1:T(8,128)S(1)}, u32[]{:S(2)}, u32[]{:S(2)}) collective-permute-start(f32[8,1,4096]{2,0,1:T(8,128)S(1)} %add.190), channel_id=1, source_target_pairs={{0,2},{1,3},{2,0},{3,1},{4,6},{5,7},{6,4},{7,5},{8,10},{9,11},{10,... | collective-permute-start | bytes 393224 | tf_op jit(solution)/shard_map/ppermute | solution.py:116
  92.9 7.3 %collective-permute-start.16 = (f32[8,1,4096]{2,0,1:T(8,128)S(1)}, f32[8,1,4096]{2,0,1:T(8,128)S(1)}, u32[]{:S(2)}, u32[]{:S(2)}) collective-permute-start(f32[8,1,4096]{2,0,1:T(8,128)S(1)} %add.191), channel_id=1, source_target_pairs={{0,4},{1,5},{2,6},{3,7},{4,0},{5,1},{6,2},{7,3},{8,12},{9,13},{10,... | collective-permute-start | bytes 393224 | tf_op jit(solution)/shard_map/ppermute | solution.py:116
  114.7 4.3 %collective-permute-start.17 = (f32[2,2,1,1,4096]{4,2,1,0,3:T(1,128)S(1)}, f32[2,2,1,1,4096]{4,2,1,0,3:T(1,128)S(1)}, u32[]{:S(2)}, u32[]{:S(2)}) collective-permute-start(f32[2,2,1,1,4096]{4,2,1,0,3:T(1,128)S(1)} %constant_dynamic-slice_fusion.1), channel_id=1, source_target_pairs={{0,1},{1,0},{2,3},{3,2},{4,5},{5,4},{6,7},{7,6},{8,9},{9,8},{10,11... | collective-permute-start | bytes 196616 | tf_op jit(solution)/shard_map/ppermute | solution.py:505
  119.1 4.0 %collective-permute-start.18 = (f32[2,1,1,1,4096]{4,2,1,0,3:T(1,128)S(1)}, f32[2,1,1,1,4096]{4,2,1,0,3:T(1,128)S(1)}, u32[]{:S(2)}, u32[]{:S(2)}) collective-permute-start(f32[2,1,1,1,4096]{4,2,1,0,3:T(1,128)S(1)} %constant_dynamic-slice_fusion), channel_id=1, source_target_pairs={{0,2},{1,3},{2,0},{3,1},{4,6},{5,7},{6,4},{7,5},{8,10},{9,11},{10,... | collective-permute-start | bytes 98312 | tf_op jit(solution)/shard_map/ppermute | solution.py:505
  123.2 5.0 %collective-permute-start.20 = (f32[1,4096]{1,0:T(1,128)S(1)}, f32[1,4096]{1,0:T(1,128)S(1)}, u32[]{:S(2)}, u32[]{:S(2)}) collective-permute-start(f32[1,4096]{1,0:T(1,128)S(1)} %dynamic-slice_bitcast_fusion), channel_id=1, source_target_pairs={{0,12},{1,13},{2,14},{3,15},{4,8},{5,9},{6,10},{7,11},{8,20},{9,21... | collective-permute-start | bytes 49160 | tf_op jit(solution)/shard_map/ppermute | solution.py:522
  123.3 5.0 %collective-permute-start.19 = (f32[1,4096]{1,0:T(1,128)S(1)}, f32[1,4096]{1,0:T(1,128)S(1)}, u32[]{:S(2)}, u32[]{:S(2)}) collective-permute-start(f32[1,4096]{1,0:T(1,128)S(1)} %bitcast_add_fusion), channel_id=1, source_target_pairs={{0,8},{1,9},{2,10},{3,11},{4,12},{5,13},{6,14},{7,15},{8,16},{9,17... | collective-permute-start | bytes 49160 | tf_op jit(solution)/shard_map/ppermute | solution.py:521

commit v10 on v9

--- a/solution.py
+++ b/solution.py
@@ -396,6 +396,17 @@
     )(rows, gate, up, down)
 
 
+class DirectGather:
+    def __init__(self, value, count, me):
+        self.slots = [value] + [
+            lax.ppermute(value, "site", shift_pairs(count, steps)) for steps in range(1, count)
+        ]
+        self.sources = (me - jnp.arange(count, dtype=jnp.int32)) % count
+
+    def finish(self):
+        return jnp.stack(self.slots), self.sources
+
+
 def heads_split(
     acts,
     patches,
@@ -426,7 +437,7 @@
     all_sites = group_size * sites_here
 
     act_rows = sites_here * model_width // hidden_width
-    ring_in = RingGather(
+    ring_in = DirectGather(
         jnp.concatenate([tile_in[0], current.reshape(act_rows, hidden_width)], axis=0),
         group_size,
         my_index,

time: 129 us -> 132 us (1.023)
  waiting for transfers between devices: 47.1 us -> 34.6 us
  starting transfers between devices: 34.8 us -> 47.2 us
  local copies, waits for them, and re-layouts: 17.1 us -> 20.9 us
    ppermute x0 -> x7, starting transfers between devices: none -> 16.5 us  [__init__(): lax.ppermute(value, 'site', shift_pairs(count, steps))]
    ppermute x8 -> x4, waiting for transfers between devices: 26.1 us -> 14.7 us  [_issue(): self.ahead = lax.ppermute(self.ahead, 'site', self.forward)]
    ppermute x8 -> x4, starting transfers between devices: 18.1 us -> 8.32 us  [_issue(): self.ahead = lax.ppermute(self.ahead, 'site', self.forward)]
    ppermute x0 -> x7, waiting for transfers between devices: none -> 4.04 us  [__init__(): lax.ppermute(value, 'site', shift_pairs(count, steps))]
    unnamed x44, local copies, waits for them, and re-layouts: 7.91 us -> 11.7 us
    ppermute x3, waiting for transfers between devices: 12.1 us -> 8.91 us  [doubling_sum(): state = state + lax.ppermute(state, 'site', xor_pairs(count, bit))]
    ppermute x2, starting transfers between devices: 1.78 us -> 4.56 us  [last_round(): state = keep + lax.ppermute(send, 'site', xor_pairs(group_size, bit))]
    ppermute x6 -> x3, starting transfers between devices: 0.53 us -> 2.59 us  [_issue(): self.behind = lax.ppermute(self.behind, 'site', self.backward)]
  transfers between devices with their start and end apart: 22 -> 22, of which waited for: 14 -> 12; matrix products, arithmetic and copies ran while one was open for 19% -> 21% of each run, Pallas kernels for 0% -> 0%
where the time goes in v10:
time: 132 us
  starting transfers between devices  47.2 us (36%)
  waiting for transfers between devices  34.6 us (26%)
  local copies, waits for them, and re-layouts  20.9 us (16%)
  Pallas kernels  12.4 us (9%)
  other arithmetic  8.74 us (7%)
  matrix products  7.73 us (6%)
    ppermute x7, starting transfers between devices, __init__(): lax.ppermute(value, 'site', shift_pairs(count, steps))  16.5 us
    ppermute x4, waiting for transfers between devices, _issue(): self.ahead = lax.ppermute(self.ahead, 'site', self.forward)  14.7 us
    pallas_call x1, Pallas kernels, gated_ffn(): pl.pallas_call(ffn_block, grid=(units // block,), in_specs=[pl.BlockSpec(...  12.4 us
    unnamed x44, local copies, waits for them, and re-layouts  11.7 us
    ppermute x3, waiting for transfers between devices, doubling_sum(): state = state + lax.ppermute(state, 'site', xor_pairs(count, bit))  8.91 us
    ppermute x4, starting transfers between devices, _issue(): self.ahead = lax.ppermute(self.ahead, 'site', self.forward)  8.32 us
    ppermute x3, starting transfers between devices, doubling_sum(): state = state + lax.ppermute(state, 'site', xor_pairs(count, bit))  7.21 us
    ppermute x2, waiting for transfers between devices, last_round(): state = keep + lax.ppermute(send, 'site', xor_pairs(group_size, bit))  5.16 us
  transfers between devices with their start and end apart: 22, of which 12 were waited for; matrix products, arithmetic and copies ran while one was open for 21% of the time, Pallas kernels for 0%

profile of v10, /device:TPU:0, one launch (start us, length us, event | category | flops | bytes accessed | tf_op | source)
XLA Modules:
  0.0 131.9 jit_solution(16060274732816192621)
XLA Ops:
  0.0 0.9 reduce.19
  0.9 0.9 pad_maximum_fusion
  1.9 5.1 %collective-permute-start.5 = (bf16[136,512]{1,0:T(8,128)(2,1)S(1)}, bf16[136,512]{1,0:T(8,128)(2,1)}, u32[]{:S(2)}, u32[]{:S(2)}) collective-permute-start(bf16[136,512]{1,0:T(8,128)(2,1)S(1)} %pad_maximum_fusion), channel_id=1, source_target_pairs={{0,6},{1,7},{2,0},{3,1},{4,2},{5,3},{6,4},{7,5},{8,14},{9,15},{10,... | collective-permute-start | bytes 417800 | tf_op jit(solution)/shard_map/ppermute | solution.py:402
  7.3 3.5 %collective-permute-start.3 = (bf16[136,512]{1,0:T(8,128)(2,1)S(1)}, bf16[136,512]{1,0:T(8,128)(2,1)}, u32[]{:S(2)}, u32[]{:S(2)}) collective-permute-start(bf16[136,512]{1,0:T(8,128)(2,1)S(1)} %pad_maximum_fusion), channel_id=1, source_target_pairs={{0,4},{1,5},{2,6},{3,7},{4,0},{5,1},{6,2},{7,3},{8,12},{9,13},{10,... | collective-permute-start | bytes 417800 | tf_op jit(solution)/shard_map/ppermute | solution.py:402
  10.8 1.5 %collective-permute-start = (bf16[136,512]{1,0:T(8,128)(2,1)S(1)}, bf16[136,512]{1,0:T(8,128)(2,1)}, u32[]{:S(2)}, u32[]{:S(2)}) collective-permute-start(bf16[136,512]{1,0:T(8,128)(2,1)S(1)} %pad_maximum_fusion), channel_id=1, source_target_pairs={{0,1},{1,2},{2,3},{3,4},{4,5},{5,6},{6,7},{7,0},{8,9},{9,10},{10,1... | collective-permute-start | bytes 417800 | tf_op jit(solution)/shard_map/ppermute | solution.py:402
  12.3 1.2 copy.35
  14.0 1.1 reshape.274
  15.1 4.5 %all-to-all-start = ((bf16[8,64,512]{2,1,0:T(8,128)(2,1)}), bf16[8,64,512]{2,1,0:T(8,128)(2,1)S(1)}, u32[]{:S(2)}, u32[]{:S(2)}) async-start(bf16[8,64,512]{2,1,0:T(8,128)(2,1)} %reshape.274), calls=%async_computation | async-start | bytes 1048576 | tf_op jit(solution)/shard_map/all_to_all | solution.py:462
  19.7 0.6 dynamic_slice.28
  20.3 0.7 compare_select_fusion
  20.9 0.6 iota_reduce_fusion
  21.6 0.6 broadcast_bitcast_fusion
  22.2 0.6 broadcast_bitcast_fusion.1
  22.8 0.6 gather_fusion.2
  23.6 3.1 %convert_reduce_fusion = f32[8,2048]{1,0:T(8,128)S(1)} fusion(s32[2048]{0:T(1024)S(1)} %bitcast.150, s32[8,256]{1,0:T(8,128)S(1)} %copy-done.6, pred[8,256]{1,0:T(8,128)(4,1)S(1)} %iota_compare_fusion), kind=kLoop, calls=%fused_computation.3 | loop fusion | flops 16760832 | bytes 83968 | tf_op jit(solution)/shard_map/reduce_sum | solution.py:486
  26.8 1.0 copy.28
  27.8 1.3 copy.29
  29.1 1.4 %gather_fusion.1 = bf16[8,256,128]{2,1,0:T(8,128)(2,1)} fusion(bf16[256,8,128]{2,0,1:T(8,128)(2,1)S(1)} %copy.29, s32[1024]{0:T(1024)S(1)} %pad_clamp_fusion.1), kind=kCustom, calls=%fused_computation.1 | custom fusion | bytes 1048608 | tf_op jit(solution)/shard_map/jit(_take)/gather | solution.py:452
  30.5 2.1 %collective-permute-start.1 = (bf16[136,512]{1,0:T(8,128)(2,1)S(1)}, bf16[136,512]{1,0:T(8,128)(2,1)S(1)}, u32[]{:S(2)}, u32[]{:S(2)}) collective-permute-start(bf16[136,512]{1,0:T(8,128)(2,1)S(1)} %pad_maximum_fusion), channel_id=1, source_target_pairs={{0,2},{1,3},{2,4},{3,5},{4,6},{5,7},{6,0},{7,1},{8,10},{9,11},{10,... | collective-permute-start | bytes 417800 | tf_op jit(solution)/shard_map/ppermute | solution.py:402
  32.6 0.9 bitcast_dynamic-update-slice_fusion.14
  33.5 4.0 %collective-permute-done.1 = bf16[136,512]{1,0:T(8,128)(2,1)S(1)} collective-permute-done((bf16[136,512]{1,0:T(8,128)(2,1)S(1)}, bf16[136,512]{1,0:T(8,128)(2,1)S(1)}, u32[]{:S(2)}, u32[]{:S(2)}) %collective-permute-start.1) | collective-permute-done | bytes 139296 | tf_op jit(solution)/shard_map/ppermute | solution.py:402
  37.5 4.0 %collective-permute-start.6 = (bf16[136,512]{1,0:T(8,128)(2,1)S(1)}, bf16[136,512]{1,0:T(8,128)(2,1)S(1)}, u32[]{:S(2)}, u32[]{:S(2)}) collective-permute-start(bf16[136,512]{1,0:T(8,128)(2,1)S(1)} %pad_maximum_fusion), channel_id=1, source_target_pairs={{0,7},{1,0},{2,1},{3,2},{4,3},{5,4},{6,5},{7,6},{8,15},{9,8},{10,9... | collective-permute-start | bytes 417800 | tf_op jit(solution)/shard_map/ppermute | solution.py:402
  41.5 0.9 bitcast_dynamic-update-slice_fusion.12
  42.5 0.9 bitcast_dynamic-update-slice_fusion.11
  43.4 0.9 bitcast_dynamic-update-slice_fusion.10
  44.3 0.9 bitcast_dynamic-update-slice_fusion.9
  45.3 1.4 %bitcast_dynamic-update-slice_fusion.7 = (bf16[8,256,512]{2,1,0:T(8,128)(2,1)}, bf16[256,512]{1,0:T(8,128)(2,1)}) fusion(bf16[8,136,512]{2,1,0:T(8,128)(2,1)S(1)} %bitcast_dynamic-update-slice_fusion.8, bf16[8,256,128]{2,1,0:T(8,128)(2,1)S(1)} %copy-done.4, pred[8]{0:T(512)(128)(4,1)S(1)} %compare_and_fusion), kind=kOutput, calls=%fused_computation.44 | convolution fusion | flops 269877248 | bytes 2097664 | tf_op jit(solution)/shard_map/dot_general | solution.py:454
  46.7 3.5 %collective-permute-start.7 = (bf16[256,512]{1,0:T(8,128)(2,1)}, bf16[256,512]{1,0:T(8,128)(2,1)S(1)}, u32[]{:S(2)}, u32[]{:S(2)}) collective-permute-start(bf16[256,512]{1,0:T(8,128)(2,1)} %get-tuple-element.10), channel_id=1, source_target_pairs={{0,2},{2,4},{4,6},{6,7},{7,5},{5,3},{3,1},{1,0},{8,10},{10,12},{12... | collective-permute-start | bytes 786440 | tf_op jit(solution)/shard_map/ppermute | solution.py:151
  50.4 0.6 gather_fusion
  51.0 4.7 %collective-permute-done.7 = bf16[256,512]{1,0:T(8,128)(2,1)S(1)} collective-permute-done((bf16[256,512]{1,0:T(8,128)(2,1)}, bf16[256,512]{1,0:T(8,128)(2,1)S(1)}, u32[]{:S(2)}, u32[]{:S(2)}) %collective-permute-start.7) | collective-permute-done | bytes 262176 | tf_op jit(solution)/shard_map/ppermute | solution.py:151
  55.8 2.5 %collective-permute-start.8 = (bf16[256,512]{1,0:T(8,128)(2,1)S(1)}, bf16[256,512]{1,0:T(8,128)(2,1)S(1)}, u32[]{:S(2)}, u32[]{:S(2)}) collective-permute-start(bf16[256,512]{1,0:T(8,128)(2,1)S(1)} %collective-permute-done.7), channel_id=1, source_target_pairs={{0,2},{2,4},{4,6},{6,7},{7,5},{5,3},{3,1},{1,0},{8,10},{10,12},{12... | collective-permute-start | bytes 786440 | tf_op jit(solution)/shard_map/ppermute | solution.py:151
  58.2 2.3 %bitcast_reduce_fusion.1 = (f32[8,2]{0,1:T(2,128)S(1)}, f32[8,256]{1,0:T(8,128)S(1)}) fusion(bf16[8,4096]{1,0:T(8,128)(2,1)S(1)} %bitcast.149, bf16[1,256,4096]{2,1,0:T(8,128)(2,1)} %param.21), kind=kOutput, calls=%fused_computation.71 | convolution fusion | flops 16785392 | bytes 2170944 | tf_op jit(solution)/shard_map/dot_general | solution.py:23
  60.5 3.2 %collective-permute-done.8 = bf16[256,512]{1,0:T(8,128)(2,1)S(1)} collective-permute-done((bf16[256,512]{1,0:T(8,128)(2,1)S(1)}, bf16[256,512]{1,0:T(8,128)(2,1)S(1)}, u32[]{:S(2)}, u32[]{:S(2)}) %collective-permute-start.8) | collective-permute-done | bytes 262176 | tf_op jit(solution)/shard_map/ppermute | solution.py:151
  63.8 1.2 collective-permute-start.9
  65.0 1.4 %collective-permute-start.12 = (bf16[256,512]{1,0:T(8,128)(2,1)S(1)}, bf16[256,512]{1,0:T(8,128)(2,1)S(1)}, u32[]{:S(2)}, u32[]{:S(2)}) collective-permute-start(bf16[256,512]{1,0:T(8,128)(2,1)S(1)} %collective-permute-done.11), channel_id=1, source_target_pairs={{0,1},{2,0},{4,2},{6,4},{7,6},{5,7},{3,5},{1,3},{8,9},{10,8},{12,1... | collective-permute-start | bytes 786440 | tf_op jit(solution)/shard_map/ppermute | solution.py:155
  66.3 0.7 bitcast_dynamic-update-slice_fusion.6
  67.0 3.9 %collective-permute-done.9 = bf16[256,512]{1,0:T(8,128)(2,1)S(1)} collective-permute-done((bf16[256,512]{1,0:T(8,128)(2,1)S(1)}, bf16[256,512]{1,0:T(8,128)(2,1)S(1)}, u32[]{:S(2)}, u32[]{:S(2)}) %collective-permute-start.9) | collective-permute-done | bytes 262176 | tf_op jit(solution)/shard_map/ppermute | solution.py:151
  70.9 1.1 collective-permute-start.10
  72.0 0.7 bitcast_dynamic-update-slice_fusion.5
  72.7 1.2 collective-permute-start.13
  73.9 0.7 bitcast_dynamic-update-slice_fusion.4
  74.7 2.9 %collective-permute-done.10 = bf16[256,512]{1,0:T(8,128)(2,1)S(1)} collective-permute-done((bf16[256,512]{1,0:T(8,128)(2,1)S(1)}, bf16[256,512]{1,0:T(8,128)(2,1)S(1)}, u32[]{:S(2)}, u32[]{:S(2)}) %collective-permute-start.10) | collective-permute-done | bytes 262176 | tf_op jit(solution)/shard_map/ppermute | solution.py:151
  77.6 0.7 bitcast_dynamic-update-slice_fusion.3
  78.3 0.7 bitcast_dynamic-update-slice_fusion.2
  79.0 0.7 bitcast_dynamic-update-slice_fusion.1
  79.8 0.8 bitcast_dynamic-update-slice_fusion
  80.5 2.9 %fusion.48 = f32[2048,512]{0,1:T(8,128)S(1)} fusion(bf16[2048,512]{1,0:T(8,128)(2,1)} %bitcast.21, bf16[512,512]{1,0:T(8,128)(2,1)S(1)} %bitcast.142), kind=kOutput, calls=%fused_computation.110 | convolution fusion | flops 1073741824 | bytes 6815744 | tf_op jit(solution)/shard_map/dot_general | solution.py:473
  84.8 0.8 convolution_bitcast_fusion
  85.6 2.0 %collective-permute-start.14 = (f32[8,1,4096]{2,0,1:T(8,128)S(1)}, f32[8,1,4096]{2,0,1:T(8,128)S(1)}, u32[]{:S(2)}, u32[]{:S(2)}) collective-permute-start(f32[8,1,4096]{2,0,1:T(8,128)S(1)} %convolution_bitcast_fusion), channel_id=1, source_target_pairs={{0,1},{1,0},{2,3},{3,2},{4,5},{5,4},{6,7},{7,6},{8,9},{9,8},{10,11... | collective-permute-start | bytes 393224 | tf_op jit(solution)/shard_map/ppermute | solution.py:116
  87.6 2.9 %collective-permute-done.14 = f32[8,1,4096]{2,0,1:T(8,128)S(1)} collective-permute-done((f32[8,1,4096]{2,0,1:T(8,128)S(1)}, f32[8,1,4096]{2,0,1:T(8,128)S(1)}, u32[]{:S(2)}, u32[]{:S(2)}) %collective-permute-start.14) | collective-permute-done | bytes 131104 | tf_op jit(solution)/shard_map/ppermute | solution.py:116
  90.6 2.1 %collective-permute-start.15 = (f32[8,1,4096]{2,0,1:T(8,128)S(1)}, f32[8,1,4096]{2,0,1:T(8,128)S(1)}, u32[]{:S(2)}, u32[]{:S(2)}) collective-permute-start(f32[8,1,4096]{2,0,1:T(8,128)S(1)} %add.193), channel_id=1, source_target_pairs={{0,2},{1,3},{2,0},{3,1},{4,6},{5,7},{6,4},{7,5},{8,10},{9,11},{10,... | collective-permute-start | bytes 393224 | tf_op jit(solution)/shard_map/ppermute | solution.py:116
  92.6 3.1 %collective-permute-done.15 = f32[8,1,4096]{2,0,1:T(8,128)S(1)} collective-permute-done((f32[8,1,4096]{2,0,1:T(8,128)S(1)}, f32[8,1,4096]{2,0,1:T(8,128)S(1)}, u32[]{:S(2)}, u32[]{:S(2)}) %collective-permute-start.15) | collective-permute-done | bytes 131104 | tf_op jit(solution)/shard_map/ppermute | solution.py:116
  95.7 3.1 %collective-permute-start.16 = (f32[8,1,4096]{2,0,1:T(8,128)S(1)}, f32[8,1,4096]{2,0,1:T(8,128)S(1)}, u32[]{:S(2)}, u32[]{:S(2)}) collective-permute-start(f32[8,1,4096]{2,0,1:T(8,128)S(1)} %add.194), channel_id=1, source_target_pairs={{0,4},{1,5},{2,6},{3,7},{4,0},{5,1},{6,2},{7,3},{8,12},{9,13},{10,... | collective-permute-start | bytes 393224 | tf_op jit(solution)/shard_map/ppermute | solution.py:116
  98.9 2.9 %collective-permute-done.16 = f32[8,1,4096]{2,0,1:T(8,128)S(1)} collective-permute-done((f32[8,1,4096]{2,0,1:T(8,128)S(1)}, f32[8,1,4096]{2,0,1:T(8,128)S(1)}, u32[]{:S(2)}, u32[]{:S(2)}) %collective-permute-start.16) | collective-permute-done | bytes 131104 | tf_op jit(solution)/shard_map/ppermute | solution.py:116
  102.0 0.7 fusion.32.rows_ref
  102.7 12.4 %shard_map.163 = f32[8,4096]{1,0:T(8,128)} custom-call(bf16[8,4096]{1,0:T(8,128)(2,1)} %fusion.32.rows_ref, bf16[896,4096]{1,0:T(8,128)(2,1)} %bitcast.137, bf16[896,4096]{1,0:T(8,128)(2,1)} %bitcast.138, bf16[896,4096]{1,0:T(8,128)(2,1)} %bitcast.139), custom_call_target="tpu_custom_call" | custom-call | tf_op jit(solution)/shard_map/pallas_call | solution.py:384
  115.1 1.0 reshape_reshape.4
  116.2 3.5 %collective-permute-start.17 = (f32[2,2,1,1,4096]{4,2,1,0,3:T(1,128)S(1)}, f32[2,2,1,1,4096]{4,2,1,0,3:T(1,128)S(1)}, u32[]{:S(2)}, u32[]{:S(2)}) collective-permute-start(f32[2,2,1,1,4096]{4,2,1,0,3:T(1,128)S(1)} %constant_dynamic-slice_fusion.1), channel_id=1, source_target_pairs={{0,1},{1,0},{2,3},{3,2},{4,5},{5,4},{6,7},{7,6},{8,9},{9,8},{10,11... | collective-permute-start | bytes 196616 | tf_op jit(solution)/shard_map/ppermute | solution.py:516
  119.7 2.2 %collective-permute-done.17 = f32[2,2,1,1,4096]{4,2,1,0,3:T(1,128)S(1)} collective-permute-done((f32[2,2,1,1,4096]{4,2,1,0,3:T(1,128)S(1)}, f32[2,2,1,1,4096]{4,2,1,0,3:T(1,128)S(1)}, u32[]{:S(2)}, u32[]{:S(2)}) %collective-permute-start.17) | collective-permute-done | bytes 65568 | tf_op jit(solution)/shard_map/ppermute | solution.py:516
  122.0 1.1 collective-permute-start.18
  123.1 2.9 %collective-permute-done.18 = f32[2,1,1,1,4096]{4,2,1,0,3:T(1,128)S(1)} collective-permute-done((f32[2,1,1,1,4096]{4,2,1,0,3:T(1,128)S(1)}, f32[2,1,1,1,4096]{4,2,1,0,3:T(1,128)S(1)}, u32[]{:S(2)}, u32[]{:S(2)}) %collective-permute-start.18) | collective-permute-done | bytes 32800 | tf_op jit(solution)/shard_map/ppermute | solution.py:516
  126.1 3.4 %collective-permute-start.19 = (f32[1,4096]{1,0:T(1,128)S(1)}, f32[1,4096]{1,0:T(1,128)S(1)}, u32[]{:S(2)}, u32[]{:S(2)}) collective-permute-start(f32[1,4096]{1,0:T(1,128)S(1)} %bitcast_add_fusion), channel_id=1, source_target_pairs={{0,8},{1,9},{2,10},{3,11},{4,12},{5,13},{6,14},{7,15},{8,16},{9,17... | collective-permute-start | bytes 49160 | tf_op jit(solution)/shard_map/ppermute | solution.py:532
  129.6 1.6 %collective-permute-done.20 = f32[1,4096]{1,0:T(1,128)S(1)} collective-permute-done((f32[1,4096]{1,0:T(1,128)S(1)}, f32[1,4096]{1,0:T(1,128)S(1)}, u32[]{:S(2)}, u32[]{:S(2)}) %collective-permute-start.20) | collective-permute-done | bytes 16416 | tf_op jit(solution)/shard_map/ppermute | solution.py:533
  131.3 0.6 convert_bitcast_fusion
  (79 shorter events, 3.2 us)
Async XLA Ops:
  0.0 84.8 %copy-start = (bf16[1,256,4096]{2,1,0:T(8,128)(2,1)S(1)}, bf16[1,256,4096]{2,1,0:T(8,128)(2,1)}, u32[]{:S(2)}) copy-start(bf16[1,256,4096]{2,1,0:T(8,128)(2,1)} %param.26) | copy-start | bytes 6291460
  1.9 42.5 %collective-permute-start.5 = (bf16[136,512]{1,0:T(8,128)(2,1)S(1)}, bf16[136,512]{1,0:T(8,128)(2,1)}, u32[]{:S(2)}, u32[]{:S(2)}) collective-permute-start(bf16[136,512]{1,0:T(8,128)(2,1)S(1)} %pad_maximum_fusion), channel_id=1, source_target_pairs={{0,6},{1,7},{2,0},{3,1},{4,2},{5,3},{6,4},{7,5},{8,14},{9,15},{10,... | collective-permute-start | bytes 417800 | tf_op jit(solution)/shard_map/ppermute | solution.py:402
  7.0 36.4 %collective-permute-start.4 = (bf16[136,512]{1,0:T(8,128)(2,1)S(1)}, bf16[136,512]{1,0:T(8,128)(2,1)}, u32[]{:S(2)}, u32[]{:S(2)}) collective-permute-start(bf16[136,512]{1,0:T(8,128)(2,1)S(1)} %pad_maximum_fusion), channel_id=1, source_target_pairs={{0,5},{1,6},{2,7},{3,0},{4,1},{5,2},{6,3},{7,4},{8,13},{9,14},{10,... | collective-permute-start | bytes 417800 | tf_op jit(solution)/shard_map/ppermute | solution.py:402
  7.3 35.1 %collective-permute-start.3 = (bf16[136,512]{1,0:T(8,128)(2,1)S(1)}, bf16[136,512]{1,0:T(8,128)(2,1)}, u32[]{:S(2)}, u32[]{:S(2)}) collective-permute-start(bf16[136,512]{1,0:T(8,128)(2,1)S(1)} %pad_maximum_fusion), channel_id=1, source_target_pairs={{0,4},{1,5},{2,6},{3,7},{4,0},{5,1},{6,2},{7,3},{8,12},{9,13},{10,... | collective-permute-start | bytes 417800 | tf_op jit(solution)/shard_map/ppermute | solution.py:402
  10.8 30.7 %collective-permute-start.2 = (bf16[136,512]{1,0:T(8,128)(2,1)S(1)}, bf16[136,512]{1,0:T(8,128)(2,1)}, u32[]{:S(2)}, u32[]{:S(2)}) collective-permute-start(bf16[136,512]{1,0:T(8,128)(2,1)S(1)} %pad_maximum_fusion), channel_id=1, source_target_pairs={{0,3},{1,4},{2,5},{3,6},{4,7},{5,0},{6,1},{7,2},{8,11},{9,12},{10,... | collective-permute-start | bytes 417800 | tf_op jit(solution)/shard_map/ppermute | solution.py:402
  10.8 19.7 %collective-permute-start = (bf16[136,512]{1,0:T(8,128)(2,1)S(1)}, bf16[136,512]{1,0:T(8,128)(2,1)}, u32[]{:S(2)}, u32[]{:S(2)}) collective-permute-start(bf16[136,512]{1,0:T(8,128)(2,1)S(1)} %pad_maximum_fusion), channel_id=1, source_target_pairs={{0,1},{1,2},{2,3},{3,4},{4,5},{5,6},{6,7},{7,0},{8,9},{9,10},{10,1... | collective-permute-start | bytes 417800 | tf_op jit(solution)/shard_map/ppermute | solution.py:402
  12.3 7.4 %copy-start.13 = (s32[8]{0:T(128)S(1)}, s32[8]{0:T(128)}, u32[]{:S(2)}) copy-start(s32[8]{0:T(128)} %constant.124.clone) | copy-start | bytes 100
  12.3 8.0 %copy-start.10 = (s32[8]{0:T(128)S(1)}, s32[8]{0:T(128)}, u32[]{:S(2)}) copy-start(s32[8]{0:T(128)} %constant.126.clone) | copy-start | bytes 100
  12.3 9.3 %copy-start.11 = (f32[1,128]{1,0:T(1,128)S(1)}, f32[1,128]{1,0:T(1,128)}, u32[]{:S(2)}) copy-start(f32[1,128]{1,0:T(1,128)} %param.22) | copy-start | bytes 1540
  12.3 9.9 %copy-start.12 = (f32[1,128]{1,0:T(1,128)S(1)}, f32[1,128]{1,0:T(1,128)}, u32[]{:S(2)}) copy-start(f32[1,128]{1,0:T(1,128)} %param.23) | copy-start | bytes 1540
  12.3 10.4 %copy-start.9 = (s32[8]{0:T(128)S(1)}, s32[8]{0:T(128)}, u32[]{:S(2)}) copy-start(s32[8]{0:T(128)} %param.20) | copy-start | bytes 100
  12.3 10.5 %copy-start.1 = (s32[8]{0:T(128)S(1)}, s32[8]{0:T(128)}, u32[]{:S(2)}) copy-start(s32[8]{0:T(128)} %constant.125.clone) | copy-start | bytes 100
  13.5 10.0 %copy-start.6 = (s32[8,256]{1,0:T(8,128)S(1)}, s32[8,256]{1,0:T(8,128)}, u32[]{:S(2)}) copy-start(s32[8,256]{1,0:T(8,128)} %param.19) | copy-start | bytes 24580
  13.5 13.2 %copy-start.2 = (bf16[1,256,1024]{2,1,0:T(8,128)(2,1)S(1)}, bf16[1,256,1024]{2,1,0:T(8,128)(2,1)}, u32[]{:S(2)}) copy-start(bf16[1,256,1024]{2,1,0:T(8,128)(2,1)} %param.18) | copy-start | bytes 1572868
  15.1 65.4 %all-to-all-start = ((bf16[8,64,512]{2,1,0:T(8,128)(2,1)}), bf16[8,64,512]{2,1,0:T(8,128)(2,1)S(1)}, u32[]{:S(2)}, u32[]{:S(2)}) async-start(bf16[8,64,512]{2,1,0:T(8,128)(2,1)} %reshape.274), calls=%async_computation | async-start | bytes 1048576 | tf_op jit(solution)/shard_map/all_to_all | solution.py:462
  19.6 10.9 %copy-start.3 = (bf16[1,128,512]{2,1,0:T(8,128)(2,1)S(1)}, bf16[1,128,512]{2,1,0:T(8,128)(2,1)}, u32[]{:S(2)}) copy-start(bf16[1,128,512]{2,1,0:T(8,128)(2,1)} %param.24) | copy-start | bytes 393220
  30.5 14.8 %copy-start.4 = (bf16[8,256,128]{2,1,0:T(8,128)(2,1)S(1)}, bf16[8,256,128]{2,1,0:T(8,128)(2,1)}, u32[]{:S(2)}) copy-start(bf16[8,256,128]{2,1,0:T(8,128)(2,1)} %gather_fusion.1) | copy-start | bytes 1572868
  30.5 7.0 %collective-permute-start.1 = (bf16[136,512]{1,0:T(8,128)(2,1)S(1)}, bf16[136,512]{1,0:T(8,128)(2,1)S(1)}, u32[]{:S(2)}, u32[]{:S(2)}) collective-permute-start(bf16[136,512]{1,0:T(8,128)(2,1)S(1)} %pad_maximum_fusion), channel_id=1, source_target_pairs={{0,2},{1,3},{2,4},{3,5},{4,6},{5,7},{6,0},{7,1},{8,10},{9,11},{10,... | collective-permute-start | bytes 417800 | tf_op jit(solution)/shard_map/ppermute | solution.py:402
  37.5 7.7 %collective-permute-start.6 = (bf16[136,512]{1,0:T(8,128)(2,1)S(1)}, bf16[136,512]{1,0:T(8,128)(2,1)S(1)}, u32[]{:S(2)}, u32[]{:S(2)}) collective-permute-start(bf16[136,512]{1,0:T(8,128)(2,1)S(1)} %pad_maximum_fusion), channel_id=1, source_target_pairs={{0,7},{1,0},{2,1},{3,2},{4,3},{5,4},{6,5},{7,6},{8,15},{9,8},{10,9... | collective-permute-start | bytes 417800 | tf_op jit(solution)/shard_map/ppermute | solution.py:402
  46.7 9.0 %collective-permute-start.7 = (bf16[256,512]{1,0:T(8,128)(2,1)}, bf16[256,512]{1,0:T(8,128)(2,1)S(1)}, u32[]{:S(2)}, u32[]{:S(2)}) collective-permute-start(bf16[256,512]{1,0:T(8,128)(2,1)} %get-tuple-element.10), channel_id=1, source_target_pairs={{0,2},{2,4},{4,6},{6,7},{7,5},{5,3},{3,1},{1,0},{8,10},{10,12},{12... | collective-permute-start | bytes 786440 | tf_op jit(solution)/shard_map/ppermute | solution.py:151
  50.3 14.7 %collective-permute-start.11 = (bf16[256,512]{1,0:T(8,128)(2,1)}, bf16[256,512]{1,0:T(8,128)(2,1)S(1)}, u32[]{:S(2)}, u32[]{:S(2)}) collective-permute-start(bf16[256,512]{1,0:T(8,128)(2,1)} %get-tuple-element.10), channel_id=1, source_target_pairs={{0,1},{2,0},{4,2},{6,4},{7,6},{5,7},{3,5},{1,3},{8,9},{10,8},{12,1... | collective-permute-start | bytes 786440 | tf_op jit(solution)/shard_map/ppermute | solution.py:155
  55.8 8.0 %collective-permute-start.8 = (bf16[256,512]{1,0:T(8,128)(2,1)S(1)}, bf16[256,512]{1,0:T(8,128)(2,1)S(1)}, u32[]{:S(2)}, u32[]{:S(2)}) collective-permute-start(bf16[256,512]{1,0:T(8,128)(2,1)S(1)} %collective-permute-done.7), channel_id=1, source_target_pairs={{0,2},{2,4},{4,6},{6,7},{7,5},{5,3},{3,1},{1,0},{8,10},{10,12},{12... | collective-permute-start | bytes 786440 | tf_op jit(solution)/shard_map/ppermute | solution.py:151
  63.8 7.2 %collective-permute-start.9 = (bf16[256,512]{1,0:T(8,128)(2,1)S(1)}, bf16[256,512]{1,0:T(8,128)(2,1)S(1)}, u32[]{:S(2)}, u32[]{:S(2)}) collective-permute-start(bf16[256,512]{1,0:T(8,128)(2,1)S(1)} %collective-permute-done.8), channel_id=1, source_target_pairs={{0,2},{2,4},{4,6},{6,7},{7,5},{5,3},{3,1},{1,0},{8,10},{10,12},{12... | collective-permute-start | bytes 786440 | tf_op jit(solution)/shard_map/ppermute | solution.py:151
  65.0 7.8 %collective-permute-start.12 = (bf16[256,512]{1,0:T(8,128)(2,1)S(1)}, bf16[256,512]{1,0:T(8,128)(2,1)S(1)}, u32[]{:S(2)}, u32[]{:S(2)}) collective-permute-start(bf16[256,512]{1,0:T(8,128)(2,1)S(1)} %collective-permute-done.11), channel_id=1, source_target_pairs={{0,1},{2,0},{4,2},{6,4},{7,6},{5,7},{3,5},{1,3},{8,9},{10,8},{12,1... | collective-permute-start | bytes 786440 | tf_op jit(solution)/shard_map/ppermute | solution.py:155
  70.9 6.6 %collective-permute-start.10 = (bf16[256,512]{1,0:T(8,128)(2,1)S(1)}, bf16[256,512]{1,0:T(8,128)(2,1)S(1)}, u32[]{:S(2)}, u32[]{:S(2)}) collective-permute-start(bf16[256,512]{1,0:T(8,128)(2,1)S(1)} %collective-permute-done.9), channel_id=1, source_target_pairs={{0,2},{2,4},{4,6},{6,7},{7,5},{5,3},{3,1},{1,0},{8,10},{10,12},{12... | collective-permute-start | bytes 786440 | tf_op jit(solution)/shard_map/ppermute | solution.py:151
  72.7 7.0 %collective-permute-start.13 = (bf16[256,512]{1,0:T(8,128)(2,1)S(1)}, bf16[256,512]{1,0:T(8,128)(2,1)S(1)}, u32[]{:S(2)}, u32[]{:S(2)}) collective-permute-start(bf16[256,512]{1,0:T(8,128)(2,1)S(1)} %collective-permute-done.12), channel_id=1, source_target_pairs={{0,1},{2,0},{4,2},{6,4},{7,6},{5,7},{3,5},{1,3},{8,9},{10,8},{12,1... | collective-permute-start | bytes 786440 | tf_op jit(solution)/shard_map/ppermute | solution.py:155
  83.4 0.7 copy-start.8
  83.8 0.7 copy-start.7
  84.8 17.2 %copy-start.5 = (f32[1,4096]{1,0:T(1,128)S(1)}, f32[1,4096]{1,0:T(1,128)}, u32[]{:S(2)}) copy-start(f32[1,4096]{1,0:T(1,128)} %param.27) | copy-start | bytes 49156
  85.6 5.0 %collective-permute-start.14 = (f32[8,1,4096]{2,0,1:T(8,128)S(1)}, f32[8,1,4096]{2,0,1:T(8,128)S(1)}, u32[]{:S(2)}, u32[]{:S(2)}) collective-permute-start(f32[8,1,4096]{2,0,1:T(8,128)S(1)} %convolution_bitcast_fusion), channel_id=1, source_target_pairs={{0,1},{1,0},{2,3},{3,2},{4,5},{5,4},{6,7},{7,6},{8,9},{9,8},{10,11... | collective-permute-start | bytes 393224 | tf_op jit(solution)/shard_map/ppermute | solution.py:116
  90.6 5.1 %collective-permute-start.15 = (f32[8,1,4096]{2,0,1:T(8,128)S(1)}, f32[8,1,4096]{2,0,1:T(8,128)S(1)}, u32[]{:S(2)}, u32[]{:S(2)}) collective-permute-start(f32[8,1,4096]{2,0,1:T(8,128)S(1)} %add.193), channel_id=1, source_target_pairs={{0,2},{1,3},{2,0},{3,1},{4,6},{5,7},{6,4},{7,5},{8,10},{9,11},{10,... | collective-permute-start | bytes 393224 | tf_op jit(solution)/shard_map/ppermute | solution.py:116
  95.7 6.1 %collective-permute-start.16 = (f32[8,1,4096]{2,0,1:T(8,128)S(1)}, f32[8,1,4096]{2,0,1:T(8,128)S(1)}, u32[]{:S(2)}, u32[]{:S(2)}) collective-permute-start(f32[8,1,4096]{2,0,1:T(8,128)S(1)} %add.194), channel_id=1, source_target_pairs={{0,4},{1,5},{2,6},{3,7},{4,0},{5,1},{6,2},{7,3},{8,12},{9,13},{10,... | collective-permute-start | bytes 393224 | tf_op jit(solution)/shard_map/ppermute | solution.py:116
  116.2 5.7 %collective-permute-start.17 = (f32[2,2,1,1,4096]{4,2,1,0,3:T(1,128)S(1)}, f32[2,2,1,1,4096]{4,2,1,0,3:T(1,128)S(1)}, u32[]{:S(2)}, u32[]{:S(2)}) collective-permute-start(f32[2,2,1,1,4096]{4,2,1,0,3:T(1,128)S(1)} %constant_dynamic-slice_fusion.1), channel_id=1, source_target_pairs={{0,1},{1,0},{2,3},{3,2},{4,5},{5,4},{6,7},{7,6},{8,9},{9,8},{10,11... | collective-permute-start | bytes 196616 | tf_op jit(solution)/shard_map/ppermute | solution.py:516
  122.0 4.0 %collective-permute-start.18 = (f32[2,1,1,1,4096]{4,2,1,0,3:T(1,128)S(1)}, f32[2,1,1,1,4096]{4,2,1,0,3:T(1,128)S(1)}, u32[]{:S(2)}, u32[]{:S(2)}) collective-permute-start(f32[2,1,1,1,4096]{4,2,1,0,3:T(1,128)S(1)} %constant_dynamic-slice_fusion), channel_id=1, source_target_pairs={{0,2},{1,3},{2,0},{3,1},{4,6},{5,7},{6,4},{7,5},{8,10},{9,11},{10,... | collective-permute-start | bytes 98312 | tf_op jit(solution)/shard_map/ppermute | solution.py:516
  126.1 5.1 %collective-permute-start.20 = (f32[1,4096]{1,0:T(1,128)S(1)}, f32[1,4096]{1,0:T(1,128)S(1)}, u32[]{:S(2)}, u32[]{:S(2)}) collective-permute-start(f32[1,4096]{1,0:T(1,128)S(1)} %dynamic-slice_bitcast_fusion), channel_id=1, source_target_pairs={{0,12},{1,13},{2,14},{3,15},{4,8},{5,9},{6,10},{7,11},{8,20},{9,21... | collective-permute-start | bytes 49160 | tf_op jit(solution)/shard_map/ppermute | solution.py:533
  126.1 5.1 %collective-permute-start.19 = (f32[1,4096]{1,0:T(1,128)S(1)}, f32[1,4096]{1,0:T(1,128)S(1)}, u32[]{:S(2)}, u32[]{:S(2)}) collective-permute-start(f32[1,4096]{1,0:T(1,128)S(1)} %bitcast_add_fusion), channel_id=1, source_target_pairs={{0,8},{1,9},{2,10},{3,11},{4,12},{5,13},{6,14},{7,15},{8,16},{9,17... | collective-permute-start | bytes 49160 | tf_op jit(solution)/shard_map/ppermute | solution.py:532

commit v11 on v9

--- a/solution.py
+++ b/solution.py
@@ -433,6 +433,17 @@
     )
     in_slots, in_sources = ring_in.finish()
     in_rows = tile_in.shape[1]
+    kv_width = tile_out.shape[-1]
+    my_cols = heads_here * head_size
+    col_blocks = tile_out[0].reshape(tile_out.shape[1], 2, group_size, my_cols)
+    col_blocks = jnp.transpose(col_blocks, (2, 0, 1, 3)).reshape(group_size, tile_out.shape[1], 2 * my_cols)
+    in_slots, col_blocks, site_tiles, site_count = lax.optimization_barrier(
+        (in_slots, col_blocks, site_tiles, site_count)
+    )
+    weight_out = lax.all_to_all(col_blocks, "site", split_axis=0, concat_axis=0, tiled=True)
+    weight_out = weight_out.reshape(-1, 2 * my_cols)
+    del kv_width
+
     slot_of_source = jnp.argmax(
         in_sources[None, :] == jnp.arange(group_size, dtype=jnp.int32)[:, None], axis=1
     ).astype(jnp.int32)
@@ -443,14 +454,6 @@
         jnp.dot(own_rows.reshape(tiles_here, -1), weight_in, preferred_element_type=jnp.float32),
         approximate=True,
     ).astype(jnp.bfloat16)
-
-    kv_width = tile_out.shape[-1]
-    my_cols = heads_here * head_size
-    col_blocks = tile_out[0].reshape(tile_out.shape[1], 2, group_size, my_cols)
-    col_blocks = jnp.transpose(col_blocks, (2, 0, 1, 3)).reshape(group_size, tile_out.shape[1], 2 * my_cols)
-    weight_out = lax.all_to_all(col_blocks, "site", split_axis=0, concat_axis=0, tiled=True)
-    weight_out = weight_out.reshape(-1, 2 * my_cols)
-    del kv_width
 
     q_part = by_rows(everyone, q_weight[0]).astype(jnp.bfloat16)
     queries = head_norm(q_part, q_gain[0]).astype(jnp.bfloat16)

time: 129 us -> 131 us (1.016)
  other arithmetic: 9.39 us -> 13.3 us
  waiting for transfers between devices: 47.1 us -> 43.2 us
    ppermute x8, waiting for transfers between devices: 26.1 us -> 18.9 us  [_issue(): self.ahead = lax.ppermute(self.ahead, 'site', self.forward)]
    ppermute x8, starting transfers between devices: 18.1 us -> 20.7 us  [_issue(): self.ahead = lax.ppermute(self.ahead, 'site', self.forward)]
    ppermute x2, starting transfers between devices: 1.78 us -> 0.14 us  [last_round(): state = keep + lax.ppermute(send, 'site', xor_pairs(group_size, bit))]
    ppermute x2, waiting for transfers between devices: 6.53 us -> 8.14 us  [last_round(): state = keep + lax.ppermute(send, 'site', xor_pairs(group_size, bit))]
    mul x2, local copies, waits for them, and re-layouts: 1.11 us -> 2.44 us  [head_norm(): shaped * lax.rsqrt(jnp.mean(shaped * shaped, axis=-1, keepdims=True) + ep...]
    unnamed x44 -> x38, local copies, waits for them, and re-layouts: 7.91 us -> 7.82 us
  transfers between devices with their start and end apart: 22 -> 22, of which waited for: 14 -> 13; matrix products, arithmetic and copies ran while one was open for 19% -> 21% of each run, Pallas kernels for 0% -> 0%
where the time goes in v11:
time: 131 us; the launch traced here: 130 us
  waiting for transfers between devices  43.2 us (33%)
  starting transfers between devices  35.2 us (27%)
  local copies, waits for them, and re-layouts  18.1 us (14%)
  other arithmetic  13.3 us (10%)
  Pallas kernels  12.4 us (9%)
  matrix products  7.7 us (6%)
    ppermute x8, starting transfers between devices, _issue(): self.ahead = lax.ppermute(self.ahead, 'site', self.forward)  20.7 us
    ppermute x8, waiting for transfers between devices, _issue(): self.ahead = lax.ppermute(self.ahead, 'site', self.forward)  18.9 us
    pallas_call x1, Pallas kernels, gated_ffn(): pl.pallas_call(ffn_block, grid=(units // block,), in_specs=[pl.BlockSpec(...  12.4 us
    ppermute x3, waiting for transfers between devices, doubling_sum(): state = state + lax.ppermute(state, 'site', xor_pairs(count, bit))  12.1 us
    ppermute x2, waiting for transfers between devices, last_round(): state = keep + lax.ppermute(send, 'site', xor_pairs(group_size, bit))  8.14 us
    unnamed x38, local copies, waits for them, and re-layouts  7.82 us
    all_to_all x1, starting transfers between devices, heads_split(): lax.all_to_all(col_blocks, 'site', split_axis=0, concat_axis=0, tiled=True)  6.25 us
    ppermute x3, starting transfers between devices, doubling_sum(): state = state + lax.ppermute(state, 'site', xor_pairs(count, bit))  5.97 us
  transfers between devices with their start and end apart: 22, of which 13 were waited for; matrix products, arithmetic and copies ran while one was open for 21% of the time, Pallas kernels for 0%

profile of v11, /device:TPU:0, one launch (start us, length us, event | category | flops | bytes accessed | tf_op | source)
XLA Modules:
  0.0 130.4 jit_solution(6428269028739826016)
XLA Ops:
  0.0 0.9 reduce.19
  1.0 1.6 %pad_maximum_fusion = bf16[136,512]{1,0:T(8,128)(2,1)} fusion(bf16[8,512]{1,0:T(8,128)(2,1)S(1)} %reshape_squeeze.9, bf16[128,512]{1,0:T(8,128)(2,1)} %bitcast.149), kind=kLoop, calls=%fused_computation.46 | loop fusion | flops 278528 | bytes 278528 | tf_op jit(solution)/shard_map/concatenate | solution.py:430
  2.5 3.0 %collective-permute-start = (bf16[136,512]{1,0:T(8,128)(2,1)}, bf16[136,512]{1,0:T(8,128)(2,1)S(1)}, u32[]{:S(2)}, u32[]{:S(2)}) collective-permute-start(bf16[136,512]{1,0:T(8,128)(2,1)} %pad_maximum_fusion), channel_id=1, source_target_pairs={{0,2},{2,4},{4,6},{6,7},{7,5},{5,3},{3,1},{1,0},{8,10},{10,12},{12... | collective-permute-start | bytes 417800 | tf_op jit(solution)/shard_map/ppermute | solution.py:151
  5.5 1.3 %dynamic_slice.31 = s32[1]{0:T(128)} dynamic-slice(s32[8]{0:T(128)} %constant.120.clone, s32[]{:T(128)S(6)} %select_n.96), dynamic_slice_sizes={1} | dynamic-slice | bytes 12 | tf_op jit(solution)/shard_map/dynamic_slice | solution.py:138
  6.9 1.4 %compare_select_fusion.3 = s32[8]{0:T(128)S(1)} fusion(s32[8]{0:T(128)} %constant.122.clone, s32[]{:T(128)} %bitcast), kind=kLoop, calls=%fused_computation.85 | loop fusion | flops 120 | bytes 68 | tf_op jit(solution)/shard_map/select_n | solution.py:139
  8.2 1.3 gather_fusion
  9.5 0.7 iota_reduce_fusion
  10.3 0.6 compare_and_fusion
  10.9 1.2 broadcast_bitcast_fusion
  12.1 1.2 broadcast_bitcast_fusion.1
  13.3 0.6 pad_clamp_fusion.1
  14.0 0.6 pad_clamp_fusion
  14.6 0.6 copy.40
  15.2 1.2 copy.32
  16.7 1.2 copy.38
  17.9 0.4 copy.42
  18.3 1.1 reshape.223
  19.4 0.8 gather_fusion.2
  20.2 0.7 bitcast_dynamic-update-slice_fusion.15
  20.9 2.1 %collective-permute-start.1 = (bf16[136,512]{1,0:T(8,128)(2,1)S(1)}, bf16[136,512]{1,0:T(8,128)(2,1)S(1)}, u32[]{:S(2)}, u32[]{:S(2)}) collective-permute-start(bf16[136,512]{1,0:T(8,128)(2,1)S(1)} %collective-permute-done), channel_id=1, source_target_pairs={{0,2},{2,4},{4,6},{6,7},{7,5},{5,3},{3,1},{1,0},{8,10},{10,12},{12... | collective-permute-start | bytes 417800 | tf_op jit(solution)/shard_map/ppermute | solution.py:151
  23.0 3.1 %collective-permute-done.1 = bf16[136,512]{1,0:T(8,128)(2,1)S(1)} collective-permute-done((bf16[136,512]{1,0:T(8,128)(2,1)S(1)}, bf16[136,512]{1,0:T(8,128)(2,1)S(1)}, u32[]{:S(2)}, u32[]{:S(2)}) %collective-permute-start.1) | collective-permute-done | bytes 139296 | tf_op jit(solution)/shard_map/ppermute | solution.py:151
  26.1 1.9 %collective-permute-start.2 = (bf16[136,512]{1,0:T(8,128)(2,1)S(1)}, bf16[136,512]{1,0:T(8,128)(2,1)S(1)}, u32[]{:S(2)}, u32[]{:S(2)}) collective-permute-start(bf16[136,512]{1,0:T(8,128)(2,1)S(1)} %collective-permute-done.1), channel_id=1, source_target_pairs={{0,2},{2,4},{4,6},{6,7},{7,5},{5,3},{3,1},{1,0},{8,10},{10,12},{12... | collective-permute-start | bytes 417800 | tf_op jit(solution)/shard_map/ppermute | solution.py:151
  28.2 3.0 %collective-permute-done.2 = bf16[136,512]{1,0:T(8,128)(2,1)S(1)} collective-permute-done((bf16[136,512]{1,0:T(8,128)(2,1)S(1)}, bf16[136,512]{1,0:T(8,128)(2,1)S(1)}, u32[]{:S(2)}, u32[]{:S(2)}) %collective-permute-start.2) | collective-permute-done | bytes 139296 | tf_op jit(solution)/shard_map/ppermute | solution.py:151
  31.2 2.4 %collective-permute-start.3 = (bf16[136,512]{1,0:T(8,128)(2,1)S(1)}, bf16[136,512]{1,0:T(8,128)(2,1)S(1)}, u32[]{:S(2)}, u32[]{:S(2)}) collective-permute-start(bf16[136,512]{1,0:T(8,128)(2,1)S(1)} %collective-permute-done.2), channel_id=1, source_target_pairs={{0,2},{2,4},{4,6},{6,7},{7,5},{5,3},{3,1},{1,0},{8,10},{10,12},{12... | collective-permute-start | bytes 417800 | tf_op jit(solution)/shard_map/ppermute | solution.py:151
  33.6 2.9 %collective-permute-done.3 = bf16[136,512]{1,0:T(8,128)(2,1)S(1)} collective-permute-done((bf16[136,512]{1,0:T(8,128)(2,1)S(1)}, bf16[136,512]{1,0:T(8,128)(2,1)S(1)}, u32[]{:S(2)}, u32[]{:S(2)}) %collective-permute-start.3) | collective-permute-done | bytes 139296 | tf_op jit(solution)/shard_map/ppermute | solution.py:151
  36.7 1.4 %bitcast_dynamic-update-slice_fusion.7 = (bf16[8,256,512]{2,1,0:T(8,128)(2,1)}, bf16[256,512]{1,0:T(8,128)(2,1)}) fusion(bf16[8,136,512]{2,1,0:T(8,128)(2,1)S(1)} %bitcast_dynamic-update-slice_fusion.8, bf16[8,256,128]{2,1,0:T(8,128)(2,1)S(1)} %gather_fusion.2, pred[8]{0:T(512)(128)(4,1)S(1)} %copy-done.10), kind=kOutput, calls=%fused_computation.44 | convolution fusion | flops 269877248 | bytes 2097664 | tf_op jit(solution)/shard_map/dot_general | solution.py:454
  38.1 2.1 %collective-permute-start.7 = (bf16[256,512]{1,0:T(8,128)(2,1)}, bf16[256,512]{1,0:T(8,128)(2,1)S(1)}, u32[]{:S(2)}, u32[]{:S(2)}) collective-permute-start(bf16[256,512]{1,0:T(8,128)(2,1)} %get-tuple-element.18), channel_id=1, source_target_pairs={{0,2},{2,4},{4,6},{6,7},{7,5},{5,3},{3,1},{1,0},{8,10},{10,12},{12... | collective-permute-start | bytes 786440 | tf_op jit(solution)/shard_map/ppermute | solution.py:151
  40.2 6.3 %all-to-all-start = ((bf16[8,64,512]{2,1,0:T(8,128)(2,1)}), bf16[8,64,512]{2,1,0:T(8,128)(2,1)S(1)}, u32[]{:S(2)}, u32[]{:S(2)}) async-start(bf16[8,64,512]{2,1,0:T(8,128)(2,1)} %reshape.223), calls=%async_computation | async-start | bytes 1048576 | tf_op jit(solution)/shard_map/all_to_all | solution.py:443
  46.5 0.7 gather_fusion.1
  47.3 3.1 %convert_reduce_fusion = f32[8,2048]{1,0:T(8,128)S(1)} fusion(s32[2048]{0:T(1024)S(1)} %bitcast.152, s32[8,256]{1,0:T(8,128)S(1)} %copy-done.5, pred[8,256]{1,0:T(8,128)(4,1)S(1)} %iota_compare_fusion), kind=kLoop, calls=%fused_computation.3 | loop fusion | flops 16760832 | bytes 83968 | tf_op jit(solution)/shard_map/reduce_sum | solution.py:478
  50.5 2.1 %collective-permute-start.8 = (bf16[256,512]{1,0:T(8,128)(2,1)S(1)}, bf16[256,512]{1,0:T(8,128)(2,1)S(1)}, u32[]{:S(2)}, u32[]{:S(2)}) collective-permute-start(bf16[256,512]{1,0:T(8,128)(2,1)S(1)} %collective-permute-done.7), channel_id=1, source_target_pairs={{0,2},{2,4},{4,6},{6,7},{7,5},{5,3},{3,1},{1,0},{8,10},{10,12},{12... | collective-permute-start | bytes 786440 | tf_op jit(solution)/shard_map/ppermute | solution.py:151
  52.6 2.3 %bitcast_reduce_fusion.1 = (f32[8,2]{0,1:T(2,128)S(1)}, f32[8,256]{1,0:T(8,128)S(1)}) fusion(bf16[8,4096]{1,0:T(8,128)(2,1)S(1)} %bitcast.151, bf16[1,256,4096]{2,1,0:T(8,128)(2,1)} %param.24), kind=kOutput, calls=%fused_computation.71 | convolution fusion | flops 16785392 | bytes 2170944 | tf_op jit(solution)/shard_map/dot_general | solution.py:23
  54.9 3.5 %collective-permute-done.8 = bf16[256,512]{1,0:T(8,128)(2,1)S(1)} collective-permute-done((bf16[256,512]{1,0:T(8,128)(2,1)S(1)}, bf16[256,512]{1,0:T(8,128)(2,1)S(1)}, u32[]{:S(2)}, u32[]{:S(2)}) %collective-permute-start.8) | collective-permute-done | bytes 262176 | tf_op jit(solution)/shard_map/ppermute | solution.py:151
  58.4 4.3 %collective-permute-start.9 = (bf16[256,512]{1,0:T(8,128)(2,1)S(1)}, bf16[256,512]{1,0:T(8,128)(2,1)S(1)}, u32[]{:S(2)}, u32[]{:S(2)}) collective-permute-start(bf16[256,512]{1,0:T(8,128)(2,1)S(1)} %collective-permute-done.8), channel_id=1, source_target_pairs={{0,2},{2,4},{4,6},{6,7},{7,5},{5,3},{3,1},{1,0},{8,10},{10,12},{12... | collective-permute-start | bytes 786440 | tf_op jit(solution)/shard_map/ppermute | solution.py:151
  62.7 0.7 bitcast_dynamic-update-slice_fusion.6
  63.4 3.4 %collective-permute-done.9 = bf16[256,512]{1,0:T(8,128)(2,1)S(1)} collective-permute-done((bf16[256,512]{1,0:T(8,128)(2,1)S(1)}, bf16[256,512]{1,0:T(8,128)(2,1)S(1)}, u32[]{:S(2)}, u32[]{:S(2)}) %collective-permute-start.9) | collective-permute-done | bytes 262176 | tf_op jit(solution)/shard_map/ppermute | solution.py:151
  66.9 2.8 %collective-permute-start.10 = (bf16[256,512]{1,0:T(8,128)(2,1)S(1)}, bf16[256,512]{1,0:T(8,128)(2,1)S(1)}, u32[]{:S(2)}, u32[]{:S(2)}) collective-permute-start(bf16[256,512]{1,0:T(8,128)(2,1)S(1)} %collective-permute-done.9), channel_id=1, source_target_pairs={{0,2},{2,4},{4,6},{6,7},{7,5},{5,3},{3,1},{1,0},{8,10},{10,12},{12... | collective-permute-start | bytes 786440 | tf_op jit(solution)/shard_map/ppermute | solution.py:151
  69.7 0.7 bitcast_dynamic-update-slice_fusion.5
  70.6 0.7 bitcast_dynamic-update-slice_fusion.4
  71.3 2.9 %collective-permute-done.10 = bf16[256,512]{1,0:T(8,128)(2,1)S(1)} collective-permute-done((bf16[256,512]{1,0:T(8,128)(2,1)S(1)}, bf16[256,512]{1,0:T(8,128)(2,1)S(1)}, u32[]{:S(2)}, u32[]{:S(2)}) %collective-permute-start.10) | collective-permute-done | bytes 262176 | tf_op jit(solution)/shard_map/ppermute | solution.py:151
  74.2 0.7 bitcast_dynamic-update-slice_fusion.3
  74.9 0.7 bitcast_dynamic-update-slice_fusion.2
  75.6 0.7 bitcast_dynamic-update-slice_fusion.1
  76.3 0.9 collective-permute-done.13
  77.2 0.7 bitcast_dynamic-update-slice_fusion
  77.9 2.9 %fusion.46 = f32[2048,512]{0,1:T(8,128)S(1)} fusion(bf16[2048,512]{1,0:T(8,128)(2,1)} %bitcast.24, bf16[512,512]{1,0:T(8,128)(2,1)S(1)} %bitcast.144), kind=kOutput, calls=%fused_computation.102 | convolution fusion | flops 1073741824 | bytes 6815744 | tf_op jit(solution)/shard_map/dot_general | solution.py:465
  81.2 0.3 copy-done.8
  81.8 0.3 fusion.2
  82.2 0.8 convolution_bitcast_fusion
  83.0 1.7 %collective-permute-start.14 = (f32[8,1,4096]{2,0,1:T(8,128)S(1)}, f32[8,1,4096]{2,0,1:T(8,128)S(1)}, u32[]{:S(2)}, u32[]{:S(2)}) collective-permute-start(f32[8,1,4096]{2,0,1:T(8,128)S(1)} %convolution_bitcast_fusion), channel_id=1, source_target_pairs={{0,1},{1,0},{2,3},{3,2},{4,5},{5,4},{6,7},{7,6},{8,9},{9,8},{10,11... | collective-permute-start | bytes 393224 | tf_op jit(solution)/shard_map/ppermute | solution.py:116
  84.7 3.3 %collective-permute-done.14 = f32[8,1,4096]{2,0,1:T(8,128)S(1)} collective-permute-done((f32[8,1,4096]{2,0,1:T(8,128)S(1)}, f32[8,1,4096]{2,0,1:T(8,128)S(1)}, u32[]{:S(2)}, u32[]{:S(2)}) %collective-permute-start.14) | collective-permute-done | bytes 131104 | tf_op jit(solution)/shard_map/ppermute | solution.py:116
  87.9 2.1 %collective-permute-start.15 = (f32[8,1,4096]{2,0,1:T(8,128)S(1)}, f32[8,1,4096]{2,0,1:T(8,128)S(1)}, u32[]{:S(2)}, u32[]{:S(2)}) collective-permute-start(f32[8,1,4096]{2,0,1:T(8,128)S(1)} %add.190), channel_id=1, source_target_pairs={{0,2},{1,3},{2,0},{3,1},{4,6},{5,7},{6,4},{7,5},{8,10},{9,11},{10,... | collective-permute-start | bytes 393224 | tf_op jit(solution)/shard_map/ppermute | solution.py:116
  90.0 3.7 %collective-permute-done.15 = f32[8,1,4096]{2,0,1:T(8,128)S(1)} collective-permute-done((f32[8,1,4096]{2,0,1:T(8,128)S(1)}, f32[8,1,4096]{2,0,1:T(8,128)S(1)}, u32[]{:S(2)}, u32[]{:S(2)}) %collective-permute-start.15) | collective-permute-done | bytes 131104 | tf_op jit(solution)/shard_map/ppermute | solution.py:116
  93.8 2.2 %collective-permute-start.16 = (f32[8,1,4096]{2,0,1:T(8,128)S(1)}, f32[8,1,4096]{2,0,1:T(8,128)S(1)}, u32[]{:S(2)}, u32[]{:S(2)}) collective-permute-start(f32[8,1,4096]{2,0,1:T(8,128)S(1)} %add.191), channel_id=1, source_target_pairs={{0,4},{1,5},{2,6},{3,7},{4,0},{5,1},{6,2},{7,3},{8,12},{9,13},{10,... | collective-permute-start | bytes 393224 | tf_op jit(solution)/shard_map/ppermute | solution.py:116
  96.0 5.1 %collective-permute-done.16 = f32[8,1,4096]{2,0,1:T(8,128)S(1)} collective-permute-done((f32[8,1,4096]{2,0,1:T(8,128)S(1)}, f32[8,1,4096]{2,0,1:T(8,128)S(1)}, u32[]{:S(2)}, u32[]{:S(2)}) %collective-permute-start.16) | collective-permute-done | bytes 131104 | tf_op jit(solution)/shard_map/ppermute | solution.py:116
  101.1 0.9 multiply_reduce_fusion
  102.0 0.7 fusion.32.rows_ref
  102.8 12.4 %shard_map.190 = f32[8,4096]{1,0:T(8,128)} custom-call(bf16[8,4096]{1,0:T(8,128)(2,1)} %fusion.32.rows_ref, bf16[896,4096]{1,0:T(8,128)(2,1)} %bitcast.139, bf16[896,4096]{1,0:T(8,128)(2,1)} %bitcast.140, bf16[896,4096]{1,0:T(8,128)(2,1)} %bitcast.141), custom_call_target="tpu_custom_call" | custom-call | tf_op jit(solution)/shard_map/pallas_call | solution.py:384
  115.1 1.0 reshape_reshape.4
  116.3 4.2 %collective-permute-done.17 = f32[2,2,1,1,4096]{4,2,1,0,3:T(1,128)S(1)} collective-permute-done((f32[2,2,1,1,4096]{4,2,1,0,3:T(1,128)S(1)}, f32[2,2,1,1,4096]{4,2,1,0,3:T(1,128)S(1)}, u32[]{:S(2)}, u32[]{:S(2)}) %collective-permute-start.17) | collective-permute-done | bytes 65568 | tf_op jit(solution)/shard_map/ppermute | solution.py:508
  120.7 3.9 %collective-permute-done.18 = f32[2,1,1,1,4096]{4,2,1,0,3:T(1,128)S(1)} collective-permute-done((f32[2,1,1,1,4096]{4,2,1,0,3:T(1,128)S(1)}, f32[2,1,1,1,4096]{4,2,1,0,3:T(1,128)S(1)}, u32[]{:S(2)}, u32[]{:S(2)}) %collective-permute-start.18) | collective-permute-done | bytes 32800 | tf_op jit(solution)/shard_map/ppermute | solution.py:508
  124.8 1.8 %collective-permute-start.19 = (f32[1,4096]{1,0:T(1,128)S(1)}, f32[1,4096]{1,0:T(1,128)S(1)}, u32[]{:S(2)}, u32[]{:S(2)}) collective-permute-start(f32[1,4096]{1,0:T(1,128)S(1)} %bitcast_add_fusion), channel_id=1, source_target_pairs={{0,8},{1,9},{2,10},{3,11},{4,12},{5,13},{6,14},{7,15},{8,16},{9,17... | collective-permute-start | bytes 49160 | tf_op jit(solution)/shard_map/ppermute | solution.py:524
  126.6 3.1 %collective-permute-done.20 = f32[1,4096]{1,0:T(1,128)S(1)} collective-permute-done((f32[1,4096]{1,0:T(1,128)S(1)}, f32[1,4096]{1,0:T(1,128)S(1)}, u32[]{:S(2)}, u32[]{:S(2)}) %collective-permute-start.20) | collective-permute-done | bytes 16416 | tf_op jit(solution)/shard_map/ppermute | solution.py:525
  129.7 0.6 convert_bitcast_fusion
  (72 shorter events, 2.2 us)
Async XLA Ops:
  0.0 82.1 %copy-start = (bf16[1,256,4096]{2,1,0:T(8,128)(2,1)S(1)}, bf16[1,256,4096]{2,1,0:T(8,128)(2,1)}, u32[]{:S(2)}) copy-start(bf16[1,256,4096]{2,1,0:T(8,128)(2,1)} %param.29) | copy-start | bytes 6291460
  0.9 1.6 %copy-start.2 = (bf16[8,512]{1,0:T(8,128)(2,1)}, bf16[8,512]{1,0:T(8,128)(2,1)S(1)}, u32[]{:S(2)}) copy-start(bf16[8,512]{1,0:T(8,128)(2,1)S(1)} %reshape_squeeze.9) | copy-start | bytes 24580
  2.5 18.4 %collective-permute-start = (bf16[136,512]{1,0:T(8,128)(2,1)}, bf16[136,512]{1,0:T(8,128)(2,1)S(1)}, u32[]{:S(2)}, u32[]{:S(2)}) collective-permute-start(bf16[136,512]{1,0:T(8,128)(2,1)} %pad_maximum_fusion), channel_id=1, source_target_pairs={{0,2},{2,4},{4,6},{6,7},{7,5},{5,3},{3,1},{1,0},{8,10},{10,12},{12... | collective-permute-start | bytes 417800 | tf_op jit(solution)/shard_map/ppermute | solution.py:151
  5.5 17.5 %collective-permute-start.4 = (bf16[136,512]{1,0:T(8,128)(2,1)}, bf16[136,512]{1,0:T(8,128)(2,1)S(1)}, u32[]{:S(2)}, u32[]{:S(2)}) collective-permute-start(bf16[136,512]{1,0:T(8,128)(2,1)} %pad_maximum_fusion), channel_id=1, source_target_pairs={{0,1},{2,0},{4,2},{6,4},{7,6},{5,7},{3,5},{1,3},{8,9},{10,8},{12,1... | collective-permute-start | bytes 417800 | tf_op jit(solution)/shard_map/ppermute | solution.py:155
  16.7 3.5 %copy-start.1 = (bf16[1,128,512]{2,1,0:T(8,128)(2,1)S(1)}, bf16[1,128,512]{2,1,0:T(8,128)(2,1)}, u32[]{:S(2)}) copy-start(bf16[1,128,512]{2,1,0:T(8,128)(2,1)} %param.27) | copy-start | bytes 393220
  20.2 16.4 %copy-start.10 = (pred[8]{0:T(512)(128)(4,1)S(1)}, pred[8]{0:T(512)(128)(4,1)}, u32[]{:S(2)}) copy-start(pred[8]{0:T(512)(128)(4,1)} %get-tuple-element.21) | copy-start | bytes 28
  20.9 5.2 %collective-permute-start.1 = (bf16[136,512]{1,0:T(8,128)(2,1)S(1)}, bf16[136,512]{1,0:T(8,128)(2,1)S(1)}, u32[]{:S(2)}, u32[]{:S(2)}) collective-permute-start(bf16[136,512]{1,0:T(8,128)(2,1)S(1)} %collective-permute-done), channel_id=1, source_target_pairs={{0,2},{2,4},{4,6},{6,7},{7,5},{5,3},{3,1},{1,0},{8,10},{10,12},{12... | collective-permute-start | bytes 417800 | tf_op jit(solution)/shard_map/ppermute | solution.py:151
  23.0 5.1 %collective-permute-start.5 = (bf16[136,512]{1,0:T(8,128)(2,1)S(1)}, bf16[136,512]{1,0:T(8,128)(2,1)S(1)}, u32[]{:S(2)}, u32[]{:S(2)}) collective-permute-start(bf16[136,512]{1,0:T(8,128)(2,1)S(1)} %collective-permute-done.4), channel_id=1, source_target_pairs={{0,1},{2,0},{4,2},{6,4},{7,6},{5,7},{3,5},{1,3},{8,9},{10,8},{12,1... | collective-permute-start | bytes 417800 | tf_op jit(solution)/shard_map/ppermute | solution.py:155
  26.1 5.1 %collective-permute-start.2 = (bf16[136,512]{1,0:T(8,128)(2,1)S(1)}, bf16[136,512]{1,0:T(8,128)(2,1)S(1)}, u32[]{:S(2)}, u32[]{:S(2)}) collective-permute-start(bf16[136,512]{1,0:T(8,128)(2,1)S(1)} %collective-permute-done.1), channel_id=1, source_target_pairs={{0,2},{2,4},{4,6},{6,7},{7,5},{5,3},{3,1},{1,0},{8,10},{10,12},{12... | collective-permute-start | bytes 417800 | tf_op jit(solution)/shard_map/ppermute | solution.py:151
  28.1 8.5 %collective-permute-start.6 = (bf16[136,512]{1,0:T(8,128)(2,1)S(1)}, bf16[136,512]{1,0:T(8,128)(2,1)S(1)}, u32[]{:S(2)}, u32[]{:S(2)}) collective-permute-start(bf16[136,512]{1,0:T(8,128)(2,1)S(1)} %collective-permute-done.5), channel_id=1, source_target_pairs={{0,1},{2,0},{4,2},{6,4},{7,6},{5,7},{3,5},{1,3},{8,9},{10,8},{12,1... | collective-permute-start | bytes 417800 | tf_op jit(solution)/shard_map/ppermute | solution.py:155
  31.2 5.3 %collective-permute-start.3 = (bf16[136,512]{1,0:T(8,128)(2,1)S(1)}, bf16[136,512]{1,0:T(8,128)(2,1)S(1)}, u32[]{:S(2)}, u32[]{:S(2)}) collective-permute-start(bf16[136,512]{1,0:T(8,128)(2,1)S(1)} %collective-permute-done.2), channel_id=1, source_target_pairs={{0,2},{2,4},{4,6},{6,7},{7,5},{5,3},{3,1},{1,0},{8,10},{10,12},{12... | collective-permute-start | bytes 417800 | tf_op jit(solution)/shard_map/ppermute | solution.py:151
  36.6 3.6 %copy-start.9 = (s32[8]{0:T(128)S(1)}, s32[8]{0:T(128)}, u32[]{:S(2)}) copy-start(s32[8]{0:T(128)} %param.23) | copy-start | bytes 100
  36.6 10.6 %copy-start.6 = (pred[8]{0:T(512)(128)(4,1)S(1)}, pred[8]{0:T(512)(128)(4,1)}, u32[]{:S(2)}) copy-start(pred[8]{0:T(512)(128)(4,1)} %get-tuple-element.22) | copy-start | bytes 28
  36.6 10.7 %copy-start.3 = (s32[1,2,8,128]{3,1,2,0:T(2,128)S(1)}, s32[1,2,8,128]{3,1,2,0:T(2,128)}, u32[]{:S(2)}) copy-start(s32[1,2,8,128]{3,1,2,0:T(2,128)} %copy.40) | copy-start | bytes 24580
  36.6 10.7 %copy-start.5 = (s32[8,256]{1,0:T(8,128)S(1)}, s32[8,256]{1,0:T(8,128)}, u32[]{:S(2)}) copy-start(s32[8,256]{1,0:T(8,128)} %param.22) | copy-start | bytes 24580
  38.1 12.4 %collective-permute-start.7 = (bf16[256,512]{1,0:T(8,128)(2,1)}, bf16[256,512]{1,0:T(8,128)(2,1)S(1)}, u32[]{:S(2)}, u32[]{:S(2)}) collective-permute-start(bf16[256,512]{1,0:T(8,128)(2,1)} %get-tuple-element.18), channel_id=1, source_target_pairs={{0,2},{2,4},{4,6},{6,7},{7,5},{5,3},{3,1},{1,0},{8,10},{10,12},{12... | collective-permute-start | bytes 786440 | tf_op jit(solution)/shard_map/ppermute | solution.py:151
  40.2 22.5 %collective-permute-start.11 = (bf16[256,512]{1,0:T(8,128)(2,1)}, bf16[256,512]{1,0:T(8,128)(2,1)S(1)}, u32[]{:S(2)}, u32[]{:S(2)}) collective-permute-start(bf16[256,512]{1,0:T(8,128)(2,1)} %get-tuple-element.18), channel_id=1, source_target_pairs={{0,1},{2,0},{4,2},{6,4},{7,6},{5,7},{3,5},{1,3},{8,9},{10,8},{12,1... | collective-permute-start | bytes 786440 | tf_op jit(solution)/shard_map/ppermute | solution.py:155
  40.2 37.7 %all-to-all-start = ((bf16[8,64,512]{2,1,0:T(8,128)(2,1)}), bf16[8,64,512]{2,1,0:T(8,128)(2,1)S(1)}, u32[]{:S(2)}, u32[]{:S(2)}) async-start(bf16[8,64,512]{2,1,0:T(8,128)(2,1)} %reshape.223), calls=%async_computation | async-start | bytes 1048576 | tf_op jit(solution)/shard_map/all_to_all | solution.py:443
  50.5 7.9 %collective-permute-start.8 = (bf16[256,512]{1,0:T(8,128)(2,1)S(1)}, bf16[256,512]{1,0:T(8,128)(2,1)S(1)}, u32[]{:S(2)}, u32[]{:S(2)}) collective-permute-start(bf16[256,512]{1,0:T(8,128)(2,1)S(1)} %collective-permute-done.7), channel_id=1, source_target_pairs={{0,2},{2,4},{4,6},{6,7},{7,5},{5,3},{3,1},{1,0},{8,10},{10,12},{12... | collective-permute-start | bytes 786440 | tf_op jit(solution)/shard_map/ppermute | solution.py:151
  58.4 8.5 %collective-permute-start.9 = (bf16[256,512]{1,0:T(8,128)(2,1)S(1)}, bf16[256,512]{1,0:T(8,128)(2,1)S(1)}, u32[]{:S(2)}, u32[]{:S(2)}) collective-permute-start(bf16[256,512]{1,0:T(8,128)(2,1)S(1)} %collective-permute-done.8), channel_id=1, source_target_pairs={{0,2},{2,4},{4,6},{6,7},{7,5},{5,3},{3,1},{1,0},{8,10},{10,12},{12... | collective-permute-start | bytes 786440 | tf_op jit(solution)/shard_map/ppermute | solution.py:151
  62.7 7.7 %collective-permute-start.12 = (bf16[256,512]{1,0:T(8,128)(2,1)S(1)}, bf16[256,512]{1,0:T(8,128)(2,1)S(1)}, u32[]{:S(2)}, u32[]{:S(2)}) collective-permute-start(bf16[256,512]{1,0:T(8,128)(2,1)S(1)} %collective-permute-done.11), channel_id=1, source_target_pairs={{0,1},{2,0},{4,2},{6,4},{7,6},{5,7},{3,5},{1,3},{8,9},{10,8},{12,1... | collective-permute-start | bytes 786440 | tf_op jit(solution)/shard_map/ppermute | solution.py:155
  66.9 7.3 %collective-permute-start.10 = (bf16[256,512]{1,0:T(8,128)(2,1)S(1)}, bf16[256,512]{1,0:T(8,128)(2,1)S(1)}, u32[]{:S(2)}, u32[]{:S(2)}) collective-permute-start(bf16[256,512]{1,0:T(8,128)(2,1)S(1)} %collective-permute-done.9), channel_id=1, source_target_pairs={{0,2},{2,4},{4,6},{6,7},{7,5},{5,3},{3,1},{1,0},{8,10},{10,12},{12... | collective-permute-start | bytes 786440 | tf_op jit(solution)/shard_map/ppermute | solution.py:151
  70.4 6.8 %collective-permute-start.13 = (bf16[256,512]{1,0:T(8,128)(2,1)S(1)}, bf16[256,512]{1,0:T(8,128)(2,1)S(1)}, u32[]{:S(2)}, u32[]{:S(2)}) collective-permute-start(bf16[256,512]{1,0:T(8,128)(2,1)S(1)} %collective-permute-done.12), channel_id=1, source_target_pairs={{0,1},{2,0},{4,2},{6,4},{7,6},{5,7},{3,5},{1,3},{8,9},{10,8},{12,1... | collective-permute-start | bytes 786440 | tf_op jit(solution)/shard_map/ppermute | solution.py:155
  80.8 0.7 copy-start.8
  81.2 0.6 copy-start.7
  82.1 19.9 %copy-start.4 = (f32[1,4096]{1,0:T(1,128)S(1)}, f32[1,4096]{1,0:T(1,128)}, u32[]{:S(2)}) copy-start(f32[1,4096]{1,0:T(1,128)} %param.30) | copy-start | bytes 49156
  83.0 5.0 %collective-permute-start.14 = (f32[8,1,4096]{2,0,1:T(8,128)S(1)}, f32[8,1,4096]{2,0,1:T(8,128)S(1)}, u32[]{:S(2)}, u32[]{:S(2)}) collective-permute-start(f32[8,1,4096]{2,0,1:T(8,128)S(1)} %convolution_bitcast_fusion), channel_id=1, source_target_pairs={{0,1},{1,0},{2,3},{3,2},{4,5},{5,4},{6,7},{7,6},{8,9},{9,8},{10,11... | collective-permute-start | bytes 393224 | tf_op jit(solution)/shard_map/ppermute | solution.py:116
  87.9 5.8 %collective-permute-start.15 = (f32[8,1,4096]{2,0,1:T(8,128)S(1)}, f32[8,1,4096]{2,0,1:T(8,128)S(1)}, u32[]{:S(2)}, u32[]{:S(2)}) collective-permute-start(f32[8,1,4096]{2,0,1:T(8,128)S(1)} %add.190), channel_id=1, source_target_pairs={{0,2},{1,3},{2,0},{3,1},{4,6},{5,7},{6,4},{7,5},{8,10},{9,11},{10,... | collective-permute-start | bytes 393224 | tf_op jit(solution)/shard_map/ppermute | solution.py:116
  93.8 7.3 %collective-permute-start.16 = (f32[8,1,4096]{2,0,1:T(8,128)S(1)}, f32[8,1,4096]{2,0,1:T(8,128)S(1)}, u32[]{:S(2)}, u32[]{:S(2)}) collective-permute-start(f32[8,1,4096]{2,0,1:T(8,128)S(1)} %add.191), channel_id=1, source_target_pairs={{0,4},{1,5},{2,6},{3,7},{4,0},{5,1},{6,2},{7,3},{8,12},{9,13},{10,... | collective-permute-start | bytes 393224 | tf_op jit(solution)/shard_map/ppermute | solution.py:116
  116.2 4.3 %collective-permute-start.17 = (f32[2,2,1,1,4096]{4,2,1,0,3:T(1,128)S(1)}, f32[2,2,1,1,4096]{4,2,1,0,3:T(1,128)S(1)}, u32[]{:S(2)}, u32[]{:S(2)}) collective-permute-start(f32[2,2,1,1,4096]{4,2,1,0,3:T(1,128)S(1)} %constant_dynamic-slice_fusion.1), channel_id=1, source_target_pairs={{0,1},{1,0},{2,3},{3,2},{4,5},{5,4},{6,7},{7,6},{8,9},{9,8},{10,11... | collective-permute-start | bytes 196616 | tf_op jit(solution)/shard_map/ppermute | solution.py:508
  120.6 4.0 %collective-permute-start.18 = (f32[2,1,1,1,4096]{4,2,1,0,3:T(1,128)S(1)}, f32[2,1,1,1,4096]{4,2,1,0,3:T(1,128)S(1)}, u32[]{:S(2)}, u32[]{:S(2)}) collective-permute-start(f32[2,1,1,1,4096]{4,2,1,0,3:T(1,128)S(1)} %constant_dynamic-slice_fusion), channel_id=1, source_target_pairs={{0,2},{1,3},{2,0},{3,1},{4,6},{5,7},{6,4},{7,5},{8,10},{9,11},{10,... | collective-permute-start | bytes 98312 | tf_op jit(solution)/shard_map/ppermute | solution.py:508
  124.7 5.0 %collective-permute-start.20 = (f32[1,4096]{1,0:T(1,128)S(1)}, f32[1,4096]{1,0:T(1,128)S(1)}, u32[]{:S(2)}, u32[]{:S(2)}) collective-permute-start(f32[1,4096]{1,0:T(1,128)S(1)} %dynamic-slice_bitcast_fusion), channel_id=1, source_target_pairs={{0,12},{1,13},{2,14},{3,15},{4,8},{5,9},{6,10},{7,11},{8,20},{9,21... | collective-permute-start | bytes 49160 | tf_op jit(solution)/shard_map/ppermute | solution.py:525
  124.8 5.0 %collective-permute-start.19 = (f32[1,4096]{1,0:T(1,128)S(1)}, f32[1,4096]{1,0:T(1,128)S(1)}, u32[]{:S(2)}, u32[]{:S(2)}) collective-permute-start(f32[1,4096]{1,0:T(1,128)S(1)} %bitcast_add_fusion), channel_id=1, source_target_pairs={{0,8},{1,9},{2,10},{3,11},{4,12},{5,13},{6,14},{7,15},{8,16},{9,17... | collective-permute-start | bytes 49160 | tf_op jit(solution)/shard_map/ppermute | solution.py:524

commit v12 on v9

--- a/solution.py
+++ b/solution.py
@@ -124,6 +124,7 @@
         if not self.direct:
             self.slots = lax.all_gather(value, "site", axis=0, tiled=False)
             self.sources = jnp.arange(count, dtype=jnp.int32)
+            self.slot_of_source = self.sources
             return
         order = list(range(0, count, 2)) + [i for i in range(count - 1, -1, -1) if i % 2 == 1]
         place = [0] * count
@@ -133,12 +134,23 @@
         self.backward = [(order[p], order[(p - 1) % count]) for p in range(count)]
         self.forward_left = count // 2
         self.backward_left = count - 1 - self.forward_left
-        offsets = [0] + [-s for s in range(1, self.forward_left + 1)]
+        offsets = [0] + [count - s for s in range(1, self.forward_left + 1)]
         offsets += list(range(1, self.backward_left + 1))
-        my_place = jnp.array(place, dtype=jnp.int32)[me]
-        self.sources = jnp.array(order, dtype=jnp.int32)[
-            (my_place + jnp.array(offsets, dtype=jnp.int32)) % count
-        ]
+        half = count // 2
+        my_place = jnp.where(me % 2 == 0, me // 2, count - 1 - me // 2)
+        place_of_slot = (my_place + jnp.array(offsets, dtype=jnp.int32)) % count
+        self.sources = jnp.where(
+            place_of_slot < half, 2 * place_of_slot, 2 * (count - 1 - place_of_slot) + 1
+        )
+        devices = jnp.arange(count, dtype=jnp.int32)
+        their_place = jnp.where(devices % 2 == 0, devices // 2, count - 1 - devices // 2)
+        delta = (their_place - my_place) % count
+        forward_count = self.forward_left
+        self.slot_of_source = jnp.where(
+            delta == 0,
+            0,
+            jnp.where(delta >= count - forward_count, count - delta, forward_count + delta),
+        )
         self.forward_slots = []
         self.backward_slots = []
         self.ahead = value
@@ -433,12 +445,16 @@
     )
     in_slots, in_sources = ring_in.finish()
     in_rows = tile_in.shape[1]
-    slot_of_source = jnp.argmax(
-        in_sources[None, :] == jnp.arange(group_size, dtype=jnp.int32)[:, None], axis=1
-    ).astype(jnp.int32)
-    everyone = jnp.take(in_slots[:, in_rows:], slot_of_source, axis=0).reshape(all_sites, model_width)
+    everyone = (
+        in_slots[:, in_rows:]
+        .at[ring_in.slot_of_source]
+        .get(mode="promise_in_bounds")
+        .reshape(all_sites, model_width)
+    )
     weight_in = in_slots[:, :in_rows].reshape(-1, hidden_width)
-    own_rows = jnp.take(patches[0].reshape(tiles_here, group_size, -1), in_sources, axis=1)
+    own_rows = (
+        patches[0].reshape(tiles_here, group_size, -1).at[:, in_sources].get(mode="promise_in_bounds")
+    )
     tile_hidden = jax.nn.gelu(
         jnp.dot(own_rows.reshape(tiles_here, -1), weight_in, preferred_element_type=jnp.float32),
         approximate=True,

time: 129 us -> 128 us (level)
  waiting for transfers between devices: 47.1 us -> 52.2 us
  local copies, waits for them, and re-layouts: 17.1 us -> 14.4 us
  starting transfers between devices: 34.8 us -> 32.1 us
  other arithmetic: 9.39 us -> 7.94 us
    ppermute x8, starting transfers between devices: 18.1 us -> 11.8 us  [_issue(): self.ahead = lax.ppermute(self.ahead, 'site', self.forward)]
    ppermute x6, starting transfers between devices: 0.53 us -> 5.41 us  [_issue(): self.behind = lax.ppermute(self.behind, 'site', self.backward)]
    ppermute x8, waiting for transfers between devices: 26.1 us -> 29.6 us  [_issue(): self.ahead = lax.ppermute(self.ahead, 'site', self.forward)]
    ppermute x1, starting transfers between devices: 2.84 us -> 0.06 us  [last_round(): mine_part = lax.ppermute(own, ('section', 'site'), forward)]
    ppermute x1, starting transfers between devices: 0.06 us -> 1.7 us  [last_round(): other_part = lax.ppermute(send.reshape(rest), ('section', 'site'), across)]
    ppermute x1, waiting for transfers between devices: 0.01 us -> 1.43 us  [last_round(): mine_part = lax.ppermute(own, ('section', 'site'), forward)]
    gather x4 -> x2, local copies, waits for them, and re-layouts: 2.63 us -> 1.96 us  [the longest x1 1.41 us: heads_split(): patches[0].reshape(tiles_here, group_size, -1).at[:, in_sources]]
    unnamed x44 -> x36, local copies, waits for them, and re-layouts: 7.91 us -> 7.58 us
  transfers between devices with their start and end apart: 22 -> 22, of which waited for: 14 -> 16; matrix products, arithmetic and copies ran while one was open for 19% -> 16% of each run, Pallas kernels for 0% -> 0%
where the time goes in v12:
time: 128 us; the launch traced here: 127 us
  waiting for transfers between devices  52.2 us (41%)
  starting transfers between devices  32.1 us (25%)
  local copies, waits for them, and re-layouts  14.4 us (11%)
  Pallas kernels  12.4 us (10%)
  other arithmetic  7.94 us (6%)
  matrix products  7.69 us (6%)
    ppermute x8, waiting for transfers between devices, _issue(): self.ahead = lax.ppermute(self.ahead, 'site', self.forward)  29.6 us
    pallas_call x1, Pallas kernels, gated_ffn(): pl.pallas_call(ffn_block, grid=(units // block,), in_specs=[pl.BlockSpec(...  12.4 us
    ppermute x3, waiting for transfers between devices, doubling_sum(): state = state + lax.ppermute(state, 'site', xor_pairs(count, bit))  12.4 us
    ppermute x8, starting transfers between devices, _issue(): self.ahead = lax.ppermute(self.ahead, 'site', self.forward)  11.8 us
    unnamed x36, local copies, waits for them, and re-layouts  7.58 us
    ppermute x2, waiting for transfers between devices, last_round(): state = keep + lax.ppermute(send, 'site', xor_pairs(group_size, bit))  6.42 us
    all_to_all x1, starting transfers between devices, heads_split(): lax.all_to_all(col_blocks, 'site', split_axis=0, concat_axis=0, tiled=True)  6.37 us
    ppermute x6, starting transfers between devices, _issue(): self.behind = lax.ppermute(self.behind, 'site', self.backward)  5.41 us
  transfers between devices with their start and end apart: 22, of which 16 were waited for; matrix products, arithmetic and copies ran while one was open for 16% of the time, Pallas kernels for 0%

profile of v12, /device:TPU:0, one launch (start us, length us, event | category | flops | bytes accessed | tf_op | source)
XLA Modules:
  0.0 127.2 jit_solution(577326404003907119)
XLA Ops:
  0.0 0.9 reduce.1
  0.9 1.6 %pad_maximum_fusion = bf16[136,512]{1,0:T(8,128)(2,1)} fusion(bf16[8,512]{1,0:T(8,128)(2,1)S(1)} %reshape_squeeze.9, bf16[128,512]{1,0:T(8,128)(2,1)} %bitcast.146), kind=kLoop, calls=%fused_computation.42 | loop fusion | flops 278528 | bytes 278528 | tf_op jit(solution)/shard_map/concatenate | solution.py:442
  2.5 3.0 %collective-permute-start = (bf16[136,512]{1,0:T(8,128)(2,1)}, bf16[136,512]{1,0:T(8,128)(2,1)}, u32[]{:S(2)}, u32[]{:S(2)}) collective-permute-start(bf16[136,512]{1,0:T(8,128)(2,1)} %pad_maximum_fusion), channel_id=1, source_target_pairs={{0,2},{2,4},{4,6},{6,7},{7,5},{5,3},{3,1},{1,0},{8,10},{10,12},{12... | collective-permute-start | bytes 417800 | tf_op jit(solution)/shard_map/ppermute | solution.py:163
  5.6 1.2 copy.34
  6.8 0.4 copy.38
  7.2 1.1 reshape.278
  8.3 6.4 %all-to-all-start = ((bf16[8,64,512]{2,1,0:T(8,128)(2,1)}), bf16[8,64,512]{2,1,0:T(8,128)(2,1)S(1)}, u32[]{:S(2)}, u32[]{:S(2)}) async-start(bf16[8,64,512]{2,1,0:T(8,128)(2,1)} %reshape.278), calls=%async_computation | async-start | bytes 1048576 | tf_op jit(solution)/shard_map/all_to_all | solution.py:467
  14.9 3.1 %convert_reduce_fusion = f32[8,2048]{1,0:T(8,128)S(1)} fusion(s32[2048]{0:T(1024)S(1)} %bitcast.149, s32[8,256]{1,0:T(8,128)S(1)} %copy-done.5, pred[8,256]{1,0:T(8,128)(4,1)S(1)} %iota_compare_fusion), kind=kLoop, calls=%fused_computation.2 | loop fusion | flops 16760832 | bytes 83968 | tf_op jit(solution)/shard_map/reduce_sum | solution.py:491
  18.1 1.0 copy.27
  19.1 1.3 %copy.28 = bf16[256,8,128]{2,0,1:T(8,128)(2,1)S(1)} copy(bf16[256,8,128]{0,2,1:T(8,128)(2,1)} %bitcast.143) | data formatting | bytes 1048576 | tf_op jit(solution)/shard_map/reshape;squeeze | solution.py:456
  20.4 1.4 %gather_fusion.1 = bf16[8,256,128]{2,1,0:T(8,128)(2,1)} fusion(bf16[256,8,128]{2,0,1:T(8,128)(2,1)S(1)} %copy.28, s32[1024]{0:T(1024)S(1)} %pad_clamp_fusion), kind=kCustom, calls=%fused_computation.1 | custom fusion | bytes 1048608 | tf_op jit(solution)/shard_map/gather | solution.py:456
  21.9 2.1 %collective-permute-start.1 = (bf16[136,512]{1,0:T(8,128)(2,1)}, bf16[136,512]{1,0:T(8,128)(2,1)S(1)}, u32[]{:S(2)}, u32[]{:S(2)}) collective-permute-start(bf16[136,512]{1,0:T(8,128)(2,1)} %collective-permute-done), channel_id=1, source_target_pairs={{0,2},{2,4},{4,6},{6,7},{7,5},{5,3},{3,1},{1,0},{8,10},{10,12},{12... | collective-permute-start | bytes 417800 | tf_op jit(solution)/shard_map/ppermute | solution.py:163
  24.0 0.9 bitcast_dynamic-update-slice_fusion.14
  24.9 3.0 %collective-permute-done.1 = bf16[136,512]{1,0:T(8,128)(2,1)S(1)} collective-permute-done((bf16[136,512]{1,0:T(8,128)(2,1)}, bf16[136,512]{1,0:T(8,128)(2,1)S(1)}, u32[]{:S(2)}, u32[]{:S(2)}) %collective-permute-start.1) | collective-permute-done | bytes 139296 | tf_op jit(solution)/shard_map/ppermute | solution.py:163
  27.9 2.2 %collective-permute-start.2 = (bf16[136,512]{1,0:T(8,128)(2,1)S(1)}, bf16[136,512]{1,0:T(8,128)(2,1)S(1)}, u32[]{:S(2)}, u32[]{:S(2)}) collective-permute-start(bf16[136,512]{1,0:T(8,128)(2,1)S(1)} %collective-permute-done.1), channel_id=1, source_target_pairs={{0,2},{2,4},{4,6},{6,7},{7,5},{5,3},{3,1},{1,0},{8,10},{10,12},{12... | collective-permute-start | bytes 417800 | tf_op jit(solution)/shard_map/ppermute | solution.py:163
  30.1 0.3 collective-permute-done.5
  30.4 2.7 %collective-permute-done.2 = bf16[136,512]{1,0:T(8,128)(2,1)S(1)} collective-permute-done((bf16[136,512]{1,0:T(8,128)(2,1)S(1)}, bf16[136,512]{1,0:T(8,128)(2,1)S(1)}, u32[]{:S(2)}, u32[]{:S(2)}) %collective-permute-start.2) | collective-permute-done | bytes 139296 | tf_op jit(solution)/shard_map/ppermute | solution.py:163
  33.1 2.1 %collective-permute-start.3 = (bf16[136,512]{1,0:T(8,128)(2,1)S(1)}, bf16[136,512]{1,0:T(8,128)(2,1)S(1)}, u32[]{:S(2)}, u32[]{:S(2)}) collective-permute-start(bf16[136,512]{1,0:T(8,128)(2,1)S(1)} %collective-permute-done.2), channel_id=1, source_target_pairs={{0,2},{2,4},{4,6},{6,7},{7,5},{5,3},{3,1},{1,0},{8,10},{10,12},{12... | collective-permute-start | bytes 417800 | tf_op jit(solution)/shard_map/ppermute | solution.py:163
  35.2 4.5 %collective-permute-done.3 = bf16[136,512]{1,0:T(8,128)(2,1)S(1)} collective-permute-done((bf16[136,512]{1,0:T(8,128)(2,1)S(1)}, bf16[136,512]{1,0:T(8,128)(2,1)S(1)}, u32[]{:S(2)}, u32[]{:S(2)}) %collective-permute-start.3) | collective-permute-done | bytes 139296 | tf_op jit(solution)/shard_map/ppermute | solution.py:163
  39.8 1.4 %bitcast_dynamic-update-slice_fusion.7 = (bf16[8,256,512]{2,1,0:T(8,128)(2,1)}, bf16[256,512]{1,0:T(8,128)(2,1)}) fusion(bf16[8,136,512]{2,1,0:T(8,128)(2,1)S(1)} %bitcast_dynamic-update-slice_fusion.8, bf16[8,256,128]{2,1,0:T(8,128)(2,1)S(1)} %copy-done.3), kind=kOutput, calls=%fused_computation.41 | convolution fusion | flops 269615104 | bytes 2097152 | tf_op jit(solution)/shard_map/dot_general | solution.py:459
  41.2 0.5 collective-permute-start.7
  41.8 1.5 %collective-permute-start.11 = (bf16[256,512]{1,0:T(8,128)(2,1)}, bf16[256,512]{1,0:T(8,128)(2,1)S(1)}, u32[]{:S(2)}, u32[]{:S(2)}) collective-permute-start(bf16[256,512]{1,0:T(8,128)(2,1)} %get-tuple-element.10), channel_id=1, source_target_pairs={{0,1},{2,0},{4,2},{6,4},{7,6},{5,7},{3,5},{1,3},{8,9},{10,8},{12,1... | collective-permute-start | bytes 786440 | tf_op jit(solution)/shard_map/ppermute | solution.py:167
  43.3 0.5 gather_fusion
  43.9 5.0 %collective-permute-done.7 = bf16[256,512]{1,0:T(8,128)(2,1)S(1)} collective-permute-done((bf16[256,512]{1,0:T(8,128)(2,1)}, bf16[256,512]{1,0:T(8,128)(2,1)S(1)}, u32[]{:S(2)}, u32[]{:S(2)}) %collective-permute-start.7) | collective-permute-done | bytes 262176 | tf_op jit(solution)/shard_map/ppermute | solution.py:163
  48.9 1.0 collective-permute-start.8
  49.9 2.3 %bitcast_reduce_fusion.1 = (f32[8,2]{0,1:T(2,128)S(1)}, f32[8,256]{1,0:T(8,128)S(1)}) fusion(bf16[8,4096]{1,0:T(8,128)(2,1)S(1)} %bitcast.148, bf16[1,256,4096]{2,1,0:T(8,128)(2,1)} %param.20), kind=kOutput, calls=%fused_computation.66 | convolution fusion | flops 16785392 | bytes 2170944 | tf_op jit(solution)/shard_map/dot_general | solution.py:23
  52.2 5.8 %collective-permute-done.8 = bf16[256,512]{1,0:T(8,128)(2,1)S(1)} collective-permute-done((bf16[256,512]{1,0:T(8,128)(2,1)S(1)}, bf16[256,512]{1,0:T(8,128)(2,1)S(1)}, u32[]{:S(2)}, u32[]{:S(2)}) %collective-permute-start.8) | collective-permute-done | bytes 262176 | tf_op jit(solution)/shard_map/ppermute | solution.py:163
  58.0 0.8 collective-permute-start.9
  58.9 2.1 %collective-permute-start.12 = (bf16[256,512]{1,0:T(8,128)(2,1)S(1)}, bf16[256,512]{1,0:T(8,128)(2,1)S(1)}, u32[]{:S(2)}, u32[]{:S(2)}) collective-permute-start(bf16[256,512]{1,0:T(8,128)(2,1)S(1)} %collective-permute-done.11), channel_id=1, source_target_pairs={{0,1},{2,0},{4,2},{6,4},{7,6},{5,7},{3,5},{1,3},{8,9},{10,8},{12,1... | collective-permute-start | bytes 786440 | tf_op jit(solution)/shard_map/ppermute | solution.py:167
  61.0 0.7 bitcast_dynamic-update-slice_fusion.6
  61.7 5.6 %collective-permute-done.9 = bf16[256,512]{1,0:T(8,128)(2,1)S(1)} collective-permute-done((bf16[256,512]{1,0:T(8,128)(2,1)S(1)}, bf16[256,512]{1,0:T(8,128)(2,1)S(1)}, u32[]{:S(2)}, u32[]{:S(2)}) %collective-permute-start.9) | collective-permute-done | bytes 262176 | tf_op jit(solution)/shard_map/ppermute | solution.py:163
  67.4 0.7 bitcast_dynamic-update-slice_fusion.5
  68.1 0.3 collective-permute-done.12
  68.4 1.7 %collective-permute-start.13 = (bf16[256,512]{1,0:T(8,128)(2,1)S(1)}, bf16[256,512]{1,0:T(8,128)(2,1)S(1)}, u32[]{:S(2)}, u32[]{:S(2)}) collective-permute-start(bf16[256,512]{1,0:T(8,128)(2,1)S(1)} %collective-permute-done.12), channel_id=1, source_target_pairs={{0,1},{2,0},{4,2},{6,4},{7,6},{5,7},{3,5},{1,3},{8,9},{10,8},{12,1... | collective-permute-start | bytes 786440 | tf_op jit(solution)/shard_map/ppermute | solution.py:167
  70.1 0.7 bitcast_dynamic-update-slice_fusion.4
  70.8 2.9 %collective-permute-done.10 = bf16[256,512]{1,0:T(8,128)(2,1)S(1)} collective-permute-done((bf16[256,512]{1,0:T(8,128)(2,1)S(1)}, bf16[256,512]{1,0:T(8,128)(2,1)S(1)}, u32[]{:S(2)}, u32[]{:S(2)}) %collective-permute-start.10) | collective-permute-done | bytes 262176 | tf_op jit(solution)/shard_map/ppermute | solution.py:163
  73.7 0.7 bitcast_dynamic-update-slice_fusion.3
  74.4 0.7 bitcast_dynamic-update-slice_fusion.2
  75.2 0.7 bitcast_dynamic-update-slice_fusion.1
  75.9 0.7 bitcast_dynamic-update-slice_fusion
  76.6 2.9 %fusion.44 = f32[2048,512]{0,1:T(8,128)S(1)} fusion(bf16[2048,512]{1,0:T(8,128)(2,1)} %bitcast.21, bf16[512,512]{1,0:T(8,128)(2,1)S(1)} %bitcast.140), kind=kOutput, calls=%fused_computation.103 | convolution fusion | flops 1073741824 | bytes 6815744 | tf_op jit(solution)/shard_map/dot_general | solution.py:478
  79.5 0.1 slice.38
  79.7 0.2 bitcast_reduce_fusion
  79.9 0.2 fusion.7
  80.1 0.3 fusion.2
  80.5 0.8 convolution_bitcast_fusion
  81.3 1.7 %collective-permute-start.14 = (f32[8,1,4096]{2,0,1:T(8,128)S(1)}, f32[8,1,4096]{2,0,1:T(8,128)S(1)}, u32[]{:S(2)}, u32[]{:S(2)}) collective-permute-start(f32[8,1,4096]{2,0,1:T(8,128)S(1)} %convolution_bitcast_fusion), channel_id=1, source_target_pairs={{0,1},{1,0},{2,3},{3,2},{4,5},{5,4},{6,7},{7,6},{8,9},{9,8},{10,11... | collective-permute-start | bytes 393224 | tf_op jit(solution)/shard_map/ppermute | solution.py:116
  83.0 3.2 %collective-permute-done.14 = f32[8,1,4096]{2,0,1:T(8,128)S(1)} collective-permute-done((f32[8,1,4096]{2,0,1:T(8,128)S(1)}, f32[8,1,4096]{2,0,1:T(8,128)S(1)}, u32[]{:S(2)}, u32[]{:S(2)}) %collective-permute-start.14) | collective-permute-done | bytes 131104 | tf_op jit(solution)/shard_map/ppermute | solution.py:116
  86.3 1.3 %collective-permute-start.15 = (f32[8,1,4096]{2,0,1:T(8,128)S(1)}, f32[8,1,4096]{2,0,1:T(8,128)S(1)}, u32[]{:S(2)}, u32[]{:S(2)}) collective-permute-start(f32[8,1,4096]{2,0,1:T(8,128)S(1)} %add.224), channel_id=1, source_target_pairs={{0,2},{1,3},{2,0},{3,1},{4,6},{5,7},{6,4},{7,5},{8,10},{9,11},{10,... | collective-permute-start | bytes 393224 | tf_op jit(solution)/shard_map/ppermute | solution.py:116
  87.6 3.7 %collective-permute-done.15 = f32[8,1,4096]{2,0,1:T(8,128)S(1)} collective-permute-done((f32[8,1,4096]{2,0,1:T(8,128)S(1)}, f32[8,1,4096]{2,0,1:T(8,128)S(1)}, u32[]{:S(2)}, u32[]{:S(2)}) %collective-permute-start.15) | collective-permute-done | bytes 131104 | tf_op jit(solution)/shard_map/ppermute | solution.py:116
  91.3 1.9 %collective-permute-start.16 = (f32[8,1,4096]{2,0,1:T(8,128)S(1)}, f32[8,1,4096]{2,0,1:T(8,128)S(1)}, u32[]{:S(2)}, u32[]{:S(2)}) collective-permute-start(f32[8,1,4096]{2,0,1:T(8,128)S(1)} %add.225), channel_id=1, source_target_pairs={{0,4},{1,5},{2,6},{3,7},{4,0},{5,1},{6,2},{7,3},{8,12},{9,13},{10,... | collective-permute-start | bytes 393224 | tf_op jit(solution)/shard_map/ppermute | solution.py:116
  93.2 5.4 %collective-permute-done.16 = f32[8,1,4096]{2,0,1:T(8,128)S(1)} collective-permute-done((f32[8,1,4096]{2,0,1:T(8,128)S(1)}, f32[8,1,4096]{2,0,1:T(8,128)S(1)}, u32[]{:S(2)}, u32[]{:S(2)}) %collective-permute-start.16) | collective-permute-done | bytes 131104 | tf_op jit(solution)/shard_map/ppermute | solution.py:116
  98.6 0.1 multiply_reduce_fusion
  98.8 0.7 fusion.29.rows_ref
  99.5 12.4 %shard_map.154 = f32[8,4096]{1,0:T(8,128)} custom-call(bf16[8,4096]{1,0:T(8,128)(2,1)} %fusion.29.rows_ref, bf16[896,4096]{1,0:T(8,128)(2,1)} %bitcast.135, bf16[896,4096]{1,0:T(8,128)(2,1)} %bitcast.136, bf16[896,4096]{1,0:T(8,128)(2,1)} %bitcast.137), custom_call_target="tpu_custom_call" | custom-call | tf_op jit(solution)/shard_map/pallas_call | solution.py:396
  111.9 1.0 reshape_reshape.4
  113.0 1.8 %collective-permute-start.17 = (f32[2,2,1,1,4096]{4,2,1,0,3:T(1,128)S(1)}, f32[2,2,1,1,4096]{4,2,1,0,3:T(1,128)S(1)}, u32[]{:S(2)}, u32[]{:S(2)}) collective-permute-start(f32[2,2,1,1,4096]{4,2,1,0,3:T(1,128)S(1)} %constant_dynamic-slice_fusion.1), channel_id=1, source_target_pairs={{0,1},{1,0},{2,3},{3,2},{4,5},{5,4},{6,7},{7,6},{8,9},{9,8},{10,11... | collective-permute-start | bytes 196616 | tf_op jit(solution)/shard_map/ppermute | solution.py:521
  114.8 2.5 %collective-permute-done.17 = f32[2,2,1,1,4096]{4,2,1,0,3:T(1,128)S(1)} collective-permute-done((f32[2,2,1,1,4096]{4,2,1,0,3:T(1,128)S(1)}, f32[2,2,1,1,4096]{4,2,1,0,3:T(1,128)S(1)}, u32[]{:S(2)}, u32[]{:S(2)}) %collective-permute-start.17) | collective-permute-done | bytes 65568 | tf_op jit(solution)/shard_map/ppermute | solution.py:521
  117.3 0.1 dynamic-slice_add_fusion
  117.5 3.9 %collective-permute-done.18 = f32[2,1,1,1,4096]{4,2,1,0,3:T(1,128)S(1)} collective-permute-done((f32[2,1,1,1,4096]{4,2,1,0,3:T(1,128)S(1)}, f32[2,1,1,1,4096]{4,2,1,0,3:T(1,128)S(1)}, u32[]{:S(2)}, u32[]{:S(2)}) %collective-permute-start.18) | collective-permute-done | bytes 32800 | tf_op jit(solution)/shard_map/ppermute | solution.py:521
  121.6 1.7 %collective-permute-start.20 = (f32[1,4096]{1,0:T(1,128)S(1)}, f32[1,4096]{1,0:T(1,128)S(1)}, u32[]{:S(2)}, u32[]{:S(2)}) collective-permute-start(f32[1,4096]{1,0:T(1,128)S(1)} %dynamic-slice_bitcast_fusion), channel_id=1, source_target_pairs={{0,12},{1,13},{2,14},{3,15},{4,8},{5,9},{6,10},{7,11},{8,20},{9,21... | collective-permute-start | bytes 49160 | tf_op jit(solution)/shard_map/ppermute | solution.py:538
  123.3 1.4 %collective-permute-done.19 = f32[1,4096]{1,0:T(1,128)S(1)} collective-permute-done((f32[1,4096]{1,0:T(1,128)S(1)}, f32[1,4096]{1,0:T(1,128)S(1)}, u32[]{:S(2)}, u32[]{:S(2)}) %collective-permute-start.19) | collective-permute-done | bytes 16416 | tf_op jit(solution)/shard_map/ppermute | solution.py:537
  124.7 1.9 %collective-permute-done.20 = f32[1,4096]{1,0:T(1,128)S(1)} collective-permute-done((f32[1,4096]{1,0:T(1,128)S(1)}, f32[1,4096]{1,0:T(1,128)S(1)}, u32[]{:S(2)}, u32[]{:S(2)}) %collective-permute-start.20) | collective-permute-done | bytes 16416 | tf_op jit(solution)/shard_map/ppermute | solution.py:538
  126.6 0.6 convert_bitcast_fusion
  (63 shorter events, 0.9 us)
Async XLA Ops:
  0.0 80.5 %copy-start = (bf16[1,256,4096]{2,1,0:T(8,128)(2,1)S(1)}, bf16[1,256,4096]{2,1,0:T(8,128)(2,1)}, u32[]{:S(2)}) copy-start(bf16[1,256,4096]{2,1,0:T(8,128)(2,1)} %param.25) | copy-start | bytes 6291460
  2.5 19.4 %collective-permute-start = (bf16[136,512]{1,0:T(8,128)(2,1)}, bf16[136,512]{1,0:T(8,128)(2,1)}, u32[]{:S(2)}, u32[]{:S(2)}) collective-permute-start(bf16[136,512]{1,0:T(8,128)(2,1)} %pad_maximum_fusion), channel_id=1, source_target_pairs={{0,2},{2,4},{4,6},{6,7},{7,5},{5,3},{3,1},{1,0},{8,10},{10,12},{12... | collective-permute-start | bytes 417800 | tf_op jit(solution)/shard_map/ppermute | solution.py:163
  5.5 18.4 %collective-permute-start.4 = (bf16[136,512]{1,0:T(8,128)(2,1)}, bf16[136,512]{1,0:T(8,128)(2,1)S(1)}, u32[]{:S(2)}, u32[]{:S(2)}) collective-permute-start(bf16[136,512]{1,0:T(8,128)(2,1)} %pad_maximum_fusion), channel_id=1, source_target_pairs={{0,1},{2,0},{4,2},{6,4},{7,6},{5,7},{3,5},{1,3},{8,9},{10,8},{12,1... | collective-permute-start | bytes 417800 | tf_op jit(solution)/shard_map/ppermute | solution.py:167
  5.5 9.2 %copy-start.7 = (s32[8]{0:T(128)S(1)}, s32[8]{0:T(128)}, u32[]{:S(2)}) copy-start(s32[8]{0:T(128)} %constant.144.clone) | copy-start | bytes 100
  5.5 9.2 %copy-start.8 = (f32[1,128]{1,0:T(1,128)S(1)}, f32[1,128]{1,0:T(1,128)}, u32[]{:S(2)}) copy-start(f32[1,128]{1,0:T(1,128)} %param.22) | copy-start | bytes 1540
  5.5 9.3 %copy-start.6 = (s32[8]{0:T(128)S(1)}, s32[8]{0:T(128)}, u32[]{:S(2)}) copy-start(s32[8]{0:T(128)} %param.19) | copy-start | bytes 100
  5.6 9.4 %copy-start.5 = (s32[8,256]{1,0:T(8,128)S(1)}, s32[8,256]{1,0:T(8,128)}, u32[]{:S(2)}) copy-start(s32[8,256]{1,0:T(8,128)} %param.18) | copy-start | bytes 24580
  5.6 12.5 %copy-start.1 = (bf16[1,256,1024]{2,1,0:T(8,128)(2,1)S(1)}, bf16[1,256,1024]{2,1,0:T(8,128)(2,1)}, u32[]{:S(2)}) copy-start(bf16[1,256,1024]{2,1,0:T(8,128)(2,1)} %param.17) | copy-start | bytes 1572868
  8.3 13.5 %copy-start.2 = (bf16[1,128,512]{2,1,0:T(8,128)(2,1)S(1)}, bf16[1,128,512]{2,1,0:T(8,128)(2,1)}, u32[]{:S(2)}) copy-start(bf16[1,128,512]{2,1,0:T(8,128)(2,1)} %param.23) | copy-start | bytes 393220
  8.3 68.3 %all-to-all-start = ((bf16[8,64,512]{2,1,0:T(8,128)(2,1)}), bf16[8,64,512]{2,1,0:T(8,128)(2,1)S(1)}, u32[]{:S(2)}, u32[]{:S(2)}) async-start(bf16[8,64,512]{2,1,0:T(8,128)(2,1)} %reshape.278), calls=%async_computation | async-start | bytes 1048576 | tf_op jit(solution)/shard_map/all_to_all | solution.py:467
  21.9 18.0 %copy-start.3 = (bf16[8,256,128]{2,1,0:T(8,128)(2,1)S(1)}, bf16[8,256,128]{2,1,0:T(8,128)(2,1)}, u32[]{:S(2)}) copy-start(bf16[8,256,128]{2,1,0:T(8,128)(2,1)} %gather_fusion.1) | copy-start | bytes 1572868
  21.9 6.0 %collective-permute-start.1 = (bf16[136,512]{1,0:T(8,128)(2,1)}, bf16[136,512]{1,0:T(8,128)(2,1)S(1)}, u32[]{:S(2)}, u32[]{:S(2)}) collective-permute-start(bf16[136,512]{1,0:T(8,128)(2,1)} %collective-permute-done), channel_id=1, source_target_pairs={{0,2},{2,4},{4,6},{6,7},{7,5},{5,3},{3,1},{1,0},{8,10},{10,12},{12... | collective-permute-start | bytes 417800 | tf_op jit(solution)/shard_map/ppermute | solution.py:163
  23.9 6.5 %collective-permute-start.5 = (bf16[136,512]{1,0:T(8,128)(2,1)S(1)}, bf16[136,512]{1,0:T(8,128)(2,1)S(1)}, u32[]{:S(2)}, u32[]{:S(2)}) collective-permute-start(bf16[136,512]{1,0:T(8,128)(2,1)S(1)} %collective-permute-done.4), channel_id=1, source_target_pairs={{0,1},{2,0},{4,2},{6,4},{7,6},{5,7},{3,5},{1,3},{8,9},{10,8},{12,1... | collective-permute-start | bytes 417800 | tf_op jit(solution)/shard_map/ppermute | solution.py:167
  27.9 5.2 %collective-permute-start.2 = (bf16[136,512]{1,0:T(8,128)(2,1)S(1)}, bf16[136,512]{1,0:T(8,128)(2,1)S(1)}, u32[]{:S(2)}, u32[]{:S(2)}) collective-permute-start(bf16[136,512]{1,0:T(8,128)(2,1)S(1)} %collective-permute-done.1), channel_id=1, source_target_pairs={{0,2},{2,4},{4,6},{6,7},{7,5},{5,3},{3,1},{1,0},{8,10},{10,12},{12... | collective-permute-start | bytes 417800 | tf_op jit(solution)/shard_map/ppermute | solution.py:163
  30.4 9.4 %collective-permute-start.6 = (bf16[136,512]{1,0:T(8,128)(2,1)S(1)}, bf16[136,512]{1,0:T(8,128)(2,1)S(1)}, u32[]{:S(2)}, u32[]{:S(2)}) collective-permute-start(bf16[136,512]{1,0:T(8,128)(2,1)S(1)} %collective-permute-done.5), channel_id=1, source_target_pairs={{0,1},{2,0},{4,2},{6,4},{7,6},{5,7},{3,5},{1,3},{8,9},{10,8},{12,1... | collective-permute-start | bytes 417800 | tf_op jit(solution)/shard_map/ppermute | solution.py:167
  33.1 6.6 %collective-permute-start.3 = (bf16[136,512]{1,0:T(8,128)(2,1)S(1)}, bf16[136,512]{1,0:T(8,128)(2,1)S(1)}, u32[]{:S(2)}, u32[]{:S(2)}) collective-permute-start(bf16[136,512]{1,0:T(8,128)(2,1)S(1)} %collective-permute-done.2), channel_id=1, source_target_pairs={{0,2},{2,4},{4,6},{6,7},{7,5},{5,3},{3,1},{1,0},{8,10},{10,12},{12... | collective-permute-start | bytes 417800 | tf_op jit(solution)/shard_map/ppermute | solution.py:163
  39.7 2.0 %copy-start.9 = (f32[1,128]{1,0:T(1,128)S(1)}, f32[1,128]{1,0:T(1,128)}, u32[]{:S(2)}) copy-start(f32[1,128]{1,0:T(1,128)} %param.21) | copy-start | bytes 1540
  41.2 7.7 %collective-permute-start.7 = (bf16[256,512]{1,0:T(8,128)(2,1)}, bf16[256,512]{1,0:T(8,128)(2,1)S(1)}, u32[]{:S(2)}, u32[]{:S(2)}) collective-permute-start(bf16[256,512]{1,0:T(8,128)(2,1)} %get-tuple-element.10), channel_id=1, source_target_pairs={{0,2},{2,4},{4,6},{6,7},{7,5},{5,3},{3,1},{1,0},{8,10},{10,12},{12... | collective-permute-start | bytes 786440 | tf_op jit(solution)/shard_map/ppermute | solution.py:163
  41.8 17.1 %collective-permute-start.11 = (bf16[256,512]{1,0:T(8,128)(2,1)}, bf16[256,512]{1,0:T(8,128)(2,1)S(1)}, u32[]{:S(2)}, u32[]{:S(2)}) collective-permute-start(bf16[256,512]{1,0:T(8,128)(2,1)} %get-tuple-element.10), channel_id=1, source_target_pairs={{0,1},{2,0},{4,2},{6,4},{7,6},{5,7},{3,5},{1,3},{8,9},{10,8},{12,1... | collective-permute-start | bytes 786440 | tf_op jit(solution)/shard_map/ppermute | solution.py:167
  48.9 9.1 %collective-permute-start.8 = (bf16[256,512]{1,0:T(8,128)(2,1)S(1)}, bf16[256,512]{1,0:T(8,128)(2,1)S(1)}, u32[]{:S(2)}, u32[]{:S(2)}) collective-permute-start(bf16[256,512]{1,0:T(8,128)(2,1)S(1)} %collective-permute-done.7), channel_id=1, source_target_pairs={{0,2},{2,4},{4,6},{6,7},{7,5},{5,3},{3,1},{1,0},{8,10},{10,12},{12... | collective-permute-start | bytes 786440 | tf_op jit(solution)/shard_map/ppermute | solution.py:163
  58.0 9.3 %collective-permute-start.9 = (bf16[256,512]{1,0:T(8,128)(2,1)S(1)}, bf16[256,512]{1,0:T(8,128)(2,1)S(1)}, u32[]{:S(2)}, u32[]{:S(2)}) collective-permute-start(bf16[256,512]{1,0:T(8,128)(2,1)S(1)} %collective-permute-done.8), channel_id=1, source_target_pairs={{0,2},{2,4},{4,6},{6,7},{7,5},{5,3},{3,1},{1,0},{8,10},{10,12},{12... | collective-permute-start | bytes 786440 | tf_op jit(solution)/shard_map/ppermute | solution.py:163
  58.9 9.5 %collective-permute-start.12 = (bf16[256,512]{1,0:T(8,128)(2,1)S(1)}, bf16[256,512]{1,0:T(8,128)(2,1)S(1)}, u32[]{:S(2)}, u32[]{:S(2)}) collective-permute-start(bf16[256,512]{1,0:T(8,128)(2,1)S(1)} %collective-permute-done.11), channel_id=1, source_target_pairs={{0,1},{2,0},{4,2},{6,4},{7,6},{5,7},{3,5},{1,3},{8,9},{10,8},{12,1... | collective-permute-start | bytes 786440 | tf_op jit(solution)/shard_map/ppermute | solution.py:167
  67.3 6.4 %collective-permute-start.10 = (bf16[256,512]{1,0:T(8,128)(2,1)S(1)}, bf16[256,512]{1,0:T(8,128)(2,1)S(1)}, u32[]{:S(2)}, u32[]{:S(2)}) collective-permute-start(bf16[256,512]{1,0:T(8,128)(2,1)S(1)} %collective-permute-done.9), channel_id=1, source_target_pairs={{0,2},{2,4},{4,6},{6,7},{7,5},{5,3},{3,1},{1,0},{8,10},{10,12},{12... | collective-permute-start | bytes 786440 | tf_op jit(solution)/shard_map/ppermute | solution.py:163
  68.4 7.5 %collective-permute-start.13 = (bf16[256,512]{1,0:T(8,128)(2,1)S(1)}, bf16[256,512]{1,0:T(8,128)(2,1)S(1)}, u32[]{:S(2)}, u32[]{:S(2)}) collective-permute-start(bf16[256,512]{1,0:T(8,128)(2,1)S(1)} %collective-permute-done.12), channel_id=1, source_target_pairs={{0,1},{2,0},{4,2},{6,4},{7,6},{5,7},{3,5},{1,3},{8,9},{10,8},{12,1... | collective-permute-start | bytes 786440 | tf_op jit(solution)/shard_map/ppermute | solution.py:167
  80.5 18.3 %copy-start.4 = (f32[1,4096]{1,0:T(1,128)S(1)}, f32[1,4096]{1,0:T(1,128)}, u32[]{:S(2)}) copy-start(f32[1,4096]{1,0:T(1,128)} %param.26) | copy-start | bytes 49156
  81.3 5.0 %collective-permute-start.14 = (f32[8,1,4096]{2,0,1:T(8,128)S(1)}, f32[8,1,4096]{2,0,1:T(8,128)S(1)}, u32[]{:S(2)}, u32[]{:S(2)}) collective-permute-start(f32[8,1,4096]{2,0,1:T(8,128)S(1)} %convolution_bitcast_fusion), channel_id=1, source_target_pairs={{0,1},{1,0},{2,3},{3,2},{4,5},{5,4},{6,7},{7,6},{8,9},{9,8},{10,11... | collective-permute-start | bytes 393224 | tf_op jit(solution)/shard_map/ppermute | solution.py:116
  86.3 5.0 %collective-permute-start.15 = (f32[8,1,4096]{2,0,1:T(8,128)S(1)}, f32[8,1,4096]{2,0,1:T(8,128)S(1)}, u32[]{:S(2)}, u32[]{:S(2)}) collective-permute-start(f32[8,1,4096]{2,0,1:T(8,128)S(1)} %add.224), channel_id=1, source_target_pairs={{0,2},{1,3},{2,0},{3,1},{4,6},{5,7},{6,4},{7,5},{8,10},{9,11},{10,... | collective-permute-start | bytes 393224 | tf_op jit(solution)/shard_map/ppermute | solution.py:116
  91.3 7.3 %collective-permute-start.16 = (f32[8,1,4096]{2,0,1:T(8,128)S(1)}, f32[8,1,4096]{2,0,1:T(8,128)S(1)}, u32[]{:S(2)}, u32[]{:S(2)}) collective-permute-start(f32[8,1,4096]{2,0,1:T(8,128)S(1)} %add.225), channel_id=1, source_target_pairs={{0,4},{1,5},{2,6},{3,7},{4,0},{5,1},{6,2},{7,3},{8,12},{9,13},{10,... | collective-permute-start | bytes 393224 | tf_op jit(solution)/shard_map/ppermute | solution.py:116
  113.0 4.3 %collective-permute-start.17 = (f32[2,2,1,1,4096]{4,2,1,0,3:T(1,128)S(1)}, f32[2,2,1,1,4096]{4,2,1,0,3:T(1,128)S(1)}, u32[]{:S(2)}, u32[]{:S(2)}) collective-permute-start(f32[2,2,1,1,4096]{4,2,1,0,3:T(1,128)S(1)} %constant_dynamic-slice_fusion.1), channel_id=1, source_target_pairs={{0,1},{1,0},{2,3},{3,2},{4,5},{5,4},{6,7},{7,6},{8,9},{9,8},{10,11... | collective-permute-start | bytes 196616 | tf_op jit(solution)/shard_map/ppermute | solution.py:521
  117.4 4.0 %collective-permute-start.18 = (f32[2,1,1,1,4096]{4,2,1,0,3:T(1,128)S(1)}, f32[2,1,1,1,4096]{4,2,1,0,3:T(1,128)S(1)}, u32[]{:S(2)}, u32[]{:S(2)}) collective-permute-start(f32[2,1,1,1,4096]{4,2,1,0,3:T(1,128)S(1)} %constant_dynamic-slice_fusion), channel_id=1, source_target_pairs={{0,2},{1,3},{2,0},{3,1},{4,6},{5,7},{6,4},{7,5},{8,10},{9,11},{10,... | collective-permute-start | bytes 98312 | tf_op jit(solution)/shard_map/ppermute | solution.py:521
  121.5 3.2 %collective-permute-start.19 = (f32[1,4096]{1,0:T(1,128)S(1)}, f32[1,4096]{1,0:T(1,128)S(1)}, u32[]{:S(2)}, u32[]{:S(2)}) collective-permute-start(f32[1,4096]{1,0:T(1,128)S(1)} %bitcast_add_fusion), channel_id=1, source_target_pairs={{0,8},{1,9},{2,10},{3,11},{4,12},{5,13},{6,14},{7,15},{8,16},{9,17... | collective-permute-start | bytes 49160 | tf_op jit(solution)/shard_map/ppermute | solution.py:537
  121.6 5.0 %collective-permute-start.20 = (f32[1,4096]{1,0:T(1,128)S(1)}, f32[1,4096]{1,0:T(1,128)S(1)}, u32[]{:S(2)}, u32[]{:S(2)}) collective-permute-start(f32[1,4096]{1,0:T(1,128)S(1)} %dynamic-slice_bitcast_fusion), channel_id=1, source_target_pairs={{0,12},{1,13},{2,14},{3,15},{4,8},{5,9},{6,10},{7,11},{8,20},{9,21... | collective-permute-start | bytes 49160 | tf_op jit(solution)/shard_map/ppermute | solution.py:538

commit v13 on v12

--- a/solution.py
+++ b/solution.py
@@ -346,12 +346,12 @@
     bits = group_size.bit_length() - 1
     rest = down_part.shape[1:]
     state = down_part.reshape((2,) * bits + rest)
-    for bit in range(bits):
+    for bit in reversed(range(bits)):
         axis = bits - 1 - bit
         mine = (my_index >> bit) & 1
         keep = lax.dynamic_index_in_dim(state, mine, axis, keepdims=True)
         send = lax.dynamic_index_in_dim(state, 1 - mine, axis, keepdims=True)
-        if bit < bits - 1:
+        if bit > 0:
             state = keep + lax.ppermute(send, "site", xor_pairs(group_size, bit))
             continue
         own = keep.reshape(rest) + residual
@@ -451,12 +451,14 @@
         .get(mode="promise_in_bounds")
         .reshape(all_sites, model_width)
     )
-    weight_in = in_slots[:, :in_rows].reshape(-1, hidden_width)
-    own_rows = (
-        patches[0].reshape(tiles_here, group_size, -1).at[:, in_sources].get(mode="promise_in_bounds")
+    weight_in = (
+        in_slots[:, :in_rows]
+        .at[ring_in.slot_of_source]
+        .get(mode="promise_in_bounds")
+        .reshape(-1, hidden_width)
     )
     tile_hidden = jax.nn.gelu(
-        jnp.dot(own_rows.reshape(tiles_here, -1), weight_in, preferred_element_type=jnp.float32),
+        jnp.dot(patches[0], weight_in, preferred_element_type=jnp.float32),
         approximate=True,
     ).astype(jnp.bfloat16)
 
@@ -512,12 +514,12 @@
     bits = group_size.bit_length() - 1
     rest = down_part.shape[1:]
     state = down_part.reshape((2,) * bits + rest)
-    for bit in range(bits):
+    for bit in reversed(range(bits)):
         axis = bits - 1 - bit
         mine = (my_index >> bit) & 1
         keep = lax.dynamic_index_in_dim(state, mine, axis, keepdims=True)
         send = lax.dynamic_index_in_dim(state, 1 - mine, axis, keepdims=True)
-        if bit < bits - 1:
+        if bit > 0:
             state = keep + lax.ppermute(send, "site", xor_pairs(group_size, bit))
             continue
         own = keep.reshape(rest) + residual

time: 128 us -> 131 us (1.023)
  starting transfers between devices: 32.1 us -> 34.5 us
  waiting for transfers between devices: 52.2 us -> 54.2 us
  matrix products: 7.69 us -> 9.03 us
    ppermute x2, waiting for transfers between devices: 6.42 us -> 8.7 us  [last_round(): state = keep + lax.ppermute(send, 'site', xor_pairs(group_size, bit))]
    ppermute x8, starting transfers between devices: 11.8 us -> 13.8 us  [_issue(): self.ahead = lax.ppermute(self.ahead, 'site', self.forward)]
    ppermute x8, waiting for transfers between devices: 29.6 us -> 31.3 us  [_issue(): self.ahead = lax.ppermute(self.ahead, 'site', self.forward)]
    ppermute x1, starting transfers between devices: 1.7 us -> 3.3 us  [last_round(): other_part = lax.ppermute(send.reshape(rest), ('section', 'site'), across)]
    ppermute x1, waiting for transfers between devices: 1.43 us -> 0.01 us  [last_round(): mine_part = lax.ppermute(own, ('section', 'site'), forward)]
    another operation x1 -> x0, local copies, waits for them, and re-layouts: 1.31 us -> none  [heads_split(): patches[0].reshape(tiles_here, group_size, -1).at[:, in_sources]]
    unnamed x36 -> x33, local copies, waits for them, and re-layouts: 7.58 us -> 6.65 us
  transfers between devices with their start and end apart: 22 -> 22, of which waited for: 16 -> 14; matrix products, arithmetic and copies ran while one was open for 16% -> 15% of each run, Pallas kernels for 0% -> 0%
where the time goes in v13:
time: 131 us
  waiting for transfers between devices  54.2 us (41%)
  starting transfers between devices  34.5 us (26%)
  local copies, waits for them, and re-layouts  13.2 us (10%)
  Pallas kernels  12.4 us (9%)
  matrix products  9.03 us (7%)
  other arithmetic  7.22 us (6%)
    ppermute x8, waiting for transfers between devices, _issue(): self.ahead = lax.ppermute(self.ahead, 'site', self.forward)  31.3 us
    ppermute x8, starting transfers between devices, _issue(): self.ahead = lax.ppermute(self.ahead, 'site', self.forward)  13.8 us
    ppermute x3, waiting for transfers between devices, doubling_sum(): state = state + lax.ppermute(state, 'site', xor_pairs(count, bit))  12.4 us
    pallas_call x1, Pallas kernels, gated_ffn(): pl.pallas_call(ffn_block, grid=(units // block,), in_specs=[pl.BlockSpec(...  12.4 us
    ppermute x2, waiting for transfers between devices, last_round(): state = keep + lax.ppermute(send, 'site', xor_pairs(group_size, bit))  8.7 us
    unnamed x33, local copies, waits for them, and re-layouts  6.65 us
    all_to_all x1, starting transfers between devices, heads_split(): lax.all_to_all(col_blocks, 'site', split_axis=0, concat_axis=0, tiled=True)  6.24 us
    ppermute x6, starting transfers between devices, _issue(): self.behind = lax.ppermute(self.behind, 'site', self.backward)  5.59 us
  transfers between devices with their start and end apart: 22, of which 14 were waited for; matrix products, arithmetic and copies ran while one was open for 15% of the time, Pallas kernels for 0%

profile of v13, /device:TPU:0, one launch (start us, length us, event | category | flops | bytes accessed | tf_op | source)
XLA Modules:
  0.0 130.8 jit_solution(3341965423957713294)
XLA Ops:
  0.0 0.9 reduce.1
  0.9 0.9 pad_maximum_fusion
  1.9 3.1 %collective-permute-start = (bf16[136,512]{1,0:T(8,128)(2,1)S(1)}, bf16[136,512]{1,0:T(8,128)(2,1)S(1)}, u32[]{:S(2)}, u32[]{:S(2)}) collective-permute-start(bf16[136,512]{1,0:T(8,128)(2,1)S(1)} %pad_maximum_fusion), channel_id=1, source_target_pairs={{0,2},{2,4},{4,6},{6,7},{7,5},{5,3},{3,1},{1,0},{8,10},{10,12},{12... | collective-permute-start | bytes 417800 | tf_op jit(solution)/shard_map/ppermute | solution.py:163
  5.0 1.2 copy.26
  6.2 0.4 copy.30
  6.6 1.1 reshape.280
  7.7 6.2 %all-to-all-start = ((bf16[8,64,512]{2,1,0:T(8,128)(2,1)}), bf16[8,64,512]{2,1,0:T(8,128)(2,1)}, u32[]{:S(2)}, u32[]{:S(2)}) async-start(bf16[8,64,512]{2,1,0:T(8,128)(2,1)} %reshape.280), calls=%async_computation | async-start | bytes 1048576 | tf_op jit(solution)/shard_map/all_to_all | solution.py:469
  14.0 0.1 add_bitcast_fusion
  14.1 0.1 iota_compare_fusion
  14.2 3.1 %convert_reduce_fusion = f32[8,2048]{1,0:T(8,128)S(1)} fusion(s32[2048]{0:T(1024)S(1)} %bitcast.149, s32[8,256]{1,0:T(8,128)S(1)} %copy-done.4, pred[8,256]{1,0:T(8,128)(4,1)S(1)} %iota_compare_fusion), kind=kLoop, calls=%fused_computation.2 | loop fusion | flops 16760832 | bytes 83968 | tf_op jit(solution)/shard_map/reduce_sum | solution.py:493
  17.3 2.1 %collective-permute-start.1 = (bf16[136,512]{1,0:T(8,128)(2,1)S(1)}, bf16[136,512]{1,0:T(8,128)(2,1)S(1)}, u32[]{:S(2)}, u32[]{:S(2)}) collective-permute-start(bf16[136,512]{1,0:T(8,128)(2,1)S(1)} %collective-permute-done), channel_id=1, source_target_pairs={{0,2},{2,4},{4,6},{6,7},{7,5},{5,3},{3,1},{1,0},{8,10},{10,12},{12... | collective-permute-start | bytes 417800 | tf_op jit(solution)/shard_map/ppermute | solution.py:163
  19.4 0.1 collective-permute-start.5
  19.5 5.5 %collective-permute-done.1 = bf16[136,512]{1,0:T(8,128)(2,1)S(1)} collective-permute-done((bf16[136,512]{1,0:T(8,128)(2,1)S(1)}, bf16[136,512]{1,0:T(8,128)(2,1)S(1)}, u32[]{:S(2)}, u32[]{:S(2)}) %collective-permute-start.1) | collective-permute-done | bytes 139296 | tf_op jit(solution)/shard_map/ppermute | solution.py:163
  25.0 4.2 %collective-permute-start.2 = (bf16[136,512]{1,0:T(8,128)(2,1)S(1)}, bf16[136,512]{1,0:T(8,128)(2,1)S(1)}, u32[]{:S(2)}, u32[]{:S(2)}) collective-permute-start(bf16[136,512]{1,0:T(8,128)(2,1)S(1)} %collective-permute-done.1), channel_id=1, source_target_pairs={{0,2},{2,4},{4,6},{6,7},{7,5},{5,3},{3,1},{1,0},{8,10},{10,12},{12... | collective-permute-start | bytes 417800 | tf_op jit(solution)/shard_map/ppermute | solution.py:163
  29.2 2.6 %collective-permute-done.2 = bf16[136,512]{1,0:T(8,128)(2,1)S(1)} collective-permute-done((bf16[136,512]{1,0:T(8,128)(2,1)S(1)}, bf16[136,512]{1,0:T(8,128)(2,1)S(1)}, u32[]{:S(2)}, u32[]{:S(2)}) %collective-permute-start.2) | collective-permute-done | bytes 139296 | tf_op jit(solution)/shard_map/ppermute | solution.py:163
  31.8 2.5 %collective-permute-start.3 = (bf16[136,512]{1,0:T(8,128)(2,1)S(1)}, bf16[136,512]{1,0:T(8,128)(2,1)S(1)}, u32[]{:S(2)}, u32[]{:S(2)}) collective-permute-start(bf16[136,512]{1,0:T(8,128)(2,1)S(1)} %collective-permute-done.2), channel_id=1, source_target_pairs={{0,2},{2,4},{4,6},{6,7},{7,5},{5,3},{3,1},{1,0},{8,10},{10,12},{12... | collective-permute-start | bytes 417800 | tf_op jit(solution)/shard_map/ppermute | solution.py:163
  34.3 4.6 %collective-permute-done.3 = bf16[136,512]{1,0:T(8,128)(2,1)S(1)} collective-permute-done((bf16[136,512]{1,0:T(8,128)(2,1)S(1)}, bf16[136,512]{1,0:T(8,128)(2,1)S(1)}, u32[]{:S(2)}, u32[]{:S(2)}) %collective-permute-start.3) | collective-permute-done | bytes 139296 | tf_op jit(solution)/shard_map/ppermute | solution.py:163
  39.0 1.0 copy-done.1
  40.0 0.1 slice.24
  40.1 1.6 %gather_fusion.1 = bf16[8,128,512]{2,1,0:T(8,128)(2,1)} fusion(bf16[8,128,512]{2,1,0:T(8,128)(2,1)S(1)} %slice.24, s32[1024]{0:T(1024)S(1)} %pad_clamp_fusion), kind=kCustom, calls=%fused_computation.1 | custom fusion | bytes 2097184 | tf_op jit(solution)/shard_map/gather | solution.py:457
  41.7 2.6 %bitcast_dynamic-update-slice_fusion.7 = (bf16[8,256,512]{2,1,0:T(8,128)(2,1)}, bf16[256,512]{1,0:T(8,128)(2,1)S(1)}) fusion(bf16[1024,512]{1,0:T(8,128)(2,1)} %bitcast.143, bf16[1,256,1024]{2,1,0:T(8,128)(2,1)} %param.16), kind=kOutput, calls=%fused_computation.40 | convolution fusion | flops 269615104 | bytes 2097152 | tf_op jit(solution)/shard_map/dot_general | solution.py:461
  44.4 0.4 collective-permute-start.7
  44.8 0.8 slice.23
  45.6 1.6 %collective-permute-start.11 = (bf16[256,512]{1,0:T(8,128)(2,1)S(1)}, bf16[256,512]{1,0:T(8,128)(2,1)S(1)}, u32[]{:S(2)}, u32[]{:S(2)}) collective-permute-start(bf16[256,512]{1,0:T(8,128)(2,1)S(1)} %get-tuple-element.8), channel_id=1, source_target_pairs={{0,1},{2,0},{4,2},{6,4},{7,6},{5,7},{3,5},{1,3},{8,9},{10,8},{12,1... | collective-permute-start | bytes 786440 | tf_op jit(solution)/shard_map/ppermute | solution.py:167
  47.3 0.5 gather_fusion
  47.9 4.0 %collective-permute-done.7 = bf16[256,512]{1,0:T(8,128)(2,1)S(1)} collective-permute-done((bf16[256,512]{1,0:T(8,128)(2,1)S(1)}, bf16[256,512]{1,0:T(8,128)(2,1)S(1)}, u32[]{:S(2)}, u32[]{:S(2)}) %collective-permute-start.7) | collective-permute-done | bytes 262176 | tf_op jit(solution)/shard_map/ppermute | solution.py:163
  51.9 0.8 collective-permute-start.8
  52.7 2.3 %bitcast_reduce_fusion.1 = (f32[8,2]{0,1:T(2,128)S(1)}, f32[8,256]{1,0:T(8,128)S(1)}) fusion(bf16[8,4096]{1,0:T(8,128)(2,1)S(1)} %bitcast.148, bf16[1,256,4096]{2,1,0:T(8,128)(2,1)} %param.19), kind=kOutput, calls=%fused_computation.65 | convolution fusion | flops 16785392 | bytes 2170944 | tf_op jit(solution)/shard_map/dot_general | solution.py:23
  55.0 6.0 %collective-permute-done.8 = bf16[256,512]{1,0:T(8,128)(2,1)S(1)} collective-permute-done((bf16[256,512]{1,0:T(8,128)(2,1)S(1)}, bf16[256,512]{1,0:T(8,128)(2,1)S(1)}, u32[]{:S(2)}, u32[]{:S(2)}) %collective-permute-start.8) | collective-permute-done | bytes 262176 | tf_op jit(solution)/shard_map/ppermute | solution.py:163
  61.0 0.8 collective-permute-start.9
  61.8 2.1 %collective-permute-start.12 = (bf16[256,512]{1,0:T(8,128)(2,1)S(1)}, bf16[256,512]{1,0:T(8,128)(2,1)S(1)}, u32[]{:S(2)}, u32[]{:S(2)}) collective-permute-start(bf16[256,512]{1,0:T(8,128)(2,1)S(1)} %collective-permute-done.11), channel_id=1, source_target_pairs={{0,1},{2,0},{4,2},{6,4},{7,6},{5,7},{3,5},{1,3},{8,9},{10,8},{12,1... | collective-permute-start | bytes 786440 | tf_op jit(solution)/shard_map/ppermute | solution.py:167
  63.9 0.7 bitcast_dynamic-update-slice_fusion.6
  64.7 5.6 %collective-permute-done.9 = bf16[256,512]{1,0:T(8,128)(2,1)S(1)} collective-permute-done((bf16[256,512]{1,0:T(8,128)(2,1)S(1)}, bf16[256,512]{1,0:T(8,128)(2,1)S(1)}, u32[]{:S(2)}, u32[]{:S(2)}) %collective-permute-start.9) | collective-permute-done | bytes 262176 | tf_op jit(solution)/shard_map/ppermute | solution.py:163
  70.3 0.7 bitcast_dynamic-update-slice_fusion.5
  71.0 0.3 collective-permute-done.12
  71.3 1.7 %collective-permute-start.13 = (bf16[256,512]{1,0:T(8,128)(2,1)S(1)}, bf16[256,512]{1,0:T(8,128)(2,1)S(1)}, u32[]{:S(2)}, u32[]{:S(2)}) collective-permute-start(bf16[256,512]{1,0:T(8,128)(2,1)S(1)} %collective-permute-done.12), channel_id=1, source_target_pairs={{0,1},{2,0},{4,2},{6,4},{7,6},{5,7},{3,5},{1,3},{8,9},{10,8},{12,1... | collective-permute-start | bytes 786440 | tf_op jit(solution)/shard_map/ppermute | solution.py:167
  73.0 0.7 bitcast_dynamic-update-slice_fusion.4
  73.8 2.9 %collective-permute-done.10 = bf16[256,512]{1,0:T(8,128)(2,1)S(1)} collective-permute-done((bf16[256,512]{1,0:T(8,128)(2,1)S(1)}, bf16[256,512]{1,0:T(8,128)(2,1)S(1)}, u32[]{:S(2)}, u32[]{:S(2)}) %collective-permute-start.10) | collective-permute-done | bytes 262176 | tf_op jit(solution)/shard_map/ppermute | solution.py:163
  76.7 0.7 bitcast_dynamic-update-slice_fusion.3
  77.4 0.7 bitcast_dynamic-update-slice_fusion.2
  78.1 0.7 bitcast_dynamic-update-slice_fusion.1
  78.8 0.8 bitcast_dynamic-update-slice_fusion
  79.6 3.0 %fusion.40 = f32[2048,512]{0,1:T(8,128)S(1)} fusion(bf16[2048,512]{1,0:T(8,128)(2,1)} %bitcast.21, bf16[512,512]{1,0:T(8,128)(2,1)} %bitcast.23), kind=kOutput, calls=%fused_computation.100 | convolution fusion | flops 1073741824 | bytes 6815744 | tf_op jit(solution)/shard_map/dot_general | solution.py:480
  82.6 0.1 slice.32
  82.7 0.2 bitcast_reduce_fusion
  82.9 0.2 fusion.7
  83.2 0.3 fusion.2
  83.5 0.8 convolution_bitcast_fusion
  84.3 1.8 %collective-permute-start.14 = (f32[8,1,4096]{2,0,1:T(8,128)S(1)}, f32[8,1,4096]{2,0,1:T(8,128)S(1)}, u32[]{:S(2)}, u32[]{:S(2)}) collective-permute-start(f32[8,1,4096]{2,0,1:T(8,128)S(1)} %convolution_bitcast_fusion), channel_id=1, source_target_pairs={{0,1},{1,0},{2,3},{3,2},{4,5},{5,4},{6,7},{7,6},{8,9},{9,8},{10,11... | collective-permute-start | bytes 393224 | tf_op jit(solution)/shard_map/ppermute | solution.py:116
  86.1 3.2 %collective-permute-done.14 = f32[8,1,4096]{2,0,1:T(8,128)S(1)} collective-permute-done((f32[8,1,4096]{2,0,1:T(8,128)S(1)}, f32[8,1,4096]{2,0,1:T(8,128)S(1)}, u32[]{:S(2)}, u32[]{:S(2)}) %collective-permute-start.14) | collective-permute-done | bytes 131104 | tf_op jit(solution)/shard_map/ppermute | solution.py:116
  89.3 1.3 %collective-permute-start.15 = (f32[8,1,4096]{2,0,1:T(8,128)S(1)}, f32[8,1,4096]{2,0,1:T(8,128)S(1)}, u32[]{:S(2)}, u32[]{:S(2)}) collective-permute-start(f32[8,1,4096]{2,0,1:T(8,128)S(1)} %add.207), channel_id=1, source_target_pairs={{0,2},{1,3},{2,0},{3,1},{4,6},{5,7},{6,4},{7,5},{8,10},{9,11},{10,... | collective-permute-start | bytes 393224 | tf_op jit(solution)/shard_map/ppermute | solution.py:116
  90.6 3.7 %collective-permute-done.15 = f32[8,1,4096]{2,0,1:T(8,128)S(1)} collective-permute-done((f32[8,1,4096]{2,0,1:T(8,128)S(1)}, f32[8,1,4096]{2,0,1:T(8,128)S(1)}, u32[]{:S(2)}, u32[]{:S(2)}) %collective-permute-start.15) | collective-permute-done | bytes 131104 | tf_op jit(solution)/shard_map/ppermute | solution.py:116
  94.3 1.8 %collective-permute-start.16 = (f32[8,1,4096]{2,0,1:T(8,128)S(1)}, f32[8,1,4096]{2,0,1:T(8,128)S(1)}, u32[]{:S(2)}, u32[]{:S(2)}) collective-permute-start(f32[8,1,4096]{2,0,1:T(8,128)S(1)} %add.208), channel_id=1, source_target_pairs={{0,4},{1,5},{2,6},{3,7},{4,0},{5,1},{6,2},{7,3},{8,12},{9,13},{10,... | collective-permute-start | bytes 393224 | tf_op jit(solution)/shard_map/ppermute | solution.py:116
  96.2 5.5 %collective-permute-done.16 = f32[8,1,4096]{2,0,1:T(8,128)S(1)} collective-permute-done((f32[8,1,4096]{2,0,1:T(8,128)S(1)}, f32[8,1,4096]{2,0,1:T(8,128)S(1)}, u32[]{:S(2)}, u32[]{:S(2)}) %collective-permute-start.16) | collective-permute-done | bytes 131104 | tf_op jit(solution)/shard_map/ppermute | solution.py:116
  101.7 0.1 multiply_reduce_fusion
  101.9 0.7 fusion.24.rows_ref
  102.6 12.4 %shard_map.145 = f32[8,4096]{1,0:T(8,128)} custom-call(bf16[8,4096]{1,0:T(8,128)(2,1)} %fusion.24.rows_ref, bf16[896,4096]{1,0:T(8,128)(2,1)} %bitcast.136, bf16[896,4096]{1,0:T(8,128)(2,1)} %bitcast.137, bf16[896,4096]{1,0:T(8,128)(2,1)} %bitcast.138), custom_call_target="tpu_custom_call" | custom-call | tf_op jit(solution)/shard_map/pallas_call | solution.py:396
  114.9 1.0 reshape_reshape.4
  116.0 0.5 collective-permute-start.17
  116.5 4.8 %collective-permute-done.17 = f32[1,2,2,1,4096]{4,2,1,0,3:T(2,128)S(1)} collective-permute-done((f32[1,2,2,1,4096]{4,2,1,0,3:T(2,128)S(1)}, f32[1,2,2,1,4096]{4,2,1,0,3:T(2,128)S(1)}, u32[]{:S(2)}, u32[]{:S(2)}) %collective-permute-start.17) | collective-permute-done | bytes 65568 | tf_op jit(solution)/shard_map/ppermute | solution.py:523
  121.4 3.9 %collective-permute-done.18 = f32[1,1,2,1,4096]{4,2,1,0,3:T(2,128)S(1)} collective-permute-done((f32[1,1,2,1,4096]{4,2,1,0,3:T(2,128)S(1)}, f32[1,1,2,1,4096]{4,2,1,0,3:T(2,128)S(1)}, u32[]{:S(2)}, u32[]{:S(2)}) %collective-permute-start.18) | collective-permute-done | bytes 32800 | tf_op jit(solution)/shard_map/ppermute | solution.py:523
  125.5 3.3 %collective-permute-start.20 = (f32[1,4096]{1,0:T(1,128)S(1)}, f32[1,4096]{1,0:T(1,128)S(1)}, u32[]{:S(2)}, u32[]{:S(2)}) collective-permute-start(f32[1,4096]{1,0:T(1,128)S(1)} %dynamic-slice_bitcast_fusion), channel_id=1, source_target_pairs={{0,9},{1,8},{2,11},{3,10},{4,13},{5,12},{6,15},{7,14},{8,17},{9,16... | collective-permute-start | bytes 49160 | tf_op jit(solution)/shard_map/ppermute | solution.py:540
  128.8 1.4 %collective-permute-done.20 = f32[1,4096]{1,0:T(1,128)S(1)} collective-permute-done((f32[1,4096]{1,0:T(1,128)S(1)}, f32[1,4096]{1,0:T(1,128)S(1)}, u32[]{:S(2)}, u32[]{:S(2)}) %collective-permute-start.20) | collective-permute-done | bytes 16416 | tf_op jit(solution)/shard_map/ppermute | solution.py:540
  130.2 0.6 convert_bitcast_fusion
  (58 shorter events, 0.6 us)
Async XLA Ops:
  0.0 83.5 %copy-start = (bf16[1,256,4096]{2,1,0:T(8,128)(2,1)S(1)}, bf16[1,256,4096]{2,1,0:T(8,128)(2,1)}, u32[]{:S(2)}) copy-start(bf16[1,256,4096]{2,1,0:T(8,128)(2,1)} %param.24) | copy-start | bytes 6291460
  1.9 15.5 %collective-permute-start = (bf16[136,512]{1,0:T(8,128)(2,1)S(1)}, bf16[136,512]{1,0:T(8,128)(2,1)S(1)}, u32[]{:S(2)}, u32[]{:S(2)}) collective-permute-start(bf16[136,512]{1,0:T(8,128)(2,1)S(1)} %pad_maximum_fusion), channel_id=1, source_target_pairs={{0,2},{2,4},{4,6},{6,7},{7,5},{5,3},{3,1},{1,0},{8,10},{10,12},{12... | collective-permute-start | bytes 417800 | tf_op jit(solution)/shard_map/ppermute | solution.py:163
  4.9 14.5 %collective-permute-start.4 = (bf16[136,512]{1,0:T(8,128)(2,1)S(1)}, bf16[136,512]{1,0:T(8,128)(2,1)S(1)}, u32[]{:S(2)}, u32[]{:S(2)}) collective-permute-start(bf16[136,512]{1,0:T(8,128)(2,1)S(1)} %pad_maximum_fusion), channel_id=1, source_target_pairs={{0,1},{2,0},{4,2},{6,4},{7,6},{5,7},{3,5},{1,3},{8,9},{10,8},{12,1... | collective-permute-start | bytes 417800 | tf_op jit(solution)/shard_map/ppermute | solution.py:167
  4.9 9.0 %copy-start.8 = (s32[8]{0:T(128)S(1)}, s32[8]{0:T(128)}, u32[]{:S(2)}) copy-start(s32[8]{0:T(128)} %constant.139.clone) | copy-start | bytes 100
  4.9 9.1 %copy-start.5 = (s32[8]{0:T(128)S(1)}, s32[8]{0:T(128)}, u32[]{:S(2)}) copy-start(s32[8]{0:T(128)} %param.18) | copy-start | bytes 100
  4.9 9.2 %copy-start.4 = (s32[8,256]{1,0:T(8,128)S(1)}, s32[8,256]{1,0:T(8,128)}, u32[]{:S(2)}) copy-start(s32[8,256]{1,0:T(8,128)} %param.17) | copy-start | bytes 24580
  5.0 12.4 %copy-start.2 = (bf16[1,128,512]{2,1,0:T(8,128)(2,1)S(1)}, bf16[1,128,512]{2,1,0:T(8,128)(2,1)}, u32[]{:S(2)}) copy-start(bf16[1,128,512]{2,1,0:T(8,128)(2,1)} %param.22) | copy-start | bytes 393220
  7.7 71.9 %all-to-all-start = ((bf16[8,64,512]{2,1,0:T(8,128)(2,1)}), bf16[8,64,512]{2,1,0:T(8,128)(2,1)}, u32[]{:S(2)}, u32[]{:S(2)}) async-start(bf16[8,64,512]{2,1,0:T(8,128)(2,1)} %reshape.280), calls=%async_computation | async-start | bytes 1048576 | tf_op jit(solution)/shard_map/all_to_all | solution.py:469
  17.3 7.7 %collective-permute-start.1 = (bf16[136,512]{1,0:T(8,128)(2,1)S(1)}, bf16[136,512]{1,0:T(8,128)(2,1)S(1)}, u32[]{:S(2)}, u32[]{:S(2)}) collective-permute-start(bf16[136,512]{1,0:T(8,128)(2,1)S(1)} %collective-permute-done), channel_id=1, source_target_pairs={{0,2},{2,4},{4,6},{6,7},{7,5},{5,3},{3,1},{1,0},{8,10},{10,12},{12... | collective-permute-start | bytes 417800 | tf_op jit(solution)/shard_map/ppermute | solution.py:163
  19.4 9.8 %collective-permute-start.5 = (bf16[136,512]{1,0:T(8,128)(2,1)S(1)}, bf16[136,512]{1,0:T(8,128)(2,1)S(1)}, u32[]{:S(2)}, u32[]{:S(2)}) collective-permute-start(bf16[136,512]{1,0:T(8,128)(2,1)S(1)} %collective-permute-done.4), channel_id=1, source_target_pairs={{0,1},{2,0},{4,2},{6,4},{7,6},{5,7},{3,5},{1,3},{8,9},{10,8},{12,1... | collective-permute-start | bytes 417800 | tf_op jit(solution)/shard_map/ppermute | solution.py:167
  25.0 6.8 %collective-permute-start.2 = (bf16[136,512]{1,0:T(8,128)(2,1)S(1)}, bf16[136,512]{1,0:T(8,128)(2,1)S(1)}, u32[]{:S(2)}, u32[]{:S(2)}) collective-permute-start(bf16[136,512]{1,0:T(8,128)(2,1)S(1)} %collective-permute-done.1), channel_id=1, source_target_pairs={{0,2},{2,4},{4,6},{6,7},{7,5},{5,3},{3,1},{1,0},{8,10},{10,12},{12... | collective-permute-start | bytes 417800 | tf_op jit(solution)/shard_map/ppermute | solution.py:163
  29.2 9.8 %collective-permute-start.6 = (bf16[136,512]{1,0:T(8,128)(2,1)S(1)}, bf16[136,512]{1,0:T(8,128)(2,1)S(1)}, u32[]{:S(2)}, u32[]{:S(2)}) collective-permute-start(bf16[136,512]{1,0:T(8,128)(2,1)S(1)} %collective-permute-done.5), channel_id=1, source_target_pairs={{0,1},{2,0},{4,2},{6,4},{7,6},{5,7},{3,5},{1,3},{8,9},{10,8},{12,1... | collective-permute-start | bytes 417800 | tf_op jit(solution)/shard_map/ppermute | solution.py:167
  31.8 7.1 %collective-permute-start.3 = (bf16[136,512]{1,0:T(8,128)(2,1)S(1)}, bf16[136,512]{1,0:T(8,128)(2,1)S(1)}, u32[]{:S(2)}, u32[]{:S(2)}) collective-permute-start(bf16[136,512]{1,0:T(8,128)(2,1)S(1)} %collective-permute-done.2), channel_id=1, source_target_pairs={{0,2},{2,4},{4,6},{6,7},{7,5},{5,3},{3,1},{1,0},{8,10},{10,12},{12... | collective-permute-start | bytes 417800 | tf_op jit(solution)/shard_map/ppermute | solution.py:163
  39.0 1.0 copy-start.1
  41.7 3.1 %copy-start.6 = (f32[1,128]{1,0:T(1,128)S(1)}, f32[1,128]{1,0:T(1,128)}, u32[]{:S(2)}) copy-start(f32[1,128]{1,0:T(1,128)} %param.21) | copy-start | bytes 1540
  41.7 3.1 %copy-start.7 = (f32[1,128]{1,0:T(1,128)S(1)}, f32[1,128]{1,0:T(1,128)}, u32[]{:S(2)}) copy-start(f32[1,128]{1,0:T(1,128)} %param.20) | copy-start | bytes 1540
  44.4 7.5 %collective-permute-start.7 = (bf16[256,512]{1,0:T(8,128)(2,1)S(1)}, bf16[256,512]{1,0:T(8,128)(2,1)S(1)}, u32[]{:S(2)}, u32[]{:S(2)}) collective-permute-start(bf16[256,512]{1,0:T(8,128)(2,1)S(1)} %get-tuple-element.8), channel_id=1, source_target_pairs={{0,2},{2,4},{4,6},{6,7},{7,5},{5,3},{3,1},{1,0},{8,10},{10,12},{12... | collective-permute-start | bytes 786440 | tf_op jit(solution)/shard_map/ppermute | solution.py:163
  45.6 16.2 %collective-permute-start.11 = (bf16[256,512]{1,0:T(8,128)(2,1)S(1)}, bf16[256,512]{1,0:T(8,128)(2,1)S(1)}, u32[]{:S(2)}, u32[]{:S(2)}) collective-permute-start(bf16[256,512]{1,0:T(8,128)(2,1)S(1)} %get-tuple-element.8), channel_id=1, source_target_pairs={{0,1},{2,0},{4,2},{6,4},{7,6},{5,7},{3,5},{1,3},{8,9},{10,8},{12,1... | collective-permute-start | bytes 786440 | tf_op jit(solution)/shard_map/ppermute | solution.py:167
  51.9 9.1 %collective-permute-start.8 = (bf16[256,512]{1,0:T(8,128)(2,1)S(1)}, bf16[256,512]{1,0:T(8,128)(2,1)S(1)}, u32[]{:S(2)}, u32[]{:S(2)}) collective-permute-start(bf16[256,512]{1,0:T(8,128)(2,1)S(1)} %collective-permute-done.7), channel_id=1, source_target_pairs={{0,2},{2,4},{4,6},{6,7},{7,5},{5,3},{3,1},{1,0},{8,10},{10,12},{12... | collective-permute-start | bytes 786440 | tf_op jit(solution)/shard_map/ppermute | solution.py:163
  61.0 9.3 %collective-permute-start.9 = (bf16[256,512]{1,0:T(8,128)(2,1)S(1)}, bf16[256,512]{1,0:T(8,128)(2,1)S(1)}, u32[]{:S(2)}, u32[]{:S(2)}) collective-permute-start(bf16[256,512]{1,0:T(8,128)(2,1)S(1)} %collective-permute-done.8), channel_id=1, source_target_pairs={{0,2},{2,4},{4,6},{6,7},{7,5},{5,3},{3,1},{1,0},{8,10},{10,12},{12... | collective-permute-start | bytes 786440 | tf_op jit(solution)/shard_map/ppermute | solution.py:163
  61.8 9.5 %collective-permute-start.12 = (bf16[256,512]{1,0:T(8,128)(2,1)S(1)}, bf16[256,512]{1,0:T(8,128)(2,1)S(1)}, u32[]{:S(2)}, u32[]{:S(2)}) collective-permute-start(bf16[256,512]{1,0:T(8,128)(2,1)S(1)} %collective-permute-done.11), channel_id=1, source_target_pairs={{0,1},{2,0},{4,2},{6,4},{7,6},{5,7},{3,5},{1,3},{8,9},{10,8},{12,1... | collective-permute-start | bytes 786440 | tf_op jit(solution)/shard_map/ppermute | solution.py:167
  70.3 6.4 %collective-permute-start.10 = (bf16[256,512]{1,0:T(8,128)(2,1)S(1)}, bf16[256,512]{1,0:T(8,128)(2,1)S(1)}, u32[]{:S(2)}, u32[]{:S(2)}) collective-permute-start(bf16[256,512]{1,0:T(8,128)(2,1)S(1)} %collective-permute-done.9), channel_id=1, source_target_pairs={{0,2},{2,4},{4,6},{6,7},{7,5},{5,3},{3,1},{1,0},{8,10},{10,12},{12... | collective-permute-start | bytes 786440 | tf_op jit(solution)/shard_map/ppermute | solution.py:163
  71.3 7.5 %collective-permute-start.13 = (bf16[256,512]{1,0:T(8,128)(2,1)S(1)}, bf16[256,512]{1,0:T(8,128)(2,1)S(1)}, u32[]{:S(2)}, u32[]{:S(2)}) collective-permute-start(bf16[256,512]{1,0:T(8,128)(2,1)S(1)} %collective-permute-done.12), channel_id=1, source_target_pairs={{0,1},{2,0},{4,2},{6,4},{7,6},{5,7},{3,5},{1,3},{8,9},{10,8},{12,1... | collective-permute-start | bytes 786440 | tf_op jit(solution)/shard_map/ppermute | solution.py:167
  83.5 18.3 %copy-start.3 = (f32[1,4096]{1,0:T(1,128)S(1)}, f32[1,4096]{1,0:T(1,128)}, u32[]{:S(2)}) copy-start(f32[1,4096]{1,0:T(1,128)} %param.25) | copy-start | bytes 49156
  84.3 5.0 %collective-permute-start.14 = (f32[8,1,4096]{2,0,1:T(8,128)S(1)}, f32[8,1,4096]{2,0,1:T(8,128)S(1)}, u32[]{:S(2)}, u32[]{:S(2)}) collective-permute-start(f32[8,1,4096]{2,0,1:T(8,128)S(1)} %convolution_bitcast_fusion), channel_id=1, source_target_pairs={{0,1},{1,0},{2,3},{3,2},{4,5},{5,4},{6,7},{7,6},{8,9},{9,8},{10,11... | collective-permute-start | bytes 393224 | tf_op jit(solution)/shard_map/ppermute | solution.py:116
  89.3 5.0 %collective-permute-start.15 = (f32[8,1,4096]{2,0,1:T(8,128)S(1)}, f32[8,1,4096]{2,0,1:T(8,128)S(1)}, u32[]{:S(2)}, u32[]{:S(2)}) collective-permute-start(f32[8,1,4096]{2,0,1:T(8,128)S(1)} %add.207), channel_id=1, source_target_pairs={{0,2},{1,3},{2,0},{3,1},{4,6},{5,7},{6,4},{7,5},{8,10},{9,11},{10,... | collective-permute-start | bytes 393224 | tf_op jit(solution)/shard_map/ppermute | solution.py:116
  94.3 7.3 %collective-permute-start.16 = (f32[8,1,4096]{2,0,1:T(8,128)S(1)}, f32[8,1,4096]{2,0,1:T(8,128)S(1)}, u32[]{:S(2)}, u32[]{:S(2)}) collective-permute-start(f32[8,1,4096]{2,0,1:T(8,128)S(1)} %add.208), channel_id=1, source_target_pairs={{0,4},{1,5},{2,6},{3,7},{4,0},{5,1},{6,2},{7,3},{8,12},{9,13},{10,... | collective-permute-start | bytes 393224 | tf_op jit(solution)/shard_map/ppermute | solution.py:116
  116.0 5.3 %collective-permute-start.17 = (f32[1,2,2,1,4096]{4,2,1,0,3:T(2,128)S(1)}, f32[1,2,2,1,4096]{4,2,1,0,3:T(2,128)S(1)}, u32[]{:S(2)}, u32[]{:S(2)}) collective-permute-start(f32[1,2,2,1,4096]{4,2,1,0,3:T(2,128)S(1)} %constant_dynamic-slice_fusion.1), channel_id=1, source_target_pairs={{0,4},{1,5},{2,6},{3,7},{4,0},{5,1},{6,2},{7,3},{8,12},{9,13},{10,... | collective-permute-start | bytes 196616 | tf_op jit(solution)/shard_map/ppermute | solution.py:523
  121.3 4.0 %collective-permute-start.18 = (f32[1,1,2,1,4096]{4,2,1,0,3:T(2,128)S(1)}, f32[1,1,2,1,4096]{4,2,1,0,3:T(2,128)S(1)}, u32[]{:S(2)}, u32[]{:S(2)}) collective-permute-start(f32[1,1,2,1,4096]{4,2,1,0,3:T(2,128)S(1)} %constant_dynamic-slice_fusion), channel_id=1, source_target_pairs={{0,2},{1,3},{2,0},{3,1},{4,6},{5,7},{6,4},{7,5},{8,10},{9,11},{10,... | collective-permute-start | bytes 98312 | tf_op jit(solution)/shard_map/ppermute | solution.py:523
  125.4 3.4 %collective-permute-start.19 = (f32[1,4096]{1,0:T(1,128)S(1)}, f32[1,4096]{1,0:T(1,128)S(1)}, u32[]{:S(2)}, u32[]{:S(2)}) collective-permute-start(f32[1,4096]{1,0:T(1,128)S(1)} %bitcast_add_fusion), channel_id=1, source_target_pairs={{0,8},{1,9},{2,10},{3,11},{4,12},{5,13},{6,14},{7,15},{8,16},{9,17... | collective-permute-start | bytes 49160 | tf_op jit(solution)/shard_map/ppermute | solution.py:539
  125.5 4.7 %collective-permute-start.20 = (f32[1,4096]{1,0:T(1,128)S(1)}, f32[1,4096]{1,0:T(1,128)S(1)}, u32[]{:S(2)}, u32[]{:S(2)}) collective-permute-start(f32[1,4096]{1,0:T(1,128)S(1)} %dynamic-slice_bitcast_fusion), channel_id=1, source_target_pairs={{0,9},{1,8},{2,11},{3,10},{4,13},{5,12},{6,15},{7,14},{8,17},{9,16... | collective-permute-start | bytes 49160 | tf_op jit(solution)/shard_map/ppermute | solution.py:540

commit v14 on v12

--- a/solution.py
+++ b/solution.py
@@ -445,6 +445,15 @@
     )
     in_slots, in_sources = ring_in.finish()
     in_rows = tile_in.shape[1]
+    kv_width = tile_out.shape[-1]
+    my_cols = heads_here * head_size
+    col_blocks = tile_out[0].reshape(tile_out.shape[1], 2, group_size, my_cols)
+    col_blocks = jnp.transpose(col_blocks, (2, 0, 1, 3)).reshape(group_size, tile_out.shape[1], 2 * my_cols)
+    in_slots, col_blocks = lax.optimization_barrier((in_slots, col_blocks))
+    weight_out = lax.all_to_all(col_blocks, "site", split_axis=0, concat_axis=0, tiled=True)
+    weight_out = weight_out.reshape(-1, 2 * my_cols)
+    del kv_width
+
     everyone = (
         in_slots[:, in_rows:]
         .at[ring_in.slot_of_source]
@@ -460,19 +469,12 @@
         approximate=True,
     ).astype(jnp.bfloat16)
 
-    kv_width = tile_out.shape[-1]
-    my_cols = heads_here * head_size
-    col_blocks = tile_out[0].reshape(tile_out.shape[1], 2, group_size, my_cols)
-    col_blocks = jnp.transpose(col_blocks, (2, 0, 1, 3)).reshape(group_size, tile_out.shape[1], 2 * my_cols)
-    weight_out = lax.all_to_all(col_blocks, "site", split_axis=0, concat_axis=0, tiled=True)
-    weight_out = weight_out.reshape(-1, 2 * my_cols)
-    del kv_width
-
     q_part = by_rows(everyone, q_weight[0]).astype(jnp.bfloat16)
     queries = head_norm(q_part, q_gain[0]).astype(jnp.bfloat16)
     query_heads = queries.reshape(all_sites, heads_here, head_size)
 
     ring_hidden = RingGather(tile_hidden, group_size, my_index)
+    site_tiles, site_count = ring_hidden.step((site_tiles, site_count))
     hidden_slots, hidden_sources = ring_hidden.finish()
     table_hidden = hidden_slots.reshape(group_size * tiles_here, hidden_width)
     keyval = jnp.dot(table_hidden, weight_out, preferred_element_type=jnp.float32)

time: 128 us -> 128 us (level)
  waiting for transfers between devices: 52.2 us -> 40.1 us
  starting transfers between devices: 32.1 us -> 38.3 us
  other arithmetic: 7.94 us -> 10.5 us
  local copies, waits for them, and re-layouts: 14.4 us -> 16.1 us
  matrix products: 7.69 us -> 9.01 us
    ppermute x8, waiting for transfers between devices: 29.6 us -> 17.2 us  [_issue(): self.ahead = lax.ppermute(self.ahead, 'site', self.forward)]
    ppermute x8, starting transfers between devices: 11.8 us -> 22.6 us  [_issue(): self.ahead = lax.ppermute(self.ahead, 'site', self.forward)]
    ppermute x6, starting transfers between devices: 5.41 us -> 0.48 us  [_issue(): self.behind = lax.ppermute(self.behind, 'site', self.backward)]
    mul x2, local copies, waits for them, and re-layouts: 0.01 us -> 2.42 us  [head_norm(): shaped * lax.rsqrt(jnp.mean(shaped * shaped, axis=-1, keepdims=True) + ep...]
    ppermute x2, starting transfers between devices: 1.88 us -> 0.36 us  [last_round(): state = keep + lax.ppermute(send, 'site', xor_pairs(group_size, bit))]
    ppermute x2, waiting for transfers between devices: 6.42 us -> 7.94 us  [last_round(): state = keep + lax.ppermute(send, 'site', xor_pairs(group_size, bit))]
    ppermute x3, starting transfers between devices: 4.93 us -> 6.25 us  [doubling_sum(): state = state + lax.ppermute(state, 'site', xor_pairs(count, bit))]
    unnamed x3, other arithmetic: 1 us -> 2.28 us
  transfers between devices with their start and end apart: 22 -> 22, of which waited for: 16 -> 13; matrix products, arithmetic and copies ran while one was open for 16% -> 18% of each run, Pallas kernels for 0% -> 0%
where the time goes in v14:
time: 128 us; the launch traced here: 127 us
  waiting for transfers between devices  40.1 us (31%)
  starting transfers between devices  38.3 us (30%)
  local copies, waits for them, and re-layouts  16.1 us (13%)
  Pallas kernels  12.4 us (10%)
  other arithmetic  10.5 us (8%)
  matrix products  9.01 us (7%)
    ppermute x8, starting transfers between devices, _issue(): self.ahead = lax.ppermute(self.ahead, 'site', self.forward)  22.6 us
    ppermute x8, waiting for transfers between devices, _issue(): self.ahead = lax.ppermute(self.ahead, 'site', self.forward)  17.2 us
    pallas_call x1, Pallas kernels, gated_ffn(): pl.pallas_call(ffn_block, grid=(units // block,), in_specs=[pl.BlockSpec(...  12.4 us
    ppermute x3, waiting for transfers between devices, doubling_sum(): state = state + lax.ppermute(state, 'site', xor_pairs(count, bit))  11.6 us
    unnamed x34, local copies, waits for them, and re-layouts  8.46 us
    ppermute x2, waiting for transfers between devices, last_round(): state = keep + lax.ppermute(send, 'site', xor_pairs(group_size, bit))  7.94 us
    all_to_all x1, starting transfers between devices, heads_split(): lax.all_to_all(col_blocks, 'site', split_axis=0, concat_axis=0, tiled=True)  6.25 us
    ppermute x3, starting transfers between devices, doubling_sum(): state = state + lax.ppermute(state, 'site', xor_pairs(count, bit))  6.25 us
  transfers between devices with their start and end apart: 22, of which 13 were waited for; matrix products, arithmetic and copies ran while one was open for 18% of the time, Pallas kernels for 0%

profile of v14, /device:TPU:0, one launch (start us, length us, event | category | flops | bytes accessed | tf_op | source)
XLA Modules:
  0.0 126.7 jit_solution(4241970621701114538)
XLA Ops:
  0.0 0.9 reduce.1
  1.0 1.6 %pad_maximum_fusion = bf16[136,512]{1,0:T(8,128)(2,1)} fusion(bf16[8,512]{1,0:T(8,128)(2,1)S(1)} %reshape_squeeze.9, bf16[128,512]{1,0:T(8,128)(2,1)} %bitcast.147), kind=kLoop, calls=%fused_computation.41 | loop fusion | flops 278528 | bytes 278528 | tf_op jit(solution)/shard_map/concatenate | solution.py:442
  2.5 3.0 %collective-permute-start = (bf16[136,512]{1,0:T(8,128)(2,1)}, bf16[136,512]{1,0:T(8,128)(2,1)S(1)}, u32[]{:S(2)}, u32[]{:S(2)}) collective-permute-start(bf16[136,512]{1,0:T(8,128)(2,1)} %pad_maximum_fusion), channel_id=1, source_target_pairs={{0,2},{2,4},{4,6},{6,7},{7,5},{5,3},{3,1},{1,0},{8,10},{10,12},{12... | collective-permute-start | bytes 417800 | tf_op jit(solution)/shard_map/ppermute | solution.py:163
  5.6 0.7 broadcast_multiply_fusion
  6.2 0.7 add_bitcast_fusion
  6.9 1.2 broadcast_bitcast_fusion.1
  8.1 1.2 broadcast_bitcast_fusion
  9.3 0.6 pad_clamp_fusion
  9.9 1.1 copy.34
  11.1 0.4 copy.38
  11.5 1.1 reshape.277
  12.6 1.2 copy.28
  13.9 0.3 copy.29
  14.2 1.3 %copy.36 = s32[1,2,8,128]{3,1,2,0:T(2,128)} copy(s32[1,2,8,128]{3,2,1,0:T(8,128)} %add_bitcast_fusion) | data formatting | bytes 16384
  15.4 0.8 gather_fusion.1
  16.2 0.7 bitcast_dynamic-update-slice_fusion.15
  17.0 2.1 %collective-permute-start.1 = (bf16[136,512]{1,0:T(8,128)(2,1)S(1)}, bf16[136,512]{1,0:T(8,128)(2,1)S(1)}, u32[]{:S(2)}, u32[]{:S(2)}) collective-permute-start(bf16[136,512]{1,0:T(8,128)(2,1)S(1)} %collective-permute-done), channel_id=1, source_target_pairs={{0,2},{2,4},{4,6},{6,7},{7,5},{5,3},{3,1},{1,0},{8,10},{10,12},{12... | collective-permute-start | bytes 417800 | tf_op jit(solution)/shard_map/ppermute | solution.py:163
  19.1 3.1 %collective-permute-done.1 = bf16[136,512]{1,0:T(8,128)(2,1)S(1)} collective-permute-done((bf16[136,512]{1,0:T(8,128)(2,1)S(1)}, bf16[136,512]{1,0:T(8,128)(2,1)S(1)}, u32[]{:S(2)}, u32[]{:S(2)}) %collective-permute-start.1) | collective-permute-done | bytes 139296 | tf_op jit(solution)/shard_map/ppermute | solution.py:163
  22.1 1.9 %collective-permute-start.2 = (bf16[136,512]{1,0:T(8,128)(2,1)S(1)}, bf16[136,512]{1,0:T(8,128)(2,1)S(1)}, u32[]{:S(2)}, u32[]{:S(2)}) collective-permute-start(bf16[136,512]{1,0:T(8,128)(2,1)S(1)} %collective-permute-done.1), channel_id=1, source_target_pairs={{0,2},{2,4},{4,6},{6,7},{7,5},{5,3},{3,1},{1,0},{8,10},{10,12},{12... | collective-permute-start | bytes 417800 | tf_op jit(solution)/shard_map/ppermute | solution.py:163
  24.2 3.0 %collective-permute-done.2 = bf16[136,512]{1,0:T(8,128)(2,1)S(1)} collective-permute-done((bf16[136,512]{1,0:T(8,128)(2,1)S(1)}, bf16[136,512]{1,0:T(8,128)(2,1)S(1)}, u32[]{:S(2)}, u32[]{:S(2)}) %collective-permute-start.2) | collective-permute-done | bytes 139296 | tf_op jit(solution)/shard_map/ppermute | solution.py:163
  27.2 2.4 %collective-permute-start.3 = (bf16[136,512]{1,0:T(8,128)(2,1)S(1)}, bf16[136,512]{1,0:T(8,128)(2,1)S(1)}, u32[]{:S(2)}, u32[]{:S(2)}) collective-permute-start(bf16[136,512]{1,0:T(8,128)(2,1)S(1)} %collective-permute-done.2), channel_id=1, source_target_pairs={{0,2},{2,4},{4,6},{6,7},{7,5},{5,3},{3,1},{1,0},{8,10},{10,12},{12... | collective-permute-start | bytes 417800 | tf_op jit(solution)/shard_map/ppermute | solution.py:163
  29.6 2.9 %collective-permute-done.3 = bf16[136,512]{1,0:T(8,128)(2,1)S(1)} collective-permute-done((bf16[136,512]{1,0:T(8,128)(2,1)S(1)}, bf16[136,512]{1,0:T(8,128)(2,1)S(1)}, u32[]{:S(2)}, u32[]{:S(2)}) %collective-permute-start.3) | collective-permute-done | bytes 139296 | tf_op jit(solution)/shard_map/ppermute | solution.py:163
  32.6 1.4 %bitcast_dynamic-update-slice_fusion.7 = (bf16[8,256,512]{2,1,0:T(8,128)(2,1)}, bf16[256,512]{1,0:T(8,128)(2,1)}) fusion(bf16[8,136,512]{2,1,0:T(8,128)(2,1)S(1)} %bitcast_dynamic-update-slice_fusion.8, bf16[8,256,128]{2,1,0:T(8,128)(2,1)S(1)} %gather_fusion.1), kind=kOutput, calls=%fused_computation.40 | convolution fusion | flops 269615104 | bytes 2097152 | tf_op jit(solution)/shard_map/dot_general | solution.py:468
  34.0 2.1 %collective-permute-start.7 = (bf16[256,512]{1,0:T(8,128)(2,1)}, bf16[256,512]{1,0:T(8,128)(2,1)S(1)}, u32[]{:S(2)}, u32[]{:S(2)}) collective-permute-start(bf16[256,512]{1,0:T(8,128)(2,1)} %get-tuple-element.22), channel_id=1, source_target_pairs={{0,2},{2,4},{4,6},{6,7},{7,5},{5,3},{3,1},{1,0},{8,10},{10,12},{12... | collective-permute-start | bytes 786440 | tf_op jit(solution)/shard_map/ppermute | solution.py:163
  36.1 6.3 %all-to-all-start = ((bf16[8,64,512]{2,1,0:T(8,128)(2,1)}), bf16[8,64,512]{2,1,0:T(8,128)(2,1)S(1)}, u32[]{:S(2)}, u32[]{:S(2)}) async-start(bf16[8,64,512]{2,1,0:T(8,128)(2,1)} %reshape.277), calls=%async_computation | async-start | bytes 1048576 | tf_op jit(solution)/shard_map/all_to_all | solution.py:453
  42.4 0.7 gather_fusion
  43.1 2.3 %bitcast_reduce_fusion.1 = (f32[8,2]{0,1:T(2,128)S(1)}, f32[8,256]{1,0:T(8,128)S(1)}) fusion(bf16[8,4096]{1,0:T(8,128)(2,1)S(1)} %bitcast.149, bf16[1,256,4096]{2,1,0:T(8,128)(2,1)} %param.20), kind=kOutput, calls=%fused_computation.67 | convolution fusion | flops 16785392 | bytes 2170944 | tf_op jit(solution)/shard_map/dot_general | solution.py:23
  45.4 3.6 %collective-permute-start.9 = (bf16[256,512]{1,0:T(8,128)(2,1)S(1)}, bf16[256,512]{1,0:T(8,128)(2,1)S(1)}, u32[]{:S(2)}, u32[]{:S(2)}) collective-permute-start(bf16[256,512]{1,0:T(8,128)(2,1)S(1)} %collective-permute-done.7), channel_id=1, source_target_pairs={{0,2},{2,4},{4,6},{6,7},{7,5},{5,3},{3,1},{1,0},{8,10},{10,12},{12... | collective-permute-start | bytes 786440 | tf_op jit(solution)/shard_map/ppermute | solution.py:163
  49.1 5.2 %collective-permute-done.9 = bf16[256,512]{1,0:T(8,128)(2,1)S(1)} collective-permute-done((bf16[256,512]{1,0:T(8,128)(2,1)S(1)}, bf16[256,512]{1,0:T(8,128)(2,1)S(1)}, u32[]{:S(2)}, u32[]{:S(2)}) %collective-permute-start.9) | collective-permute-done | bytes 262176 | tf_op jit(solution)/shard_map/ppermute | solution.py:163
  54.3 4.3 %collective-permute-start.10 = (bf16[256,512]{1,0:T(8,128)(2,1)S(1)}, bf16[256,512]{1,0:T(8,128)(2,1)S(1)}, u32[]{:S(2)}, u32[]{:S(2)}) collective-permute-start(bf16[256,512]{1,0:T(8,128)(2,1)S(1)} %collective-permute-done.9), channel_id=1, source_target_pairs={{0,2},{2,4},{4,6},{6,7},{7,5},{5,3},{3,1},{1,0},{8,10},{10,12},{12... | collective-permute-start | bytes 786440 | tf_op jit(solution)/shard_map/ppermute | solution.py:163
  58.6 3.1 %convert_reduce_fusion = f32[8,2048]{1,0:T(8,128)S(1)} fusion(s32[2048]{0:T(1024)S(1)} %bitcast.150, s32[8,256]{1,0:T(8,128)S(1)} %copy-done.5, pred[8,256]{1,0:T(8,128)(4,1)S(1)} %iota_compare_fusion), kind=kLoop, calls=%fused_computation.2 | loop fusion | flops 16760832 | bytes 83968 | tf_op jit(solution)/shard_map/reduce_sum | solution.py:493
  61.8 0.7 bitcast_dynamic-update-slice_fusion.6
  62.5 3.1 %collective-permute-start.11 = (bf16[256,512]{1,0:T(8,128)(2,1)S(1)}, bf16[256,512]{1,0:T(8,128)(2,1)S(1)}, u32[]{:S(2)}, u32[]{:S(2)}) collective-permute-start(bf16[256,512]{1,0:T(8,128)(2,1)S(1)} %collective-permute-done.10), channel_id=1, source_target_pairs={{0,2},{2,4},{4,6},{6,7},{7,5},{5,3},{3,1},{1,0},{8,10},{10,12},{12... | collective-permute-start | bytes 786440 | tf_op jit(solution)/shard_map/ppermute | solution.py:163
  65.7 0.7 bitcast_dynamic-update-slice_fusion.5
  66.4 0.4 collective-permute-start.13
  66.8 0.7 bitcast_dynamic-update-slice_fusion.4
  67.5 2.9 %collective-permute-done.11 = bf16[256,512]{1,0:T(8,128)(2,1)S(1)} collective-permute-done((bf16[256,512]{1,0:T(8,128)(2,1)S(1)}, bf16[256,512]{1,0:T(8,128)(2,1)S(1)}, u32[]{:S(2)}, u32[]{:S(2)}) %collective-permute-start.11) | collective-permute-done | bytes 262176 | tf_op jit(solution)/shard_map/ppermute | solution.py:163
  70.4 0.7 bitcast_dynamic-update-slice_fusion.3
  71.1 0.7 bitcast_dynamic-update-slice_fusion.2
  71.9 0.7 bitcast_dynamic-update-slice_fusion.1
  72.6 0.6 collective-permute-done.13
  73.2 0.7 bitcast_dynamic-update-slice_fusion
  74.0 2.9 %fusion.43 = f32[2048,512]{0,1:T(8,128)S(1)} fusion(bf16[2048,512]{1,0:T(8,128)(2,1)} %bitcast.22, bf16[512,512]{1,0:T(8,128)(2,1)S(1)} %bitcast.141), kind=kOutput, calls=%fused_computation.103 | convolution fusion | flops 1073741824 | bytes 6815744 | tf_op jit(solution)/shard_map/dot_general | solution.py:480
  77.0 0.2 bitcast_reduce_fusion
  77.2 0.3 copy-done.6
  77.5 0.2 fusion.6
  77.8 1.0 multiply_reduce_fusion.1
  78.8 1.5 %convolution_bitcast_fusion = f32[8,1,4096]{2,0,1:T(8,128)S(1)} fusion(bf16[1,256,4096]{2,1,0:T(8,128)(2,1)S(1)} %copy-done, bf16[2048,2,128]{0,2,1:T(8,128)(2,1)S(1)} %bitcast.139, f32[8,2,2048]{2,0,1:T(8,128)S(1)} %get-tuple-element.26, f32[8,2]{0,1:T(2,128)} %get-tuple-element.25, f32[8,2048]{1,0:T(8,128)S(1)} %convert_reduce_fusion), kind=kOutput, calls=%fused_computation.3 | convolution fusion | flops 25266176 | bytes 3473472 | tf_op jit(solution)/shard_map/dot_general | solution.py:503
  80.3 1.7 %collective-permute-start.14 = (f32[8,1,4096]{2,0,1:T(8,128)S(1)}, f32[8,1,4096]{2,0,1:T(8,128)S(1)}, u32[]{:S(2)}, u32[]{:S(2)}) collective-permute-start(f32[8,1,4096]{2,0,1:T(8,128)S(1)} %convolution_bitcast_fusion), channel_id=1, source_target_pairs={{0,1},{1,0},{2,3},{3,2},{4,5},{5,4},{6,7},{7,6},{8,9},{9,8},{10,11... | collective-permute-start | bytes 393224 | tf_op jit(solution)/shard_map/ppermute | solution.py:116
  81.9 3.3 %collective-permute-done.14 = f32[8,1,4096]{2,0,1:T(8,128)S(1)} collective-permute-done((f32[8,1,4096]{2,0,1:T(8,128)S(1)}, f32[8,1,4096]{2,0,1:T(8,128)S(1)}, u32[]{:S(2)}, u32[]{:S(2)}) %collective-permute-start.14) | collective-permute-done | bytes 131104 | tf_op jit(solution)/shard_map/ppermute | solution.py:116
  85.2 2.1 %collective-permute-start.15 = (f32[8,1,4096]{2,0,1:T(8,128)S(1)}, f32[8,1,4096]{2,0,1:T(8,128)S(1)}, u32[]{:S(2)}, u32[]{:S(2)}) collective-permute-start(f32[8,1,4096]{2,0,1:T(8,128)S(1)} %add.224), channel_id=1, source_target_pairs={{0,2},{1,3},{2,0},{3,1},{4,6},{5,7},{6,4},{7,5},{8,10},{9,11},{10,... | collective-permute-start | bytes 393224 | tf_op jit(solution)/shard_map/ppermute | solution.py:116
  87.3 3.4 %collective-permute-done.15 = f32[8,1,4096]{2,0,1:T(8,128)S(1)} collective-permute-done((f32[8,1,4096]{2,0,1:T(8,128)S(1)}, f32[8,1,4096]{2,0,1:T(8,128)S(1)}, u32[]{:S(2)}, u32[]{:S(2)}) %collective-permute-start.15) | collective-permute-done | bytes 131104 | tf_op jit(solution)/shard_map/ppermute | solution.py:116
  90.8 2.5 %collective-permute-start.16 = (f32[8,1,4096]{2,0,1:T(8,128)S(1)}, f32[8,1,4096]{2,0,1:T(8,128)S(1)}, u32[]{:S(2)}, u32[]{:S(2)}) collective-permute-start(f32[8,1,4096]{2,0,1:T(8,128)S(1)} %add.225), channel_id=1, source_target_pairs={{0,4},{1,5},{2,6},{3,7},{4,0},{5,1},{6,2},{7,3},{8,12},{9,13},{10,... | collective-permute-start | bytes 393224 | tf_op jit(solution)/shard_map/ppermute | solution.py:116
  93.3 4.8 %collective-permute-done.16 = f32[8,1,4096]{2,0,1:T(8,128)S(1)} collective-permute-done((f32[8,1,4096]{2,0,1:T(8,128)S(1)}, f32[8,1,4096]{2,0,1:T(8,128)S(1)}, u32[]{:S(2)}, u32[]{:S(2)}) %collective-permute-start.16) | collective-permute-done | bytes 131104 | tf_op jit(solution)/shard_map/ppermute | solution.py:116
  98.3 0.7 fusion.28.rows_ref
  99.0 12.4 %shard_map.154 = f32[8,4096]{1,0:T(8,128)} custom-call(bf16[8,4096]{1,0:T(8,128)(2,1)} %fusion.28.rows_ref, bf16[896,4096]{1,0:T(8,128)(2,1)} %bitcast.136, bf16[896,4096]{1,0:T(8,128)(2,1)} %bitcast.137, bf16[896,4096]{1,0:T(8,128)(2,1)} %bitcast.138), custom_call_target="tpu_custom_call" | custom-call | tf_op jit(solution)/shard_map/pallas_call | solution.py:396
  111.4 1.0 reshape_reshape.4
  112.6 4.2 %collective-permute-done.17 = f32[2,2,1,1,4096]{4,2,1,0,3:T(1,128)S(1)} collective-permute-done((f32[2,2,1,1,4096]{4,2,1,0,3:T(1,128)S(1)}, f32[2,2,1,1,4096]{4,2,1,0,3:T(1,128)S(1)}, u32[]{:S(2)}, u32[]{:S(2)}) %collective-permute-start.17) | collective-permute-done | bytes 65568 | tf_op jit(solution)/shard_map/ppermute | solution.py:523
  116.9 0.3 collective-permute-start.18
  117.2 3.7 %collective-permute-done.18 = f32[2,1,1,1,4096]{4,2,1,0,3:T(1,128)S(1)} collective-permute-done((f32[2,1,1,1,4096]{4,2,1,0,3:T(1,128)S(1)}, f32[2,1,1,1,4096]{4,2,1,0,3:T(1,128)S(1)}, u32[]{:S(2)}, u32[]{:S(2)}) %collective-permute-start.18) | collective-permute-done | bytes 32800 | tf_op jit(solution)/shard_map/ppermute | solution.py:523
  121.0 2.3 %collective-permute-start.20 = (f32[1,4096]{1,0:T(1,128)S(1)}, f32[1,4096]{1,0:T(1,128)S(1)}, u32[]{:S(2)}, u32[]{:S(2)}) collective-permute-start(f32[1,4096]{1,0:T(1,128)S(1)} %dynamic-slice_bitcast_fusion), channel_id=1, source_target_pairs={{0,12},{1,13},{2,14},{3,15},{4,8},{5,9},{6,10},{7,11},{8,20},{9,21... | collective-permute-start | bytes 49160 | tf_op jit(solution)/shard_map/ppermute | solution.py:540
  123.4 0.8 collective-permute-done.19
  124.2 1.9 %collective-permute-done.20 = f32[1,4096]{1,0:T(1,128)S(1)} collective-permute-done((f32[1,4096]{1,0:T(1,128)S(1)}, f32[1,4096]{1,0:T(1,128)S(1)}, u32[]{:S(2)}, u32[]{:S(2)}) %collective-permute-start.20) | collective-permute-done | bytes 16416 | tf_op jit(solution)/shard_map/ppermute | solution.py:540
  126.1 0.6 convert_bitcast_fusion
  (60 shorter events, 1.2 us)
Async XLA Ops:
  0.0 78.8 %copy-start = (bf16[1,256,4096]{2,1,0:T(8,128)(2,1)S(1)}, bf16[1,256,4096]{2,1,0:T(8,128)(2,1)}, u32[]{:S(2)}) copy-start(bf16[1,256,4096]{2,1,0:T(8,128)(2,1)} %param.25) | copy-start | bytes 6291460
  0.9 10.1 %copy-start.2 = (bf16[8,512]{1,0:T(8,128)(2,1)}, bf16[8,512]{1,0:T(8,128)(2,1)S(1)}, u32[]{:S(2)}) copy-start(bf16[8,512]{1,0:T(8,128)(2,1)S(1)} %reshape_squeeze.9) | copy-start | bytes 24580
  2.5 14.4 %collective-permute-start = (bf16[136,512]{1,0:T(8,128)(2,1)}, bf16[136,512]{1,0:T(8,128)(2,1)S(1)}, u32[]{:S(2)}, u32[]{:S(2)}) collective-permute-start(bf16[136,512]{1,0:T(8,128)(2,1)} %pad_maximum_fusion), channel_id=1, source_target_pairs={{0,2},{2,4},{4,6},{6,7},{7,5},{5,3},{3,1},{1,0},{8,10},{10,12},{12... | collective-permute-start | bytes 417800 | tf_op jit(solution)/shard_map/ppermute | solution.py:163
  5.5 13.5 %collective-permute-start.4 = (bf16[136,512]{1,0:T(8,128)(2,1)}, bf16[136,512]{1,0:T(8,128)(2,1)S(1)}, u32[]{:S(2)}, u32[]{:S(2)}) collective-permute-start(bf16[136,512]{1,0:T(8,128)(2,1)} %pad_maximum_fusion), channel_id=1, source_target_pairs={{0,1},{2,0},{4,2},{6,4},{7,6},{5,7},{3,5},{1,3},{8,9},{10,8},{12,1... | collective-permute-start | bytes 417800 | tf_op jit(solution)/shard_map/ppermute | solution.py:167
  11.5 4.7 %copy-start.1 = (bf16[1,128,512]{2,1,0:T(8,128)(2,1)S(1)}, bf16[1,128,512]{2,1,0:T(8,128)(2,1)}, u32[]{:S(2)}) copy-start(bf16[1,128,512]{2,1,0:T(8,128)(2,1)} %param.23) | copy-start | bytes 393220
  17.0 5.2 %collective-permute-start.1 = (bf16[136,512]{1,0:T(8,128)(2,1)S(1)}, bf16[136,512]{1,0:T(8,128)(2,1)S(1)}, u32[]{:S(2)}, u32[]{:S(2)}) collective-permute-start(bf16[136,512]{1,0:T(8,128)(2,1)S(1)} %collective-permute-done), channel_id=1, source_target_pairs={{0,2},{2,4},{4,6},{6,7},{7,5},{5,3},{3,1},{1,0},{8,10},{10,12},{12... | collective-permute-start | bytes 417800 | tf_op jit(solution)/shard_map/ppermute | solution.py:163
  19.0 5.1 %collective-permute-start.5 = (bf16[136,512]{1,0:T(8,128)(2,1)S(1)}, bf16[136,512]{1,0:T(8,128)(2,1)S(1)}, u32[]{:S(2)}, u32[]{:S(2)}) collective-permute-start(bf16[136,512]{1,0:T(8,128)(2,1)S(1)} %collective-permute-done.4), channel_id=1, source_target_pairs={{0,1},{2,0},{4,2},{6,4},{7,6},{5,7},{3,5},{1,3},{8,9},{10,8},{12,1... | collective-permute-start | bytes 417800 | tf_op jit(solution)/shard_map/ppermute | solution.py:167
  22.1 5.1 %collective-permute-start.2 = (bf16[136,512]{1,0:T(8,128)(2,1)S(1)}, bf16[136,512]{1,0:T(8,128)(2,1)S(1)}, u32[]{:S(2)}, u32[]{:S(2)}) collective-permute-start(bf16[136,512]{1,0:T(8,128)(2,1)S(1)} %collective-permute-done.1), channel_id=1, source_target_pairs={{0,2},{2,4},{4,6},{6,7},{7,5},{5,3},{3,1},{1,0},{8,10},{10,12},{12... | collective-permute-start | bytes 417800 | tf_op jit(solution)/shard_map/ppermute | solution.py:163
  24.1 8.5 %collective-permute-start.6 = (bf16[136,512]{1,0:T(8,128)(2,1)S(1)}, bf16[136,512]{1,0:T(8,128)(2,1)S(1)}, u32[]{:S(2)}, u32[]{:S(2)}) collective-permute-start(bf16[136,512]{1,0:T(8,128)(2,1)S(1)} %collective-permute-done.5), channel_id=1, source_target_pairs={{0,1},{2,0},{4,2},{6,4},{7,6},{5,7},{3,5},{1,3},{8,9},{10,8},{12,1... | collective-permute-start | bytes 417800 | tf_op jit(solution)/shard_map/ppermute | solution.py:167
  27.2 5.3 %collective-permute-start.3 = (bf16[136,512]{1,0:T(8,128)(2,1)S(1)}, bf16[136,512]{1,0:T(8,128)(2,1)S(1)}, u32[]{:S(2)}, u32[]{:S(2)}) collective-permute-start(bf16[136,512]{1,0:T(8,128)(2,1)S(1)} %collective-permute-done.2), channel_id=1, source_target_pairs={{0,2},{2,4},{4,6},{6,7},{7,5},{5,3},{3,1},{1,0},{8,10},{10,12},{12... | collective-permute-start | bytes 417800 | tf_op jit(solution)/shard_map/ppermute | solution.py:163
  34.0 15.0 %copy-start.8 = (s32[8]{0:T(128)S(1)}, s32[8]{0:T(128)}, u32[]{:S(2)}) copy-start(s32[8]{0:T(128)} %param.19) | copy-start | bytes 100
  34.0 24.6 %copy-start.3 = (s32[1,2,8,128]{3,1,2,0:T(2,128)S(1)}, s32[1,2,8,128]{3,1,2,0:T(2,128)}, u32[]{:S(2)}) copy-start(s32[1,2,8,128]{3,1,2,0:T(2,128)} %copy.36) | copy-start | bytes 24580
  34.0 24.6 %copy-start.5 = (s32[8,256]{1,0:T(8,128)S(1)}, s32[8,256]{1,0:T(8,128)}, u32[]{:S(2)}) copy-start(s32[8,256]{1,0:T(8,128)} %param.18) | copy-start | bytes 24580
  34.0 11.4 %collective-permute-start.7 = (bf16[256,512]{1,0:T(8,128)(2,1)}, bf16[256,512]{1,0:T(8,128)(2,1)S(1)}, u32[]{:S(2)}, u32[]{:S(2)}) collective-permute-start(bf16[256,512]{1,0:T(8,128)(2,1)} %get-tuple-element.22), channel_id=1, source_target_pairs={{0,2},{2,4},{4,6},{6,7},{7,5},{5,3},{3,1},{1,0},{8,10},{10,12},{12... | collective-permute-start | bytes 786440 | tf_op jit(solution)/shard_map/ppermute | solution.py:163
  36.1 9.3 %collective-permute-start.8 = (bf16[256,512]{1,0:T(8,128)(2,1)}, bf16[256,512]{1,0:T(8,128)(2,1)S(1)}, u32[]{:S(2)}, u32[]{:S(2)}) collective-permute-start(bf16[256,512]{1,0:T(8,128)(2,1)} %get-tuple-element.22), channel_id=1, source_target_pairs={{0,1},{2,0},{4,2},{6,4},{7,6},{5,7},{3,5},{1,3},{8,9},{10,8},{12,1... | collective-permute-start | bytes 786440 | tf_op jit(solution)/shard_map/ppermute | solution.py:167
  36.1 37.9 %all-to-all-start = ((bf16[8,64,512]{2,1,0:T(8,128)(2,1)}), bf16[8,64,512]{2,1,0:T(8,128)(2,1)S(1)}, u32[]{:S(2)}, u32[]{:S(2)}) async-start(bf16[8,64,512]{2,1,0:T(8,128)(2,1)} %reshape.277), calls=%async_computation | async-start | bytes 1048576 | tf_op jit(solution)/shard_map/all_to_all | solution.py:453
  45.4 8.9 %collective-permute-start.9 = (bf16[256,512]{1,0:T(8,128)(2,1)S(1)}, bf16[256,512]{1,0:T(8,128)(2,1)S(1)}, u32[]{:S(2)}, u32[]{:S(2)}) collective-permute-start(bf16[256,512]{1,0:T(8,128)(2,1)S(1)} %collective-permute-done.7), channel_id=1, source_target_pairs={{0,2},{2,4},{4,6},{6,7},{7,5},{5,3},{3,1},{1,0},{8,10},{10,12},{12... | collective-permute-start | bytes 786440 | tf_op jit(solution)/shard_map/ppermute | solution.py:163
  49.0 17.4 %collective-permute-start.12 = (bf16[256,512]{1,0:T(8,128)(2,1)S(1)}, bf16[256,512]{1,0:T(8,128)(2,1)S(1)}, u32[]{:S(2)}, u32[]{:S(2)}) collective-permute-start(bf16[256,512]{1,0:T(8,128)(2,1)S(1)} %collective-permute-done.8), channel_id=1, source_target_pairs={{0,1},{2,0},{4,2},{6,4},{7,6},{5,7},{3,5},{1,3},{8,9},{10,8},{12,1... | collective-permute-start | bytes 786440 | tf_op jit(solution)/shard_map/ppermute | solution.py:167
  54.3 8.2 %collective-permute-start.10 = (bf16[256,512]{1,0:T(8,128)(2,1)S(1)}, bf16[256,512]{1,0:T(8,128)(2,1)S(1)}, u32[]{:S(2)}, u32[]{:S(2)}) collective-permute-start(bf16[256,512]{1,0:T(8,128)(2,1)S(1)} %collective-permute-done.9), channel_id=1, source_target_pairs={{0,2},{2,4},{4,6},{6,7},{7,5},{5,3},{3,1},{1,0},{8,10},{10,12},{12... | collective-permute-start | bytes 786440 | tf_op jit(solution)/shard_map/ppermute | solution.py:163
  62.5 7.9 %collective-permute-start.11 = (bf16[256,512]{1,0:T(8,128)(2,1)S(1)}, bf16[256,512]{1,0:T(8,128)(2,1)S(1)}, u32[]{:S(2)}, u32[]{:S(2)}) collective-permute-start(bf16[256,512]{1,0:T(8,128)(2,1)S(1)} %collective-permute-done.10), channel_id=1, source_target_pairs={{0,2},{2,4},{4,6},{6,7},{7,5},{5,3},{3,1},{1,0},{8,10},{10,12},{12... | collective-permute-start | bytes 786440 | tf_op jit(solution)/shard_map/ppermute | solution.py:163
  66.4 6.8 %collective-permute-start.13 = (bf16[256,512]{1,0:T(8,128)(2,1)S(1)}, bf16[256,512]{1,0:T(8,128)(2,1)S(1)}, u32[]{:S(2)}, u32[]{:S(2)}) collective-permute-start(bf16[256,512]{1,0:T(8,128)(2,1)S(1)} %collective-permute-done.12), channel_id=1, source_target_pairs={{0,1},{2,0},{4,2},{6,4},{7,6},{5,7},{3,5},{1,3},{8,9},{10,8},{12,1... | collective-permute-start | bytes 786440 | tf_op jit(solution)/shard_map/ppermute | solution.py:167
  76.9 0.7 copy-start.6
  77.2 0.6 copy-start.7
  78.8 19.5 %copy-start.4 = (f32[1,4096]{1,0:T(1,128)S(1)}, f32[1,4096]{1,0:T(1,128)}, u32[]{:S(2)}) copy-start(f32[1,4096]{1,0:T(1,128)} %param.26) | copy-start | bytes 49156
  80.3 5.0 %collective-permute-start.14 = (f32[8,1,4096]{2,0,1:T(8,128)S(1)}, f32[8,1,4096]{2,0,1:T(8,128)S(1)}, u32[]{:S(2)}, u32[]{:S(2)}) collective-permute-start(f32[8,1,4096]{2,0,1:T(8,128)S(1)} %convolution_bitcast_fusion), channel_id=1, source_target_pairs={{0,1},{1,0},{2,3},{3,2},{4,5},{5,4},{6,7},{7,6},{8,9},{9,8},{10,11... | collective-permute-start | bytes 393224 | tf_op jit(solution)/shard_map/ppermute | solution.py:116
  85.2 5.5 %collective-permute-start.15 = (f32[8,1,4096]{2,0,1:T(8,128)S(1)}, f32[8,1,4096]{2,0,1:T(8,128)S(1)}, u32[]{:S(2)}, u32[]{:S(2)}) collective-permute-start(f32[8,1,4096]{2,0,1:T(8,128)S(1)} %add.224), channel_id=1, source_target_pairs={{0,2},{1,3},{2,0},{3,1},{4,6},{5,7},{6,4},{7,5},{8,10},{9,11},{10,... | collective-permute-start | bytes 393224 | tf_op jit(solution)/shard_map/ppermute | solution.py:116
  90.8 7.3 %collective-permute-start.16 = (f32[8,1,4096]{2,0,1:T(8,128)S(1)}, f32[8,1,4096]{2,0,1:T(8,128)S(1)}, u32[]{:S(2)}, u32[]{:S(2)}) collective-permute-start(f32[8,1,4096]{2,0,1:T(8,128)S(1)} %add.225), channel_id=1, source_target_pairs={{0,4},{1,5},{2,6},{3,7},{4,0},{5,1},{6,2},{7,3},{8,12},{9,13},{10,... | collective-permute-start | bytes 393224 | tf_op jit(solution)/shard_map/ppermute | solution.py:116
  112.5 4.3 %collective-permute-start.17 = (f32[2,2,1,1,4096]{4,2,1,0,3:T(1,128)S(1)}, f32[2,2,1,1,4096]{4,2,1,0,3:T(1,128)S(1)}, u32[]{:S(2)}, u32[]{:S(2)}) collective-permute-start(f32[2,2,1,1,4096]{4,2,1,0,3:T(1,128)S(1)} %constant_dynamic-slice_fusion.1), channel_id=1, source_target_pairs={{0,1},{1,0},{2,3},{3,2},{4,5},{5,4},{6,7},{7,6},{8,9},{9,8},{10,11... | collective-permute-start | bytes 196616 | tf_op jit(solution)/shard_map/ppermute | solution.py:523
  116.9 4.0 %collective-permute-start.18 = (f32[2,1,1,1,4096]{4,2,1,0,3:T(1,128)S(1)}, f32[2,1,1,1,4096]{4,2,1,0,3:T(1,128)S(1)}, u32[]{:S(2)}, u32[]{:S(2)}) collective-permute-start(f32[2,1,1,1,4096]{4,2,1,0,3:T(1,128)S(1)} %constant_dynamic-slice_fusion), channel_id=1, source_target_pairs={{0,2},{1,3},{2,0},{3,1},{4,6},{5,7},{6,4},{7,5},{8,10},{9,11},{10,... | collective-permute-start | bytes 98312 | tf_op jit(solution)/shard_map/ppermute | solution.py:523
  121.0 3.2 %collective-permute-start.19 = (f32[1,4096]{1,0:T(1,128)S(1)}, f32[1,4096]{1,0:T(1,128)S(1)}, u32[]{:S(2)}, u32[]{:S(2)}) collective-permute-start(f32[1,4096]{1,0:T(1,128)S(1)} %bitcast_add_fusion), channel_id=1, source_target_pairs={{0,8},{1,9},{2,10},{3,11},{4,12},{5,13},{6,14},{7,15},{8,16},{9,17... | collective-permute-start | bytes 49160 | tf_op jit(solution)/shard_map/ppermute | solution.py:539
  121.0 5.0 %collective-permute-start.20 = (f32[1,4096]{1,0:T(1,128)S(1)}, f32[1,4096]{1,0:T(1,128)S(1)}, u32[]{:S(2)}, u32[]{:S(2)}) collective-permute-start(f32[1,4096]{1,0:T(1,128)S(1)} %dynamic-slice_bitcast_fusion), channel_id=1, source_target_pairs={{0,12},{1,13},{2,14},{3,15},{4,8},{5,9},{6,10},{7,11},{8,20},{9,21... | collective-permute-start | bytes 49160 | tf_op jit(solution)/shard_map/ppermute | solution.py:540

commit v15 on v14

--- a/solution.py
+++ b/solution.py
@@ -374,38 +374,41 @@
     return output_rows[None]
 
 
-def ffn_block(rows_ref, gate_ref, up_ref, down_ref, out_ref):
+def ffn_block(rows_ref, gate_a, gate_b, up_a, up_b, down_a, down_b, out_ref):
     step = pl.program_id(0)
 
     @pl.when(step == 0)
     def _():
         out_ref[...] = jnp.zeros_like(out_ref)
 
-    rows = rows_ref[...]
+    half = gate_a.shape[1]
+    rows_a = rows_ref[:, :half]
+    rows_b = rows_ref[:, half:]
     dims = (((1,), (1,)), ((), ()))
-    gate_sum = lax.dot_general(rows, gate_ref[...], dims, preferred_element_type=jnp.float32)
-    up_sum = lax.dot_general(rows, up_ref[...], dims, preferred_element_type=jnp.float32)
+    gate_sum = lax.dot_general(rows_a, gate_a[...], dims, preferred_element_type=jnp.float32)
+    gate_sum += lax.dot_general(rows_b, gate_b[...], dims, preferred_element_type=jnp.float32)
+    up_sum = lax.dot_general(rows_a, up_a[...], dims, preferred_element_type=jnp.float32)
+    up_sum += lax.dot_general(rows_b, up_b[...], dims, preferred_element_type=jnp.float32)
     hidden = (gate_sum * jax.nn.sigmoid(gate_sum) * up_sum).astype(jnp.bfloat16)
-    out_ref[...] += jnp.dot(hidden, down_ref[...], preferred_element_type=jnp.float32)
+    out_ref[:, :half] += jnp.dot(hidden, down_a[...], preferred_element_type=jnp.float32)
+    out_ref[:, half:] += jnp.dot(hidden, down_b[...], preferred_element_type=jnp.float32)
 
 
 def gated_ffn(rows, gate, up, down):
     units, width = gate.shape
     block = 128 if units % 128 == 0 else units
+    half = width // 2
     count = rows.shape[0]
+    first = pl.BlockSpec((block, half), lambda i: (i, 0))
+    second = pl.BlockSpec((block, half), lambda i: (i, 1))
     return pl.pallas_call(
         ffn_block,
         grid=(units // block,),
-        in_specs=[
-            pl.BlockSpec((count, width), lambda i: (0, 0)),
-            pl.BlockSpec((block, width), lambda i: (i, 0)),
-            pl.BlockSpec((block, width), lambda i: (i, 0)),
-            pl.BlockSpec((block, width), lambda i: (i, 0)),
-        ],
+        in_specs=[pl.BlockSpec((count, width), lambda i: (0, 0)), first, second, first, second, first, second],
         out_specs=pl.BlockSpec((count, width), lambda i: (0, 0)),
         out_shape=jax.ShapeDtypeStruct((count, width), jnp.float32),
         compiler_params=pltpu.CompilerParams(dimension_semantics=("arbitrary",)),
-    )(rows, gate, up, down)
+    )(rows, gate, gate, up, up, down, down)
 
 
 def heads_split(

time: 128 us -> 127 us (level)
  no operation moved by 1% of the time
where the time goes in v15:
time: 127 us; the launch traced here: 126 us
  waiting for transfers between devices  40.1 us (32%)
  starting transfers between devices  38.3 us (30%)
  local copies, waits for them, and re-layouts  16.1 us (13%)
  Pallas kernels  12 us (9%)
  other arithmetic  10.5 us (8%)
  matrix products  9.01 us (7%)
    ppermute x8, starting transfers between devices, _issue(): self.ahead = lax.ppermute(self.ahead, 'site', self.forward)  22.6 us
    ppermute x8, waiting for transfers between devices, _issue(): self.ahead = lax.ppermute(self.ahead, 'site', self.forward)  17.2 us
    pallas_call x1, Pallas kernels, gated_ffn(): pl.pallas_call(ffn_block, grid=(units // block,), in_specs=[pl.BlockSpec(...  12 us
    ppermute x3, waiting for transfers between devices, doubling_sum(): state = state + lax.ppermute(state, 'site', xor_pairs(count, bit))  11.6 us
    unnamed x34, local copies, waits for them, and re-layouts  8.46 us
    ppermute x2, waiting for transfers between devices, last_round(): state = keep + lax.ppermute(send, 'site', xor_pairs(group_size, bit))  7.94 us
    all_to_all x1, starting transfers between devices, heads_split(): lax.all_to_all(col_blocks, 'site', split_axis=0, concat_axis=0, tiled=True)  6.25 us
    ppermute x3, starting transfers between devices, doubling_sum(): state = state + lax.ppermute(state, 'site', xor_pairs(count, bit))  6.25 us
  transfers between devices with their start and end apart: 22, of which 13 were waited for; matrix products, arithmetic and copies ran while one was open for 18% of the time, Pallas kernels for 0%

profile of v15, /device:TPU:0, one launch (start us, length us, event | category | flops | bytes accessed | tf_op | source)
XLA Modules:
  0.0 126.3 jit_solution(12689337492576681309)
XLA Ops:
  0.0 0.9 reduce.1
  1.0 1.6 %pad_maximum_fusion = bf16[136,512]{1,0:T(8,128)(2,1)} fusion(bf16[8,512]{1,0:T(8,128)(2,1)S(1)} %reshape_squeeze.9, bf16[128,512]{1,0:T(8,128)(2,1)} %bitcast.150), kind=kLoop, calls=%fused_computation.41 | loop fusion | flops 278528 | bytes 278528 | tf_op jit(solution)/shard_map/concatenate | solution.py:445
  2.5 3.0 %collective-permute-start = (bf16[136,512]{1,0:T(8,128)(2,1)}, bf16[136,512]{1,0:T(8,128)(2,1)S(1)}, u32[]{:S(2)}, u32[]{:S(2)}) collective-permute-start(bf16[136,512]{1,0:T(8,128)(2,1)} %pad_maximum_fusion), channel_id=1, source_target_pairs={{0,2},{2,4},{4,6},{6,7},{7,5},{5,3},{3,1},{1,0},{8,10},{10,12},{12... | collective-permute-start | bytes 417800 | tf_op jit(solution)/shard_map/ppermute | solution.py:163
  5.6 0.7 broadcast_multiply_fusion
  6.2 0.7 add_bitcast_fusion
  6.9 1.2 broadcast_bitcast_fusion.1
  8.1 1.2 broadcast_bitcast_fusion
  9.3 0.6 pad_clamp_fusion
  9.9 1.1 copy.34
  11.1 0.4 copy.38
  11.5 1.1 reshape.277
  12.6 1.2 copy.28
  13.9 0.3 copy.29
  14.2 1.3 %copy.36 = s32[1,2,8,128]{3,1,2,0:T(2,128)} copy(s32[1,2,8,128]{3,2,1,0:T(8,128)} %add_bitcast_fusion) | data formatting | bytes 16384
  15.4 0.8 gather_fusion.1
  16.2 0.7 bitcast_dynamic-update-slice_fusion.15
  17.0 2.1 %collective-permute-start.1 = (bf16[136,512]{1,0:T(8,128)(2,1)S(1)}, bf16[136,512]{1,0:T(8,128)(2,1)S(1)}, u32[]{:S(2)}, u32[]{:S(2)}) collective-permute-start(bf16[136,512]{1,0:T(8,128)(2,1)S(1)} %collective-permute-done), channel_id=1, source_target_pairs={{0,2},{2,4},{4,6},{6,7},{7,5},{5,3},{3,1},{1,0},{8,10},{10,12},{12... | collective-permute-start | bytes 417800 | tf_op jit(solution)/shard_map/ppermute | solution.py:163
  19.1 3.1 %collective-permute-done.1 = bf16[136,512]{1,0:T(8,128)(2,1)S(1)} collective-permute-done((bf16[136,512]{1,0:T(8,128)(2,1)S(1)}, bf16[136,512]{1,0:T(8,128)(2,1)S(1)}, u32[]{:S(2)}, u32[]{:S(2)}) %collective-permute-start.1) | collective-permute-done | bytes 139296 | tf_op jit(solution)/shard_map/ppermute | solution.py:163
  22.1 1.9 %collective-permute-start.2 = (bf16[136,512]{1,0:T(8,128)(2,1)S(1)}, bf16[136,512]{1,0:T(8,128)(2,1)S(1)}, u32[]{:S(2)}, u32[]{:S(2)}) collective-permute-start(bf16[136,512]{1,0:T(8,128)(2,1)S(1)} %collective-permute-done.1), channel_id=1, source_target_pairs={{0,2},{2,4},{4,6},{6,7},{7,5},{5,3},{3,1},{1,0},{8,10},{10,12},{12... | collective-permute-start | bytes 417800 | tf_op jit(solution)/shard_map/ppermute | solution.py:163
  24.2 3.0 %collective-permute-done.2 = bf16[136,512]{1,0:T(8,128)(2,1)S(1)} collective-permute-done((bf16[136,512]{1,0:T(8,128)(2,1)S(1)}, bf16[136,512]{1,0:T(8,128)(2,1)S(1)}, u32[]{:S(2)}, u32[]{:S(2)}) %collective-permute-start.2) | collective-permute-done | bytes 139296 | tf_op jit(solution)/shard_map/ppermute | solution.py:163
  27.2 2.4 %collective-permute-start.3 = (bf16[136,512]{1,0:T(8,128)(2,1)S(1)}, bf16[136,512]{1,0:T(8,128)(2,1)S(1)}, u32[]{:S(2)}, u32[]{:S(2)}) collective-permute-start(bf16[136,512]{1,0:T(8,128)(2,1)S(1)} %collective-permute-done.2), channel_id=1, source_target_pairs={{0,2},{2,4},{4,6},{6,7},{7,5},{5,3},{3,1},{1,0},{8,10},{10,12},{12... | collective-permute-start | bytes 417800 | tf_op jit(solution)/shard_map/ppermute | solution.py:163
  29.6 2.9 %collective-permute-done.3 = bf16[136,512]{1,0:T(8,128)(2,1)S(1)} collective-permute-done((bf16[136,512]{1,0:T(8,128)(2,1)S(1)}, bf16[136,512]{1,0:T(8,128)(2,1)S(1)}, u32[]{:S(2)}, u32[]{:S(2)}) %collective-permute-start.3) | collective-permute-done | bytes 139296 | tf_op jit(solution)/shard_map/ppermute | solution.py:163
  32.6 1.4 %bitcast_dynamic-update-slice_fusion.7 = (bf16[8,256,512]{2,1,0:T(8,128)(2,1)}, bf16[256,512]{1,0:T(8,128)(2,1)}) fusion(bf16[8,136,512]{2,1,0:T(8,128)(2,1)S(1)} %bitcast_dynamic-update-slice_fusion.8, bf16[8,256,128]{2,1,0:T(8,128)(2,1)S(1)} %gather_fusion.1), kind=kOutput, calls=%fused_computation.40 | convolution fusion | flops 269615104 | bytes 2097152 | tf_op jit(solution)/shard_map/dot_general | solution.py:471
  34.0 2.1 %collective-permute-start.7 = (bf16[256,512]{1,0:T(8,128)(2,1)}, bf16[256,512]{1,0:T(8,128)(2,1)S(1)}, u32[]{:S(2)}, u32[]{:S(2)}) collective-permute-start(bf16[256,512]{1,0:T(8,128)(2,1)} %get-tuple-element.22), channel_id=1, source_target_pairs={{0,2},{2,4},{4,6},{6,7},{7,5},{5,3},{3,1},{1,0},{8,10},{10,12},{12... | collective-permute-start | bytes 786440 | tf_op jit(solution)/shard_map/ppermute | solution.py:163
  36.1 6.3 %all-to-all-start = ((bf16[8,64,512]{2,1,0:T(8,128)(2,1)}), bf16[8,64,512]{2,1,0:T(8,128)(2,1)S(1)}, u32[]{:S(2)}, u32[]{:S(2)}) async-start(bf16[8,64,512]{2,1,0:T(8,128)(2,1)} %reshape.277), calls=%async_computation | async-start | bytes 1048576 | tf_op jit(solution)/shard_map/all_to_all | solution.py:456
  42.4 0.7 gather_fusion
  43.1 2.3 %bitcast_reduce_fusion.1 = (f32[8,2]{0,1:T(2,128)S(1)}, f32[8,256]{1,0:T(8,128)S(1)}) fusion(bf16[8,4096]{1,0:T(8,128)(2,1)S(1)} %bitcast.152, bf16[1,256,4096]{2,1,0:T(8,128)(2,1)} %param.20), kind=kOutput, calls=%fused_computation.67 | convolution fusion | flops 16785392 | bytes 2170944 | tf_op jit(solution)/shard_map/dot_general | solution.py:23
  45.4 3.6 %collective-permute-start.9 = (bf16[256,512]{1,0:T(8,128)(2,1)S(1)}, bf16[256,512]{1,0:T(8,128)(2,1)S(1)}, u32[]{:S(2)}, u32[]{:S(2)}) collective-permute-start(bf16[256,512]{1,0:T(8,128)(2,1)S(1)} %collective-permute-done.7), channel_id=1, source_target_pairs={{0,2},{2,4},{4,6},{6,7},{7,5},{5,3},{3,1},{1,0},{8,10},{10,12},{12... | collective-permute-start | bytes 786440 | tf_op jit(solution)/shard_map/ppermute | solution.py:163
  49.1 5.2 %collective-permute-done.9 = bf16[256,512]{1,0:T(8,128)(2,1)S(1)} collective-permute-done((bf16[256,512]{1,0:T(8,128)(2,1)S(1)}, bf16[256,512]{1,0:T(8,128)(2,1)S(1)}, u32[]{:S(2)}, u32[]{:S(2)}) %collective-permute-start.9) | collective-permute-done | bytes 262176 | tf_op jit(solution)/shard_map/ppermute | solution.py:163
  54.3 4.3 %collective-permute-start.10 = (bf16[256,512]{1,0:T(8,128)(2,1)S(1)}, bf16[256,512]{1,0:T(8,128)(2,1)S(1)}, u32[]{:S(2)}, u32[]{:S(2)}) collective-permute-start(bf16[256,512]{1,0:T(8,128)(2,1)S(1)} %collective-permute-done.9), channel_id=1, source_target_pairs={{0,2},{2,4},{4,6},{6,7},{7,5},{5,3},{3,1},{1,0},{8,10},{10,12},{12... | collective-permute-start | bytes 786440 | tf_op jit(solution)/shard_map/ppermute | solution.py:163
  58.6 3.1 %convert_reduce_fusion = f32[8,2048]{1,0:T(8,128)S(1)} fusion(s32[2048]{0:T(1024)S(1)} %bitcast.153, s32[8,256]{1,0:T(8,128)S(1)} %copy-done.5, pred[8,256]{1,0:T(8,128)(4,1)S(1)} %iota_compare_fusion), kind=kLoop, calls=%fused_computation.2 | loop fusion | flops 16760832 | bytes 83968 | tf_op jit(solution)/shard_map/reduce_sum | solution.py:496
  61.8 0.7 bitcast_dynamic-update-slice_fusion.6
  62.5 3.1 %collective-permute-start.11 = (bf16[256,512]{1,0:T(8,128)(2,1)S(1)}, bf16[256,512]{1,0:T(8,128)(2,1)S(1)}, u32[]{:S(2)}, u32[]{:S(2)}) collective-permute-start(bf16[256,512]{1,0:T(8,128)(2,1)S(1)} %collective-permute-done.10), channel_id=1, source_target_pairs={{0,2},{2,4},{4,6},{6,7},{7,5},{5,3},{3,1},{1,0},{8,10},{10,12},{12... | collective-permute-start | bytes 786440 | tf_op jit(solution)/shard_map/ppermute | solution.py:163
  65.7 0.7 bitcast_dynamic-update-slice_fusion.5
  66.4 0.4 collective-permute-start.13
  66.8 0.7 bitcast_dynamic-update-slice_fusion.4
  67.5 2.9 %collective-permute-done.11 = bf16[256,512]{1,0:T(8,128)(2,1)S(1)} collective-permute-done((bf16[256,512]{1,0:T(8,128)(2,1)S(1)}, bf16[256,512]{1,0:T(8,128)(2,1)S(1)}, u32[]{:S(2)}, u32[]{:S(2)}) %collective-permute-start.11) | collective-permute-done | bytes 262176 | tf_op jit(solution)/shard_map/ppermute | solution.py:163
  70.4 0.7 bitcast_dynamic-update-slice_fusion.3
  71.1 0.7 bitcast_dynamic-update-slice_fusion.2
  71.9 0.7 bitcast_dynamic-update-slice_fusion.1
  72.6 0.6 collective-permute-done.13
  73.2 0.7 bitcast_dynamic-update-slice_fusion
  74.0 2.9 %fusion.43 = f32[2048,512]{0,1:T(8,128)S(1)} fusion(bf16[2048,512]{1,0:T(8,128)(2,1)} %bitcast.22, bf16[512,512]{1,0:T(8,128)(2,1)S(1)} %bitcast.144), kind=kOutput, calls=%fused_computation.103 | convolution fusion | flops 1073741824 | bytes 6815744 | tf_op jit(solution)/shard_map/dot_general | solution.py:483
  77.0 0.2 bitcast_reduce_fusion
  77.2 0.3 copy-done.6
  77.5 0.2 fusion.6
  77.8 1.0 multiply_reduce_fusion.1
  78.8 1.5 %convolution_bitcast_fusion = f32[8,1,4096]{2,0,1:T(8,128)S(1)} fusion(bf16[1,256,4096]{2,1,0:T(8,128)(2,1)S(1)} %copy-done, bf16[2048,2,128]{0,2,1:T(8,128)(2,1)S(1)} %bitcast.142, f32[8,2,2048]{2,0,1:T(8,128)S(1)} %get-tuple-element.26, f32[8,2]{0,1:T(2,128)} %get-tuple-element.25, f32[8,2048]{1,0:T(8,128)S(1)} %convert_reduce_fusion), kind=kOutput, calls=%fused_computation.3 | convolution fusion | flops 25266176 | bytes 3473472 | tf_op jit(solution)/shard_map/dot_general | solution.py:506
  80.3 1.7 %collective-permute-start.14 = (f32[8,1,4096]{2,0,1:T(8,128)S(1)}, f32[8,1,4096]{2,0,1:T(8,128)S(1)}, u32[]{:S(2)}, u32[]{:S(2)}) collective-permute-start(f32[8,1,4096]{2,0,1:T(8,128)S(1)} %convolution_bitcast_fusion), channel_id=1, source_target_pairs={{0,1},{1,0},{2,3},{3,2},{4,5},{5,4},{6,7},{7,6},{8,9},{9,8},{10,11... | collective-permute-start | bytes 393224 | tf_op jit(solution)/shard_map/ppermute | solution.py:116
  81.9 3.3 %collective-permute-done.14 = f32[8,1,4096]{2,0,1:T(8,128)S(1)} collective-permute-done((f32[8,1,4096]{2,0,1:T(8,128)S(1)}, f32[8,1,4096]{2,0,1:T(8,128)S(1)}, u32[]{:S(2)}, u32[]{:S(2)}) %collective-permute-start.14) | collective-permute-done | bytes 131104 | tf_op jit(solution)/shard_map/ppermute | solution.py:116
  85.2 2.1 %collective-permute-start.15 = (f32[8,1,4096]{2,0,1:T(8,128)S(1)}, f32[8,1,4096]{2,0,1:T(8,128)S(1)}, u32[]{:S(2)}, u32[]{:S(2)}) collective-permute-start(f32[8,1,4096]{2,0,1:T(8,128)S(1)} %add.224), channel_id=1, source_target_pairs={{0,2},{1,3},{2,0},{3,1},{4,6},{5,7},{6,4},{7,5},{8,10},{9,11},{10,... | collective-permute-start | bytes 393224 | tf_op jit(solution)/shard_map/ppermute | solution.py:116
  87.3 3.4 %collective-permute-done.15 = f32[8,1,4096]{2,0,1:T(8,128)S(1)} collective-permute-done((f32[8,1,4096]{2,0,1:T(8,128)S(1)}, f32[8,1,4096]{2,0,1:T(8,128)S(1)}, u32[]{:S(2)}, u32[]{:S(2)}) %collective-permute-start.15) | collective-permute-done | bytes 131104 | tf_op jit(solution)/shard_map/ppermute | solution.py:116
  90.8 2.5 %collective-permute-start.16 = (f32[8,1,4096]{2,0,1:T(8,128)S(1)}, f32[8,1,4096]{2,0,1:T(8,128)S(1)}, u32[]{:S(2)}, u32[]{:S(2)}) collective-permute-start(f32[8,1,4096]{2,0,1:T(8,128)S(1)} %add.225), channel_id=1, source_target_pairs={{0,4},{1,5},{2,6},{3,7},{4,0},{5,1},{6,2},{7,3},{8,12},{9,13},{10,... | collective-permute-start | bytes 393224 | tf_op jit(solution)/shard_map/ppermute | solution.py:116
  93.3 4.8 %collective-permute-done.16 = f32[8,1,4096]{2,0,1:T(8,128)S(1)} collective-permute-done((f32[8,1,4096]{2,0,1:T(8,128)S(1)}, f32[8,1,4096]{2,0,1:T(8,128)S(1)}, u32[]{:S(2)}, u32[]{:S(2)}) %collective-permute-start.16) | collective-permute-done | bytes 131104 | tf_op jit(solution)/shard_map/ppermute | solution.py:116
  98.3 0.7 fusion.28.rows_ref
  99.0 12.0 %shard_map.154 = f32[8,4096]{1,0:T(8,128)} custom-call(bf16[8,4096]{1,0:T(8,128)(2,1)} %fusion.28.rows_ref, bf16[896,4096]{1,0:T(8,128)(2,1)} %bitcast.136, bf16[896,4096]{1,0:T(8,128)(2,1)} %bitcast.137, bf16[896,4096]{1,0:T(8,128)(2,1)} %bitcast.138, bf16[896,4096]{1,0:T(8,128)(2,1)} %bitcast.139, bf16[896,4096]{1,0:T(8,128)(2,1)} %bitcast.140, ...), custom_call_target="tpu_custom_call" | custom-call | tf_op jit(solution)/shard_map/pallas_call | solution.py:404
  111.0 1.0 reshape_reshape.4
  112.2 4.2 %collective-permute-done.17 = f32[2,2,1,1,4096]{4,2,1,0,3:T(1,128)S(1)} collective-permute-done((f32[2,2,1,1,4096]{4,2,1,0,3:T(1,128)S(1)}, f32[2,2,1,1,4096]{4,2,1,0,3:T(1,128)S(1)}, u32[]{:S(2)}, u32[]{:S(2)}) %collective-permute-start.17) | collective-permute-done | bytes 65568 | tf_op jit(solution)/shard_map/ppermute | solution.py:526
  116.5 0.3 collective-permute-start.18
  116.8 3.7 %collective-permute-done.18 = f32[2,1,1,1,4096]{4,2,1,0,3:T(1,128)S(1)} collective-permute-done((f32[2,1,1,1,4096]{4,2,1,0,3:T(1,128)S(1)}, f32[2,1,1,1,4096]{4,2,1,0,3:T(1,128)S(1)}, u32[]{:S(2)}, u32[]{:S(2)}) %collective-permute-start.18) | collective-permute-done | bytes 32800 | tf_op jit(solution)/shard_map/ppermute | solution.py:526
  120.7 2.3 %collective-permute-start.20 = (f32[1,4096]{1,0:T(1,128)S(1)}, f32[1,4096]{1,0:T(1,128)S(1)}, u32[]{:S(2)}, u32[]{:S(2)}) collective-permute-start(f32[1,4096]{1,0:T(1,128)S(1)} %dynamic-slice_bitcast_fusion), channel_id=1, source_target_pairs={{0,12},{1,13},{2,14},{3,15},{4,8},{5,9},{6,10},{7,11},{8,20},{9,21... | collective-permute-start | bytes 49160 | tf_op jit(solution)/shard_map/ppermute | solution.py:543
  123.0 0.8 collective-permute-done.19
  123.8 1.9 %collective-permute-done.20 = f32[1,4096]{1,0:T(1,128)S(1)} collective-permute-done((f32[1,4096]{1,0:T(1,128)S(1)}, f32[1,4096]{1,0:T(1,128)S(1)}, u32[]{:S(2)}, u32[]{:S(2)}) %collective-permute-start.20) | collective-permute-done | bytes 16416 | tf_op jit(solution)/shard_map/ppermute | solution.py:543
  125.7 0.6 convert_bitcast_fusion
  (60 shorter events, 1.2 us)
Async XLA Ops:
  0.0 78.8 %copy-start = (bf16[1,256,4096]{2,1,0:T(8,128)(2,1)S(1)}, bf16[1,256,4096]{2,1,0:T(8,128)(2,1)}, u32[]{:S(2)}) copy-start(bf16[1,256,4096]{2,1,0:T(8,128)(2,1)} %param.25) | copy-start | bytes 6291460
  0.9 10.1 %copy-start.2 = (bf16[8,512]{1,0:T(8,128)(2,1)}, bf16[8,512]{1,0:T(8,128)(2,1)S(1)}, u32[]{:S(2)}) copy-start(bf16[8,512]{1,0:T(8,128)(2,1)S(1)} %reshape_squeeze.9) | copy-start | bytes 24580
  2.5 14.4 %collective-permute-start = (bf16[136,512]{1,0:T(8,128)(2,1)}, bf16[136,512]{1,0:T(8,128)(2,1)S(1)}, u32[]{:S(2)}, u32[]{:S(2)}) collective-permute-start(bf16[136,512]{1,0:T(8,128)(2,1)} %pad_maximum_fusion), channel_id=1, source_target_pairs={{0,2},{2,4},{4,6},{6,7},{7,5},{5,3},{3,1},{1,0},{8,10},{10,12},{12... | collective-permute-start | bytes 417800 | tf_op jit(solution)/shard_map/ppermute | solution.py:163
  5.5 13.5 %collective-permute-start.4 = (bf16[136,512]{1,0:T(8,128)(2,1)}, bf16[136,512]{1,0:T(8,128)(2,1)S(1)}, u32[]{:S(2)}, u32[]{:S(2)}) collective-permute-start(bf16[136,512]{1,0:T(8,128)(2,1)} %pad_maximum_fusion), channel_id=1, source_target_pairs={{0,1},{2,0},{4,2},{6,4},{7,6},{5,7},{3,5},{1,3},{8,9},{10,8},{12,1... | collective-permute-start | bytes 417800 | tf_op jit(solution)/shard_map/ppermute | solution.py:167
  11.5 4.7 %copy-start.1 = (bf16[1,128,512]{2,1,0:T(8,128)(2,1)S(1)}, bf16[1,128,512]{2,1,0:T(8,128)(2,1)}, u32[]{:S(2)}) copy-start(bf16[1,128,512]{2,1,0:T(8,128)(2,1)} %param.23) | copy-start | bytes 393220
  17.0 5.2 %collective-permute-start.1 = (bf16[136,512]{1,0:T(8,128)(2,1)S(1)}, bf16[136,512]{1,0:T(8,128)(2,1)S(1)}, u32[]{:S(2)}, u32[]{:S(2)}) collective-permute-start(bf16[136,512]{1,0:T(8,128)(2,1)S(1)} %collective-permute-done), channel_id=1, source_target_pairs={{0,2},{2,4},{4,6},{6,7},{7,5},{5,3},{3,1},{1,0},{8,10},{10,12},{12... | collective-permute-start | bytes 417800 | tf_op jit(solution)/shard_map/ppermute | solution.py:163
  19.0 5.1 %collective-permute-start.5 = (bf16[136,512]{1,0:T(8,128)(2,1)S(1)}, bf16[136,512]{1,0:T(8,128)(2,1)S(1)}, u32[]{:S(2)}, u32[]{:S(2)}) collective-permute-start(bf16[136,512]{1,0:T(8,128)(2,1)S(1)} %collective-permute-done.4), channel_id=1, source_target_pairs={{0,1},{2,0},{4,2},{6,4},{7,6},{5,7},{3,5},{1,3},{8,9},{10,8},{12,1... | collective-permute-start | bytes 417800 | tf_op jit(solution)/shard_map/ppermute | solution.py:167
  22.1 5.1 %collective-permute-start.2 = (bf16[136,512]{1,0:T(8,128)(2,1)S(1)}, bf16[136,512]{1,0:T(8,128)(2,1)S(1)}, u32[]{:S(2)}, u32[]{:S(2)}) collective-permute-start(bf16[136,512]{1,0:T(8,128)(2,1)S(1)} %collective-permute-done.1), channel_id=1, source_target_pairs={{0,2},{2,4},{4,6},{6,7},{7,5},{5,3},{3,1},{1,0},{8,10},{10,12},{12... | collective-permute-start | bytes 417800 | tf_op jit(solution)/shard_map/ppermute | solution.py:163
  24.1 8.5 %collective-permute-start.6 = (bf16[136,512]{1,0:T(8,128)(2,1)S(1)}, bf16[136,512]{1,0:T(8,128)(2,1)S(1)}, u32[]{:S(2)}, u32[]{:S(2)}) collective-permute-start(bf16[136,512]{1,0:T(8,128)(2,1)S(1)} %collective-permute-done.5), channel_id=1, source_target_pairs={{0,1},{2,0},{4,2},{6,4},{7,6},{5,7},{3,5},{1,3},{8,9},{10,8},{12,1... | collective-permute-start | bytes 417800 | tf_op jit(solution)/shard_map/ppermute | solution.py:167
  27.2 5.3 %collective-permute-start.3 = (bf16[136,512]{1,0:T(8,128)(2,1)S(1)}, bf16[136,512]{1,0:T(8,128)(2,1)S(1)}, u32[]{:S(2)}, u32[]{:S(2)}) collective-permute-start(bf16[136,512]{1,0:T(8,128)(2,1)S(1)} %collective-permute-done.2), channel_id=1, source_target_pairs={{0,2},{2,4},{4,6},{6,7},{7,5},{5,3},{3,1},{1,0},{8,10},{10,12},{12... | collective-permute-start | bytes 417800 | tf_op jit(solution)/shard_map/ppermute | solution.py:163
  34.0 15.0 %copy-start.8 = (s32[8]{0:T(128)S(1)}, s32[8]{0:T(128)}, u32[]{:S(2)}) copy-start(s32[8]{0:T(128)} %param.19) | copy-start | bytes 100
  34.0 24.6 %copy-start.3 = (s32[1,2,8,128]{3,1,2,0:T(2,128)S(1)}, s32[1,2,8,128]{3,1,2,0:T(2,128)}, u32[]{:S(2)}) copy-start(s32[1,2,8,128]{3,1,2,0:T(2,128)} %copy.36) | copy-start | bytes 24580
  34.0 24.6 %copy-start.5 = (s32[8,256]{1,0:T(8,128)S(1)}, s32[8,256]{1,0:T(8,128)}, u32[]{:S(2)}) copy-start(s32[8,256]{1,0:T(8,128)} %param.18) | copy-start | bytes 24580
  34.0 11.4 %collective-permute-start.7 = (bf16[256,512]{1,0:T(8,128)(2,1)}, bf16[256,512]{1,0:T(8,128)(2,1)S(1)}, u32[]{:S(2)}, u32[]{:S(2)}) collective-permute-start(bf16[256,512]{1,0:T(8,128)(2,1)} %get-tuple-element.22), channel_id=1, source_target_pairs={{0,2},{2,4},{4,6},{6,7},{7,5},{5,3},{3,1},{1,0},{8,10},{10,12},{12... | collective-permute-start | bytes 786440 | tf_op jit(solution)/shard_map/ppermute | solution.py:163
  36.1 9.3 %collective-permute-start.8 = (bf16[256,512]{1,0:T(8,128)(2,1)}, bf16[256,512]{1,0:T(8,128)(2,1)S(1)}, u32[]{:S(2)}, u32[]{:S(2)}) collective-permute-start(bf16[256,512]{1,0:T(8,128)(2,1)} %get-tuple-element.22), channel_id=1, source_target_pairs={{0,1},{2,0},{4,2},{6,4},{7,6},{5,7},{3,5},{1,3},{8,9},{10,8},{12,1... | collective-permute-start | bytes 786440 | tf_op jit(solution)/shard_map/ppermute | solution.py:167
  36.1 37.9 %all-to-all-start = ((bf16[8,64,512]{2,1,0:T(8,128)(2,1)}), bf16[8,64,512]{2,1,0:T(8,128)(2,1)S(1)}, u32[]{:S(2)}, u32[]{:S(2)}) async-start(bf16[8,64,512]{2,1,0:T(8,128)(2,1)} %reshape.277), calls=%async_computation | async-start | bytes 1048576 | tf_op jit(solution)/shard_map/all_to_all | solution.py:456
  45.4 8.9 %collective-permute-start.9 = (bf16[256,512]{1,0:T(8,128)(2,1)S(1)}, bf16[256,512]{1,0:T(8,128)(2,1)S(1)}, u32[]{:S(2)}, u32[]{:S(2)}) collective-permute-start(bf16[256,512]{1,0:T(8,128)(2,1)S(1)} %collective-permute-done.7), channel_id=1, source_target_pairs={{0,2},{2,4},{4,6},{6,7},{7,5},{5,3},{3,1},{1,0},{8,10},{10,12},{12... | collective-permute-start | bytes 786440 | tf_op jit(solution)/shard_map/ppermute | solution.py:163
  49.0 17.4 %collective-permute-start.12 = (bf16[256,512]{1,0:T(8,128)(2,1)S(1)}, bf16[256,512]{1,0:T(8,128)(2,1)S(1)}, u32[]{:S(2)}, u32[]{:S(2)}) collective-permute-start(bf16[256,512]{1,0:T(8,128)(2,1)S(1)} %collective-permute-done.8), channel_id=1, source_target_pairs={{0,1},{2,0},{4,2},{6,4},{7,6},{5,7},{3,5},{1,3},{8,9},{10,8},{12,1... | collective-permute-start | bytes 786440 | tf_op jit(solution)/shard_map/ppermute | solution.py:167
  54.3 8.2 %collective-permute-start.10 = (bf16[256,512]{1,0:T(8,128)(2,1)S(1)}, bf16[256,512]{1,0:T(8,128)(2,1)S(1)}, u32[]{:S(2)}, u32[]{:S(2)}) collective-permute-start(bf16[256,512]{1,0:T(8,128)(2,1)S(1)} %collective-permute-done.9), channel_id=1, source_target_pairs={{0,2},{2,4},{4,6},{6,7},{7,5},{5,3},{3,1},{1,0},{8,10},{10,12},{12... | collective-permute-start | bytes 786440 | tf_op jit(solution)/shard_map/ppermute | solution.py:163
  62.5 7.9 %collective-permute-start.11 = (bf16[256,512]{1,0:T(8,128)(2,1)S(1)}, bf16[256,512]{1,0:T(8,128)(2,1)S(1)}, u32[]{:S(2)}, u32[]{:S(2)}) collective-permute-start(bf16[256,512]{1,0:T(8,128)(2,1)S(1)} %collective-permute-done.10), channel_id=1, source_target_pairs={{0,2},{2,4},{4,6},{6,7},{7,5},{5,3},{3,1},{1,0},{8,10},{10,12},{12... | collective-permute-start | bytes 786440 | tf_op jit(solution)/shard_map/ppermute | solution.py:163
  66.4 6.8 %collective-permute-start.13 = (bf16[256,512]{1,0:T(8,128)(2,1)S(1)}, bf16[256,512]{1,0:T(8,128)(2,1)S(1)}, u32[]{:S(2)}, u32[]{:S(2)}) collective-permute-start(bf16[256,512]{1,0:T(8,128)(2,1)S(1)} %collective-permute-done.12), channel_id=1, source_target_pairs={{0,1},{2,0},{4,2},{6,4},{7,6},{5,7},{3,5},{1,3},{8,9},{10,8},{12,1... | collective-permute-start | bytes 786440 | tf_op jit(solution)/shard_map/ppermute | solution.py:167
  76.9 0.7 copy-start.6
  77.2 0.6 copy-start.7
  78.8 19.5 %copy-start.4 = (f32[1,4096]{1,0:T(1,128)S(1)}, f32[1,4096]{1,0:T(1,128)}, u32[]{:S(2)}) copy-start(f32[1,4096]{1,0:T(1,128)} %param.26) | copy-start | bytes 49156
  80.3 5.0 %collective-permute-start.14 = (f32[8,1,4096]{2,0,1:T(8,128)S(1)}, f32[8,1,4096]{2,0,1:T(8,128)S(1)}, u32[]{:S(2)}, u32[]{:S(2)}) collective-permute-start(f32[8,1,4096]{2,0,1:T(8,128)S(1)} %convolution_bitcast_fusion), channel_id=1, source_target_pairs={{0,1},{1,0},{2,3},{3,2},{4,5},{5,4},{6,7},{7,6},{8,9},{9,8},{10,11... | collective-permute-start | bytes 393224 | tf_op jit(solution)/shard_map/ppermute | solution.py:116
  85.2 5.5 %collective-permute-start.15 = (f32[8,1,4096]{2,0,1:T(8,128)S(1)}, f32[8,1,4096]{2,0,1:T(8,128)S(1)}, u32[]{:S(2)}, u32[]{:S(2)}) collective-permute-start(f32[8,1,4096]{2,0,1:T(8,128)S(1)} %add.224), channel_id=1, source_target_pairs={{0,2},{1,3},{2,0},{3,1},{4,6},{5,7},{6,4},{7,5},{8,10},{9,11},{10,... | collective-permute-start | bytes 393224 | tf_op jit(solution)/shard_map/ppermute | solution.py:116
  90.8 7.3 %collective-permute-start.16 = (f32[8,1,4096]{2,0,1:T(8,128)S(1)}, f32[8,1,4096]{2,0,1:T(8,128)S(1)}, u32[]{:S(2)}, u32[]{:S(2)}) collective-permute-start(f32[8,1,4096]{2,0,1:T(8,128)S(1)} %add.225), channel_id=1, source_target_pairs={{0,4},{1,5},{2,6},{3,7},{4,0},{5,1},{6,2},{7,3},{8,12},{9,13},{10,... | collective-permute-start | bytes 393224 | tf_op jit(solution)/shard_map/ppermute | solution.py:116
  112.1 4.3 %collective-permute-start.17 = (f32[2,2,1,1,4096]{4,2,1,0,3:T(1,128)S(1)}, f32[2,2,1,1,4096]{4,2,1,0,3:T(1,128)S(1)}, u32[]{:S(2)}, u32[]{:S(2)}) collective-permute-start(f32[2,2,1,1,4096]{4,2,1,0,3:T(1,128)S(1)} %constant_dynamic-slice_fusion.1), channel_id=1, source_target_pairs={{0,1},{1,0},{2,3},{3,2},{4,5},{5,4},{6,7},{7,6},{8,9},{9,8},{10,11... | collective-permute-start | bytes 196616 | tf_op jit(solution)/shard_map/ppermute | solution.py:526
  116.5 4.0 %collective-permute-start.18 = (f32[2,1,1,1,4096]{4,2,1,0,3:T(1,128)S(1)}, f32[2,1,1,1,4096]{4,2,1,0,3:T(1,128)S(1)}, u32[]{:S(2)}, u32[]{:S(2)}) collective-permute-start(f32[2,1,1,1,4096]{4,2,1,0,3:T(1,128)S(1)} %constant_dynamic-slice_fusion), channel_id=1, source_target_pairs={{0,2},{1,3},{2,0},{3,1},{4,6},{5,7},{6,4},{7,5},{8,10},{9,11},{10,... | collective-permute-start | bytes 98312 | tf_op jit(solution)/shard_map/ppermute | solution.py:526
  120.6 3.2 %collective-permute-start.19 = (f32[1,4096]{1,0:T(1,128)S(1)}, f32[1,4096]{1,0:T(1,128)S(1)}, u32[]{:S(2)}, u32[]{:S(2)}) collective-permute-start(f32[1,4096]{1,0:T(1,128)S(1)} %bitcast_add_fusion), channel_id=1, source_target_pairs={{0,8},{1,9},{2,10},{3,11},{4,12},{5,13},{6,14},{7,15},{8,16},{9,17... | collective-permute-start | bytes 49160 | tf_op jit(solution)/shard_map/ppermute | solution.py:542
  120.7 5.0 %collective-permute-start.20 = (f32[1,4096]{1,0:T(1,128)S(1)}, f32[1,4096]{1,0:T(1,128)S(1)}, u32[]{:S(2)}, u32[]{:S(2)}) collective-permute-start(f32[1,4096]{1,0:T(1,128)S(1)} %dynamic-slice_bitcast_fusion), channel_id=1, source_target_pairs={{0,12},{1,13},{2,14},{3,15},{4,8},{5,9},{6,10},{7,11},{8,20},{9,21... | collective-permute-start | bytes 49160 | tf_op jit(solution)/shard_map/ppermute | solution.py:543

commit v16 on v15

--- a/solution.py
+++ b/solution.py
@@ -374,12 +374,14 @@
     return output_rows[None]
 
 
-def ffn_block(rows_ref, gate_a, gate_b, up_a, up_b, down_a, down_b, out_ref):
+def ffn_block(acts_ref, attn_ref, gain_ref, gate_a, gate_b, up_a, up_b, down_a, down_b, out_ref, rows_ref):
     step = pl.program_id(0)
 
     @pl.when(step == 0)
     def _():
         out_ref[...] = jnp.zeros_like(out_ref)
+        residual = acts_ref[...].astype(jnp.float32) + attn_ref[...]
+        rows_ref[...] = rms_norm(residual, gain_ref[...]).astype(rows_ref.dtype)
 
     half = gate_a.shape[1]
     rows_a = rows_ref[:, :half]
@@ -394,21 +396,33 @@
     out_ref[:, half:] += jnp.dot(hidden, down_b[...], preferred_element_type=jnp.float32)
 
 
-def gated_ffn(rows, gate, up, down):
+def gated_ffn(acts_rows, attn_rows, gain, gate, up, down):
     units, width = gate.shape
     block = 128 if units % 128 == 0 else units
     half = width // 2
-    count = rows.shape[0]
+    count = acts_rows.shape[0]
+    whole = pl.BlockSpec((count, width), lambda i: (0, 0))
     first = pl.BlockSpec((block, half), lambda i: (i, 0))
     second = pl.BlockSpec((block, half), lambda i: (i, 1))
     return pl.pallas_call(
         ffn_block,
         grid=(units // block,),
-        in_specs=[pl.BlockSpec((count, width), lambda i: (0, 0)), first, second, first, second, first, second],
-        out_specs=pl.BlockSpec((count, width), lambda i: (0, 0)),
+        in_specs=[
+            whole,
+            whole,
+            pl.BlockSpec((1, width), lambda i: (0, 0)),
+            first,
+            second,
+            first,
+            second,
+            first,
+            second,
+        ],
+        out_specs=whole,
         out_shape=jax.ShapeDtypeStruct((count, width), jnp.float32),
+        scratch_shapes=[pltpu.VMEM((count, width), jnp.bfloat16)],
         compiler_params=pltpu.CompilerParams(dimension_semantics=("arbitrary",)),
-    )(rows, gate, gate, up, up, down, down)
+    )(acts_rows, attn_rows, gain.reshape(1, width), gate, gate, up, up, down, down)
 
 
 def heads_split(
@@ -507,8 +521,14 @@
     attn_all = doubling_sum(attn_part.reshape(group_size, sites_here, -1), group_size)
     residual_all = everyone.reshape(group_size, sites_here, -1).astype(jnp.float32) + attn_all
     residual = lax.dynamic_index_in_dim(residual_all, my_index, 0, keepdims=False)
-    normed_rows = rms_norm(residual_all, ffn_gain[0]).astype(jnp.bfloat16).reshape(-1, model_width)
-    down_part = gated_ffn(normed_rows, gate_weight[0], up_weight[0], down_weight[0])
+    down_part = gated_ffn(
+        everyone,
+        attn_all.reshape(-1, model_width),
+        ffn_gain[0],
+        gate_weight[0],
+        up_weight[0],
+        down_weight[0],
+    )
     down_part = down_part.reshape(group_size, sites_here, -1)
     return last_round(down_part, residual, group_size, section_count, my_index)
 

time: 127 us -> 126 us (level)
    ppermute x1, starting transfers between devices: 2.33 us -> 0.06 us  [last_round(): other_part = lax.ppermute(send.reshape(rest), ('section', 'site'), across)]
    ppermute x1, starting transfers between devices: 0.06 us -> 2.2 us  [last_round(): mine_part = lax.ppermute(own, ('section', 'site'), forward)]
  transfers between devices with their start and end apart: 22 -> 22, of which waited for: 13 -> 12; matrix products, arithmetic and copies ran while one was open for 18% -> 18% of each run, Pallas kernels for 0% -> 0%
where the time goes in v16:
time: 126 us; the launch traced here: 125 us
  waiting for transfers between devices  39.4 us (31%)
  starting transfers between devices  38.1 us (30%)
  local copies, waits for them, and re-layouts  15.5 us (12%)
  Pallas kernels  12.3 us (10%)
  other arithmetic  10.6 us (8%)
  matrix products  9.25 us (7%)
    ppermute x8, starting transfers between devices, _issue(): self.ahead = lax.ppermute(self.ahead, 'site', self.forward)  22.6 us
    ppermute x8, waiting for transfers between devices, _issue(): self.ahead = lax.ppermute(self.ahead, 'site', self.forward)  17.2 us
    pallas_call x1, Pallas kernels, gated_ffn(): pl.pallas_call(ffn_block, grid=(units // block,), in_specs=[whole, whole,...  12.3 us
    ppermute x3, waiting for transfers between devices, doubling_sum(): state = state + lax.ppermute(state, 'site', xor_pairs(count, bit))  11.6 us
    ppermute x2, waiting for transfers between devices, last_round(): state = keep + lax.ppermute(send, 'site', xor_pairs(group_size, bit))  7.9 us
    unnamed x34, local copies, waits for them, and re-layouts  7.84 us
    all_to_all x1, starting transfers between devices, heads_split(): lax.all_to_all(col_blocks, 'site', split_axis=0, concat_axis=0, tiled=True)  6.25 us
    ppermute x3, starting transfers between devices, doubling_sum(): state = state + lax.ppermute(state, 'site', xor_pairs(count, bit))  6.2 us
  transfers between devices with their start and end apart: 22, of which 12 were waited for; matrix products, arithmetic and copies ran while one was open for 18% of the time, Pallas kernels for 0%

profile of v16, /device:TPU:0, one launch (start us, length us, event | category | flops | bytes accessed | tf_op | source)
XLA Modules:
  0.0 125.5 jit_solution(14672488452222250858)
XLA Ops:
  0.0 0.9 reduce
  1.0 1.6 %pad_maximum_fusion = bf16[136,512]{1,0:T(8,128)(2,1)} fusion(bf16[8,512]{1,0:T(8,128)(2,1)S(1)} %reshape_squeeze.9, bf16[128,512]{1,0:T(8,128)(2,1)} %bitcast.153), kind=kLoop, calls=%fused_computation.41 | loop fusion | flops 278528 | bytes 278528 | tf_op jit(solution)/shard_map/concatenate | solution.py:459
  2.5 3.0 %collective-permute-start = (bf16[136,512]{1,0:T(8,128)(2,1)}, bf16[136,512]{1,0:T(8,128)(2,1)S(1)}, u32[]{:S(2)}, u32[]{:S(2)}) collective-permute-start(bf16[136,512]{1,0:T(8,128)(2,1)} %pad_maximum_fusion), channel_id=1, source_target_pairs={{0,2},{2,4},{4,6},{6,7},{7,5},{5,3},{3,1},{1,0},{8,10},{10,12},{12... | collective-permute-start | bytes 417800 | tf_op jit(solution)/shard_map/ppermute | solution.py:163
  5.6 0.7 broadcast_multiply_fusion
  6.2 1.2 broadcast_bitcast_fusion
  7.5 1.2 broadcast_bitcast_fusion.1
  8.8 0.6 pad_clamp_fusion
  9.3 0.6 copy.36
  9.9 1.2 copy.28
  11.2 0.3 copy.29
  11.5 1.2 copy.34
  12.7 0.4 copy.38
  13.1 1.1 reshape.261
  14.2 0.8 gather_fusion.1
  15.0 0.7 bitcast_dynamic-update-slice_fusion.15
  15.7 2.1 %collective-permute-start.1 = (bf16[136,512]{1,0:T(8,128)(2,1)S(1)}, bf16[136,512]{1,0:T(8,128)(2,1)S(1)}, u32[]{:S(2)}, u32[]{:S(2)}) collective-permute-start(bf16[136,512]{1,0:T(8,128)(2,1)S(1)} %collective-permute-done), channel_id=1, source_target_pairs={{0,2},{2,4},{4,6},{6,7},{7,5},{5,3},{3,1},{1,0},{8,10},{10,12},{12... | collective-permute-start | bytes 417800 | tf_op jit(solution)/shard_map/ppermute | solution.py:163
  17.8 3.1 %collective-permute-done.1 = bf16[136,512]{1,0:T(8,128)(2,1)S(1)} collective-permute-done((bf16[136,512]{1,0:T(8,128)(2,1)S(1)}, bf16[136,512]{1,0:T(8,128)(2,1)S(1)}, u32[]{:S(2)}, u32[]{:S(2)}) %collective-permute-start.1) | collective-permute-done | bytes 139296 | tf_op jit(solution)/shard_map/ppermute | solution.py:163
  20.9 1.9 %collective-permute-start.2 = (bf16[136,512]{1,0:T(8,128)(2,1)S(1)}, bf16[136,512]{1,0:T(8,128)(2,1)S(1)}, u32[]{:S(2)}, u32[]{:S(2)}) collective-permute-start(bf16[136,512]{1,0:T(8,128)(2,1)S(1)} %collective-permute-done.1), channel_id=1, source_target_pairs={{0,2},{2,4},{4,6},{6,7},{7,5},{5,3},{3,1},{1,0},{8,10},{10,12},{12... | collective-permute-start | bytes 417800 | tf_op jit(solution)/shard_map/ppermute | solution.py:163
  22.9 3.0 %collective-permute-done.2 = bf16[136,512]{1,0:T(8,128)(2,1)S(1)} collective-permute-done((bf16[136,512]{1,0:T(8,128)(2,1)S(1)}, bf16[136,512]{1,0:T(8,128)(2,1)S(1)}, u32[]{:S(2)}, u32[]{:S(2)}) %collective-permute-start.2) | collective-permute-done | bytes 139296 | tf_op jit(solution)/shard_map/ppermute | solution.py:163
  26.0 2.4 %collective-permute-start.3 = (bf16[136,512]{1,0:T(8,128)(2,1)S(1)}, bf16[136,512]{1,0:T(8,128)(2,1)S(1)}, u32[]{:S(2)}, u32[]{:S(2)}) collective-permute-start(bf16[136,512]{1,0:T(8,128)(2,1)S(1)} %collective-permute-done.2), channel_id=1, source_target_pairs={{0,2},{2,4},{4,6},{6,7},{7,5},{5,3},{3,1},{1,0},{8,10},{10,12},{12... | collective-permute-start | bytes 417800 | tf_op jit(solution)/shard_map/ppermute | solution.py:163
  28.3 2.9 %collective-permute-done.3 = bf16[136,512]{1,0:T(8,128)(2,1)S(1)} collective-permute-done((bf16[136,512]{1,0:T(8,128)(2,1)S(1)}, bf16[136,512]{1,0:T(8,128)(2,1)S(1)}, u32[]{:S(2)}, u32[]{:S(2)}) %collective-permute-start.3) | collective-permute-done | bytes 139296 | tf_op jit(solution)/shard_map/ppermute | solution.py:163
  31.4 1.4 %bitcast_dynamic-update-slice_fusion.7 = (bf16[8,256,512]{2,1,0:T(8,128)(2,1)}, bf16[256,512]{1,0:T(8,128)(2,1)}) fusion(bf16[8,136,512]{2,1,0:T(8,128)(2,1)S(1)} %bitcast_dynamic-update-slice_fusion.8, bf16[8,256,128]{2,1,0:T(8,128)(2,1)S(1)} %gather_fusion.1), kind=kOutput, calls=%fused_computation.40 | convolution fusion | flops 269615104 | bytes 2097152 | tf_op jit(solution)/shard_map/dot_general | solution.py:485
  32.8 2.1 %collective-permute-start.7 = (bf16[256,512]{1,0:T(8,128)(2,1)}, bf16[256,512]{1,0:T(8,128)(2,1)S(1)}, u32[]{:S(2)}, u32[]{:S(2)}) collective-permute-start(bf16[256,512]{1,0:T(8,128)(2,1)} %get-tuple-element.20), channel_id=1, source_target_pairs={{0,2},{2,4},{4,6},{6,7},{7,5},{5,3},{3,1},{1,0},{8,10},{10,12},{12... | collective-permute-start | bytes 786440 | tf_op jit(solution)/shard_map/ppermute | solution.py:163
  34.9 6.3 %all-to-all-start = ((bf16[8,64,512]{2,1,0:T(8,128)(2,1)}), bf16[8,64,512]{2,1,0:T(8,128)(2,1)S(1)}, u32[]{:S(2)}, u32[]{:S(2)}) async-start(bf16[8,64,512]{2,1,0:T(8,128)(2,1)} %reshape.261), calls=%async_computation | async-start | bytes 1048576 | tf_op jit(solution)/shard_map/all_to_all | solution.py:470
  41.1 0.7 gather_fusion
  41.8 2.3 %bitcast_reduce_fusion.1 = (f32[8,2]{0,1:T(2,128)S(1)}, f32[8,256]{1,0:T(8,128)S(1)}) fusion(bf16[8,4096]{1,0:T(8,128)(2,1)S(1)} %bitcast.149, bf16[1,256,4096]{2,1,0:T(8,128)(2,1)} %param.20), kind=kOutput, calls=%fused_computation.65 | convolution fusion | flops 16785392 | bytes 2170944 | tf_op jit(solution)/shard_map/dot_general | solution.py:23
  44.2 3.6 %collective-permute-start.9 = (bf16[256,512]{1,0:T(8,128)(2,1)S(1)}, bf16[256,512]{1,0:T(8,128)(2,1)S(1)}, u32[]{:S(2)}, u32[]{:S(2)}) collective-permute-start(bf16[256,512]{1,0:T(8,128)(2,1)S(1)} %collective-permute-done.7), channel_id=1, source_target_pairs={{0,2},{2,4},{4,6},{6,7},{7,5},{5,3},{3,1},{1,0},{8,10},{10,12},{12... | collective-permute-start | bytes 786440 | tf_op jit(solution)/shard_map/ppermute | solution.py:163
  47.8 5.2 %collective-permute-done.9 = bf16[256,512]{1,0:T(8,128)(2,1)S(1)} collective-permute-done((bf16[256,512]{1,0:T(8,128)(2,1)S(1)}, bf16[256,512]{1,0:T(8,128)(2,1)S(1)}, u32[]{:S(2)}, u32[]{:S(2)}) %collective-permute-start.9) | collective-permute-done | bytes 262176 | tf_op jit(solution)/shard_map/ppermute | solution.py:163
  53.1 4.3 %collective-permute-start.10 = (bf16[256,512]{1,0:T(8,128)(2,1)S(1)}, bf16[256,512]{1,0:T(8,128)(2,1)S(1)}, u32[]{:S(2)}, u32[]{:S(2)}) collective-permute-start(bf16[256,512]{1,0:T(8,128)(2,1)S(1)} %collective-permute-done.9), channel_id=1, source_target_pairs={{0,2},{2,4},{4,6},{6,7},{7,5},{5,3},{3,1},{1,0},{8,10},{10,12},{12... | collective-permute-start | bytes 786440 | tf_op jit(solution)/shard_map/ppermute | solution.py:163
  57.4 3.2 %convert_reduce_fusion = f32[8,2048]{1,0:T(8,128)S(1)} fusion(s32[2048]{0:T(1024)S(1)} %bitcast.155, s32[8,256]{1,0:T(8,128)S(1)} %copy-done.5, pred[8,256]{1,0:T(8,128)(4,1)S(1)} %iota_compare_fusion), kind=kLoop, calls=%fused_computation.2 | loop fusion | flops 16760832 | bytes 83968 | tf_op jit(solution)/shard_map/reduce_sum | solution.py:510
  60.6 0.7 bitcast_dynamic-update-slice_fusion.6
  61.3 3.1 %collective-permute-start.11 = (bf16[256,512]{1,0:T(8,128)(2,1)S(1)}, bf16[256,512]{1,0:T(8,128)(2,1)S(1)}, u32[]{:S(2)}, u32[]{:S(2)}) collective-permute-start(bf16[256,512]{1,0:T(8,128)(2,1)S(1)} %collective-permute-done.10), channel_id=1, source_target_pairs={{0,2},{2,4},{4,6},{6,7},{7,5},{5,3},{3,1},{1,0},{8,10},{10,12},{12... | collective-permute-start | bytes 786440 | tf_op jit(solution)/shard_map/ppermute | solution.py:163
  64.4 0.7 bitcast_dynamic-update-slice_fusion.5
  65.1 0.4 collective-permute-start.13
  65.5 0.7 bitcast_dynamic-update-slice_fusion.4
  66.3 2.9 %collective-permute-done.11 = bf16[256,512]{1,0:T(8,128)(2,1)S(1)} collective-permute-done((bf16[256,512]{1,0:T(8,128)(2,1)S(1)}, bf16[256,512]{1,0:T(8,128)(2,1)S(1)}, u32[]{:S(2)}, u32[]{:S(2)}) %collective-permute-start.11) | collective-permute-done | bytes 262176 | tf_op jit(solution)/shard_map/ppermute | solution.py:163
  69.2 0.7 bitcast_dynamic-update-slice_fusion.3
  69.9 0.7 bitcast_dynamic-update-slice_fusion.2
  70.6 0.7 bitcast_dynamic-update-slice_fusion.1
  71.3 0.7 collective-permute-done.13
  72.0 0.7 bitcast_dynamic-update-slice_fusion
  72.7 2.9 %fusion.44 = f32[2048,512]{0,1:T(8,128)S(1)} fusion(bf16[2048,512]{1,0:T(8,128)(2,1)} %bitcast.22, bf16[512,512]{1,0:T(8,128)(2,1)S(1)} %bitcast.144), kind=kOutput, calls=%fused_computation.100 | convolution fusion | flops 1073741824 | bytes 6815744 | tf_op jit(solution)/shard_map/dot_general | solution.py:497
  75.6 0.2 bitcast_reduce_fusion
  76.0 0.3 copy-done.6
  76.2 0.2 fusion.6
  76.5 0.1 copy-done.7
  76.6 1.0 multiply_reduce_fusion
  77.6 1.7 %convolution_bitcast_fusion = f32[8,1,4096]{2,0,1:T(8,128)S(1)} fusion(bf16[1,256,4096]{2,1,0:T(8,128)(2,1)S(1)} %copy-done, bf16[2048,2,128]{0,2,1:T(8,128)(2,1)S(1)} %bitcast.142, f32[8,2,2048]{2,0,1:T(8,128)} %get-tuple-element.24, f32[8,2]{0,1:T(2,128)S(1)} %get-tuple-element.23, f32[8,2048]{1,0:T(8,128)S(1)} %convert_reduce_fusion), kind=kOutput, calls=%fused_computation.3 | convolution fusion | flops 25266176 | bytes 3473472 | tf_op jit(solution)/shard_map/dot_general | solution.py:520
  79.3 1.6 %collective-permute-start.14 = (f32[8,1,4096]{2,0,1:T(8,128)S(1)}, f32[8,1,4096]{2,0,1:T(8,128)S(1)}, u32[]{:S(2)}, u32[]{:S(2)}) collective-permute-start(f32[8,1,4096]{2,0,1:T(8,128)S(1)} %convolution_bitcast_fusion), channel_id=1, source_target_pairs={{0,1},{1,0},{2,3},{3,2},{4,5},{5,4},{6,7},{7,6},{8,9},{9,8},{10,11... | collective-permute-start | bytes 393224 | tf_op jit(solution)/shard_map/ppermute | solution.py:116
  80.9 3.3 %collective-permute-done.14 = f32[8,1,4096]{2,0,1:T(8,128)S(1)} collective-permute-done((f32[8,1,4096]{2,0,1:T(8,128)S(1)}, f32[8,1,4096]{2,0,1:T(8,128)S(1)}, u32[]{:S(2)}, u32[]{:S(2)}) %collective-permute-start.14) | collective-permute-done | bytes 131104 | tf_op jit(solution)/shard_map/ppermute | solution.py:116
  84.3 2.1 %collective-permute-start.15 = (f32[8,1,4096]{2,0,1:T(8,128)S(1)}, f32[8,1,4096]{2,0,1:T(8,128)S(1)}, u32[]{:S(2)}, u32[]{:S(2)}) collective-permute-start(f32[8,1,4096]{2,0,1:T(8,128)S(1)} %add.216), channel_id=1, source_target_pairs={{0,2},{1,3},{2,0},{3,1},{4,6},{5,7},{6,4},{7,5},{8,10},{9,11},{10,... | collective-permute-start | bytes 393224 | tf_op jit(solution)/shard_map/ppermute | solution.py:116
  86.3 3.4 %collective-permute-done.15 = f32[8,1,4096]{2,0,1:T(8,128)S(1)} collective-permute-done((f32[8,1,4096]{2,0,1:T(8,128)S(1)}, f32[8,1,4096]{2,0,1:T(8,128)S(1)}, u32[]{:S(2)}, u32[]{:S(2)}) %collective-permute-start.15) | collective-permute-done | bytes 131104 | tf_op jit(solution)/shard_map/ppermute | solution.py:116
  89.8 2.5 %collective-permute-start.16 = (f32[8,1,4096]{2,0,1:T(8,128)S(1)}, f32[8,1,4096]{2,0,1:T(8,128)S(1)}, u32[]{:S(2)}, u32[]{:S(2)}) collective-permute-start(f32[8,1,4096]{2,0,1:T(8,128)S(1)} %add.217), channel_id=1, source_target_pairs={{0,4},{1,5},{2,6},{3,7},{4,0},{5,1},{6,2},{7,3},{8,12},{9,13},{10,... | collective-permute-start | bytes 393224 | tf_op jit(solution)/shard_map/ppermute | solution.py:116
  92.3 4.9 %collective-permute-done.16 = f32[8,1,4096]{2,0,1:T(8,128)S(1)} collective-permute-done((f32[8,1,4096]{2,0,1:T(8,128)S(1)}, f32[8,1,4096]{2,0,1:T(8,128)S(1)}, u32[]{:S(2)}, u32[]{:S(2)}) %collective-permute-start.16) | collective-permute-done | bytes 131104 | tf_op jit(solution)/shard_map/ppermute | solution.py:116
  97.1 0.7 add.218
  97.8 12.3 %shard_map.154 = f32[8,4096]{1,0:T(8,128)} custom-call(bf16[8,4096]{1,0:T(8,128)(2,1)} %bitcast.150, f32[8,4096]{1,0:T(8,128)} %bitcast.148, f32[1,4096]{1,0:T(1,128)} %gain_ref.1, bf16[896,4096]{1,0:T(8,128)(2,1)} %bitcast.136, bf16[896,4096]{1,0:T(8,128)(2,1)} %bitcast.137, bf16[896,4096]{1,0:T(8,128)(2,1)} %bitcast.138, bf16[896,4096]{1,0:T(8,128)(2,1)} %bitcast.139, ...), custom_call_target="tpu_custom_call" | custom-call | tf_op jit(solution)/shard_map/pallas_call | solution.py:407
  110.1 1.0 reshape_reshape.4
  111.3 4.2 %collective-permute-done.17 = f32[2,2,1,1,4096]{4,2,1,0,3:T(1,128)S(1)} collective-permute-done((f32[2,2,1,1,4096]{4,2,1,0,3:T(1,128)S(1)}, f32[2,2,1,1,4096]{4,2,1,0,3:T(1,128)S(1)}, u32[]{:S(2)}, u32[]{:S(2)}) %collective-permute-start.17) | collective-permute-done | bytes 65568 | tf_op jit(solution)/shard_map/ppermute | solution.py:546
  115.6 0.3 collective-permute-start.18
  116.0 3.7 %collective-permute-done.18 = f32[2,1,1,1,4096]{4,2,1,0,3:T(1,128)S(1)} collective-permute-done((f32[2,1,1,1,4096]{4,2,1,0,3:T(1,128)S(1)}, f32[2,1,1,1,4096]{4,2,1,0,3:T(1,128)S(1)}, u32[]{:S(2)}, u32[]{:S(2)}) %collective-permute-start.18) | collective-permute-done | bytes 32800 | tf_op jit(solution)/shard_map/ppermute | solution.py:546
  119.7 0.9 fusion.33
  120.7 2.2 %collective-permute-start.19 = (f32[1,4096]{1,0:T(1,128)S(1)}, f32[1,4096]{1,0:T(1,128)S(1)}, u32[]{:S(2)}, u32[]{:S(2)}) collective-permute-start(f32[1,4096]{1,0:T(1,128)S(1)} %fusion.33), channel_id=1, source_target_pairs={{0,8},{1,9},{2,10},{3,11},{4,12},{5,13},{6,14},{7,15},{8,16},{9,17... | collective-permute-start | bytes 49160 | tf_op jit(solution)/shard_map/ppermute | solution.py:562
  122.9 2.0 %collective-permute-done.20 = f32[1,4096]{1,0:T(1,128)S(1)} collective-permute-done((f32[1,4096]{1,0:T(1,128)S(1)}, f32[1,4096]{1,0:T(1,128)S(1)}, u32[]{:S(2)}, u32[]{:S(2)}) %collective-permute-start.20) | collective-permute-done | bytes 16416 | tf_op jit(solution)/shard_map/ppermute | solution.py:563
  124.8 0.6 convert_bitcast_fusion
  (58 shorter events, 1.0 us)
Async XLA Ops:
  0.0 77.6 %copy-start = (bf16[1,256,4096]{2,1,0:T(8,128)(2,1)S(1)}, bf16[1,256,4096]{2,1,0:T(8,128)(2,1)}, u32[]{:S(2)}) copy-start(bf16[1,256,4096]{2,1,0:T(8,128)(2,1)} %param.25) | copy-start | bytes 6291460
  0.9 10.2 %copy-start.3 = (bf16[8,512]{1,0:T(8,128)(2,1)}, bf16[8,512]{1,0:T(8,128)(2,1)S(1)}, u32[]{:S(2)}) copy-start(bf16[8,512]{1,0:T(8,128)(2,1)S(1)} %reshape_squeeze.9) | copy-start | bytes 24580
  2.5 13.2 %collective-permute-start = (bf16[136,512]{1,0:T(8,128)(2,1)}, bf16[136,512]{1,0:T(8,128)(2,1)S(1)}, u32[]{:S(2)}, u32[]{:S(2)}) collective-permute-start(bf16[136,512]{1,0:T(8,128)(2,1)} %pad_maximum_fusion), channel_id=1, source_target_pairs={{0,2},{2,4},{4,6},{6,7},{7,5},{5,3},{3,1},{1,0},{8,10},{10,12},{12... | collective-permute-start | bytes 417800 | tf_op jit(solution)/shard_map/ppermute | solution.py:163
  5.5 12.2 %collective-permute-start.4 = (bf16[136,512]{1,0:T(8,128)(2,1)}, bf16[136,512]{1,0:T(8,128)(2,1)S(1)}, u32[]{:S(2)}, u32[]{:S(2)}) collective-permute-start(bf16[136,512]{1,0:T(8,128)(2,1)} %pad_maximum_fusion), channel_id=1, source_target_pairs={{0,1},{2,0},{4,2},{6,4},{7,6},{5,7},{3,5},{1,3},{8,9},{10,8},{12,1... | collective-permute-start | bytes 417800 | tf_op jit(solution)/shard_map/ppermute | solution.py:167
  11.5 3.5 %copy-start.2 = (bf16[1,128,512]{2,1,0:T(8,128)(2,1)S(1)}, bf16[1,128,512]{2,1,0:T(8,128)(2,1)}, u32[]{:S(2)}) copy-start(bf16[1,128,512]{2,1,0:T(8,128)(2,1)} %param.23) | copy-start | bytes 393220
  15.7 5.2 %collective-permute-start.1 = (bf16[136,512]{1,0:T(8,128)(2,1)S(1)}, bf16[136,512]{1,0:T(8,128)(2,1)S(1)}, u32[]{:S(2)}, u32[]{:S(2)}) collective-permute-start(bf16[136,512]{1,0:T(8,128)(2,1)S(1)} %collective-permute-done), channel_id=1, source_target_pairs={{0,2},{2,4},{4,6},{6,7},{7,5},{5,3},{3,1},{1,0},{8,10},{10,12},{12... | collective-permute-start | bytes 417800 | tf_op jit(solution)/shard_map/ppermute | solution.py:163
  17.8 5.1 %collective-permute-start.5 = (bf16[136,512]{1,0:T(8,128)(2,1)S(1)}, bf16[136,512]{1,0:T(8,128)(2,1)S(1)}, u32[]{:S(2)}, u32[]{:S(2)}) collective-permute-start(bf16[136,512]{1,0:T(8,128)(2,1)S(1)} %collective-permute-done.4), channel_id=1, source_target_pairs={{0,1},{2,0},{4,2},{6,4},{7,6},{5,7},{3,5},{1,3},{8,9},{10,8},{12,1... | collective-permute-start | bytes 417800 | tf_op jit(solution)/shard_map/ppermute | solution.py:167
  20.9 5.1 %collective-permute-start.2 = (bf16[136,512]{1,0:T(8,128)(2,1)S(1)}, bf16[136,512]{1,0:T(8,128)(2,1)S(1)}, u32[]{:S(2)}, u32[]{:S(2)}) collective-permute-start(bf16[136,512]{1,0:T(8,128)(2,1)S(1)} %collective-permute-done.1), channel_id=1, source_target_pairs={{0,2},{2,4},{4,6},{6,7},{7,5},{5,3},{3,1},{1,0},{8,10},{10,12},{12... | collective-permute-start | bytes 417800 | tf_op jit(solution)/shard_map/ppermute | solution.py:163
  22.9 8.5 %collective-permute-start.6 = (bf16[136,512]{1,0:T(8,128)(2,1)S(1)}, bf16[136,512]{1,0:T(8,128)(2,1)S(1)}, u32[]{:S(2)}, u32[]{:S(2)}) collective-permute-start(bf16[136,512]{1,0:T(8,128)(2,1)S(1)} %collective-permute-done.5), channel_id=1, source_target_pairs={{0,1},{2,0},{4,2},{6,4},{7,6},{5,7},{3,5},{1,3},{8,9},{10,8},{12,1... | collective-permute-start | bytes 417800 | tf_op jit(solution)/shard_map/ppermute | solution.py:167
  26.0 5.3 %collective-permute-start.3 = (bf16[136,512]{1,0:T(8,128)(2,1)S(1)}, bf16[136,512]{1,0:T(8,128)(2,1)S(1)}, u32[]{:S(2)}, u32[]{:S(2)}) collective-permute-start(bf16[136,512]{1,0:T(8,128)(2,1)S(1)} %collective-permute-done.2), channel_id=1, source_target_pairs={{0,2},{2,4},{4,6},{6,7},{7,5},{5,3},{3,1},{1,0},{8,10},{10,12},{12... | collective-permute-start | bytes 417800 | tf_op jit(solution)/shard_map/ppermute | solution.py:163
  32.7 15.0 %copy-start.8 = (s32[8]{0:T(128)S(1)}, s32[8]{0:T(128)}, u32[]{:S(2)}) copy-start(s32[8]{0:T(128)} %param.19) | copy-start | bytes 100
  32.7 24.6 %copy-start.4 = (s32[1,2,8,128]{3,1,2,0:T(2,128)S(1)}, s32[1,2,8,128]{3,1,2,0:T(2,128)}, u32[]{:S(2)}) copy-start(s32[1,2,8,128]{3,1,2,0:T(2,128)} %copy.36) | copy-start | bytes 24580
  32.8 24.6 %copy-start.5 = (s32[8,256]{1,0:T(8,128)S(1)}, s32[8,256]{1,0:T(8,128)}, u32[]{:S(2)}) copy-start(s32[8,256]{1,0:T(8,128)} %param.18) | copy-start | bytes 24580
  32.8 11.4 %collective-permute-start.7 = (bf16[256,512]{1,0:T(8,128)(2,1)}, bf16[256,512]{1,0:T(8,128)(2,1)S(1)}, u32[]{:S(2)}, u32[]{:S(2)}) collective-permute-start(bf16[256,512]{1,0:T(8,128)(2,1)} %get-tuple-element.20), channel_id=1, source_target_pairs={{0,2},{2,4},{4,6},{6,7},{7,5},{5,3},{3,1},{1,0},{8,10},{10,12},{12... | collective-permute-start | bytes 786440 | tf_op jit(solution)/shard_map/ppermute | solution.py:163
  34.9 9.3 %collective-permute-start.8 = (bf16[256,512]{1,0:T(8,128)(2,1)}, bf16[256,512]{1,0:T(8,128)(2,1)S(1)}, u32[]{:S(2)}, u32[]{:S(2)}) collective-permute-start(bf16[256,512]{1,0:T(8,128)(2,1)} %get-tuple-element.20), channel_id=1, source_target_pairs={{0,1},{2,0},{4,2},{6,4},{7,6},{5,7},{3,5},{1,3},{8,9},{10,8},{12,1... | collective-permute-start | bytes 786440 | tf_op jit(solution)/shard_map/ppermute | solution.py:167
  34.9 37.8 %all-to-all-start = ((bf16[8,64,512]{2,1,0:T(8,128)(2,1)}), bf16[8,64,512]{2,1,0:T(8,128)(2,1)S(1)}, u32[]{:S(2)}, u32[]{:S(2)}) async-start(bf16[8,64,512]{2,1,0:T(8,128)(2,1)} %reshape.261), calls=%async_computation | async-start | bytes 1048576 | tf_op jit(solution)/shard_map/all_to_all | solution.py:470
  41.8 28.1 %copy-start.1 = (bf16[1,8,8,512]{3,1,2,0:T(8,128)(2,1)}, bf16[1,8,8,512]{3,1,2,0:T(8,128)(2,1)S(1)}, u32[]{:S(2)}) copy-start(bf16[1,8,8,512]{3,1,2,0:T(8,128)(2,1)S(1)} %copy.35) | copy-start | bytes 196612
  44.2 8.9 %collective-permute-start.9 = (bf16[256,512]{1,0:T(8,128)(2,1)S(1)}, bf16[256,512]{1,0:T(8,128)(2,1)S(1)}, u32[]{:S(2)}, u32[]{:S(2)}) collective-permute-start(bf16[256,512]{1,0:T(8,128)(2,1)S(1)} %collective-permute-done.7), channel_id=1, source_target_pairs={{0,2},{2,4},{4,6},{6,7},{7,5},{5,3},{3,1},{1,0},{8,10},{10,12},{12... | collective-permute-start | bytes 786440 | tf_op jit(solution)/shard_map/ppermute | solution.py:163
  47.8 17.4 %collective-permute-start.12 = (bf16[256,512]{1,0:T(8,128)(2,1)S(1)}, bf16[256,512]{1,0:T(8,128)(2,1)S(1)}, u32[]{:S(2)}, u32[]{:S(2)}) collective-permute-start(bf16[256,512]{1,0:T(8,128)(2,1)S(1)} %collective-permute-done.8), channel_id=1, source_target_pairs={{0,1},{2,0},{4,2},{6,4},{7,6},{5,7},{3,5},{1,3},{8,9},{10,8},{12,1... | collective-permute-start | bytes 786440 | tf_op jit(solution)/shard_map/ppermute | solution.py:167
  53.1 8.2 %collective-permute-start.10 = (bf16[256,512]{1,0:T(8,128)(2,1)S(1)}, bf16[256,512]{1,0:T(8,128)(2,1)S(1)}, u32[]{:S(2)}, u32[]{:S(2)}) collective-permute-start(bf16[256,512]{1,0:T(8,128)(2,1)S(1)} %collective-permute-done.9), channel_id=1, source_target_pairs={{0,2},{2,4},{4,6},{6,7},{7,5},{5,3},{3,1},{1,0},{8,10},{10,12},{12... | collective-permute-start | bytes 786440 | tf_op jit(solution)/shard_map/ppermute | solution.py:163
  61.3 7.9 %collective-permute-start.11 = (bf16[256,512]{1,0:T(8,128)(2,1)S(1)}, bf16[256,512]{1,0:T(8,128)(2,1)S(1)}, u32[]{:S(2)}, u32[]{:S(2)}) collective-permute-start(bf16[256,512]{1,0:T(8,128)(2,1)S(1)} %collective-permute-done.10), channel_id=1, source_target_pairs={{0,2},{2,4},{4,6},{6,7},{7,5},{5,3},{3,1},{1,0},{8,10},{10,12},{12... | collective-permute-start | bytes 786440 | tf_op jit(solution)/shard_map/ppermute | solution.py:163
  65.1 6.8 %collective-permute-start.13 = (bf16[256,512]{1,0:T(8,128)(2,1)S(1)}, bf16[256,512]{1,0:T(8,128)(2,1)S(1)}, u32[]{:S(2)}, u32[]{:S(2)}) collective-permute-start(bf16[256,512]{1,0:T(8,128)(2,1)S(1)} %collective-permute-done.12), channel_id=1, source_target_pairs={{0,1},{2,0},{4,2},{6,4},{7,6},{5,7},{3,5},{1,3},{8,9},{10,8},{12,1... | collective-permute-start | bytes 786440 | tf_op jit(solution)/shard_map/ppermute | solution.py:167
  75.6 0.6 copy-start.6
  76.0 0.7 copy-start.7
  79.3 5.0 %collective-permute-start.14 = (f32[8,1,4096]{2,0,1:T(8,128)S(1)}, f32[8,1,4096]{2,0,1:T(8,128)S(1)}, u32[]{:S(2)}, u32[]{:S(2)}) collective-permute-start(f32[8,1,4096]{2,0,1:T(8,128)S(1)} %convolution_bitcast_fusion), channel_id=1, source_target_pairs={{0,1},{1,0},{2,3},{3,2},{4,5},{5,4},{6,7},{7,6},{8,9},{9,8},{10,11... | collective-permute-start | bytes 393224 | tf_op jit(solution)/shard_map/ppermute | solution.py:116
  84.3 5.5 %collective-permute-start.15 = (f32[8,1,4096]{2,0,1:T(8,128)S(1)}, f32[8,1,4096]{2,0,1:T(8,128)S(1)}, u32[]{:S(2)}, u32[]{:S(2)}) collective-permute-start(f32[8,1,4096]{2,0,1:T(8,128)S(1)} %add.216), channel_id=1, source_target_pairs={{0,2},{1,3},{2,0},{3,1},{4,6},{5,7},{6,4},{7,5},{8,10},{9,11},{10,... | collective-permute-start | bytes 393224 | tf_op jit(solution)/shard_map/ppermute | solution.py:116
  89.8 7.3 %collective-permute-start.16 = (f32[8,1,4096]{2,0,1:T(8,128)S(1)}, f32[8,1,4096]{2,0,1:T(8,128)S(1)}, u32[]{:S(2)}, u32[]{:S(2)}) collective-permute-start(f32[8,1,4096]{2,0,1:T(8,128)S(1)} %add.217), channel_id=1, source_target_pairs={{0,4},{1,5},{2,6},{3,7},{4,0},{5,1},{6,2},{7,3},{8,12},{9,13},{10,... | collective-permute-start | bytes 393224 | tf_op jit(solution)/shard_map/ppermute | solution.py:116
  111.2 4.3 %collective-permute-start.17 = (f32[2,2,1,1,4096]{4,2,1,0,3:T(1,128)S(1)}, f32[2,2,1,1,4096]{4,2,1,0,3:T(1,128)S(1)}, u32[]{:S(2)}, u32[]{:S(2)}) collective-permute-start(f32[2,2,1,1,4096]{4,2,1,0,3:T(1,128)S(1)} %constant_dynamic-slice_fusion.1), channel_id=1, source_target_pairs={{0,1},{1,0},{2,3},{3,2},{4,5},{5,4},{6,7},{7,6},{8,9},{9,8},{10,11... | collective-permute-start | bytes 196616 | tf_op jit(solution)/shard_map/ppermute | solution.py:546
  115.6 4.0 %collective-permute-start.18 = (f32[2,1,1,1,4096]{4,2,1,0,3:T(1,128)S(1)}, f32[2,1,1,1,4096]{4,2,1,0,3:T(1,128)S(1)}, u32[]{:S(2)}, u32[]{:S(2)}) collective-permute-start(f32[2,1,1,1,4096]{4,2,1,0,3:T(1,128)S(1)} %constant_dynamic-slice_fusion), channel_id=1, source_target_pairs={{0,2},{1,3},{2,0},{3,1},{4,6},{5,7},{6,4},{7,5},{8,10},{9,11},{10,... | collective-permute-start | bytes 98312 | tf_op jit(solution)/shard_map/ppermute | solution.py:546
  119.7 5.2 %collective-permute-start.20 = (f32[1,4096]{1,0:T(1,128)S(1)}, f32[1,4096]{1,0:T(1,128)S(1)}, u32[]{:S(2)}, u32[]{:S(2)}) collective-permute-start(f32[1,4096]{1,0:T(1,128)S(1)} %dynamic-slice_bitcast_fusion), channel_id=1, source_target_pairs={{0,12},{1,13},{2,14},{3,15},{4,8},{5,9},{6,10},{7,11},{8,20},{9,21... | collective-permute-start | bytes 49160 | tf_op jit(solution)/shard_map/ppermute | solution.py:563
  120.7 4.2 %collective-permute-start.19 = (f32[1,4096]{1,0:T(1,128)S(1)}, f32[1,4096]{1,0:T(1,128)S(1)}, u32[]{:S(2)}, u32[]{:S(2)}) collective-permute-start(f32[1,4096]{1,0:T(1,128)S(1)} %fusion.33), channel_id=1, source_target_pairs={{0,8},{1,9},{2,10},{3,11},{4,12},{5,13},{6,14},{7,15},{8,16},{9,17... | collective-permute-start | bytes 49160 | tf_op jit(solution)/shard_map/ppermute | solution.py:562

commit v17 on v16

--- a/solution.py
+++ b/solution.py
@@ -493,11 +493,25 @@
     ring_hidden = RingGather(tile_hidden, group_size, my_index)
     site_tiles, site_count = ring_hidden.step((site_tiles, site_count))
     hidden_slots, hidden_sources = ring_hidden.finish()
-    table_hidden = hidden_slots.reshape(group_size * tiles_here, hidden_width)
-    keyval = jnp.dot(table_hidden, weight_out, preferred_element_type=jnp.float32)
-    normed_keys = head_norm(keyval[:, :my_cols], k_gain[0])
-    table = jnp.concatenate([normed_keys, keyval[:, my_cols:]], axis=1).astype(jnp.bfloat16)
-    table = table.reshape(group_size * tiles_here, 2, heads_here, head_size)
+    if ring_hidden.direct and ring_hidden.forward_slots:
+        last = len(ring_hidden.forward_slots)
+        early = [ring_hidden.value] + ring_hidden.forward_slots[:-1] + ring_hidden.backward_slots
+        parts = [jnp.stack(early), ring_hidden.forward_slots[-1][None]]
+        order = [i for i in range(group_size) if i != last] + [last]
+        hidden_sources = jnp.stack([hidden_sources[i] for i in order])
+    else:
+        parts = [hidden_slots]
+    tables = []
+    for part in parts:
+        keyval = jnp.dot(
+            part.reshape(-1, hidden_width), weight_out, preferred_element_type=jnp.float32
+        )
+        normed_keys = head_norm(keyval[:, :my_cols], k_gain[0])
+        tables.append(
+            jnp.concatenate([normed_keys, keyval[:, my_cols:]], axis=1)
+            .astype(jnp.bfloat16)
+            .reshape(-1, 2, heads_here, head_size)
+        )
 
     tile_of_row = (
         hidden_sources[:, None] * tiles_here + jnp.arange(tiles_here, dtype=jnp.int32)[None, :]
@@ -508,14 +522,27 @@
         site_tiles[:, :, None] == tile_of_row[None, None, :], live[:, :, None]
     )
     uses = jnp.sum(named.astype(jnp.float32), axis=1)
-    scores = jnp.einsum(
-        "nhd,rhd->nhr", query_heads, table[:, 0], preferred_element_type=jnp.float32
+    scores = jnp.concatenate(
+        [
+            jnp.einsum("nhd,rhd->nhr", query_heads, table[:, 0], preferred_element_type=jnp.float32)
+            for table in tables
+        ],
+        axis=-1,
     ) / math.sqrt(head_size)
     exponents = jnp.exp(scores) * uses[:, None, :]
     weights = (exponents / jnp.sum(exponents, axis=-1, keepdims=True)).astype(jnp.bfloat16)
-    combined = jnp.einsum(
-        "nhr,rhd->nhd", weights, table[:, 1], preferred_element_type=jnp.float32
-    )
+    combined = None
+    start = 0
+    for table in tables:
+        rows_here = table.shape[0]
+        term = jnp.einsum(
+            "nhr,rhd->nhd",
+            weights[:, :, start : start + rows_here],
+            table[:, 1],
+            preferred_element_type=jnp.float32,
+        )
+        combined = term if combined is None else combined + term
+        start += rows_here
     combined = combined.reshape(all_sites, my_cols).astype(jnp.bfloat16)
     attn_part = jnp.dot(combined, out_weight[0], preferred_element_type=jnp.float32)
     attn_all = doubling_sum(attn_part.reshape(group_size, sites_here, -1), group_size)

time: 126 us -> 135 us (1.071)
  other arithmetic: 10.6 us -> 17.4 us
  local copies, waits for them, and re-layouts: 15.5 us -> 20.4 us
  starting transfers between devices: 38.1 us -> 35.3 us
  waiting for transfers between devices: 39.4 us -> 37.1 us
  matrix products: 9.25 us -> 11.2 us
    ppermute x8, waiting for transfers between devices: 17.2 us -> 13 us  [_issue(): self.ahead = lax.ppermute(self.ahead, 'site', self.forward)]
    ppermute x3, waiting for transfers between devices: 11.6 us -> 13.7 us  [doubling_sum(): state = state + lax.ppermute(state, 'site', xor_pairs(count, bit))]
    unnamed x34 -> x43, local copies, waits for them, and re-layouts: 7.84 us -> 9.88 us
    reduce_sum x1 -> x2, other arithmetic: 0.19 us -> 2.11 us  [head_norm(): jnp.mean(shaped * shaped, axis=-1, keepdims=True) + epsilon]
    mul x0 -> x1, local copies, waits for them, and re-layouts: none -> 1.83 us  [head_norm(): shaped * shaped]
    dot_general x1 -> x3, matrix products: 2.9 us -> 4.25 us  [the longest x2 3.92 us: heads_split(): jnp.dot(part.reshape(-1, hidden_width), weight_out, preferred_element_typ...]
    mul x2 -> x3, local copies, waits for them, and re-layouts: 2.43 us -> 2.82 us  [head_norm(): shaped * lax.rsqrt(jnp.mean(shaped * shaped, axis=-1, keepdims=True) + ep...]
  transfers between devices with their start and end apart: 22 -> 22, of which waited for: 12 -> 11; matrix products, arithmetic and copies ran while one was open for 18% -> 21% of each run, Pallas kernels for 0% -> 0%
where the time goes in v17:
time: 135 us; the launch traced here: 134 us
  waiting for transfers between devices  37.1 us (27%)
  starting transfers between devices  35.3 us (26%)
  local copies, waits for them, and re-layouts  20.4 us (15%)
  other arithmetic  17.4 us (13%)
  Pallas kernels  12.4 us (9%)
  matrix products  11.2 us (8%)
    ppermute x8, starting transfers between devices, _issue(): self.ahead = lax.ppermute(self.ahead, 'site', self.forward)  22 us
    ppermute x3, waiting for transfers between devices, doubling_sum(): state = state + lax.ppermute(state, 'site', xor_pairs(count, bit))  13.7 us
    ppermute x8, waiting for transfers between devices, _issue(): self.ahead = lax.ppermute(self.ahead, 'site', self.forward)  13 us
    pallas_call x1, Pallas kernels, gated_ffn(): pl.pallas_call(ffn_block, grid=(units // block,), in_specs=[whole, whole,...  12.4 us
    unnamed x43, local copies, waits for them, and re-layouts  9.88 us
    ppermute x2, waiting for transfers between devices, last_round(): state = keep + lax.ppermute(send, 'site', xor_pairs(group_size, bit))  7.89 us
    all_to_all x1, starting transfers between devices, heads_split(): lax.all_to_all(col_blocks, 'site', split_axis=0, concat_axis=0, tiled=True)  6.25 us
    ppermute x3, starting transfers between devices, doubling_sum(): state = state + lax.ppermute(state, 'site', xor_pairs(count, bit))  5.08 us
  transfers between devices with their start and end apart: 22, of which 11 were waited for; matrix products, arithmetic and copies ran while one was open for 21% of the time, Pallas kernels for 0%

profile of v17, /device:TPU:0, one launch (start us, length us, event | category | flops | bytes accessed | tf_op | source)
XLA Modules:
  0.0 134.1 jit_solution(8226956521777649964)
XLA Ops:
  0.0 0.9 reduce
  1.0 1.6 %pad_maximum_fusion = bf16[136,512]{1,0:T(8,128)(2,1)} fusion(bf16[8,512]{1,0:T(8,128)(2,1)S(1)} %reshape_squeeze.9, bf16[128,512]{1,0:T(8,128)(2,1)} %bitcast.183), kind=kLoop, calls=%fused_computation.45 | loop fusion | flops 278528 | bytes 278528 | tf_op jit(solution)/shard_map/concatenate | solution.py:459
  2.5 3.0 %collective-permute-start = (bf16[136,512]{1,0:T(8,128)(2,1)}, bf16[136,512]{1,0:T(8,128)(2,1)S(1)}, u32[]{:S(2)}, u32[]{:S(2)}) collective-permute-start(bf16[136,512]{1,0:T(8,128)(2,1)} %pad_maximum_fusion), channel_id=1, source_target_pairs={{0,2},{2,4},{4,6},{6,7},{7,5},{5,3},{3,1},{1,0},{8,10},{10,12},{12... | collective-permute-start | bytes 417800 | tf_op jit(solution)/shard_map/ppermute | solution.py:163
  5.6 0.7 compare_select_fusion
  6.9 1.2 broadcast_bitcast_fusion
  8.1 1.2 broadcast_bitcast_fusion.1
  9.4 0.6 add_multiply_fusion
  10.1 0.6 pad_clamp_fusion
  11.3 1.2 copy.49
  12.8 1.1 copy.61
  14.4 1.1 reshape.302
  15.5 0.8 gather_fusion.1
  16.3 0.7 bitcast_dynamic-update-slice_fusion.14
  17.0 2.1 %collective-permute-start.1 = (bf16[136,512]{1,0:T(8,128)(2,1)S(1)}, bf16[136,512]{1,0:T(8,128)(2,1)S(1)}, u32[]{:S(2)}, u32[]{:S(2)}) collective-permute-start(bf16[136,512]{1,0:T(8,128)(2,1)S(1)} %collective-permute-done), channel_id=1, source_target_pairs={{0,2},{2,4},{4,6},{6,7},{7,5},{5,3},{3,1},{1,0},{8,10},{10,12},{12... | collective-permute-start | bytes 417800 | tf_op jit(solution)/shard_map/ppermute | solution.py:163
  19.1 3.1 %collective-permute-done.1 = bf16[136,512]{1,0:T(8,128)(2,1)S(1)} collective-permute-done((bf16[136,512]{1,0:T(8,128)(2,1)S(1)}, bf16[136,512]{1,0:T(8,128)(2,1)S(1)}, u32[]{:S(2)}, u32[]{:S(2)}) %collective-permute-start.1) | collective-permute-done | bytes 139296 | tf_op jit(solution)/shard_map/ppermute | solution.py:163
  22.2 1.9 %collective-permute-start.2 = (bf16[136,512]{1,0:T(8,128)(2,1)S(1)}, bf16[136,512]{1,0:T(8,128)(2,1)S(1)}, u32[]{:S(2)}, u32[]{:S(2)}) collective-permute-start(bf16[136,512]{1,0:T(8,128)(2,1)S(1)} %collective-permute-done.1), channel_id=1, source_target_pairs={{0,2},{2,4},{4,6},{6,7},{7,5},{5,3},{3,1},{1,0},{8,10},{10,12},{12... | collective-permute-start | bytes 417800 | tf_op jit(solution)/shard_map/ppermute | solution.py:163
  24.3 3.0 %collective-permute-done.2 = bf16[136,512]{1,0:T(8,128)(2,1)S(1)} collective-permute-done((bf16[136,512]{1,0:T(8,128)(2,1)S(1)}, bf16[136,512]{1,0:T(8,128)(2,1)S(1)}, u32[]{:S(2)}, u32[]{:S(2)}) %collective-permute-start.2) | collective-permute-done | bytes 139296 | tf_op jit(solution)/shard_map/ppermute | solution.py:163
  27.3 2.4 %collective-permute-start.3 = (bf16[136,512]{1,0:T(8,128)(2,1)S(1)}, bf16[136,512]{1,0:T(8,128)(2,1)S(1)}, u32[]{:S(2)}, u32[]{:S(2)}) collective-permute-start(bf16[136,512]{1,0:T(8,128)(2,1)S(1)} %collective-permute-done.2), channel_id=1, source_target_pairs={{0,2},{2,4},{4,6},{6,7},{7,5},{5,3},{3,1},{1,0},{8,10},{10,12},{12... | collective-permute-start | bytes 417800 | tf_op jit(solution)/shard_map/ppermute | solution.py:163
  29.7 2.9 %collective-permute-done.3 = bf16[136,512]{1,0:T(8,128)(2,1)S(1)} collective-permute-done((bf16[136,512]{1,0:T(8,128)(2,1)S(1)}, bf16[136,512]{1,0:T(8,128)(2,1)S(1)}, u32[]{:S(2)}, u32[]{:S(2)}) %collective-permute-start.3) | collective-permute-done | bytes 139296 | tf_op jit(solution)/shard_map/ppermute | solution.py:163
  32.7 1.3 bitcast_dynamic-update-slice_fusion.6
  34.0 2.1 %collective-permute-start.7 = (bf16[256,512]{1,0:T(8,128)(2,1)}, bf16[256,512]{1,0:T(8,128)(2,1)S(1)}, u32[]{:S(2)}, u32[]{:S(2)}) collective-permute-start(bf16[256,512]{1,0:T(8,128)(2,1)} %get-tuple-element.20), channel_id=1, source_target_pairs={{0,2},{2,4},{4,6},{6,7},{7,5},{5,3},{3,1},{1,0},{8,10},{10,12},{12... | collective-permute-start | bytes 786440 | tf_op jit(solution)/shard_map/ppermute | solution.py:163
  36.2 6.3 %all-to-all-start = ((bf16[8,64,512]{2,1,0:T(8,128)(2,1)}), bf16[8,64,512]{2,1,0:T(8,128)(2,1)S(1)}, u32[]{:S(2)}, u32[]{:S(2)}) async-start(bf16[8,64,512]{2,1,0:T(8,128)(2,1)} %reshape.302), calls=%async_computation | async-start | bytes 1048576 | tf_op jit(solution)/shard_map/all_to_all | solution.py:470
  42.4 0.7 gather_fusion
  43.1 2.3 %bitcast_reduce_fusion.1 = (f32[8,2]{0,1:T(2,128)S(1)}, f32[8,256]{1,0:T(8,128)S(1)}) fusion(bf16[8,4096]{1,0:T(8,128)(2,1)S(1)} %bitcast.179, bf16[1,256,4096]{2,1,0:T(8,128)(2,1)} %param.20), kind=kOutput, calls=%fused_computation.80 | convolution fusion | flops 16785392 | bytes 2170944 | tf_op jit(solution)/shard_map/dot_general | solution.py:23
  45.6 3.5 %collective-permute-start.9 = (bf16[256,512]{1,0:T(8,128)(2,1)S(1)}, bf16[256,512]{1,0:T(8,128)(2,1)S(1)}, u32[]{:S(2)}, u32[]{:S(2)}) collective-permute-start(bf16[256,512]{1,0:T(8,128)(2,1)S(1)} %collective-permute-done.7), channel_id=1, source_target_pairs={{0,2},{2,4},{4,6},{6,7},{7,5},{5,3},{3,1},{1,0},{8,10},{10,12},{12... | collective-permute-start | bytes 786440 | tf_op jit(solution)/shard_map/ppermute | solution.py:163
  49.1 3.8 %convert_reduce_fusion = f32[8,2048]{1,0:T(8,128)} fusion(s32[2048]{0:T(1024)S(1)} %bitcast.185, s32[8,256]{1,0:T(8,128)S(1)} %copy-done.10, pred[8,256]{1,0:T(8,128)(4,1)S(1)} %iota_compare_fusion), kind=kLoop, calls=%fused_computation.2 | loop fusion | flops 16760832 | bytes 83968 | tf_op jit(solution)/shard_map/reduce_sum | solution.py:524
  52.9 1.4 %collective-permute-done.9 = bf16[256,512]{1,0:T(8,128)(2,1)S(1)} collective-permute-done((bf16[256,512]{1,0:T(8,128)(2,1)S(1)}, bf16[256,512]{1,0:T(8,128)(2,1)S(1)}, u32[]{:S(2)}, u32[]{:S(2)}) %collective-permute-start.9) | collective-permute-done | bytes 262176 | tf_op jit(solution)/shard_map/ppermute | solution.py:163
  54.4 4.3 %collective-permute-start.10 = (bf16[256,512]{1,0:T(8,128)(2,1)S(1)}, bf16[256,512]{1,0:T(8,128)(2,1)}, u32[]{:S(2)}, u32[]{:S(2)}) collective-permute-start(bf16[256,512]{1,0:T(8,128)(2,1)S(1)} %collective-permute-done.9), channel_id=1, source_target_pairs={{0,2},{2,4},{4,6},{6,7},{7,5},{5,3},{3,1},{1,0},{8,10},{10,12},{12... | collective-permute-start | bytes 786440 | tf_op jit(solution)/shard_map/ppermute | solution.py:163
  58.7 0.7 bitcast_dynamic-update-slice_fusion.5
  59.4 0.7 bitcast_dynamic-update-slice_fusion.4
  60.1 2.5 %collective-permute-done.10 = bf16[256,512]{1,0:T(8,128)(2,1)} collective-permute-done((bf16[256,512]{1,0:T(8,128)(2,1)S(1)}, bf16[256,512]{1,0:T(8,128)(2,1)}, u32[]{:S(2)}, u32[]{:S(2)}) %collective-permute-start.10) | collective-permute-done | bytes 262176 | tf_op jit(solution)/shard_map/ppermute | solution.py:163
  62.6 1.7 %bitcast_dynamic-update-slice_fusion.3 = bf16[7,256,512]{2,1,0:T(8,128)(2,1)} fusion(bf16[7,256,512]{2,1,0:T(8,128)(2,1)} %bitcast_dynamic-update-slice_fusion.4, bf16[256,512]{1,0:T(8,128)(2,1)} %collective-permute-done.10), kind=kLoop, calls=%fused_computation.40 | loop fusion | bytes 524288
  64.3 0.7 bitcast_dynamic-update-slice_fusion.2
  65.0 2.6 %collective-permute-start.13 = (bf16[256,512]{1,0:T(8,128)(2,1)}, bf16[256,512]{1,0:T(8,128)(2,1)}, u32[]{:S(2)}, u32[]{:S(2)}) collective-permute-start(bf16[256,512]{1,0:T(8,128)(2,1)} %collective-permute-done.10), channel_id=1, source_target_pairs={{0,2},{2,4},{4,6},{6,7},{7,5},{5,3},{3,1},{1,0},{8,10},{10,12},{12... | collective-permute-start | bytes 786440 | tf_op jit(solution)/shard_map/ppermute | solution.py:163
  67.6 0.7 bitcast_dynamic-update-slice_fusion.1
  68.3 0.7 bitcast_dynamic-update-slice_fusion
  69.0 2.7 %fusion.55 = f32[1792,512]{0,1:T(8,128)S(1)} fusion(bf16[1792,512]{1,0:T(8,128)(2,1)} %bitcast.21, bf16[512,512]{1,0:T(8,128)(2,1)S(1)} %bitcast.170), kind=kOutput, calls=%fused_computation.113 | convolution fusion | flops 939524096 | bytes 6029312 | tf_op jit(solution)/shard_map/dot_general | solution.py:506
  73.0 0.9 convolution_bitcast_fusion.1
  74.0 1.2 fusion.56
  75.2 0.8 copy-done.1
  76.0 0.7 slice_multiply_fusion.1
  76.7 1.8 %mul.169 = f32[256,2,128]{2,1,0:T(2,128)} reshape(f32[256,256]{1,0:T(8,128)} %slice_multiply_fusion.1) | data formatting | bytes 524288 | tf_op jit(solution)/shard_map/mul | solution.py:31
  78.6 2.0 %reduce_sum.47 = f32[256,2]{1,0:T(8,128)} reduce(f32[256,2,128]{2,1,0:T(2,128)} %mul.169, f32[]{:T(128)} %constant.137.clone.1), dimensions={2}, to_apply=%region_2.3 | reduce | flops 65024 | bytes 264196 | tf_op jit(solution)/shard_map/reduce_sum | solution.py:31
  80.5 0.9 add_rsqrt_fusion
  81.8 1.1 convolution_bitcast_fusion.3
  82.9 1.0 fusion.39
  83.9 1.0 divide_convert_fusion
  84.9 0.6 copy-done.7
  85.9 1.2 convolution_bitcast_fusion
  87.1 0.7 collective-permute-start.14
  87.7 4.3 %collective-permute-done.14 = f32[8,1,4096]{2,0,1:T(8,128)S(1)} collective-permute-done((f32[8,1,4096]{2,0,1:T(8,128)S(1)}, f32[8,1,4096]{2,0,1:T(8,128)S(1)}, u32[]{:S(2)}, u32[]{:S(2)}) %collective-permute-start.14) | collective-permute-done | bytes 131104 | tf_op jit(solution)/shard_map/ppermute | solution.py:116
  92.1 2.5 %collective-permute-start.15 = (f32[8,1,4096]{2,0,1:T(8,128)S(1)}, f32[8,1,4096]{2,0,1:T(8,128)S(1)}, u32[]{:S(2)}, u32[]{:S(2)}) collective-permute-start(f32[8,1,4096]{2,0,1:T(8,128)S(1)} %add.234), channel_id=1, source_target_pairs={{0,2},{1,3},{2,0},{3,1},{4,6},{5,7},{6,4},{7,5},{8,10},{9,11},{10,... | collective-permute-start | bytes 393224 | tf_op jit(solution)/shard_map/ppermute | solution.py:116
  94.6 3.9 %collective-permute-done.15 = f32[8,1,4096]{2,0,1:T(8,128)S(1)} collective-permute-done((f32[8,1,4096]{2,0,1:T(8,128)S(1)}, f32[8,1,4096]{2,0,1:T(8,128)S(1)}, u32[]{:S(2)}, u32[]{:S(2)}) %collective-permute-start.15) | collective-permute-done | bytes 131104 | tf_op jit(solution)/shard_map/ppermute | solution.py:116
  98.6 1.9 %collective-permute-start.16 = (f32[8,1,4096]{2,0,1:T(8,128)S(1)}, f32[8,1,4096]{2,0,1:T(8,128)S(1)}, u32[]{:S(2)}, u32[]{:S(2)}) collective-permute-start(f32[8,1,4096]{2,0,1:T(8,128)S(1)} %add.235), channel_id=1, source_target_pairs={{0,4},{1,5},{2,6},{3,7},{4,0},{5,1},{6,2},{7,3},{8,12},{9,13},{10,... | collective-permute-start | bytes 393224 | tf_op jit(solution)/shard_map/ppermute | solution.py:116
  100.5 5.5 %collective-permute-done.16 = f32[8,1,4096]{2,0,1:T(8,128)S(1)} collective-permute-done((f32[8,1,4096]{2,0,1:T(8,128)S(1)}, f32[8,1,4096]{2,0,1:T(8,128)S(1)}, u32[]{:S(2)}, u32[]{:S(2)}) %collective-permute-start.16) | collective-permute-done | bytes 131104 | tf_op jit(solution)/shard_map/ppermute | solution.py:116
  105.9 0.7 add.236
  106.6 12.4 %shard_map.154 = f32[8,4096]{1,0:T(8,128)} custom-call(bf16[8,4096]{1,0:T(8,128)(2,1)} %bitcast.180, f32[8,4096]{1,0:T(8,128)} %bitcast.178, f32[1,4096]{1,0:T(1,128)} %gain_ref.1, bf16[896,4096]{1,0:T(8,128)(2,1)} %bitcast.164, bf16[896,4096]{1,0:T(8,128)(2,1)} %bitcast.165, bf16[896,4096]{1,0:T(8,128)(2,1)} %bitcast.166, bf16[896,4096]{1,0:T(8,128)(2,1)} %bitcast.167, ...), custom_call_target="tpu_custom_call" | custom-call | tf_op jit(solution)/shard_map/pallas_call | solution.py:407
  119.0 1.0 reshape_reshape.4
  120.3 4.0 %collective-permute-done.17 = f32[2,2,1,1,4096]{4,2,1,0,3:T(1,128)S(1)} collective-permute-done((f32[2,2,1,1,4096]{4,2,1,0,3:T(1,128)S(1)}, f32[2,2,1,1,4096]{4,2,1,0,3:T(1,128)S(1)}, u32[]{:S(2)}, u32[]{:S(2)}) %collective-permute-start.17) | collective-permute-done | bytes 65568 | tf_op jit(solution)/shard_map/ppermute | solution.py:573
  124.6 3.8 %collective-permute-done.18 = f32[2,1,1,1,4096]{4,2,1,0,3:T(1,128)S(1)} collective-permute-done((f32[2,1,1,1,4096]{4,2,1,0,3:T(1,128)S(1)}, f32[2,1,1,1,4096]{4,2,1,0,3:T(1,128)S(1)}, u32[]{:S(2)}, u32[]{:S(2)}) %collective-permute-start.18) | collective-permute-done | bytes 32800 | tf_op jit(solution)/shard_map/ppermute | solution.py:573
  128.6 0.9 fusion.43
  129.5 1.5 %collective-permute-start.19 = (f32[1,4096]{1,0:T(1,128)S(1)}, f32[1,4096]{1,0:T(1,128)S(1)}, u32[]{:S(2)}, u32[]{:S(2)}) collective-permute-start(f32[1,4096]{1,0:T(1,128)S(1)} %fusion.43), channel_id=1, source_target_pairs={{0,8},{1,9},{2,10},{3,11},{4,12},{5,13},{6,14},{7,15},{8,16},{9,17... | collective-permute-start | bytes 49160 | tf_op jit(solution)/shard_map/ppermute | solution.py:589
  131.0 2.5 %collective-permute-done.20 = f32[1,4096]{1,0:T(1,128)S(1)} collective-permute-done((f32[1,4096]{1,0:T(1,128)S(1)}, f32[1,4096]{1,0:T(1,128)S(1)}, u32[]{:S(2)}, u32[]{:S(2)}) %collective-permute-start.20) | collective-permute-done | bytes 16416 | tf_op jit(solution)/shard_map/ppermute | solution.py:590
  133.5 0.6 convert_bitcast_fusion
  (79 shorter events, 5.1 us)
Async XLA Ops:
  0.0 85.9 %copy-start = (bf16[1,256,4096]{2,1,0:T(8,128)(2,1)S(1)}, bf16[1,256,4096]{2,1,0:T(8,128)(2,1)}, u32[]{:S(2)}) copy-start(bf16[1,256,4096]{2,1,0:T(8,128)(2,1)} %param.25) | copy-start | bytes 6291460
  0.9 11.6 %copy-start.8 = (bf16[8,512]{1,0:T(8,128)(2,1)}, bf16[8,512]{1,0:T(8,128)(2,1)S(1)}, u32[]{:S(2)}) copy-start(bf16[8,512]{1,0:T(8,128)(2,1)S(1)} %reshape_squeeze.9) | copy-start | bytes 24580
  2.5 14.5 %collective-permute-start = (bf16[136,512]{1,0:T(8,128)(2,1)}, bf16[136,512]{1,0:T(8,128)(2,1)S(1)}, u32[]{:S(2)}, u32[]{:S(2)}) collective-permute-start(bf16[136,512]{1,0:T(8,128)(2,1)} %pad_maximum_fusion), channel_id=1, source_target_pairs={{0,2},{2,4},{4,6},{6,7},{7,5},{5,3},{3,1},{1,0},{8,10},{10,12},{12... | collective-permute-start | bytes 417800 | tf_op jit(solution)/shard_map/ppermute | solution.py:163
  5.5 13.6 %collective-permute-start.4 = (bf16[136,512]{1,0:T(8,128)(2,1)}, bf16[136,512]{1,0:T(8,128)(2,1)S(1)}, u32[]{:S(2)}, u32[]{:S(2)}) collective-permute-start(bf16[136,512]{1,0:T(8,128)(2,1)} %pad_maximum_fusion), channel_id=1, source_target_pairs={{0,1},{2,0},{4,2},{6,4},{7,6},{5,7},{3,5},{1,3},{8,9},{10,8},{12,1... | collective-permute-start | bytes 417800 | tf_op jit(solution)/shard_map/ppermute | solution.py:167
  14.0 2.3 %copy-start.6 = (bf16[1,128,512]{2,1,0:T(8,128)(2,1)S(1)}, bf16[1,128,512]{2,1,0:T(8,128)(2,1)}, u32[]{:S(2)}) copy-start(bf16[1,128,512]{2,1,0:T(8,128)(2,1)} %param.23) | copy-start | bytes 393220
  17.0 5.2 %collective-permute-start.1 = (bf16[136,512]{1,0:T(8,128)(2,1)S(1)}, bf16[136,512]{1,0:T(8,128)(2,1)S(1)}, u32[]{:S(2)}, u32[]{:S(2)}) collective-permute-start(bf16[136,512]{1,0:T(8,128)(2,1)S(1)} %collective-permute-done), channel_id=1, source_target_pairs={{0,2},{2,4},{4,6},{6,7},{7,5},{5,3},{3,1},{1,0},{8,10},{10,12},{12... | collective-permute-start | bytes 417800 | tf_op jit(solution)/shard_map/ppermute | solution.py:163
  19.1 5.1 %collective-permute-start.5 = (bf16[136,512]{1,0:T(8,128)(2,1)S(1)}, bf16[136,512]{1,0:T(8,128)(2,1)S(1)}, u32[]{:S(2)}, u32[]{:S(2)}) collective-permute-start(bf16[136,512]{1,0:T(8,128)(2,1)S(1)} %collective-permute-done.4), channel_id=1, source_target_pairs={{0,1},{2,0},{4,2},{6,4},{7,6},{5,7},{3,5},{1,3},{8,9},{10,8},{12,1... | collective-permute-start | bytes 417800 | tf_op jit(solution)/shard_map/ppermute | solution.py:167
  22.2 5.1 %collective-permute-start.2 = (bf16[136,512]{1,0:T(8,128)(2,1)S(1)}, bf16[136,512]{1,0:T(8,128)(2,1)S(1)}, u32[]{:S(2)}, u32[]{:S(2)}) collective-permute-start(bf16[136,512]{1,0:T(8,128)(2,1)S(1)} %collective-permute-done.1), channel_id=1, source_target_pairs={{0,2},{2,4},{4,6},{6,7},{7,5},{5,3},{3,1},{1,0},{8,10},{10,12},{12... | collective-permute-start | bytes 417800 | tf_op jit(solution)/shard_map/ppermute | solution.py:163
  24.2 8.5 %collective-permute-start.6 = (bf16[136,512]{1,0:T(8,128)(2,1)S(1)}, bf16[136,512]{1,0:T(8,128)(2,1)S(1)}, u32[]{:S(2)}, u32[]{:S(2)}) collective-permute-start(bf16[136,512]{1,0:T(8,128)(2,1)S(1)} %collective-permute-done.5), channel_id=1, source_target_pairs={{0,1},{2,0},{4,2},{6,4},{7,6},{5,7},{3,5},{1,3},{8,9},{10,8},{12,1... | collective-permute-start | bytes 417800 | tf_op jit(solution)/shard_map/ppermute | solution.py:167
  27.3 5.3 %collective-permute-start.3 = (bf16[136,512]{1,0:T(8,128)(2,1)S(1)}, bf16[136,512]{1,0:T(8,128)(2,1)S(1)}, u32[]{:S(2)}, u32[]{:S(2)}) collective-permute-start(bf16[136,512]{1,0:T(8,128)(2,1)S(1)} %collective-permute-done.2), channel_id=1, source_target_pairs={{0,2},{2,4},{4,6},{6,7},{7,5},{5,3},{3,1},{1,0},{8,10},{10,12},{12... | collective-permute-start | bytes 417800 | tf_op jit(solution)/shard_map/ppermute | solution.py:163
  34.0 11.5 %copy-start.13 = (s32[8]{0:T(128)S(1)}, s32[8]{0:T(128)}, u32[]{:S(2)}) copy-start(s32[8]{0:T(128)} %param.19) | copy-start | bytes 100
  34.0 15.1 %copy-start.9 = (s32[1,2,8,128]{3,1,2,0:T(2,128)S(1)}, s32[1,2,8,128]{3,1,2,0:T(2,128)}, u32[]{:S(2)}) copy-start(s32[1,2,8,128]{3,1,2,0:T(2,128)} %copy.64) | copy-start | bytes 24580
  34.0 15.1 %copy-start.10 = (s32[8,256]{1,0:T(8,128)S(1)}, s32[8,256]{1,0:T(8,128)}, u32[]{:S(2)}) copy-start(s32[8,256]{1,0:T(8,128)} %param.18) | copy-start | bytes 24580
  34.0 11.5 %collective-permute-start.7 = (bf16[256,512]{1,0:T(8,128)(2,1)}, bf16[256,512]{1,0:T(8,128)(2,1)S(1)}, u32[]{:S(2)}, u32[]{:S(2)}) collective-permute-start(bf16[256,512]{1,0:T(8,128)(2,1)} %get-tuple-element.20), channel_id=1, source_target_pairs={{0,2},{2,4},{4,6},{6,7},{7,5},{5,3},{3,1},{1,0},{8,10},{10,12},{12... | collective-permute-start | bytes 786440 | tf_op jit(solution)/shard_map/ppermute | solution.py:163
  36.2 9.4 %collective-permute-start.8 = (bf16[256,512]{1,0:T(8,128)(2,1)}, bf16[256,512]{1,0:T(8,128)(2,1)S(1)}, u32[]{:S(2)}, u32[]{:S(2)}) collective-permute-start(bf16[256,512]{1,0:T(8,128)(2,1)} %get-tuple-element.20), channel_id=1, source_target_pairs={{0,1},{2,0},{4,2},{6,4},{7,6},{5,7},{3,5},{1,3},{8,9},{10,8},{12,1... | collective-permute-start | bytes 786440 | tf_op jit(solution)/shard_map/ppermute | solution.py:167
  36.2 32.8 %all-to-all-start = ((bf16[8,64,512]{2,1,0:T(8,128)(2,1)}), bf16[8,64,512]{2,1,0:T(8,128)(2,1)S(1)}, u32[]{:S(2)}, u32[]{:S(2)}) async-start(bf16[8,64,512]{2,1,0:T(8,128)(2,1)} %reshape.302), calls=%async_computation | async-start | bytes 1048576 | tf_op jit(solution)/shard_map/all_to_all | solution.py:470
  43.1 21.2 %copy-start.4 = (bf16[8,8,512]{2,1,0:T(8,128)(2,1)}, bf16[8,8,512]{2,1,0:T(8,128)(2,1)S(1)}, u32[]{:S(2)}) copy-start(bf16[8,8,512]{2,1,0:T(8,128)(2,1)S(1)} %gather_fusion) | copy-start | bytes 196612
  43.1 21.1 %copy-start.3 = (bf16[1,8,8,512]{3,1,2,0:T(8,128)(2,1)}, bf16[1,8,8,512]{3,1,2,0:T(8,128)(2,1)S(1)}, u32[]{:S(2)}) copy-start(bf16[1,8,8,512]{3,1,2,0:T(8,128)(2,1)S(1)} %copy.62) | copy-start | bytes 196612
  45.6 8.7 %collective-permute-start.9 = (bf16[256,512]{1,0:T(8,128)(2,1)S(1)}, bf16[256,512]{1,0:T(8,128)(2,1)S(1)}, u32[]{:S(2)}, u32[]{:S(2)}) collective-permute-start(bf16[256,512]{1,0:T(8,128)(2,1)S(1)} %collective-permute-done.7), channel_id=1, source_target_pairs={{0,2},{2,4},{4,6},{6,7},{7,5},{5,3},{3,1},{1,0},{8,10},{10,12},{12... | collective-permute-start | bytes 786440 | tf_op jit(solution)/shard_map/ppermute | solution.py:163
  49.1 10.3 %collective-permute-start.11 = (bf16[256,512]{1,0:T(8,128)(2,1)S(1)}, bf16[256,512]{1,0:T(8,128)(2,1)S(1)}, u32[]{:S(2)}, u32[]{:S(2)}) collective-permute-start(bf16[256,512]{1,0:T(8,128)(2,1)S(1)} %collective-permute-done.8), channel_id=1, source_target_pairs={{0,1},{2,0},{4,2},{6,4},{7,6},{5,7},{3,5},{1,3},{8,9},{10,8},{12,1... | collective-permute-start | bytes 786440 | tf_op jit(solution)/shard_map/ppermute | solution.py:167
  54.4 8.2 %collective-permute-start.10 = (bf16[256,512]{1,0:T(8,128)(2,1)S(1)}, bf16[256,512]{1,0:T(8,128)(2,1)}, u32[]{:S(2)}, u32[]{:S(2)}) collective-permute-start(bf16[256,512]{1,0:T(8,128)(2,1)S(1)} %collective-permute-done.9), channel_id=1, source_target_pairs={{0,2},{2,4},{4,6},{6,7},{7,5},{5,3},{3,1},{1,0},{8,10},{10,12},{12... | collective-permute-start | bytes 786440 | tf_op jit(solution)/shard_map/ppermute | solution.py:163
  59.4 8.9 %collective-permute-start.12 = (bf16[256,512]{1,0:T(8,128)(2,1)S(1)}, bf16[256,512]{1,0:T(8,128)(2,1)S(1)}, u32[]{:S(2)}, u32[]{:S(2)}) collective-permute-start(bf16[256,512]{1,0:T(8,128)(2,1)S(1)} %collective-permute-done.11), channel_id=1, source_target_pairs={{0,1},{2,0},{4,2},{6,4},{7,6},{5,7},{3,5},{1,3},{8,9},{10,8},{12,1... | collective-permute-start | bytes 786440 | tf_op jit(solution)/shard_map/ppermute | solution.py:167
  65.0 9.0 %collective-permute-start.13 = (bf16[256,512]{1,0:T(8,128)(2,1)}, bf16[256,512]{1,0:T(8,128)(2,1)}, u32[]{:S(2)}, u32[]{:S(2)}) collective-permute-start(bf16[256,512]{1,0:T(8,128)(2,1)} %collective-permute-done.10), channel_id=1, source_target_pairs={{0,2},{2,4},{4,6},{6,7},{7,5},{5,3},{3,1},{1,0},{8,10},{10,12},{12... | collective-permute-start | bytes 786440 | tf_op jit(solution)/shard_map/ppermute | solution.py:163
  71.7 0.7 copy-start.11
  72.3 0.7 copy-start.12
  75.2 0.8 copy-start.1
  76.7 9.2 %copy-start.2 = (f32[256,512]{1,0:T(8,128)S(1)}, f32[256,512]{1,0:T(8,128)}, u32[]{:S(2)}) copy-start(f32[256,512]{1,0:T(8,128)} %copy-done.1) | copy-start | bytes 1572868
  84.9 0.6 copy-start.7
  87.1 5.0 %collective-permute-start.14 = (f32[8,1,4096]{2,0,1:T(8,128)S(1)}, f32[8,1,4096]{2,0,1:T(8,128)S(1)}, u32[]{:S(2)}, u32[]{:S(2)}) collective-permute-start(f32[8,1,4096]{2,0,1:T(8,128)S(1)} %convolution_bitcast_fusion), channel_id=1, source_target_pairs={{0,1},{1,0},{2,3},{3,2},{4,5},{5,4},{6,7},{7,6},{8,9},{9,8},{10,11... | collective-permute-start | bytes 393224 | tf_op jit(solution)/shard_map/ppermute | solution.py:116
  92.1 6.5 %collective-permute-start.15 = (f32[8,1,4096]{2,0,1:T(8,128)S(1)}, f32[8,1,4096]{2,0,1:T(8,128)S(1)}, u32[]{:S(2)}, u32[]{:S(2)}) collective-permute-start(f32[8,1,4096]{2,0,1:T(8,128)S(1)} %add.234), channel_id=1, source_target_pairs={{0,2},{1,3},{2,0},{3,1},{4,6},{5,7},{6,4},{7,5},{8,10},{9,11},{10,... | collective-permute-start | bytes 393224 | tf_op jit(solution)/shard_map/ppermute | solution.py:116
  98.6 7.3 %collective-permute-start.16 = (f32[8,1,4096]{2,0,1:T(8,128)S(1)}, f32[8,1,4096]{2,0,1:T(8,128)S(1)}, u32[]{:S(2)}, u32[]{:S(2)}) collective-permute-start(f32[8,1,4096]{2,0,1:T(8,128)S(1)} %add.235), channel_id=1, source_target_pairs={{0,4},{1,5},{2,6},{3,7},{4,0},{5,1},{6,2},{7,3},{8,12},{9,13},{10,... | collective-permute-start | bytes 393224 | tf_op jit(solution)/shard_map/ppermute | solution.py:116
  106.6 18.0 %copy-start.5 = (bf16[8,8,512]{2,1,0:T(8,128)(2,1)S(1)}, bf16[8,8,512]{2,1,0:T(8,128)(2,1)}, u32[]{:S(2)}) copy-start(bf16[8,8,512]{2,1,0:T(8,128)(2,1)} %copy-done.4) | copy-start | bytes 196612
  120.0 4.3 %collective-permute-start.17 = (f32[2,2,1,1,4096]{4,2,1,0,3:T(1,128)S(1)}, f32[2,2,1,1,4096]{4,2,1,0,3:T(1,128)S(1)}, u32[]{:S(2)}, u32[]{:S(2)}) collective-permute-start(f32[2,2,1,1,4096]{4,2,1,0,3:T(1,128)S(1)} %constant_dynamic-slice_fusion.1), channel_id=1, source_target_pairs={{0,1},{1,0},{2,3},{3,2},{4,5},{5,4},{6,7},{7,6},{8,9},{9,8},{10,11... | collective-permute-start | bytes 196616 | tf_op jit(solution)/shard_map/ppermute | solution.py:573
  124.5 4.0 %collective-permute-start.18 = (f32[2,1,1,1,4096]{4,2,1,0,3:T(1,128)S(1)}, f32[2,1,1,1,4096]{4,2,1,0,3:T(1,128)S(1)}, u32[]{:S(2)}, u32[]{:S(2)}) collective-permute-start(f32[2,1,1,1,4096]{4,2,1,0,3:T(1,128)S(1)} %constant_dynamic-slice_fusion), channel_id=1, source_target_pairs={{0,2},{1,3},{2,0},{3,1},{4,6},{5,7},{6,4},{7,5},{8,10},{9,11},{10,... | collective-permute-start | bytes 98312 | tf_op jit(solution)/shard_map/ppermute | solution.py:573
  128.5 5.0 %collective-permute-start.20 = (f32[1,4096]{1,0:T(1,128)S(1)}, f32[1,4096]{1,0:T(1,128)S(1)}, u32[]{:S(2)}, u32[]{:S(2)}) collective-permute-start(f32[1,4096]{1,0:T(1,128)S(1)} %dynamic-slice_bitcast_fusion), channel_id=1, source_target_pairs={{0,12},{1,13},{2,14},{3,15},{4,8},{5,9},{6,10},{7,11},{8,20},{9,21... | collective-permute-start | bytes 49160 | tf_op jit(solution)/shard_map/ppermute | solution.py:590
  129.5 4.0 %collective-permute-start.19 = (f32[1,4096]{1,0:T(1,128)S(1)}, f32[1,4096]{1,0:T(1,128)S(1)}, u32[]{:S(2)}, u32[]{:S(2)}) collective-permute-start(f32[1,4096]{1,0:T(1,128)S(1)} %fusion.43), channel_id=1, source_target_pairs={{0,8},{1,9},{2,10},{3,11},{4,12},{5,13},{6,14},{7,15},{8,16},{9,17... | collective-permute-start | bytes 49160 | tf_op jit(solution)/shard_map/ppermute | solution.py:589

commit v18 on v16

--- a/solution.py
+++ b/solution.py
@@ -466,9 +466,6 @@
     my_cols = heads_here * head_size
     col_blocks = tile_out[0].reshape(tile_out.shape[1], 2, group_size, my_cols)
     col_blocks = jnp.transpose(col_blocks, (2, 0, 1, 3)).reshape(group_size, tile_out.shape[1], 2 * my_cols)
-    in_slots, col_blocks = lax.optimization_barrier((in_slots, col_blocks))
-    weight_out = lax.all_to_all(col_blocks, "site", split_axis=0, concat_axis=0, tiled=True)
-    weight_out = weight_out.reshape(-1, 2 * my_cols)
     del kv_width
 
     everyone = (
@@ -492,6 +489,9 @@
 
     ring_hidden = RingGather(tile_hidden, group_size, my_index)
     site_tiles, site_count = ring_hidden.step((site_tiles, site_count))
+    col_blocks = ring_hidden.step(col_blocks)
+    weight_out = lax.all_to_all(col_blocks, "site", split_axis=0, concat_axis=0, tiled=True)
+    weight_out = weight_out.reshape(-1, 2 * my_cols)
     hidden_slots, hidden_sources = ring_hidden.finish()
     table_hidden = hidden_slots.reshape(group_size * tiles_here, hidden_width)
     keyval = jnp.dot(table_hidden, weight_out, preferred_element_type=jnp.float32)

time: 126 us -> 132 us (1.048)
  waiting for transfers between devices: 39.4 us -> 45.4 us
  local copies, waits for them, and re-layouts: 15.5 us -> 17.3 us
  matrix products: 9.25 us -> 7.65 us
    ppermute x6, waiting for transfers between devices: 0.69 us -> 6.67 us  [_issue(): self.behind = lax.ppermute(self.behind, 'site', self.backward)]
    ppermute x8, starting transfers between devices: 22.6 us -> 17.5 us  [_issue(): self.ahead = lax.ppermute(self.ahead, 'site', self.forward)]
    ppermute x8, waiting for transfers between devices: 17.2 us -> 21.2 us  [_issue(): self.ahead = lax.ppermute(self.ahead, 'site', self.forward)]
    ppermute x2, starting transfers between devices: 0.36 us -> 4.12 us  [last_round(): state = keep + lax.ppermute(send, 'site', xor_pairs(group_size, bit))]
    ppermute x2, waiting for transfers between devices: 7.9 us -> 4.16 us  [last_round(): state = keep + lax.ppermute(send, 'site', xor_pairs(group_size, bit))]
    all_to_all x1, starting transfers between devices: 6.25 us -> 4.01 us  [heads_split(): lax.all_to_all(col_blocks, 'site', split_axis=0, concat_axis=0, tiled=True)]
    ppermute x6, starting transfers between devices: 0.48 us -> 2.72 us  [_issue(): self.behind = lax.ppermute(self.behind, 'site', self.backward)]
    unnamed x34, local copies, waits for them, and re-layouts: 7.84 us -> 9.66 us
  transfers between devices with their start and end apart: 22 -> 22, of which waited for: 12 -> 15; matrix products, arithmetic and copies ran while one was open for 18% -> 19% of each run, Pallas kernels for 0% -> 0%
where the time goes in v18:
time: 132 us; the launch traced here: 131 us
  waiting for transfers between devices  45.4 us (34%)
  starting transfers between devices  36.8 us (28%)
  local copies, waits for them, and re-layouts  17.3 us (13%)
  Pallas kernels  12.3 us (9%)
  other arithmetic  11.2 us (8%)
  matrix products  7.65 us (6%)
    ppermute x8, waiting for transfers between devices, _issue(): self.ahead = lax.ppermute(self.ahead, 'site', self.forward)  21.2 us
    ppermute x8, starting transfers between devices, _issue(): self.ahead = lax.ppermute(self.ahead, 'site', self.forward)  17.5 us
    pallas_call x1, Pallas kernels, gated_ffn(): pl.pallas_call(ffn_block, grid=(units // block,), in_specs=[whole, whole,...  12.3 us
    ppermute x3, waiting for transfers between devices, doubling_sum(): state = state + lax.ppermute(state, 'site', xor_pairs(count, bit))  11.8 us
    unnamed x34, local copies, waits for them, and re-layouts  9.66 us
    ppermute x6, waiting for transfers between devices, _issue(): self.behind = lax.ppermute(self.behind, 'site', self.backward)  6.67 us
    ppermute x3, starting transfers between devices, doubling_sum(): state = state + lax.ppermute(state, 'site', xor_pairs(count, bit))  4.9 us
    ppermute x2, waiting for transfers between devices, last_round(): state = keep + lax.ppermute(send, 'site', xor_pairs(group_size, bit))  4.16 us
  transfers between devices with their start and end apart: 22, of which 15 were waited for; matrix products, arithmetic and copies ran while one was open for 19% of the time, Pallas kernels for 0%

profile of v18, /device:TPU:0, one launch (start us, length us, event | category | flops | bytes accessed | tf_op | source)
XLA Modules:
  0.0 130.9 jit_solution(8438205997779951849)
XLA Ops:
  0.0 0.9 reduce
  1.0 1.6 %pad_maximum_fusion = bf16[136,512]{1,0:T(8,128)(2,1)} fusion(bf16[8,512]{1,0:T(8,128)(2,1)S(1)} %reshape_squeeze.9, bf16[128,512]{1,0:T(8,128)(2,1)} %bitcast.153), kind=kLoop, calls=%fused_computation.41 | loop fusion | flops 278528 | bytes 278528 | tf_op jit(solution)/shard_map/concatenate | solution.py:459
  2.5 3.0 %collective-permute-start = (bf16[136,512]{1,0:T(8,128)(2,1)}, bf16[136,512]{1,0:T(8,128)(2,1)S(1)}, u32[]{:S(2)}, u32[]{:S(2)}) collective-permute-start(bf16[136,512]{1,0:T(8,128)(2,1)} %pad_maximum_fusion), channel_id=1, source_target_pairs={{0,2},{2,4},{4,6},{6,7},{7,5},{5,3},{3,1},{1,0},{8,10},{10,12},{12... | collective-permute-start | bytes 417800 | tf_op jit(solution)/shard_map/ppermute | solution.py:163
  5.6 0.7 broadcast_multiply_fusion
  6.3 1.2 broadcast_bitcast_fusion
  7.4 1.2 broadcast_bitcast_fusion.1
  8.7 0.6 pad_clamp_fusion
  9.3 0.6 pad_clamp_fusion.1
  9.9 0.6 copy.36
  10.5 1.2 copy.27
  12.1 1.2 copy.35
  13.3 0.4 copy.38
  13.7 1.1 reshape.262
  14.8 0.8 gather_fusion.1
  15.6 0.7 bitcast_dynamic-update-slice_fusion.15
  16.3 2.1 %collective-permute-start.1 = (bf16[136,512]{1,0:T(8,128)(2,1)S(1)}, bf16[136,512]{1,0:T(8,128)(2,1)S(1)}, u32[]{:S(2)}, u32[]{:S(2)}) collective-permute-start(bf16[136,512]{1,0:T(8,128)(2,1)S(1)} %collective-permute-done), channel_id=1, source_target_pairs={{0,2},{2,4},{4,6},{6,7},{7,5},{5,3},{3,1},{1,0},{8,10},{10,12},{12... | collective-permute-start | bytes 417800 | tf_op jit(solution)/shard_map/ppermute | solution.py:163
  18.4 3.1 %collective-permute-done.1 = bf16[136,512]{1,0:T(8,128)(2,1)S(1)} collective-permute-done((bf16[136,512]{1,0:T(8,128)(2,1)S(1)}, bf16[136,512]{1,0:T(8,128)(2,1)S(1)}, u32[]{:S(2)}, u32[]{:S(2)}) %collective-permute-start.1) | collective-permute-done | bytes 139296 | tf_op jit(solution)/shard_map/ppermute | solution.py:163
  21.5 1.9 %collective-permute-start.2 = (bf16[136,512]{1,0:T(8,128)(2,1)S(1)}, bf16[136,512]{1,0:T(8,128)(2,1)S(1)}, u32[]{:S(2)}, u32[]{:S(2)}) collective-permute-start(bf16[136,512]{1,0:T(8,128)(2,1)S(1)} %collective-permute-done.1), channel_id=1, source_target_pairs={{0,2},{2,4},{4,6},{6,7},{7,5},{5,3},{3,1},{1,0},{8,10},{10,12},{12... | collective-permute-start | bytes 417800 | tf_op jit(solution)/shard_map/ppermute | solution.py:163
  23.5 3.0 %collective-permute-done.2 = bf16[136,512]{1,0:T(8,128)(2,1)S(1)} collective-permute-done((bf16[136,512]{1,0:T(8,128)(2,1)S(1)}, bf16[136,512]{1,0:T(8,128)(2,1)S(1)}, u32[]{:S(2)}, u32[]{:S(2)}) %collective-permute-start.2) | collective-permute-done | bytes 139296 | tf_op jit(solution)/shard_map/ppermute | solution.py:163
  26.5 2.4 %collective-permute-start.3 = (bf16[136,512]{1,0:T(8,128)(2,1)S(1)}, bf16[136,512]{1,0:T(8,128)(2,1)S(1)}, u32[]{:S(2)}, u32[]{:S(2)}) collective-permute-start(bf16[136,512]{1,0:T(8,128)(2,1)S(1)} %collective-permute-done.2), channel_id=1, source_target_pairs={{0,2},{2,4},{4,6},{6,7},{7,5},{5,3},{3,1},{1,0},{8,10},{10,12},{12... | collective-permute-start | bytes 417800 | tf_op jit(solution)/shard_map/ppermute | solution.py:163
  28.9 2.9 %collective-permute-done.3 = bf16[136,512]{1,0:T(8,128)(2,1)S(1)} collective-permute-done((bf16[136,512]{1,0:T(8,128)(2,1)S(1)}, bf16[136,512]{1,0:T(8,128)(2,1)S(1)}, u32[]{:S(2)}, u32[]{:S(2)}) %collective-permute-start.3) | collective-permute-done | bytes 139296 | tf_op jit(solution)/shard_map/ppermute | solution.py:163
  32.0 1.2 bitcast_dynamic-update-slice_fusion.7
  33.2 2.1 %collective-permute-start.7 = (bf16[256,512]{1,0:T(8,128)(2,1)S(1)}, bf16[256,512]{1,0:T(8,128)(2,1)S(1)}, u32[]{:S(2)}, u32[]{:S(2)}) collective-permute-start(bf16[256,512]{1,0:T(8,128)(2,1)S(1)} %get-tuple-element.22), channel_id=1, source_target_pairs={{0,2},{2,4},{4,6},{6,7},{7,5},{5,3},{3,1},{1,0},{8,10},{10,12},{12... | collective-permute-start | bytes 786440 | tf_op jit(solution)/shard_map/ppermute | solution.py:163
  35.5 0.7 gather_fusion
  36.2 2.3 %bitcast_reduce_fusion.1 = (f32[8,2]{0,1:T(2,128)S(1)}, f32[8,256]{1,0:T(8,128)S(1)}) fusion(bf16[8,4096]{1,0:T(8,128)(2,1)S(1)} %bitcast.149, bf16[1,256,4096]{2,1,0:T(8,128)(2,1)} %param.20), kind=kOutput, calls=%fused_computation.65 | convolution fusion | flops 16785392 | bytes 2170944 | tf_op jit(solution)/shard_map/dot_general | solution.py:23
  38.5 2.0 %collective-permute-done.7 = bf16[256,512]{1,0:T(8,128)(2,1)S(1)} collective-permute-done((bf16[256,512]{1,0:T(8,128)(2,1)S(1)}, bf16[256,512]{1,0:T(8,128)(2,1)S(1)}, u32[]{:S(2)}, u32[]{:S(2)}) %collective-permute-start.7) | collective-permute-done | bytes 262176 | tf_op jit(solution)/shard_map/ppermute | solution.py:163
  40.5 2.5 %collective-permute-done.8 = bf16[256,512]{1,0:T(8,128)(2,1)S(1)} collective-permute-done((bf16[256,512]{1,0:T(8,128)(2,1)S(1)}, bf16[256,512]{1,0:T(8,128)(2,1)S(1)}, u32[]{:S(2)}, u32[]{:S(2)}) %collective-permute-start.8) | collective-permute-done | bytes 262176 | tf_op jit(solution)/shard_map/ppermute | solution.py:167
  43.0 1.6 %collective-permute-start.9 = (bf16[256,512]{1,0:T(8,128)(2,1)S(1)}, bf16[256,512]{1,0:T(8,128)(2,1)S(1)}, u32[]{:S(2)}, u32[]{:S(2)}) collective-permute-start(bf16[256,512]{1,0:T(8,128)(2,1)S(1)} %collective-permute-done.7), channel_id=1, source_target_pairs={{0,2},{2,4},{4,6},{6,7},{7,5},{5,3},{3,1},{1,0},{8,10},{10,12},{12... | collective-permute-start | bytes 786440 | tf_op jit(solution)/shard_map/ppermute | solution.py:163
  44.6 0.4 collective-permute-start.10
  45.1 6.8 %collective-permute-done.9 = bf16[256,512]{1,0:T(8,128)(2,1)S(1)} collective-permute-done((bf16[256,512]{1,0:T(8,128)(2,1)S(1)}, bf16[256,512]{1,0:T(8,128)(2,1)S(1)}, u32[]{:S(2)}, u32[]{:S(2)}) %collective-permute-start.9) | collective-permute-done | bytes 262176 | tf_op jit(solution)/shard_map/ppermute | solution.py:163
  51.9 1.6 %collective-permute-start.11 = (bf16[256,512]{1,0:T(8,128)(2,1)S(1)}, bf16[256,512]{1,0:T(8,128)(2,1)}, u32[]{:S(2)}, u32[]{:S(2)}) collective-permute-start(bf16[256,512]{1,0:T(8,128)(2,1)S(1)} %collective-permute-done.9), channel_id=1, source_target_pairs={{0,2},{2,4},{4,6},{6,7},{7,5},{5,3},{3,1},{1,0},{8,10},{10,12},{12... | collective-permute-start | bytes 786440 | tf_op jit(solution)/shard_map/ppermute | solution.py:163
  53.5 3.1 %convert_reduce_fusion = f32[8,2048]{1,0:T(8,128)S(1)} fusion(s32[2048]{0:T(1024)S(1)} %bitcast.155, s32[8,256]{1,0:T(8,128)S(1)} %copy-done.5, pred[8,256]{1,0:T(8,128)(4,1)S(1)} %iota_compare_fusion), kind=kLoop, calls=%fused_computation.2 | loop fusion | flops 16760832 | bytes 83968 | tf_op jit(solution)/shard_map/reduce_sum | solution.py:510
  56.7 0.7 bitcast_dynamic-update-slice_fusion.6
  57.4 3.4 %collective-permute-done.11 = bf16[256,512]{1,0:T(8,128)(2,1)} collective-permute-done((bf16[256,512]{1,0:T(8,128)(2,1)S(1)}, bf16[256,512]{1,0:T(8,128)(2,1)}, u32[]{:S(2)}, u32[]{:S(2)}) %collective-permute-start.11) | collective-permute-done | bytes 262176 | tf_op jit(solution)/shard_map/ppermute | solution.py:163
  60.8 2.8 %collective-permute-start.12 = (bf16[256,512]{1,0:T(8,128)(2,1)}, bf16[256,512]{1,0:T(8,128)(2,1)}, u32[]{:S(2)}, u32[]{:S(2)}) collective-permute-start(bf16[256,512]{1,0:T(8,128)(2,1)} %collective-permute-done.11), channel_id=1, source_target_pairs={{0,2},{2,4},{4,6},{6,7},{7,5},{5,3},{3,1},{1,0},{8,10},{10,12},{12... | collective-permute-start | bytes 786440 | tf_op jit(solution)/shard_map/ppermute | solution.py:163
  63.6 0.7 bitcast_dynamic-update-slice_fusion.5
  64.3 4.0 %all-to-all-start = ((bf16[8,64,512]{2,1,0:T(8,128)(2,1)}), bf16[8,64,512]{2,1,0:T(8,128)(2,1)S(1)}, u32[]{:S(2)}, u32[]{:S(2)}) async-start(bf16[8,64,512]{2,1,0:T(8,128)(2,1)} %reshape.262), calls=%async_computation | async-start | bytes 1048576 | tf_op jit(solution)/shard_map/all_to_all | solution.py:493
  68.3 2.0 %collective-permute-start.13 = (bf16[256,512]{1,0:T(8,128)(2,1)S(1)}, bf16[256,512]{1,0:T(8,128)(2,1)S(1)}, u32[]{:S(2)}, u32[]{:S(2)}) collective-permute-start(bf16[256,512]{1,0:T(8,128)(2,1)S(1)} %collective-permute-done.10), channel_id=1, source_target_pairs={{0,1},{2,0},{4,2},{6,4},{7,6},{5,7},{3,5},{1,3},{8,9},{10,8},{12,1... | collective-permute-start | bytes 786440 | tf_op jit(solution)/shard_map/ppermute | solution.py:167
  70.4 1.7 %bitcast_dynamic-update-slice_fusion.4 = bf16[8,256,512]{2,1,0:T(8,128)(2,1)} fusion(bf16[8,256,512]{2,1,0:T(8,128)(2,1)} %bitcast_dynamic-update-slice_fusion.5, bf16[256,512]{1,0:T(8,128)(2,1)} %collective-permute-done.11), kind=kLoop, calls=%fused_computation.37 | loop fusion | bytes 524288
  72.0 1.7 %bitcast_dynamic-update-slice_fusion.3 = bf16[8,256,512]{2,1,0:T(8,128)(2,1)} fusion(bf16[8,256,512]{2,1,0:T(8,128)(2,1)} %bitcast_dynamic-update-slice_fusion.4, bf16[256,512]{1,0:T(8,128)(2,1)} %collective-permute-done.12), kind=kLoop, calls=%fused_computation.36 | loop fusion | bytes 524288
  73.7 0.7 bitcast_dynamic-update-slice_fusion.2
  74.4 0.7 bitcast_dynamic-update-slice_fusion.1
  75.1 4.1 %collective-permute-done.13 = bf16[256,512]{1,0:T(8,128)(2,1)S(1)} collective-permute-done((bf16[256,512]{1,0:T(8,128)(2,1)S(1)}, bf16[256,512]{1,0:T(8,128)(2,1)S(1)}, u32[]{:S(2)}, u32[]{:S(2)}) %collective-permute-start.13) | collective-permute-done | bytes 262176 | tf_op jit(solution)/shard_map/ppermute | solution.py:167
  79.2 0.7 bitcast_dynamic-update-slice_fusion
  80.0 2.9 %fusion.44 = f32[2048,512]{0,1:T(8,128)S(1)} fusion(bf16[2048,512]{1,0:T(8,128)(2,1)} %bitcast.22, bf16[512,512]{1,0:T(8,128)(2,1)S(1)} %bitcast.144), kind=kOutput, calls=%fused_computation.100 | convolution fusion | flops 1073741824 | bytes 6815744 | tf_op jit(solution)/shard_map/dot_general | solution.py:497
  84.2 0.8 convolution_bitcast_fusion
  85.0 0.4 collective-permute-start.14
  85.4 4.5 %collective-permute-done.14 = f32[8,1,4096]{2,0,1:T(8,128)S(1)} collective-permute-done((f32[8,1,4096]{2,0,1:T(8,128)S(1)}, f32[8,1,4096]{2,0,1:T(8,128)S(1)}, u32[]{:S(2)}, u32[]{:S(2)}) %collective-permute-start.14) | collective-permute-done | bytes 131104 | tf_op jit(solution)/shard_map/ppermute | solution.py:116
  90.0 2.9 %collective-permute-start.15 = (f32[8,1,4096]{2,0,1:T(8,128)S(1)}, f32[8,1,4096]{2,0,1:T(8,128)S(1)}, u32[]{:S(2)}, u32[]{:S(2)}) collective-permute-start(f32[8,1,4096]{2,0,1:T(8,128)S(1)} %add.216), channel_id=1, source_target_pairs={{0,2},{1,3},{2,0},{3,1},{4,6},{5,7},{6,4},{7,5},{8,10},{9,11},{10,... | collective-permute-start | bytes 393224 | tf_op jit(solution)/shard_map/ppermute | solution.py:116
  92.9 2.9 %collective-permute-done.15 = f32[8,1,4096]{2,0,1:T(8,128)S(1)} collective-permute-done((f32[8,1,4096]{2,0,1:T(8,128)S(1)}, f32[8,1,4096]{2,0,1:T(8,128)S(1)}, u32[]{:S(2)}, u32[]{:S(2)}) %collective-permute-start.15) | collective-permute-done | bytes 131104 | tf_op jit(solution)/shard_map/ppermute | solution.py:116
  95.8 1.6 %collective-permute-start.16 = (f32[8,1,4096]{2,0,1:T(8,128)S(1)}, f32[8,1,4096]{2,0,1:T(8,128)S(1)}, u32[]{:S(2)}, u32[]{:S(2)}) collective-permute-start(f32[8,1,4096]{2,0,1:T(8,128)S(1)} %add.217), channel_id=1, source_target_pairs={{0,4},{1,5},{2,6},{3,7},{4,0},{5,1},{6,2},{7,3},{8,12},{9,13},{10,... | collective-permute-start | bytes 393224 | tf_op jit(solution)/shard_map/ppermute | solution.py:116
  97.4 4.3 %collective-permute-done.16 = f32[8,1,4096]{2,0,1:T(8,128)S(1)} collective-permute-done((f32[8,1,4096]{2,0,1:T(8,128)S(1)}, f32[8,1,4096]{2,0,1:T(8,128)S(1)}, u32[]{:S(2)}, u32[]{:S(2)}) %collective-permute-start.16) | collective-permute-done | bytes 131104 | tf_op jit(solution)/shard_map/ppermute | solution.py:116
  101.8 0.7 add.218
  102.4 12.3 %shard_map.154 = f32[8,4096]{1,0:T(8,128)} custom-call(bf16[8,4096]{1,0:T(8,128)(2,1)} %bitcast.150, f32[8,4096]{1,0:T(8,128)} %bitcast.148, f32[1,4096]{1,0:T(1,128)} %gain_ref.1, bf16[896,4096]{1,0:T(8,128)(2,1)} %bitcast.136, bf16[896,4096]{1,0:T(8,128)(2,1)} %bitcast.137, bf16[896,4096]{1,0:T(8,128)(2,1)} %bitcast.138, bf16[896,4096]{1,0:T(8,128)(2,1)} %bitcast.139, ...), custom_call_target="tpu_custom_call" | custom-call | tf_op jit(solution)/shard_map/pallas_call | solution.py:407
  114.8 1.0 reshape_reshape.4
  115.8 2.0 %collective-permute-start.17 = (f32[2,2,1,1,4096]{4,2,1,0,3:T(1,128)S(1)}, f32[2,2,1,1,4096]{4,2,1,0,3:T(1,128)S(1)}, u32[]{:S(2)}, u32[]{:S(2)}) collective-permute-start(f32[2,2,1,1,4096]{4,2,1,0,3:T(1,128)S(1)} %constant_dynamic-slice_fusion.1), channel_id=1, source_target_pairs={{0,1},{1,0},{2,3},{3,2},{4,5},{5,4},{6,7},{7,6},{8,9},{9,8},{10,11... | collective-permute-start | bytes 196616 | tf_op jit(solution)/shard_map/ppermute | solution.py:546
  117.9 2.3 %collective-permute-done.17 = f32[2,2,1,1,4096]{4,2,1,0,3:T(1,128)S(1)} collective-permute-done((f32[2,2,1,1,4096]{4,2,1,0,3:T(1,128)S(1)}, f32[2,2,1,1,4096]{4,2,1,0,3:T(1,128)S(1)}, u32[]{:S(2)}, u32[]{:S(2)}) %collective-permute-start.17) | collective-permute-done | bytes 65568 | tf_op jit(solution)/shard_map/ppermute | solution.py:546
  120.3 2.1 %collective-permute-start.18 = (f32[2,1,1,1,4096]{4,2,1,0,3:T(1,128)S(1)}, f32[2,1,1,1,4096]{4,2,1,0,3:T(1,128)S(1)}, u32[]{:S(2)}, u32[]{:S(2)}) collective-permute-start(f32[2,1,1,1,4096]{4,2,1,0,3:T(1,128)S(1)} %constant_dynamic-slice_fusion), channel_id=1, source_target_pairs={{0,2},{1,3},{2,0},{3,1},{4,6},{5,7},{6,4},{7,5},{8,10},{9,11},{10,... | collective-permute-start | bytes 98312 | tf_op jit(solution)/shard_map/ppermute | solution.py:546
  122.4 1.9 %collective-permute-done.18 = f32[2,1,1,1,4096]{4,2,1,0,3:T(1,128)S(1)} collective-permute-done((f32[2,1,1,1,4096]{4,2,1,0,3:T(1,128)S(1)}, f32[2,1,1,1,4096]{4,2,1,0,3:T(1,128)S(1)}, u32[]{:S(2)}, u32[]{:S(2)}) %collective-permute-start.18) | collective-permute-done | bytes 32800 | tf_op jit(solution)/shard_map/ppermute | solution.py:546
  124.4 0.9 fusion.33
  125.3 3.4 %collective-permute-start.19 = (f32[1,4096]{1,0:T(1,128)S(1)}, f32[1,4096]{1,0:T(1,128)S(1)}, u32[]{:S(2)}, u32[]{:S(2)}) collective-permute-start(f32[1,4096]{1,0:T(1,128)S(1)} %fusion.33), channel_id=1, source_target_pairs={{0,8},{1,9},{2,10},{3,11},{4,12},{5,13},{6,14},{7,15},{8,16},{9,17... | collective-permute-start | bytes 49160 | tf_op jit(solution)/shard_map/ppermute | solution.py:562
  128.7 0.7 collective-permute-done.20
  129.5 0.8 collective-permute-done.19
  130.3 0.6 convert_bitcast_fusion
  (59 shorter events, 2.5 us)
Async XLA Ops:
  0.0 84.2 %copy-start = (bf16[1,256,4096]{2,1,0:T(8,128)(2,1)S(1)}, bf16[1,256,4096]{2,1,0:T(8,128)(2,1)}, u32[]{:S(2)}) copy-start(bf16[1,256,4096]{2,1,0:T(8,128)(2,1)} %param.25) | copy-start | bytes 6291460
  0.9 1.6 %copy-start.3 = (bf16[8,512]{1,0:T(8,128)(2,1)}, bf16[8,512]{1,0:T(8,128)(2,1)S(1)}, u32[]{:S(2)}) copy-start(bf16[8,512]{1,0:T(8,128)(2,1)S(1)} %reshape_squeeze.9) | copy-start | bytes 24580
  2.5 13.8 %collective-permute-start = (bf16[136,512]{1,0:T(8,128)(2,1)}, bf16[136,512]{1,0:T(8,128)(2,1)S(1)}, u32[]{:S(2)}, u32[]{:S(2)}) collective-permute-start(bf16[136,512]{1,0:T(8,128)(2,1)} %pad_maximum_fusion), channel_id=1, source_target_pairs={{0,2},{2,4},{4,6},{6,7},{7,5},{5,3},{3,1},{1,0},{8,10},{10,12},{12... | collective-permute-start | bytes 417800 | tf_op jit(solution)/shard_map/ppermute | solution.py:163
  5.6 12.8 %collective-permute-start.4 = (bf16[136,512]{1,0:T(8,128)(2,1)}, bf16[136,512]{1,0:T(8,128)(2,1)S(1)}, u32[]{:S(2)}, u32[]{:S(2)}) collective-permute-start(bf16[136,512]{1,0:T(8,128)(2,1)} %pad_maximum_fusion), channel_id=1, source_target_pairs={{0,1},{2,0},{4,2},{6,4},{7,6},{5,7},{3,5},{1,3},{8,9},{10,8},{12,1... | collective-permute-start | bytes 417800 | tf_op jit(solution)/shard_map/ppermute | solution.py:167
  12.1 3.5 %copy-start.2 = (bf16[1,128,512]{2,1,0:T(8,128)(2,1)S(1)}, bf16[1,128,512]{2,1,0:T(8,128)(2,1)}, u32[]{:S(2)}) copy-start(bf16[1,128,512]{2,1,0:T(8,128)(2,1)} %param.23) | copy-start | bytes 393220
  16.3 5.2 %collective-permute-start.1 = (bf16[136,512]{1,0:T(8,128)(2,1)S(1)}, bf16[136,512]{1,0:T(8,128)(2,1)S(1)}, u32[]{:S(2)}, u32[]{:S(2)}) collective-permute-start(bf16[136,512]{1,0:T(8,128)(2,1)S(1)} %collective-permute-done), channel_id=1, source_target_pairs={{0,2},{2,4},{4,6},{6,7},{7,5},{5,3},{3,1},{1,0},{8,10},{10,12},{12... | collective-permute-start | bytes 417800 | tf_op jit(solution)/shard_map/ppermute | solution.py:163
  18.4 5.1 %collective-permute-start.5 = (bf16[136,512]{1,0:T(8,128)(2,1)S(1)}, bf16[136,512]{1,0:T(8,128)(2,1)S(1)}, u32[]{:S(2)}, u32[]{:S(2)}) collective-permute-start(bf16[136,512]{1,0:T(8,128)(2,1)S(1)} %collective-permute-done.4), channel_id=1, source_target_pairs={{0,1},{2,0},{4,2},{6,4},{7,6},{5,7},{3,5},{1,3},{8,9},{10,8},{12,1... | collective-permute-start | bytes 417800 | tf_op jit(solution)/shard_map/ppermute | solution.py:167
  21.5 5.1 %collective-permute-start.2 = (bf16[136,512]{1,0:T(8,128)(2,1)S(1)}, bf16[136,512]{1,0:T(8,128)(2,1)S(1)}, u32[]{:S(2)}, u32[]{:S(2)}) collective-permute-start(bf16[136,512]{1,0:T(8,128)(2,1)S(1)} %collective-permute-done.1), channel_id=1, source_target_pairs={{0,2},{2,4},{4,6},{6,7},{7,5},{5,3},{3,1},{1,0},{8,10},{10,12},{12... | collective-permute-start | bytes 417800 | tf_op jit(solution)/shard_map/ppermute | solution.py:163
  23.4 8.5 %collective-permute-start.6 = (bf16[136,512]{1,0:T(8,128)(2,1)S(1)}, bf16[136,512]{1,0:T(8,128)(2,1)S(1)}, u32[]{:S(2)}, u32[]{:S(2)}) collective-permute-start(bf16[136,512]{1,0:T(8,128)(2,1)S(1)} %collective-permute-done.5), channel_id=1, source_target_pairs={{0,1},{2,0},{4,2},{6,4},{7,6},{5,7},{3,5},{1,3},{8,9},{10,8},{12,1... | collective-permute-start | bytes 417800 | tf_op jit(solution)/shard_map/ppermute | solution.py:167
  26.5 5.3 %collective-permute-start.3 = (bf16[136,512]{1,0:T(8,128)(2,1)S(1)}, bf16[136,512]{1,0:T(8,128)(2,1)S(1)}, u32[]{:S(2)}, u32[]{:S(2)}) collective-permute-start(bf16[136,512]{1,0:T(8,128)(2,1)S(1)} %collective-permute-done.2), channel_id=1, source_target_pairs={{0,2},{2,4},{4,6},{6,7},{7,5},{5,3},{3,1},{1,0},{8,10},{10,12},{12... | collective-permute-start | bytes 417800 | tf_op jit(solution)/shard_map/ppermute | solution.py:163
  33.2 11.9 %copy-start.8 = (s32[8]{0:T(128)S(1)}, s32[8]{0:T(128)}, u32[]{:S(2)}) copy-start(s32[8]{0:T(128)} %param.19) | copy-start | bytes 100
  33.2 20.3 %copy-start.4 = (s32[1,2,8,128]{3,1,2,0:T(2,128)S(1)}, s32[1,2,8,128]{3,1,2,0:T(2,128)}, u32[]{:S(2)}) copy-start(s32[1,2,8,128]{3,1,2,0:T(2,128)} %copy.36) | copy-start | bytes 24580
  33.2 20.3 %copy-start.5 = (s32[8,256]{1,0:T(8,128)S(1)}, s32[8,256]{1,0:T(8,128)}, u32[]{:S(2)}) copy-start(s32[8,256]{1,0:T(8,128)} %param.18) | copy-start | bytes 24580
  33.2 7.3 %collective-permute-start.7 = (bf16[256,512]{1,0:T(8,128)(2,1)S(1)}, bf16[256,512]{1,0:T(8,128)(2,1)S(1)}, u32[]{:S(2)}, u32[]{:S(2)}) collective-permute-start(bf16[256,512]{1,0:T(8,128)(2,1)S(1)} %get-tuple-element.22), channel_id=1, source_target_pairs={{0,2},{2,4},{4,6},{6,7},{7,5},{5,3},{3,1},{1,0},{8,10},{10,12},{12... | collective-permute-start | bytes 786440 | tf_op jit(solution)/shard_map/ppermute | solution.py:163
  35.3 7.7 %collective-permute-start.8 = (bf16[256,512]{1,0:T(8,128)(2,1)S(1)}, bf16[256,512]{1,0:T(8,128)(2,1)S(1)}, u32[]{:S(2)}, u32[]{:S(2)}) collective-permute-start(bf16[256,512]{1,0:T(8,128)(2,1)S(1)} %get-tuple-element.22), channel_id=1, source_target_pairs={{0,1},{2,0},{4,2},{6,4},{7,6},{5,7},{3,5},{1,3},{8,9},{10,8},{12,1... | collective-permute-start | bytes 786440 | tf_op jit(solution)/shard_map/ppermute | solution.py:167
  36.2 28.1 %copy-start.1 = (bf16[1,8,8,512]{3,1,2,0:T(8,128)(2,1)}, bf16[1,8,8,512]{3,1,2,0:T(8,128)(2,1)S(1)}, u32[]{:S(2)}) copy-start(bf16[1,8,8,512]{3,1,2,0:T(8,128)(2,1)S(1)} %copy.34) | copy-start | bytes 196612
  43.0 8.9 %collective-permute-start.9 = (bf16[256,512]{1,0:T(8,128)(2,1)S(1)}, bf16[256,512]{1,0:T(8,128)(2,1)S(1)}, u32[]{:S(2)}, u32[]{:S(2)}) collective-permute-start(bf16[256,512]{1,0:T(8,128)(2,1)S(1)} %collective-permute-done.7), channel_id=1, source_target_pairs={{0,2},{2,4},{4,6},{6,7},{7,5},{5,3},{3,1},{1,0},{8,10},{10,12},{12... | collective-permute-start | bytes 786440 | tf_op jit(solution)/shard_map/ppermute | solution.py:163
  44.6 7.3 %collective-permute-start.10 = (bf16[256,512]{1,0:T(8,128)(2,1)S(1)}, bf16[256,512]{1,0:T(8,128)(2,1)S(1)}, u32[]{:S(2)}, u32[]{:S(2)}) collective-permute-start(bf16[256,512]{1,0:T(8,128)(2,1)S(1)} %collective-permute-done.8), channel_id=1, source_target_pairs={{0,1},{2,0},{4,2},{6,4},{7,6},{5,7},{3,5},{1,3},{8,9},{10,8},{12,1... | collective-permute-start | bytes 786440 | tf_op jit(solution)/shard_map/ppermute | solution.py:167
  51.9 8.9 %collective-permute-start.11 = (bf16[256,512]{1,0:T(8,128)(2,1)S(1)}, bf16[256,512]{1,0:T(8,128)(2,1)}, u32[]{:S(2)}, u32[]{:S(2)}) collective-permute-start(bf16[256,512]{1,0:T(8,128)(2,1)S(1)} %collective-permute-done.9), channel_id=1, source_target_pairs={{0,2},{2,4},{4,6},{6,7},{7,5},{5,3},{3,1},{1,0},{8,10},{10,12},{12... | collective-permute-start | bytes 786440 | tf_op jit(solution)/shard_map/ppermute | solution.py:163
  60.8 11.2 %collective-permute-start.12 = (bf16[256,512]{1,0:T(8,128)(2,1)}, bf16[256,512]{1,0:T(8,128)(2,1)}, u32[]{:S(2)}, u32[]{:S(2)}) collective-permute-start(bf16[256,512]{1,0:T(8,128)(2,1)} %collective-permute-done.11), channel_id=1, source_target_pairs={{0,2},{2,4},{4,6},{6,7},{7,5},{5,3},{3,1},{1,0},{8,10},{10,12},{12... | collective-permute-start | bytes 786440 | tf_op jit(solution)/shard_map/ppermute | solution.py:163
  64.3 15.6 %all-to-all-start = ((bf16[8,64,512]{2,1,0:T(8,128)(2,1)}), bf16[8,64,512]{2,1,0:T(8,128)(2,1)S(1)}, u32[]{:S(2)}, u32[]{:S(2)}) async-start(bf16[8,64,512]{2,1,0:T(8,128)(2,1)} %reshape.262), calls=%async_computation | async-start | bytes 1048576 | tf_op jit(solution)/shard_map/all_to_all | solution.py:493
  68.3 10.9 %collective-permute-start.13 = (bf16[256,512]{1,0:T(8,128)(2,1)S(1)}, bf16[256,512]{1,0:T(8,128)(2,1)S(1)}, u32[]{:S(2)}, u32[]{:S(2)}) collective-permute-start(bf16[256,512]{1,0:T(8,128)(2,1)S(1)} %collective-permute-done.10), channel_id=1, source_target_pairs={{0,1},{2,0},{4,2},{6,4},{7,6},{5,7},{3,5},{1,3},{8,9},{10,8},{12,1... | collective-permute-start | bytes 786440 | tf_op jit(solution)/shard_map/ppermute | solution.py:167
  82.9 0.7 copy-start.6
  83.2 0.6 copy-start.7
  85.0 5.0 %collective-permute-start.14 = (f32[8,1,4096]{2,0,1:T(8,128)S(1)}, f32[8,1,4096]{2,0,1:T(8,128)S(1)}, u32[]{:S(2)}, u32[]{:S(2)}) collective-permute-start(f32[8,1,4096]{2,0,1:T(8,128)S(1)} %convolution_bitcast_fusion), channel_id=1, source_target_pairs={{0,1},{1,0},{2,3},{3,2},{4,5},{5,4},{6,7},{7,6},{8,9},{9,8},{10,11... | collective-permute-start | bytes 393224 | tf_op jit(solution)/shard_map/ppermute | solution.py:116
  90.0 5.8 %collective-permute-start.15 = (f32[8,1,4096]{2,0,1:T(8,128)S(1)}, f32[8,1,4096]{2,0,1:T(8,128)S(1)}, u32[]{:S(2)}, u32[]{:S(2)}) collective-permute-start(f32[8,1,4096]{2,0,1:T(8,128)S(1)} %add.216), channel_id=1, source_target_pairs={{0,2},{1,3},{2,0},{3,1},{4,6},{5,7},{6,4},{7,5},{8,10},{9,11},{10,... | collective-permute-start | bytes 393224 | tf_op jit(solution)/shard_map/ppermute | solution.py:116
  95.8 5.9 %collective-permute-start.16 = (f32[8,1,4096]{2,0,1:T(8,128)S(1)}, f32[8,1,4096]{2,0,1:T(8,128)S(1)}, u32[]{:S(2)}, u32[]{:S(2)}) collective-permute-start(f32[8,1,4096]{2,0,1:T(8,128)S(1)} %add.217), channel_id=1, source_target_pairs={{0,4},{1,5},{2,6},{3,7},{4,0},{5,1},{6,2},{7,3},{8,12},{9,13},{10,... | collective-permute-start | bytes 393224 | tf_op jit(solution)/shard_map/ppermute | solution.py:116
  115.8 4.3 %collective-permute-start.17 = (f32[2,2,1,1,4096]{4,2,1,0,3:T(1,128)S(1)}, f32[2,2,1,1,4096]{4,2,1,0,3:T(1,128)S(1)}, u32[]{:S(2)}, u32[]{:S(2)}) collective-permute-start(f32[2,2,1,1,4096]{4,2,1,0,3:T(1,128)S(1)} %constant_dynamic-slice_fusion.1), channel_id=1, source_target_pairs={{0,1},{1,0},{2,3},{3,2},{4,5},{5,4},{6,7},{7,6},{8,9},{9,8},{10,11... | collective-permute-start | bytes 196616 | tf_op jit(solution)/shard_map/ppermute | solution.py:546
  120.3 4.0 %collective-permute-start.18 = (f32[2,1,1,1,4096]{4,2,1,0,3:T(1,128)S(1)}, f32[2,1,1,1,4096]{4,2,1,0,3:T(1,128)S(1)}, u32[]{:S(2)}, u32[]{:S(2)}) collective-permute-start(f32[2,1,1,1,4096]{4,2,1,0,3:T(1,128)S(1)} %constant_dynamic-slice_fusion), channel_id=1, source_target_pairs={{0,2},{1,3},{2,0},{3,1},{4,6},{5,7},{6,4},{7,5},{8,10},{9,11},{10,... | collective-permute-start | bytes 98312 | tf_op jit(solution)/shard_map/ppermute | solution.py:546
  124.3 5.2 %collective-permute-start.20 = (f32[1,4096]{1,0:T(1,128)S(1)}, f32[1,4096]{1,0:T(1,128)S(1)}, u32[]{:S(2)}, u32[]{:S(2)}) collective-permute-start(f32[1,4096]{1,0:T(1,128)S(1)} %dynamic-slice_bitcast_fusion), channel_id=1, source_target_pairs={{0,12},{1,13},{2,14},{3,15},{4,8},{5,9},{6,10},{7,11},{8,20},{9,21... | collective-permute-start | bytes 49160 | tf_op jit(solution)/shard_map/ppermute | solution.py:563
  125.3 5.0 %collective-permute-start.19 = (f32[1,4096]{1,0:T(1,128)S(1)}, f32[1,4096]{1,0:T(1,128)S(1)}, u32[]{:S(2)}, u32[]{:S(2)}) collective-permute-start(f32[1,4096]{1,0:T(1,128)S(1)} %fusion.33), channel_id=1, source_target_pairs={{0,8},{1,9},{2,10},{3,11},{4,12},{5,13},{6,14},{7,15},{8,16},{9,17... | collective-permute-start | bytes 49160 | tf_op jit(solution)/shard_map/ppermute | solution.py:562
